TPU v7x, 32 devices: a whole 2x2x4 slice. The times are simulated.
32 devices in a mesh: groups: 2 (over y), lon: 4 (over z), chan: 2 (over x), lat: 2 (over core).
Axes of the slice: x: 2, y: 2, z: 4, core: 2. Of those that a mesh axis runs over, the one named last changes fastest.
Arguments:
- inputs: bfloat16 [256, 64, 512], P('chan', ('groups', 'lat'), 'lon'), parts along dimension 1, may hold values from -6 to 6
- cotangent: bfloat16 [256, 64, 512], P('chan', ('groups', 'lat'), 'lon'), parts along dimension 1, may hold values from -6 to 6
- weight: bfloat16 [3, 3, 256, 256], P(None, None, 'chan'), may hold values from -0.125 to 0.125
- bias_vector: float32 [256], P('chan'), may hold values from -4 to 4
Outputs:
- input_grad: bfloat16 [256, 64, 512], P('chan', ('groups', 'lat'), 'lon'), parts along dimension 1
- weight_grad: float32 [6, 3, 256, 256], P('groups', None, 'chan'), parts along dimension 0
- bias_grad: float32 [512], P(('groups', 'chan')), parts along dimension 0
There are 2 independent parts, one for each index of `groups`. A program takes and returns all parts, laid end to end along the dimension named above; an argument that names none is the same for every part. Nothing has to cross between parts.
All inputs are finite; a program needn't handle non-finite values.
Results may differ from a plain program's by a relative error of at most 0.007.
Values may be sent and summed in bfloat16 or wider, within the bound.
No kernel may reach another device: no remote copies, remote signals or barrier semaphores. Data moves between devices by JAX's collectives and lax.ppermute only.
A program may use at most 64 MiB of HBM per device.

v0:
```python
import jax
import jax.numpy as jnp
from jax import lax
from jax.sharding import PartitionSpec as P


def padded_2(shard, sides, width):
    for axis, dim in sides:
        devices, length = (lax.axis_size(axis), shard.shape[dim])
        up = [(i, (i + 1) % devices) for i in range(devices)]
        down = [(j, i) for i, j in up]
        last = lax.slice_in_dim(shard, length - width, length, axis=dim)
        initial = lax.slice_in_dim(shard, 0, width, axis=dim)
        before = lax.ppermute(last, axis, up)
        after = lax.ppermute(initial, axis, down)
        shard = jnp.concatenate([before, shard, after], axis=dim)
    return shard


def gelu_slope(preact):
    normal_cdf = 0.5 * (1.0 + jax.scipy.special.erf(preact * 0.7071067811865476))
    density = jnp.exp(-0.5 * preact * preact) * 0.3989422804014327
    return normal_cdf + preact * density


def mask_rims(padded):
    lat_index = lax.axis_index("lat")
    band_count = lax.axis_size("lat")
    row_ids = jnp.arange(padded.shape[1])
    outside = (row_ids == 0) & (lat_index == 0) | (row_ids == padded.shape[1] - 1) & (
        lat_index == band_count - 1
    )
    return jnp.where(outside[None, :, None], jnp.zeros((), padded.dtype), padded)


def window_of(field, first_row, first_col, row_count, column_count):
    return field[
        :, first_row : first_row + row_count, first_col : first_col + column_count
    ].reshape(field.shape[0], -1)


def local(inputs, cotangent, weight, bias_vector):
    own_channels, row_count, column_count = inputs.shape
    input_pad = mask_rims(padded_2(inputs, (("lon", 2), ("lat", 1)), 1))
    input_all = lax.all_gather(input_pad, "chan", axis=0, tiled=True)
    preact = jnp.zeros((own_channels, row_count * column_count), jnp.float32)
    for tap_row in range(3):
        for tap_col in range(3):
            window = window_of(input_all, tap_row, tap_col, row_count, column_count)
            preact = preact + jnp.dot(
                weight[tap_row, tap_col], window, preferred_element_type=jnp.float32
            )
    preact = preact + bias_vector[:, None]
    upstream = cotangent.reshape(own_channels, -1).astype(jnp.float32)
    grad_pre = (upstream * gelu_slope(preact)).astype(jnp.bfloat16)
    bias_part = jnp.sum(grad_pre.astype(jnp.float32), axis=1)
    taps = []
    for tap_row in range(3):
        row_taps = []
        for tap_col in range(3):
            window = window_of(input_all, tap_row, tap_col, row_count, column_count)
            row_taps.append(
                lax.dot_general(
                    grad_pre, window, (((1,), (1,)), ((), ())), preferred_element_type=jnp.float32
                )
            )
        taps.append(jnp.stack(row_taps))
    weight_part = jnp.stack(taps)
    weight_grad, bias_grad = lax.psum((weight_part, bias_part), ("lon", "lat"))
    grad_field = grad_pre.reshape(own_channels, row_count, column_count)
    grad_pad = mask_rims(padded_2(grad_field, (("lon", 2), ("lat", 1)), 1))
    amount = lax.axis_size("chan") * own_channels
    summed = jnp.zeros((amount, row_count * column_count), jnp.float32)
    for tap_row in range(3):
        for tap_col in range(3):
            kernel_cols = weight[tap_row, tap_col]
            window = window_of(grad_pad, 2 - tap_row, 2 - tap_col, row_count, column_count)
            summed = summed + lax.dot_general(
                kernel_cols, window, (((0,), (0,)), ((), ())), preferred_element_type=jnp.float32
            )
    input_sum = lax.psum_scatter(
        summed.reshape(amount, row_count, column_count), "chan", scatter_dimension=0, tiled=True
    )
    return (input_sum.astype(jnp.bfloat16), weight_grad, bias_grad)


def solution(mesh):
    placed = (
        P("chan", ("groups", "lat"), "lon"),
        P("chan", ("groups", "lat"), "lon"),
        P(None, None, "chan", None),
        P("chan"),
    )
    return jax.shard_map(
        local,
        mesh=mesh,
        in_specs=placed,
        out_specs=(
            P("chan", ("groups", "lat"), "lon"),
            P("groups", None, "chan", None),
            P(("groups", "chan")),
        ),
        check_vma=False,
    )
```

profile of v0, /device:TPU:0, one launch (start us, length us, event | category | flops | bytes accessed | tf_op | source)
XLA Modules:
  0.0 177.4 jit_solution(9235394544272731963)
XLA Ops:
  7.2 1.5 copy.13
  8.8 3.1 %collective-permute-start = (bf16[128,16,1]{0,2,1:T(2,128)(2,1)S(1)}, bf16[128,16,1]{0,2,1:T(2,128)(2,1)S(1)}, u32[]{:S(2)}, u32[]{:S(2)}) collective-permute-start(bf16[128,16,1]{0,2,1:T(2,128)(2,1)S(1)} %get-tuple-element.27), channel_id=1, source_target_pairs={{0,4},{4,8},{8,12},{12,0},{1,5},{5,9},{9,13},{13,1},{2,6},{6,10},{... | collective-permute-start | bytes 12296 | tf_op jit(solution)/shard_map/ppermute | solution.py:14
  11.8 2.1 %collective-permute-start.1 = (bf16[128,16,1]{0,2,1:T(2,128)(2,1)S(1)}, bf16[128,16,1]{0,2,1:T(2,128)(2,1)S(1)}, u32[]{:S(2)}, u32[]{:S(2)}) collective-permute-start(bf16[128,16,1]{0,2,1:T(2,128)(2,1)S(1)} %get-tuple-element.28), channel_id=1, source_target_pairs={{4,0},{8,4},{12,8},{0,12},{5,1},{9,5},{13,9},{1,13},{6,2},{10,6},{... | collective-permute-start | bytes 12296 | tf_op jit(solution)/shard_map/ppermute | solution.py:15
  13.9 1.6 collective-permute-done
  15.7 0.5 collective-permute-start.3
  16.2 0.7 collective-permute-done.2
  17.0 1.1 maximum_select_fusion
  18.2 1.4 copy.12
  19.6 23.9 %all-gather.2.cloned.1.call-done = bf16[256,18,130]{0,2,1:T(8,128)(2,1)} async-done(((bf16[128,18,130]{0,2,1:T(8,128)(2,1)}), bf16[256,18,130]{0,2,1:T(8,128)(2,1)}) %all-gather.2.cloned.1.call-update) | async-done | bytes 1198096 | tf_op jit(solution)/shard_map/all_gather | solution.py:45
  43.5 8.3 %fusion.46 = (bf16[256,16,128]{0,2,1:T(8,128)(2,1)S(1)}, bf16[256,16,128]{0,2,1:T(8,128)(2,1)S(1)}, bf16[256,16,128]{0,2,1:T(8,128)(2,1)S(1)}, bf16[256,16,128]{...) fusion(bf16[256,18,130]{0,2,1:T(8,128)(2,1)} %all-gather.2.clon, ...), kind=kLoop, calls=%fused_computation.86 | loop fusion | bytes 18874368 | tf_op jit(solution)/shard_map/slice | solution.py:37
  52.3 0.4 convolution_add_fusion.15
  54.6 0.4 convolution_add_fusion.10
  55.6 0.7 copy-done.13
  56.3 0.7 convert_reduce_fusion
  57.1 1.5 collective-permute-start.4
  58.6 2.3 %collective-permute-start.5 = (bf16[128,16,1]{0,2,1:T(2,128)(2,1)S(1)}, bf16[128,16,1]{0,2,1:T(2,128)(2,1)S(1)}, u32[]{:S(2)}, u32[]{:S(2)}) collective-permute-start(bf16[128,16,1]{0,2,1:T(2,128)(2,1)S(1)} %get-tuple-element.26), channel_id=1, source_target_pairs={{4,0},{8,4},{12,8},{0,12},{5,1},{9,5},{13,9},{1,13},{6,2},{10,6},{... | collective-permute-start | bytes 12296 | tf_op jit(solution)/shard_map/ppermute | solution.py:15
  60.9 1.6 collective-permute-done.4
  62.7 0.5 collective-permute-start.7
  63.2 0.7 collective-permute-done.6
  64.4 0.9 fusion.47
  68.6 1.7 convolution_add_fusion
  70.4 3.0 %copy.16 = f32[256,16,128]{2,1,0:T(8,128)} copy(f32[256,16,128]{0,2,1:T(8,128)} %bitcast.154) | data formatting | bytes 4194304 | tf_op jit(solution)/shard_map/reshape | solution.py:82
  73.6 1.7 convolution_bitcast_fusion
  75.3 1.7 convolution_bitcast_fusion.1
  77.8 0.4 copy-done.5
  79.0 0.5 copy-done.1
  80.6 1.1 pad_maximum_fusion
  81.8 17.9 %psum.15 = f32[128]{0:T(128)} all-reduce(f32[128]{0:T(128)S(1)} %get-tuple-element.29), channel_id=1, replica_groups=mesh['groups'=2,'lon'=4,'chan'=2,'lat'=2] {'lon','lat'}, use_global_device_ids=true, to_apply=%region_3.4 | all-reduce | flops 128 | bytes 1024 | tf_op jit(solution)/shard_map/psum | solution.py:69
  99.6 6.3 %reduce-scatter.2.cloned.1.call-done = f32[128,16,128]{2,1,0:T(8,128)} async-done(((f32[256,16,128]{2,1,0:T(8,128)}), f32[128,16,128]{2,1,0:T(8,128)}) %reduce-scatter.2.cloned.1.call-update) | async-done | bytes 1048592 | tf_op jit(solution)/shard_map/reduce_scatter | solution.py:81
  105.9 2.1 %convert_element_type.18 = bf16[128,16,128]{2,1,0:T(8,128)(2,1)} convert(f32[128,16,128]{2,1,0:T(8,128)} %reduce-scatter.2.cloned.1.call-done) | non-fusion elementwise | flops 262144 | bytes 1572864 | tf_op jit(solution)/shard_map/convert_element_type | solution.py:84
  108.0 60.5 %all-reduce.2.cloned.1.call-done = f32[3,3,128,256]{3,2,1,0:T(8,128)} async-done(((f32[3,3,128,256]{3,2,1,0:T(8,128)}), f32[3,3,128,256]{3,2,1,0:T(8,128)}) %all-reduce.2.cloned.1.call-update) | async-done | bytes 1179664 | tf_op jit(solution)/shard_map/psum | solution.py:69
  168.5 2.4 %copy.18 = f32[3,3,128,256]{3,2,1,0:T(8,128)} copy(f32[3,3,128,256]{3,2,1,0:T(8,128)} %all-reduce.2.cloned.1.call-done) | data formatting | bytes 2359296
  (70 shorter events, 9.9 us)
Async XLA Ops:
  7.2 11.1 %copy-start.14 = (bf16[128,16,128]{2,1,0:T(8,128)(2,1)S(1)}, bf16[128,16,128]{2,1,0:T(8,128)(2,1)}, u32[]{:S(2)}) copy-start(bf16[128,16,128]{2,1,0:T(8,128)(2,1)} %param.5) | copy-start | bytes 1572868
  7.2 36.3 %all-gather.2.cloned.1.call-start = ((), (), s32[]{:S(2)}) async-start(), calls=%async_computation.1 | async-start | bytes 1880064 | tf_op jit(solution)/shard_map/all_gather | solution.py:45
  8.8 6.8 %collective-permute-start = (bf16[128,16,1]{0,2,1:T(2,128)(2,1)S(1)}, bf16[128,16,1]{0,2,1:T(2,128)(2,1)S(1)}, u32[]{:S(2)}, u32[]{:S(2)}) collective-permute-start(bf16[128,16,1]{0,2,1:T(2,128)(2,1)S(1)} %get-tuple-element.27), channel_id=1, source_target_pairs={{0,4},{4,8},{8,12},{12,0},{1,5},{5,9},{9,13},{13,1},{2,6},{6,10},{... | collective-permute-start | bytes 12296 | tf_op jit(solution)/shard_map/ppermute | solution.py:14
  11.8 3.7 %collective-permute-start.1 = (bf16[128,16,1]{0,2,1:T(2,128)(2,1)S(1)}, bf16[128,16,1]{0,2,1:T(2,128)(2,1)S(1)}, u32[]{:S(2)}, u32[]{:S(2)}) collective-permute-start(bf16[128,16,1]{0,2,1:T(2,128)(2,1)S(1)} %get-tuple-element.28), channel_id=1, source_target_pairs={{4,0},{8,4},{12,8},{0,12},{5,1},{9,5},{13,9},{1,13},{6,2},{10,6},{... | collective-permute-start | bytes 12296 | tf_op jit(solution)/shard_map/ppermute | solution.py:15
  15.6 1.3 collective-permute-start.2
  15.7 1.4 collective-permute-start.3
  18.2 87.8 %reduce-scatter.2.cloned.1.call-start = ((), (), s32[]{:S(2)}) async-start(), calls=%async_computation.2 | async-start | bytes 3145728 | tf_op jit(solution)/shard_map/reduce_scatter | solution.py:81
  19.6 32.3 %copy-start.12 = (bf16[3,3,128,256]{3,2,1,0:T(8,128)(2,1)S(1)}, bf16[3,3,128,256]{3,2,1,0:T(8,128)(2,1)}, u32[]{:S(2)}) copy-start(bf16[3,3,128,256]{3,2,1,0:T(8,128)(2,1)} %param.6) | copy-start | bytes 1769476
  51.8 1.0 copy-start
  51.9 1.4 copy-start.2
  51.9 1.9 %copy-start.4 = (bf16[256,16,128]{0,2,1:T(8,128)(2,1)}, bf16[256,16,128]{0,2,1:T(8,128)(2,1)S(1)}, u32[]{:S(2)}) copy-start(bf16[256,16,128]{0,2,1:T(8,128)(2,1)S(1)} %get-tuple-element.7) | copy-start | bytes 3145732
  51.9 2.3 %copy-start.6 = (bf16[256,16,128]{0,2,1:T(8,128)(2,1)}, bf16[256,16,128]{0,2,1:T(8,128)(2,1)S(1)}, u32[]{:S(2)}) copy-start(bf16[256,16,128]{0,2,1:T(8,128)(2,1)S(1)} %get-tuple-element.6) | copy-start | bytes 3145732
  51.9 2.7 %copy-start.8 = (bf16[256,16,128]{0,2,1:T(8,128)(2,1)}, bf16[256,16,128]{0,2,1:T(8,128)(2,1)S(1)}, u32[]{:S(2)}) copy-start(bf16[256,16,128]{0,2,1:T(8,128)(2,1)S(1)} %get-tuple-element.5) | copy-start | bytes 3145732
  51.9 3.2 %copy-start.10 = (bf16[256,16,128]{0,2,1:T(8,128)(2,1)}, bf16[256,16,128]{0,2,1:T(8,128)(2,1)S(1)}, u32[]{:S(2)}) copy-start(bf16[256,16,128]{0,2,1:T(8,128)(2,1)S(1)} %get-tuple-element.4) | copy-start | bytes 3145732
  51.9 3.6 %copy-start.11 = (bf16[256,16,128]{0,2,1:T(8,128)(2,1)}, bf16[256,16,128]{0,2,1:T(8,128)(2,1)S(1)}, u32[]{:S(2)}) copy-start(bf16[256,16,128]{0,2,1:T(8,128)(2,1)S(1)} %get-tuple-element.3) | copy-start | bytes 3145732
  55.1 1.2 copy-start.13
  55.1 1.2 copy-start.15
  57.1 5.5 %collective-permute-start.4 = (bf16[128,16,1]{0,2,1:T(2,128)(2,1)S(1)}, bf16[128,16,1]{0,2,1:T(2,128)(2,1)S(1)}, u32[]{:S(2)}, u32[]{:S(2)}) collective-permute-start(bf16[128,16,1]{0,2,1:T(2,128)(2,1)S(1)} %get-tuple-element.25), channel_id=1, source_target_pairs={{0,4},{4,8},{8,12},{12,0},{1,5},{5,9},{9,13},{13,1},{2,6},{6,10},{... | collective-permute-start | bytes 12296 | tf_op jit(solution)/shard_map/ppermute | solution.py:14
  58.6 4.0 %collective-permute-start.5 = (bf16[128,16,1]{0,2,1:T(2,128)(2,1)S(1)}, bf16[128,16,1]{0,2,1:T(2,128)(2,1)S(1)}, u32[]{:S(2)}, u32[]{:S(2)}) collective-permute-start(bf16[128,16,1]{0,2,1:T(2,128)(2,1)S(1)} %get-tuple-element.26), channel_id=1, source_target_pairs={{4,0},{8,4},{12,8},{0,12},{5,1},{9,5},{13,9},{1,13},{6,2},{10,6},{... | collective-permute-start | bytes 12296 | tf_op jit(solution)/shard_map/ppermute | solution.py:15
  62.6 1.3 collective-permute-start.6
  62.7 1.4 collective-permute-start.7
  73.4 95.1 %all-reduce.2.cloned.1.call-start = ((), (), s32[]{:S(2)}) async-start(), calls=%async_computation.3 | async-start | bytes 2359296 | tf_op jit(solution)/shard_map/psum | solution.py:69
  73.6 3.3 %copy-start.9 = (bf16[256,16,128]{0,2,1:T(8,128)(2,1)S(1)}, bf16[256,16,128]{0,2,1:T(8,128)(2,1)}, u32[]{:S(2)}) copy-start(bf16[256,16,128]{0,2,1:T(8,128)(2,1)} %copy-done.8) | copy-start | bytes 3145732
  75.3 2.1 %copy-start.7 = (bf16[256,16,128]{0,2,1:T(8,128)(2,1)S(1)}, bf16[256,16,128]{0,2,1:T(8,128)(2,1)}, u32[]{:S(2)}) copy-start(bf16[256,16,128]{0,2,1:T(8,128)(2,1)} %copy-done.6) | copy-start | bytes 3145732
  77.0 1.2 copy-start.5
  77.4 1.3 copy-start.3
  78.2 1.3 copy-start.1
Sparse Core Ops, SparseCore 0:
  18.3 25.1 all-gather.1
  73.5 32.3 reduce-scatter.1
  109.0 59.5 all-reduce.1
where the time goes:
time: 178 us; the launch traced here: 177 us
  waiting for transfers between devices  95.8 us (54%)
  local copies, waits for them, and re-layouts  19.5 us (11%)
  blocking collectives  17.9 us (10%)
  matrix products  15 us (8%)
  between operations  14.2 us (8%)
  starting transfers between devices  10.5 us (6%)
  other arithmetic  4.73 us (3%)
    psum x1, waiting for transfers between devices, local(): weight_grad, bias_grad = lax.psum((weight_part, bias_part), ('lon', 'lat'))  60.5 us
    all_gather x1, waiting for transfers between devices, local(): input_all = lax.all_gather(input_pad, 'chan', axis=0, tiled=True)  23.9 us
    psum x1, blocking collectives, local(): weight_grad, bias_grad = lax.psum((weight_part, bias_part), ('lon', 'lat'))  17.9 us
    slice x2, local copies, waits for them, and re-layouts, window_of(): field[:, first_row:first_row + row_count, first_col:first_col + column_co...  9.24 us
    reduce_scatter x1, waiting for transfers between devices, local(): lax.psum_scatter(summed.reshape(amount, row_count, column_count), 'chan',...  6.31 us
    unnamed x34, local copies, waits for them, and re-layouts  5.76 us
    dot_general x9, matrix products, local(): lax.dot_general(grad_pre, window, (((1,), (1,)), ((), ())), preferred_ele...  5.76 us
    ppermute x4, starting transfers between devices, padded_2(): after = lax.ppermute(initial, axis, down)  5.42 us
  transfers between devices with their start and end apart: 11, of which 9 were waited for; matrix products, arithmetic and copies ran while one was open for 6% of the time, Pallas kernels for 0%

commit v1 on v0

--- a/solution.py
+++ b/solution.py
@@ -39,26 +39,48 @@
     ].reshape(field.shape[0], -1)
 
 
+def conv_taps(kernel, field, row_count, column_count, flip):
+    total = None
+    for tap_row in range(3):
+        for tap_col in range(3):
+            if flip:
+                window = window_of(field, 2 - tap_row, 2 - tap_col, row_count, column_count)
+            else:
+                window = window_of(field, tap_row, tap_col, row_count, column_count)
+            part = jnp.dot(kernel[tap_row, tap_col], window, preferred_element_type=jnp.float32)
+            total = part if total is None else total + part
+    return total
+
+
 def local(inputs, cotangent, weight, bias_vector):
     own_channels, row_count, column_count = inputs.shape
+    chan_count = lax.axis_size("chan")
+    chan_index = lax.axis_index("chan")
     input_pad = mask_rims(padded_2(inputs, (("lon", 2), ("lat", 1)), 1))
-    input_all = lax.all_gather(input_pad, "chan", axis=0, tiled=True)
-    preact = jnp.zeros((own_channels, row_count * column_count), jnp.float32)
-    for tap_row in range(3):
-        for tap_col in range(3):
-            window = window_of(input_all, tap_row, tap_col, row_count, column_count)
-            preact = preact + jnp.dot(
-                weight[tap_row, tap_col], window, preferred_element_type=jnp.float32
-            )
+    blocks = [input_pad]
+    for shift in range(1, chan_count):
+        pairs = [(i, (i - shift) % chan_count) for i in range(chan_count)]
+        blocks.append(lax.ppermute(input_pad, "chan", pairs))
+    kernel_cols = []
+    for shift in range(chan_count):
+        source = (chan_index + shift) % chan_count
+        kernel_cols.append(
+            lax.dynamic_slice_in_dim(weight, source * own_channels, own_channels, axis=3)
+        )
+    preact = None
+    for shift in range(chan_count):
+        part = conv_taps(kernel_cols[shift], blocks[shift], row_count, column_count, False)
+        preact = part if preact is None else preact + part
     preact = preact + bias_vector[:, None]
     upstream = cotangent.reshape(own_channels, -1).astype(jnp.float32)
     grad_pre = (upstream * gelu_slope(preact)).astype(jnp.bfloat16)
     bias_part = jnp.sum(grad_pre.astype(jnp.float32), axis=1)
+    input_local = jnp.concatenate(blocks, axis=0)
     taps = []
     for tap_row in range(3):
         row_taps = []
         for tap_col in range(3):
-            window = window_of(input_all, tap_row, tap_col, row_count, column_count)
+            window = window_of(input_local, tap_row, tap_col, row_count, column_count)
             row_taps.append(
                 lax.dot_general(
                     grad_pre, window, (((1,), (1,)), ((), ())), preferred_element_type=jnp.float32
@@ -66,22 +88,27 @@
             )
         taps.append(jnp.stack(row_taps))
     weight_part = jnp.stack(taps)
-    weight_grad, bias_grad = lax.psum((weight_part, bias_part), ("lon", "lat"))
+    flat = jnp.concatenate([weight_part.reshape(-1), bias_part])
+    flat = lax.psum(flat, ("lon", "lat"))
+    weight_local = flat[: weight_part.size].reshape(weight_part.shape)
+    bias_grad = flat[weight_part.size :]
+    doubled = jnp.concatenate([weight_local, weight_local], axis=3)
+    weight_grad = lax.dynamic_slice_in_dim(
+        doubled, (chan_count - chan_index) % chan_count * own_channels, chan_count * own_channels, axis=3
+    )
     grad_field = grad_pre.reshape(own_channels, row_count, column_count)
     grad_pad = mask_rims(padded_2(grad_field, (("lon", 2), ("lat", 1)), 1))
-    amount = lax.axis_size("chan") * own_channels
-    summed = jnp.zeros((amount, row_count * column_count), jnp.float32)
-    for tap_row in range(3):
-        for tap_col in range(3):
-            kernel_cols = weight[tap_row, tap_col]
-            window = window_of(grad_pad, 2 - tap_row, 2 - tap_col, row_count, column_count)
-            summed = summed + lax.dot_general(
-                kernel_cols, window, (((0,), (0,)), ((), ())), preferred_element_type=jnp.float32
-            )
-    input_sum = lax.psum_scatter(
-        summed.reshape(amount, row_count, column_count), "chan", scatter_dimension=0, tiled=True
-    )
-    return (input_sum.astype(jnp.bfloat16), weight_grad, bias_grad)
+    received = []
+    for shift in range(1, chan_count):
+        kernel_t = jnp.swapaxes(kernel_cols[shift], 2, 3)
+        part = conv_taps(kernel_t, grad_pad, row_count, column_count, True)
+        pairs = [(i, (i + shift) % chan_count) for i in range(chan_count)]
+        received.append(lax.ppermute(part.astype(jnp.bfloat16), "chan", pairs))
+    own_part = conv_taps(jnp.swapaxes(kernel_cols[0], 2, 3), grad_pad, row_count, column_count, True)
+    for piece in received:
+        own_part = own_part + piece.astype(jnp.float32)
+    input_grad = own_part.astype(jnp.bfloat16).reshape(own_channels, row_count, column_count)
+    return (input_grad, weight_grad, bias_grad)
 
 
 def solution(mesh):

time: 178 us -> 124 us (0.70)
  waiting for transfers between devices: 95.8 us -> 64.2 us
  blocking collectives: 17.9 us -> 0 us
  local copies, waits for them, and re-layouts: 19.5 us -> 10.7 us
  starting transfers between devices: 10.5 us -> 13.8 us
    all_gather x1 -> x0, waiting for transfers between devices: 23.9 us -> none  [local(): input_all = lax.all_gather(input_pad, 'chan', axis=0, tiled=True)]
    ppermute x0 -> x2, waiting for transfers between devices: none -> 23.6 us  [the longest x1 12 us: local(): blocks.append(lax.ppermute(input_pad, 'chan', pairs))]
    psum x1, waiting for transfers between devices: 60.5 us -> 38.5 us  [local(): flat = lax.psum(flat, ('lon', 'lat'))]
    psum x1 -> x0, blocking collectives: 17.9 us -> none  [local(): weight_grad, bias_grad = lax.psum((weight_part, bias_part), ('lon', 'lat'))]
    slice x2 -> x3, local copies, waits for them, and re-layouts: 9.24 us -> 2.77 us  [window_of(): field[:, first_row:first_row + row_count, first_col:first_col + column_co...]
    reduce_scatter x1 -> x0, waiting for transfers between devices: 6.31 us -> none  [local(): lax.psum_scatter(summed.reshape(amount, row_count, column_count), 'chan',...]
    concatenate x0 -> x3, other arithmetic: none -> 4.8 us  [the longest x1 2.53 us: local(): input_local = jnp.concatenate(blocks, axis=0)]
    ppermute x0 -> x2, starting transfers between devices: none -> 3.37 us  [the longest x1 1.69 us: local(): blocks.append(lax.ppermute(input_pad, 'chan', pairs))]
  transfers between devices with their start and end apart: 11 -> 11, of which waited for: 9 -> 7; matrix products, arithmetic and copies ran while one was open for 6% -> 11% of each run, Pallas kernels for 0% -> 0%
where the time goes in v1:
time: 124 us
  waiting for transfers between devices  64.2 us (52%)
  matrix products  15.1 us (12%)
  between operations  14.5 us (12%)
  starting transfers between devices  13.8 us (11%)
  local copies, waits for them, and re-layouts  10.7 us (9%)
  other arithmetic  5.77 us (5%)
    psum x1, waiting for transfers between devices, local(): flat = lax.psum(flat, ('lon', 'lat'))  38.5 us
    dot_general x36, matrix products, conv_taps(): jnp.dot(kernel[tap_row, tap_col], window, preferred_element_type=jnp.floa...  12.3 us
    ppermute x1, waiting for transfers between devices, local(): blocks.append(lax.ppermute(input_pad, 'chan', pairs))  12 us
    ppermute x1, waiting for transfers between devices, local(): received.append(lax.ppermute(part.astype(jnp.bfloat16), 'chan', pairs))  11.6 us
    ppermute x4, starting transfers between devices, padded_2(): after = lax.ppermute(initial, axis, down)  5.63 us
    ppermute x4, starting transfers between devices, padded_2(): before = lax.ppermute(last, axis, up)  4.75 us
    unnamed x15, local copies, waits for them, and re-layouts  4.54 us
    dot_general x9, matrix products, local(): lax.dot_general(grad_pre, window, (((1,), (1,)), ((), ())), preferred_ele...  2.85 us
  transfers between devices with their start and end apart: 11, of which 7 were waited for; matrix products, arithmetic and copies ran while one was open for 11% of the time, Pallas kernels for 0%

profile of v1, /device:TPU:0, one launch (start us, length us, event | category | flops | bytes accessed | tf_op | source)
XLA Modules:
  0.0 124.1 jit_solution(772174788698631369)
XLA Ops:
  7.2 1.5 %copy.7 = bf16[128,16,128]{0,2,1:T(8,128)(2,1)S(1)} copy(bf16[128,16,128]{2,1,0:T(8,128)(2,1)} %param.4) | data formatting | bytes 1048576 | tf_op args[0]
  8.8 3.1 %collective-permute-start = (bf16[128,16,1]{0,2,1:T(2,128)(2,1)S(1)}, bf16[128,16,1]{0,2,1:T(2,128)(2,1)S(1)}, u32[]{:S(2)}, u32[]{:S(2)}) collective-permute-start(bf16[128,16,1]{0,2,1:T(2,128)(2,1)S(1)} %get-tuple-element.47), channel_id=1, source_target_pairs={{0,4},{4,8},{8,12},{12,0},{1,5},{5,9},{9,13},{13,1},{2,6},{6,10},{... | collective-permute-start | bytes 12296 | tf_op jit(solution)/shard_map/ppermute | solution.py:14
  11.9 2.1 %collective-permute-start.1 = (bf16[128,16,1]{0,2,1:T(2,128)(2,1)S(1)}, bf16[128,16,1]{0,2,1:T(2,128)(2,1)S(1)}, u32[]{:S(2)}, u32[]{:S(2)}) collective-permute-start(bf16[128,16,1]{0,2,1:T(2,128)(2,1)S(1)} %get-tuple-element.48), channel_id=1, source_target_pairs={{4,0},{8,4},{12,8},{0,12},{5,1},{9,5},{13,9},{1,13},{6,2},{10,6},{... | collective-permute-start | bytes 12296 | tf_op jit(solution)/shard_map/ppermute | solution.py:15
  14.1 0.9 dynamic-slice_bitcast_fusion.1
  15.0 0.6 collective-permute-done
  15.7 0.5 collective-permute-start.3
  16.2 0.7 collective-permute-done.2
  17.4 0.9 fusion.57
  18.3 1.7 %collective-permute-start.4 = (bf16[128,18,130]{0,2,1:T(8,128)(2,1)S(1)}, bf16[128,18,130]{0,2,1:T(8,128)(2,1)S(1)}, u32[]{:S(2)}, u32[]{:S(2)}) collective-permute-start(bf16[128,18,130]{0,2,1:T(8,128)(2,1)S(1)} %maximum_select_fusion), channel_id=1, source_target_pairs={{0,2},{2,0},{1,3},{3,1},{4,6},{6,4},{5,7},{7,5},{8,10},{10,8},{9,1... | collective-permute-start | bytes 1797128 | tf_op jit(solution)/shard_map/ppermute | solution.py:63
  22.8 12.0 %collective-permute-done.4 = bf16[128,18,130]{0,2,1:T(8,128)(2,1)S(1)} collective-permute-done((bf16[128,18,130]{0,2,1:T(8,128)(2,1)S(1)}, bf16[128,18,130]{0,2,1:T(8,128)(2,1)S(1)}, u32[]{:S(2)}, u32[]{:S(2)}) %collective-permute-start.4) | collective-permute-done | bytes 599072 | tf_op jit(solution)/shard_map/ppermute | solution.py:63
  34.8 0.9 fusion.56
  38.2 0.3 copy-done.5
  38.5 1.4 %convert_reduce_fusion = (f32[128]{0:T(128)S(1)}, bf16[128,2048]{1,0:T(8,128)(2,1)S(1)}) fusion(f32[128]{0:T(128)S(1)} %copy-done.5, f32[128,2048]{1,0:T(8,128)S(1)} %convolution_add_fusion.17, f32[128,2048]{1,0:T(8,128)S(1)} %fusion.27, f32[128,2048]{1,0:T(8,128)S(1)} %fusion.28, f32[128,2048]{1,0:T(8,128)S(1)} %fusion.29, f32[128,2048]{1,0:T(8,128)S(1)} %fusion.30, ...), kind=kOutput, calls=%fused_computation.81 | convolution fusion | flops 72875904 | bytes 11568132 | tf_op jit(solution)/shard_map/dot_general | solution.py:50
  40.2 2.5 %fusion.18 = (bf16[256,16,128]{0,2,1:T(8,128)(2,1)S(1)}, bf16[256,16,128]{0,2,1:T(8,128)(2,1)S(1)}, bf16[256,16,128]{0,2,1:T(8,128)(2,1)S(1)}, bf16[256,16,128]{...) fusion(bf16[128,18,130]{0,2,1:T(8,128)(2,1)S(1)} %maximum_selec, ...), kind=kLoop, calls=%fused_computation.73 | loop fusion | flops 18874368 | bytes 10635264 | tf_op jit(solution)/shard_map/concatenate | solution.py:78
  45.7 1.5 %collective-permute-start.5 = (bf16[128,16,1]{0,2,1:T(2,128)(2,1)S(1)}, bf16[128,16,1]{0,2,1:T(2,128)(2,1)S(1)}, u32[]{:S(2)}, u32[]{:S(2)}) collective-permute-start(bf16[128,16,1]{0,2,1:T(2,128)(2,1)S(1)} %get-tuple-element.45), channel_id=1, source_target_pairs={{0,4},{4,8},{8,12},{12,0},{1,5},{5,9},{9,13},{13,1},{2,6},{6,10},{... | collective-permute-start | bytes 12296 | tf_op jit(solution)/shard_map/ppermute | solution.py:14
  47.2 2.5 %collective-permute-start.6 = (bf16[128,16,1]{0,2,1:T(2,128)(2,1)S(1)}, bf16[128,16,1]{0,2,1:T(2,128)(2,1)S(1)}, u32[]{:S(2)}, u32[]{:S(2)}) collective-permute-start(bf16[128,16,1]{0,2,1:T(2,128)(2,1)S(1)} %get-tuple-element.46), channel_id=1, source_target_pairs={{4,0},{8,4},{12,8},{0,12},{5,1},{9,5},{13,9},{1,13},{6,2},{10,6},{... | collective-permute-start | bytes 12296 | tf_op jit(solution)/shard_map/ppermute | solution.py:15
  49.9 0.6 copy.16
  50.5 0.6 collective-permute-done.5
  51.3 0.5 collective-permute-start.8
  51.8 1.1 pad_maximum_fusion
  52.9 0.3 maximum_select_fusion.1
  53.3 0.9 fusion.55
  54.5 0.6 copy-done.2
  59.7 1.7 %collective-permute-start.9 = (bf16[128,2048]{1,0:T(8,128)(2,1)S(1)}, bf16[128,2048]{1,0:T(8,128)(2,1)S(1)}, u32[]{:S(2)}, u32[]{:S(2)}) collective-permute-start(bf16[128,2048]{1,0:T(8,128)(2,1)S(1)} %fusion.9), channel_id=1, source_target_pairs={{0,2},{2,0},{1,3},{3,1},{4,6},{6,4},{5,7},{7,5},{8,10},{10,8},{9,1... | collective-permute-start | bytes 1572872 | tf_op jit(solution)/shard_map/ppermute | solution.py:106
  62.1 11.6 %collective-permute-done.9 = bf16[128,2048]{1,0:T(8,128)(2,1)S(1)} collective-permute-done((bf16[128,2048]{1,0:T(8,128)(2,1)S(1)}, bf16[128,2048]{1,0:T(8,128)(2,1)S(1)}, u32[]{:S(2)}, u32[]{:S(2)}) %collective-permute-start.9) | collective-permute-done | bytes 524320 | tf_op jit(solution)/shard_map/ppermute | solution.py:106
  74.0 0.9 copy.15
  74.9 38.5 %all-reduce.2.cloned.1.call-done = f32[295040]{0:T(1024)} async-done(((f32[295040]{0:T(1024)}), f32[295040]{0:T(1024)}) %all-reduce.2.cloned.1.call-update) | async-done | bytes 1180176 | tf_op jit(solution)/shard_map/psum | solution.py:92
  113.5 1.3 %slice-done = f32[294912]{0:T(1024)S(1)} async-done(((f32[295040]{0:T(1024)}), f32[294912]{0:T(1024)S(1)}, s32[]{:S(2)}) %slice-start) | async-done | bytes 1179672 | tf_op jit(solution)/shard_map/slice | solution.py:93
  114.7 0.3 reshape.187
  115.1 1.2 fusion.10
  116.2 0.5 copy-done
  116.7 0.5 slice.403
  (74 shorter events, 15.1 us)
Async XLA Ops:
  7.2 6.8 %copy-start.4 = (bf16[128,16,128]{2,1,0:T(8,128)(2,1)S(1)}, bf16[128,16,128]{2,1,0:T(8,128)(2,1)}, u32[]{:S(2)}) copy-start(bf16[128,16,128]{2,1,0:T(8,128)(2,1)} %param.5) | copy-start | bytes 1572868
  7.2 6.9 %copy-start.1 = (bf16[3,3,128,256]{3,2,1,0:T(8,128)(2,1)S(1)}, bf16[3,3,128,256]{3,2,1,0:T(8,128)(2,1)}, u32[]{:S(2)}) copy-start(bf16[3,3,128,256]{3,2,1,0:T(8,128)(2,1)} %param.6) | copy-start | bytes 1769476
  7.2 106.3 %all-reduce.2.cloned.1.call-start = ((), (), s32[]{:S(2)}) async-start(), calls=%async_computation | async-start | bytes 2367488 | tf_op jit(solution)/shard_map/psum | solution.py:92
  8.8 6.8 %collective-permute-start = (bf16[128,16,1]{0,2,1:T(2,128)(2,1)S(1)}, bf16[128,16,1]{0,2,1:T(2,128)(2,1)S(1)}, u32[]{:S(2)}, u32[]{:S(2)}) collective-permute-start(bf16[128,16,1]{0,2,1:T(2,128)(2,1)S(1)} %get-tuple-element.47), channel_id=1, source_target_pairs={{0,4},{4,8},{8,12},{12,0},{1,5},{5,9},{9,13},{13,1},{2,6},{6,10},{... | collective-permute-start | bytes 12296 | tf_op jit(solution)/shard_map/ppermute | solution.py:14
  11.9 3.7 %collective-permute-start.1 = (bf16[128,16,1]{0,2,1:T(2,128)(2,1)S(1)}, bf16[128,16,1]{0,2,1:T(2,128)(2,1)S(1)}, u32[]{:S(2)}, u32[]{:S(2)}) collective-permute-start(bf16[128,16,1]{0,2,1:T(2,128)(2,1)S(1)} %get-tuple-element.48), channel_id=1, source_target_pairs={{4,0},{8,4},{12,8},{0,12},{5,1},{9,5},{13,9},{1,13},{6,2},{10,6},{... | collective-permute-start | bytes 12296 | tf_op jit(solution)/shard_map/ppermute | solution.py:15
  15.7 1.3 %collective-permute-start.2 = (bf16[128,1,130]{0,2,1:T(8,128)(2,1)S(1)}, bf16[128,1,130]{0,2,1:T(8,128)(2,1)S(1)}, u32[]{:S(2)}, u32[]{:S(2)}) collective-permute-start(bf16[128,1,130]{0,2,1:T(8,128)(2,1)S(1)} %get-tuple-element.43), channel_id=1, source_target_pairs={{0,1},{1,0},{2,3},{3,2},{4,5},{5,4},{6,7},{7,6},{8,9},{9,8},{10,11... | collective-permute-start | bytes 99848 | tf_op jit(solution)/shard_map/ppermute | solution.py:14
  15.7 1.4 %collective-permute-start.3 = (bf16[128,1,130]{0,2,1:T(8,128)(2,1)S(1)}, bf16[128,1,130]{0,2,1:T(8,128)(2,1)S(1)}, u32[]{:S(2)}, u32[]{:S(2)}) collective-permute-start(bf16[128,1,130]{0,2,1:T(8,128)(2,1)S(1)} %get-tuple-element.44), channel_id=1, source_target_pairs={{1,0},{0,1},{3,2},{2,3},{5,4},{4,5},{7,6},{6,7},{9,8},{8,9},{11,10... | collective-permute-start | bytes 99848 | tf_op jit(solution)/shard_map/ppermute | solution.py:15
  18.3 16.4 %collective-permute-start.4 = (bf16[128,18,130]{0,2,1:T(8,128)(2,1)S(1)}, bf16[128,18,130]{0,2,1:T(8,128)(2,1)S(1)}, u32[]{:S(2)}, u32[]{:S(2)}) collective-permute-start(bf16[128,18,130]{0,2,1:T(8,128)(2,1)S(1)} %maximum_select_fusion), channel_id=1, source_target_pairs={{0,2},{2,0},{1,3},{3,1},{4,6},{6,4},{5,7},{7,5},{8,10},{10,8},{9,1... | collective-permute-start | bytes 1797128 | tf_op jit(solution)/shard_map/ppermute | solution.py:63
  37.8 0.7 copy-start.5
  45.7 5.5 %collective-permute-start.5 = (bf16[128,16,1]{0,2,1:T(2,128)(2,1)S(1)}, bf16[128,16,1]{0,2,1:T(2,128)(2,1)S(1)}, u32[]{:S(2)}, u32[]{:S(2)}) collective-permute-start(bf16[128,16,1]{0,2,1:T(2,128)(2,1)S(1)} %get-tuple-element.45), channel_id=1, source_target_pairs={{0,4},{4,8},{8,12},{12,0},{1,5},{5,9},{9,13},{13,1},{2,6},{6,10},{... | collective-permute-start | bytes 12296 | tf_op jit(solution)/shard_map/ppermute | solution.py:14
  47.2 4.0 %collective-permute-start.6 = (bf16[128,16,1]{0,2,1:T(2,128)(2,1)S(1)}, bf16[128,16,1]{0,2,1:T(2,128)(2,1)S(1)}, u32[]{:S(2)}, u32[]{:S(2)}) collective-permute-start(bf16[128,16,1]{0,2,1:T(2,128)(2,1)S(1)} %get-tuple-element.46), channel_id=1, source_target_pairs={{4,0},{8,4},{12,8},{0,12},{5,1},{9,5},{13,9},{1,13},{6,2},{10,6},{... | collective-permute-start | bytes 12296 | tf_op jit(solution)/shard_map/ppermute | solution.py:15
  51.2 1.7 %collective-permute-start.7 = (bf16[128,1,130]{0,2,1:T(8,128)(2,1)S(1)}, bf16[128,1,130]{0,2,1:T(8,128)(2,1)S(1)}, u32[]{:S(2)}, u32[]{:S(2)}) collective-permute-start(bf16[128,1,130]{0,2,1:T(8,128)(2,1)S(1)} %get-tuple-element.41), channel_id=1, source_target_pairs={{0,1},{1,0},{2,3},{3,2},{4,5},{5,4},{6,7},{7,6},{8,9},{9,8},{10,11... | collective-permute-start | bytes 99848 | tf_op jit(solution)/shard_map/ppermute | solution.py:14
  51.3 1.6 %collective-permute-start.8 = (bf16[128,1,130]{0,2,1:T(8,128)(2,1)S(1)}, bf16[128,1,130]{0,2,1:T(8,128)(2,1)S(1)}, u32[]{:S(2)}, u32[]{:S(2)}) collective-permute-start(bf16[128,1,130]{0,2,1:T(8,128)(2,1)S(1)} %get-tuple-element.42), channel_id=1, source_target_pairs={{1,0},{0,1},{3,2},{2,3},{5,4},{4,5},{7,6},{6,7},{9,8},{8,9},{11,10... | collective-permute-start | bytes 99848 | tf_op jit(solution)/shard_map/ppermute | solution.py:15
  53.2 1.0 copy-start.3
  54.2 1.0 copy-start.2
  59.7 14.0 %collective-permute-start.9 = (bf16[128,2048]{1,0:T(8,128)(2,1)S(1)}, bf16[128,2048]{1,0:T(8,128)(2,1)S(1)}, u32[]{:S(2)}, u32[]{:S(2)}) collective-permute-start(bf16[128,2048]{1,0:T(8,128)(2,1)S(1)} %fusion.9), channel_id=1, source_target_pairs={{0,2},{2,0},{1,3},{3,1},{4,6},{6,4},{5,7},{7,5},{8,10},{10,8},{9,1... | collective-permute-start | bytes 1572872 | tf_op jit(solution)/shard_map/ppermute | solution.py:106
  113.4 1.3 %slice-start = ((f32[295040]{0:T(1024)}), f32[294912]{0:T(1024)S(1)}, s32[]{:S(2)}) async-start(f32[295040]{0:T(1024)} %all-reduce.2.cloned.1.call-done), calls=%async_computation.1 | async-start | bytes 2359296 | tf_op jit(solution)/shard_map/slice | solution.py:93
  115.1 1.7 %copy-start = (f32[295040]{0:T(1024)S(1)}, f32[295040]{0:T(1024)}, u32[]{:S(2)}) copy-start(f32[295040]{0:T(1024)} %all-reduce.2.cloned.1.call-done) | copy-start | bytes 3540484
Sparse Core Ops, SparseCore 0:
  53.0 60.3 all-reduce.1

commit v2 on v1

--- a/solution.py
+++ b/solution.py
@@ -52,6 +52,45 @@
     return total
 
 
+def ring_reduce_scatter(rows, axis, send_dtype):
+    count, index = lax.axis_size(axis), lax.axis_index(axis)
+    if count == 1:
+        return rows
+    chunks = rows.reshape(count, -1, rows.shape[-1])
+    pairs = [(j, (j + 1) % count) for j in range(count)]
+    acc = lax.dynamic_index_in_dim(chunks, (index - 1) % count, keepdims=False)
+    for step in range(1, count):
+        moved = lax.ppermute(acc.astype(send_dtype), axis, pairs).astype(jnp.float32)
+        acc = moved + lax.dynamic_index_in_dim(chunks, (index - 1 - step) % count, keepdims=False)
+    return acc
+
+
+def ring_all_gather(chunk, axis, send_dtype):
+    count, index = lax.axis_size(axis), lax.axis_index(axis)
+    if count == 1:
+        return chunk
+    pairs = [(j, (j + 1) % count) for j in range(count)]
+    pieces = [chunk]
+    current = chunk.astype(send_dtype)
+    for step in range(1, count):
+        current = lax.ppermute(current, axis, pairs)
+        pieces.append(current.astype(jnp.float32))
+    stacked = jnp.stack(pieces[::-1])
+    stacked = jnp.roll(stacked, (index + 1) % count, axis=0)
+    return stacked.reshape(-1, chunk.shape[-1])
+
+
+def all_sum(flat, send_dtype):
+    parts = lax.axis_size("lat") * lax.axis_size("lon")
+    quantum = parts * 8 * 128
+    padded = jnp.pad(flat, (0, (-flat.size) % quantum)).reshape(-1, 128)
+    rows = ring_reduce_scatter(padded, "lat", send_dtype)
+    rows = ring_reduce_scatter(rows, "lon", send_dtype)
+    rows = ring_all_gather(rows, "lon", send_dtype)
+    rows = ring_all_gather(rows, "lat", send_dtype)
+    return rows.reshape(-1)[: flat.size]
+
+
 def local(inputs, cotangent, weight, bias_vector):
     own_channels, row_count, column_count = inputs.shape
     chan_count = lax.axis_size("chan")
@@ -89,7 +128,7 @@
         taps.append(jnp.stack(row_taps))
     weight_part = jnp.stack(taps)
     flat = jnp.concatenate([weight_part.reshape(-1), bias_part])
-    flat = lax.psum(flat, ("lon", "lat"))
+    flat = all_sum(flat, jnp.float32)
     weight_local = flat[: weight_part.size].reshape(weight_part.shape)
     bias_grad = flat[weight_part.size :]
     doubled = jnp.concatenate([weight_local, weight_local], axis=3)

time: 124 us -> 101 us (0.81)
  between operations: 14.5 us -> 1.27 us
  waiting for transfers between devices: 64.2 us -> 56.2 us
  local copies, waits for them, and re-layouts: 10.7 us -> 8.27 us
  starting transfers between devices: 13.8 us -> 15.4 us
    ppermute x0 -> x8, waiting for transfers between devices: none -> 40.7 us  [the longest x4 20.5 us: ring_all_gather(): current = lax.ppermute(current, axis, pairs)]
    psum x1 -> x0, waiting for transfers between devices: 38.5 us -> none  [local(): flat = lax.psum(flat, ('lon', 'lat'))]
    ppermute x1, waiting for transfers between devices: 11.6 us -> 0.01 us  [local(): received.append(lax.ppermute(part.astype(jnp.bfloat16), 'chan', pairs))]
    ppermute x0 -> x8, starting transfers between devices: none -> 1.57 us  [the longest x4 1.44 us: ring_reduce_scatter(): lax.ppermute(acc.astype(send_dtype), axis, pairs).astype(jnp.float32)]
    unnamed x15 -> x20, local copies, waits for them, and re-layouts: 4.54 us -> 3.23 us
  transfers between devices with their start and end apart: 11 -> 18, of which waited for: 7 -> 14; matrix products, arithmetic and copies ran while one was open for 11% -> 12% of each run, Pallas kernels for 0% -> 0%
where the time goes in v2:
time: 101 us
  waiting for transfers between devices  56.2 us (56%)
  starting transfers between devices  15.4 us (15%)
  matrix products  15.1 us (15%)
  local copies, waits for them, and re-layouts  8.27 us (8%)
  other arithmetic  5.11 us (5%)
  between operations  1.27 us (1%)
    ppermute x4, waiting for transfers between devices, ring_all_gather(): current = lax.ppermute(current, axis, pairs)  20.5 us
    ppermute x4, waiting for transfers between devices, ring_reduce_scatter(): lax.ppermute(acc.astype(send_dtype), axis, pairs).astype(jnp.float32)  20.3 us
    dot_general x36, matrix products, conv_taps(): jnp.dot(kernel[tap_row, tap_col], window, preferred_element_type=jnp.floa...  12.3 us
    ppermute x1, waiting for transfers between devices, local(): blocks.append(lax.ppermute(input_pad, 'chan', pairs))  12 us
    ppermute x4, starting transfers between devices, padded_2(): after = lax.ppermute(initial, axis, down)  5.64 us
    ppermute x4, starting transfers between devices, padded_2(): before = lax.ppermute(last, axis, up)  4.76 us
    unnamed x20, local copies, waits for them, and re-layouts  3.23 us
    ppermute x4, waiting for transfers between devices, padded_2(): before = lax.ppermute(last, axis, up)  3.11 us
  transfers between devices with their start and end apart: 18, of which 14 were waited for; matrix products, arithmetic and copies ran while one was open for 12% of the time, Pallas kernels for 0%

profile of v2, /device:TPU:0, one launch (start us, length us, event | category | flops | bytes accessed | tf_op | source)
XLA Modules:
  0.0 101.3 jit_solution(12449575928214546529)
XLA Ops:
  0.7 1.6 %copy.7 = bf16[128,16,128]{0,2,1:T(8,128)(2,1)S(1)} copy(bf16[128,16,128]{2,1,0:T(8,128)(2,1)} %param.4) | data formatting | bytes 1048576 | tf_op args[0]
  2.2 3.1 %collective-permute-start = (bf16[128,16,1]{0,2,1:T(2,128)(2,1)S(1)}, bf16[128,16,1]{0,2,1:T(2,128)(2,1)S(1)}, u32[]{:S(2)}, u32[]{:S(2)}) collective-permute-start(bf16[128,16,1]{0,2,1:T(2,128)(2,1)S(1)} %get-tuple-element.47), channel_id=1, source_target_pairs={{0,4},{4,8},{8,12},{12,0},{1,5},{5,9},{9,13},{13,1},{2,6},{6,10},{... | collective-permute-start | bytes 12296 | tf_op jit(solution)/shard_map/ppermute | solution.py:14
  5.3 2.1 %collective-permute-start.1 = (bf16[128,16,1]{0,2,1:T(2,128)(2,1)S(1)}, bf16[128,16,1]{0,2,1:T(2,128)(2,1)S(1)}, u32[]{:S(2)}, u32[]{:S(2)}) collective-permute-start(bf16[128,16,1]{0,2,1:T(2,128)(2,1)S(1)} %get-tuple-element.48), channel_id=1, source_target_pairs={{4,0},{8,4},{12,8},{0,12},{5,1},{9,5},{13,9},{1,13},{6,2},{10,6},{... | collective-permute-start | bytes 12296 | tf_op jit(solution)/shard_map/ppermute | solution.py:15
  7.5 0.9 dynamic-slice_bitcast_fusion.2
  8.5 0.6 collective-permute-done
  9.2 0.5 collective-permute-start.3
  9.7 0.7 collective-permute-done.2
  10.8 0.9 fusion.60
  11.8 1.7 %collective-permute-start.4 = (bf16[128,18,130]{0,2,1:T(8,128)(2,1)S(1)}, bf16[128,18,130]{0,2,1:T(8,128)(2,1)S(1)}, u32[]{:S(2)}, u32[]{:S(2)}) collective-permute-start(bf16[128,18,130]{0,2,1:T(8,128)(2,1)S(1)} %maximum_select_fusion), channel_id=1, source_target_pairs={{0,2},{2,0},{1,3},{3,1},{4,6},{6,4},{5,7},{7,5},{8,10},{10,8},{9,1... | collective-permute-start | bytes 1797128 | tf_op jit(solution)/shard_map/ppermute | solution.py:102
  16.2 12.0 %collective-permute-done.4 = bf16[128,18,130]{0,2,1:T(8,128)(2,1)S(1)} collective-permute-done((bf16[128,18,130]{0,2,1:T(8,128)(2,1)S(1)}, bf16[128,18,130]{0,2,1:T(8,128)(2,1)S(1)}, u32[]{:S(2)}, u32[]{:S(2)}) %collective-permute-start.4) | collective-permute-done | bytes 599072 | tf_op jit(solution)/shard_map/ppermute | solution.py:102
  28.2 0.9 fusion.59
  31.6 1.4 %convert_reduce_fusion = (f32[128]{0:T(128)S(1)}, bf16[128,2048]{1,0:T(8,128)(2,1)S(1)}) fusion(f32[128]{0:T(128)S(1)} %copy-done.4, f32[128,2048]{1,0:T(8,128)S(1)} %convolution_add_fusion.17, f32[128,2048]{1,0:T(8,128)S(1)} %fusion.30, f32[128,2048]{1,0:T(8,128)S(1)} %fusion.31, f32[128,2048]{1,0:T(8,128)S(1)} %fusion.32, f32[128,2048]{1,0:T(8,128)S(1)} %fusion.33, ...), kind=kOutput, calls=%fused_computation.89 | convolution fusion | flops 72875904 | bytes 11568132 | tf_op jit(solution)/shard_map/dot_general | solution.py:50
  33.3 2.5 %fusion.21 = (bf16[256,16,128]{0,2,1:T(8,128)(2,1)S(1)}, bf16[256,16,128]{0,2,1:T(8,128)(2,1)S(1)}, bf16[256,16,128]{0,2,1:T(8,128)(2,1)S(1)}, bf16[256,16,128]{...) fusion(bf16[128,18,130]{0,2,1:T(8,128)(2,1)S(1)} %maximum_selec, ...), kind=kLoop, calls=%fused_computation.81 | loop fusion | flops 18874368 | bytes 10635264 | tf_op jit(solution)/shard_map/concatenate | solution.py:117
  38.9 0.6 copy.16
  39.6 1.5 %collective-permute-start.5 = (bf16[128,16,1]{0,2,1:T(2,128)(2,1)S(1)}, bf16[128,16,1]{0,2,1:T(2,128)(2,1)S(1)}, u32[]{:S(2)}, u32[]{:S(2)}) collective-permute-start(bf16[128,16,1]{0,2,1:T(2,128)(2,1)S(1)} %get-tuple-element.45), channel_id=1, source_target_pairs={{0,4},{4,8},{8,12},{12,0},{1,5},{5,9},{9,13},{13,1},{2,6},{6,10},{... | collective-permute-start | bytes 12296 | tf_op jit(solution)/shard_map/ppermute | solution.py:14
  41.1 2.6 %collective-permute-start.6 = (bf16[128,16,1]{0,2,1:T(2,128)(2,1)S(1)}, bf16[128,16,1]{0,2,1:T(2,128)(2,1)S(1)}, u32[]{:S(2)}, u32[]{:S(2)}) collective-permute-start(bf16[128,16,1]{0,2,1:T(2,128)(2,1)S(1)} %get-tuple-element.46), channel_id=1, source_target_pairs={{4,0},{8,4},{12,8},{0,12},{5,1},{9,5},{13,9},{1,13},{6,2},{10,6},{... | collective-permute-start | bytes 12296 | tf_op jit(solution)/shard_map/ppermute | solution.py:15
  43.8 1.3 %collective-permute-done.5 = bf16[128,16,1]{0,2,1:T(2,128)(2,1)S(1)} collective-permute-done((bf16[128,16,1]{0,2,1:T(2,128)(2,1)S(1)}, bf16[128,16,1]{0,2,1:T(2,128)(2,1)S(1)}, u32[]{:S(2)}, u32[]{:S(2)}) %collective-permute-start.5) | collective-permute-done | bytes 4128 | tf_op jit(solution)/shard_map/ppermute | solution.py:14
  45.2 0.5 collective-permute-start.8
  45.9 0.5 collective-permute-done.7
  46.9 0.9 fusion.58
  50.8 1.7 %collective-permute-start.9 = (bf16[128,2048]{1,0:T(8,128)(2,1)S(1)}, bf16[128,2048]{1,0:T(8,128)(2,1)S(1)}, u32[]{:S(2)}, u32[]{:S(2)}) collective-permute-start(bf16[128,2048]{1,0:T(8,128)(2,1)S(1)} %fusion.9), channel_id=1, source_target_pairs={{0,2},{2,0},{1,3},{3,1},{4,6},{6,4},{5,7},{7,5},{8,10},{10,8},{9,1... | collective-permute-start | bytes 1572872 | tf_op jit(solution)/shard_map/ppermute | solution.py:145
  52.6 1.2 %collective-permute-start.11 = (f32[296,128]{1,0:T(8,128)S(1)}, f32[296,128]{1,0:T(8,128)S(1)}, u32[]{:S(2)}, u32[]{:S(2)}) collective-permute-start(f32[296,128]{1,0:T(8,128)S(1)} %dynamic-slice_bitcast_fusion.3), channel_id=1, source_target_pairs={{0,4},{4,8},{8,12},{12,0},{1,5},{5,9},{9,13},{13,1},{2,6},{6,10},{... | collective-permute-start | bytes 454664 | tf_op jit(solution)/shard_map/ppermute | solution.py:63
  54.1 6.8 %collective-permute-done.11 = f32[296,128]{1,0:T(8,128)S(1)} collective-permute-done((f32[296,128]{1,0:T(8,128)S(1)}, f32[296,128]{1,0:T(8,128)S(1)}, u32[]{:S(2)}, u32[]{:S(2)}) %collective-permute-start.11) | collective-permute-done | bytes 151584 | tf_op jit(solution)/shard_map/ppermute | solution.py:63
  61.3 6.8 %collective-permute-done.12 = f32[296,128]{1,0:T(8,128)S(1)} collective-permute-done((f32[296,128]{1,0:T(8,128)S(1)}, f32[296,128]{1,0:T(8,128)S(1)}, u32[]{:S(2)}, u32[]{:S(2)}) %collective-permute-start.12) | collective-permute-done | bytes 151584 | tf_op jit(solution)/shard_map/ppermute | solution.py:63
  68.5 6.6 %collective-permute-done.13 = f32[296,128]{1,0:T(8,128)S(1)} collective-permute-done((f32[296,128]{1,0:T(8,128)S(1)}, f32[296,128]{1,0:T(8,128)S(1)}, u32[]{:S(2)}, u32[]{:S(2)}) %collective-permute-start.13) | collective-permute-done | bytes 151584 | tf_op jit(solution)/shard_map/ppermute | solution.py:63
  75.6 6.6 %collective-permute-done.14 = f32[296,128]{1,0:T(8,128)S(1)} collective-permute-done((f32[296,128]{1,0:T(8,128)S(1)}, f32[296,128]{1,0:T(8,128)S(1)}, u32[]{:S(2)}, u32[]{:S(2)}) %collective-permute-start.14) | collective-permute-done | bytes 151584 | tf_op jit(solution)/shard_map/ppermute | solution.py:76
  82.6 7.0 %collective-permute-done.15 = f32[296,128]{1,0:T(8,128)S(1)} collective-permute-done((f32[296,128]{1,0:T(8,128)S(1)}, f32[296,128]{1,0:T(8,128)S(1)}, u32[]{:S(2)}, u32[]{:S(2)}) %collective-permute-start.15) | collective-permute-done | bytes 151584 | tf_op jit(solution)/shard_map/ppermute | solution.py:76
  90.0 6.7 %collective-permute-done.16 = f32[296,128]{1,0:T(8,128)S(1)} collective-permute-done((f32[296,128]{1,0:T(8,128)S(1)}, f32[296,128]{1,0:T(8,128)S(1)}, u32[]{:S(2)}, u32[]{:S(2)}) %collective-permute-start.16) | collective-permute-done | bytes 151584 | tf_op jit(solution)/shard_map/ppermute | solution.py:76
  97.9 0.9 copy.15
  99.3 0.5 slice.406
  99.8 0.3 reshape.195
  100.1 1.2 %fusion.13 = f32[3,3,128,256]{3,2,1,0:T(8,128)} fusion(s32[]{:T(128)S(6)} %select_n.130, f32[3,3,128,256]{3,2,1,0:T(8,128)S(1)} %reshape.195), kind=kLoop, calls=%fused_computation.63 | loop fusion | flops 294912 | bytes 2359300 | tf_op jit(solution)/shard_map/concatenate | solution.py:134
  (100 shorter events, 16.8 us)
Async XLA Ops:
  0.6 6.8 %copy-start.3 = (bf16[128,16,128]{2,1,0:T(8,128)(2,1)S(1)}, bf16[128,16,128]{2,1,0:T(8,128)(2,1)}, u32[]{:S(2)}) copy-start(bf16[128,16,128]{2,1,0:T(8,128)(2,1)} %param.5) | copy-start | bytes 1572868
  0.6 6.9 %copy-start = (bf16[3,3,128,256]{3,2,1,0:T(8,128)(2,1)S(1)}, bf16[3,3,128,256]{3,2,1,0:T(8,128)(2,1)}, u32[]{:S(2)}) copy-start(bf16[3,3,128,256]{3,2,1,0:T(8,128)(2,1)} %param.6) | copy-start | bytes 1769476
  2.2 6.8 %collective-permute-start = (bf16[128,16,1]{0,2,1:T(2,128)(2,1)S(1)}, bf16[128,16,1]{0,2,1:T(2,128)(2,1)S(1)}, u32[]{:S(2)}, u32[]{:S(2)}) collective-permute-start(bf16[128,16,1]{0,2,1:T(2,128)(2,1)S(1)} %get-tuple-element.47), channel_id=1, source_target_pairs={{0,4},{4,8},{8,12},{12,0},{1,5},{5,9},{9,13},{13,1},{2,6},{6,10},{... | collective-permute-start | bytes 12296 | tf_op jit(solution)/shard_map/ppermute | solution.py:14
  5.3 3.7 %collective-permute-start.1 = (bf16[128,16,1]{0,2,1:T(2,128)(2,1)S(1)}, bf16[128,16,1]{0,2,1:T(2,128)(2,1)S(1)}, u32[]{:S(2)}, u32[]{:S(2)}) collective-permute-start(bf16[128,16,1]{0,2,1:T(2,128)(2,1)S(1)} %get-tuple-element.48), channel_id=1, source_target_pairs={{4,0},{8,4},{12,8},{0,12},{5,1},{9,5},{13,9},{1,13},{6,2},{10,6},{... | collective-permute-start | bytes 12296 | tf_op jit(solution)/shard_map/ppermute | solution.py:15
  9.1 1.3 %collective-permute-start.2 = (bf16[128,1,130]{0,2,1:T(8,128)(2,1)S(1)}, bf16[128,1,130]{0,2,1:T(8,128)(2,1)S(1)}, u32[]{:S(2)}, u32[]{:S(2)}) collective-permute-start(bf16[128,1,130]{0,2,1:T(8,128)(2,1)S(1)} %get-tuple-element.43), channel_id=1, source_target_pairs={{0,1},{1,0},{2,3},{3,2},{4,5},{5,4},{6,7},{7,6},{8,9},{9,8},{10,11... | collective-permute-start | bytes 99848 | tf_op jit(solution)/shard_map/ppermute | solution.py:14
  9.2 1.4 %collective-permute-start.3 = (bf16[128,1,130]{0,2,1:T(8,128)(2,1)S(1)}, bf16[128,1,130]{0,2,1:T(8,128)(2,1)S(1)}, u32[]{:S(2)}, u32[]{:S(2)}) collective-permute-start(bf16[128,1,130]{0,2,1:T(8,128)(2,1)S(1)} %get-tuple-element.44), channel_id=1, source_target_pairs={{1,0},{0,1},{3,2},{2,3},{5,4},{4,5},{7,6},{6,7},{9,8},{8,9},{11,10... | collective-permute-start | bytes 99848 | tf_op jit(solution)/shard_map/ppermute | solution.py:15
  11.8 16.4 %collective-permute-start.4 = (bf16[128,18,130]{0,2,1:T(8,128)(2,1)S(1)}, bf16[128,18,130]{0,2,1:T(8,128)(2,1)S(1)}, u32[]{:S(2)}, u32[]{:S(2)}) collective-permute-start(bf16[128,18,130]{0,2,1:T(8,128)(2,1)S(1)} %maximum_select_fusion), channel_id=1, source_target_pairs={{0,2},{2,0},{1,3},{3,1},{4,6},{6,4},{5,7},{7,5},{8,10},{10,8},{9,1... | collective-permute-start | bytes 1797128 | tf_op jit(solution)/shard_map/ppermute | solution.py:102
  31.0 0.7 copy-start.4
  39.6 5.5 %collective-permute-start.5 = (bf16[128,16,1]{0,2,1:T(2,128)(2,1)S(1)}, bf16[128,16,1]{0,2,1:T(2,128)(2,1)S(1)}, u32[]{:S(2)}, u32[]{:S(2)}) collective-permute-start(bf16[128,16,1]{0,2,1:T(2,128)(2,1)S(1)} %get-tuple-element.45), channel_id=1, source_target_pairs={{0,4},{4,8},{8,12},{12,0},{1,5},{5,9},{9,13},{13,1},{2,6},{6,10},{... | collective-permute-start | bytes 12296 | tf_op jit(solution)/shard_map/ppermute | solution.py:14
  41.1 4.0 %collective-permute-start.6 = (bf16[128,16,1]{0,2,1:T(2,128)(2,1)S(1)}, bf16[128,16,1]{0,2,1:T(2,128)(2,1)S(1)}, u32[]{:S(2)}, u32[]{:S(2)}) collective-permute-start(bf16[128,16,1]{0,2,1:T(2,128)(2,1)S(1)} %get-tuple-element.46), channel_id=1, source_target_pairs={{4,0},{8,4},{12,8},{0,12},{5,1},{9,5},{13,9},{1,13},{6,2},{10,6},{... | collective-permute-start | bytes 12296 | tf_op jit(solution)/shard_map/ppermute | solution.py:15
  45.1 1.3 %collective-permute-start.7 = (bf16[128,1,130]{0,2,1:T(8,128)(2,1)S(1)}, bf16[128,1,130]{0,2,1:T(8,128)(2,1)S(1)}, u32[]{:S(2)}, u32[]{:S(2)}) collective-permute-start(bf16[128,1,130]{0,2,1:T(8,128)(2,1)S(1)} %get-tuple-element.41), channel_id=1, source_target_pairs={{0,1},{1,0},{2,3},{3,2},{4,5},{5,4},{6,7},{7,6},{8,9},{9,8},{10,11... | collective-permute-start | bytes 99848 | tf_op jit(solution)/shard_map/ppermute | solution.py:14
  45.2 1.4 %collective-permute-start.8 = (bf16[128,1,130]{0,2,1:T(8,128)(2,1)S(1)}, bf16[128,1,130]{0,2,1:T(8,128)(2,1)S(1)}, u32[]{:S(2)}, u32[]{:S(2)}) collective-permute-start(bf16[128,1,130]{0,2,1:T(8,128)(2,1)S(1)} %get-tuple-element.42), channel_id=1, source_target_pairs={{1,0},{0,1},{3,2},{2,3},{5,4},{4,5},{7,6},{6,7},{9,8},{8,9},{11,10... | collective-permute-start | bytes 99848 | tf_op jit(solution)/shard_map/ppermute | solution.py:15
  45.7 6.8 %collective-permute-start.10 = (f32[1184,128]{1,0:T(8,128)S(1)}, f32[1184,128]{1,0:T(8,128)S(1)}, u32[]{:S(2)}, u32[]{:S(2)}) collective-permute-start(f32[1184,128]{1,0:T(8,128)S(1)} %dynamic-slice_bitcast_fusion), channel_id=1, source_target_pairs={{0,1},{1,0},{2,3},{3,2},{4,5},{5,4},{6,7},{7,6},{8,9},{9,8},{10,11... | collective-permute-start | bytes 1818632 | tf_op jit(solution)/shard_map/ppermute | solution.py:63
  46.9 1.0 copy-start.1
  50.8 3.0 %copy-start.2 = (bf16[3,3,128,128]{2,3,1,0:T(8,128)(2,1)S(1)}, bf16[3,3,128,128]{2,3,1,0:T(8,128)(2,1)}, u32[]{:S(2)}) copy-start(bf16[3,3,128,128]{2,3,1,0:T(8,128)(2,1)} %get-tuple-element.39) | copy-start | bytes 884740
  50.8 46.8 %collective-permute-start.9 = (bf16[128,2048]{1,0:T(8,128)(2,1)S(1)}, bf16[128,2048]{1,0:T(8,128)(2,1)S(1)}, u32[]{:S(2)}, u32[]{:S(2)}) collective-permute-start(bf16[128,2048]{1,0:T(8,128)(2,1)S(1)} %fusion.9), channel_id=1, source_target_pairs={{0,2},{2,0},{1,3},{3,1},{4,6},{6,4},{5,7},{7,5},{8,10},{10,8},{9,1... | collective-permute-start | bytes 1572872 | tf_op jit(solution)/shard_map/ppermute | solution.py:145
  52.6 8.3 %collective-permute-start.11 = (f32[296,128]{1,0:T(8,128)S(1)}, f32[296,128]{1,0:T(8,128)S(1)}, u32[]{:S(2)}, u32[]{:S(2)}) collective-permute-start(f32[296,128]{1,0:T(8,128)S(1)} %dynamic-slice_bitcast_fusion.3), channel_id=1, source_target_pairs={{0,4},{4,8},{8,12},{12,0},{1,5},{5,9},{9,13},{13,1},{2,6},{6,10},{... | collective-permute-start | bytes 454664 | tf_op jit(solution)/shard_map/ppermute | solution.py:63
  60.9 7.2 %collective-permute-start.12 = (f32[296,128]{1,0:T(8,128)S(1)}, f32[296,128]{1,0:T(8,128)S(1)}, u32[]{:S(2)}, u32[]{:S(2)}) collective-permute-start(f32[296,128]{1,0:T(8,128)S(1)} %bitcast_add_fusion.3), channel_id=1, source_target_pairs={{0,4},{4,8},{8,12},{12,0},{1,5},{5,9},{9,13},{13,1},{2,6},{6,10},{... | collective-permute-start | bytes 454664 | tf_op jit(solution)/shard_map/ppermute | solution.py:63
  68.2 7.0 %collective-permute-start.13 = (f32[296,128]{1,0:T(8,128)S(1)}, f32[296,128]{1,0:T(8,128)S(1)}, u32[]{:S(2)}, u32[]{:S(2)}) collective-permute-start(f32[296,128]{1,0:T(8,128)S(1)} %bitcast_add_fusion.2), channel_id=1, source_target_pairs={{0,4},{4,8},{8,12},{12,0},{1,5},{5,9},{9,13},{13,1},{2,6},{6,10},{... | collective-permute-start | bytes 454664 | tf_op jit(solution)/shard_map/ppermute | solution.py:63
  75.2 7.0 %collective-permute-start.14 = (f32[296,128]{1,0:T(8,128)S(1)}, f32[296,128]{1,0:T(8,128)S(1)}, u32[]{:S(2)}, u32[]{:S(2)}) collective-permute-start(f32[296,128]{1,0:T(8,128)S(1)} %bitcast_add_fusion.1), channel_id=1, source_target_pairs={{0,4},{4,8},{8,12},{12,0},{1,5},{5,9},{9,13},{13,1},{2,6},{6,10},{... | collective-permute-start | bytes 454664 | tf_op jit(solution)/shard_map/ppermute | solution.py:76
  82.3 7.4 %collective-permute-start.15 = (f32[296,128]{1,0:T(8,128)S(1)}, f32[296,128]{1,0:T(8,128)S(1)}, u32[]{:S(2)}, u32[]{:S(2)}) collective-permute-start(f32[296,128]{1,0:T(8,128)S(1)} %collective-permute-done.14), channel_id=1, source_target_pairs={{0,4},{4,8},{8,12},{12,0},{1,5},{5,9},{9,13},{13,1},{2,6},{6,10},{... | collective-permute-start | bytes 454664 | tf_op jit(solution)/shard_map/ppermute | solution.py:76
  89.6 7.0 %collective-permute-start.16 = (f32[296,128]{1,0:T(8,128)S(1)}, f32[296,128]{1,0:T(8,128)S(1)}, u32[]{:S(2)}, u32[]{:S(2)}) collective-permute-start(f32[296,128]{1,0:T(8,128)S(1)} %collective-permute-done.15), channel_id=1, source_target_pairs={{0,4},{4,8},{8,12},{12,0},{1,5},{5,9},{9,13},{13,1},{2,6},{6,10},{... | collective-permute-start | bytes 454664 | tf_op jit(solution)/shard_map/ppermute | solution.py:76
  96.8 2.1 %collective-permute-start.17 = (f32[1184,128]{1,0:T(8,128)S(1)}, f32[1184,128]{1,0:T(8,128)S(1)}, u32[]{:S(2)}, u32[]{:S(2)}) collective-permute-start(f32[1184,128]{1,0:T(8,128)S(1)} %bitcast.307), channel_id=1, source_target_pairs={{0,1},{1,0},{2,3},{3,2},{4,5},{5,4},{6,7},{7,6},{8,9},{9,8},{10,11... | collective-permute-start | bytes 1818632 | tf_op jit(solution)/shard_map/ppermute | solution.py:76

commit v3 on v2

--- a/solution.py
+++ b/solution.py
@@ -52,29 +52,28 @@
     return total
 
 
-def ring_reduce_scatter(rows, axis, send_dtype):
+def direct_reduce_scatter(rows, axis, send_dtype):
     count, index = lax.axis_size(axis), lax.axis_index(axis)
     if count == 1:
         return rows
     chunks = rows.reshape(count, -1, rows.shape[-1])
-    pairs = [(j, (j + 1) % count) for j in range(count)]
-    acc = lax.dynamic_index_in_dim(chunks, (index - 1) % count, keepdims=False)
+    acc = lax.dynamic_index_in_dim(chunks, index, keepdims=False)
     for step in range(1, count):
-        moved = lax.ppermute(acc.astype(send_dtype), axis, pairs).astype(jnp.float32)
-        acc = moved + lax.dynamic_index_in_dim(chunks, (index - 1 - step) % count, keepdims=False)
+        pairs = [(j, (j + step) % count) for j in range(count)]
+        piece = lax.dynamic_index_in_dim(chunks, (index + step) % count, keepdims=False)
+        acc = acc + lax.ppermute(piece.astype(send_dtype), axis, pairs).astype(jnp.float32)
     return acc
 
 
-def ring_all_gather(chunk, axis, send_dtype):
+def direct_all_gather(chunk, axis, send_dtype):
     count, index = lax.axis_size(axis), lax.axis_index(axis)
     if count == 1:
         return chunk
-    pairs = [(j, (j + 1) % count) for j in range(count)]
     pieces = [chunk]
-    current = chunk.astype(send_dtype)
+    sent = chunk.astype(send_dtype)
     for step in range(1, count):
-        current = lax.ppermute(current, axis, pairs)
-        pieces.append(current.astype(jnp.float32))
+        pairs = [(j, (j + step) % count) for j in range(count)]
+        pieces.append(lax.ppermute(sent, axis, pairs).astype(jnp.float32))
     stacked = jnp.stack(pieces[::-1])
     stacked = jnp.roll(stacked, (index + 1) % count, axis=0)
     return stacked.reshape(-1, chunk.shape[-1])
@@ -84,10 +83,10 @@
     parts = lax.axis_size("lat") * lax.axis_size("lon")
     quantum = parts * 8 * 128
     padded = jnp.pad(flat, (0, (-flat.size) % quantum)).reshape(-1, 128)
-    rows = ring_reduce_scatter(padded, "lat", send_dtype)
-    rows = ring_reduce_scatter(rows, "lon", send_dtype)
-    rows = ring_all_gather(rows, "lon", send_dtype)
-    rows = ring_all_gather(rows, "lat", send_dtype)
+    rows = direct_reduce_scatter(padded, "lat", jnp.float32)
+    rows = direct_reduce_scatter(rows, "lon", send_dtype)
+    rows = direct_all_gather(rows, "lon", send_dtype)
+    rows = direct_all_gather(rows, "lat", jnp.float32)
     return rows.reshape(-1)[: flat.size]
 
 
@@ -128,7 +127,7 @@
         taps.append(jnp.stack(row_taps))
     weight_part = jnp.stack(taps)
     flat = jnp.concatenate([weight_part.reshape(-1), bias_part])
-    flat = all_sum(flat, jnp.float32)
+    flat = all_sum(flat, jnp.bfloat16)
     weight_local = flat[: weight_part.size].reshape(weight_part.shape)
     bias_grad = flat[weight_part.size :]
     doubled = jnp.concatenate([weight_local, weight_local], axis=3)

time: 101 us -> 82.1 us (0.81)
  waiting for transfers between devices: 56.2 us -> 28.6 us
  starting transfers between devices: 15.4 us -> 22.9 us
    ppermute x8, waiting for transfers between devices: 40.7 us -> 10.8 us  [the longest x4 6.14 us: direct_all_gather(): pieces.append(lax.ppermute(sent, axis, pairs).astype(jnp.float32))]
    ppermute x8, starting transfers between devices: 1.57 us -> 9.11 us  [the longest x4 5.69 us: direct_reduce_scatter(): lax.ppermute(piece.astype(send_dtype), axis, pairs).astype(jnp.float32)]
    ppermute x1, waiting for transfers between devices: 0.01 us -> 2.35 us  [local(): received.append(lax.ppermute(part.astype(jnp.bfloat16), 'chan', pairs))]
    unnamed x20 -> x14, local copies, waits for them, and re-layouts: 3.23 us -> 3.77 us
  transfers between devices with their start and end apart: 18 -> 18, of which waited for: 14 -> 13; matrix products, arithmetic and copies ran while one was open for 12% -> 15% of each run, Pallas kernels for 0% -> 0%
where the time goes in v3:
time: 82.1 us; the launch traced here: 81.9 us
  waiting for transfers between devices  28.6 us (35%)
  starting transfers between devices  22.9 us (28%)
  matrix products  15.1 us (18%)
  local copies, waits for them, and re-layouts  8.83 us (11%)
  other arithmetic  5.18 us (6%)
  between operations  1.24 us (2%)
    dot_general x36, matrix products, conv_taps(): jnp.dot(kernel[tap_row, tap_col], window, preferred_element_type=jnp.floa...  12.3 us
    ppermute x1, waiting for transfers between devices, local(): blocks.append(lax.ppermute(input_pad, 'chan', pairs))  12 us
    ppermute x4, waiting for transfers between devices, direct_all_gather(): pieces.append(lax.ppermute(sent, axis, pairs).astype(jnp.float32))  6.14 us
    ppermute x4, starting transfers between devices, direct_reduce_scatter(): lax.ppermute(piece.astype(send_dtype), axis, pairs).astype(jnp.float32)  5.69 us
    ppermute x4, starting transfers between devices, padded_2(): after = lax.ppermute(initial, axis, down)  5.64 us
    ppermute x4, starting transfers between devices, padded_2(): before = lax.ppermute(last, axis, up)  4.76 us
    ppermute x4, waiting for transfers between devices, direct_reduce_scatter(): lax.ppermute(piece.astype(send_dtype), axis, pairs).astype(jnp.float32)  4.69 us
    unnamed x14, local copies, waits for them, and re-layouts  3.77 us
  transfers between devices with their start and end apart: 18, of which 13 were waited for; matrix products, arithmetic and copies ran while one was open for 15% of the time, Pallas kernels for 0%

profile of v3, /device:TPU:0, one launch (start us, length us, event | category | flops | bytes accessed | tf_op | source)
XLA Modules:
  0.0 81.9 jit_solution(13868051946673434037)
XLA Ops:
  0.7 1.6 %copy.7 = bf16[128,16,128]{0,2,1:T(8,128)(2,1)S(1)} copy(bf16[128,16,128]{2,1,0:T(8,128)(2,1)} %param.4) | data formatting | bytes 1048576 | tf_op args[0]
  2.2 3.1 %collective-permute-start = (bf16[128,16,1]{0,2,1:T(2,128)(2,1)S(1)}, bf16[128,16,1]{0,2,1:T(2,128)(2,1)S(1)}, u32[]{:S(2)}, u32[]{:S(2)}) collective-permute-start(bf16[128,16,1]{0,2,1:T(2,128)(2,1)S(1)} %get-tuple-element.52), channel_id=1, source_target_pairs={{0,4},{4,8},{8,12},{12,0},{1,5},{5,9},{9,13},{13,1},{2,6},{6,10},{... | collective-permute-start | bytes 12296 | tf_op jit(solution)/shard_map/ppermute | solution.py:14
  5.3 2.1 %collective-permute-start.1 = (bf16[128,16,1]{0,2,1:T(2,128)(2,1)S(1)}, bf16[128,16,1]{0,2,1:T(2,128)(2,1)S(1)}, u32[]{:S(2)}, u32[]{:S(2)}) collective-permute-start(bf16[128,16,1]{0,2,1:T(2,128)(2,1)S(1)} %get-tuple-element.53), channel_id=1, source_target_pairs={{4,0},{8,4},{12,8},{0,12},{5,1},{9,5},{13,9},{1,13},{6,2},{10,6},{... | collective-permute-start | bytes 12296 | tf_op jit(solution)/shard_map/ppermute | solution.py:15
  7.5 0.9 %dynamic-slice_bitcast_fusion.2 = (bf16[3,3,128,128]{2,3,1,0:T(8,128)(2,1)}, bf16[3,3,128,128]{2,3,1,0:T(8,128)(2,1)}) fusion(bf16[3,3,128,256]{3,2,1,0:T(8,128)(2,1)S(1)} %copy-done, s32[]{:T(128)S(6)} %select_n.94, s32[]{:T(128)S(6)} %select_n.97), kind=kLoop, calls=%fused_computation.100 | loop fusion | bytes 1179656 | tf_op jit(solution)/shard_map/transpose | solution.py:145
  8.5 0.6 collective-permute-done
  9.7 0.7 collective-permute-done.2
  10.8 0.9 %fusion.67 = (bf16[128,16,128]{0,2,1:T(8,128)(2,1)S(1)}, bf16[128,16,128]{0,2,1:T(8,128)(2,1)S(1)}, bf16[128,16,128]{0,2,1:T(8,128)(2,1)S(1)}, bf16[128,16,128]{...) fusion(bf16[128,18,130]{0,2,1:T(8,128)(2,1)S(1)} %maximum_selec, ...), kind=kLoop, calls=%fused_computation.194 | loop fusion | bytes 9437184 | tf_op jit(solution)/shard_map/slice | solution.py:37
  11.8 1.7 %collective-permute-start.4 = (bf16[128,18,130]{0,2,1:T(8,128)(2,1)S(1)}, bf16[128,18,130]{0,2,1:T(8,128)(2,1)S(1)}, u32[]{:S(2)}, u32[]{:S(2)}) collective-permute-start(bf16[128,18,130]{0,2,1:T(8,128)(2,1)S(1)} %maximum_select_fusion), channel_id=1, source_target_pairs={{0,2},{2,0},{1,3},{3,1},{4,6},{6,4},{5,7},{7,5},{8,10},{10,8},{9,1... | collective-permute-start | bytes 1797128 | tf_op jit(solution)/shard_map/ppermute | solution.py:101
  16.2 12.0 %collective-permute-done.4 = bf16[128,18,130]{0,2,1:T(8,128)(2,1)S(1)} collective-permute-done((bf16[128,18,130]{0,2,1:T(8,128)(2,1)S(1)}, bf16[128,18,130]{0,2,1:T(8,128)(2,1)S(1)}, u32[]{:S(2)}, u32[]{:S(2)}) %collective-permute-start.4) | collective-permute-done | bytes 599072 | tf_op jit(solution)/shard_map/ppermute | solution.py:101
  28.2 0.9 %fusion.66 = (bf16[128,16,128]{0,2,1:T(8,128)(2,1)S(1)}, bf16[128,16,128]{0,2,1:T(8,128)(2,1)S(1)}, bf16[128,16,128]{0,2,1:T(8,128)(2,1)S(1)}, bf16[128,16,128]{...) fusion(bf16[128,18,130]{0,2,1:T(8,128)(2,1)S(1)} %collective-pe, ...), kind=kLoop, calls=%fused_computation.193 | loop fusion | bytes 9437184 | tf_op jit(solution)/shard_map/slice | solution.py:37
  31.6 1.4 %convert_reduce_fusion = (f32[128]{0:T(128)S(1)}, bf16[128,2048]{1,0:T(8,128)(2,1)S(1)}) fusion(f32[128]{0:T(128)S(1)} %copy-done.4, f32[128,2048]{1,0:T(8,128)S(1)} %convolution_add_fusion.17, f32[128,2048]{1,0:T(8,128)S(1)} %fusion.35, f32[128,2048]{1,0:T(8,128)S(1)} %fusion.36, f32[128,2048]{1,0:T(8,128)S(1)} %fusion.37, f32[128,2048]{1,0:T(8,128)S(1)} %fusion.38, ...), kind=kOutput, calls=%fused_computation.89 | convolution fusion | flops 72875904 | bytes 11568132 | tf_op jit(solution)/shard_map/dot_general | solution.py:50
  33.3 2.5 %fusion.21 = (bf16[256,16,128]{0,2,1:T(8,128)(2,1)S(1)}, bf16[256,16,128]{0,2,1:T(8,128)(2,1)S(1)}, bf16[256,16,128]{0,2,1:T(8,128)(2,1)S(1)}, bf16[256,16,128]{...) fusion(bf16[128,18,130]{0,2,1:T(8,128)(2,1)S(1)} %maximum_selec, ...), kind=kLoop, calls=%fused_computation.81 | loop fusion | flops 18874368 | bytes 10635264 | tf_op jit(solution)/shard_map/concatenate | solution.py:116
  38.9 0.6 copy.16
  39.6 1.5 %collective-permute-start.5 = (bf16[128,16,1]{0,2,1:T(2,128)(2,1)S(1)}, bf16[128,16,1]{0,2,1:T(2,128)(2,1)S(1)}, u32[]{:S(2)}, u32[]{:S(2)}) collective-permute-start(bf16[128,16,1]{0,2,1:T(2,128)(2,1)S(1)} %get-tuple-element.50), channel_id=1, source_target_pairs={{0,4},{4,8},{8,12},{12,0},{1,5},{5,9},{9,13},{13,1},{2,6},{6,10},{... | collective-permute-start | bytes 12296 | tf_op jit(solution)/shard_map/ppermute | solution.py:14
  41.1 2.6 %collective-permute-start.6 = (bf16[128,16,1]{0,2,1:T(2,128)(2,1)S(1)}, bf16[128,16,1]{0,2,1:T(2,128)(2,1)S(1)}, u32[]{:S(2)}, u32[]{:S(2)}) collective-permute-start(bf16[128,16,1]{0,2,1:T(2,128)(2,1)S(1)} %get-tuple-element.51), channel_id=1, source_target_pairs={{4,0},{8,4},{12,8},{0,12},{5,1},{9,5},{13,9},{1,13},{6,2},{10,6},{... | collective-permute-start | bytes 12296 | tf_op jit(solution)/shard_map/ppermute | solution.py:15
  43.8 1.3 %collective-permute-done.5 = bf16[128,16,1]{0,2,1:T(2,128)(2,1)S(1)} collective-permute-done((bf16[128,16,1]{0,2,1:T(2,128)(2,1)S(1)}, bf16[128,16,1]{0,2,1:T(2,128)(2,1)S(1)}, u32[]{:S(2)}, u32[]{:S(2)}) %collective-permute-start.5) | collective-permute-done | bytes 4128 | tf_op jit(solution)/shard_map/ppermute | solution.py:14
  46.9 0.9 %fusion.65 = (bf16[128,16,128]{0,2,1:T(8,128)(2,1)S(1)}, bf16[128,16,128]{0,2,1:T(8,128)(2,1)S(1)}, bf16[128,16,128]{0,2,1:T(8,128)(2,1)S(1)}, bf16[128,16,128]{...) fusion(bf16[128,18,130]{0,2,1:T(8,128)(2,1)S(1)} %maximum_selec, ...), kind=kLoop, calls=%fused_computation.192 | loop fusion | bytes 9437184 | tf_op jit(solution)/shard_map/slice | solution.py:37
  48.2 0.6 copy-done.1
  52.9 1.3 %collective-permute-start.11 = (bf16[296,128]{1,0:T(8,128)(2,1)S(1)}, bf16[296,128]{1,0:T(8,128)(2,1)S(1)}, u32[]{:S(2)}, u32[]{:S(2)}) collective-permute-start(bf16[296,128]{1,0:T(8,128)(2,1)S(1)} %get-tuple-element.41), channel_id=1, source_target_pairs={{0,4},{4,8},{8,12},{12,0},{1,5},{5,9},{9,13},{13,1},{2,6},{6,10},{... | collective-permute-start | bytes 227336 | tf_op jit(solution)/shard_map/ppermute | solution.py:64
  54.2 3.3 %collective-permute-start.12 = (bf16[296,128]{1,0:T(8,128)(2,1)S(1)}, bf16[296,128]{1,0:T(8,128)(2,1)S(1)}, u32[]{:S(2)}, u32[]{:S(2)}) collective-permute-start(bf16[296,128]{1,0:T(8,128)(2,1)S(1)} %get-tuple-element.43), channel_id=1, source_target_pairs={{0,8},{4,12},{8,0},{12,4},{1,9},{5,13},{9,1},{13,5},{2,10},{6,14},... | collective-permute-start | bytes 227336 | tf_op jit(solution)/shard_map/ppermute | solution.py:64
  57.5 0.9 %collective-permute-start.13 = (bf16[296,128]{1,0:T(8,128)(2,1)S(1)}, bf16[296,128]{1,0:T(8,128)(2,1)S(1)}, u32[]{:S(2)}, u32[]{:S(2)}) collective-permute-start(bf16[296,128]{1,0:T(8,128)(2,1)S(1)} %get-tuple-element.42), channel_id=1, source_target_pairs={{0,12},{4,0},{8,4},{12,8},{1,13},{5,1},{9,5},{13,9},{2,14},{6,2},{... | collective-permute-start | bytes 227336 | tf_op jit(solution)/shard_map/ppermute | solution.py:64
  58.7 1.5 %collective-permute-done.11 = bf16[296,128]{1,0:T(8,128)(2,1)S(1)} collective-permute-done((bf16[296,128]{1,0:T(8,128)(2,1)S(1)}, bf16[296,128]{1,0:T(8,128)(2,1)S(1)}, u32[]{:S(2)}, u32[]{:S(2)}) %collective-permute-start.11) | collective-permute-done | bytes 75808 | tf_op jit(solution)/shard_map/ppermute | solution.py:64
  60.2 2.9 %collective-permute-done.12 = bf16[296,128]{1,0:T(8,128)(2,1)S(1)} collective-permute-done((bf16[296,128]{1,0:T(8,128)(2,1)S(1)}, bf16[296,128]{1,0:T(8,128)(2,1)S(1)}, u32[]{:S(2)}, u32[]{:S(2)}) %collective-permute-start.12) | collective-permute-done | bytes 75808 | tf_op jit(solution)/shard_map/ppermute | solution.py:64
  63.5 2.4 %collective-permute-start.14 = (bf16[296,128]{1,0:T(8,128)(2,1)S(1)}, bf16[296,128]{1,0:T(8,128)(2,1)S(1)}, u32[]{:S(2)}, u32[]{:S(2)}) collective-permute-start(bf16[296,128]{1,0:T(8,128)(2,1)S(1)} %get-tuple-element.3), channel_id=1, source_target_pairs={{0,12},{4,0},{8,4},{12,8},{1,13},{5,1},{9,5},{13,9},{2,14},{6,2},{... | collective-permute-start | bytes 227336 | tf_op jit(solution)/shard_map/ppermute | solution.py:76
  66.2 1.7 %collective-permute-start.9 = (bf16[128,2048]{1,0:T(8,128)(2,1)S(1)}, bf16[128,2048]{1,0:T(8,128)(2,1)S(1)}, u32[]{:S(2)}, u32[]{:S(2)}) collective-permute-start(bf16[128,2048]{1,0:T(8,128)(2,1)S(1)} %fusion.9), channel_id=1, source_target_pairs={{0,2},{2,0},{1,3},{3,1},{4,6},{6,4},{5,7},{7,5},{8,10},{10,8},{9,1... | collective-permute-start | bytes 1572872 | tf_op jit(solution)/shard_map/ppermute | solution.py:144
  68.0 0.9 %collective-permute-start.15 = (bf16[296,128]{1,0:T(8,128)(2,1)S(1)}, bf16[296,128]{1,0:T(8,128)(2,1)S(1)}, u32[]{:S(2)}, u32[]{:S(2)}) collective-permute-start(bf16[296,128]{1,0:T(8,128)(2,1)S(1)} %get-tuple-element.3), channel_id=1, source_target_pairs={{0,8},{4,12},{8,0},{12,4},{1,9},{5,13},{9,1},{13,5},{2,10},{6,14},... | collective-permute-start | bytes 227336 | tf_op jit(solution)/shard_map/ppermute | solution.py:76
  68.9 5.2 %collective-permute-done.15 = bf16[296,128]{1,0:T(8,128)(2,1)S(1)} collective-permute-done((bf16[296,128]{1,0:T(8,128)(2,1)S(1)}, bf16[296,128]{1,0:T(8,128)(2,1)S(1)}, u32[]{:S(2)}, u32[]{:S(2)}) %collective-permute-start.15) | collective-permute-done | bytes 75808 | tf_op jit(solution)/shard_map/ppermute | solution.py:76
  74.1 1.0 %collective-permute-done.16 = bf16[296,128]{1,0:T(8,128)(2,1)S(1)} collective-permute-done((bf16[296,128]{1,0:T(8,128)(2,1)S(1)}, bf16[296,128]{1,0:T(8,128)(2,1)S(1)}, u32[]{:S(2)}, u32[]{:S(2)}) %collective-permute-start.16) | collective-permute-done | bytes 75808 | tf_op jit(solution)/shard_map/ppermute | solution.py:76
  75.9 2.4 %collective-permute-done.9 = bf16[128,2048]{1,0:T(8,128)(2,1)S(1)} collective-permute-done((bf16[128,2048]{1,0:T(8,128)(2,1)S(1)}, bf16[128,2048]{1,0:T(8,128)(2,1)S(1)}, u32[]{:S(2)}, u32[]{:S(2)}) %collective-permute-start.9) | collective-permute-done | bytes 524320 | tf_op jit(solution)/shard_map/ppermute | solution.py:144
  78.6 0.9 %copy.15 = bf16[16,8,16,128]{3,2,1,0:T(8,128)(2,1)} copy(bf16[16,8,16,128]{3,1,2,0:T(8,128)(2,1)S(1)} %fusion.28) | data formatting | bytes 1048576
  79.9 0.5 slice.406
  80.7 1.2 %fusion.13 = f32[3,3,128,256]{3,2,1,0:T(8,128)} fusion(s32[]{:T(128)S(6)} %select_n.114, f32[3,3,128,256]{3,2,1,0:T(8,128)S(1)} %reshape.198), kind=kLoop, calls=%fused_computation.63 | loop fusion | flops 294912 | bytes 2359300 | tf_op jit(solution)/shard_map/concatenate | solution.py:133
  (98 shorter events, 18.6 us)
Async XLA Ops:
  0.6 6.8 %copy-start.3 = (bf16[128,16,128]{2,1,0:T(8,128)(2,1)S(1)}, bf16[128,16,128]{2,1,0:T(8,128)(2,1)}, u32[]{:S(2)}) copy-start(bf16[128,16,128]{2,1,0:T(8,128)(2,1)} %param.5) | copy-start | bytes 1572868
  0.6 6.9 %copy-start = (bf16[3,3,128,256]{3,2,1,0:T(8,128)(2,1)S(1)}, bf16[3,3,128,256]{3,2,1,0:T(8,128)(2,1)}, u32[]{:S(2)}) copy-start(bf16[3,3,128,256]{3,2,1,0:T(8,128)(2,1)} %param.6) | copy-start | bytes 1769476
  2.2 6.8 %collective-permute-start = (bf16[128,16,1]{0,2,1:T(2,128)(2,1)S(1)}, bf16[128,16,1]{0,2,1:T(2,128)(2,1)S(1)}, u32[]{:S(2)}, u32[]{:S(2)}) collective-permute-start(bf16[128,16,1]{0,2,1:T(2,128)(2,1)S(1)} %get-tuple-element.52), channel_id=1, source_target_pairs={{0,4},{4,8},{8,12},{12,0},{1,5},{5,9},{9,13},{13,1},{2,6},{6,10},{... | collective-permute-start | bytes 12296 | tf_op jit(solution)/shard_map/ppermute | solution.py:14
  5.3 3.7 %collective-permute-start.1 = (bf16[128,16,1]{0,2,1:T(2,128)(2,1)S(1)}, bf16[128,16,1]{0,2,1:T(2,128)(2,1)S(1)}, u32[]{:S(2)}, u32[]{:S(2)}) collective-permute-start(bf16[128,16,1]{0,2,1:T(2,128)(2,1)S(1)} %get-tuple-element.53), channel_id=1, source_target_pairs={{4,0},{8,4},{12,8},{0,12},{5,1},{9,5},{13,9},{1,13},{6,2},{10,6},{... | collective-permute-start | bytes 12296 | tf_op jit(solution)/shard_map/ppermute | solution.py:15
  9.1 1.3 %collective-permute-start.2 = (bf16[128,1,130]{0,2,1:T(8,128)(2,1)S(1)}, bf16[128,1,130]{0,2,1:T(8,128)(2,1)S(1)}, u32[]{:S(2)}, u32[]{:S(2)}) collective-permute-start(bf16[128,1,130]{0,2,1:T(8,128)(2,1)S(1)} %get-tuple-element.48), channel_id=1, source_target_pairs={{0,1},{1,0},{2,3},{3,2},{4,5},{5,4},{6,7},{7,6},{8,9},{9,8},{10,11... | collective-permute-start | bytes 99848 | tf_op jit(solution)/shard_map/ppermute | solution.py:14
  9.2 1.4 %collective-permute-start.3 = (bf16[128,1,130]{0,2,1:T(8,128)(2,1)S(1)}, bf16[128,1,130]{0,2,1:T(8,128)(2,1)S(1)}, u32[]{:S(2)}, u32[]{:S(2)}) collective-permute-start(bf16[128,1,130]{0,2,1:T(8,128)(2,1)S(1)} %get-tuple-element.49), channel_id=1, source_target_pairs={{1,0},{0,1},{3,2},{2,3},{5,4},{4,5},{7,6},{6,7},{9,8},{8,9},{11,10... | collective-permute-start | bytes 99848 | tf_op jit(solution)/shard_map/ppermute | solution.py:15
  11.8 16.4 %collective-permute-start.4 = (bf16[128,18,130]{0,2,1:T(8,128)(2,1)S(1)}, bf16[128,18,130]{0,2,1:T(8,128)(2,1)S(1)}, u32[]{:S(2)}, u32[]{:S(2)}) collective-permute-start(bf16[128,18,130]{0,2,1:T(8,128)(2,1)S(1)} %maximum_select_fusion), channel_id=1, source_target_pairs={{0,2},{2,0},{1,3},{3,1},{4,6},{6,4},{5,7},{7,5},{8,10},{10,8},{9,1... | collective-permute-start | bytes 1797128 | tf_op jit(solution)/shard_map/ppermute | solution.py:101
  31.0 0.7 copy-start.4
  39.6 5.5 %collective-permute-start.5 = (bf16[128,16,1]{0,2,1:T(2,128)(2,1)S(1)}, bf16[128,16,1]{0,2,1:T(2,128)(2,1)S(1)}, u32[]{:S(2)}, u32[]{:S(2)}) collective-permute-start(bf16[128,16,1]{0,2,1:T(2,128)(2,1)S(1)} %get-tuple-element.50), channel_id=1, source_target_pairs={{0,4},{4,8},{8,12},{12,0},{1,5},{5,9},{9,13},{13,1},{2,6},{6,10},{... | collective-permute-start | bytes 12296 | tf_op jit(solution)/shard_map/ppermute | solution.py:14
  41.1 4.0 %collective-permute-start.6 = (bf16[128,16,1]{0,2,1:T(2,128)(2,1)S(1)}, bf16[128,16,1]{0,2,1:T(2,128)(2,1)S(1)}, u32[]{:S(2)}, u32[]{:S(2)}) collective-permute-start(bf16[128,16,1]{0,2,1:T(2,128)(2,1)S(1)} %get-tuple-element.51), channel_id=1, source_target_pairs={{4,0},{8,4},{12,8},{0,12},{5,1},{9,5},{13,9},{1,13},{6,2},{10,6},{... | collective-permute-start | bytes 12296 | tf_op jit(solution)/shard_map/ppermute | solution.py:15
  45.1 1.3 %collective-permute-start.7 = (bf16[128,1,130]{0,2,1:T(8,128)(2,1)S(1)}, bf16[128,1,130]{0,2,1:T(8,128)(2,1)S(1)}, u32[]{:S(2)}, u32[]{:S(2)}) collective-permute-start(bf16[128,1,130]{0,2,1:T(8,128)(2,1)S(1)} %get-tuple-element.46), channel_id=1, source_target_pairs={{0,1},{1,0},{2,3},{3,2},{4,5},{5,4},{6,7},{7,6},{8,9},{9,8},{10,11... | collective-permute-start | bytes 99848 | tf_op jit(solution)/shard_map/ppermute | solution.py:14
  45.2 1.4 %collective-permute-start.8 = (bf16[128,1,130]{0,2,1:T(8,128)(2,1)S(1)}, bf16[128,1,130]{0,2,1:T(8,128)(2,1)S(1)}, u32[]{:S(2)}, u32[]{:S(2)}) collective-permute-start(bf16[128,1,130]{0,2,1:T(8,128)(2,1)S(1)} %get-tuple-element.47), channel_id=1, source_target_pairs={{1,0},{0,1},{3,2},{2,3},{5,4},{4,5},{7,6},{6,7},{9,8},{8,9},{11,10... | collective-permute-start | bytes 99848 | tf_op jit(solution)/shard_map/ppermute | solution.py:15
  45.7 7.0 %collective-permute-start.10 = (f32[1184,128]{1,0:T(8,128)S(1)}, f32[1184,128]{1,0:T(8,128)S(1)}, u32[]{:S(2)}, u32[]{:S(2)}) collective-permute-start(f32[1184,128]{1,0:T(8,128)S(1)} %dynamic-slice_bitcast_fusion), channel_id=1, source_target_pairs={{0,1},{1,0},{2,3},{3,2},{4,5},{5,4},{6,7},{7,6},{8,9},{9,8},{10,11... | collective-permute-start | bytes 1818632 | tf_op jit(solution)/shard_map/ppermute | solution.py:64
  46.9 1.0 %copy-start.2 = (bf16[3,3,128,128]{2,3,1,0:T(8,128)(2,1)S(1)}, bf16[3,3,128,128]{2,3,1,0:T(8,128)(2,1)}, u32[]{:S(2)}) copy-start(bf16[3,3,128,128]{2,3,1,0:T(8,128)(2,1)} %get-tuple-element.44) | copy-start | bytes 884740
  47.8 1.0 %copy-start.1 = (bf16[3,3,128,128]{2,3,1,0:T(8,128)(2,1)S(1)}, bf16[3,3,128,128]{2,3,1,0:T(8,128)(2,1)}, u32[]{:S(2)}) copy-start(bf16[3,3,128,128]{2,3,1,0:T(8,128)(2,1)} %get-tuple-element.45) | copy-start | bytes 884740
  52.9 7.4 %collective-permute-start.11 = (bf16[296,128]{1,0:T(8,128)(2,1)S(1)}, bf16[296,128]{1,0:T(8,128)(2,1)S(1)}, u32[]{:S(2)}, u32[]{:S(2)}) collective-permute-start(bf16[296,128]{1,0:T(8,128)(2,1)S(1)} %get-tuple-element.41), channel_id=1, source_target_pairs={{0,4},{4,8},{8,12},{12,0},{1,5},{5,9},{9,13},{13,1},{2,6},{6,10},{... | collective-permute-start | bytes 227336 | tf_op jit(solution)/shard_map/ppermute | solution.py:64
  54.2 9.0 %collective-permute-start.12 = (bf16[296,128]{1,0:T(8,128)(2,1)S(1)}, bf16[296,128]{1,0:T(8,128)(2,1)S(1)}, u32[]{:S(2)}, u32[]{:S(2)}) collective-permute-start(bf16[296,128]{1,0:T(8,128)(2,1)S(1)} %get-tuple-element.43), channel_id=1, source_target_pairs={{0,8},{4,12},{8,0},{12,4},{1,9},{5,13},{9,1},{13,5},{2,10},{6,14},... | collective-permute-start | bytes 227336 | tf_op jit(solution)/shard_map/ppermute | solution.py:64
  57.5 5.9 %collective-permute-start.13 = (bf16[296,128]{1,0:T(8,128)(2,1)S(1)}, bf16[296,128]{1,0:T(8,128)(2,1)S(1)}, u32[]{:S(2)}, u32[]{:S(2)}) collective-permute-start(bf16[296,128]{1,0:T(8,128)(2,1)S(1)} %get-tuple-element.42), channel_id=1, source_target_pairs={{0,12},{4,0},{8,4},{12,8},{1,13},{5,1},{9,5},{13,9},{2,14},{6,2},{... | collective-permute-start | bytes 227336 | tf_op jit(solution)/shard_map/ppermute | solution.py:64
  63.5 5.4 %collective-permute-start.14 = (bf16[296,128]{1,0:T(8,128)(2,1)S(1)}, bf16[296,128]{1,0:T(8,128)(2,1)S(1)}, u32[]{:S(2)}, u32[]{:S(2)}) collective-permute-start(bf16[296,128]{1,0:T(8,128)(2,1)S(1)} %get-tuple-element.3), channel_id=1, source_target_pairs={{0,12},{4,0},{8,4},{12,8},{1,13},{5,1},{9,5},{13,9},{2,14},{6,2},{... | collective-permute-start | bytes 227336 | tf_op jit(solution)/shard_map/ppermute | solution.py:76
  66.2 12.1 %collective-permute-start.9 = (bf16[128,2048]{1,0:T(8,128)(2,1)S(1)}, bf16[128,2048]{1,0:T(8,128)(2,1)S(1)}, u32[]{:S(2)}, u32[]{:S(2)}) collective-permute-start(bf16[128,2048]{1,0:T(8,128)(2,1)S(1)} %fusion.9), channel_id=1, source_target_pairs={{0,2},{2,0},{1,3},{3,1},{4,6},{6,4},{5,7},{7,5},{8,10},{10,8},{9,1... | collective-permute-start | bytes 1572872 | tf_op jit(solution)/shard_map/ppermute | solution.py:144
  68.0 6.1 %collective-permute-start.15 = (bf16[296,128]{1,0:T(8,128)(2,1)S(1)}, bf16[296,128]{1,0:T(8,128)(2,1)S(1)}, u32[]{:S(2)}, u32[]{:S(2)}) collective-permute-start(bf16[296,128]{1,0:T(8,128)(2,1)S(1)} %get-tuple-element.3), channel_id=1, source_target_pairs={{0,8},{4,12},{8,0},{12,4},{1,9},{5,13},{9,1},{13,5},{2,10},{6,14},... | collective-permute-start | bytes 227336 | tf_op jit(solution)/shard_map/ppermute | solution.py:76
  68.9 6.2 %collective-permute-start.16 = (bf16[296,128]{1,0:T(8,128)(2,1)S(1)}, bf16[296,128]{1,0:T(8,128)(2,1)S(1)}, u32[]{:S(2)}, u32[]{:S(2)}) collective-permute-start(bf16[296,128]{1,0:T(8,128)(2,1)S(1)} %get-tuple-element.3), channel_id=1, source_target_pairs={{0,4},{4,8},{8,12},{12,0},{1,5},{5,9},{9,13},{13,1},{2,6},{6,10},{... | collective-permute-start | bytes 227336 | tf_op jit(solution)/shard_map/ppermute | solution.py:76
  75.2 4.3 %collective-permute-start.17 = (f32[1184,128]{1,0:T(8,128)S(1)}, f32[1184,128]{1,0:T(8,128)S(1)}, u32[]{:S(2)}, u32[]{:S(2)}) collective-permute-start(f32[1184,128]{1,0:T(8,128)S(1)} %bitcast.315), channel_id=1, source_target_pairs={{0,1},{1,0},{2,3},{3,2},{4,5},{5,4},{6,7},{7,6},{8,9},{9,8},{10,11... | collective-permute-start | bytes 1818632 | tf_op jit(solution)/shard_map/ppermute | solution.py:76

commit v4 on v3

--- a/solution.py
+++ b/solution.py
@@ -90,50 +90,76 @@
     return rows.reshape(-1)[: flat.size]
 
 
+def border_of(padded):
+    rows, cols = padded.shape[1], padded.shape[2]
+    return jnp.concatenate(
+        [padded[:, 0, :], padded[:, rows - 1, :], padded[:, 1 : rows - 1, 0], padded[:, 1 : rows - 1, cols - 1]],
+        axis=1,
+    )
+
+
+def with_border(field, border):
+    rows, cols = field.shape[1], field.shape[2]
+    top = border[:, : cols + 2]
+    bottom = border[:, cols + 2 : 2 * cols + 4]
+    left = border[:, 2 * cols + 4 : 2 * cols + 4 + rows]
+    right = border[:, 2 * cols + 4 + rows :]
+    middle = jnp.concatenate([left[:, :, None], field, right[:, :, None]], axis=2)
+    return jnp.concatenate([top[:, None, :], middle, bottom[:, None, :]], axis=1)
+
+
 def local(inputs, cotangent, weight, bias_vector):
     own_channels, row_count, column_count = inputs.shape
     chan_count = lax.axis_size("chan")
     chan_index = lax.axis_index("chan")
+    raw_blocks = []
+    for shift in range(1, chan_count):
+        pairs = [(i, (i - shift) % chan_count) for i in range(chan_count)]
+        raw_blocks.append(lax.ppermute(inputs, "chan", pairs))
     input_pad = mask_rims(padded_2(inputs, (("lon", 2), ("lat", 1)), 1))
+    own_border = border_of(input_pad)
     blocks = [input_pad]
     for shift in range(1, chan_count):
         pairs = [(i, (i - shift) % chan_count) for i in range(chan_count)]
-        blocks.append(lax.ppermute(input_pad, "chan", pairs))
+        border = lax.ppermute(own_border, "chan", pairs)
+        blocks.append(with_border(raw_blocks[shift - 1], border))
     kernel_cols = []
     for shift in range(chan_count):
         source = (chan_index + shift) % chan_count
         kernel_cols.append(
             lax.dynamic_slice_in_dim(weight, source * own_channels, own_channels, axis=3)
         )
+    windows = [
+        [window_of(block, tap // 3, tap % 3, row_count, column_count) for tap in range(9)]
+        for block in blocks
+    ]
     preact = None
     for shift in range(chan_count):
-        part = conv_taps(kernel_cols[shift], blocks[shift], row_count, column_count, False)
-        preact = part if preact is None else preact + part
+        for tap in range(9):
+            part = jnp.dot(
+                kernel_cols[shift][tap // 3, tap % 3], windows[shift][tap], preferred_element_type=jnp.float32
+            )
+            preact = part if preact is None else preact + part
     preact = preact + bias_vector[:, None]
     upstream = cotangent.reshape(own_channels, -1).astype(jnp.float32)
     grad_pre = (upstream * gelu_slope(preact)).astype(jnp.bfloat16)
     bias_part = jnp.sum(grad_pre.astype(jnp.float32), axis=1)
-    input_local = jnp.concatenate(blocks, axis=0)
-    taps = []
-    for tap_row in range(3):
-        row_taps = []
-        for tap_col in range(3):
-            window = window_of(input_local, tap_row, tap_col, row_count, column_count)
-            row_taps.append(
+    pieces = []
+    for shift in range(chan_count):
+        for tap in range(9):
+            pieces.append(
                 lax.dot_general(
-                    grad_pre, window, (((1,), (1,)), ((), ())), preferred_element_type=jnp.float32
-                )
+                    grad_pre, windows[shift][tap], (((1,), (1,)), ((), ())), preferred_element_type=jnp.float32
+                ).reshape(-1)
             )
-        taps.append(jnp.stack(row_taps))
-    weight_part = jnp.stack(taps)
-    flat = jnp.concatenate([weight_part.reshape(-1), bias_part])
+    flat = jnp.concatenate(pieces + [bias_part])
     flat = all_sum(flat, jnp.bfloat16)
-    weight_local = flat[: weight_part.size].reshape(weight_part.shape)
-    bias_grad = flat[weight_part.size :]
-    doubled = jnp.concatenate([weight_local, weight_local], axis=3)
-    weight_grad = lax.dynamic_slice_in_dim(
-        doubled, (chan_count - chan_index) % chan_count * own_channels, chan_count * own_channels, axis=3
-    )
+    block_size = 9 * own_channels * own_channels
+    weight_local = flat[: chan_count * block_size].reshape(chan_count, 3, 3, own_channels, own_channels)
+    bias_grad = flat[chan_count * block_size :]
+    doubled = jnp.concatenate([weight_local, weight_local], axis=0)
+    ordered = lax.dynamic_slice_in_dim(doubled, (chan_count - chan_index) % chan_count, chan_count, axis=0)
+    weight_grad = jnp.transpose(ordered, (1, 2, 3, 0, 4)).reshape(3, 3, own_channels, chan_count * own_channels)
     grad_field = grad_pre.reshape(own_channels, row_count, column_count)
     grad_pad = mask_rims(padded_2(grad_field, (("lon", 2), ("lat", 1)), 1))
     received = []

time: 82.1 us -> 87.5 us (1.066)
  matrix products: 15.1 us -> 30.3 us
  waiting for transfers between devices: 28.6 us -> 17.4 us
  local copies, waits for them, and re-layouts: 8.83 us -> 12.1 us
  other arithmetic: 5.18 us -> 3.04 us
    dot_general x9 -> x36, matrix products: 2.84 us -> 24.5 us  [the longest x18 17.7 us: local(): lax.dot_general(grad_pre, windows[shift][tap], (((1,), (1,)), ((), ())),...]
    ppermute x1 -> x2, waiting for transfers between devices: 12 us -> 1.69 us  [the longest x1 1.69 us: local(): border = lax.ppermute(own_border, 'chan', pairs)]
    dot_general x36 -> x18, matrix products: 12.3 us -> 5.78 us  [conv_taps(): jnp.dot(kernel[tap_row, tap_col], window, preferred_element_type=jnp.floa...]
    concatenate x3, other arithmetic: 3.78 us -> 0.58 us  [the longest x1 0.31 us: with_border(): jnp.concatenate([left[:, :, None], field, right[:, :, None]], axis=2)]
    ppermute x4, waiting for transfers between devices: 3.11 us -> 1.21 us  [padded_2(): before = lax.ppermute(last, axis, up)]
    ppermute x1 -> x2, starting transfers between devices: 1.69 us -> 3.45 us  [the longest x1 3 us: local(): raw_blocks.append(lax.ppermute(inputs, 'chan', pairs))]
    unnamed x14 -> x65, local copies, waits for them, and re-layouts: 3.77 us -> 5.46 us
    pad x0 -> x1, local copies, waits for them, and re-layouts: none -> 1.35 us  [all_sum(): padded = jnp.pad(flat, (0, -flat.size % quantum)).reshape(-1, 128)]
  transfers between devices with their start and end apart: 18 -> 19, of which waited for: 13 -> 11; matrix products, arithmetic and copies ran while one was open for 15% -> 18% of each run, Pallas kernels for 0% -> 0%
where the time goes in v4:
time: 87.5 us; the launch traced here: 87.1 us
  matrix products  30.3 us (35%)
  starting transfers between devices  22.9 us (26%)
  waiting for transfers between devices  17.4 us (20%)
  local copies, waits for them, and re-layouts  12.1 us (14%)
  other arithmetic  3.04 us (3%)
  between operations  1.4 us (2%)
    dot_general x18, matrix products, local(): lax.dot_general(grad_pre, windows[shift][tap], (((1,), (1,)), ((), ())),...  17.7 us
    dot_general x18, matrix products, local(): jnp.dot(kernel_cols[shift][tap // 3, tap % 3], windows[shift][tap], prefe...  6.84 us
    ppermute x4, waiting for transfers between devices, direct_all_gather(): pieces.append(lax.ppermute(sent, axis, pairs).astype(jnp.float32))  6.14 us
    dot_general x18, matrix products, conv_taps(): jnp.dot(kernel[tap_row, tap_col], window, preferred_element_type=jnp.floa...  5.78 us
    unnamed x65, local copies, waits for them, and re-layouts  5.46 us
    ppermute x4, starting transfers between devices, padded_2(): after = lax.ppermute(initial, axis, down)  5.33 us
    ppermute x4, starting transfers between devices, direct_reduce_scatter(): lax.ppermute(piece.astype(send_dtype), axis, pairs).astype(jnp.float32)  5.3 us
    ppermute x4, waiting for transfers between devices, direct_reduce_scatter(): lax.ppermute(piece.astype(send_dtype), axis, pairs).astype(jnp.float32)  4.5 us
  transfers between devices with their start and end apart: 19, of which 11 were waited for; matrix products, arithmetic and copies ran while one was open for 18% of the time, Pallas kernels for 0%

profile of v4, /device:TPU:0, one launch (start us, length us, event | category | flops | bytes accessed | tf_op | source)
XLA Modules:
  0.0 87.1 jit_solution(8822464099225009783)
XLA Ops:
  0.7 1.6 %copy.45 = bf16[128,16,128]{0,2,1:T(8,128)(2,1)S(1)} copy(bf16[128,16,128]{2,1,0:T(8,128)(2,1)} %param.4) | data formatting | bytes 1048576 | tf_op args[0]
  2.2 3.0 %collective-permute-start.5 = (bf16[128,16,128]{0,2,1:T(8,128)(2,1)S(1)}, bf16[128,16,128]{0,2,1:T(8,128)(2,1)S(1)}, u32[]{:S(2)}, u32[]{:S(2)}) collective-permute-start(bf16[128,16,128]{0,2,1:T(8,128)(2,1)S(1)} %copy.45), channel_id=1, source_target_pairs={{0,2},{2,0},{1,3},{3,1},{4,6},{6,4},{5,7},{7,5},{8,10},{10,8},{9,1... | collective-permute-start | bytes 1572872 | tf_op jit(solution)/shard_map/ppermute | solution.py:118
  5.2 1.6 %collective-permute-start = (bf16[128,16,1]{0,2,1:T(2,128)(2,1)S(1)}, bf16[128,16,1]{0,2,1:T(2,128)(2,1)S(1)}, u32[]{:S(2)}, u32[]{:S(2)}) collective-permute-start(bf16[128,16,1]{0,2,1:T(2,128)(2,1)S(1)} %get-tuple-element.54), channel_id=1, source_target_pairs={{0,4},{4,8},{8,12},{12,0},{1,5},{5,9},{9,13},{13,1},{2,6},{6,10},{... | collective-permute-start | bytes 12296 | tf_op jit(solution)/shard_map/ppermute | solution.py:14
  6.9 2.2 %collective-permute-start.1 = (bf16[128,16,1]{0,2,1:T(2,128)(2,1)S(1)}, bf16[128,16,1]{0,2,1:T(2,128)(2,1)S(1)}, u32[]{:S(2)}, u32[]{:S(2)}) collective-permute-start(bf16[128,16,1]{0,2,1:T(2,128)(2,1)S(1)} %get-tuple-element.55), channel_id=1, source_target_pairs={{4,0},{8,4},{12,8},{0,12},{5,1},{9,5},{13,9},{1,13},{6,2},{10,6},{... | collective-permute-start | bytes 12296 | tf_op jit(solution)/shard_map/ppermute | solution.py:15
  9.1 1.1 %bitcast_convert_fusion = f32[16,8,16,128]{3,2,1,0:T(8,128)} fusion(bf16[128,16,128]{2,1,0:T(8,128)(2,1)S(1)} %copy-done.28), kind=kLoop, calls=%fused_computation.205 | loop fusion | flops 262144 | bytes 1572864
  17.1 1.7 %collective-permute-done.4 = bf16[128,292]{0,1:T(8,128)(2,1)S(1)} collective-permute-done((bf16[128,292]{0,1:T(8,128)(2,1)S(1)}, bf16[128,292]{0,1:T(8,128)(2,1)S(1)}, u32[]{:S(2)}, u32[]{:S(2)}) %collective-permute-start.4) | collective-permute-done | bytes 74784 | tf_op jit(solution)/shard_map/ppermute | solution.py:124
  24.2 1.7 %convert_reduce_fusion = (f32[128]{0:T(128)S(1)}, bf16[128,2048]{1,0:T(8,128)(2,1)S(1)}) fusion(f32[128]{0:T(128)S(1)} %copy-done.29, f32[128,2048]{1,0:T(8,128)S(1)} %convolution_add_fusion.17, bf16[128,2048]{0,1:T(8,128)(2,1)S(1)} %bitcast.417, bf16[3,3,128,256]{3,2,1,0:T(8,128)(2,1)} %param.6, s32[]{:T(128)S(6)} %add.291, s32[]{:T(128)S(6)} %select_n.97, ...), kind=kOutput, calls=%fused_computation.89 | convolution fusion | flops 70778752 | bytes 3179528 | tf_op jit(solution)/shard_map/dot_general | solution.py:139
  25.9 0.9 %fusion.22 = f32[295040]{0:T(1024)} fusion(bf16[128,2048]{1,0:T(8,128)(2,1)S(1)} %get-tuple-element.61, bf16[128,2048]{0,1:T(8,128)(2,1)S(1)} %bitcast.383), kind=kOutput, calls=%fused_computation.76 | convolution fusion | flops 67108864 | bytes 1114112 | tf_op jit(solution)/shard_map/dot_general | solution.py:151
  27.1 2.0 %fusion.21 = f32[295040]{0:T(1024)} fusion(f32[295040]{0:T(1024)} %fusion.22, bf16[128,2048]{1,0:T(8,128)(2,1)S(1)} %get-tuple-element.61, bf16[128,2048]{0,1:T(8,128)(2,1)} %bitcast.376), kind=kOutput, calls=%fused_computation.74 | convolution fusion | flops 67108864 | bytes 1114112 | tf_op jit(solution)/shard_map/dot_general | solution.py:151
  29.1 0.9 %fusion.20 = f32[295040]{0:T(1024)} fusion(f32[295040]{0:T(1024)} %fusion.21, bf16[128,2048]{1,0:T(8,128)(2,1)S(1)} %get-tuple-element.61, bf16[128,2048]{0,1:T(8,128)(2,1)S(1)} %bitcast.374), kind=kOutput, calls=%fused_computation.72 | convolution fusion | flops 67108864 | bytes 1114112 | tf_op jit(solution)/shard_map/dot_general | solution.py:151
  30.1 0.9 %fusion.19 = f32[295040]{0:T(1024)} fusion(f32[295040]{0:T(1024)} %fusion.20, bf16[128,2048]{1,0:T(8,128)(2,1)S(1)} %get-tuple-element.61, bf16[128,2048]{0,1:T(8,128)(2,1)S(1)} %bitcast.372), kind=kOutput, calls=%fused_computation.70 | convolution fusion | flops 67108864 | bytes 1114112 | tf_op jit(solution)/shard_map/dot_general | solution.py:151
  31.9 0.9 %fusion.17 = f32[295040]{0:T(1024)} fusion(f32[295040]{0:T(1024)} %fusion.18, bf16[128,2048]{1,0:T(8,128)(2,1)S(1)} %get-tuple-element.61, bf16[128,2048]{0,1:T(8,128)(2,1)S(1)} %bitcast.388), kind=kOutput, calls=%fused_computation.66 | convolution fusion | flops 67108864 | bytes 1114112 | tf_op jit(solution)/shard_map/dot_general | solution.py:151
  35.5 0.9 %fusion.13 = f32[295040]{0:T(1024)} fusion(f32[295040]{0:T(1024)} %fusion.14, bf16[128,2048]{1,0:T(8,128)(2,1)S(1)} %get-tuple-element.61, bf16[128,2048]{0,1:T(8,128)(2,1)S(1)} %bitcast.414), kind=kOutput, calls=%fused_computation.58 | convolution fusion | flops 67108864 | bytes 1114112 | tf_op jit(solution)/shard_map/dot_general | solution.py:151
  36.4 0.9 %fusion.12 = f32[295040]{0:T(1024)} fusion(f32[295040]{0:T(1024)} %fusion.13, bf16[128,2048]{1,0:T(8,128)(2,1)S(1)} %get-tuple-element.61, bf16[128,2048]{0,1:T(8,128)(2,1)S(1)} %bitcast.392), kind=kOutput, calls=%fused_computation.56 | convolution fusion | flops 67108864 | bytes 1114112 | tf_op jit(solution)/shard_map/dot_general | solution.py:151
  37.4 0.9 %fusion.11 = f32[295040]{0:T(1024)} fusion(f32[295040]{0:T(1024)} %fusion.12, bf16[128,2048]{1,0:T(8,128)(2,1)S(1)} %get-tuple-element.61, bf16[128,2048]{0,1:T(8,128)(2,1)S(1)} %bitcast.390), kind=kOutput, calls=%fused_computation.54 | convolution fusion | flops 67108864 | bytes 1114112 | tf_op jit(solution)/shard_map/dot_general | solution.py:151
  41.0 1.1 %fusion.7 = f32[295040]{0:T(1024)} fusion(f32[295040]{0:T(1024)} %fusion.8, bf16[128,2048]{1,0:T(8,128)(2,1)S(1)} %get-tuple-element.61, bf16[128,2048]{0,1:T(8,128)(2,1)S(1)} %bitcast.412), kind=kOutput, calls=%fused_computation.46 | convolution fusion | flops 67108864 | bytes 1114112 | tf_op jit(solution)/shard_map/dot_general | solution.py:151
  42.1 0.9 %fusion.6 = f32[295040]{0:T(1024)} fusion(f32[295040]{0:T(1024)} %fusion.7, bf16[128,2048]{1,0:T(8,128)(2,1)S(1)} %get-tuple-element.61, bf16[128,2048]{0,1:T(8,128)(2,1)S(1)} %bitcast.410), kind=kOutput, calls=%fused_computation.44 | convolution fusion | flops 67108864 | bytes 1114112 | tf_op jit(solution)/shard_map/dot_general | solution.py:151
  43.9 1.8 %collective-permute-start.6 = (bf16[128,16,1]{0,2,1:T(2,128)(2,1)S(1)}, bf16[128,16,1]{0,2,1:T(2,128)(2,1)S(1)}, u32[]{:S(2)}, u32[]{:S(2)}) collective-permute-start(bf16[128,16,1]{0,2,1:T(2,128)(2,1)S(1)} %get-tuple-element.50), channel_id=1, source_target_pairs={{0,4},{4,8},{8,12},{12,0},{1,5},{5,9},{9,13},{13,1},{2,6},{6,10},{... | collective-permute-start | bytes 12296 | tf_op jit(solution)/shard_map/ppermute | solution.py:14
  45.8 2.1 %collective-permute-start.7 = (bf16[128,16,1]{0,2,1:T(2,128)(2,1)S(1)}, bf16[128,16,1]{0,2,1:T(2,128)(2,1)S(1)}, u32[]{:S(2)}, u32[]{:S(2)}) collective-permute-start(bf16[128,16,1]{0,2,1:T(2,128)(2,1)S(1)} %get-tuple-element.51), channel_id=1, source_target_pairs={{4,0},{8,4},{12,8},{0,12},{5,1},{9,5},{13,9},{1,13},{6,2},{10,6},{... | collective-permute-start | bytes 12296 | tf_op jit(solution)/shard_map/ppermute | solution.py:15
  48.4 1.4 %pad.4 = f32[303104]{0:T(1024)S(1)} pad(f32[295040]{0:T(1024)} %constant_dynamic-update-slice_fusion, f32[]{:T(128)} %constant.122.clone.1), padding=0_8064 | pad | bytes 2392580 | tf_op jit(solution)/shard_map/jit(_pad)/pad | solution.py:85
  57.0 1.2 %collective-permute-start.12 = (bf16[296,128]{1,0:T(8,128)(2,1)S(1)}, bf16[296,128]{1,0:T(8,128)(2,1)S(1)}, u32[]{:S(2)}, u32[]{:S(2)}) collective-permute-start(bf16[296,128]{1,0:T(8,128)(2,1)S(1)} %get-tuple-element.33), channel_id=1, source_target_pairs={{0,4},{4,8},{8,12},{12,0},{1,5},{5,9},{9,13},{13,1},{2,6},{6,10},{... | collective-permute-start | bytes 227336 | tf_op jit(solution)/shard_map/ppermute | solution.py:64
  58.2 2.9 %collective-permute-start.13 = (bf16[296,128]{1,0:T(8,128)(2,1)S(1)}, bf16[296,128]{1,0:T(8,128)(2,1)S(1)}, u32[]{:S(2)}, u32[]{:S(2)}) collective-permute-start(bf16[296,128]{1,0:T(8,128)(2,1)S(1)} %get-tuple-element.35), channel_id=1, source_target_pairs={{0,8},{4,12},{8,0},{12,4},{1,9},{5,13},{9,1},{13,5},{2,10},{6,14},... | collective-permute-start | bytes 227336 | tf_op jit(solution)/shard_map/ppermute | solution.py:64
  61.1 1.1 %collective-permute-start.14 = (bf16[296,128]{1,0:T(8,128)(2,1)S(1)}, bf16[296,128]{1,0:T(8,128)(2,1)S(1)}, u32[]{:S(2)}, u32[]{:S(2)}) collective-permute-start(bf16[296,128]{1,0:T(8,128)(2,1)S(1)} %get-tuple-element.34), channel_id=1, source_target_pairs={{0,12},{4,0},{8,4},{12,8},{1,13},{5,1},{9,5},{13,9},{2,14},{6,2},{... | collective-permute-start | bytes 227336 | tf_op jit(solution)/shard_map/ppermute | solution.py:64
  62.5 1.6 %collective-permute-done.12 = bf16[296,128]{1,0:T(8,128)(2,1)S(1)} collective-permute-done((bf16[296,128]{1,0:T(8,128)(2,1)S(1)}, bf16[296,128]{1,0:T(8,128)(2,1)S(1)}, u32[]{:S(2)}, u32[]{:S(2)}) %collective-permute-start.12) | collective-permute-done | bytes 75808 | tf_op jit(solution)/shard_map/ppermute | solution.py:64
  64.1 2.7 %collective-permute-done.13 = bf16[296,128]{1,0:T(8,128)(2,1)S(1)} collective-permute-done((bf16[296,128]{1,0:T(8,128)(2,1)S(1)}, bf16[296,128]{1,0:T(8,128)(2,1)S(1)}, u32[]{:S(2)}, u32[]{:S(2)}) %collective-permute-start.13) | collective-permute-done | bytes 75808 | tf_op jit(solution)/shard_map/ppermute | solution.py:64
  67.0 2.6 %collective-permute-start.15 = (bf16[296,128]{1,0:T(8,128)(2,1)S(1)}, bf16[296,128]{1,0:T(8,128)(2,1)S(1)}, u32[]{:S(2)}, u32[]{:S(2)}) collective-permute-start(bf16[296,128]{1,0:T(8,128)(2,1)S(1)} %get-tuple-element.9), channel_id=1, source_target_pairs={{0,12},{4,0},{8,4},{12,8},{1,13},{5,1},{9,5},{13,9},{2,14},{6,2},{... | collective-permute-start | bytes 227336 | tf_op jit(solution)/shard_map/ppermute | solution.py:76
  70.0 1.6 %collective-permute-start.10 = (bf16[128,2048]{1,0:T(8,128)(2,1)S(1)}, bf16[128,2048]{1,0:T(8,128)(2,1)S(1)}, u32[]{:S(2)}, u32[]{:S(2)}) collective-permute-start(bf16[128,2048]{1,0:T(8,128)(2,1)S(1)} %fusion.4), channel_id=1, source_target_pairs={{0,2},{2,0},{1,3},{3,1},{4,6},{6,4},{5,7},{7,5},{8,10},{10,8},{9,1... | collective-permute-start | bytes 1572872 | tf_op jit(solution)/shard_map/ppermute | solution.py:170
  71.5 0.9 %collective-permute-start.16 = (bf16[296,128]{1,0:T(8,128)(2,1)S(1)}, bf16[296,128]{1,0:T(8,128)(2,1)S(1)}, u32[]{:S(2)}, u32[]{:S(2)}) collective-permute-start(bf16[296,128]{1,0:T(8,128)(2,1)S(1)} %get-tuple-element.9), channel_id=1, source_target_pairs={{0,8},{4,12},{8,0},{12,4},{1,9},{5,13},{9,1},{13,5},{2,10},{6,14},... | collective-permute-start | bytes 227336 | tf_op jit(solution)/shard_map/ppermute | solution.py:76
  72.5 5.1 %collective-permute-done.16 = bf16[296,128]{1,0:T(8,128)(2,1)S(1)} collective-permute-done((bf16[296,128]{1,0:T(8,128)(2,1)S(1)}, bf16[296,128]{1,0:T(8,128)(2,1)S(1)}, u32[]{:S(2)}, u32[]{:S(2)}) %collective-permute-start.16) | collective-permute-done | bytes 75808 | tf_op jit(solution)/shard_map/ppermute | solution.py:76
  77.6 1.0 %collective-permute-done.17 = bf16[296,128]{1,0:T(8,128)(2,1)S(1)} collective-permute-done((bf16[296,128]{1,0:T(8,128)(2,1)S(1)}, bf16[296,128]{1,0:T(8,128)(2,1)S(1)}, u32[]{:S(2)}, u32[]{:S(2)}) %collective-permute-start.17) | collective-permute-done | bytes 75808 | tf_op jit(solution)/shard_map/ppermute | solution.py:76
  79.6 3.5 %collective-permute-done.10 = bf16[128,2048]{1,0:T(8,128)(2,1)S(1)} collective-permute-done((bf16[128,2048]{1,0:T(8,128)(2,1)S(1)}, bf16[128,2048]{1,0:T(8,128)(2,1)S(1)}, u32[]{:S(2)}, u32[]{:S(2)}) %collective-permute-start.10) | collective-permute-done | bytes 524320 | tf_op jit(solution)/shard_map/ppermute | solution.py:170
  85.8 1.4 %copy.57 = f32[3,3,128,256]{3,2,1,0:T(8,128)} copy(f32[3,3,128,256]{2,3,1,0:T(8,128)S(1)} %bitcast.384) | data formatting | bytes 2359296
  (167 shorter events, 31.5 us)
Async XLA Ops:
  0.6 8.5 %copy-start.28 = (bf16[128,16,128]{2,1,0:T(8,128)(2,1)S(1)}, bf16[128,16,128]{2,1,0:T(8,128)(2,1)}, u32[]{:S(2)}) copy-start(bf16[128,16,128]{2,1,0:T(8,128)(2,1)} %param.5) | copy-start | bytes 1572868
  0.6 9.6 %copy-start.23 = (bf16[3,3,128,256]{3,2,1,0:T(8,128)(2,1)S(1)}, bf16[3,3,128,256]{3,2,1,0:T(8,128)(2,1)}, u32[]{:S(2)}) copy-start(bf16[3,3,128,256]{3,2,1,0:T(8,128)(2,1)} %param.6) | copy-start | bytes 1769476
  2.2 16.6 %collective-permute-start.5 = (bf16[128,16,128]{0,2,1:T(8,128)(2,1)S(1)}, bf16[128,16,128]{0,2,1:T(8,128)(2,1)S(1)}, u32[]{:S(2)}, u32[]{:S(2)}) collective-permute-start(bf16[128,16,128]{0,2,1:T(8,128)(2,1)S(1)} %copy.45), channel_id=1, source_target_pairs={{0,2},{2,0},{1,3},{3,1},{4,6},{6,4},{5,7},{7,5},{8,10},{10,8},{9,1... | collective-permute-start | bytes 1572872 | tf_op jit(solution)/shard_map/ppermute | solution.py:118
  5.2 5.8 %collective-permute-start = (bf16[128,16,1]{0,2,1:T(2,128)(2,1)S(1)}, bf16[128,16,1]{0,2,1:T(2,128)(2,1)S(1)}, u32[]{:S(2)}, u32[]{:S(2)}) collective-permute-start(bf16[128,16,1]{0,2,1:T(2,128)(2,1)S(1)} %get-tuple-element.54), channel_id=1, source_target_pairs={{0,4},{4,8},{8,12},{12,0},{1,5},{5,9},{9,13},{13,1},{2,6},{6,10},{... | collective-permute-start | bytes 12296 | tf_op jit(solution)/shard_map/ppermute | solution.py:14
  6.9 4.2 %collective-permute-start.1 = (bf16[128,16,1]{0,2,1:T(2,128)(2,1)S(1)}, bf16[128,16,1]{0,2,1:T(2,128)(2,1)S(1)}, u32[]{:S(2)}, u32[]{:S(2)}) collective-permute-start(bf16[128,16,1]{0,2,1:T(2,128)(2,1)S(1)} %get-tuple-element.55), channel_id=1, source_target_pairs={{4,0},{8,4},{12,8},{0,12},{5,1},{9,5},{13,9},{1,13},{6,2},{10,6},{... | collective-permute-start | bytes 12296 | tf_op jit(solution)/shard_map/ppermute | solution.py:15
  11.1 1.3 %collective-permute-start.2 = (bf16[128,1,130]{0,2,1:T(8,128)(2,1)S(1)}, bf16[128,1,130]{0,2,1:T(8,128)(2,1)S(1)}, u32[]{:S(2)}, u32[]{:S(2)}) collective-permute-start(bf16[128,1,130]{0,2,1:T(8,128)(2,1)S(1)} %get-tuple-element.48), channel_id=1, source_target_pairs={{0,1},{1,0},{2,3},{3,2},{4,5},{5,4},{6,7},{7,6},{8,9},{9,8},{10,11... | collective-permute-start | bytes 99848 | tf_op jit(solution)/shard_map/ppermute | solution.py:14
  11.2 1.4 %collective-permute-start.3 = (bf16[128,1,130]{0,2,1:T(8,128)(2,1)S(1)}, bf16[128,1,130]{0,2,1:T(8,128)(2,1)S(1)}, u32[]{:S(2)}, u32[]{:S(2)}) collective-permute-start(bf16[128,1,130]{0,2,1:T(8,128)(2,1)S(1)} %get-tuple-element.49), channel_id=1, source_target_pairs={{1,0},{0,1},{3,2},{2,3},{5,4},{4,5},{7,6},{6,7},{9,8},{8,9},{11,10... | collective-permute-start | bytes 99848 | tf_op jit(solution)/shard_map/ppermute | solution.py:15
  13.8 2.1 %copy-start.11 = (bf16[128,16,128]{0,2,1:T(8,128)(2,1)}, bf16[128,16,128]{0,2,1:T(8,128)(2,1)S(1)}, u32[]{:S(2)}) copy-start(bf16[128,16,128]{0,2,1:T(8,128)(2,1)S(1)} %get-tuple-element.23) | copy-start | bytes 1572868
  13.8 2.7 %copy-start.9 = (bf16[128,16,128]{0,2,1:T(8,128)(2,1)}, bf16[128,16,128]{0,2,1:T(8,128)(2,1)S(1)}, u32[]{:S(2)}) copy-start(bf16[128,16,128]{0,2,1:T(8,128)(2,1)S(1)} %get-tuple-element.21) | copy-start | bytes 1572868
  14.2 4.6 %collective-permute-start.4 = (bf16[128,292]{0,1:T(8,128)(2,1)S(1)}, bf16[128,292]{0,1:T(8,128)(2,1)S(1)}, u32[]{:S(2)}, u32[]{:S(2)}) collective-permute-start(bf16[128,292]{0,1:T(8,128)(2,1)S(1)} %pad_maximum_fusion.3), channel_id=1, source_target_pairs={{0,2},{2,0},{1,3},{3,1},{4,6},{6,4},{5,7},{7,5},{8,10},{10,8},{9,1... | collective-permute-start | bytes 224264 | tf_op jit(solution)/shard_map/ppermute | solution.py:124
  19.5 2.1 %copy-start.21 = (bf16[128,16,128]{0,2,1:T(8,128)(2,1)}, bf16[128,16,128]{0,2,1:T(8,128)(2,1)S(1)}, u32[]{:S(2)}) copy-start(bf16[128,16,128]{0,2,1:T(8,128)(2,1)S(1)} %get-tuple-element.41) | copy-start | bytes 1572868
  19.5 2.4 %copy-start.15 = (bf16[128,16,128]{0,2,1:T(8,128)(2,1)}, bf16[128,16,128]{0,2,1:T(8,128)(2,1)S(1)}, u32[]{:S(2)}) copy-start(bf16[128,16,128]{0,2,1:T(8,128)(2,1)S(1)} %get-tuple-element.40) | copy-start | bytes 1572868
  19.5 2.7 %copy-start.13 = (bf16[128,16,128]{0,2,1:T(8,128)(2,1)}, bf16[128,16,128]{0,2,1:T(8,128)(2,1)S(1)}, u32[]{:S(2)}) copy-start(bf16[128,16,128]{0,2,1:T(8,128)(2,1)S(1)} %get-tuple-element.39) | copy-start | bytes 1572868
  19.8 2.7 %copy-start.7 = (bf16[128,16,128]{0,2,1:T(8,128)(2,1)}, bf16[128,16,128]{0,2,1:T(8,128)(2,1)S(1)}, u32[]{:S(2)}) copy-start(bf16[128,16,128]{0,2,1:T(8,128)(2,1)S(1)} %get-tuple-element.52) | copy-start | bytes 1572868
  20.8 2.1 %copy-start.17 = (bf16[128,16,128]{0,2,1:T(8,128)(2,1)}, bf16[128,16,128]{0,2,1:T(8,128)(2,1)S(1)}, u32[]{:S(2)}) copy-start(bf16[128,16,128]{0,2,1:T(8,128)(2,1)S(1)} %get-tuple-element.37) | copy-start | bytes 1572868
  20.8 2.5 %copy-start.24 = (bf16[128,16,128]{0,2,1:T(8,128)(2,1)}, bf16[128,16,128]{0,2,1:T(8,128)(2,1)S(1)}, u32[]{:S(2)}) copy-start(bf16[128,16,128]{0,2,1:T(8,128)(2,1)S(1)} %get-tuple-element.36) | copy-start | bytes 1572868
  27.1 2.1 %copy-start.3 = (bf16[128,16,128]{0,2,1:T(8,128)(2,1)S(1)}, bf16[128,16,128]{0,2,1:T(8,128)(2,1)}, u32[]{:S(2)}) copy-start(bf16[128,16,128]{0,2,1:T(8,128)(2,1)} %copy-done.2) | copy-start | bytes 1572868
  27.1 3.0 %copy-start.1 = (bf16[128,16,128]{0,2,1:T(8,128)(2,1)S(1)}, bf16[128,16,128]{0,2,1:T(8,128)(2,1)}, u32[]{:S(2)}) copy-start(bf16[128,16,128]{0,2,1:T(8,128)(2,1)} %copy-done) | copy-start | bytes 1572868
  41.0 2.0 %copy-start.25 = (bf16[128,16,128]{0,2,1:T(8,128)(2,1)S(1)}, bf16[128,16,128]{0,2,1:T(8,128)(2,1)}, u32[]{:S(2)}) copy-start(bf16[128,16,128]{0,2,1:T(8,128)(2,1)} %copy-done.24) | copy-start | bytes 1572868
  43.9 5.9 %collective-permute-start.6 = (bf16[128,16,1]{0,2,1:T(2,128)(2,1)S(1)}, bf16[128,16,1]{0,2,1:T(2,128)(2,1)S(1)}, u32[]{:S(2)}, u32[]{:S(2)}) collective-permute-start(bf16[128,16,1]{0,2,1:T(2,128)(2,1)S(1)} %get-tuple-element.50), channel_id=1, source_target_pairs={{0,4},{4,8},{8,12},{12,0},{1,5},{5,9},{9,13},{13,1},{2,6},{6,10},{... | collective-permute-start | bytes 12296 | tf_op jit(solution)/shard_map/ppermute | solution.py:14
  45.8 4.1 %collective-permute-start.7 = (bf16[128,16,1]{0,2,1:T(2,128)(2,1)S(1)}, bf16[128,16,1]{0,2,1:T(2,128)(2,1)S(1)}, u32[]{:S(2)}, u32[]{:S(2)}) collective-permute-start(bf16[128,16,1]{0,2,1:T(2,128)(2,1)S(1)} %get-tuple-element.51), channel_id=1, source_target_pairs={{4,0},{8,4},{12,8},{0,12},{5,1},{9,5},{13,9},{1,13},{6,2},{10,6},{... | collective-permute-start | bytes 12296 | tf_op jit(solution)/shard_map/ppermute | solution.py:15
  49.9 1.3 %collective-permute-start.8 = (bf16[128,1,130]{0,2,1:T(8,128)(2,1)S(1)}, bf16[128,1,130]{0,2,1:T(8,128)(2,1)S(1)}, u32[]{:S(2)}, u32[]{:S(2)}) collective-permute-start(bf16[128,1,130]{0,2,1:T(8,128)(2,1)S(1)} %get-tuple-element.44), channel_id=1, source_target_pairs={{0,1},{1,0},{2,3},{3,2},{4,5},{5,4},{6,7},{7,6},{8,9},{9,8},{10,11... | collective-permute-start | bytes 99848 | tf_op jit(solution)/shard_map/ppermute | solution.py:14
  49.9 1.4 %collective-permute-start.9 = (bf16[128,1,130]{0,2,1:T(8,128)(2,1)S(1)}, bf16[128,1,130]{0,2,1:T(8,128)(2,1)S(1)}, u32[]{:S(2)}, u32[]{:S(2)}) collective-permute-start(bf16[128,1,130]{0,2,1:T(8,128)(2,1)S(1)} %get-tuple-element.45), channel_id=1, source_target_pairs={{1,0},{0,1},{3,2},{2,3},{5,4},{4,5},{7,6},{6,7},{9,8},{8,9},{11,10... | collective-permute-start | bytes 99848 | tf_op jit(solution)/shard_map/ppermute | solution.py:15
  50.5 6.4 %collective-permute-start.11 = (f32[1184,128]{1,0:T(8,128)S(1)}, f32[1184,128]{1,0:T(8,128)S(1)}, u32[]{:S(2)}, u32[]{:S(2)}) collective-permute-start(f32[1184,128]{1,0:T(8,128)S(1)} %dynamic-slice_bitcast_fusion), channel_id=1, source_target_pairs={{0,1},{1,0},{2,3},{3,2},{4,5},{5,4},{6,7},{7,6},{8,9},{9,8},{10,11... | collective-permute-start | bytes 1818632 | tf_op jit(solution)/shard_map/ppermute | solution.py:64
  57.0 7.1 %collective-permute-start.12 = (bf16[296,128]{1,0:T(8,128)(2,1)S(1)}, bf16[296,128]{1,0:T(8,128)(2,1)S(1)}, u32[]{:S(2)}, u32[]{:S(2)}) collective-permute-start(bf16[296,128]{1,0:T(8,128)(2,1)S(1)} %get-tuple-element.33), channel_id=1, source_target_pairs={{0,4},{4,8},{8,12},{12,0},{1,5},{5,9},{9,13},{13,1},{2,6},{6,10},{... | collective-permute-start | bytes 227336 | tf_op jit(solution)/shard_map/ppermute | solution.py:64
  58.2 8.6 %collective-permute-start.13 = (bf16[296,128]{1,0:T(8,128)(2,1)S(1)}, bf16[296,128]{1,0:T(8,128)(2,1)S(1)}, u32[]{:S(2)}, u32[]{:S(2)}) collective-permute-start(bf16[296,128]{1,0:T(8,128)(2,1)S(1)} %get-tuple-element.35), channel_id=1, source_target_pairs={{0,8},{4,12},{8,0},{12,4},{1,9},{5,13},{9,1},{13,5},{2,10},{6,14},... | collective-permute-start | bytes 227336 | tf_op jit(solution)/shard_map/ppermute | solution.py:64
  61.1 5.9 %collective-permute-start.14 = (bf16[296,128]{1,0:T(8,128)(2,1)S(1)}, bf16[296,128]{1,0:T(8,128)(2,1)S(1)}, u32[]{:S(2)}, u32[]{:S(2)}) collective-permute-start(bf16[296,128]{1,0:T(8,128)(2,1)S(1)} %get-tuple-element.34), channel_id=1, source_target_pairs={{0,12},{4,0},{8,4},{12,8},{1,13},{5,1},{9,5},{13,9},{2,14},{6,2},{... | collective-permute-start | bytes 227336 | tf_op jit(solution)/shard_map/ppermute | solution.py:64
  67.0 5.5 %collective-permute-start.15 = (bf16[296,128]{1,0:T(8,128)(2,1)S(1)}, bf16[296,128]{1,0:T(8,128)(2,1)S(1)}, u32[]{:S(2)}, u32[]{:S(2)}) collective-permute-start(bf16[296,128]{1,0:T(8,128)(2,1)S(1)} %get-tuple-element.9), channel_id=1, source_target_pairs={{0,12},{4,0},{8,4},{12,8},{1,13},{5,1},{9,5},{13,9},{2,14},{6,2},{... | collective-permute-start | bytes 227336 | tf_op jit(solution)/shard_map/ppermute | solution.py:76
  70.0 13.1 %collective-permute-start.10 = (bf16[128,2048]{1,0:T(8,128)(2,1)S(1)}, bf16[128,2048]{1,0:T(8,128)(2,1)S(1)}, u32[]{:S(2)}, u32[]{:S(2)}) collective-permute-start(bf16[128,2048]{1,0:T(8,128)(2,1)S(1)} %fusion.4), channel_id=1, source_target_pairs={{0,2},{2,0},{1,3},{3,1},{4,6},{6,4},{5,7},{7,5},{8,10},{10,8},{9,1... | collective-permute-start | bytes 1572872 | tf_op jit(solution)/shard_map/ppermute | solution.py:170
  71.5 6.1 %collective-permute-start.16 = (bf16[296,128]{1,0:T(8,128)(2,1)S(1)}, bf16[296,128]{1,0:T(8,128)(2,1)S(1)}, u32[]{:S(2)}, u32[]{:S(2)}) collective-permute-start(bf16[296,128]{1,0:T(8,128)(2,1)S(1)} %get-tuple-element.9), channel_id=1, source_target_pairs={{0,8},{4,12},{8,0},{12,4},{1,9},{5,13},{9,1},{13,5},{2,10},{6,14},... | collective-permute-start | bytes 227336 | tf_op jit(solution)/shard_map/ppermute | solution.py:76
  72.5 6.2 %collective-permute-start.17 = (bf16[296,128]{1,0:T(8,128)(2,1)S(1)}, bf16[296,128]{1,0:T(8,128)(2,1)S(1)}, u32[]{:S(2)}, u32[]{:S(2)}) collective-permute-start(bf16[296,128]{1,0:T(8,128)(2,1)S(1)} %get-tuple-element.9), channel_id=1, source_target_pairs={{0,4},{4,8},{8,12},{12,0},{1,5},{5,9},{9,13},{13,1},{2,6},{6,10},{... | collective-permute-start | bytes 227336 | tf_op jit(solution)/shard_map/ppermute | solution.py:76
  78.8 5.5 %collective-permute-start.18 = (f32[1184,128]{1,0:T(8,128)S(1)}, f32[1184,128]{1,0:T(8,128)S(1)}, u32[]{:S(2)}, u32[]{:S(2)}) collective-permute-start(f32[1184,128]{1,0:T(8,128)S(1)} %bitcast.415), channel_id=1, source_target_pairs={{0,1},{1,0},{2,3},{3,2},{4,5},{5,4},{6,7},{7,6},{8,9},{9,8},{10,11... | collective-permute-start | bytes 1818632 | tf_op jit(solution)/shard_map/ppermute | solution.py:76
  (17 other events, 25.6 us)

commit v5 on v4

--- a/solution.py
+++ b/solution.py
@@ -79,15 +79,15 @@
     return stacked.reshape(-1, chunk.shape[-1])
 
 
-def all_sum(flat, send_dtype):
+def all_sum(rows, send_dtype):
     parts = lax.axis_size("lat") * lax.axis_size("lon")
-    quantum = parts * 8 * 128
-    padded = jnp.pad(flat, (0, (-flat.size) % quantum)).reshape(-1, 128)
-    rows = direct_reduce_scatter(padded, "lat", jnp.float32)
-    rows = direct_reduce_scatter(rows, "lon", send_dtype)
-    rows = direct_all_gather(rows, "lon", send_dtype)
-    rows = direct_all_gather(rows, "lat", jnp.float32)
-    return rows.reshape(-1)[: flat.size]
+    quantum = parts * 8
+    padded = jnp.pad(rows, ((0, (-rows.shape[0]) % quantum), (0, 0)))
+    total = direct_reduce_scatter(padded, "lat", jnp.float32)
+    total = direct_reduce_scatter(total, "lon", send_dtype)
+    total = direct_all_gather(total, "lon", send_dtype)
+    total = direct_all_gather(total, "lat", jnp.float32)
+    return total[: rows.shape[0]]
 
 
 def border_of(padded):
@@ -150,13 +150,13 @@
             pieces.append(
                 lax.dot_general(
                     grad_pre, windows[shift][tap], (((1,), (1,)), ((), ())), preferred_element_type=jnp.float32
-                ).reshape(-1)
+                )
             )
-    flat = jnp.concatenate(pieces + [bias_part])
-    flat = all_sum(flat, jnp.bfloat16)
-    block_size = 9 * own_channels * own_channels
-    weight_local = flat[: chan_count * block_size].reshape(chan_count, 3, 3, own_channels, own_channels)
-    bias_grad = flat[chan_count * block_size :]
+    weight_rows = jnp.concatenate(pieces, axis=0).reshape(-1, 128)
+    bias_rows = jnp.pad(bias_part, (0, (-bias_part.size) % 128)).reshape(-1, 128)
+    summed = all_sum(jnp.concatenate([weight_rows, bias_rows], axis=0), jnp.bfloat16)
+    weight_local = summed[: weight_rows.shape[0]].reshape(chan_count, 3, 3, own_channels, own_channels)
+    bias_grad = summed[weight_rows.shape[0] :].reshape(-1)[: bias_part.size]
     doubled = jnp.concatenate([weight_local, weight_local], axis=0)
     ordered = lax.dynamic_slice_in_dim(doubled, (chan_count - chan_index) % chan_count, chan_count, axis=0)
     weight_grad = jnp.transpose(ordered, (1, 2, 3, 0, 4)).reshape(3, 3, own_channels, chan_count * own_channels)

time: 87.5 us -> 90.7 us (1.037)
  local copies, waits for them, and re-layouts: 12.1 us -> 13.8 us
  starting transfers between devices: 22.9 us -> 21.4 us
  waiting for transfers between devices: 17.4 us -> 18.9 us
  other arithmetic: 3.04 us -> 4.46 us
    reshape x0 -> x3, local copies, waits for them, and re-layouts: none -> 3.38 us  [the longest x1 1.96 us: local(): jnp.transpose(ordered, (1, 2, 3, 0, 4))]
    transpose x1, other arithmetic: 0.22 us -> 1.68 us  [local(): jnp.transpose(ordered, (1, 2, 3, 0, 4))]
    unnamed x65 -> x64, local copies, waits for them, and re-layouts: 5.46 us -> 4.02 us
    ppermute x4, starting transfers between devices: 5.3 us -> 4.06 us  [direct_reduce_scatter(): lax.ppermute(piece.astype(send_dtype), axis, pairs).astype(jnp.float32)]
  transfers between devices with their start and end apart: 19 -> 19, of which waited for: 11 -> 9; matrix products, arithmetic and copies ran while one was open for 18% -> 19% of each run, Pallas kernels for 0% -> 0%
where the time goes in v5:
time: 90.7 us; the launch traced here: 90.3 us
  matrix products  30.3 us (33%)
  starting transfers between devices  21.4 us (24%)
  waiting for transfers between devices  18.9 us (21%)
  local copies, waits for them, and re-layouts  13.8 us (15%)
  other arithmetic  4.46 us (5%)
  between operations  1.42 us (2%)
    dot_general x18, matrix products, local(): lax.dot_general(grad_pre, windows[shift][tap], (((1,), (1,)), ((), ())),...  17.8 us
    dot_general x18, matrix products, local(): jnp.dot(kernel_cols[shift][tap // 3, tap % 3], windows[shift][tap], prefe...  6.8 us
    ppermute x4, waiting for transfers between devices, direct_all_gather(): pieces.append(lax.ppermute(sent, axis, pairs).astype(jnp.float32))  6.32 us
    dot_general x18, matrix products, conv_taps(): jnp.dot(kernel[tap_row, tap_col], window, preferred_element_type=jnp.floa...  5.79 us
    ppermute x4, starting transfers between devices, padded_2(): after = lax.ppermute(initial, axis, down)  5.33 us
    ppermute x4, waiting for transfers between devices, direct_reduce_scatter(): lax.ppermute(piece.astype(send_dtype), axis, pairs).astype(jnp.float32)  5.16 us
    ppermute x4, starting transfers between devices, direct_reduce_scatter(): lax.ppermute(piece.astype(send_dtype), axis, pairs).astype(jnp.float32)  4.06 us
    ppermute x1, waiting for transfers between devices, local(): received.append(lax.ppermute(part.astype(jnp.bfloat16), 'chan', pairs))  4.05 us
  transfers between devices with their start and end apart: 19, of which 9 were waited for; matrix products, arithmetic and copies ran while one was open for 19% of the time, Pallas kernels for 0%

profile of v5, /device:TPU:0, one launch (start us, length us, event | category | flops | bytes accessed | tf_op | source)
XLA Modules:
  0.0 90.3 jit_solution(9205708126725440923)
XLA Ops:
  0.7 1.6 %copy.49 = bf16[128,16,128]{0,2,1:T(8,128)(2,1)S(1)} copy(bf16[128,16,128]{2,1,0:T(8,128)(2,1)} %param.4) | data formatting | bytes 1048576 | tf_op args[0]
  2.2 3.0 %collective-permute-start.5 = (bf16[128,16,128]{0,2,1:T(8,128)(2,1)S(1)}, bf16[128,16,128]{0,2,1:T(8,128)(2,1)S(1)}, u32[]{:S(2)}, u32[]{:S(2)}) collective-permute-start(bf16[128,16,128]{0,2,1:T(8,128)(2,1)S(1)} %copy.49), channel_id=1, source_target_pairs={{0,2},{2,0},{1,3},{3,1},{4,6},{6,4},{5,7},{7,5},{8,10},{10,8},{9,1... | collective-permute-start | bytes 1572872 | tf_op jit(solution)/shard_map/ppermute | solution.py:118
  5.2 1.6 %collective-permute-start = (bf16[128,16,1]{0,2,1:T(2,128)(2,1)S(1)}, bf16[128,16,1]{0,2,1:T(2,128)(2,1)S(1)}, u32[]{:S(2)}, u32[]{:S(2)}) collective-permute-start(bf16[128,16,1]{0,2,1:T(2,128)(2,1)S(1)} %get-tuple-element.48), channel_id=1, source_target_pairs={{0,4},{4,8},{8,12},{12,0},{1,5},{5,9},{9,13},{13,1},{2,6},{6,10},{... | collective-permute-start | bytes 12296 | tf_op jit(solution)/shard_map/ppermute | solution.py:14
  6.9 2.2 %collective-permute-start.1 = (bf16[128,16,1]{0,2,1:T(2,128)(2,1)S(1)}, bf16[128,16,1]{0,2,1:T(2,128)(2,1)S(1)}, u32[]{:S(2)}, u32[]{:S(2)}) collective-permute-start(bf16[128,16,1]{0,2,1:T(2,128)(2,1)S(1)} %get-tuple-element.49), channel_id=1, source_target_pairs={{4,0},{8,4},{12,8},{0,12},{5,1},{9,5},{13,9},{1,13},{6,2},{10,6},{... | collective-permute-start | bytes 12296 | tf_op jit(solution)/shard_map/ppermute | solution.py:15
  9.1 1.1 %bitcast_convert_fusion = f32[16,8,16,128]{3,2,1,0:T(8,128)} fusion(bf16[128,16,128]{2,1,0:T(8,128)(2,1)S(1)} %copy-done.28), kind=kLoop, calls=%fused_computation.187 | loop fusion | flops 262144 | bytes 1572864
  17.0 1.8 %collective-permute-done.4 = bf16[128,292]{0,1:T(8,128)(2,1)S(1)} collective-permute-done((bf16[128,292]{0,1:T(8,128)(2,1)S(1)}, bf16[128,292]{0,1:T(8,128)(2,1)S(1)}, u32[]{:S(2)}, u32[]{:S(2)}) %collective-permute-start.4) | collective-permute-done | bytes 74784 | tf_op jit(solution)/shard_map/ppermute | solution.py:124
  24.1 1.7 %convert_reduce_fusion = (f32[128]{0:T(128)S(1)}, bf16[128,2048]{1,0:T(8,128)(2,1)S(1)}) fusion(f32[128]{0:T(128)S(1)} %copy-done.29, f32[128,2048]{1,0:T(8,128)S(1)} %convolution_add_fusion.17, bf16[128,2048]{0,1:T(8,128)(2,1)S(1)} %bitcast.346, bf16[3,3,128,256]{3,2,1,0:T(8,128)(2,1)} %param.6, s32[]{:T(128)S(6)} %add.291, s32[]{:T(128)S(6)} %select_n.97, ...), kind=kOutput, calls=%fused_computation.71 | convolution fusion | flops 70778752 | bytes 3179528 | tf_op jit(solution)/shard_map/dot_general | solution.py:139
  25.8 0.9 %convolution_dynamic-update-slice_fusion.17 = f32[2305,128]{1,0:T(8,128)} fusion(bf16[128,2048]{1,0:T(8,128)(2,1)S(1)} %get-tuple-element.55, bf16[128,2048]{0,1:T(8,128)(2,1)S(1)} %bitcast.312), kind=kOutput, calls=%fused_computation.64 | convolution fusion | flops 67108864 | bytes 1114112 | tf_op jit(solution)/shard_map/dot_general | solution.py:151
  27.0 2.0 %convolution_dynamic-update-slice_fusion.16 = f32[2305,128]{1,0:T(8,128)} fusion(f32[2305,128]{1,0:T(8,128)} %convolution_dynamic-update-slice_fusion.17, bf16[128,2048]{1,0:T(8,128)(2,1)S(1)} %get-tuple-element.55, bf16[128,2048]{0,1:T(8,128)(2,1)} %bitcast.306), kind=kOutput, calls=%fused_computation.63 | convolution fusion | flops 67108864 | bytes 1114112 | tf_op jit(solution)/shard_map/dot_general | solution.py:151
  30.0 0.9 %convolution_dynamic-update-slice_fusion.14 = f32[2305,128]{1,0:T(8,128)} fusion(f32[2305,128]{1,0:T(8,128)} %convolution_dynamic-update-slice_fusion.15, bf16[128,2048]{1,0:T(8,128)(2,1)S(1)} %get-tuple-element.55, bf16[128,2048]{0,1:T(8,128)(2,1)S(1)} %bitcast.302), kind=kOutput, calls=%fused_computation.61 | convolution fusion | flops 67108864 | bytes 1114112 | tf_op jit(solution)/shard_map/dot_general | solution.py:151
  33.6 0.9 %convolution_dynamic-update-slice_fusion.10 = f32[2305,128]{1,0:T(8,128)} fusion(f32[2305,128]{1,0:T(8,128)} %convolution_dynamic-update-slice_fusion.11, bf16[128,2048]{1,0:T(8,128)(2,1)S(1)} %get-tuple-element.55, bf16[128,2048]{0,1:T(8,128)(2,1)S(1)} %bitcast.315), kind=kOutput, calls=%fused_computation.57 | convolution fusion | flops 67108864 | bytes 1114112 | tf_op jit(solution)/shard_map/dot_general | solution.py:151
  35.5 0.9 %convolution_dynamic-update-slice_fusion.8 = f32[2305,128]{1,0:T(8,128)} fusion(f32[2305,128]{1,0:T(8,128)} %convolution_dynamic-update-slice_fusion.9, bf16[128,2048]{1,0:T(8,128)(2,1)S(1)} %get-tuple-element.55, bf16[128,2048]{0,1:T(8,128)(2,1)S(1)} %bitcast.343), kind=kOutput, calls=%fused_computation.55 | convolution fusion | flops 67108864 | bytes 1114112 | tf_op jit(solution)/shard_map/dot_general | solution.py:151
  36.4 0.9 %convolution_dynamic-update-slice_fusion.7 = f32[2305,128]{1,0:T(8,128)} fusion(f32[2305,128]{1,0:T(8,128)} %convolution_dynamic-update-slice_fusion.8, bf16[128,2048]{1,0:T(8,128)(2,1)S(1)} %get-tuple-element.55, bf16[128,2048]{0,1:T(8,128)(2,1)S(1)} %bitcast.321), kind=kOutput, calls=%fused_computation.54 | convolution fusion | flops 67108864 | bytes 1114112 | tf_op jit(solution)/shard_map/dot_general | solution.py:151
  37.3 0.9 %convolution_dynamic-update-slice_fusion.6 = f32[2305,128]{1,0:T(8,128)} fusion(f32[2305,128]{1,0:T(8,128)} %convolution_dynamic-update-slice_fusion.7, bf16[128,2048]{1,0:T(8,128)(2,1)S(1)} %get-tuple-element.55, bf16[128,2048]{0,1:T(8,128)(2,1)S(1)} %bitcast.319), kind=kOutput, calls=%fused_computation.53 | convolution fusion | flops 67108864 | bytes 1114112 | tf_op jit(solution)/shard_map/dot_general | solution.py:151
  40.0 0.9 %convolution_dynamic-update-slice_fusion.3 = f32[2305,128]{1,0:T(8,128)} fusion(f32[2305,128]{1,0:T(8,128)} %convolution_dynamic-update-slice_fusion.4, bf16[128,2048]{1,0:T(8,128)(2,1)S(1)} %get-tuple-element.55, bf16[128,2048]{0,1:T(8,128)(2,1)S(1)} %bitcast.308), kind=kOutput, calls=%fused_computation.50 | convolution fusion | flops 67108864 | bytes 1114112 | tf_op jit(solution)/shard_map/dot_general | solution.py:151
  41.0 1.1 %convolution_dynamic-update-slice_fusion.2 = f32[2305,128]{1,0:T(8,128)} fusion(f32[2305,128]{1,0:T(8,128)} %convolution_dynamic-update-slice_fusion.3, bf16[128,2048]{1,0:T(8,128)(2,1)S(1)} %get-tuple-element.55, bf16[128,2048]{0,1:T(8,128)(2,1)S(1)} %bitcast.341), kind=kOutput, calls=%fused_computation.49 | convolution fusion | flops 67108864 | bytes 1114112 | tf_op jit(solution)/shard_map/dot_general | solution.py:151
  42.1 0.9 %convolution_dynamic-update-slice_fusion.1 = f32[2305,128]{1,0:T(8,128)} fusion(f32[2305,128]{1,0:T(8,128)} %convolution_dynamic-update-slice_fusion.2, bf16[128,2048]{1,0:T(8,128)(2,1)S(1)} %get-tuple-element.55, bf16[128,2048]{0,1:T(8,128)(2,1)S(1)} %bitcast.339), kind=kOutput, calls=%fused_computation.48 | convolution fusion | flops 67108864 | bytes 1114112 | tf_op jit(solution)/shard_map/dot_general | solution.py:151
  43.0 1.9 %collective-permute-start.6 = (bf16[128,16,1]{0,2,1:T(2,128)(2,1)S(1)}, bf16[128,16,1]{0,2,1:T(2,128)(2,1)S(1)}, u32[]{:S(2)}, u32[]{:S(2)}) collective-permute-start(bf16[128,16,1]{0,2,1:T(2,128)(2,1)S(1)} %get-tuple-element.44), channel_id=1, source_target_pairs={{0,4},{4,8},{8,12},{12,0},{1,5},{5,9},{9,13},{13,1},{2,6},{6,10},{... | collective-permute-start | bytes 12296 | tf_op jit(solution)/shard_map/ppermute | solution.py:14
  44.9 2.1 %collective-permute-start.7 = (bf16[128,16,1]{0,2,1:T(2,128)(2,1)S(1)}, bf16[128,16,1]{0,2,1:T(2,128)(2,1)S(1)}, u32[]{:S(2)}, u32[]{:S(2)}) collective-permute-start(bf16[128,16,1]{0,2,1:T(2,128)(2,1)S(1)} %get-tuple-element.45), channel_id=1, source_target_pairs={{4,0},{8,4},{12,8},{0,12},{5,1},{9,5},{13,9},{1,13},{6,2},{10,6},{... | collective-permute-start | bytes 12296 | tf_op jit(solution)/shard_map/ppermute | solution.py:15
  47.9 1.3 %dynamic-update-slice.26 = f32[2305,128]{1,0:T(8,128)} dynamic-update-slice(f32[2305,128]{1,0:T(8,128)} %convolution_dynamic-update-slice_fusion, f32[1,128]{1,0:T(1,128)S(1)} %bitcast.352, s32[]{} %constant.158, s32[]{} %constant.133) | dynamic-update-slice | bytes 1028 | tf_op jit(solution)/shard_map/concatenate | solution.py:157
  49.2 1.4 %pad.4 = f32[2368,128]{1,0:T(8,128)S(1)} pad(f32[2305,128]{1,0:T(8,128)} %dynamic-update-slice.26, f32[]{:T(128)} %constant.122.clone.1), padding=0_63x0_0 | pad | bytes 2392580 | tf_op jit(solution)/shard_map/jit(_pad)/pad | solution.py:85
  52.4 0.9 %fusion.48 = (bf16[128,16,128]{0,2,1:T(8,128)(2,1)S(1)}, bf16[128,16,128]{0,2,1:T(8,128)(2,1)S(1)}, bf16[128,16,128]{0,2,1:T(8,128)(2,1)S(1)}, bf16[128,16,128]{...) fusion(bf16[128,18,130]{0,2,1:T(8,128)(2,1)S(1)} %maximum_selec, ...), kind=kLoop, calls=%fused_computation.180 | loop fusion | bytes 9437184 | tf_op jit(solution)/shard_map/slice | solution.py:37
  57.8 2.5 %collective-permute-start.13 = (bf16[296,128]{1,0:T(8,128)(2,1)S(1)}, bf16[296,128]{1,0:T(8,128)(2,1)S(1)}, u32[]{:S(2)}, u32[]{:S(2)}) collective-permute-start(bf16[296,128]{1,0:T(8,128)(2,1)S(1)} %get-tuple-element.29), channel_id=1, source_target_pairs={{0,8},{4,12},{8,0},{12,4},{1,9},{5,13},{9,1},{13,5},{2,10},{6,14},... | collective-permute-start | bytes 227336 | tf_op jit(solution)/shard_map/ppermute | solution.py:64
  60.3 1.3 %collective-permute-start.14 = (bf16[296,128]{1,0:T(8,128)(2,1)S(1)}, bf16[296,128]{1,0:T(8,128)(2,1)S(1)}, u32[]{:S(2)}, u32[]{:S(2)}) collective-permute-start(bf16[296,128]{1,0:T(8,128)(2,1)S(1)} %get-tuple-element.28), channel_id=1, source_target_pairs={{0,12},{4,0},{8,4},{12,8},{1,13},{5,1},{9,5},{13,9},{2,14},{6,2},{... | collective-permute-start | bytes 227336 | tf_op jit(solution)/shard_map/ppermute | solution.py:64
  62.0 2.8 %collective-permute-done.12 = bf16[296,128]{1,0:T(8,128)(2,1)S(1)} collective-permute-done((bf16[296,128]{1,0:T(8,128)(2,1)S(1)}, bf16[296,128]{1,0:T(8,128)(2,1)S(1)}, u32[]{:S(2)}, u32[]{:S(2)}) %collective-permute-start.12) | collective-permute-done | bytes 75808 | tf_op jit(solution)/shard_map/ppermute | solution.py:64
  64.8 2.3 %collective-permute-done.13 = bf16[296,128]{1,0:T(8,128)(2,1)S(1)} collective-permute-done((bf16[296,128]{1,0:T(8,128)(2,1)S(1)}, bf16[296,128]{1,0:T(8,128)(2,1)S(1)}, u32[]{:S(2)}, u32[]{:S(2)}) %collective-permute-start.13) | collective-permute-done | bytes 75808 | tf_op jit(solution)/shard_map/ppermute | solution.py:64
  67.2 2.6 %collective-permute-start.15 = (bf16[296,128]{1,0:T(8,128)(2,1)S(1)}, bf16[296,128]{1,0:T(8,128)(2,1)S(1)}, u32[]{:S(2)}, u32[]{:S(2)}) collective-permute-start(bf16[296,128]{1,0:T(8,128)(2,1)S(1)} %get-tuple-element.3), channel_id=1, source_target_pairs={{0,12},{4,0},{8,4},{12,8},{1,13},{5,1},{9,5},{13,9},{2,14},{6,2},{... | collective-permute-start | bytes 227336 | tf_op jit(solution)/shard_map/ppermute | solution.py:76
  70.1 1.6 %collective-permute-start.10 = (bf16[128,2048]{1,0:T(8,128)(2,1)S(1)}, bf16[128,2048]{1,0:T(8,128)(2,1)S(1)}, u32[]{:S(2)}, u32[]{:S(2)}) collective-permute-start(bf16[128,2048]{1,0:T(8,128)(2,1)S(1)} %fusion.4), channel_id=1, source_target_pairs={{0,2},{2,0},{1,3},{3,1},{4,6},{6,4},{5,7},{7,5},{8,10},{10,8},{9,1... | collective-permute-start | bytes 1572872 | tf_op jit(solution)/shard_map/ppermute | solution.py:170
  72.4 6.3 %collective-permute-done.16 = bf16[296,128]{1,0:T(8,128)(2,1)S(1)} collective-permute-done((bf16[296,128]{1,0:T(8,128)(2,1)S(1)}, bf16[296,128]{1,0:T(8,128)(2,1)S(1)}, u32[]{:S(2)}, u32[]{:S(2)}) %collective-permute-start.16) | collective-permute-done | bytes 75808 | tf_op jit(solution)/shard_map/ppermute | solution.py:76
  79.6 4.1 %collective-permute-done.10 = bf16[128,2048]{1,0:T(8,128)(2,1)S(1)} collective-permute-done((bf16[128,2048]{1,0:T(8,128)(2,1)S(1)}, bf16[128,2048]{1,0:T(8,128)(2,1)S(1)}, u32[]{:S(2)}, u32[]{:S(2)}) %collective-permute-start.10) | collective-permute-done | bytes 524320 | tf_op jit(solution)/shard_map/ppermute | solution.py:170
  86.7 1.7 %fusion.9 = f32[3,3,128,2,128]{4,3,2,1,0:T(2,128)S(1)} fusion(s32[]{:T(128)S(6)} %select_n.114, f32[2,3,3,128,128]{4,0,3,2,1:T(2,128)S(1)} %copy.60), kind=kLoop, calls=%fused_computation.46 | loop fusion | flops 294912 | bytes 2359300 | tf_op jit(solution)/shard_map/transpose | solution.py:162
  88.4 2.0 %reshape.177 = f32[3,3,128,256]{3,2,1,0:T(8,128)} reshape(f32[3,3,128,2,128]{4,3,2,1,0:T(2,128)S(1)} %fusion.9) | data formatting | bytes 2359296 | tf_op jit(solution)/shard_map/reshape | solution.py:162
  (167 shorter events, 30.7 us)
Async XLA Ops:
  0.6 8.5 %copy-start.28 = (bf16[128,16,128]{2,1,0:T(8,128)(2,1)S(1)}, bf16[128,16,128]{2,1,0:T(8,128)(2,1)}, u32[]{:S(2)}) copy-start(bf16[128,16,128]{2,1,0:T(8,128)(2,1)} %param.5) | copy-start | bytes 1572868
  0.6 9.6 %copy-start.23 = (bf16[3,3,128,256]{3,2,1,0:T(8,128)(2,1)S(1)}, bf16[3,3,128,256]{3,2,1,0:T(8,128)(2,1)}, u32[]{:S(2)}) copy-start(bf16[3,3,128,256]{3,2,1,0:T(8,128)(2,1)} %param.6) | copy-start | bytes 1769476
  2.2 16.6 %collective-permute-start.5 = (bf16[128,16,128]{0,2,1:T(8,128)(2,1)S(1)}, bf16[128,16,128]{0,2,1:T(8,128)(2,1)S(1)}, u32[]{:S(2)}, u32[]{:S(2)}) collective-permute-start(bf16[128,16,128]{0,2,1:T(8,128)(2,1)S(1)} %copy.49), channel_id=1, source_target_pairs={{0,2},{2,0},{1,3},{3,1},{4,6},{6,4},{5,7},{7,5},{8,10},{10,8},{9,1... | collective-permute-start | bytes 1572872 | tf_op jit(solution)/shard_map/ppermute | solution.py:118
  5.2 5.8 %collective-permute-start = (bf16[128,16,1]{0,2,1:T(2,128)(2,1)S(1)}, bf16[128,16,1]{0,2,1:T(2,128)(2,1)S(1)}, u32[]{:S(2)}, u32[]{:S(2)}) collective-permute-start(bf16[128,16,1]{0,2,1:T(2,128)(2,1)S(1)} %get-tuple-element.48), channel_id=1, source_target_pairs={{0,4},{4,8},{8,12},{12,0},{1,5},{5,9},{9,13},{13,1},{2,6},{6,10},{... | collective-permute-start | bytes 12296 | tf_op jit(solution)/shard_map/ppermute | solution.py:14
  6.9 4.2 %collective-permute-start.1 = (bf16[128,16,1]{0,2,1:T(2,128)(2,1)S(1)}, bf16[128,16,1]{0,2,1:T(2,128)(2,1)S(1)}, u32[]{:S(2)}, u32[]{:S(2)}) collective-permute-start(bf16[128,16,1]{0,2,1:T(2,128)(2,1)S(1)} %get-tuple-element.49), channel_id=1, source_target_pairs={{4,0},{8,4},{12,8},{0,12},{5,1},{9,5},{13,9},{1,13},{6,2},{10,6},{... | collective-permute-start | bytes 12296 | tf_op jit(solution)/shard_map/ppermute | solution.py:15
  11.1 1.3 %collective-permute-start.2 = (bf16[128,1,130]{0,2,1:T(8,128)(2,1)S(1)}, bf16[128,1,130]{0,2,1:T(8,128)(2,1)S(1)}, u32[]{:S(2)}, u32[]{:S(2)}) collective-permute-start(bf16[128,1,130]{0,2,1:T(8,128)(2,1)S(1)} %get-tuple-element.42), channel_id=1, source_target_pairs={{0,1},{1,0},{2,3},{3,2},{4,5},{5,4},{6,7},{7,6},{8,9},{9,8},{10,11... | collective-permute-start | bytes 99848 | tf_op jit(solution)/shard_map/ppermute | solution.py:14
  11.2 1.4 %collective-permute-start.3 = (bf16[128,1,130]{0,2,1:T(8,128)(2,1)S(1)}, bf16[128,1,130]{0,2,1:T(8,128)(2,1)S(1)}, u32[]{:S(2)}, u32[]{:S(2)}) collective-permute-start(bf16[128,1,130]{0,2,1:T(8,128)(2,1)S(1)} %get-tuple-element.43), channel_id=1, source_target_pairs={{1,0},{0,1},{3,2},{2,3},{5,4},{4,5},{7,6},{6,7},{9,8},{8,9},{11,10... | collective-permute-start | bytes 99848 | tf_op jit(solution)/shard_map/ppermute | solution.py:15
  13.6 2.1 %copy-start.11 = (bf16[128,16,128]{0,2,1:T(8,128)(2,1)}, bf16[128,16,128]{0,2,1:T(8,128)(2,1)S(1)}, u32[]{:S(2)}) copy-start(bf16[128,16,128]{0,2,1:T(8,128)(2,1)S(1)} %get-tuple-element.17) | copy-start | bytes 1572868
  13.6 2.7 %copy-start.9 = (bf16[128,16,128]{0,2,1:T(8,128)(2,1)}, bf16[128,16,128]{0,2,1:T(8,128)(2,1)S(1)}, u32[]{:S(2)}) copy-start(bf16[128,16,128]{0,2,1:T(8,128)(2,1)S(1)} %get-tuple-element.15) | copy-start | bytes 1572868
  14.0 4.7 %collective-permute-start.4 = (bf16[128,292]{0,1:T(8,128)(2,1)S(1)}, bf16[128,292]{0,1:T(8,128)(2,1)S(1)}, u32[]{:S(2)}, u32[]{:S(2)}) collective-permute-start(bf16[128,292]{0,1:T(8,128)(2,1)S(1)} %pad_maximum_fusion.3), channel_id=1, source_target_pairs={{0,2},{2,0},{1,3},{3,1},{4,6},{6,4},{5,7},{7,5},{8,10},{10,8},{9,1... | collective-permute-start | bytes 224264 | tf_op jit(solution)/shard_map/ppermute | solution.py:124
  19.4 2.1 %copy-start.21 = (bf16[128,16,128]{0,2,1:T(8,128)(2,1)}, bf16[128,16,128]{0,2,1:T(8,128)(2,1)S(1)}, u32[]{:S(2)}) copy-start(bf16[128,16,128]{0,2,1:T(8,128)(2,1)S(1)} %get-tuple-element.35) | copy-start | bytes 1572868
  19.5 2.4 %copy-start.15 = (bf16[128,16,128]{0,2,1:T(8,128)(2,1)}, bf16[128,16,128]{0,2,1:T(8,128)(2,1)S(1)}, u32[]{:S(2)}) copy-start(bf16[128,16,128]{0,2,1:T(8,128)(2,1)S(1)} %get-tuple-element.34) | copy-start | bytes 1572868
  19.5 2.7 %copy-start.13 = (bf16[128,16,128]{0,2,1:T(8,128)(2,1)}, bf16[128,16,128]{0,2,1:T(8,128)(2,1)S(1)}, u32[]{:S(2)}) copy-start(bf16[128,16,128]{0,2,1:T(8,128)(2,1)S(1)} %get-tuple-element.33) | copy-start | bytes 1572868
  19.8 2.8 %copy-start.7 = (bf16[128,16,128]{0,2,1:T(8,128)(2,1)}, bf16[128,16,128]{0,2,1:T(8,128)(2,1)S(1)}, u32[]{:S(2)}) copy-start(bf16[128,16,128]{0,2,1:T(8,128)(2,1)S(1)} %get-tuple-element.46) | copy-start | bytes 1572868
  20.8 2.1 %copy-start.17 = (bf16[128,16,128]{0,2,1:T(8,128)(2,1)}, bf16[128,16,128]{0,2,1:T(8,128)(2,1)S(1)}, u32[]{:S(2)}) copy-start(bf16[128,16,128]{0,2,1:T(8,128)(2,1)S(1)} %get-tuple-element.31) | copy-start | bytes 1572868
  20.8 2.5 %copy-start.24 = (bf16[128,16,128]{0,2,1:T(8,128)(2,1)}, bf16[128,16,128]{0,2,1:T(8,128)(2,1)S(1)}, u32[]{:S(2)}) copy-start(bf16[128,16,128]{0,2,1:T(8,128)(2,1)S(1)} %get-tuple-element.30) | copy-start | bytes 1572868
  27.0 2.1 %copy-start.3 = (bf16[128,16,128]{0,2,1:T(8,128)(2,1)S(1)}, bf16[128,16,128]{0,2,1:T(8,128)(2,1)}, u32[]{:S(2)}) copy-start(bf16[128,16,128]{0,2,1:T(8,128)(2,1)} %copy-done.2) | copy-start | bytes 1572868
  27.0 3.0 %copy-start.1 = (bf16[128,16,128]{0,2,1:T(8,128)(2,1)S(1)}, bf16[128,16,128]{0,2,1:T(8,128)(2,1)}, u32[]{:S(2)}) copy-start(bf16[128,16,128]{0,2,1:T(8,128)(2,1)} %copy-done) | copy-start | bytes 1572868
  41.0 6.0 %copy-start.25 = (bf16[128,16,128]{0,2,1:T(8,128)(2,1)S(1)}, bf16[128,16,128]{0,2,1:T(8,128)(2,1)}, u32[]{:S(2)}) copy-start(bf16[128,16,128]{0,2,1:T(8,128)(2,1)} %copy-done.24) | copy-start | bytes 1572868
  43.0 7.5 %collective-permute-start.6 = (bf16[128,16,1]{0,2,1:T(2,128)(2,1)S(1)}, bf16[128,16,1]{0,2,1:T(2,128)(2,1)S(1)}, u32[]{:S(2)}, u32[]{:S(2)}) collective-permute-start(bf16[128,16,1]{0,2,1:T(2,128)(2,1)S(1)} %get-tuple-element.44), channel_id=1, source_target_pairs={{0,4},{4,8},{8,12},{12,0},{1,5},{5,9},{9,13},{13,1},{2,6},{6,10},{... | collective-permute-start | bytes 12296 | tf_op jit(solution)/shard_map/ppermute | solution.py:14
  44.9 5.7 %collective-permute-start.7 = (bf16[128,16,1]{0,2,1:T(2,128)(2,1)S(1)}, bf16[128,16,1]{0,2,1:T(2,128)(2,1)S(1)}, u32[]{:S(2)}, u32[]{:S(2)}) collective-permute-start(bf16[128,16,1]{0,2,1:T(2,128)(2,1)S(1)} %get-tuple-element.45), channel_id=1, source_target_pairs={{4,0},{8,4},{12,8},{0,12},{5,1},{9,5},{13,9},{1,13},{6,2},{10,6},{... | collective-permute-start | bytes 12296 | tf_op jit(solution)/shard_map/ppermute | solution.py:15
  50.6 1.3 %collective-permute-start.8 = (bf16[128,1,130]{0,2,1:T(8,128)(2,1)S(1)}, bf16[128,1,130]{0,2,1:T(8,128)(2,1)S(1)}, u32[]{:S(2)}, u32[]{:S(2)}) collective-permute-start(bf16[128,1,130]{0,2,1:T(8,128)(2,1)S(1)} %get-tuple-element.38), channel_id=1, source_target_pairs={{0,1},{1,0},{2,3},{3,2},{4,5},{5,4},{6,7},{7,6},{8,9},{9,8},{10,11... | collective-permute-start | bytes 99848 | tf_op jit(solution)/shard_map/ppermute | solution.py:14
  50.7 1.4 %collective-permute-start.9 = (bf16[128,1,130]{0,2,1:T(8,128)(2,1)S(1)}, bf16[128,1,130]{0,2,1:T(8,128)(2,1)S(1)}, u32[]{:S(2)}, u32[]{:S(2)}) collective-permute-start(bf16[128,1,130]{0,2,1:T(8,128)(2,1)S(1)} %get-tuple-element.39), channel_id=1, source_target_pairs={{1,0},{0,1},{3,2},{2,3},{5,4},{4,5},{7,6},{6,7},{9,8},{8,9},{11,10... | collective-permute-start | bytes 99848 | tf_op jit(solution)/shard_map/ppermute | solution.py:15
  51.2 6.4 %collective-permute-start.11 = (f32[1184,128]{1,0:T(8,128)S(1)}, f32[1184,128]{1,0:T(8,128)S(1)}, u32[]{:S(2)}, u32[]{:S(2)}) collective-permute-start(f32[1184,128]{1,0:T(8,128)S(1)} %dynamic-slice_bitcast_fusion), channel_id=1, source_target_pairs={{0,1},{1,0},{2,3},{3,2},{4,5},{5,4},{6,7},{7,6},{8,9},{9,8},{10,11... | collective-permute-start | bytes 1818632 | tf_op jit(solution)/shard_map/ppermute | solution.py:64
  57.7 7.1 %collective-permute-start.12 = (bf16[296,128]{1,0:T(8,128)(2,1)S(1)}, bf16[296,128]{1,0:T(8,128)(2,1)S(1)}, u32[]{:S(2)}, u32[]{:S(2)}) collective-permute-start(bf16[296,128]{1,0:T(8,128)(2,1)S(1)} %get-tuple-element.27), channel_id=1, source_target_pairs={{0,4},{4,8},{8,12},{12,0},{1,5},{5,9},{9,13},{13,1},{2,6},{6,10},{... | collective-permute-start | bytes 227336 | tf_op jit(solution)/shard_map/ppermute | solution.py:64
  57.8 9.3 %collective-permute-start.13 = (bf16[296,128]{1,0:T(8,128)(2,1)S(1)}, bf16[296,128]{1,0:T(8,128)(2,1)S(1)}, u32[]{:S(2)}, u32[]{:S(2)}) collective-permute-start(bf16[296,128]{1,0:T(8,128)(2,1)S(1)} %get-tuple-element.29), channel_id=1, source_target_pairs={{0,8},{4,12},{8,0},{12,4},{1,9},{5,13},{9,1},{13,5},{2,10},{6,14},... | collective-permute-start | bytes 227336 | tf_op jit(solution)/shard_map/ppermute | solution.py:64
  60.3 6.8 %collective-permute-start.14 = (bf16[296,128]{1,0:T(8,128)(2,1)S(1)}, bf16[296,128]{1,0:T(8,128)(2,1)S(1)}, u32[]{:S(2)}, u32[]{:S(2)}) collective-permute-start(bf16[296,128]{1,0:T(8,128)(2,1)S(1)} %get-tuple-element.28), channel_id=1, source_target_pairs={{0,12},{4,0},{8,4},{12,8},{1,13},{5,1},{9,5},{13,9},{2,14},{6,2},{... | collective-permute-start | bytes 227336 | tf_op jit(solution)/shard_map/ppermute | solution.py:64
  67.2 5.2 %collective-permute-start.15 = (bf16[296,128]{1,0:T(8,128)(2,1)S(1)}, bf16[296,128]{1,0:T(8,128)(2,1)S(1)}, u32[]{:S(2)}, u32[]{:S(2)}) collective-permute-start(bf16[296,128]{1,0:T(8,128)(2,1)S(1)} %get-tuple-element.3), channel_id=1, source_target_pairs={{0,12},{4,0},{8,4},{12,8},{1,13},{5,1},{9,5},{13,9},{2,14},{6,2},{... | collective-permute-start | bytes 227336 | tf_op jit(solution)/shard_map/ppermute | solution.py:76
  70.1 13.6 %collective-permute-start.10 = (bf16[128,2048]{1,0:T(8,128)(2,1)S(1)}, bf16[128,2048]{1,0:T(8,128)(2,1)S(1)}, u32[]{:S(2)}, u32[]{:S(2)}) collective-permute-start(bf16[128,2048]{1,0:T(8,128)(2,1)S(1)} %fusion.4), channel_id=1, source_target_pairs={{0,2},{2,0},{1,3},{3,1},{4,6},{6,4},{5,7},{7,5},{8,10},{10,8},{9,1... | collective-permute-start | bytes 1572872 | tf_op jit(solution)/shard_map/ppermute | solution.py:170
  71.7 7.0 %collective-permute-start.16 = (bf16[296,128]{1,0:T(8,128)(2,1)S(1)}, bf16[296,128]{1,0:T(8,128)(2,1)S(1)}, u32[]{:S(2)}, u32[]{:S(2)}) collective-permute-start(bf16[296,128]{1,0:T(8,128)(2,1)S(1)} %get-tuple-element.3), channel_id=1, source_target_pairs={{0,8},{4,12},{8,0},{12,4},{1,9},{5,13},{9,1},{13,5},{2,10},{6,14},... | collective-permute-start | bytes 227336 | tf_op jit(solution)/shard_map/ppermute | solution.py:76
  72.4 6.4 %collective-permute-start.17 = (bf16[296,128]{1,0:T(8,128)(2,1)S(1)}, bf16[296,128]{1,0:T(8,128)(2,1)S(1)}, u32[]{:S(2)}, u32[]{:S(2)}) collective-permute-start(bf16[296,128]{1,0:T(8,128)(2,1)S(1)} %get-tuple-element.3), channel_id=1, source_target_pairs={{0,4},{4,8},{8,12},{12,0},{1,5},{5,9},{9,13},{13,1},{2,6},{6,10},{... | collective-permute-start | bytes 227336 | tf_op jit(solution)/shard_map/ppermute | solution.py:76
  78.9 6.0 %collective-permute-start.18 = (f32[1184,128]{1,0:T(8,128)S(1)}, f32[1184,128]{1,0:T(8,128)S(1)}, u32[]{:S(2)}, u32[]{:S(2)}) collective-permute-start(f32[1184,128]{1,0:T(8,128)S(1)} %bitcast.344), channel_id=1, source_target_pairs={{0,1},{1,0},{2,3},{3,2},{4,5},{5,4},{6,7},{7,6},{8,9},{9,8},{10,11... | collective-permute-start | bytes 1818632 | tf_op jit(solution)/shard_map/ppermute | solution.py:76
  (17 other events, 25.8 us)

commit v6 on v5

--- a/solution.py
+++ b/solution.py
@@ -144,22 +144,22 @@
     upstream = cotangent.reshape(own_channels, -1).astype(jnp.float32)
     grad_pre = (upstream * gelu_slope(preact)).astype(jnp.bfloat16)
     bias_part = jnp.sum(grad_pre.astype(jnp.float32), axis=1)
-    pieces = []
-    for shift in range(chan_count):
-        for tap in range(9):
-            pieces.append(
-                lax.dot_general(
-                    grad_pre, windows[shift][tap], (((1,), (1,)), ((), ())), preferred_element_type=jnp.float32
-                )
-            )
-    weight_rows = jnp.concatenate(pieces, axis=0).reshape(-1, 128)
+    input_local = jnp.concatenate(blocks, axis=0)
+    taps = []
+    for tap in range(9):
+        window = window_of(input_local, tap // 3, tap % 3, row_count, column_count)
+        taps.append(
+            lax.dot_general(grad_pre, window, (((1,), (1,)), ((), ())), preferred_element_type=jnp.float32)
+        )
+    weight_rows = jnp.stack(taps).reshape(-1, 128)
     bias_rows = jnp.pad(bias_part, (0, (-bias_part.size) % 128)).reshape(-1, 128)
     summed = all_sum(jnp.concatenate([weight_rows, bias_rows], axis=0), jnp.bfloat16)
-    weight_local = summed[: weight_rows.shape[0]].reshape(chan_count, 3, 3, own_channels, own_channels)
+    weight_local = summed[: weight_rows.shape[0]].reshape(3, 3, own_channels, chan_count * own_channels)
     bias_grad = summed[weight_rows.shape[0] :].reshape(-1)[: bias_part.size]
-    doubled = jnp.concatenate([weight_local, weight_local], axis=0)
-    ordered = lax.dynamic_slice_in_dim(doubled, (chan_count - chan_index) % chan_count, chan_count, axis=0)
-    weight_grad = jnp.transpose(ordered, (1, 2, 3, 0, 4)).reshape(3, 3, own_channels, chan_count * own_channels)
+    doubled = jnp.concatenate([weight_local, weight_local], axis=3)
+    weight_grad = lax.dynamic_slice_in_dim(
+        doubled, (chan_count - chan_index) % chan_count * own_channels, chan_count * own_channels, axis=3
+    )
     grad_field = grad_pre.reshape(own_channels, row_count, column_count)
     grad_pad = mask_rims(padded_2(grad_field, (("lon", 2), ("lat", 1)), 1))
     received = []

time: 90.7 us -> 87.5 us (0.965)
  matrix products: 30.3 us -> 26.6 us
  starting transfers between devices: 21.4 us -> 23.2 us
    dot_general x18 -> x9, matrix products: 17.8 us -> 10 us  [local(): lax.dot_general(grad_pre, window, (((1,), (1,)), ((), ())), preferred_ele...]
    slice x4 -> x5, local copies, waits for them, and re-layouts: 2.35 us -> 6.35 us  [window_of(): field[:, first_row:first_row + row_count, first_col:first_col + column_co...]
    dot_general x18, matrix products: 6.8 us -> 10.7 us  [local(): jnp.dot(kernel_cols[shift][tap // 3, tap % 3], windows[shift][tap], prefe...]
    transpose x1 -> x0, other arithmetic: 1.68 us -> none  [local(): jnp.transpose(ordered, (1, 2, 3, 0, 4))]
    concatenate x0 -> x3, other arithmetic: none -> 1.62 us  [the longest x1 1.18 us: local(): doubled = jnp.concatenate([weight_local, weight_local], axis=3)]
    ppermute x4, starting transfers between devices: 4.06 us -> 5.63 us  [direct_reduce_scatter(): lax.ppermute(piece.astype(send_dtype), axis, pairs).astype(jnp.float32)]
    ppermute x1, waiting for transfers between devices: 4.05 us -> 2.51 us  [local(): received.append(lax.ppermute(part.astype(jnp.bfloat16), 'chan', pairs))]
    ppermute x4, waiting for transfers between devices: 1.21 us -> 2.58 us  [padded_2(): before = lax.ppermute(last, axis, up)]
  transfers between devices with their start and end apart: 19 -> 19, of which waited for: 9 -> 12; matrix products, arithmetic and copies ran while one was open for 19% -> 16% of each run, Pallas kernels for 0% -> 0%
where the time goes in v6:
time: 87.5 us; the launch traced here: 86.8 us
  matrix products  26.6 us (30%)
  starting transfers between devices  23.2 us (27%)
  waiting for transfers between devices  18 us (21%)
  local copies, waits for them, and re-layouts  13.5 us (15%)
  other arithmetic  4.39 us (5%)
  between operations  1.21 us (1%)
    dot_general x18, matrix products, local(): jnp.dot(kernel_cols[shift][tap // 3, tap % 3], windows[shift][tap], prefe...  10.7 us
    dot_general x9, matrix products, local(): lax.dot_general(grad_pre, window, (((1,), (1,)), ((), ())), preferred_ele...  10 us
    slice x5, local copies, waits for them, and re-layouts, window_of(): field[:, first_row:first_row + row_count, first_col:first_col + column_co...  6.35 us
    ppermute x4, waiting for transfers between devices, direct_all_gather(): pieces.append(lax.ppermute(sent, axis, pairs).astype(jnp.float32))  6.14 us
    dot_general x18, matrix products, conv_taps(): jnp.dot(kernel[tap_row, tap_col], window, preferred_element_type=jnp.floa...  5.78 us
    ppermute x4, starting transfers between devices, direct_reduce_scatter(): lax.ppermute(piece.astype(send_dtype), axis, pairs).astype(jnp.float32)  5.63 us
    ppermute x4, starting transfers between devices, padded_2(): after = lax.ppermute(initial, axis, down)  5.52 us
    ppermute x4, waiting for transfers between devices, direct_reduce_scatter(): lax.ppermute(piece.astype(send_dtype), axis, pairs).astype(jnp.float32)  4.7 us
  transfers between devices with their start and end apart: 19, of which 12 were waited for; matrix products, arithmetic and copies ran while one was open for 16% of the time, Pallas kernels for 0%

profile of v6, /device:TPU:0, one launch (start us, length us, event | category | flops | bytes accessed | tf_op | source)
XLA Modules:
  0.0 86.8 jit_solution(5855849981974193799)
XLA Ops:
  0.7 1.6 %copy.22 = bf16[128,16,128]{0,2,1:T(8,128)(2,1)S(1)} copy(bf16[128,16,128]{2,1,0:T(8,128)(2,1)} %param.4) | data formatting | bytes 1048576 | tf_op args[0]
  2.2 3.0 %collective-permute-start.5 = (bf16[128,16,128]{0,2,1:T(8,128)(2,1)S(1)}, bf16[128,16,128]{0,2,1:T(8,128)(2,1)S(1)}, u32[]{:S(2)}, u32[]{:S(2)}) collective-permute-start(bf16[128,16,128]{0,2,1:T(8,128)(2,1)S(1)} %copy.22), channel_id=1, source_target_pairs={{0,2},{2,0},{1,3},{3,1},{4,6},{6,4},{5,7},{7,5},{8,10},{10,8},{9,1... | collective-permute-start | bytes 1572872 | tf_op jit(solution)/shard_map/ppermute | solution.py:118
  5.2 1.6 %collective-permute-start = (bf16[128,16,1]{0,2,1:T(2,128)(2,1)S(1)}, bf16[128,16,1]{0,2,1:T(2,128)(2,1)S(1)}, u32[]{:S(2)}, u32[]{:S(2)}) collective-permute-start(bf16[128,16,1]{0,2,1:T(2,128)(2,1)S(1)} %get-tuple-element.57), channel_id=1, source_target_pairs={{0,4},{4,8},{8,12},{12,0},{1,5},{5,9},{9,13},{13,1},{2,6},{6,10},{... | collective-permute-start | bytes 12296 | tf_op jit(solution)/shard_map/ppermute | solution.py:14
  6.9 2.2 %collective-permute-start.1 = (bf16[128,16,1]{0,2,1:T(2,128)(2,1)S(1)}, bf16[128,16,1]{0,2,1:T(2,128)(2,1)S(1)}, u32[]{:S(2)}, u32[]{:S(2)}) collective-permute-start(bf16[128,16,1]{0,2,1:T(2,128)(2,1)S(1)} %get-tuple-element.58), channel_id=1, source_target_pairs={{4,0},{8,4},{12,8},{0,12},{5,1},{9,5},{13,9},{1,13},{6,2},{10,6},{... | collective-permute-start | bytes 12296 | tf_op jit(solution)/shard_map/ppermute | solution.py:15
  9.1 1.1 %bitcast_convert_fusion = f32[16,8,16,128]{3,2,1,0:T(8,128)} fusion(bf16[128,16,128]{2,1,0:T(8,128)(2,1)S(1)} %copy-done.9), kind=kLoop, calls=%fused_computation.190 | loop fusion | flops 262144 | bytes 1572864
  17.0 1.7 %collective-permute-done.4 = bf16[128,292]{0,1:T(8,128)(2,1)S(1)} collective-permute-done((bf16[128,292]{0,1:T(8,128)(2,1)S(1)}, bf16[128,292]{0,1:T(8,128)(2,1)S(1)}, u32[]{:S(2)}, u32[]{:S(2)}) %collective-permute-start.4) | collective-permute-done | bytes 74784 | tf_op jit(solution)/shard_map/ppermute | solution.py:124
  21.4 3.9 %fusion.56 = (bf16[256,16,128]{0,2,1:T(8,128)(2,1)S(1)}, bf16[256,16,128]{0,2,1:T(8,128)(2,1)S(1)}, bf16[256,16,128]{0,2,1:T(8,128)(2,1)}, bf16[256,16,128]{0,2,...) fusion(bf16[256,18,130]{0,2,1:T(8,128)(2,1)S(1)} %maximum_maxim, ...), kind=kLoop, calls=%fused_computation.182 | loop fusion | bytes 18874368 | tf_op jit(solution)/shard_map/slice | solution.py:37
  25.3 1.1 %convolution_add_fusion.21 = f32[128,2048]{1,0:T(8,128)S(1)} fusion(f32[128,2048]{1,0:T(8,128)S(1)} %convolution_add_fusion.22, bf16[128,2048]{0,1:T(8,128)(2,1)S(1)} %bitcast.359, bf16[3,3,128,256]{3,2,1,0:T(8,128)(2,1)} %param.6, s32[]{:T(128)S(6)} %select_n.97), kind=kOutput, calls=%fused_computation.25 | convolution fusion | flops 67371008 | bytes 2654212 | tf_op jit(solution)/shard_map/dot_general | solution.py:139
  26.3 1.1 %convolution_add_fusion.20 = f32[128,2048]{1,0:T(8,128)S(1)} fusion(f32[128,2048]{1,0:T(8,128)S(1)} %convolution_add_fusion.21, bf16[128,2048]{0,1:T(8,128)(2,1)S(1)} %bitcast.357, bf16[3,3,128,256]{3,2,1,0:T(8,128)(2,1)} %param.6, s32[]{:T(128)S(6)} %add.290, s32[]{:T(128)S(6)} %select_n.97), kind=kOutput, calls=%fused_computation.24 | convolution fusion | flops 67371008 | bytes 2654216 | tf_op jit(solution)/shard_map/dot_general | solution.py:139
  27.4 1.1 %convolution_add_fusion.19 = f32[128,2048]{1,0:T(8,128)S(1)} fusion(f32[128,2048]{1,0:T(8,128)S(1)} %convolution_add_fusion.20, bf16[128,2048]{0,1:T(8,128)(2,1)S(1)} %bitcast.356, bf16[3,3,128,256]{3,2,1,0:T(8,128)(2,1)} %param.6, s32[]{:T(128)S(6)} %add.291, s32[]{:T(128)S(6)} %select_n.97), kind=kOutput, calls=%fused_computation.23 | convolution fusion | flops 67371008 | bytes 2654216 | tf_op jit(solution)/shard_map/dot_general | solution.py:139
  28.5 1.1 %fusion.3 = f32[128,2048]{1,0:T(8,128)S(1)} fusion(f32[128,2048]{1,0:T(8,128)S(1)} %fusion.31, f32[128,2048]{1,0:T(8,128)S(1)} %fusion.32, f32[128,2048]{1,0:T(8,128)S(1)} %fusion.33, f32[128,2048]{1,0:T(8,128)S(1)} %convolution_add_fusion.19, bf16[128,2048]{0,1:T(8,128)(2,1)S(1)} %bitcast.347, bf16[3,3,128,256]{3,2,1,0:T(8,128)(2,1)} %param.6, ...), kind=kOutput, calls=%fused_computation.22 | convolution fusion | flops 68157440 | bytes 5799944 | tf_op jit(solution)/shard_map/dot_general | solution.py:139
  29.6 1.2 %convolution_add_fusion.17 = f32[128,2048]{1,0:T(8,128)S(1)} fusion(f32[128,2048]{1,0:T(8,128)S(1)} %fusion.3, bf16[128,2048]{0,1:T(8,128)(2,1)S(1)} %bitcast.358, bf16[3,3,128,256]{3,2,1,0:T(8,128)(2,1)} %param.6, s32[]{:T(128)S(6)} %add.291, s32[]{:T(128)S(6)} %add.290, s32[]{:T(128)S(6)} %select_n.97), kind=kOutput, calls=%fused_computation.18 | convolution fusion | flops 67371008 | bytes 2654220 | tf_op jit(solution)/shard_map/dot_general | solution.py:139
  30.9 1.7 %convert_reduce_fusion = (f32[128]{0:T(128)S(1)}, bf16[128,2048]{1,0:T(8,128)(2,1)S(1)}) fusion(f32[128]{0:T(128)S(1)} %copy-done.10, f32[128,2048]{1,0:T(8,128)S(1)} %convolution_add_fusion.17, bf16[128,2048]{0,1:T(8,128)(2,1)S(1)} %bitcast.365, bf16[3,3,128,256]{3,2,1,0:T(8,128)(2,1)} %param.6, s32[]{:T(128)S(6)} %add.291, s32[]{:T(128)S(6)} %select_n.97, ...), kind=kOutput, calls=%fused_computation.73 | convolution fusion | flops 70778752 | bytes 3179528 | tf_op jit(solution)/shard_map/dot_general | solution.py:139
  32.8 2.3 %fusion.17 = f32[9,128,256]{2,1,0:T(8,128)} fusion(bf16[128,2048]{1,0:T(8,128)(2,1)S(1)} %get-tuple-element.64, bf16[256,2048]{0,1:T(8,128)(2,1)} %bitcast.342), kind=kOutput, calls=%fused_computation.66 | convolution fusion | flops 134217728 | bytes 1703936 | tf_op jit(solution)/shard_map/dot_general | solution.py:152
  35.1 1.0 %fusion.16 = f32[9,128,256]{2,1,0:T(8,128)} fusion(f32[9,128,256]{2,1,0:T(8,128)} %fusion.17, bf16[128,2048]{1,0:T(8,128)(2,1)S(1)} %get-tuple-element.64, bf16[256,2048]{0,1:T(8,128)(2,1)S(1)} %bitcast.341), kind=kOutput, calls=%fused_computation.64 | convolution fusion | flops 134217728 | bytes 1703936 | tf_op jit(solution)/shard_map/dot_general | solution.py:152
  38.6 1.0 %fusion.13 = f32[9,128,256]{2,1,0:T(8,128)} fusion(f32[9,128,256]{2,1,0:T(8,128)} %fusion.14, bf16[128,2048]{1,0:T(8,128)(2,1)S(1)} %get-tuple-element.64, bf16[256,2048]{0,1:T(8,128)(2,1)S(1)} %bitcast.338), kind=kOutput, calls=%fused_computation.58 | convolution fusion | flops 134217728 | bytes 1703936 | tf_op jit(solution)/shard_map/dot_general | solution.py:152
  39.6 1.0 %fusion.12 = f32[9,128,256]{2,1,0:T(8,128)} fusion(f32[9,128,256]{2,1,0:T(8,128)} %fusion.13, bf16[128,2048]{1,0:T(8,128)(2,1)S(1)} %get-tuple-element.64, bf16[256,2048]{0,1:T(8,128)(2,1)S(1)} %bitcast.337), kind=kOutput, calls=%fused_computation.56 | convolution fusion | flops 134217728 | bytes 1703936 | tf_op jit(solution)/shard_map/dot_general | solution.py:152
  40.8 1.0 %fusion.11 = f32[9,128,256]{2,1,0:T(8,128)} fusion(f32[9,128,256]{2,1,0:T(8,128)} %fusion.12, bf16[128,2048]{1,0:T(8,128)(2,1)S(1)} %get-tuple-element.64, bf16[256,2048]{0,1:T(8,128)(2,1)S(1)} %bitcast.336), kind=kOutput, calls=%fused_computation.54 | convolution fusion | flops 134217728 | bytes 1703936 | tf_op jit(solution)/shard_map/dot_general | solution.py:152
  43.7 1.3 %reshape.207 = f32[2304,128]{1,0:T(8,128)S(1)} reshape(f32[9,128,256]{2,1,0:T(8,128)} %fusion.9) | data formatting | bytes 2359296 | tf_op jit(solution)/shard_map/reshape | solution.py:154
  45.1 1.9 %collective-permute-start.6 = (bf16[128,16,1]{0,2,1:T(2,128)(2,1)S(1)}, bf16[128,16,1]{0,2,1:T(2,128)(2,1)S(1)}, u32[]{:S(2)}, u32[]{:S(2)}) collective-permute-start(bf16[128,16,1]{0,2,1:T(2,128)(2,1)S(1)} %get-tuple-element.53), channel_id=1, source_target_pairs={{0,4},{4,8},{8,12},{12,0},{1,5},{5,9},{9,13},{13,1},{2,6},{6,10},{... | collective-permute-start | bytes 12296 | tf_op jit(solution)/shard_map/ppermute | solution.py:14
  47.0 2.3 %collective-permute-start.7 = (bf16[128,16,1]{0,2,1:T(2,128)(2,1)S(1)}, bf16[128,16,1]{0,2,1:T(2,128)(2,1)S(1)}, u32[]{:S(2)}, u32[]{:S(2)}) collective-permute-start(bf16[128,16,1]{0,2,1:T(2,128)(2,1)S(1)} %get-tuple-element.54), channel_id=1, source_target_pairs={{4,0},{8,4},{12,8},{0,12},{5,1},{9,5},{13,9},{1,13},{6,2},{10,6},{... | collective-permute-start | bytes 12296 | tf_op jit(solution)/shard_map/ppermute | solution.py:15
  49.3 1.4 %collective-permute-done.6 = bf16[128,16,1]{0,2,1:T(2,128)(2,1)S(1)} collective-permute-done((bf16[128,16,1]{0,2,1:T(2,128)(2,1)S(1)}, bf16[128,16,1]{0,2,1:T(2,128)(2,1)S(1)}, u32[]{:S(2)}, u32[]{:S(2)}) %collective-permute-start.6) | collective-permute-done | bytes 4128 | tf_op jit(solution)/shard_map/ppermute | solution.py:14
  57.9 1.5 %collective-permute-start.12 = (bf16[296,128]{1,0:T(8,128)(2,1)S(1)}, bf16[296,128]{1,0:T(8,128)(2,1)S(1)}, u32[]{:S(2)}, u32[]{:S(2)}) collective-permute-start(bf16[296,128]{1,0:T(8,128)(2,1)S(1)} %get-tuple-element.36), channel_id=1, source_target_pairs={{0,4},{4,8},{8,12},{12,0},{1,5},{5,9},{9,13},{13,1},{2,6},{6,10},{... | collective-permute-start | bytes 227336 | tf_op jit(solution)/shard_map/ppermute | solution.py:64
  59.4 3.1 %collective-permute-start.13 = (bf16[296,128]{1,0:T(8,128)(2,1)S(1)}, bf16[296,128]{1,0:T(8,128)(2,1)S(1)}, u32[]{:S(2)}, u32[]{:S(2)}) collective-permute-start(bf16[296,128]{1,0:T(8,128)(2,1)S(1)} %get-tuple-element.38), channel_id=1, source_target_pairs={{0,8},{4,12},{8,0},{12,4},{1,9},{5,13},{9,1},{13,5},{2,10},{6,14},... | collective-permute-start | bytes 227336 | tf_op jit(solution)/shard_map/ppermute | solution.py:64
  63.7 1.4 %collective-permute-done.12 = bf16[296,128]{1,0:T(8,128)(2,1)S(1)} collective-permute-done((bf16[296,128]{1,0:T(8,128)(2,1)S(1)}, bf16[296,128]{1,0:T(8,128)(2,1)S(1)}, u32[]{:S(2)}, u32[]{:S(2)}) %collective-permute-start.12) | collective-permute-done | bytes 75808 | tf_op jit(solution)/shard_map/ppermute | solution.py:64
  65.1 3.0 %collective-permute-done.13 = bf16[296,128]{1,0:T(8,128)(2,1)S(1)} collective-permute-done((bf16[296,128]{1,0:T(8,128)(2,1)S(1)}, bf16[296,128]{1,0:T(8,128)(2,1)S(1)}, u32[]{:S(2)}, u32[]{:S(2)}) %collective-permute-start.13) | collective-permute-done | bytes 75808 | tf_op jit(solution)/shard_map/ppermute | solution.py:64
  68.4 2.4 %collective-permute-start.15 = (bf16[296,128]{1,0:T(8,128)(2,1)S(1)}, bf16[296,128]{1,0:T(8,128)(2,1)S(1)}, u32[]{:S(2)}, u32[]{:S(2)}) collective-permute-start(bf16[296,128]{1,0:T(8,128)(2,1)S(1)} %get-tuple-element.3), channel_id=1, source_target_pairs={{0,12},{4,0},{8,4},{12,8},{1,13},{5,1},{9,5},{13,9},{2,14},{6,2},{... | collective-permute-start | bytes 227336 | tf_op jit(solution)/shard_map/ppermute | solution.py:76
  71.2 1.5 %collective-permute-start.10 = (bf16[128,2048]{1,0:T(8,128)(2,1)S(1)}, bf16[128,2048]{1,0:T(8,128)(2,1)S(1)}, u32[]{:S(2)}, u32[]{:S(2)}) collective-permute-start(bf16[128,2048]{1,0:T(8,128)(2,1)S(1)} %fusion.4), channel_id=1, source_target_pairs={{0,2},{2,0},{1,3},{3,1},{4,6},{6,4},{5,7},{7,5},{8,10},{10,8},{9,1... | collective-permute-start | bytes 1572872 | tf_op jit(solution)/shard_map/ppermute | solution.py:170
  73.7 5.2 %collective-permute-done.16 = bf16[296,128]{1,0:T(8,128)(2,1)S(1)} collective-permute-done((bf16[296,128]{1,0:T(8,128)(2,1)S(1)}, bf16[296,128]{1,0:T(8,128)(2,1)S(1)}, u32[]{:S(2)}, u32[]{:S(2)}) %collective-permute-start.16) | collective-permute-done | bytes 75808 | tf_op jit(solution)/shard_map/ppermute | solution.py:76
  78.8 1.0 %collective-permute-done.17 = bf16[296,128]{1,0:T(8,128)(2,1)S(1)} collective-permute-done((bf16[296,128]{1,0:T(8,128)(2,1)S(1)}, bf16[296,128]{1,0:T(8,128)(2,1)S(1)}, u32[]{:S(2)}, u32[]{:S(2)}) %collective-permute-start.17) | collective-permute-done | bytes 75808 | tf_op jit(solution)/shard_map/ppermute | solution.py:76
  80.7 2.5 %collective-permute-done.10 = bf16[128,2048]{1,0:T(8,128)(2,1)S(1)} collective-permute-done((bf16[128,2048]{1,0:T(8,128)(2,1)S(1)}, bf16[128,2048]{1,0:T(8,128)(2,1)S(1)}, u32[]{:S(2)}, u32[]{:S(2)}) %collective-permute-start.10) | collective-permute-done | bytes 524320 | tf_op jit(solution)/shard_map/ppermute | solution.py:170
  85.6 1.2 %fusion.8 = f32[3,3,128,256]{3,2,1,0:T(8,128)} fusion(s32[]{:T(128)S(6)} %select_n.114, f32[3,3,128,256]{3,2,1,0:T(8,128)S(1)} %reshape.213), kind=kLoop, calls=%fused_computation.48 | loop fusion | flops 294912 | bytes 2359300 | tf_op jit(solution)/shard_map/concatenate | solution.py:159
  (121 shorter events, 27.4 us)
Async XLA Ops:
  0.6 8.5 %copy-start.9 = (bf16[128,16,128]{2,1,0:T(8,128)(2,1)S(1)}, bf16[128,16,128]{2,1,0:T(8,128)(2,1)}, u32[]{:S(2)}) copy-start(bf16[128,16,128]{2,1,0:T(8,128)(2,1)} %param.5) | copy-start | bytes 1572868
  0.6 9.6 %copy-start.6 = (bf16[3,3,128,256]{3,2,1,0:T(8,128)(2,1)S(1)}, bf16[3,3,128,256]{3,2,1,0:T(8,128)(2,1)}, u32[]{:S(2)}) copy-start(bf16[3,3,128,256]{3,2,1,0:T(8,128)(2,1)} %param.6) | copy-start | bytes 1769476
  2.2 16.6 %collective-permute-start.5 = (bf16[128,16,128]{0,2,1:T(8,128)(2,1)S(1)}, bf16[128,16,128]{0,2,1:T(8,128)(2,1)S(1)}, u32[]{:S(2)}, u32[]{:S(2)}) collective-permute-start(bf16[128,16,128]{0,2,1:T(8,128)(2,1)S(1)} %copy.22), channel_id=1, source_target_pairs={{0,2},{2,0},{1,3},{3,1},{4,6},{6,4},{5,7},{7,5},{8,10},{10,8},{9,1... | collective-permute-start | bytes 1572872 | tf_op jit(solution)/shard_map/ppermute | solution.py:118
  5.2 5.8 %collective-permute-start = (bf16[128,16,1]{0,2,1:T(2,128)(2,1)S(1)}, bf16[128,16,1]{0,2,1:T(2,128)(2,1)S(1)}, u32[]{:S(2)}, u32[]{:S(2)}) collective-permute-start(bf16[128,16,1]{0,2,1:T(2,128)(2,1)S(1)} %get-tuple-element.57), channel_id=1, source_target_pairs={{0,4},{4,8},{8,12},{12,0},{1,5},{5,9},{9,13},{13,1},{2,6},{6,10},{... | collective-permute-start | bytes 12296 | tf_op jit(solution)/shard_map/ppermute | solution.py:14
  6.9 4.2 %collective-permute-start.1 = (bf16[128,16,1]{0,2,1:T(2,128)(2,1)S(1)}, bf16[128,16,1]{0,2,1:T(2,128)(2,1)S(1)}, u32[]{:S(2)}, u32[]{:S(2)}) collective-permute-start(bf16[128,16,1]{0,2,1:T(2,128)(2,1)S(1)} %get-tuple-element.58), channel_id=1, source_target_pairs={{4,0},{8,4},{12,8},{0,12},{5,1},{9,5},{13,9},{1,13},{6,2},{10,6},{... | collective-permute-start | bytes 12296 | tf_op jit(solution)/shard_map/ppermute | solution.py:15
  11.0 1.3 %collective-permute-start.2 = (bf16[128,1,130]{0,2,1:T(8,128)(2,1)S(1)}, bf16[128,1,130]{0,2,1:T(8,128)(2,1)S(1)}, u32[]{:S(2)}, u32[]{:S(2)}) collective-permute-start(bf16[128,1,130]{0,2,1:T(8,128)(2,1)S(1)} %get-tuple-element.51), channel_id=1, source_target_pairs={{0,1},{1,0},{2,3},{3,2},{4,5},{5,4},{6,7},{7,6},{8,9},{9,8},{10,11... | collective-permute-start | bytes 99848 | tf_op jit(solution)/shard_map/ppermute | solution.py:14
  11.1 1.4 %collective-permute-start.3 = (bf16[128,1,130]{0,2,1:T(8,128)(2,1)S(1)}, bf16[128,1,130]{0,2,1:T(8,128)(2,1)S(1)}, u32[]{:S(2)}, u32[]{:S(2)}) collective-permute-start(bf16[128,1,130]{0,2,1:T(8,128)(2,1)S(1)} %get-tuple-element.52), channel_id=1, source_target_pairs={{1,0},{0,1},{3,2},{2,3},{5,4},{4,5},{7,6},{6,7},{9,8},{8,9},{11,10... | collective-permute-start | bytes 99848 | tf_op jit(solution)/shard_map/ppermute | solution.py:15
  14.1 4.6 %collective-permute-start.4 = (bf16[128,292]{0,1:T(8,128)(2,1)S(1)}, bf16[128,292]{0,1:T(8,128)(2,1)S(1)}, u32[]{:S(2)}, u32[]{:S(2)}) collective-permute-start(bf16[128,292]{0,1:T(8,128)(2,1)S(1)} %pad_maximum_fusion.3), channel_id=1, source_target_pairs={{0,2},{2,0},{1,3},{3,1},{4,6},{6,4},{5,7},{7,5},{8,10},{10,8},{9,1... | collective-permute-start | bytes 224264 | tf_op jit(solution)/shard_map/ppermute | solution.py:124
  29.6 1.2 %copy-start.8 = (f32[16,8,16,128]{3,2,1,0:T(8,128)S(1)}, f32[16,8,16,128]{3,2,1,0:T(8,128)}, u32[]{:S(2)}) copy-start(f32[16,8,16,128]{3,2,1,0:T(8,128)} %bitcast_convert_fusion) | copy-start | bytes 3145732
  29.6 1.2 %copy-start.10 = (f32[128]{0:T(128)S(1)}, f32[128]{0:T(128)}, u32[]{:S(2)}) copy-start(f32[128]{0:T(128)} %param.7) | copy-start | bytes 1540
  32.8 2.3 %copy-start.5 = (bf16[256,16,128]{0,2,1:T(8,128)(2,1)S(1)}, bf16[256,16,128]{0,2,1:T(8,128)(2,1)}, u32[]{:S(2)}) copy-start(bf16[256,16,128]{0,2,1:T(8,128)(2,1)} %get-tuple-element.12) | copy-start | bytes 3145732
  35.1 1.2 %copy-start.4 = (bf16[256,16,128]{0,2,1:T(8,128)(2,1)S(1)}, bf16[256,16,128]{0,2,1:T(8,128)(2,1)}, u32[]{:S(2)}) copy-start(bf16[256,16,128]{0,2,1:T(8,128)(2,1)} %get-tuple-element.11) | copy-start | bytes 3145732
  36.1 1.3 %copy-start.3 = (bf16[256,16,128]{0,2,1:T(8,128)(2,1)S(1)}, bf16[256,16,128]{0,2,1:T(8,128)(2,1)}, u32[]{:S(2)}) copy-start(bf16[256,16,128]{0,2,1:T(8,128)(2,1)} %get-tuple-element.10) | copy-start | bytes 3145732
  37.3 1.2 %copy-start.2 = (bf16[256,16,128]{0,2,1:T(8,128)(2,1)S(1)}, bf16[256,16,128]{0,2,1:T(8,128)(2,1)}, u32[]{:S(2)}) copy-start(bf16[256,16,128]{0,2,1:T(8,128)(2,1)} %get-tuple-element.9) | copy-start | bytes 3145732
  38.4 1.3 %copy-start.1 = (bf16[256,16,128]{0,2,1:T(8,128)(2,1)S(1)}, bf16[256,16,128]{0,2,1:T(8,128)(2,1)}, u32[]{:S(2)}) copy-start(bf16[256,16,128]{0,2,1:T(8,128)(2,1)} %get-tuple-element.8) | copy-start | bytes 3145732
  39.5 1.2 %copy-start = (bf16[256,16,128]{0,2,1:T(8,128)(2,1)S(1)}, bf16[256,16,128]{0,2,1:T(8,128)(2,1)}, u32[]{:S(2)}) copy-start(bf16[256,16,128]{0,2,1:T(8,128)(2,1)} %get-tuple-element.7) | copy-start | bytes 3145732
  45.1 5.6 %collective-permute-start.6 = (bf16[128,16,1]{0,2,1:T(2,128)(2,1)S(1)}, bf16[128,16,1]{0,2,1:T(2,128)(2,1)S(1)}, u32[]{:S(2)}, u32[]{:S(2)}) collective-permute-start(bf16[128,16,1]{0,2,1:T(2,128)(2,1)S(1)} %get-tuple-element.53), channel_id=1, source_target_pairs={{0,4},{4,8},{8,12},{12,0},{1,5},{5,9},{9,13},{13,1},{2,6},{6,10},{... | collective-permute-start | bytes 12296 | tf_op jit(solution)/shard_map/ppermute | solution.py:14
  47.0 3.7 %collective-permute-start.7 = (bf16[128,16,1]{0,2,1:T(2,128)(2,1)S(1)}, bf16[128,16,1]{0,2,1:T(2,128)(2,1)S(1)}, u32[]{:S(2)}, u32[]{:S(2)}) collective-permute-start(bf16[128,16,1]{0,2,1:T(2,128)(2,1)S(1)} %get-tuple-element.54), channel_id=1, source_target_pairs={{4,0},{8,4},{12,8},{0,12},{5,1},{9,5},{13,9},{1,13},{6,2},{10,6},{... | collective-permute-start | bytes 12296 | tf_op jit(solution)/shard_map/ppermute | solution.py:15
  50.7 1.3 %collective-permute-start.8 = (bf16[128,1,130]{0,2,1:T(8,128)(2,1)S(1)}, bf16[128,1,130]{0,2,1:T(8,128)(2,1)S(1)}, u32[]{:S(2)}, u32[]{:S(2)}) collective-permute-start(bf16[128,1,130]{0,2,1:T(8,128)(2,1)S(1)} %get-tuple-element.47), channel_id=1, source_target_pairs={{0,1},{1,0},{2,3},{3,2},{4,5},{5,4},{6,7},{7,6},{8,9},{9,8},{10,11... | collective-permute-start | bytes 99848 | tf_op jit(solution)/shard_map/ppermute | solution.py:14
  50.8 1.4 %collective-permute-start.9 = (bf16[128,1,130]{0,2,1:T(8,128)(2,1)S(1)}, bf16[128,1,130]{0,2,1:T(8,128)(2,1)S(1)}, u32[]{:S(2)}, u32[]{:S(2)}) collective-permute-start(bf16[128,1,130]{0,2,1:T(8,128)(2,1)S(1)} %get-tuple-element.48), channel_id=1, source_target_pairs={{1,0},{0,1},{3,2},{2,3},{5,4},{4,5},{7,6},{6,7},{9,8},{8,9},{11,10... | collective-permute-start | bytes 99848 | tf_op jit(solution)/shard_map/ppermute | solution.py:15
  51.3 6.4 %collective-permute-start.11 = (f32[1184,128]{1,0:T(8,128)S(1)}, f32[1184,128]{1,0:T(8,128)S(1)}, u32[]{:S(2)}, u32[]{:S(2)}) collective-permute-start(f32[1184,128]{1,0:T(8,128)S(1)} %dynamic-slice_bitcast_fusion), channel_id=1, source_target_pairs={{0,1},{1,0},{2,3},{3,2},{4,5},{5,4},{6,7},{7,6},{8,9},{9,8},{10,11... | collective-permute-start | bytes 1818632 | tf_op jit(solution)/shard_map/ppermute | solution.py:64
  52.5 1.0 %copy-start.7 = (bf16[3,3,128,128]{2,3,1,0:T(8,128)(2,1)S(1)}, bf16[3,3,128,128]{2,3,1,0:T(8,128)(2,1)}, u32[]{:S(2)}) copy-start(bf16[3,3,128,128]{2,3,1,0:T(8,128)(2,1)} %get-tuple-element.45) | copy-start | bytes 884740
  57.9 7.2 %collective-permute-start.12 = (bf16[296,128]{1,0:T(8,128)(2,1)S(1)}, bf16[296,128]{1,0:T(8,128)(2,1)S(1)}, u32[]{:S(2)}, u32[]{:S(2)}) collective-permute-start(bf16[296,128]{1,0:T(8,128)(2,1)S(1)} %get-tuple-element.36), channel_id=1, source_target_pairs={{0,4},{4,8},{8,12},{12,0},{1,5},{5,9},{9,13},{13,1},{2,6},{6,10},{... | collective-permute-start | bytes 227336 | tf_op jit(solution)/shard_map/ppermute | solution.py:64
  59.4 8.7 %collective-permute-start.13 = (bf16[296,128]{1,0:T(8,128)(2,1)S(1)}, bf16[296,128]{1,0:T(8,128)(2,1)S(1)}, u32[]{:S(2)}, u32[]{:S(2)}) collective-permute-start(bf16[296,128]{1,0:T(8,128)(2,1)S(1)} %get-tuple-element.38), channel_id=1, source_target_pairs={{0,8},{4,12},{8,0},{12,4},{1,9},{5,13},{9,1},{13,5},{2,10},{6,14},... | collective-permute-start | bytes 227336 | tf_op jit(solution)/shard_map/ppermute | solution.py:64
  62.5 5.9 %collective-permute-start.14 = (bf16[296,128]{1,0:T(8,128)(2,1)S(1)}, bf16[296,128]{1,0:T(8,128)(2,1)S(1)}, u32[]{:S(2)}, u32[]{:S(2)}) collective-permute-start(bf16[296,128]{1,0:T(8,128)(2,1)S(1)} %get-tuple-element.37), channel_id=1, source_target_pairs={{0,12},{4,0},{8,4},{12,8},{1,13},{5,1},{9,5},{13,9},{2,14},{6,2},{... | collective-permute-start | bytes 227336 | tf_op jit(solution)/shard_map/ppermute | solution.py:64
  68.4 5.2 %collective-permute-start.15 = (bf16[296,128]{1,0:T(8,128)(2,1)S(1)}, bf16[296,128]{1,0:T(8,128)(2,1)S(1)}, u32[]{:S(2)}, u32[]{:S(2)}) collective-permute-start(bf16[296,128]{1,0:T(8,128)(2,1)S(1)} %get-tuple-element.3), channel_id=1, source_target_pairs={{0,12},{4,0},{8,4},{12,8},{1,13},{5,1},{9,5},{13,9},{2,14},{6,2},{... | collective-permute-start | bytes 227336 | tf_op jit(solution)/shard_map/ppermute | solution.py:76
  71.2 12.1 %collective-permute-start.10 = (bf16[128,2048]{1,0:T(8,128)(2,1)S(1)}, bf16[128,2048]{1,0:T(8,128)(2,1)S(1)}, u32[]{:S(2)}, u32[]{:S(2)}) collective-permute-start(bf16[128,2048]{1,0:T(8,128)(2,1)S(1)} %fusion.4), channel_id=1, source_target_pairs={{0,2},{2,0},{1,3},{3,1},{4,6},{6,4},{5,7},{7,5},{8,10},{10,8},{9,1... | collective-permute-start | bytes 1572872 | tf_op jit(solution)/shard_map/ppermute | solution.py:170
  72.7 6.1 %collective-permute-start.16 = (bf16[296,128]{1,0:T(8,128)(2,1)S(1)}, bf16[296,128]{1,0:T(8,128)(2,1)S(1)}, u32[]{:S(2)}, u32[]{:S(2)}) collective-permute-start(bf16[296,128]{1,0:T(8,128)(2,1)S(1)} %get-tuple-element.3), channel_id=1, source_target_pairs={{0,8},{4,12},{8,0},{12,4},{1,9},{5,13},{9,1},{13,5},{2,10},{6,14},... | collective-permute-start | bytes 227336 | tf_op jit(solution)/shard_map/ppermute | solution.py:76
  73.6 6.2 %collective-permute-start.17 = (bf16[296,128]{1,0:T(8,128)(2,1)S(1)}, bf16[296,128]{1,0:T(8,128)(2,1)S(1)}, u32[]{:S(2)}, u32[]{:S(2)}) collective-permute-start(bf16[296,128]{1,0:T(8,128)(2,1)S(1)} %get-tuple-element.3), channel_id=1, source_target_pairs={{0,4},{4,8},{8,12},{12,0},{1,5},{5,9},{9,13},{13,1},{2,6},{6,10},{... | collective-permute-start | bytes 227336 | tf_op jit(solution)/shard_map/ppermute | solution.py:76
  80.0 4.5 %collective-permute-start.18 = (f32[1184,128]{1,0:T(8,128)S(1)}, f32[1184,128]{1,0:T(8,128)S(1)}, u32[]{:S(2)}, u32[]{:S(2)}) collective-permute-start(f32[1184,128]{1,0:T(8,128)S(1)} %bitcast.343), channel_id=1, source_target_pairs={{0,1},{1,0},{2,3},{3,2},{4,5},{5,4},{6,7},{7,6},{8,9},{9,8},{10,11... | collective-permute-start | bytes 1818632 | tf_op jit(solution)/shard_map/ppermute | solution.py:76

commit v7 on v3

--- a/solution.py
+++ b/solution.py
@@ -90,15 +90,39 @@
     return rows.reshape(-1)[: flat.size]
 
 
+def border_of(padded):
+    rows, cols = padded.shape[1], padded.shape[2]
+    return jnp.concatenate(
+        [padded[:, 0, :], padded[:, rows - 1, :], padded[:, 1 : rows - 1, 0], padded[:, 1 : rows - 1, cols - 1]],
+        axis=1,
+    )
+
+
+def with_border(field, border):
+    rows, cols = field.shape[1], field.shape[2]
+    top = border[:, : cols + 2]
+    bottom = border[:, cols + 2 : 2 * cols + 4]
+    left = border[:, 2 * cols + 4 : 2 * cols + 4 + rows]
+    right = border[:, 2 * cols + 4 + rows :]
+    middle = jnp.concatenate([left[:, :, None], field, right[:, :, None]], axis=2)
+    return jnp.concatenate([top[:, None, :], middle, bottom[:, None, :]], axis=1)
+
+
 def local(inputs, cotangent, weight, bias_vector):
     own_channels, row_count, column_count = inputs.shape
     chan_count = lax.axis_size("chan")
     chan_index = lax.axis_index("chan")
+    raw_blocks = []
+    for shift in range(1, chan_count):
+        pairs = [(i, (i - shift) % chan_count) for i in range(chan_count)]
+        raw_blocks.append(lax.ppermute(inputs, "chan", pairs))
     input_pad = mask_rims(padded_2(inputs, (("lon", 2), ("lat", 1)), 1))
+    own_border = border_of(input_pad)
     blocks = [input_pad]
     for shift in range(1, chan_count):
         pairs = [(i, (i - shift) % chan_count) for i in range(chan_count)]
-        blocks.append(lax.ppermute(input_pad, "chan", pairs))
+        border = lax.ppermute(own_border, "chan", pairs)
+        blocks.append(lax.optimization_barrier(with_border(raw_blocks[shift - 1], border)))
     kernel_cols = []
     for shift in range(chan_count):
         source = (chan_index + shift) % chan_count

time: 82.1 us -> 79.3 us (0.966)
  waiting for transfers between devices: 28.6 us -> 18 us
  local copies, waits for them, and re-layouts: 8.83 us -> 11.8 us
  other arithmetic: 5.18 us -> 7.78 us
  matrix products: 15.1 us -> 16.8 us
    ppermute x1 -> x2, waiting for transfers between devices: 12 us -> 1.73 us  [the longest x1 1.73 us: local(): border = lax.ppermute(own_border, 'chan', pairs)]
    unnamed x14 -> x27, local copies, waits for them, and re-layouts: 3.77 us -> 6.78 us
    ppermute x1 -> x2, starting transfers between devices: 1.69 us -> 3.45 us  [the longest x1 3 us: local(): raw_blocks.append(lax.ppermute(inputs, 'chan', pairs))]
    concatenate x1, other arithmetic: 2.53 us -> 3.94 us  [local(): input_local = jnp.concatenate(blocks, axis=0)]
    dot_general x9, matrix products: 2.84 us -> 4.12 us  [local(): lax.dot_general(grad_pre, window, (((1,), (1,)), ((), ())), preferred_ele...]
    ppermute x4, starting transfers between devices: 4.76 us -> 3.66 us  [padded_2(): before = lax.ppermute(last, axis, up)]
    unnamed x7, other arithmetic: 0.18 us -> 1.16 us
  transfers between devices with their start and end apart: 18 -> 19, of which waited for: 13 -> 12; matrix products, arithmetic and copies ran while one was open for 15% -> 18% of each run, Pallas kernels for 0% -> 0%
where the time goes in v7:
time: 79.3 us; the launch traced here: 78.9 us
  starting transfers between devices  23.2 us (29%)
  waiting for transfers between devices  18 us (23%)
  matrix products  16.8 us (21%)
  local copies, waits for them, and re-layouts  11.8 us (15%)
  other arithmetic  7.78 us (10%)
  between operations  1.34 us (2%)
    dot_general x36, matrix products, conv_taps(): jnp.dot(kernel[tap_row, tap_col], window, preferred_element_type=jnp.floa...  12.6 us
    unnamed x27, local copies, waits for them, and re-layouts  6.78 us
    ppermute x4, waiting for transfers between devices, direct_all_gather(): pieces.append(lax.ppermute(sent, axis, pairs).astype(jnp.float32))  6.14 us
    ppermute x4, starting transfers between devices, direct_reduce_scatter(): lax.ppermute(piece.astype(send_dtype), axis, pairs).astype(jnp.float32)  5.62 us
    ppermute x4, starting transfers between devices, padded_2(): after = lax.ppermute(initial, axis, down)  5.51 us
    ppermute x4, waiting for transfers between devices, direct_reduce_scatter(): lax.ppermute(piece.astype(send_dtype), axis, pairs).astype(jnp.float32)  4.69 us
    dot_general x9, matrix products, local(): lax.dot_general(grad_pre, window, (((1,), (1,)), ((), ())), preferred_ele...  4.12 us
    concatenate x1, other arithmetic, local(): input_local = jnp.concatenate(blocks, axis=0)  3.94 us
  transfers between devices with their start and end apart: 19, of which 12 were waited for; matrix products, arithmetic and copies ran while one was open for 18% of the time, Pallas kernels for 0%

profile of v7, /device:TPU:0, one launch (start us, length us, event | category | flops | bytes accessed | tf_op | source)
XLA Modules:
  0.0 78.9 jit_solution(10833526837504374404)
XLA Ops:
  0.7 1.6 %copy.12 = bf16[128,16,128]{0,2,1:T(8,128)(2,1)S(1)} copy(bf16[128,16,128]{2,1,0:T(8,128)(2,1)} %param.4) | data formatting | bytes 1048576 | tf_op args[0]
  2.2 3.0 %collective-permute-start.5 = (bf16[128,16,128]{0,2,1:T(8,128)(2,1)S(1)}, bf16[128,16,128]{0,2,1:T(8,128)(2,1)S(1)}, u32[]{:S(2)}, u32[]{:S(2)}) collective-permute-start(bf16[128,16,128]{0,2,1:T(8,128)(2,1)S(1)} %copy.12), channel_id=1, source_target_pairs={{0,2},{2,0},{1,3},{3,1},{4,6},{6,4},{5,7},{7,5},{8,10},{10,8},{9,1... | collective-permute-start | bytes 1572872 | tf_op jit(solution)/shard_map/ppermute | solution.py:118
  5.2 1.6 %collective-permute-start = (bf16[128,16,1]{0,2,1:T(2,128)(2,1)S(1)}, bf16[128,16,1]{0,2,1:T(2,128)(2,1)S(1)}, u32[]{:S(2)}, u32[]{:S(2)}) collective-permute-start(bf16[128,16,1]{0,2,1:T(2,128)(2,1)S(1)} %get-tuple-element.56), channel_id=1, source_target_pairs={{0,4},{4,8},{8,12},{12,0},{1,5},{5,9},{9,13},{13,1},{2,6},{6,10},{... | collective-permute-start | bytes 12296 | tf_op jit(solution)/shard_map/ppermute | solution.py:14
  6.9 2.2 %collective-permute-start.1 = (bf16[128,16,1]{0,2,1:T(2,128)(2,1)S(1)}, bf16[128,16,1]{0,2,1:T(2,128)(2,1)S(1)}, u32[]{:S(2)}, u32[]{:S(2)}) collective-permute-start(bf16[128,16,1]{0,2,1:T(2,128)(2,1)S(1)} %get-tuple-element.57), channel_id=1, source_target_pairs={{4,0},{8,4},{12,8},{0,12},{5,1},{9,5},{13,9},{1,13},{6,2},{10,6},{... | collective-permute-start | bytes 12296 | tf_op jit(solution)/shard_map/ppermute | solution.py:15
  9.1 1.1 %bitcast_convert_fusion = f32[16,8,16,128]{3,2,1,0:T(8,128)} fusion(bf16[128,16,128]{2,1,0:T(8,128)(2,1)S(1)} %copy-done.9), kind=kLoop, calls=%fused_computation.201 | loop fusion | flops 262144 | bytes 1572864
  10.2 0.8 %dynamic-slice_bitcast_fusion.2 = (bf16[3,3,128,128]{2,3,1,0:T(8,128)(2,1)}, bf16[3,3,128,128]{2,3,1,0:T(8,128)(2,1)S(1)}) fusion(bf16[3,3,128,256]{3,2,1,0:T(8,128)(2,1)S(1)} %copy-done.7, s32[]{:T(128)S(6)} %select_n.94, s32[]{:T(128)S(6)} %select_n.97), kind=kLoop, calls=%fused_computation.101 | loop fusion | bytes 1179656 | tf_op jit(solution)/shard_map/transpose | solution.py:169
  12.8 0.9 %fusion.54 = (bf16[128,16,128]{0,2,1:T(8,128)(2,1)S(1)}, bf16[128,16,128]{0,2,1:T(8,128)(2,1)S(1)}, bf16[128,16,128]{0,2,1:T(8,128)(2,1)S(1)}, bf16[128,16,128]{...) fusion(bf16[128,18,130]{0,2,1:T(8,128)(2,1)S(1)} %maximum_selec, ...), kind=kLoop, calls=%fused_computation.198 | loop fusion | bytes 9437184 | tf_op jit(solution)/shard_map/slice | solution.py:37
  17.0 1.7 %collective-permute-done.4 = bf16[128,292]{0,1:T(8,128)(2,1)S(1)} collective-permute-done((bf16[128,292]{0,1:T(8,128)(2,1)S(1)}, bf16[128,292]{0,1:T(8,128)(2,1)S(1)}, u32[]{:S(2)}, u32[]{:S(2)}) %collective-permute-start.4) | collective-permute-done | bytes 74784 | tf_op jit(solution)/shard_map/ppermute | solution.py:124
  19.0 1.0 %fusion.52 = (bf16[128,16,128]{0,2,1:T(8,128)(2,1)S(1)}, bf16[128,16,128]{0,2,1:T(8,128)(2,1)S(1)}, bf16[128,16,128]{0,2,1:T(8,128)(2,1)S(1)}, bf16[128,16,128]{...) fusion(bf16[128,18,130]{0,2,1:T(8,128)(2,1)S(1)} %pad_maximum_f, ...), kind=kLoop, calls=%fused_computation.196 | loop fusion | bytes 9437184 | tf_op jit(solution)/shard_map/slice | solution.py:37
  20.0 3.9 %fusion.14 = (bf16[256,16,128]{0,2,1:T(8,128)(2,1)}, bf16[256,16,128]{0,2,1:T(8,128)(2,1)}, bf16[256,16,128]{0,2,1:T(8,128)(2,1)}, bf16[256,16,128]{0,2,1:T(8,12...) fusion(bf16[128,18,130]{0,2,1:T(8,128)(2,1)S(1)} %maximum_selec, ...), kind=kLoop, calls=%fused_computation.81 | loop fusion | flops 18874368 | bytes 10635264 | tf_op jit(solution)/shard_map/concatenate | solution.py:140
  26.4 0.9 %copy-done.6 = f32[16,8,16,128]{3,2,1,0:T(8,128)S(1)} copy-done((f32[16,8,16,128]{3,2,1,0:T(8,128)S(1)}, f32[16,8,16,128]{3,2,1,0:T(8,128)}, u32[]{:S(2)}) %copy-start.6) | copy-done | bytes 1048600
  27.3 1.8 %convert_reduce_fusion = (f32[128]{0:T(128)S(1)}, bf16[128,2048]{1,0:T(8,128)(2,1)S(1)}) fusion(f32[128]{0:T(128)S(1)} %copy-done.10, f32[128,2048]{1,0:T(8,128)S(1)} %convolution_add_fusion.24, f32[128,2048]{1,0:T(8,128)S(1)} %convolution_add_fusion.17, bf16[128,2048]{0,1:T(8,128)(2,1)S(1)} %bitcast.350, bf16[3,3,128,256]{3,2,1,0:T(8,128)(2,1)} %param.6, ...), kind=kOutput, calls=%fused_computation.89 | convolution fusion | flops 71040896 | bytes 4228104 | tf_op jit(solution)/shard_map/dot_general | solution.py:50
  29.4 1.6 %convolution_bitcast_fusion.6 = f32[1,128,256]{2,1,0:T(8,128)S(1)} fusion(bf16[128,2048]{1,0:T(8,128)(2,1)S(1)} %get-tuple-element.63, bf16[256,2048]{0,1:T(8,128)(2,1)} %bitcast.330), kind=kOutput, calls=%fused_computation.71 | convolution fusion | flops 134217728 | bytes 1703936 | tf_op jit(solution)/shard_map/dot_general | solution.py:147
  31.3 0.9 %copy-done.4 = bf16[256,16,128]{0,2,1:T(8,128)(2,1)S(1)} copy-done((bf16[256,16,128]{0,2,1:T(8,128)(2,1)S(1)}, bf16[256,16,128]{0,2,1:T(8,128)(2,1)}, u32[]{:S(2)}) %copy-start.4) | copy-done | bytes 1048600
  33.0 0.8 %copy-done.2 = bf16[256,16,128]{0,2,1:T(8,128)(2,1)S(1)} copy-done((bf16[256,16,128]{0,2,1:T(8,128)(2,1)S(1)}, bf16[256,16,128]{0,2,1:T(8,128)(2,1)}, u32[]{:S(2)}) %copy-start.2) | copy-done | bytes 1048600
  37.2 1.9 %collective-permute-start.6 = (bf16[128,16,1]{0,2,1:T(2,128)(2,1)S(1)}, bf16[128,16,1]{0,2,1:T(2,128)(2,1)S(1)}, u32[]{:S(2)}, u32[]{:S(2)}) collective-permute-start(bf16[128,16,1]{0,2,1:T(2,128)(2,1)S(1)} %get-tuple-element.54), channel_id=1, source_target_pairs={{0,4},{4,8},{8,12},{12,0},{1,5},{5,9},{9,13},{13,1},{2,6},{6,10},{... | collective-permute-start | bytes 12296 | tf_op jit(solution)/shard_map/ppermute | solution.py:14
  39.0 2.3 %collective-permute-start.7 = (bf16[128,16,1]{0,2,1:T(2,128)(2,1)S(1)}, bf16[128,16,1]{0,2,1:T(2,128)(2,1)S(1)}, u32[]{:S(2)}, u32[]{:S(2)}) collective-permute-start(bf16[128,16,1]{0,2,1:T(2,128)(2,1)S(1)} %get-tuple-element.55), channel_id=1, source_target_pairs={{4,0},{8,4},{12,8},{0,12},{5,1},{9,5},{13,9},{1,13},{6,2},{10,6},{... | collective-permute-start | bytes 12296 | tf_op jit(solution)/shard_map/ppermute | solution.py:15
  41.4 1.4 %collective-permute-done.6 = bf16[128,16,1]{0,2,1:T(2,128)(2,1)S(1)} collective-permute-done((bf16[128,16,1]{0,2,1:T(2,128)(2,1)S(1)}, bf16[128,16,1]{0,2,1:T(2,128)(2,1)S(1)}, u32[]{:S(2)}, u32[]{:S(2)}) %collective-permute-start.6) | collective-permute-done | bytes 4128 | tf_op jit(solution)/shard_map/ppermute | solution.py:14
  44.6 0.9 %fusion.51 = (bf16[128,16,128]{0,2,1:T(8,128)(2,1)S(1)}, bf16[128,16,128]{0,2,1:T(8,128)(2,1)S(1)}, bf16[128,16,128]{0,2,1:T(8,128)(2,1)S(1)}, bf16[128,16,128]{...) fusion(bf16[128,18,130]{0,2,1:T(8,128)(2,1)S(1)} %maximum_selec, ...), kind=kLoop, calls=%fused_computation.195 | loop fusion | bytes 9437184 | tf_op jit(solution)/shard_map/slice | solution.py:37
  50.0 1.5 %collective-permute-start.12 = (bf16[296,128]{1,0:T(8,128)(2,1)S(1)}, bf16[296,128]{1,0:T(8,128)(2,1)S(1)}, u32[]{:S(2)}, u32[]{:S(2)}) collective-permute-start(bf16[296,128]{1,0:T(8,128)(2,1)S(1)} %get-tuple-element.45), channel_id=1, source_target_pairs={{0,4},{4,8},{8,12},{12,0},{1,5},{5,9},{9,13},{13,1},{2,6},{6,10},{... | collective-permute-start | bytes 227336 | tf_op jit(solution)/shard_map/ppermute | solution.py:64
  51.5 3.1 %collective-permute-start.13 = (bf16[296,128]{1,0:T(8,128)(2,1)S(1)}, bf16[296,128]{1,0:T(8,128)(2,1)S(1)}, u32[]{:S(2)}, u32[]{:S(2)}) collective-permute-start(bf16[296,128]{1,0:T(8,128)(2,1)S(1)} %get-tuple-element.47), channel_id=1, source_target_pairs={{0,8},{4,12},{8,0},{12,4},{1,9},{5,13},{9,1},{13,5},{2,10},{6,14},... | collective-permute-start | bytes 227336 | tf_op jit(solution)/shard_map/ppermute | solution.py:64
  54.5 0.9 %collective-permute-start.14 = (bf16[296,128]{1,0:T(8,128)(2,1)S(1)}, bf16[296,128]{1,0:T(8,128)(2,1)S(1)}, u32[]{:S(2)}, u32[]{:S(2)}) collective-permute-start(bf16[296,128]{1,0:T(8,128)(2,1)S(1)} %get-tuple-element.46), channel_id=1, source_target_pairs={{0,12},{4,0},{8,4},{12,8},{1,13},{5,1},{9,5},{13,9},{2,14},{6,2},{... | collective-permute-start | bytes 227336 | tf_op jit(solution)/shard_map/ppermute | solution.py:64
  55.8 1.5 %collective-permute-done.12 = bf16[296,128]{1,0:T(8,128)(2,1)S(1)} collective-permute-done((bf16[296,128]{1,0:T(8,128)(2,1)S(1)}, bf16[296,128]{1,0:T(8,128)(2,1)S(1)}, u32[]{:S(2)}, u32[]{:S(2)}) %collective-permute-start.12) | collective-permute-done | bytes 75808 | tf_op jit(solution)/shard_map/ppermute | solution.py:64
  57.2 2.9 %collective-permute-done.13 = bf16[296,128]{1,0:T(8,128)(2,1)S(1)} collective-permute-done((bf16[296,128]{1,0:T(8,128)(2,1)S(1)}, bf16[296,128]{1,0:T(8,128)(2,1)S(1)}, u32[]{:S(2)}, u32[]{:S(2)}) %collective-permute-start.13) | collective-permute-done | bytes 75808 | tf_op jit(solution)/shard_map/ppermute | solution.py:64
  60.5 2.4 %collective-permute-start.15 = (bf16[296,128]{1,0:T(8,128)(2,1)S(1)}, bf16[296,128]{1,0:T(8,128)(2,1)S(1)}, u32[]{:S(2)}, u32[]{:S(2)}) collective-permute-start(bf16[296,128]{1,0:T(8,128)(2,1)S(1)} %get-tuple-element.3), channel_id=1, source_target_pairs={{0,12},{4,0},{8,4},{12,8},{1,13},{5,1},{9,5},{13,9},{2,14},{6,2},{... | collective-permute-start | bytes 227336 | tf_op jit(solution)/shard_map/ppermute | solution.py:76
  63.3 1.6 %collective-permute-start.10 = (bf16[128,2048]{1,0:T(8,128)(2,1)S(1)}, bf16[128,2048]{1,0:T(8,128)(2,1)S(1)}, u32[]{:S(2)}, u32[]{:S(2)}) collective-permute-start(bf16[128,2048]{1,0:T(8,128)(2,1)S(1)} %fusion.2), channel_id=1, source_target_pairs={{0,2},{2,0},{1,3},{3,1},{4,6},{6,4},{5,7},{7,5},{8,10},{10,8},{9,1... | collective-permute-start | bytes 1572872 | tf_op jit(solution)/shard_map/ppermute | solution.py:168
  64.8 0.9 %collective-permute-start.16 = (bf16[296,128]{1,0:T(8,128)(2,1)S(1)}, bf16[296,128]{1,0:T(8,128)(2,1)S(1)}, u32[]{:S(2)}, u32[]{:S(2)}) collective-permute-start(bf16[296,128]{1,0:T(8,128)(2,1)S(1)} %get-tuple-element.3), channel_id=1, source_target_pairs={{0,8},{4,12},{8,0},{12,4},{1,9},{5,13},{9,1},{13,5},{2,10},{6,14},... | collective-permute-start | bytes 227336 | tf_op jit(solution)/shard_map/ppermute | solution.py:76
  65.7 5.2 %collective-permute-done.16 = bf16[296,128]{1,0:T(8,128)(2,1)S(1)} collective-permute-done((bf16[296,128]{1,0:T(8,128)(2,1)S(1)}, bf16[296,128]{1,0:T(8,128)(2,1)S(1)}, u32[]{:S(2)}, u32[]{:S(2)}) %collective-permute-start.16) | collective-permute-done | bytes 75808 | tf_op jit(solution)/shard_map/ppermute | solution.py:76
  70.9 1.0 %collective-permute-done.17 = bf16[296,128]{1,0:T(8,128)(2,1)S(1)} collective-permute-done((bf16[296,128]{1,0:T(8,128)(2,1)S(1)}, bf16[296,128]{1,0:T(8,128)(2,1)S(1)}, u32[]{:S(2)}, u32[]{:S(2)}) %collective-permute-start.17) | collective-permute-done | bytes 75808 | tf_op jit(solution)/shard_map/ppermute | solution.py:76
  72.8 2.5 %collective-permute-done.10 = bf16[128,2048]{1,0:T(8,128)(2,1)S(1)} collective-permute-done((bf16[128,2048]{1,0:T(8,128)(2,1)S(1)}, bf16[128,2048]{1,0:T(8,128)(2,1)S(1)}, u32[]{:S(2)}, u32[]{:S(2)}) %collective-permute-start.10) | collective-permute-done | bytes 524320 | tf_op jit(solution)/shard_map/ppermute | solution.py:168
  75.7 0.9 %copy.25 = bf16[16,8,16,128]{3,2,1,0:T(8,128)(2,1)} copy(bf16[16,8,16,128]{3,1,2,0:T(8,128)(2,1)S(1)} %fusion.21) | data formatting | bytes 1048576
  77.7 1.2 %fusion.6 = f32[3,3,128,256]{3,2,1,0:T(8,128)} fusion(s32[]{:T(128)S(6)} %select_n.114, f32[3,3,128,256]{3,2,1,0:T(8,128)S(1)} %reshape.198), kind=kLoop, calls=%fused_computation.63 | loop fusion | flops 294912 | bytes 2359300 | tf_op jit(solution)/shard_map/concatenate | solution.py:157
  (122 shorter events, 21.8 us)
Async XLA Ops:
  0.6 8.5 %copy-start.9 = (bf16[128,16,128]{2,1,0:T(8,128)(2,1)S(1)}, bf16[128,16,128]{2,1,0:T(8,128)(2,1)}, u32[]{:S(2)}) copy-start(bf16[128,16,128]{2,1,0:T(8,128)(2,1)} %param.5) | copy-start | bytes 1572868
  0.6 9.6 %copy-start.7 = (bf16[3,3,128,256]{3,2,1,0:T(8,128)(2,1)S(1)}, bf16[3,3,128,256]{3,2,1,0:T(8,128)(2,1)}, u32[]{:S(2)}) copy-start(bf16[3,3,128,256]{3,2,1,0:T(8,128)(2,1)} %param.6) | copy-start | bytes 1769476
  2.2 16.6 %collective-permute-start.5 = (bf16[128,16,128]{0,2,1:T(8,128)(2,1)S(1)}, bf16[128,16,128]{0,2,1:T(8,128)(2,1)S(1)}, u32[]{:S(2)}, u32[]{:S(2)}) collective-permute-start(bf16[128,16,128]{0,2,1:T(8,128)(2,1)S(1)} %copy.12), channel_id=1, source_target_pairs={{0,2},{2,0},{1,3},{3,1},{4,6},{6,4},{5,7},{7,5},{8,10},{10,8},{9,1... | collective-permute-start | bytes 1572872 | tf_op jit(solution)/shard_map/ppermute | solution.py:118
  5.2 5.8 %collective-permute-start = (bf16[128,16,1]{0,2,1:T(2,128)(2,1)S(1)}, bf16[128,16,1]{0,2,1:T(2,128)(2,1)S(1)}, u32[]{:S(2)}, u32[]{:S(2)}) collective-permute-start(bf16[128,16,1]{0,2,1:T(2,128)(2,1)S(1)} %get-tuple-element.56), channel_id=1, source_target_pairs={{0,4},{4,8},{8,12},{12,0},{1,5},{5,9},{9,13},{13,1},{2,6},{6,10},{... | collective-permute-start | bytes 12296 | tf_op jit(solution)/shard_map/ppermute | solution.py:14
  6.9 4.2 %collective-permute-start.1 = (bf16[128,16,1]{0,2,1:T(2,128)(2,1)S(1)}, bf16[128,16,1]{0,2,1:T(2,128)(2,1)S(1)}, u32[]{:S(2)}, u32[]{:S(2)}) collective-permute-start(bf16[128,16,1]{0,2,1:T(2,128)(2,1)S(1)} %get-tuple-element.57), channel_id=1, source_target_pairs={{4,0},{8,4},{12,8},{0,12},{5,1},{9,5},{13,9},{1,13},{6,2},{10,6},{... | collective-permute-start | bytes 12296 | tf_op jit(solution)/shard_map/ppermute | solution.py:15
  11.0 1.3 %collective-permute-start.2 = (bf16[128,1,130]{0,2,1:T(8,128)(2,1)S(1)}, bf16[128,1,130]{0,2,1:T(8,128)(2,1)S(1)}, u32[]{:S(2)}, u32[]{:S(2)}) collective-permute-start(bf16[128,1,130]{0,2,1:T(8,128)(2,1)S(1)} %get-tuple-element.52), channel_id=1, source_target_pairs={{0,1},{1,0},{2,3},{3,2},{4,5},{5,4},{6,7},{7,6},{8,9},{9,8},{10,11... | collective-permute-start | bytes 99848 | tf_op jit(solution)/shard_map/ppermute | solution.py:14
  11.1 1.4 %collective-permute-start.3 = (bf16[128,1,130]{0,2,1:T(8,128)(2,1)S(1)}, bf16[128,1,130]{0,2,1:T(8,128)(2,1)S(1)}, u32[]{:S(2)}, u32[]{:S(2)}) collective-permute-start(bf16[128,1,130]{0,2,1:T(8,128)(2,1)S(1)} %get-tuple-element.53), channel_id=1, source_target_pairs={{1,0},{0,1},{3,2},{2,3},{5,4},{4,5},{7,6},{6,7},{9,8},{8,9},{11,10... | collective-permute-start | bytes 99848 | tf_op jit(solution)/shard_map/ppermute | solution.py:15
  13.8 4.9 %collective-permute-start.4 = (bf16[128,292]{0,1:T(8,128)(2,1)S(1)}, bf16[128,292]{0,1:T(8,128)(2,1)S(1)}, u32[]{:S(2)}, u32[]{:S(2)}) collective-permute-start(bf16[128,292]{0,1:T(8,128)(2,1)S(1)} %pad_maximum_fusion.3), channel_id=1, source_target_pairs={{0,2},{2,0},{1,3},{3,1},{4,6},{6,4},{5,7},{7,5},{8,10},{10,8},{9,1... | collective-permute-start | bytes 224264 | tf_op jit(solution)/shard_map/ppermute | solution.py:124
  26.1 1.2 %copy-start.6 = (f32[16,8,16,128]{3,2,1,0:T(8,128)S(1)}, f32[16,8,16,128]{3,2,1,0:T(8,128)}, u32[]{:S(2)}) copy-start(f32[16,8,16,128]{3,2,1,0:T(8,128)} %bitcast_convert_fusion) | copy-start | bytes 3145732
  26.1 1.2 %copy-start.10 = (f32[128]{0:T(128)S(1)}, f32[128]{0:T(128)}, u32[]{:S(2)}) copy-start(f32[128]{0:T(128)} %param.7) | copy-start | bytes 1540
  29.3 1.7 %copy-start.5 = (bf16[256,16,128]{0,2,1:T(8,128)(2,1)S(1)}, bf16[256,16,128]{0,2,1:T(8,128)(2,1)}, u32[]{:S(2)}) copy-start(bf16[256,16,128]{0,2,1:T(8,128)(2,1)} %get-tuple-element.6) | copy-start | bytes 3145732
  31.0 1.2 %copy-start.4 = (bf16[256,16,128]{0,2,1:T(8,128)(2,1)S(1)}, bf16[256,16,128]{0,2,1:T(8,128)(2,1)}, u32[]{:S(2)}) copy-start(bf16[256,16,128]{0,2,1:T(8,128)(2,1)} %get-tuple-element.5) | copy-start | bytes 3145732
  31.3 1.3 %copy-start.3 = (bf16[256,16,128]{0,2,1:T(8,128)(2,1)S(1)}, bf16[256,16,128]{0,2,1:T(8,128)(2,1)}, u32[]{:S(2)}) copy-start(bf16[256,16,128]{0,2,1:T(8,128)(2,1)} %get-tuple-element.10) | copy-start | bytes 3145732
  32.5 1.2 %copy-start.2 = (bf16[256,16,128]{0,2,1:T(8,128)(2,1)S(1)}, bf16[256,16,128]{0,2,1:T(8,128)(2,1)}, u32[]{:S(2)}) copy-start(bf16[256,16,128]{0,2,1:T(8,128)(2,1)} %get-tuple-element.9) | copy-start | bytes 3145732
  33.0 1.3 %copy-start.1 = (bf16[256,16,128]{0,2,1:T(8,128)(2,1)S(1)}, bf16[256,16,128]{0,2,1:T(8,128)(2,1)}, u32[]{:S(2)}) copy-start(bf16[256,16,128]{0,2,1:T(8,128)(2,1)} %get-tuple-element.8) | copy-start | bytes 3145732
  34.1 1.3 %copy-start = (bf16[256,16,128]{0,2,1:T(8,128)(2,1)S(1)}, bf16[256,16,128]{0,2,1:T(8,128)(2,1)}, u32[]{:S(2)}) copy-start(bf16[256,16,128]{0,2,1:T(8,128)(2,1)} %get-tuple-element.12) | copy-start | bytes 3145732
  37.2 5.6 %collective-permute-start.6 = (bf16[128,16,1]{0,2,1:T(2,128)(2,1)S(1)}, bf16[128,16,1]{0,2,1:T(2,128)(2,1)S(1)}, u32[]{:S(2)}, u32[]{:S(2)}) collective-permute-start(bf16[128,16,1]{0,2,1:T(2,128)(2,1)S(1)} %get-tuple-element.54), channel_id=1, source_target_pairs={{0,4},{4,8},{8,12},{12,0},{1,5},{5,9},{9,13},{13,1},{2,6},{6,10},{... | collective-permute-start | bytes 12296 | tf_op jit(solution)/shard_map/ppermute | solution.py:14
  39.0 3.7 %collective-permute-start.7 = (bf16[128,16,1]{0,2,1:T(2,128)(2,1)S(1)}, bf16[128,16,1]{0,2,1:T(2,128)(2,1)S(1)}, u32[]{:S(2)}, u32[]{:S(2)}) collective-permute-start(bf16[128,16,1]{0,2,1:T(2,128)(2,1)S(1)} %get-tuple-element.55), channel_id=1, source_target_pairs={{4,0},{8,4},{12,8},{0,12},{5,1},{9,5},{13,9},{1,13},{6,2},{10,6},{... | collective-permute-start | bytes 12296 | tf_op jit(solution)/shard_map/ppermute | solution.py:15
  42.8 1.3 %collective-permute-start.8 = (bf16[128,1,130]{0,2,1:T(8,128)(2,1)S(1)}, bf16[128,1,130]{0,2,1:T(8,128)(2,1)S(1)}, u32[]{:S(2)}, u32[]{:S(2)}) collective-permute-start(bf16[128,1,130]{0,2,1:T(8,128)(2,1)S(1)} %get-tuple-element.50), channel_id=1, source_target_pairs={{0,1},{1,0},{2,3},{3,2},{4,5},{5,4},{6,7},{7,6},{8,9},{9,8},{10,11... | collective-permute-start | bytes 99848 | tf_op jit(solution)/shard_map/ppermute | solution.py:14
  42.9 1.4 %collective-permute-start.9 = (bf16[128,1,130]{0,2,1:T(8,128)(2,1)S(1)}, bf16[128,1,130]{0,2,1:T(8,128)(2,1)S(1)}, u32[]{:S(2)}, u32[]{:S(2)}) collective-permute-start(bf16[128,1,130]{0,2,1:T(8,128)(2,1)S(1)} %get-tuple-element.51), channel_id=1, source_target_pairs={{1,0},{0,1},{3,2},{2,3},{5,4},{4,5},{7,6},{6,7},{9,8},{8,9},{11,10... | collective-permute-start | bytes 99848 | tf_op jit(solution)/shard_map/ppermute | solution.py:15
  43.4 6.4 %collective-permute-start.11 = (f32[1184,128]{1,0:T(8,128)S(1)}, f32[1184,128]{1,0:T(8,128)S(1)}, u32[]{:S(2)}, u32[]{:S(2)}) collective-permute-start(f32[1184,128]{1,0:T(8,128)S(1)} %dynamic-slice_bitcast_fusion), channel_id=1, source_target_pairs={{0,1},{1,0},{2,3},{3,2},{4,5},{5,4},{6,7},{7,6},{8,9},{9,8},{10,11... | collective-permute-start | bytes 1818632 | tf_op jit(solution)/shard_map/ppermute | solution.py:64
  44.6 1.0 %copy-start.8 = (bf16[3,3,128,128]{2,3,1,0:T(8,128)(2,1)S(1)}, bf16[3,3,128,128]{2,3,1,0:T(8,128)(2,1)}, u32[]{:S(2)}) copy-start(bf16[3,3,128,128]{2,3,1,0:T(8,128)(2,1)} %get-tuple-element.48) | copy-start | bytes 884740
  50.0 7.3 %collective-permute-start.12 = (bf16[296,128]{1,0:T(8,128)(2,1)S(1)}, bf16[296,128]{1,0:T(8,128)(2,1)S(1)}, u32[]{:S(2)}, u32[]{:S(2)}) collective-permute-start(bf16[296,128]{1,0:T(8,128)(2,1)S(1)} %get-tuple-element.45), channel_id=1, source_target_pairs={{0,4},{4,8},{8,12},{12,0},{1,5},{5,9},{9,13},{13,1},{2,6},{6,10},{... | collective-permute-start | bytes 227336 | tf_op jit(solution)/shard_map/ppermute | solution.py:64
  51.5 8.7 %collective-permute-start.13 = (bf16[296,128]{1,0:T(8,128)(2,1)S(1)}, bf16[296,128]{1,0:T(8,128)(2,1)S(1)}, u32[]{:S(2)}, u32[]{:S(2)}) collective-permute-start(bf16[296,128]{1,0:T(8,128)(2,1)S(1)} %get-tuple-element.47), channel_id=1, source_target_pairs={{0,8},{4,12},{8,0},{12,4},{1,9},{5,13},{9,1},{13,5},{2,10},{6,14},... | collective-permute-start | bytes 227336 | tf_op jit(solution)/shard_map/ppermute | solution.py:64
  54.5 5.9 %collective-permute-start.14 = (bf16[296,128]{1,0:T(8,128)(2,1)S(1)}, bf16[296,128]{1,0:T(8,128)(2,1)S(1)}, u32[]{:S(2)}, u32[]{:S(2)}) collective-permute-start(bf16[296,128]{1,0:T(8,128)(2,1)S(1)} %get-tuple-element.46), channel_id=1, source_target_pairs={{0,12},{4,0},{8,4},{12,8},{1,13},{5,1},{9,5},{13,9},{2,14},{6,2},{... | collective-permute-start | bytes 227336 | tf_op jit(solution)/shard_map/ppermute | solution.py:64
  60.5 5.2 %collective-permute-start.15 = (bf16[296,128]{1,0:T(8,128)(2,1)S(1)}, bf16[296,128]{1,0:T(8,128)(2,1)S(1)}, u32[]{:S(2)}, u32[]{:S(2)}) collective-permute-start(bf16[296,128]{1,0:T(8,128)(2,1)S(1)} %get-tuple-element.3), channel_id=1, source_target_pairs={{0,12},{4,0},{8,4},{12,8},{1,13},{5,1},{9,5},{13,9},{2,14},{6,2},{... | collective-permute-start | bytes 227336 | tf_op jit(solution)/shard_map/ppermute | solution.py:76
  63.3 12.1 %collective-permute-start.10 = (bf16[128,2048]{1,0:T(8,128)(2,1)S(1)}, bf16[128,2048]{1,0:T(8,128)(2,1)S(1)}, u32[]{:S(2)}, u32[]{:S(2)}) collective-permute-start(bf16[128,2048]{1,0:T(8,128)(2,1)S(1)} %fusion.2), channel_id=1, source_target_pairs={{0,2},{2,0},{1,3},{3,1},{4,6},{6,4},{5,7},{7,5},{8,10},{10,8},{9,1... | collective-permute-start | bytes 1572872 | tf_op jit(solution)/shard_map/ppermute | solution.py:168
  64.8 6.1 %collective-permute-start.16 = (bf16[296,128]{1,0:T(8,128)(2,1)S(1)}, bf16[296,128]{1,0:T(8,128)(2,1)S(1)}, u32[]{:S(2)}, u32[]{:S(2)}) collective-permute-start(bf16[296,128]{1,0:T(8,128)(2,1)S(1)} %get-tuple-element.3), channel_id=1, source_target_pairs={{0,8},{4,12},{8,0},{12,4},{1,9},{5,13},{9,1},{13,5},{2,10},{6,14},... | collective-permute-start | bytes 227336 | tf_op jit(solution)/shard_map/ppermute | solution.py:76
  65.7 6.2 %collective-permute-start.17 = (bf16[296,128]{1,0:T(8,128)(2,1)S(1)}, bf16[296,128]{1,0:T(8,128)(2,1)S(1)}, u32[]{:S(2)}, u32[]{:S(2)}) collective-permute-start(bf16[296,128]{1,0:T(8,128)(2,1)S(1)} %get-tuple-element.3), channel_id=1, source_target_pairs={{0,4},{4,8},{8,12},{12,0},{1,5},{5,9},{9,13},{13,1},{2,6},{6,10},{... | collective-permute-start | bytes 227336 | tf_op jit(solution)/shard_map/ppermute | solution.py:76
  72.1 4.5 %collective-permute-start.18 = (f32[1184,128]{1,0:T(8,128)S(1)}, f32[1184,128]{1,0:T(8,128)S(1)}, u32[]{:S(2)}, u32[]{:S(2)}) collective-permute-start(f32[1184,128]{1,0:T(8,128)S(1)} %bitcast.331), channel_id=1, source_target_pairs={{0,1},{1,0},{2,3},{3,2},{4,5},{5,4},{6,7},{7,6},{8,9},{9,8},{10,11... | collective-permute-start | bytes 1818632 | tf_op jit(solution)/shard_map/ppermute | solution.py:76

commit v8 on v7

--- a/solution.py
+++ b/solution.py
@@ -79,15 +79,18 @@
     return stacked.reshape(-1, chunk.shape[-1])
 
 
-def all_sum(flat, send_dtype):
+def sum_start(flat, send_dtype):
     parts = lax.axis_size("lat") * lax.axis_size("lon")
     quantum = parts * 8 * 128
     padded = jnp.pad(flat, (0, (-flat.size) % quantum)).reshape(-1, 128)
     rows = direct_reduce_scatter(padded, "lat", jnp.float32)
-    rows = direct_reduce_scatter(rows, "lon", send_dtype)
+    return direct_reduce_scatter(rows, "lon", send_dtype)
+
+
+def sum_finish(rows, size, send_dtype):
     rows = direct_all_gather(rows, "lon", send_dtype)
     rows = direct_all_gather(rows, "lat", jnp.float32)
-    return rows.reshape(-1)[: flat.size]
+    return rows.reshape(-1)[:size]
 
 
 def border_of(padded):
@@ -151,7 +154,9 @@
         taps.append(jnp.stack(row_taps))
     weight_part = jnp.stack(taps)
     flat = jnp.concatenate([weight_part.reshape(-1), bias_part])
-    flat = all_sum(flat, jnp.bfloat16)
+    scattered = sum_start(flat, jnp.bfloat16)
+    grad_pre, scattered = lax.optimization_barrier((grad_pre, scattered))
+    flat = sum_finish(scattered, flat.size, jnp.bfloat16)
     weight_local = flat[: weight_part.size].reshape(weight_part.shape)
     bias_grad = flat[weight_part.size :]
     doubled = jnp.concatenate([weight_local, weight_local], axis=3)

time: 79.3 us -> 75.8 us (0.956)
  waiting for transfers between devices: 18 us -> 30 us
  starting transfers between devices: 23.2 us -> 16.3 us
  local copies, waits for them, and re-layouts: 11.8 us -> 7.72 us
  other arithmetic: 7.78 us -> 5.38 us
  matrix products: 16.8 us -> 14.8 us
    ppermute x1, waiting for transfers between devices: 2.51 us -> 8.91 us  [local(): received.append(lax.ppermute(part.astype(jnp.bfloat16), 'chan', pairs))]
    ppermute x4, waiting for transfers between devices: 6.14 us -> 0.01 us  [direct_all_gather(): pieces.append(lax.ppermute(sent, axis, pairs).astype(jnp.float32))]
    ppermute x4, waiting for transfers between devices: 2.59 us -> 7.29 us  [padded_2(): before = lax.ppermute(last, axis, up)]
    ppermute x4, waiting for transfers between devices: 4.69 us -> 8.99 us  [direct_reduce_scatter(): lax.ppermute(piece.astype(send_dtype), axis, pairs).astype(jnp.float32)]
    ppermute x4, starting transfers between devices: 5.62 us -> 2.15 us  [direct_reduce_scatter(): lax.ppermute(piece.astype(send_dtype), axis, pairs).astype(jnp.float32)]
    unnamed x27 -> x11, local copies, waits for them, and re-layouts: 6.78 us -> 3.4 us
    ppermute x4, waiting for transfers between devices: 0.33 us -> 3.56 us  [padded_2(): after = lax.ppermute(initial, axis, down)]
    ppermute x4, starting transfers between devices: 3.66 us -> 1.78 us  [padded_2(): before = lax.ppermute(last, axis, up)]
  transfers between devices with their start and end apart: 19 -> 19, of which waited for: 12 -> 11; matrix products, arithmetic and copies ran while one was open for 18% -> 16% of each run, Pallas kernels for 0% -> 0%
where the time goes in v8:
time: 75.8 us; the launch traced here: 75.7 us
  waiting for transfers between devices  30 us (40%)
  starting transfers between devices  16.3 us (22%)
  matrix products  14.8 us (20%)
  local copies, waits for them, and re-layouts  7.72 us (10%)
  other arithmetic  5.38 us (7%)
  between operations  1.46 us (2%)
    dot_general x36, matrix products, conv_taps(): jnp.dot(kernel[tap_row, tap_col], window, preferred_element_type=jnp.floa...  11.9 us
    ppermute x4, waiting for transfers between devices, direct_reduce_scatter(): lax.ppermute(piece.astype(send_dtype), axis, pairs).astype(jnp.float32)  8.99 us
    ppermute x1, waiting for transfers between devices, local(): received.append(lax.ppermute(part.astype(jnp.bfloat16), 'chan', pairs))  8.91 us
    ppermute x4, waiting for transfers between devices, padded_2(): before = lax.ppermute(last, axis, up)  7.29 us
    ppermute x4, starting transfers between devices, padded_2(): after = lax.ppermute(initial, axis, down)  5.1 us
    ppermute x4, waiting for transfers between devices, padded_2(): after = lax.ppermute(initial, axis, down)  3.56 us
    unnamed x11, local copies, waits for them, and re-layouts  3.4 us
    ppermute x1, starting transfers between devices, local(): raw_blocks.append(lax.ppermute(inputs, 'chan', pairs))  3 us
  transfers between devices with their start and end apart: 19, of which 11 were waited for; matrix products, arithmetic and copies ran while one was open for 16% of the time, Pallas kernels for 0%

profile of v8, /device:TPU:0, one launch (start us, length us, event | category | flops | bytes accessed | tf_op | source)
XLA Modules:
  0.0 75.7 jit_solution(6995470683629483656)
XLA Ops:
  0.6 1.5 %copy.12 = bf16[128,16,128]{0,2,1:T(8,128)(2,1)S(1)} copy(bf16[128,16,128]{2,1,0:T(8,128)(2,1)} %param.4) | data formatting | bytes 1048576 | tf_op args[0]
  2.2 3.0 %collective-permute-start.5 = (bf16[128,16,128]{0,2,1:T(8,128)(2,1)S(1)}, bf16[128,16,128]{0,2,1:T(8,128)(2,1)S(1)}, u32[]{:S(2)}, u32[]{:S(2)}) collective-permute-start(bf16[128,16,128]{0,2,1:T(8,128)(2,1)S(1)} %copy.12), channel_id=1, source_target_pairs={{0,2},{2,0},{1,3},{3,1},{4,6},{6,4},{5,7},{7,5},{8,10},{10,8},{9,1... | collective-permute-start | bytes 1572872 | tf_op jit(solution)/shard_map/ppermute | solution.py:121
  5.2 3.7 %collective-permute-start.1 = (bf16[128,16,1]{0,2,1:T(2,128)(2,1)S(1)}, bf16[128,16,1]{0,2,1:T(2,128)(2,1)S(1)}, u32[]{:S(2)}, u32[]{:S(2)}) collective-permute-start(bf16[128,16,1]{0,2,1:T(2,128)(2,1)S(1)} %get-tuple-element.59), channel_id=1, source_target_pairs={{4,0},{8,4},{12,8},{0,12},{5,1},{9,5},{13,9},{1,13},{6,2},{10,6},{... | collective-permute-start | bytes 12296 | tf_op jit(solution)/shard_map/ppermute | solution.py:15
  9.0 1.2 %collective-permute-done.1 = bf16[128,16,1]{0,2,1:T(2,128)(2,1)S(1)} collective-permute-done((bf16[128,16,1]{0,2,1:T(2,128)(2,1)S(1)}, bf16[128,16,1]{0,2,1:T(2,128)(2,1)S(1)}, u32[]{:S(2)}, u32[]{:S(2)}) %collective-permute-start.1) | collective-permute-done | bytes 4128 | tf_op jit(solution)/shard_map/ppermute | solution.py:15
  10.2 4.1 %collective-permute-done = bf16[128,16,1]{0,2,1:T(2,128)(2,1)S(1)} collective-permute-done((bf16[128,16,1]{0,2,1:T(2,128)(2,1)S(1)}, bf16[128,16,1]{0,2,1:T(2,128)(2,1)S(1)}, u32[]{:S(2)}, u32[]{:S(2)}) %collective-permute-start) | collective-permute-done | bytes 4128 | tf_op jit(solution)/shard_map/ppermute | solution.py:14
  14.4 0.5 collective-permute-start.2
  14.9 0.7 collective-permute-done.3
  16.1 0.9 %fusion.52 = (bf16[128,16,128]{0,2,1:T(8,128)(2,1)S(1)}, bf16[128,16,128]{0,2,1:T(8,128)(2,1)S(1)}, bf16[128,16,128]{0,2,1:T(8,128)(2,1)S(1)}, bf16[128,16,128]{...) fusion(bf16[128,18,130]{0,2,1:T(8,128)(2,1)S(1)} %maximum_selec, ...), kind=kLoop, calls=%fused_computation.197 | loop fusion | bytes 9437184 | tf_op jit(solution)/shard_map/slice | solution.py:37
  17.1 0.6 collective-permute-start.4
  20.5 1.3 %collective-permute-done.4 = bf16[128,292]{0,1:T(8,128)(2,1)S(1)} collective-permute-done((bf16[128,292]{0,1:T(8,128)(2,1)S(1)}, bf16[128,292]{0,1:T(8,128)(2,1)S(1)}, u32[]{:S(2)}, u32[]{:S(2)}) %collective-permute-start.4) | collective-permute-done | bytes 74784 | tf_op jit(solution)/shard_map/ppermute | solution.py:127
  22.0 0.9 %fusion.50 = (bf16[128,16,128]{0,2,1:T(8,128)(2,1)S(1)}, bf16[128,16,128]{0,2,1:T(8,128)(2,1)S(1)}, bf16[128,16,128]{0,2,1:T(8,128)(2,1)S(1)}, bf16[128,16,128]{...) fusion(bf16[128,18,130]{0,2,1:T(8,128)(2,1)S(1)} %pad_maximum_f, ...), kind=kLoop, calls=%fused_computation.195 | loop fusion | bytes 9437184 | tf_op jit(solution)/shard_map/slice | solution.py:37
  22.9 2.5 %fusion.14 = (bf16[256,16,128]{0,2,1:T(8,128)(2,1)S(1)}, bf16[256,16,128]{0,2,1:T(8,128)(2,1)S(1)}, bf16[256,16,128]{0,2,1:T(8,128)(2,1)S(1)}, bf16[256,16,128]{...) fusion(bf16[128,18,130]{0,2,1:T(8,128)(2,1)S(1)} %maximum_selec, ...), kind=kLoop, calls=%fused_computation.81 | loop fusion | flops 18874368 | bytes 10635264 | tf_op jit(solution)/shard_map/concatenate | solution.py:143
  28.3 1.0 %convert_reduce_fusion = (f32[128]{0:T(128)S(1)}, bf16[128,2048]{1,0:T(8,128)(2,1)S(1)}) fusion(f32[128]{0:T(128)S(1)} %copy-done.2, f32[128,2048]{1,0:T(8,128)S(1)} %convolution_add_fusion.24, f32[128,2048]{1,0:T(8,128)S(1)} %convolution_add_fusion.17, bf16[128,2048]{0,1:T(8,128)(2,1)S(1)} %bitcast.349, bf16[3,3,128,256]{3,2,1,0:T(8,128)(2,1)S(1)} %copy-done, ...), kind=kOutput, calls=%fused_computation.90 | convolution fusion | flops 71040896 | bytes 4228104 | tf_op jit(solution)/shard_map/dot_general | solution.py:50
  32.4 0.6 copy.25
  33.3 2.0 %collective-permute-done.6 = f32[1184,128]{1,0:T(8,128)S(1)} collective-permute-done((f32[1184,128]{1,0:T(8,128)S(1)}, f32[1184,128]{1,0:T(8,128)S(1)}, u32[]{:S(2)}, u32[]{:S(2)}) %collective-permute-start.6) | collective-permute-done | bytes 606240 | tf_op jit(solution)/shard_map/ppermute | solution.py:64
  35.4 0.9 %collective-permute-start.9 = (bf16[296,128]{1,0:T(8,128)(2,1)S(1)}, bf16[296,128]{1,0:T(8,128)(2,1)S(1)}, u32[]{:S(2)}, u32[]{:S(2)}) collective-permute-start(bf16[296,128]{1,0:T(8,128)(2,1)S(1)} %get-tuple-element.48), channel_id=1, source_target_pairs={{0,12},{4,0},{8,4},{12,8},{1,13},{5,1},{9,5},{13,9},{2,14},{6,2},{... | collective-permute-start | bytes 227336 | tf_op jit(solution)/shard_map/ppermute | solution.py:64
  36.3 1.2 %collective-permute-start.7 = (bf16[296,128]{1,0:T(8,128)(2,1)S(1)}, bf16[296,128]{1,0:T(8,128)(2,1)S(1)}, u32[]{:S(2)}, u32[]{:S(2)}) collective-permute-start(bf16[296,128]{1,0:T(8,128)(2,1)S(1)} %get-tuple-element.47), channel_id=1, source_target_pairs={{0,4},{4,8},{8,12},{12,0},{1,5},{5,9},{9,13},{13,1},{2,6},{6,10},{... | collective-permute-start | bytes 227336 | tf_op jit(solution)/shard_map/ppermute | solution.py:64
  37.5 3.1 %collective-permute-done.9 = bf16[296,128]{1,0:T(8,128)(2,1)S(1)} collective-permute-done((bf16[296,128]{1,0:T(8,128)(2,1)S(1)}, bf16[296,128]{1,0:T(8,128)(2,1)S(1)}, u32[]{:S(2)}, u32[]{:S(2)}) %collective-permute-start.9) | collective-permute-done | bytes 75808 | tf_op jit(solution)/shard_map/ppermute | solution.py:64
  40.5 3.9 %collective-permute-done.8 = bf16[296,128]{1,0:T(8,128)(2,1)S(1)} collective-permute-done((bf16[296,128]{1,0:T(8,128)(2,1)S(1)}, bf16[296,128]{1,0:T(8,128)(2,1)S(1)}, u32[]{:S(2)}, u32[]{:S(2)}) %collective-permute-start.8) | collective-permute-done | bytes 75808 | tf_op jit(solution)/shard_map/ppermute | solution.py:64
  44.8 1.3 %collective-permute-start.11 = (bf16[128,16,1]{0,2,1:T(2,128)(2,1)S(1)}, bf16[128,16,1]{0,2,1:T(2,128)(2,1)S(1)}, u32[]{:S(2)}, u32[]{:S(2)}) collective-permute-start(bf16[128,16,1]{0,2,1:T(2,128)(2,1)S(1)} %get-tuple-element.57), channel_id=1, source_target_pairs={{4,0},{8,4},{12,8},{0,12},{5,1},{9,5},{13,9},{1,13},{6,2},{10,6},{... | collective-permute-start | bytes 12296 | tf_op jit(solution)/shard_map/ppermute | solution.py:15
  46.1 0.8 %collective-permute-start.10 = (bf16[128,16,1]{0,2,1:T(2,128)(2,1)S(1)}, bf16[128,16,1]{0,2,1:T(2,128)(2,1)S(1)}, u32[]{:S(2)}, u32[]{:S(2)}) collective-permute-start(bf16[128,16,1]{0,2,1:T(2,128)(2,1)S(1)} %get-tuple-element.56), channel_id=1, source_target_pairs={{0,4},{4,8},{8,12},{12,0},{1,5},{5,9},{9,13},{13,1},{2,6},{6,10},{... | collective-permute-start | bytes 12296 | tf_op jit(solution)/shard_map/ppermute | solution.py:14
  46.9 1.6 %collective-permute-done.11 = bf16[128,16,1]{0,2,1:T(2,128)(2,1)S(1)} collective-permute-done((bf16[128,16,1]{0,2,1:T(2,128)(2,1)S(1)}, bf16[128,16,1]{0,2,1:T(2,128)(2,1)S(1)}, u32[]{:S(2)}, u32[]{:S(2)}) %collective-permute-start.11) | collective-permute-done | bytes 4128 | tf_op jit(solution)/shard_map/ppermute | solution.py:15
  48.5 3.0 %collective-permute-done.10 = bf16[128,16,1]{0,2,1:T(2,128)(2,1)S(1)} collective-permute-done((bf16[128,16,1]{0,2,1:T(2,128)(2,1)S(1)}, bf16[128,16,1]{0,2,1:T(2,128)(2,1)S(1)}, u32[]{:S(2)}, u32[]{:S(2)}) %collective-permute-start.10) | collective-permute-done | bytes 4128 | tf_op jit(solution)/shard_map/ppermute | solution.py:14
  51.7 0.5 collective-permute-start.12
  52.5 0.4 collective-permute-start.16
  52.9 1.6 %collective-permute-start.17 = (bf16[296,128]{1,0:T(8,128)(2,1)S(1)}, bf16[296,128]{1,0:T(8,128)(2,1)S(1)}, u32[]{:S(2)}, u32[]{:S(2)}) collective-permute-start(bf16[296,128]{1,0:T(8,128)(2,1)S(1)} %convert_element_type.72), channel_id=1, source_target_pairs={{0,4},{4,8},{8,12},{12,0},{1,5},{5,9},{9,13},{13,1},{2,6},{6,10},{... | collective-permute-start | bytes 227336 | tf_op jit(solution)/shard_map/ppermute | solution.py:76
  54.8 0.9 %fusion.49 = (bf16[128,16,128]{0,2,1:T(8,128)(2,1)S(1)}, bf16[128,16,128]{0,2,1:T(8,128)(2,1)S(1)}, bf16[128,16,128]{0,2,1:T(8,128)(2,1)S(1)}, bf16[128,16,128]{...) fusion(bf16[128,18,130]{0,2,1:T(8,128)(2,1)S(1)} %maximum_selec, ...), kind=kLoop, calls=%fused_computation.194 | loop fusion | bytes 9437184 | tf_op jit(solution)/shard_map/slice | solution.py:37
  58.7 1.5 %collective-permute-start.14 = (bf16[128,2048]{1,0:T(8,128)(2,1)S(1)}, bf16[128,2048]{1,0:T(8,128)(2,1)S(1)}, u32[]{:S(2)}, u32[]{:S(2)}) collective-permute-start(bf16[128,2048]{1,0:T(8,128)(2,1)S(1)} %fusion.2), channel_id=1, source_target_pairs={{0,2},{2,0},{1,3},{3,1},{4,6},{6,4},{5,7},{7,5},{8,10},{10,8},{9,1... | collective-permute-start | bytes 1572872 | tf_op jit(solution)/shard_map/ppermute | solution.py:173
  63.2 8.9 %collective-permute-done.14 = bf16[128,2048]{1,0:T(8,128)(2,1)S(1)} collective-permute-done((bf16[128,2048]{1,0:T(8,128)(2,1)S(1)}, bf16[128,2048]{1,0:T(8,128)(2,1)S(1)}, u32[]{:S(2)}, u32[]{:S(2)}) %collective-permute-start.14) | collective-permute-done | bytes 524320 | tf_op jit(solution)/shard_map/ppermute | solution.py:173
  72.4 0.9 %copy.26 = bf16[16,8,16,128]{3,2,1,0:T(8,128)(2,1)} copy(bf16[16,8,16,128]{3,1,2,0:T(8,128)(2,1)S(1)} %fusion.21) | data formatting | bytes 1048576
  73.6 0.5 slice.446
  74.5 1.2 %fusion.6 = f32[3,3,128,256]{3,2,1,0:T(8,128)} fusion(s32[]{:T(128)S(6)} %select_n.114, f32[3,3,128,256]{3,2,1,0:T(8,128)S(1)} %reshape.198), kind=kLoop, calls=%fused_computation.63 | loop fusion | flops 294912 | bytes 2359300 | tf_op jit(solution)/shard_map/concatenate | solution.py:162
  (107 shorter events, 17.4 us)
Async XLA Ops:
  0.6 8.2 %copy-start.1 = (bf16[128,16,128]{2,1,0:T(8,128)(2,1)S(1)}, bf16[128,16,128]{2,1,0:T(8,128)(2,1)}, u32[]{:S(2)}) copy-start(bf16[128,16,128]{2,1,0:T(8,128)(2,1)} %param.5) | copy-start | bytes 1572868
  2.2 19.6 %collective-permute-start.5 = (bf16[128,16,128]{0,2,1:T(8,128)(2,1)S(1)}, bf16[128,16,128]{0,2,1:T(8,128)(2,1)S(1)}, u32[]{:S(2)}, u32[]{:S(2)}) collective-permute-start(bf16[128,16,128]{0,2,1:T(8,128)(2,1)S(1)} %copy.12), channel_id=1, source_target_pairs={{0,2},{2,0},{1,3},{3,1},{4,6},{6,4},{5,7},{7,5},{8,10},{10,8},{9,1... | collective-permute-start | bytes 1572872 | tf_op jit(solution)/shard_map/ppermute | solution.py:121
  5.2 5.0 %collective-permute-start.1 = (bf16[128,16,1]{0,2,1:T(2,128)(2,1)S(1)}, bf16[128,16,1]{0,2,1:T(2,128)(2,1)S(1)}, u32[]{:S(2)}, u32[]{:S(2)}) collective-permute-start(bf16[128,16,1]{0,2,1:T(2,128)(2,1)S(1)} %get-tuple-element.59), channel_id=1, source_target_pairs={{4,0},{8,4},{12,8},{0,12},{5,1},{9,5},{13,9},{1,13},{6,2},{10,6},{... | collective-permute-start | bytes 12296 | tf_op jit(solution)/shard_map/ppermute | solution.py:15
  8.8 5.4 %collective-permute-start = (bf16[128,16,1]{0,2,1:T(2,128)(2,1)S(1)}, bf16[128,16,1]{0,2,1:T(2,128)(2,1)S(1)}, u32[]{:S(2)}, u32[]{:S(2)}) collective-permute-start(bf16[128,16,1]{0,2,1:T(2,128)(2,1)S(1)} %get-tuple-element.58), channel_id=1, source_target_pairs={{0,4},{4,8},{8,12},{12,0},{1,5},{5,9},{9,13},{13,1},{2,6},{6,10},{... | collective-permute-start | bytes 12296 | tf_op jit(solution)/shard_map/ppermute | solution.py:14
  14.3 1.3 %collective-permute-start.3 = (bf16[128,1,130]{0,2,1:T(8,128)(2,1)S(1)}, bf16[128,1,130]{0,2,1:T(8,128)(2,1)S(1)}, u32[]{:S(2)}, u32[]{:S(2)}) collective-permute-start(bf16[128,1,130]{0,2,1:T(8,128)(2,1)S(1)} %get-tuple-element.55), channel_id=1, source_target_pairs={{1,0},{0,1},{3,2},{2,3},{5,4},{4,5},{7,6},{6,7},{9,8},{8,9},{11,10... | collective-permute-start | bytes 99848 | tf_op jit(solution)/shard_map/ppermute | solution.py:15
  14.4 1.4 %collective-permute-start.2 = (bf16[128,1,130]{0,2,1:T(8,128)(2,1)S(1)}, bf16[128,1,130]{0,2,1:T(8,128)(2,1)S(1)}, u32[]{:S(2)}, u32[]{:S(2)}) collective-permute-start(bf16[128,1,130]{0,2,1:T(8,128)(2,1)S(1)} %get-tuple-element.54), channel_id=1, source_target_pairs={{0,1},{1,0},{2,3},{3,2},{4,5},{5,4},{6,7},{7,6},{8,9},{9,8},{10,11... | collective-permute-start | bytes 99848 | tf_op jit(solution)/shard_map/ppermute | solution.py:14
  16.1 1.6 %copy-start = (bf16[3,3,128,256]{3,2,1,0:T(8,128)(2,1)S(1)}, bf16[3,3,128,256]{3,2,1,0:T(8,128)(2,1)}, u32[]{:S(2)}) copy-start(bf16[3,3,128,256]{3,2,1,0:T(8,128)(2,1)} %param.6) | copy-start | bytes 1769476
  17.1 4.6 %collective-permute-start.4 = (bf16[128,292]{0,1:T(8,128)(2,1)S(1)}, bf16[128,292]{0,1:T(8,128)(2,1)S(1)}, u32[]{:S(2)}, u32[]{:S(2)}) collective-permute-start(bf16[128,292]{0,1:T(8,128)(2,1)S(1)} %pad_maximum_fusion.3), channel_id=1, source_target_pairs={{0,2},{2,0},{1,3},{3,1},{4,6},{6,4},{5,7},{7,5},{8,10},{10,8},{9,1... | collective-permute-start | bytes 224264 | tf_op jit(solution)/shard_map/ppermute | solution.py:127
  27.6 0.7 copy-start.2
  33.2 2.1 %collective-permute-start.6 = (f32[1184,128]{1,0:T(8,128)S(1)}, f32[1184,128]{1,0:T(8,128)S(1)}, u32[]{:S(2)}, u32[]{:S(2)}) collective-permute-start(f32[1184,128]{1,0:T(8,128)S(1)} %dynamic-slice_bitcast_fusion), channel_id=1, source_target_pairs={{0,1},{1,0},{2,3},{3,2},{4,5},{5,4},{6,7},{7,6},{8,9},{9,8},{10,11... | collective-permute-start | bytes 1818632 | tf_op jit(solution)/shard_map/ppermute | solution.py:64
  35.4 5.2 %collective-permute-start.9 = (bf16[296,128]{1,0:T(8,128)(2,1)S(1)}, bf16[296,128]{1,0:T(8,128)(2,1)S(1)}, u32[]{:S(2)}, u32[]{:S(2)}) collective-permute-start(bf16[296,128]{1,0:T(8,128)(2,1)S(1)} %get-tuple-element.48), channel_id=1, source_target_pairs={{0,12},{4,0},{8,4},{12,8},{1,13},{5,1},{9,5},{13,9},{2,14},{6,2},{... | collective-permute-start | bytes 227336 | tf_op jit(solution)/shard_map/ppermute | solution.py:64
  36.2 8.2 %collective-permute-start.8 = (bf16[296,128]{1,0:T(8,128)(2,1)S(1)}, bf16[296,128]{1,0:T(8,128)(2,1)S(1)}, u32[]{:S(2)}, u32[]{:S(2)}) collective-permute-start(bf16[296,128]{1,0:T(8,128)(2,1)S(1)} %get-tuple-element.49), channel_id=1, source_target_pairs={{0,8},{4,12},{8,0},{12,4},{1,9},{5,13},{9,1},{13,5},{2,10},{6,14},... | collective-permute-start | bytes 227336 | tf_op jit(solution)/shard_map/ppermute | solution.py:64
  36.3 8.2 %collective-permute-start.7 = (bf16[296,128]{1,0:T(8,128)(2,1)S(1)}, bf16[296,128]{1,0:T(8,128)(2,1)S(1)}, u32[]{:S(2)}, u32[]{:S(2)}) collective-permute-start(bf16[296,128]{1,0:T(8,128)(2,1)S(1)} %get-tuple-element.47), channel_id=1, source_target_pairs={{0,4},{4,8},{8,12},{12,0},{1,5},{5,9},{9,13},{13,1},{2,6},{6,10},{... | collective-permute-start | bytes 227336 | tf_op jit(solution)/shard_map/ppermute | solution.py:64
  44.8 3.7 %collective-permute-start.11 = (bf16[128,16,1]{0,2,1:T(2,128)(2,1)S(1)}, bf16[128,16,1]{0,2,1:T(2,128)(2,1)S(1)}, u32[]{:S(2)}, u32[]{:S(2)}) collective-permute-start(bf16[128,16,1]{0,2,1:T(2,128)(2,1)S(1)} %get-tuple-element.57), channel_id=1, source_target_pairs={{4,0},{8,4},{12,8},{0,12},{5,1},{9,5},{13,9},{1,13},{6,2},{10,6},{... | collective-permute-start | bytes 12296 | tf_op jit(solution)/shard_map/ppermute | solution.py:15
  46.1 5.4 %collective-permute-start.10 = (bf16[128,16,1]{0,2,1:T(2,128)(2,1)S(1)}, bf16[128,16,1]{0,2,1:T(2,128)(2,1)S(1)}, u32[]{:S(2)}, u32[]{:S(2)}) collective-permute-start(bf16[128,16,1]{0,2,1:T(2,128)(2,1)S(1)} %get-tuple-element.56), channel_id=1, source_target_pairs={{0,4},{4,8},{8,12},{12,0},{1,5},{5,9},{9,13},{13,1},{2,6},{6,10},{... | collective-permute-start | bytes 12296 | tf_op jit(solution)/shard_map/ppermute | solution.py:14
  51.6 2.9 %collective-permute-start.13 = (bf16[128,1,130]{0,2,1:T(8,128)(2,1)S(1)}, bf16[128,1,130]{0,2,1:T(8,128)(2,1)S(1)}, u32[]{:S(2)}, u32[]{:S(2)}) collective-permute-start(bf16[128,1,130]{0,2,1:T(8,128)(2,1)S(1)} %get-tuple-element.53), channel_id=1, source_target_pairs={{1,0},{0,1},{3,2},{2,3},{5,4},{4,5},{7,6},{6,7},{9,8},{8,9},{11,10... | collective-permute-start | bytes 99848 | tf_op jit(solution)/shard_map/ppermute | solution.py:15
  51.7 2.8 %collective-permute-start.12 = (bf16[128,1,130]{0,2,1:T(8,128)(2,1)S(1)}, bf16[128,1,130]{0,2,1:T(8,128)(2,1)S(1)}, u32[]{:S(2)}, u32[]{:S(2)}) collective-permute-start(bf16[128,1,130]{0,2,1:T(8,128)(2,1)S(1)} %get-tuple-element.52), channel_id=1, source_target_pairs={{0,1},{1,0},{2,3},{3,2},{4,5},{5,4},{6,7},{7,6},{8,9},{9,8},{10,11... | collective-permute-start | bytes 99848 | tf_op jit(solution)/shard_map/ppermute | solution.py:14
  52.4 9.8 %collective-permute-start.15 = (bf16[296,128]{1,0:T(8,128)(2,1)S(1)}, bf16[296,128]{1,0:T(8,128)(2,1)S(1)}, u32[]{:S(2)}, u32[]{:S(2)}) collective-permute-start(bf16[296,128]{1,0:T(8,128)(2,1)S(1)} %convert_element_type.72), channel_id=1, source_target_pairs={{0,12},{4,0},{8,4},{12,8},{1,13},{5,1},{9,5},{13,9},{2,14},{6,2},{... | collective-permute-start | bytes 227336 | tf_op jit(solution)/shard_map/ppermute | solution.py:76
  52.5 9.7 %collective-permute-start.16 = (bf16[296,128]{1,0:T(8,128)(2,1)S(1)}, bf16[296,128]{1,0:T(8,128)(2,1)S(1)}, u32[]{:S(2)}, u32[]{:S(2)}) collective-permute-start(bf16[296,128]{1,0:T(8,128)(2,1)S(1)} %convert_element_type.72), channel_id=1, source_target_pairs={{0,8},{4,12},{8,0},{12,4},{1,9},{5,13},{9,1},{13,5},{2,10},{6,14},... | collective-permute-start | bytes 227336 | tf_op jit(solution)/shard_map/ppermute | solution.py:76
  52.9 9.4 %collective-permute-start.17 = (bf16[296,128]{1,0:T(8,128)(2,1)S(1)}, bf16[296,128]{1,0:T(8,128)(2,1)S(1)}, u32[]{:S(2)}, u32[]{:S(2)}) collective-permute-start(bf16[296,128]{1,0:T(8,128)(2,1)S(1)} %convert_element_type.72), channel_id=1, source_target_pairs={{0,4},{4,8},{8,12},{12,0},{1,5},{5,9},{9,13},{13,1},{2,6},{6,10},{... | collective-permute-start | bytes 227336 | tf_op jit(solution)/shard_map/ppermute | solution.py:76
  58.7 13.4 %collective-permute-start.14 = (bf16[128,2048]{1,0:T(8,128)(2,1)S(1)}, bf16[128,2048]{1,0:T(8,128)(2,1)S(1)}, u32[]{:S(2)}, u32[]{:S(2)}) collective-permute-start(bf16[128,2048]{1,0:T(8,128)(2,1)S(1)} %fusion.2), channel_id=1, source_target_pairs={{0,2},{2,0},{1,3},{3,1},{4,6},{6,4},{5,7},{7,5},{8,10},{10,8},{9,1... | collective-permute-start | bytes 1572872 | tf_op jit(solution)/shard_map/ppermute | solution.py:173
  62.4 10.9 %collective-permute-start.18 = (f32[1184,128]{1,0:T(8,128)S(1)}, f32[1184,128]{1,0:T(8,128)S(1)}, u32[]{:S(2)}, u32[]{:S(2)}) collective-permute-start(f32[1184,128]{1,0:T(8,128)S(1)} %bitcast.330), channel_id=1, source_target_pairs={{0,1},{1,0},{2,3},{3,2},{4,5},{5,4},{6,7},{7,6},{8,9},{9,8},{10,11... | collective-permute-start | bytes 1818632 | tf_op jit(solution)/shard_map/ppermute | solution.py:76

commit v9 on v8

--- a/solution.py
+++ b/solution.py
@@ -132,6 +132,15 @@
         kernel_cols.append(
             lax.dynamic_slice_in_dim(weight, source * own_channels, own_channels, axis=3)
         )
+    kernel_sends = []
+    for shift in range(1, chan_count):
+        target = (chan_index + shift) % chan_count
+        kernel_sends.append(lax.dynamic_slice_in_dim(weight, target * own_channels, own_channels, axis=3))
+    kernel_sends, _ = lax.optimization_barrier((kernel_sends, raw_blocks))
+    kernel_blocks = []
+    for shift in range(1, chan_count):
+        pairs = [(i, (i + shift) % chan_count) for i in range(chan_count)]
+        kernel_blocks.append(lax.ppermute(kernel_sends[shift - 1], "chan", pairs))
     preact = None
     for shift in range(chan_count):
         part = conv_taps(kernel_cols[shift], blocks[shift], row_count, column_count, False)
@@ -155,7 +164,12 @@
     weight_part = jnp.stack(taps)
     flat = jnp.concatenate([weight_part.reshape(-1), bias_part])
     scattered = sum_start(flat, jnp.bfloat16)
-    grad_pre, scattered = lax.optimization_barrier((grad_pre, scattered))
+    grad_field = grad_pre.reshape(own_channels, row_count, column_count)
+    grad_blocks = []
+    for shift in range(1, chan_count):
+        pairs = [(i, (i + shift) % chan_count) for i in range(chan_count)]
+        grad_blocks.append(lax.ppermute(grad_field, "chan", pairs))
+    grad_field, scattered = lax.optimization_barrier((grad_field, scattered))
     flat = sum_finish(scattered, flat.size, jnp.bfloat16)
     weight_local = flat[: weight_part.size].reshape(weight_part.shape)
     bias_grad = flat[weight_part.size :]
@@ -163,18 +177,16 @@
     weight_grad = lax.dynamic_slice_in_dim(
         doubled, (chan_count - chan_index) % chan_count * own_channels, chan_count * own_channels, axis=3
     )
-    grad_field = grad_pre.reshape(own_channels, row_count, column_count)
     grad_pad = mask_rims(padded_2(grad_field, (("lon", 2), ("lat", 1)), 1))
-    received = []
-    for shift in range(1, chan_count):
-        kernel_t = jnp.swapaxes(kernel_cols[shift], 2, 3)
-        part = conv_taps(kernel_t, grad_pad, row_count, column_count, True)
+    grad_border = border_of(grad_pad)
+    input_sum = conv_taps(jnp.swapaxes(kernel_cols[0], 2, 3), grad_pad, row_count, column_count, True)
+    for shift in range(1, chan_count):
         pairs = [(i, (i + shift) % chan_count) for i in range(chan_count)]
-        received.append(lax.ppermute(part.astype(jnp.bfloat16), "chan", pairs))
-    own_part = conv_taps(jnp.swapaxes(kernel_cols[0], 2, 3), grad_pad, row_count, column_count, True)
-    for piece in received:
-        own_part = own_part + piece.astype(jnp.float32)
-    input_grad = own_part.astype(jnp.bfloat16).reshape(own_channels, row_count, column_count)
+        border = lax.ppermute(grad_border, "chan", pairs)
+        block = lax.optimization_barrier(with_border(grad_blocks[shift - 1], border))
+        kernel_t = jnp.swapaxes(kernel_blocks[shift - 1], 2, 3)
+        input_sum = input_sum + conv_taps(kernel_t, block, row_count, column_count, True)
+    input_grad = input_sum.astype(jnp.bfloat16).reshape(own_channels, row_count, column_count)
     return (input_grad, weight_grad, bias_grad)
 
 

time: 75.8 us -> 82.8 us (1.092)
  waiting for transfers between devices: 30 us -> 32.5 us
  starting transfers between devices: 16.3 us -> 18.5 us
  local copies, waits for them, and re-layouts: 7.72 us -> 9.49 us
    ppermute x1 -> x3, waiting for transfers between devices: 8.91 us -> 11.2 us  [the longest x1 11.2 us: local(): border = lax.ppermute(grad_border, 'chan', pairs)]
    ppermute x1 -> x3, starting transfers between devices: 1.54 us -> 3.63 us  [the longest x1 1.54 us: local(): grad_blocks.append(lax.ppermute(grad_field, 'chan', pairs))]
    slice x3 -> x4, local copies, waits for them, and re-layouts: 2.77 us -> 3.7 us  [window_of(): field[:, first_row:first_row + row_count, first_col:first_col + column_co...]
    unnamed x11 -> x14, local copies, waits for them, and re-layouts: 3.4 us -> 3.52 us
  transfers between devices with their start and end apart: 19 -> 21, of which waited for: 11 -> 12; matrix products, arithmetic and copies ran while one was open for 16% -> 18% of each run, Pallas kernels for 0% -> 0%
where the time goes in v9:
time: 82.8 us; the launch traced here: 82.6 us
  waiting for transfers between devices  32.5 us (39%)
  starting transfers between devices  18.5 us (22%)
  matrix products  15.1 us (18%)
  local copies, waits for them, and re-layouts  9.49 us (11%)
  other arithmetic  5.57 us (7%)
  between operations  1.5 us (2%)
    dot_general x36, matrix products, conv_taps(): jnp.dot(kernel[tap_row, tap_col], window, preferred_element_type=jnp.floa...  12.2 us
    ppermute x1, waiting for transfers between devices, local(): border = lax.ppermute(grad_border, 'chan', pairs)  11.2 us
    ppermute x4, waiting for transfers between devices, direct_reduce_scatter(): lax.ppermute(piece.astype(send_dtype), axis, pairs).astype(jnp.float32)  8.87 us
    ppermute x4, waiting for transfers between devices, padded_2(): before = lax.ppermute(last, axis, up)  7.29 us
    ppermute x4, starting transfers between devices, padded_2(): after = lax.ppermute(initial, axis, down)  5.09 us
    slice x4, local copies, waits for them, and re-layouts, window_of(): field[:, first_row:first_row + row_count, first_col:first_col + column_co...  3.7 us
    ppermute x4, waiting for transfers between devices, padded_2(): after = lax.ppermute(initial, axis, down)  3.56 us
    unnamed x14, local copies, waits for them, and re-layouts  3.52 us
  transfers between devices with their start and end apart: 21, of which 12 were waited for; matrix products, arithmetic and copies ran while one was open for 18% of the time, Pallas kernels for 0%

profile of v9, /device:TPU:0, one launch (start us, length us, event | category | flops | bytes accessed | tf_op | source)
XLA Modules:
  0.0 82.6 jit_solution(17211883724398420016)
XLA Ops:
  0.6 1.5 %copy.30 = bf16[128,16,128]{0,2,1:T(8,128)(2,1)S(1)} copy(bf16[128,16,128]{2,1,0:T(8,128)(2,1)} %param.4) | data formatting | bytes 1048576 | tf_op args[0]
  2.2 3.0 %collective-permute-start.5 = (bf16[128,16,128]{0,2,1:T(8,128)(2,1)S(1)}, bf16[128,16,128]{0,2,1:T(8,128)(2,1)S(1)}, u32[]{:S(2)}, u32[]{:S(2)}) collective-permute-start(bf16[128,16,128]{0,2,1:T(8,128)(2,1)S(1)} %copy.30), channel_id=1, source_target_pairs={{0,2},{2,0},{1,3},{3,1},{4,6},{6,4},{5,7},{7,5},{8,10},{10,8},{9,1... | collective-permute-start | bytes 1572872 | tf_op jit(solution)/shard_map/ppermute | solution.py:121
  5.2 3.7 %collective-permute-start.1 = (bf16[128,16,1]{0,2,1:T(2,128)(2,1)S(1)}, bf16[128,16,1]{0,2,1:T(2,128)(2,1)S(1)}, u32[]{:S(2)}, u32[]{:S(2)}) collective-permute-start(bf16[128,16,1]{0,2,1:T(2,128)(2,1)S(1)} %get-tuple-element.74), channel_id=1, source_target_pairs={{4,0},{8,4},{12,8},{0,12},{5,1},{9,5},{13,9},{1,13},{6,2},{10,6},{... | collective-permute-start | bytes 12296 | tf_op jit(solution)/shard_map/ppermute | solution.py:15
  9.0 1.2 %collective-permute-done.1 = bf16[128,16,1]{0,2,1:T(2,128)(2,1)S(1)} collective-permute-done((bf16[128,16,1]{0,2,1:T(2,128)(2,1)S(1)}, bf16[128,16,1]{0,2,1:T(2,128)(2,1)S(1)}, u32[]{:S(2)}, u32[]{:S(2)}) %collective-permute-start.1) | collective-permute-done | bytes 4128 | tf_op jit(solution)/shard_map/ppermute | solution.py:15
  10.2 4.1 %collective-permute-done = bf16[128,16,1]{0,2,1:T(2,128)(2,1)S(1)} collective-permute-done((bf16[128,16,1]{0,2,1:T(2,128)(2,1)S(1)}, bf16[128,16,1]{0,2,1:T(2,128)(2,1)S(1)}, u32[]{:S(2)}, u32[]{:S(2)}) %collective-permute-start) | collective-permute-done | bytes 4128 | tf_op jit(solution)/shard_map/ppermute | solution.py:14
  14.9 0.7 collective-permute-done.3
  16.1 0.9 %fusion.69 = (bf16[128,16,128]{0,2,1:T(8,128)(2,1)S(1)}, bf16[128,16,128]{0,2,1:T(8,128)(2,1)S(1)}, bf16[128,16,128]{0,2,1:T(8,128)(2,1)S(1)}, bf16[128,16,128]{...) fusion(bf16[128,18,130]{0,2,1:T(8,128)(2,1)S(1)} %maximum_selec, ...), kind=kLoop, calls=%fused_computation.216 | loop fusion | bytes 9437184 | tf_op jit(solution)/shard_map/slice | solution.py:37
  17.1 0.6 collective-permute-start.4
  20.5 1.3 %collective-permute-done.4 = bf16[128,292]{0,1:T(8,128)(2,1)S(1)} collective-permute-done((bf16[128,292]{0,1:T(8,128)(2,1)S(1)}, bf16[128,292]{0,1:T(8,128)(2,1)S(1)}, u32[]{:S(2)}, u32[]{:S(2)}) %collective-permute-start.4) | collective-permute-done | bytes 74784 | tf_op jit(solution)/shard_map/ppermute | solution.py:127
  22.0 0.9 %fusion.67 = (bf16[128,16,128]{0,2,1:T(8,128)(2,1)S(1)}, bf16[128,16,128]{0,2,1:T(8,128)(2,1)S(1)}, bf16[128,16,128]{0,2,1:T(8,128)(2,1)S(1)}, bf16[128,16,128]{...) fusion(bf16[128,18,130]{0,2,1:T(8,128)(2,1)S(1)} %pad_maximum_f, ...), kind=kLoop, calls=%fused_computation.214 | loop fusion | bytes 9437184 | tf_op jit(solution)/shard_map/slice | solution.py:37
  22.9 2.5 %fusion.23 = (bf16[256,16,128]{0,2,1:T(8,128)(2,1)S(1)}, bf16[256,16,128]{0,2,1:T(8,128)(2,1)S(1)}, bf16[256,16,128]{0,2,1:T(8,128)(2,1)S(1)}, bf16[256,16,128]{...) fusion(bf16[128,18,130]{0,2,1:T(8,128)(2,1)S(1)} %maximum_selec, ...), kind=kLoop, calls=%fused_computation.83 | loop fusion | flops 18874368 | bytes 10635264 | tf_op jit(solution)/shard_map/concatenate | solution.py:152
  28.3 1.0 %convert_reduce_fusion = (f32[128]{0:T(128)S(1)}, bf16[128,2048]{1,0:T(8,128)(2,1)S(1)}) fusion(f32[128]{0:T(128)S(1)} %copy-done.2, f32[128,2048]{1,0:T(8,128)S(1)} %convolution_add_fusion.17, f32[128,2048]{1,0:T(8,128)S(1)} %convolution_add_fusion.10, bf16[128,2048]{0,1:T(8,128)(2,1)S(1)} %bitcast.374, bf16[3,3,128,256]{3,2,1,0:T(8,128)(2,1)S(1)} %copy-done, ...), kind=kOutput, calls=%fused_computation.91 | convolution fusion | flops 71040896 | bytes 4228104 | tf_op jit(solution)/shard_map/dot_general | solution.py:50
  32.4 0.6 copy.48
  33.3 2.0 %collective-permute-done.6 = f32[1184,128]{1,0:T(8,128)S(1)} collective-permute-done((f32[1184,128]{1,0:T(8,128)S(1)}, f32[1184,128]{1,0:T(8,128)S(1)}, u32[]{:S(2)}, u32[]{:S(2)}) %collective-permute-start.6) | collective-permute-done | bytes 606240 | tf_op jit(solution)/shard_map/ppermute | solution.py:64
  35.4 0.9 %collective-permute-start.9 = (bf16[296,128]{1,0:T(8,128)(2,1)S(1)}, bf16[296,128]{1,0:T(8,128)(2,1)S(1)}, u32[]{:S(2)}, u32[]{:S(2)}) collective-permute-start(bf16[296,128]{1,0:T(8,128)(2,1)S(1)} %get-tuple-element.63), channel_id=1, source_target_pairs={{0,12},{4,0},{8,4},{12,8},{1,13},{5,1},{9,5},{13,9},{2,14},{6,2},{... | collective-permute-start | bytes 227336 | tf_op jit(solution)/shard_map/ppermute | solution.py:64
  36.3 1.2 %collective-permute-start.7 = (bf16[296,128]{1,0:T(8,128)(2,1)S(1)}, bf16[296,128]{1,0:T(8,128)(2,1)S(1)}, u32[]{:S(2)}, u32[]{:S(2)}) collective-permute-start(bf16[296,128]{1,0:T(8,128)(2,1)S(1)} %get-tuple-element.62), channel_id=1, source_target_pairs={{0,4},{4,8},{8,12},{12,0},{1,5},{5,9},{9,13},{13,1},{2,6},{6,10},{... | collective-permute-start | bytes 227336 | tf_op jit(solution)/shard_map/ppermute | solution.py:64
  37.6 3.0 %collective-permute-done.9 = bf16[296,128]{1,0:T(8,128)(2,1)S(1)} collective-permute-done((bf16[296,128]{1,0:T(8,128)(2,1)S(1)}, bf16[296,128]{1,0:T(8,128)(2,1)S(1)}, u32[]{:S(2)}, u32[]{:S(2)}) %collective-permute-start.9) | collective-permute-done | bytes 75808 | tf_op jit(solution)/shard_map/ppermute | solution.py:64
  40.5 3.9 %collective-permute-done.8 = bf16[296,128]{1,0:T(8,128)(2,1)S(1)} collective-permute-done((bf16[296,128]{1,0:T(8,128)(2,1)S(1)}, bf16[296,128]{1,0:T(8,128)(2,1)S(1)}, u32[]{:S(2)}, u32[]{:S(2)}) %collective-permute-start.8) | collective-permute-done | bytes 75808 | tf_op jit(solution)/shard_map/ppermute | solution.py:64
  45.0 1.3 %collective-permute-start.11 = (bf16[128,16,1]{0,2,1:T(2,128)(2,1)S(1)}, bf16[128,16,1]{0,2,1:T(2,128)(2,1)S(1)}, u32[]{:S(2)}, u32[]{:S(2)}) collective-permute-start(bf16[128,16,1]{0,2,1:T(2,128)(2,1)S(1)} %get-tuple-element.72), channel_id=1, source_target_pairs={{4,0},{8,4},{12,8},{0,12},{5,1},{9,5},{13,9},{1,13},{6,2},{10,6},{... | collective-permute-start | bytes 12296 | tf_op jit(solution)/shard_map/ppermute | solution.py:15
  46.3 0.8 collective-permute-start.10
  47.1 1.6 %collective-permute-done.11 = bf16[128,16,1]{0,2,1:T(2,128)(2,1)S(1)} collective-permute-done((bf16[128,16,1]{0,2,1:T(2,128)(2,1)S(1)}, bf16[128,16,1]{0,2,1:T(2,128)(2,1)S(1)}, u32[]{:S(2)}, u32[]{:S(2)}) %collective-permute-start.11) | collective-permute-done | bytes 4128 | tf_op jit(solution)/shard_map/ppermute | solution.py:15
  48.7 3.0 %collective-permute-done.10 = bf16[128,16,1]{0,2,1:T(2,128)(2,1)S(1)} collective-permute-done((bf16[128,16,1]{0,2,1:T(2,128)(2,1)S(1)}, bf16[128,16,1]{0,2,1:T(2,128)(2,1)S(1)}, u32[]{:S(2)}, u32[]{:S(2)}) %collective-permute-start.10) | collective-permute-done | bytes 4128 | tf_op jit(solution)/shard_map/ppermute | solution.py:14
  53.0 1.5 %collective-permute-start.16 = (bf16[128,16,128]{0,2,1:T(8,128)(2,1)S(1)}, bf16[128,16,128]{0,2,1:T(8,128)(2,1)S(1)}, u32[]{:S(2)}, u32[]{:S(2)}) collective-permute-start(bf16[128,16,128]{0,2,1:T(8,128)(2,1)S(1)} %copy.39), channel_id=1, source_target_pairs={{0,2},{2,0},{1,3},{3,1},{4,6},{6,4},{5,7},{7,5},{8,10},{10,8},{9,1... | collective-permute-start | bytes 1572872 | tf_op jit(solution)/shard_map/ppermute | solution.py:171
  54.5 0.5 collective-permute-start.14
  55.6 1.6 %collective-permute-start.19 = (bf16[296,128]{1,0:T(8,128)(2,1)S(1)}, bf16[296,128]{1,0:T(8,128)(2,1)S(1)}, u32[]{:S(2)}, u32[]{:S(2)}) collective-permute-start(bf16[296,128]{1,0:T(8,128)(2,1)S(1)} %convert_element_type.64), channel_id=1, source_target_pairs={{0,4},{4,8},{8,12},{12,0},{1,5},{5,9},{9,13},{13,1},{2,6},{6,10},{... | collective-permute-start | bytes 227336 | tf_op jit(solution)/shard_map/ppermute | solution.py:76
  57.6 0.9 %fusion.66 = (bf16[128,16,128]{0,2,1:T(8,128)(2,1)S(1)}, bf16[128,16,128]{0,2,1:T(8,128)(2,1)S(1)}, bf16[128,16,128]{0,2,1:T(8,128)(2,1)S(1)}, bf16[128,16,128]{...) fusion(bf16[128,18,130]{0,2,1:T(8,128)(2,1)S(1)} %maximum_selec, ...), kind=kLoop, calls=%fused_computation.213 | loop fusion | bytes 9437184 | tf_op jit(solution)/shard_map/slice | solution.py:37
  61.6 1.5 %collective-permute-start.15 = (bf16[128,292]{0,1:T(8,128)(2,1)S(1)}, bf16[128,292]{0,1:T(8,128)(2,1)S(1)}, u32[]{:S(2)}, u32[]{:S(2)}) collective-permute-start(bf16[128,292]{0,1:T(8,128)(2,1)S(1)} %pad_maximum_fusion.5), channel_id=1, source_target_pairs={{0,2},{2,0},{1,3},{3,1},{4,6},{6,4},{5,7},{7,5},{8,10},{10,8},{9,1... | collective-permute-start | bytes 224264 | tf_op jit(solution)/shard_map/ppermute | solution.py:185
  63.7 11.2 %collective-permute-done.15 = bf16[128,292]{0,1:T(8,128)(2,1)S(1)} collective-permute-done((bf16[128,292]{0,1:T(8,128)(2,1)S(1)}, bf16[128,292]{0,1:T(8,128)(2,1)S(1)}, u32[]{:S(2)}, u32[]{:S(2)}) %collective-permute-start.15) | collective-permute-done | bytes 74784 | tf_op jit(solution)/shard_map/ppermute | solution.py:185
  75.2 0.9 %fusion.64 = (bf16[128,16,128]{0,2,1:T(8,128)(2,1)S(1)}, bf16[128,16,128]{0,2,1:T(8,128)(2,1)S(1)}, bf16[128,16,128]{0,2,1:T(8,128)(2,1)S(1)}, bf16[128,16,128]{...) fusion(bf16[128,18,130]{0,2,1:T(8,128)(2,1)S(1)} %pad_maximum_f, ...), kind=kLoop, calls=%fused_computation.211 | loop fusion | bytes 9437184 | tf_op jit(solution)/shard_map/slice | solution.py:37
  78.7 0.7 fusion.11
  79.4 0.9 %copy.49 = bf16[16,8,16,128]{3,2,1,0:T(8,128)(2,1)} copy(bf16[16,8,16,128]{3,1,2,0:T(8,128)(2,1)S(1)} %fusion.11) | data formatting | bytes 1048576
  81.5 1.2 %fusion.15 = f32[3,3,128,256]{3,2,1,0:T(8,128)} fusion(s32[]{:T(128)S(6)} %select_n.117, f32[3,3,128,256]{3,2,1,0:T(8,128)S(1)} %reshape.225), kind=kLoop, calls=%fused_computation.65 | loop fusion | flops 294912 | bytes 2359300 | tf_op jit(solution)/shard_map/concatenate | solution.py:176
  (124 shorter events, 20.3 us)
Async XLA Ops:
  0.6 8.2 %copy-start.1 = (bf16[128,16,128]{2,1,0:T(8,128)(2,1)S(1)}, bf16[128,16,128]{2,1,0:T(8,128)(2,1)}, u32[]{:S(2)}) copy-start(bf16[128,16,128]{2,1,0:T(8,128)(2,1)} %param.5) | copy-start | bytes 1572868
  2.2 19.6 %collective-permute-start.5 = (bf16[128,16,128]{0,2,1:T(8,128)(2,1)S(1)}, bf16[128,16,128]{0,2,1:T(8,128)(2,1)S(1)}, u32[]{:S(2)}, u32[]{:S(2)}) collective-permute-start(bf16[128,16,128]{0,2,1:T(8,128)(2,1)S(1)} %copy.30), channel_id=1, source_target_pairs={{0,2},{2,0},{1,3},{3,1},{4,6},{6,4},{5,7},{7,5},{8,10},{10,8},{9,1... | collective-permute-start | bytes 1572872 | tf_op jit(solution)/shard_map/ppermute | solution.py:121
  5.2 5.0 %collective-permute-start.1 = (bf16[128,16,1]{0,2,1:T(2,128)(2,1)S(1)}, bf16[128,16,1]{0,2,1:T(2,128)(2,1)S(1)}, u32[]{:S(2)}, u32[]{:S(2)}) collective-permute-start(bf16[128,16,1]{0,2,1:T(2,128)(2,1)S(1)} %get-tuple-element.74), channel_id=1, source_target_pairs={{4,0},{8,4},{12,8},{0,12},{5,1},{9,5},{13,9},{1,13},{6,2},{10,6},{... | collective-permute-start | bytes 12296 | tf_op jit(solution)/shard_map/ppermute | solution.py:15
  8.8 5.4 %collective-permute-start = (bf16[128,16,1]{0,2,1:T(2,128)(2,1)S(1)}, bf16[128,16,1]{0,2,1:T(2,128)(2,1)S(1)}, u32[]{:S(2)}, u32[]{:S(2)}) collective-permute-start(bf16[128,16,1]{0,2,1:T(2,128)(2,1)S(1)} %get-tuple-element.73), channel_id=1, source_target_pairs={{0,4},{4,8},{8,12},{12,0},{1,5},{5,9},{9,13},{13,1},{2,6},{6,10},{... | collective-permute-start | bytes 12296 | tf_op jit(solution)/shard_map/ppermute | solution.py:14
  14.3 1.3 %collective-permute-start.3 = (bf16[128,1,130]{0,2,1:T(8,128)(2,1)S(1)}, bf16[128,1,130]{0,2,1:T(8,128)(2,1)S(1)}, u32[]{:S(2)}, u32[]{:S(2)}) collective-permute-start(bf16[128,1,130]{0,2,1:T(8,128)(2,1)S(1)} %get-tuple-element.70), channel_id=1, source_target_pairs={{1,0},{0,1},{3,2},{2,3},{5,4},{4,5},{7,6},{6,7},{9,8},{8,9},{11,10... | collective-permute-start | bytes 99848 | tf_op jit(solution)/shard_map/ppermute | solution.py:15
  14.4 1.4 %collective-permute-start.2 = (bf16[128,1,130]{0,2,1:T(8,128)(2,1)S(1)}, bf16[128,1,130]{0,2,1:T(8,128)(2,1)S(1)}, u32[]{:S(2)}, u32[]{:S(2)}) collective-permute-start(bf16[128,1,130]{0,2,1:T(8,128)(2,1)S(1)} %get-tuple-element.69), channel_id=1, source_target_pairs={{0,1},{1,0},{2,3},{3,2},{4,5},{5,4},{6,7},{7,6},{8,9},{9,8},{10,11... | collective-permute-start | bytes 99848 | tf_op jit(solution)/shard_map/ppermute | solution.py:14
  16.1 1.6 %copy-start = (bf16[3,3,128,256]{3,2,1,0:T(8,128)(2,1)S(1)}, bf16[3,3,128,256]{3,2,1,0:T(8,128)(2,1)}, u32[]{:S(2)}) copy-start(bf16[3,3,128,256]{3,2,1,0:T(8,128)(2,1)} %param.6) | copy-start | bytes 1769476
  17.1 4.6 %collective-permute-start.4 = (bf16[128,292]{0,1:T(8,128)(2,1)S(1)}, bf16[128,292]{0,1:T(8,128)(2,1)S(1)}, u32[]{:S(2)}, u32[]{:S(2)}) collective-permute-start(bf16[128,292]{0,1:T(8,128)(2,1)S(1)} %pad_maximum_fusion.4), channel_id=1, source_target_pairs={{0,2},{2,0},{1,3},{3,1},{4,6},{6,4},{5,7},{7,5},{8,10},{10,8},{9,1... | collective-permute-start | bytes 224264 | tf_op jit(solution)/shard_map/ppermute | solution.py:127
  27.6 0.7 copy-start.2
  33.2 2.1 %collective-permute-start.6 = (f32[1184,128]{1,0:T(8,128)S(1)}, f32[1184,128]{1,0:T(8,128)S(1)}, u32[]{:S(2)}, u32[]{:S(2)}) collective-permute-start(f32[1184,128]{1,0:T(8,128)S(1)} %dynamic-slice_bitcast_fusion), channel_id=1, source_target_pairs={{0,1},{1,0},{2,3},{3,2},{4,5},{5,4},{6,7},{7,6},{8,9},{9,8},{10,11... | collective-permute-start | bytes 1818632 | tf_op jit(solution)/shard_map/ppermute | solution.py:64
  35.4 5.2 %collective-permute-start.9 = (bf16[296,128]{1,0:T(8,128)(2,1)S(1)}, bf16[296,128]{1,0:T(8,128)(2,1)S(1)}, u32[]{:S(2)}, u32[]{:S(2)}) collective-permute-start(bf16[296,128]{1,0:T(8,128)(2,1)S(1)} %get-tuple-element.63), channel_id=1, source_target_pairs={{0,12},{4,0},{8,4},{12,8},{1,13},{5,1},{9,5},{13,9},{2,14},{6,2},{... | collective-permute-start | bytes 227336 | tf_op jit(solution)/shard_map/ppermute | solution.py:64
  36.2 8.2 %collective-permute-start.8 = (bf16[296,128]{1,0:T(8,128)(2,1)S(1)}, bf16[296,128]{1,0:T(8,128)(2,1)S(1)}, u32[]{:S(2)}, u32[]{:S(2)}) collective-permute-start(bf16[296,128]{1,0:T(8,128)(2,1)S(1)} %get-tuple-element.64), channel_id=1, source_target_pairs={{0,8},{4,12},{8,0},{12,4},{1,9},{5,13},{9,1},{13,5},{2,10},{6,14},... | collective-permute-start | bytes 227336 | tf_op jit(solution)/shard_map/ppermute | solution.py:64
  36.3 8.2 %collective-permute-start.7 = (bf16[296,128]{1,0:T(8,128)(2,1)S(1)}, bf16[296,128]{1,0:T(8,128)(2,1)S(1)}, u32[]{:S(2)}, u32[]{:S(2)}) collective-permute-start(bf16[296,128]{1,0:T(8,128)(2,1)S(1)} %get-tuple-element.62), channel_id=1, source_target_pairs={{0,4},{4,8},{8,12},{12,0},{1,5},{5,9},{9,13},{13,1},{2,6},{6,10},{... | collective-permute-start | bytes 227336 | tf_op jit(solution)/shard_map/ppermute | solution.py:64
  45.0 3.7 %collective-permute-start.11 = (bf16[128,16,1]{0,2,1:T(2,128)(2,1)S(1)}, bf16[128,16,1]{0,2,1:T(2,128)(2,1)S(1)}, u32[]{:S(2)}, u32[]{:S(2)}) collective-permute-start(bf16[128,16,1]{0,2,1:T(2,128)(2,1)S(1)} %get-tuple-element.72), channel_id=1, source_target_pairs={{4,0},{8,4},{12,8},{0,12},{5,1},{9,5},{13,9},{1,13},{6,2},{10,6},{... | collective-permute-start | bytes 12296 | tf_op jit(solution)/shard_map/ppermute | solution.py:15
  46.3 5.4 %collective-permute-start.10 = (bf16[128,16,1]{0,2,1:T(2,128)(2,1)S(1)}, bf16[128,16,1]{0,2,1:T(2,128)(2,1)S(1)}, u32[]{:S(2)}, u32[]{:S(2)}) collective-permute-start(bf16[128,16,1]{0,2,1:T(2,128)(2,1)S(1)} %get-tuple-element.71), channel_id=1, source_target_pairs={{0,4},{4,8},{8,12},{12,0},{1,5},{5,9},{9,13},{13,1},{2,6},{6,10},{... | collective-permute-start | bytes 12296 | tf_op jit(solution)/shard_map/ppermute | solution.py:14
  51.8 3.5 %collective-permute-start.13 = (bf16[128,1,130]{0,2,1:T(8,128)(2,1)S(1)}, bf16[128,1,130]{0,2,1:T(8,128)(2,1)S(1)}, u32[]{:S(2)}, u32[]{:S(2)}) collective-permute-start(bf16[128,1,130]{0,2,1:T(8,128)(2,1)S(1)} %get-tuple-element.68), channel_id=1, source_target_pairs={{1,0},{0,1},{3,2},{2,3},{5,4},{4,5},{7,6},{6,7},{9,8},{8,9},{11,10... | collective-permute-start | bytes 99848 | tf_op jit(solution)/shard_map/ppermute | solution.py:15
  51.9 3.8 %collective-permute-start.12 = (bf16[128,1,130]{0,2,1:T(8,128)(2,1)S(1)}, bf16[128,1,130]{0,2,1:T(8,128)(2,1)S(1)}, u32[]{:S(2)}, u32[]{:S(2)}) collective-permute-start(bf16[128,1,130]{0,2,1:T(8,128)(2,1)S(1)} %get-tuple-element.67), channel_id=1, source_target_pairs={{0,1},{1,0},{2,3},{3,2},{4,5},{5,4},{6,7},{7,6},{8,9},{9,8},{10,11... | collective-permute-start | bytes 99848 | tf_op jit(solution)/shard_map/ppermute | solution.py:14
  53.0 22.0 %collective-permute-start.16 = (bf16[128,16,128]{0,2,1:T(8,128)(2,1)S(1)}, bf16[128,16,128]{0,2,1:T(8,128)(2,1)S(1)}, u32[]{:S(2)}, u32[]{:S(2)}) collective-permute-start(bf16[128,16,128]{0,2,1:T(8,128)(2,1)S(1)} %copy.39), channel_id=1, source_target_pairs={{0,2},{2,0},{1,3},{3,1},{4,6},{6,4},{5,7},{7,5},{8,10},{10,8},{9,1... | collective-permute-start | bytes 1572872 | tf_op jit(solution)/shard_map/ppermute | solution.py:171
  54.5 21.6 %collective-permute-start.14 = (bf16[3,3,128,128]{3,2,1,0:T(8,128)(2,1)S(1)}, bf16[3,3,128,128]{3,2,1,0:T(8,128)(2,1)S(1)}, u32[]{:S(2)}, u32[]{:S(2)}) collective-permute-start(bf16[3,3,128,128]{3,2,1,0:T(8,128)(2,1)S(1)} %get-tuple-element.7), channel_id=1, source_target_pairs={{0,2},{2,0},{1,3},{3,1},{4,6},{6,4},{5,7},{7,5},{8,10},{10,8},{9,1... | collective-permute-start | bytes 884744 | tf_op jit(solution)/shard_map/ppermute | solution.py:143
  55.1 6.5 %collective-permute-start.17 = (bf16[296,128]{1,0:T(8,128)(2,1)S(1)}, bf16[296,128]{1,0:T(8,128)(2,1)S(1)}, u32[]{:S(2)}, u32[]{:S(2)}) collective-permute-start(bf16[296,128]{1,0:T(8,128)(2,1)S(1)} %convert_element_type.64), channel_id=1, source_target_pairs={{0,12},{4,0},{8,4},{12,8},{1,13},{5,1},{9,5},{13,9},{2,14},{6,2},{... | collective-permute-start | bytes 227336 | tf_op jit(solution)/shard_map/ppermute | solution.py:76
  55.3 8.2 %collective-permute-start.18 = (bf16[296,128]{1,0:T(8,128)(2,1)S(1)}, bf16[296,128]{1,0:T(8,128)(2,1)S(1)}, u32[]{:S(2)}, u32[]{:S(2)}) collective-permute-start(bf16[296,128]{1,0:T(8,128)(2,1)S(1)} %convert_element_type.64), channel_id=1, source_target_pairs={{0,8},{4,12},{8,0},{12,4},{1,9},{5,13},{9,1},{13,5},{2,10},{6,14},... | collective-permute-start | bytes 227336 | tf_op jit(solution)/shard_map/ppermute | solution.py:76
  55.6 7.8 %collective-permute-start.19 = (bf16[296,128]{1,0:T(8,128)(2,1)S(1)}, bf16[296,128]{1,0:T(8,128)(2,1)S(1)}, u32[]{:S(2)}, u32[]{:S(2)}) collective-permute-start(bf16[296,128]{1,0:T(8,128)(2,1)S(1)} %convert_element_type.64), channel_id=1, source_target_pairs={{0,4},{4,8},{8,12},{12,0},{1,5},{5,9},{9,13},{13,1},{2,6},{6,10},{... | collective-permute-start | bytes 227336 | tf_op jit(solution)/shard_map/ppermute | solution.py:76
  61.6 13.4 %collective-permute-start.15 = (bf16[128,292]{0,1:T(8,128)(2,1)S(1)}, bf16[128,292]{0,1:T(8,128)(2,1)S(1)}, u32[]{:S(2)}, u32[]{:S(2)}) collective-permute-start(bf16[128,292]{0,1:T(8,128)(2,1)S(1)} %pad_maximum_fusion.5), channel_id=1, source_target_pairs={{0,2},{2,0},{1,3},{3,1},{4,6},{6,4},{5,7},{7,5},{8,10},{10,8},{9,1... | collective-permute-start | bytes 224264 | tf_op jit(solution)/shard_map/ppermute | solution.py:185
  63.6 16.6 %collective-permute-start.20 = (f32[1184,128]{1,0:T(8,128)S(1)}, f32[1184,128]{1,0:T(8,128)S(1)}, u32[]{:S(2)}, u32[]{:S(2)}) collective-permute-start(f32[1184,128]{1,0:T(8,128)S(1)} %bitcast.337), channel_id=1, source_target_pairs={{0,1},{1,0},{2,3},{3,2},{4,5},{5,4},{6,7},{7,6},{8,9},{9,8},{10,11... | collective-permute-start | bytes 1818632 | tf_op jit(solution)/shard_map/ppermute | solution.py:76

commit v10 on v9

--- a/solution.py
+++ b/solution.py
@@ -148,6 +148,7 @@
     preact = preact + bias_vector[:, None]
     upstream = cotangent.reshape(own_channels, -1).astype(jnp.float32)
     grad_pre = (upstream * gelu_slope(preact)).astype(jnp.bfloat16)
+    grad_pre, kernel_blocks = lax.optimization_barrier((grad_pre, kernel_blocks))
     bias_part = jnp.sum(grad_pre.astype(jnp.float32), axis=1)
     input_local = jnp.concatenate(blocks, axis=0)
     taps = []
@@ -169,7 +170,7 @@
     for shift in range(1, chan_count):
         pairs = [(i, (i + shift) % chan_count) for i in range(chan_count)]
         grad_blocks.append(lax.ppermute(grad_field, "chan", pairs))
-    grad_field, scattered = lax.optimization_barrier((grad_field, scattered))
+    grad_field, scattered, grad_blocks = lax.optimization_barrier((grad_field, scattered, grad_blocks))
     flat = sum_finish(scattered, flat.size, jnp.bfloat16)
     weight_local = flat[: weight_part.size].reshape(weight_part.shape)
     bias_grad = flat[weight_part.size :]

time: 82.8 us -> 79.1 us (0.955)
  waiting for transfers between devices: 32.5 us -> 18.4 us
  starting transfers between devices: 18.5 us -> 25.8 us
  other arithmetic: 5.57 us -> 8.89 us
    ppermute x1, waiting for transfers between devices: 11.2 us -> 0.01 us  [local(): border = lax.ppermute(grad_border, 'chan', pairs)]
    ppermute x4, waiting for transfers between devices: 7.29 us -> 3.75 us  [padded_2(): before = lax.ppermute(last, axis, up)]
    ppermute x4, waiting for transfers between devices: 3.56 us -> 0.17 us  [padded_2(): after = lax.ppermute(initial, axis, down)]
    ppermute x1, waiting for transfers between devices: 0.01 us -> 3.37 us  [local(): kernel_blocks.append(lax.ppermute(kernel_sends[shift - 1], 'chan', pairs))]
    ppermute x4, starting transfers between devices: 2.15 us -> 4.75 us  [direct_reduce_scatter(): lax.ppermute(piece.astype(send_dtype), axis, pairs).astype(jnp.float32)]
    ppermute x4, starting transfers between devices: 2.21 us -> 4.56 us  [direct_all_gather(): pieces.append(lax.ppermute(sent, axis, pairs).astype(jnp.float32))]
    concatenate x2, other arithmetic: 0.35 us -> 2.44 us  [with_border(): jnp.concatenate([top[:, None, :], middle, bottom[:, None, :]], axis=1)]
    ppermute x1, starting transfers between devices: 0.55 us -> 1.81 us  [local(): kernel_blocks.append(lax.ppermute(kernel_sends[shift - 1], 'chan', pairs))]
  transfers between devices with their start and end apart: 21 -> 21, of which waited for: 12 -> 11; matrix products, arithmetic and copies ran while one was open for 18% -> 25% of each run, Pallas kernels for 0% -> 0%
where the time goes in v10:
time: 79.1 us; the launch traced here: 78.7 us
  starting transfers between devices  25.8 us (33%)
  waiting for transfers between devices  18.4 us (23%)
  matrix products  14.6 us (18%)
  local copies, waits for them, and re-layouts  9.52 us (12%)
  other arithmetic  8.89 us (11%)
  between operations  1.5 us (2%)
    dot_general x36, matrix products, conv_taps(): jnp.dot(kernel[tap_row, tap_col], window, preferred_element_type=jnp.floa...  11.8 us
    ppermute x4, waiting for transfers between devices, direct_reduce_scatter(): lax.ppermute(piece.astype(send_dtype), axis, pairs).astype(jnp.float32)  7.73 us
    ppermute x4, starting transfers between devices, padded_2(): after = lax.ppermute(initial, axis, down)  6.08 us
    ppermute x4, starting transfers between devices, direct_reduce_scatter(): lax.ppermute(piece.astype(send_dtype), axis, pairs).astype(jnp.float32)  4.75 us
    ppermute x4, starting transfers between devices, direct_all_gather(): pieces.append(lax.ppermute(sent, axis, pairs).astype(jnp.float32))  4.56 us
    ppermute x4, waiting for transfers between devices, padded_2(): before = lax.ppermute(last, axis, up)  3.75 us
    slice x4, local copies, waits for them, and re-layouts, window_of(): field[:, first_row:first_row + row_count, first_col:first_col + column_co...  3.69 us
    unnamed x18, local copies, waits for them, and re-layouts  3.55 us
  transfers between devices with their start and end apart: 21, of which 11 were waited for; matrix products, arithmetic and copies ran while one was open for 25% of the time, Pallas kernels for 0%

profile of v10, /device:TPU:0, one launch (start us, length us, event | category | flops | bytes accessed | tf_op | source)
XLA Modules:
  0.0 78.7 jit_solution(13069536878493697930)
XLA Ops:
  0.6 1.5 %copy.30 = bf16[128,16,128]{0,2,1:T(8,128)(2,1)S(1)} copy(bf16[128,16,128]{2,1,0:T(8,128)(2,1)} %param.4) | data formatting | bytes 1048576 | tf_op args[0]
  2.2 3.0 %collective-permute-start.5 = (bf16[128,16,128]{0,2,1:T(8,128)(2,1)S(1)}, bf16[128,16,128]{0,2,1:T(8,128)(2,1)}, u32[]{:S(2)}, u32[]{:S(2)}) collective-permute-start(bf16[128,16,128]{0,2,1:T(8,128)(2,1)S(1)} %copy.30), channel_id=1, source_target_pairs={{0,2},{2,0},{1,3},{3,1},{4,6},{6,4},{5,7},{7,5},{8,10},{10,8},{9,1... | collective-permute-start | bytes 1572872 | tf_op jit(solution)/shard_map/ppermute | solution.py:121
  5.2 1.6 %collective-permute-start = (bf16[128,16,1]{0,2,1:T(2,128)(2,1)S(1)}, bf16[128,16,1]{0,2,1:T(2,128)(2,1)S(1)}, u32[]{:S(2)}, u32[]{:S(2)}) collective-permute-start(bf16[128,16,1]{0,2,1:T(2,128)(2,1)S(1)} %get-tuple-element.79), channel_id=1, source_target_pairs={{0,4},{4,8},{8,12},{12,0},{1,5},{5,9},{9,13},{13,1},{2,6},{6,10},{... | collective-permute-start | bytes 12296 | tf_op jit(solution)/shard_map/ppermute | solution.py:14
  6.8 2.2 %collective-permute-start.1 = (bf16[128,16,1]{0,2,1:T(2,128)(2,1)S(1)}, bf16[128,16,1]{0,2,1:T(2,128)(2,1)S(1)}, u32[]{:S(2)}, u32[]{:S(2)}) collective-permute-start(bf16[128,16,1]{0,2,1:T(2,128)(2,1)S(1)} %get-tuple-element.80), channel_id=1, source_target_pairs={{4,0},{8,4},{12,8},{0,12},{5,1},{9,5},{13,9},{1,13},{6,2},{10,6},{... | collective-permute-start | bytes 12296 | tf_op jit(solution)/shard_map/ppermute | solution.py:15
  9.2 1.5 %collective-permute-done = bf16[128,16,1]{0,2,1:T(2,128)(2,1)S(1)} collective-permute-done((bf16[128,16,1]{0,2,1:T(2,128)(2,1)S(1)}, bf16[128,16,1]{0,2,1:T(2,128)(2,1)S(1)}, u32[]{:S(2)}, u32[]{:S(2)}) %collective-permute-start) | collective-permute-done | bytes 4128 | tf_op jit(solution)/shard_map/ppermute | solution.py:14
  12.5 0.9 %fusion.55 = (bf16[128,16,128]{0,2,1:T(8,128)(2,1)S(1)}, bf16[128,16,128]{0,2,1:T(8,128)(2,1)S(1)}, bf16[128,16,128]{0,2,1:T(8,128)(2,1)S(1)}, bf16[128,16,128]{...) fusion(bf16[128,18,130]{0,2,1:T(8,128)(2,1)S(1)} %maximum_selec, ...), kind=kLoop, calls=%fused_computation.209 | loop fusion | bytes 9437184 | tf_op jit(solution)/shard_map/slice | solution.py:37
  16.7 2.0 %collective-permute-done.4 = bf16[128,292]{0,1:T(8,128)(2,1)S(1)} collective-permute-done((bf16[128,292]{0,1:T(8,128)(2,1)S(1)}, bf16[128,292]{0,1:T(8,128)(2,1)S(1)}, u32[]{:S(2)}, u32[]{:S(2)}) %collective-permute-start.4) | collective-permute-done | bytes 74784 | tf_op jit(solution)/shard_map/ppermute | solution.py:127
  18.8 1.2 %pad_maximum_fusion.2 = bf16[128,18,130]{0,2,1:T(8,128)(2,1)S(1)} fusion(bf16[128,1,130]{0,2,1:T(8,128)(2,1)S(1)} %get-tuple-element.86, bf16[128,16,1]{0,2,1:T(2,128)(2,1)S(1)} %copy.35, bf16[128,16,128]{0,2,1:T(8,128)(2,1)} %collective-permute-done.5, bf16[128,16,1]{0,2,1:T(2,128)(2,1)S(1)} %copy.34, bf16[128,1,130]{0,2,1:T(8,128)(2,1)S(1)} %get-tuple-element.85), kind=kLoop, calls=%fused_computation.93 | loop fusion | flops 2995200 | bytes 1198080 | tf_op jit(solution)/shard_map/concatenate | solution.py:111
  20.0 0.9 %fusion.53 = (bf16[128,16,128]{0,2,1:T(8,128)(2,1)S(1)}, bf16[128,16,128]{0,2,1:T(8,128)(2,1)S(1)}, bf16[128,16,128]{0,2,1:T(8,128)(2,1)S(1)}, bf16[128,16,128]{...) fusion(bf16[128,18,130]{0,2,1:T(8,128)(2,1)S(1)} %pad_maximum_f, ...), kind=kLoop, calls=%fused_computation.207 | loop fusion | bytes 9437184 | tf_op jit(solution)/shard_map/slice | solution.py:37
  20.9 2.5 %fusion.16 = (bf16[256,16,128]{0,2,1:T(8,128)(2,1)S(1)}, bf16[256,16,128]{0,2,1:T(8,128)(2,1)S(1)}, bf16[256,16,128]{0,2,1:T(8,128)(2,1)S(1)}, bf16[256,16,128]{...) fusion(bf16[128,18,130]{0,2,1:T(8,128)(2,1)S(1)} %maximum_selec, ...), kind=kLoop, calls=%fused_computation.83 | loop fusion | flops 18874368 | bytes 10635264 | tf_op jit(solution)/shard_map/concatenate | solution.py:153
  23.8 1.8 %collective-permute-start.6 = (bf16[3,3,128,128]{3,2,1,0:T(8,128)(2,1)S(1)}, bf16[3,3,128,128]{3,2,1,0:T(8,128)(2,1)S(1)}, u32[]{:S(2)}, u32[]{:S(2)}) collective-permute-start(bf16[3,3,128,128]{3,2,1,0:T(8,128)(2,1)S(1)} %get-tuple-element.9), channel_id=1, source_target_pairs={{0,2},{2,0},{1,3},{3,1},{4,6},{6,4},{5,7},{7,5},{8,10},{10,8},{9,1... | collective-permute-start | bytes 884744 | tf_op jit(solution)/shard_map/ppermute | solution.py:143
  28.1 0.9 %fusion.14 = bf16[128,2048]{1,0:T(8,128)(2,1)S(1)} fusion(f32[16,8,16,128]{3,2,1,0:T(8,128)S(1)} %convert.13, f32[128,2048]{1,0:T(8,128)S(1)} %convolution_add_fusion.24, f32[128,2048]{1,0:T(8,128)S(1)} %convolution_add_fusion.17, bf16[128,2048]{0,1:T(8,128)(2,1)S(1)} %bitcast.336, f32[128]{0:T(128)S(1)} %copy-done.4, ...), kind=kOutput, calls=%fused_computation.81 | convolution fusion | flops 70516736 | bytes 4227592 | tf_op jit(solution)/shard_map/dot_general | solution.py:50
  29.0 3.4 %collective-permute-done.6 = bf16[3,3,128,128]{3,2,1,0:T(8,128)(2,1)S(1)} collective-permute-done((bf16[3,3,128,128]{3,2,1,0:T(8,128)(2,1)S(1)}, bf16[3,3,128,128]{3,2,1,0:T(8,128)(2,1)S(1)}, u32[]{:S(2)}, u32[]{:S(2)}) %collective-permute-start.6) | collective-permute-done | bytes 294944 | tf_op jit(solution)/shard_map/ppermute | solution.py:143
  37.1 1.3 %collective-permute-start.11 = (bf16[128,16,128]{0,2,1:T(8,128)(2,1)S(1)}, bf16[128,16,128]{0,2,1:T(8,128)(2,1)}, u32[]{:S(2)}, u32[]{:S(2)}) collective-permute-start(bf16[128,16,128]{0,2,1:T(8,128)(2,1)S(1)} %copy.36), channel_id=1, source_target_pairs={{0,2},{2,0},{1,3},{3,1},{4,6},{6,4},{5,7},{7,5},{8,10},{10,8},{9,1... | collective-permute-start | bytes 1572872 | tf_op jit(solution)/shard_map/ppermute | solution.py:172
  38.6 1.1 %bitcast_add_fusion = f32[1184,128]{1,0:T(8,128)S(1)} fusion(f32[1184,128]{1,0:T(8,128)} %collective-permute-done.7, f32[2,1184,128]{2,1,0:T(8,128)S(1)} %bitcast.318, s32[]{:T(128)S(6)} %select_n.101), kind=kLoop, calls=%fused_computation.96 | loop fusion | flops 151552 | bytes 1818628 | tf_op jit(solution)/shard_map/add | solution.py:64
  39.8 3.9 %collective-permute-start.10 = (bf16[296,128]{1,0:T(8,128)(2,1)S(1)}, bf16[296,128]{1,0:T(8,128)(2,1)S(1)}, u32[]{:S(2)}, u32[]{:S(2)}) collective-permute-start(bf16[296,128]{1,0:T(8,128)(2,1)S(1)} %get-tuple-element.69), channel_id=1, source_target_pairs={{0,12},{4,0},{8,4},{12,8},{1,13},{5,1},{9,5},{13,9},{2,14},{6,2},{... | collective-permute-start | bytes 227336 | tf_op jit(solution)/shard_map/ppermute | solution.py:64
  43.7 0.8 %collective-permute-start.9 = (bf16[296,128]{1,0:T(8,128)(2,1)S(1)}, bf16[296,128]{1,0:T(8,128)(2,1)S(1)}, u32[]{:S(2)}, u32[]{:S(2)}) collective-permute-start(bf16[296,128]{1,0:T(8,128)(2,1)S(1)} %get-tuple-element.70), channel_id=1, source_target_pairs={{0,8},{4,12},{8,0},{12,4},{1,9},{5,13},{9,1},{13,5},{2,10},{6,14},... | collective-permute-start | bytes 227336 | tf_op jit(solution)/shard_map/ppermute | solution.py:64
  44.5 1.9 %collective-permute-done.10 = bf16[296,128]{1,0:T(8,128)(2,1)S(1)} collective-permute-done((bf16[296,128]{1,0:T(8,128)(2,1)S(1)}, bf16[296,128]{1,0:T(8,128)(2,1)S(1)}, u32[]{:S(2)}, u32[]{:S(2)}) %collective-permute-start.10) | collective-permute-done | bytes 75808 | tf_op jit(solution)/shard_map/ppermute | solution.py:64
  46.4 4.1 %collective-permute-done.8 = bf16[296,128]{1,0:T(8,128)(2,1)S(1)} collective-permute-done((bf16[296,128]{1,0:T(8,128)(2,1)S(1)}, bf16[296,128]{1,0:T(8,128)(2,1)S(1)}, u32[]{:S(2)}, u32[]{:S(2)}) %collective-permute-start.8) | collective-permute-done | bytes 75808 | tf_op jit(solution)/shard_map/ppermute | solution.py:64
  50.5 1.5 %collective-permute-done.9 = bf16[296,128]{1,0:T(8,128)(2,1)S(1)} collective-permute-done((bf16[296,128]{1,0:T(8,128)(2,1)S(1)}, bf16[296,128]{1,0:T(8,128)(2,1)S(1)}, u32[]{:S(2)}, u32[]{:S(2)}) %collective-permute-start.9) | collective-permute-done | bytes 75808 | tf_op jit(solution)/shard_map/ppermute | solution.py:64
  52.5 1.0 %collective-permute-start.12 = (bf16[128,16,1]{0,2,1:T(2,128)(2,1)S(1)}, bf16[128,16,1]{0,2,1:T(2,128)(2,1)S(1)}, u32[]{:S(2)}, u32[]{:S(2)}) collective-permute-start(bf16[128,16,1]{0,2,1:T(2,128)(2,1)S(1)} %get-tuple-element.77), channel_id=1, source_target_pairs={{0,4},{4,8},{8,12},{12,0},{1,5},{5,9},{9,13},{13,1},{2,6},{6,10},{... | collective-permute-start | bytes 12296 | tf_op jit(solution)/shard_map/ppermute | solution.py:14
  53.6 2.8 %collective-permute-start.13 = (bf16[128,16,1]{0,2,1:T(2,128)(2,1)S(1)}, bf16[128,16,1]{0,2,1:T(2,128)(2,1)S(1)}, u32[]{:S(2)}, u32[]{:S(2)}) collective-permute-start(bf16[128,16,1]{0,2,1:T(2,128)(2,1)S(1)} %get-tuple-element.78), channel_id=1, source_target_pairs={{4,0},{8,4},{12,8},{0,12},{5,1},{9,5},{13,9},{1,13},{6,2},{10,6},{... | collective-permute-start | bytes 12296 | tf_op jit(solution)/shard_map/ppermute | solution.py:15
  56.4 1.7 %collective-permute-done.12 = bf16[128,16,1]{0,2,1:T(2,128)(2,1)S(1)} collective-permute-done((bf16[128,16,1]{0,2,1:T(2,128)(2,1)S(1)}, bf16[128,16,1]{0,2,1:T(2,128)(2,1)S(1)}, u32[]{:S(2)}, u32[]{:S(2)}) %collective-permute-start.12) | collective-permute-done | bytes 4128 | tf_op jit(solution)/shard_map/ppermute | solution.py:14
  58.7 3.8 %collective-permute-start.17 = (bf16[296,128]{1,0:T(8,128)(2,1)S(1)}, bf16[296,128]{1,0:T(8,128)(2,1)S(1)}, u32[]{:S(2)}, u32[]{:S(2)}) collective-permute-start(bf16[296,128]{1,0:T(8,128)(2,1)S(1)} %convert_element_type.64), channel_id=1, source_target_pairs={{0,12},{4,0},{8,4},{12,8},{1,13},{5,1},{9,5},{13,9},{2,14},{6,2},{... | collective-permute-start | bytes 227336 | tf_op jit(solution)/shard_map/ppermute | solution.py:76
  62.5 0.6 collective-permute-start.19
  63.5 0.9 %fusion.52 = (bf16[128,16,128]{0,2,1:T(8,128)(2,1)S(1)}, bf16[128,16,128]{0,2,1:T(8,128)(2,1)S(1)}, bf16[128,16,128]{0,2,1:T(8,128)(2,1)S(1)}, bf16[128,16,128]{...) fusion(bf16[128,18,130]{0,2,1:T(8,128)(2,1)S(1)} %maximum_selec, ...), kind=kLoop, calls=%fused_computation.206 | loop fusion | bytes 9437184 | tf_op jit(solution)/shard_map/slice | solution.py:37
  64.5 1.1 %collective-permute-start.16 = (bf16[128,292]{0,1:T(8,128)(2,1)S(1)}, bf16[128,292]{0,1:T(8,128)(2,1)S(1)}, u32[]{:S(2)}, u32[]{:S(2)}) collective-permute-start(bf16[128,292]{0,1:T(8,128)(2,1)S(1)} %pad_maximum_fusion.5), channel_id=1, source_target_pairs={{0,2},{2,0},{1,3},{3,1},{4,6},{6,4},{5,7},{7,5},{8,10},{10,8},{9,1... | collective-permute-start | bytes 224264 | tf_op jit(solution)/shard_map/ppermute | solution.py:186
  68.6 1.4 %collective-permute-done.18 = bf16[296,128]{1,0:T(8,128)(2,1)S(1)} collective-permute-done((bf16[296,128]{1,0:T(8,128)(2,1)S(1)}, bf16[296,128]{1,0:T(8,128)(2,1)S(1)}, u32[]{:S(2)}, u32[]{:S(2)}) %collective-permute-start.18) | collective-permute-done | bytes 75808 | tf_op jit(solution)/shard_map/ppermute | solution.py:76
  70.3 1.2 %pad_maximum_fusion.3 = bf16[128,18,130]{0,2,1:T(8,128)(2,1)S(1)} fusion(bf16[128,1,130]{0,2,1:T(8,128)(2,1)S(1)} %get-tuple-element.82, bf16[128,16,1]{0,2,1:T(2,128)(2,1)S(1)} %copy.41, bf16[128,16,128]{0,2,1:T(8,128)(2,1)} %collective-permute-done.11, bf16[128,16,1]{0,2,1:T(2,128)(2,1)S(1)} %copy.40, bf16[128,1,130]{0,2,1:T(8,128)(2,1)S(1)} %get-tuple-element.81), kind=kLoop, calls=%fused_computation.95 | loop fusion | flops 2995200 | bytes 1198080 | tf_op jit(solution)/shard_map/concatenate | solution.py:111
  71.6 0.9 %fusion.50 = (bf16[128,16,128]{0,2,1:T(8,128)(2,1)S(1)}, bf16[128,16,128]{0,2,1:T(8,128)(2,1)S(1)}, bf16[128,16,128]{0,2,1:T(8,128)(2,1)S(1)}, bf16[128,16,128]{...) fusion(bf16[128,18,130]{0,2,1:T(8,128)(2,1)S(1)} %pad_maximum_f, ...), kind=kLoop, calls=%fused_computation.204 | loop fusion | bytes 9437184 | tf_op jit(solution)/shard_map/slice | solution.py:37
  75.5 0.9 %copy.49 = bf16[16,8,16,128]{3,2,1,0:T(8,128)(2,1)} copy(bf16[16,8,16,128]{3,1,2,0:T(8,128)(2,1)S(1)} %fusion.4) | data formatting | bytes 1048576
  77.5 1.2 %fusion.8 = f32[3,3,128,256]{3,2,1,0:T(8,128)} fusion(s32[]{:T(128)S(6)} %select_n.117, f32[3,3,128,256]{3,2,1,0:T(8,128)S(1)} %reshape.225), kind=kLoop, calls=%fused_computation.65 | loop fusion | flops 294912 | bytes 2359300 | tf_op jit(solution)/shard_map/concatenate | solution.py:177
  (129 shorter events, 21.5 us)
Async XLA Ops:
  0.6 8.5 %copy-start = (bf16[3,3,128,256]{3,2,1,0:T(8,128)(2,1)S(1)}, bf16[3,3,128,256]{3,2,1,0:T(8,128)(2,1)}, u32[]{:S(2)}) copy-start(bf16[3,3,128,256]{3,2,1,0:T(8,128)(2,1)} %param.6) | copy-start | bytes 1769476
  2.2 9.2 %copy-start.1 = (bf16[128,16,128]{2,1,0:T(8,128)(2,1)S(1)}, bf16[128,16,128]{2,1,0:T(8,128)(2,1)}, u32[]{:S(2)}) copy-start(bf16[128,16,128]{2,1,0:T(8,128)(2,1)} %param.5) | copy-start | bytes 1572868
  2.2 16.6 %collective-permute-start.5 = (bf16[128,16,128]{0,2,1:T(8,128)(2,1)S(1)}, bf16[128,16,128]{0,2,1:T(8,128)(2,1)}, u32[]{:S(2)}, u32[]{:S(2)}) collective-permute-start(bf16[128,16,128]{0,2,1:T(8,128)(2,1)S(1)} %copy.30), channel_id=1, source_target_pairs={{0,2},{2,0},{1,3},{3,1},{4,6},{6,4},{5,7},{7,5},{8,10},{10,8},{9,1... | collective-permute-start | bytes 1572872 | tf_op jit(solution)/shard_map/ppermute | solution.py:121
  5.2 5.5 %collective-permute-start = (bf16[128,16,1]{0,2,1:T(2,128)(2,1)S(1)}, bf16[128,16,1]{0,2,1:T(2,128)(2,1)S(1)}, u32[]{:S(2)}, u32[]{:S(2)}) collective-permute-start(bf16[128,16,1]{0,2,1:T(2,128)(2,1)S(1)} %get-tuple-element.79), channel_id=1, source_target_pairs={{0,4},{4,8},{8,12},{12,0},{1,5},{5,9},{9,13},{13,1},{2,6},{6,10},{... | collective-permute-start | bytes 12296 | tf_op jit(solution)/shard_map/ppermute | solution.py:14
  6.8 3.9 %collective-permute-start.1 = (bf16[128,16,1]{0,2,1:T(2,128)(2,1)S(1)}, bf16[128,16,1]{0,2,1:T(2,128)(2,1)S(1)}, u32[]{:S(2)}, u32[]{:S(2)}) collective-permute-start(bf16[128,16,1]{0,2,1:T(2,128)(2,1)S(1)} %get-tuple-element.80), channel_id=1, source_target_pairs={{4,0},{8,4},{12,8},{0,12},{5,1},{9,5},{13,9},{1,13},{6,2},{10,6},{... | collective-permute-start | bytes 12296 | tf_op jit(solution)/shard_map/ppermute | solution.py:15
  10.7 1.3 %collective-permute-start.2 = (bf16[128,1,130]{0,2,1:T(8,128)(2,1)S(1)}, bf16[128,1,130]{0,2,1:T(8,128)(2,1)S(1)}, u32[]{:S(2)}, u32[]{:S(2)}) collective-permute-start(bf16[128,1,130]{0,2,1:T(8,128)(2,1)S(1)} %get-tuple-element.75), channel_id=1, source_target_pairs={{0,1},{1,0},{2,3},{3,2},{4,5},{5,4},{6,7},{7,6},{8,9},{9,8},{10,11... | collective-permute-start | bytes 99848 | tf_op jit(solution)/shard_map/ppermute | solution.py:14
  10.8 1.4 %collective-permute-start.3 = (bf16[128,1,130]{0,2,1:T(8,128)(2,1)S(1)}, bf16[128,1,130]{0,2,1:T(8,128)(2,1)S(1)}, u32[]{:S(2)}, u32[]{:S(2)}) collective-permute-start(bf16[128,1,130]{0,2,1:T(8,128)(2,1)S(1)} %get-tuple-element.76), channel_id=1, source_target_pairs={{1,0},{0,1},{3,2},{2,3},{5,4},{4,5},{7,6},{6,7},{9,8},{8,9},{11,10... | collective-permute-start | bytes 99848 | tf_op jit(solution)/shard_map/ppermute | solution.py:15
  13.5 5.2 %collective-permute-start.4 = (bf16[128,292]{0,1:T(8,128)(2,1)S(1)}, bf16[128,292]{0,1:T(8,128)(2,1)S(1)}, u32[]{:S(2)}, u32[]{:S(2)}) collective-permute-start(bf16[128,292]{0,1:T(8,128)(2,1)S(1)} %pad_maximum_fusion.4), channel_id=1, source_target_pairs={{0,2},{2,0},{1,3},{3,1},{4,6},{6,4},{5,7},{7,5},{8,10},{10,8},{9,1... | collective-permute-start | bytes 224264 | tf_op jit(solution)/shard_map/ppermute | solution.py:127
  23.8 8.6 %collective-permute-start.6 = (bf16[3,3,128,128]{3,2,1,0:T(8,128)(2,1)S(1)}, bf16[3,3,128,128]{3,2,1,0:T(8,128)(2,1)S(1)}, u32[]{:S(2)}, u32[]{:S(2)}) collective-permute-start(bf16[3,3,128,128]{3,2,1,0:T(8,128)(2,1)S(1)} %get-tuple-element.9), channel_id=1, source_target_pairs={{0,2},{2,0},{1,3},{3,1},{4,6},{6,4},{5,7},{7,5},{8,10},{10,8},{9,1... | collective-permute-start | bytes 884744 | tf_op jit(solution)/shard_map/ppermute | solution.py:143
  27.4 0.7 copy-start.4
  32.4 0.8 %copy-start.2 = (bf16[3,3,128,128]{3,2,1,0:T(8,128)(2,1)}, bf16[3,3,128,128]{3,2,1,0:T(8,128)(2,1)S(1)}, u32[]{:S(2)}) copy-start(bf16[3,3,128,128]{3,2,1,0:T(8,128)(2,1)S(1)} %collective-permute-done.6) | copy-start | bytes 884740
  36.4 2.2 %collective-permute-start.7 = (f32[1184,128]{1,0:T(8,128)S(1)}, f32[1184,128]{1,0:T(8,128)}, u32[]{:S(2)}, u32[]{:S(2)}) collective-permute-start(f32[1184,128]{1,0:T(8,128)S(1)} %dynamic-slice_bitcast_fusion), channel_id=1, source_target_pairs={{0,1},{1,0},{2,3},{3,2},{4,5},{5,4},{6,7},{7,6},{8,9},{9,8},{10,11... | collective-permute-start | bytes 1818632 | tf_op jit(solution)/shard_map/ppermute | solution.py:64
  37.1 14.9 %collective-permute-start.11 = (bf16[128,16,128]{0,2,1:T(8,128)(2,1)S(1)}, bf16[128,16,128]{0,2,1:T(8,128)(2,1)}, u32[]{:S(2)}, u32[]{:S(2)}) collective-permute-start(bf16[128,16,128]{0,2,1:T(8,128)(2,1)S(1)} %copy.36), channel_id=1, source_target_pairs={{0,2},{2,0},{1,3},{3,1},{4,6},{6,4},{5,7},{7,5},{8,10},{10,8},{9,1... | collective-permute-start | bytes 1572872 | tf_op jit(solution)/shard_map/ppermute | solution.py:172
  39.8 6.5 %collective-permute-start.10 = (bf16[296,128]{1,0:T(8,128)(2,1)S(1)}, bf16[296,128]{1,0:T(8,128)(2,1)S(1)}, u32[]{:S(2)}, u32[]{:S(2)}) collective-permute-start(bf16[296,128]{1,0:T(8,128)(2,1)S(1)} %get-tuple-element.69), channel_id=1, source_target_pairs={{0,12},{4,0},{8,4},{12,8},{1,13},{5,1},{9,5},{13,9},{2,14},{6,2},{... | collective-permute-start | bytes 227336 | tf_op jit(solution)/shard_map/ppermute | solution.py:64
  43.7 6.8 %collective-permute-start.8 = (bf16[296,128]{1,0:T(8,128)(2,1)S(1)}, bf16[296,128]{1,0:T(8,128)(2,1)S(1)}, u32[]{:S(2)}, u32[]{:S(2)}) collective-permute-start(bf16[296,128]{1,0:T(8,128)(2,1)S(1)} %get-tuple-element.68), channel_id=1, source_target_pairs={{0,4},{4,8},{8,12},{12,0},{1,5},{5,9},{9,13},{13,1},{2,6},{6,10},{... | collective-permute-start | bytes 227336 | tf_op jit(solution)/shard_map/ppermute | solution.py:64
  43.7 8.3 %collective-permute-start.9 = (bf16[296,128]{1,0:T(8,128)(2,1)S(1)}, bf16[296,128]{1,0:T(8,128)(2,1)S(1)}, u32[]{:S(2)}, u32[]{:S(2)}) collective-permute-start(bf16[296,128]{1,0:T(8,128)(2,1)S(1)} %get-tuple-element.70), channel_id=1, source_target_pairs={{0,8},{4,12},{8,0},{12,4},{1,9},{5,13},{9,1},{13,5},{2,10},{6,14},... | collective-permute-start | bytes 227336 | tf_op jit(solution)/shard_map/ppermute | solution.py:64
  52.5 5.5 %collective-permute-start.12 = (bf16[128,16,1]{0,2,1:T(2,128)(2,1)S(1)}, bf16[128,16,1]{0,2,1:T(2,128)(2,1)S(1)}, u32[]{:S(2)}, u32[]{:S(2)}) collective-permute-start(bf16[128,16,1]{0,2,1:T(2,128)(2,1)S(1)} %get-tuple-element.77), channel_id=1, source_target_pairs={{0,4},{4,8},{8,12},{12,0},{1,5},{5,9},{9,13},{13,1},{2,6},{6,10},{... | collective-permute-start | bytes 12296 | tf_op jit(solution)/shard_map/ppermute | solution.py:14
  53.6 4.5 %collective-permute-start.13 = (bf16[128,16,1]{0,2,1:T(2,128)(2,1)S(1)}, bf16[128,16,1]{0,2,1:T(2,128)(2,1)S(1)}, u32[]{:S(2)}, u32[]{:S(2)}) collective-permute-start(bf16[128,16,1]{0,2,1:T(2,128)(2,1)S(1)} %get-tuple-element.78), channel_id=1, source_target_pairs={{4,0},{8,4},{12,8},{0,12},{5,1},{9,5},{13,9},{1,13},{6,2},{10,6},{... | collective-permute-start | bytes 12296 | tf_op jit(solution)/shard_map/ppermute | solution.py:15
  58.1 5.1 %collective-permute-start.14 = (bf16[128,1,130]{0,2,1:T(8,128)(2,1)S(1)}, bf16[128,1,130]{0,2,1:T(8,128)(2,1)S(1)}, u32[]{:S(2)}, u32[]{:S(2)}) collective-permute-start(bf16[128,1,130]{0,2,1:T(8,128)(2,1)S(1)} %get-tuple-element.73), channel_id=1, source_target_pairs={{0,1},{1,0},{2,3},{3,2},{4,5},{5,4},{6,7},{7,6},{8,9},{9,8},{10,11... | collective-permute-start | bytes 99848 | tf_op jit(solution)/shard_map/ppermute | solution.py:14
  58.2 5.0 %collective-permute-start.15 = (bf16[128,1,130]{0,2,1:T(8,128)(2,1)S(1)}, bf16[128,1,130]{0,2,1:T(8,128)(2,1)S(1)}, u32[]{:S(2)}, u32[]{:S(2)}) collective-permute-start(bf16[128,1,130]{0,2,1:T(8,128)(2,1)S(1)} %get-tuple-element.74), channel_id=1, source_target_pairs={{1,0},{0,1},{3,2},{2,3},{5,4},{4,5},{7,6},{6,7},{9,8},{8,9},{11,10... | collective-permute-start | bytes 99848 | tf_op jit(solution)/shard_map/ppermute | solution.py:15
  58.7 9.8 %collective-permute-start.17 = (bf16[296,128]{1,0:T(8,128)(2,1)S(1)}, bf16[296,128]{1,0:T(8,128)(2,1)S(1)}, u32[]{:S(2)}, u32[]{:S(2)}) collective-permute-start(bf16[296,128]{1,0:T(8,128)(2,1)S(1)} %convert_element_type.64), channel_id=1, source_target_pairs={{0,12},{4,0},{8,4},{12,8},{1,13},{5,1},{9,5},{13,9},{2,14},{6,2},{... | collective-permute-start | bytes 227336 | tf_op jit(solution)/shard_map/ppermute | solution.py:76
  62.5 7.4 %collective-permute-start.18 = (bf16[296,128]{1,0:T(8,128)(2,1)S(1)}, bf16[296,128]{1,0:T(8,128)(2,1)S(1)}, u32[]{:S(2)}, u32[]{:S(2)}) collective-permute-start(bf16[296,128]{1,0:T(8,128)(2,1)S(1)} %convert_element_type.64), channel_id=1, source_target_pairs={{0,8},{4,12},{8,0},{12,4},{1,9},{5,13},{9,1},{13,5},{2,10},{6,14},... | collective-permute-start | bytes 227336 | tf_op jit(solution)/shard_map/ppermute | solution.py:76
  62.5 7.4 %collective-permute-start.19 = (bf16[296,128]{1,0:T(8,128)(2,1)S(1)}, bf16[296,128]{1,0:T(8,128)(2,1)S(1)}, u32[]{:S(2)}, u32[]{:S(2)}) collective-permute-start(bf16[296,128]{1,0:T(8,128)(2,1)S(1)} %convert_element_type.64), channel_id=1, source_target_pairs={{0,4},{4,8},{8,12},{12,0},{1,5},{5,9},{9,13},{13,1},{2,6},{6,10},{... | collective-permute-start | bytes 227336 | tf_op jit(solution)/shard_map/ppermute | solution.py:76
  64.5 5.7 %collective-permute-start.16 = (bf16[128,292]{0,1:T(8,128)(2,1)S(1)}, bf16[128,292]{0,1:T(8,128)(2,1)S(1)}, u32[]{:S(2)}, u32[]{:S(2)}) collective-permute-start(bf16[128,292]{0,1:T(8,128)(2,1)S(1)} %pad_maximum_fusion.5), channel_id=1, source_target_pairs={{0,2},{2,0},{1,3},{3,1},{4,6},{6,4},{5,7},{7,5},{8,10},{10,8},{9,1... | collective-permute-start | bytes 224264 | tf_op jit(solution)/shard_map/ppermute | solution.py:186
  70.2 6.2 %collective-permute-start.20 = (f32[1184,128]{1,0:T(8,128)S(1)}, f32[1184,128]{1,0:T(8,128)S(1)}, u32[]{:S(2)}, u32[]{:S(2)}) collective-permute-start(f32[1184,128]{1,0:T(8,128)S(1)} %bitcast.334), channel_id=1, source_target_pairs={{0,1},{1,0},{2,3},{3,2},{4,5},{5,4},{6,7},{7,6},{8,9},{9,8},{10,11... | collective-permute-start | bytes 1818632 | tf_op jit(solution)/shard_map/ppermute | solution.py:76
  71.6 1.0 %copy-start.3 = (bf16[3,3,128,128]{3,2,1,0:T(8,128)(2,1)S(1)}, bf16[3,3,128,128]{3,2,1,0:T(8,128)(2,1)}, u32[]{:S(2)}) copy-start(bf16[3,3,128,128]{3,2,1,0:T(8,128)(2,1)} %copy-done.2) | copy-start | bytes 884740

commit v11 on v8

--- a/solution.py
+++ b/solution.py
@@ -79,12 +79,33 @@
     return stacked.reshape(-1, chunk.shape[-1])
 
 
-def sum_start(flat, send_dtype):
+def sum_start(flat, send_dtype, columns):
     parts = lax.axis_size("lat") * lax.axis_size("lon")
-    quantum = parts * 8 * 128
+    quantum = parts * 16 * 128
     padded = jnp.pad(flat, (0, (-flat.size) % quantum)).reshape(-1, 128)
     rows = direct_reduce_scatter(padded, "lat", jnp.float32)
-    return direct_reduce_scatter(rows, "lon", send_dtype)
+    count, index = lax.axis_size("lon"), lax.axis_index("lon")
+    last, first = columns
+    if count < 3:
+        up = [(i, (i + 1) % count) for i in range(count)]
+        down = [(j, i) for i, j in up]
+        halo = (lax.ppermute(last, "lon", up), lax.ppermute(first, "lon", down))
+        return direct_reduce_scatter(rows, "lon", send_dtype), halo
+    chunks = rows.reshape(count, -1, rows.shape[-1])
+    size = chunks.shape[1]
+    acc = lax.dynamic_index_in_dim(chunks, index, keepdims=False)
+    extra = {1: last, count - 1: first}
+    got = {}
+    for step in range(1, count):
+        pairs = [(j, (j + step) % count) for j in range(count)]
+        piece = lax.dynamic_index_in_dim(chunks, (index + step) % count, keepdims=False).astype(send_dtype)
+        if step in extra:
+            piece = jnp.concatenate([piece, extra[step].astype(send_dtype).reshape(-1, rows.shape[-1])], axis=0)
+        moved = lax.ppermute(piece, "lon", pairs)
+        acc = acc + moved[:size].astype(jnp.float32)
+        if step in extra:
+            got[step] = moved[size:].reshape(last.shape).astype(last.dtype)
+    return acc, (got[1], got[count - 1])
 
 
 def sum_finish(rows, size, send_dtype):
@@ -154,8 +175,9 @@
         taps.append(jnp.stack(row_taps))
     weight_part = jnp.stack(taps)
     flat = jnp.concatenate([weight_part.reshape(-1), bias_part])
-    scattered = sum_start(flat, jnp.bfloat16)
-    grad_pre, scattered = lax.optimization_barrier((grad_pre, scattered))
+    grad_field = grad_pre.reshape(own_channels, row_count, column_count)
+    edges = (grad_field[:, :, column_count - 1 :], grad_field[:, :, :1])
+    scattered, (before, after) = sum_start(flat, jnp.bfloat16, edges)
     flat = sum_finish(scattered, flat.size, jnp.bfloat16)
     weight_local = flat[: weight_part.size].reshape(weight_part.shape)
     bias_grad = flat[weight_part.size :]
@@ -163,8 +185,8 @@
     weight_grad = lax.dynamic_slice_in_dim(
         doubled, (chan_count - chan_index) % chan_count * own_channels, chan_count * own_channels, axis=3
     )
-    grad_field = grad_pre.reshape(own_channels, row_count, column_count)
-    grad_pad = mask_rims(padded_2(grad_field, (("lon", 2), ("lat", 1)), 1))
+    grad_wide = jnp.concatenate([before, grad_field, after], axis=2)
+    grad_pad = mask_rims(padded_2(grad_wide, (("lat", 1),), 1))
     received = []
     for shift in range(1, chan_count):
         kernel_t = jnp.swapaxes(kernel_cols[shift], 2, 3)

time: 75.8 us -> 71.5 us (0.943)
  waiting for transfers between devices: 30 us -> 21.3 us
  local copies, waits for them, and re-layouts: 7.72 us -> 9.36 us
  starting transfers between devices: 16.3 us -> 17.9 us
  other arithmetic: 5.38 us -> 6.5 us
    ppermute x4 -> x1, waiting for transfers between devices: 8.99 us -> 0.94 us  [direct_reduce_scatter(): lax.ppermute(piece.astype(send_dtype), axis, pairs).astype(jnp.float32)]
    ppermute x0 -> x3, waiting for transfers between devices: none -> 5.21 us  [sum_start(): moved = lax.ppermute(piece, 'lon', pairs)]
    ppermute x4 -> x3, waiting for transfers between devices: 7.29 us -> 2.2 us  [padded_2(): before = lax.ppermute(last, axis, up)]
    ppermute x0 -> x3, starting transfers between devices: none -> 4.99 us  [sum_start(): moved = lax.ppermute(piece, 'lon', pairs)]
    ppermute x4 -> x3, waiting for transfers between devices: 3.56 us -> 0.17 us  [padded_2(): after = lax.ppermute(initial, axis, down)]
    ppermute x4 -> x3, starting transfers between devices: 5.1 us -> 2.82 us  [padded_2(): after = lax.ppermute(initial, axis, down)]
    ppermute x4 -> x1, starting transfers between devices: 2.15 us -> 0.07 us  [direct_reduce_scatter(): lax.ppermute(piece.astype(send_dtype), axis, pairs).astype(jnp.float32)]
    ppermute x1, waiting for transfers between devices: 8.91 us -> 10.8 us  [local(): received.append(lax.ppermute(part.astype(jnp.bfloat16), 'chan', pairs))]
  transfers between devices with their start and end apart: 19 -> 17, of which waited for: 11 -> 9; matrix products, arithmetic and copies ran while one was open for 16% -> 20% of each run, Pallas kernels for 0% -> 0%
where the time goes in v11:
time: 71.5 us; the launch traced here: 71.3 us
  waiting for transfers between devices  21.3 us (30%)
  starting transfers between devices  17.9 us (25%)
  matrix products  14.8 us (21%)
  local copies, waits for them, and re-layouts  9.36 us (13%)
  other arithmetic  6.5 us (9%)
  between operations  1.45 us (2%)
    dot_general x36, matrix products, conv_taps(): jnp.dot(kernel[tap_row, tap_col], window, preferred_element_type=jnp.floa...  11.9 us
    ppermute x1, waiting for transfers between devices, local(): received.append(lax.ppermute(part.astype(jnp.bfloat16), 'chan', pairs))  10.8 us
    ppermute x3, waiting for transfers between devices, sum_start(): moved = lax.ppermute(piece, 'lon', pairs)  5.21 us
    ppermute x3, starting transfers between devices, sum_start(): moved = lax.ppermute(piece, 'lon', pairs)  4.99 us
    unnamed x12, local copies, waits for them, and re-layouts  3.51 us
    ppermute x1, starting transfers between devices, local(): raw_blocks.append(lax.ppermute(inputs, 'chan', pairs))  3 us
    dot_general x9, matrix products, local(): lax.dot_general(grad_pre, window, (((1,), (1,)), ((), ())), preferred_ele...  2.85 us
    ppermute x3, starting transfers between devices, padded_2(): after = lax.ppermute(initial, axis, down)  2.82 us
  transfers between devices with their start and end apart: 17, of which 9 were waited for; matrix products, arithmetic and copies ran while one was open for 20% of the time, Pallas kernels for 0%

profile of v11, /device:TPU:0, one launch (start us, length us, event | category | flops | bytes accessed | tf_op | source)
XLA Modules:
  0.0 71.3 jit_solution(14804650682177717308)
XLA Ops:
  0.6 1.5 %copy.12 = bf16[128,16,128]{0,2,1:T(8,128)(2,1)S(1)} copy(bf16[128,16,128]{2,1,0:T(8,128)(2,1)} %param.4) | data formatting | bytes 1048576 | tf_op args[0]
  2.2 3.0 %collective-permute-start.5 = (bf16[128,16,128]{0,2,1:T(8,128)(2,1)S(1)}, bf16[128,16,128]{0,2,1:T(8,128)(2,1)S(1)}, u32[]{:S(2)}, u32[]{:S(2)}) collective-permute-start(bf16[128,16,128]{0,2,1:T(8,128)(2,1)S(1)} %copy.12), channel_id=1, source_target_pairs={{0,2},{2,0},{1,3},{3,1},{4,6},{6,4},{5,7},{7,5},{8,10},{10,8},{9,1... | collective-permute-start | bytes 1572872 | tf_op jit(solution)/shard_map/ppermute | solution.py:142
  5.2 1.6 %collective-permute-start = (bf16[128,16,1]{0,2,1:T(2,128)(2,1)S(1)}, bf16[128,16,1]{0,2,1:T(2,128)(2,1)S(1)}, u32[]{:S(2)}, u32[]{:S(2)}) collective-permute-start(bf16[128,16,1]{0,2,1:T(2,128)(2,1)S(1)} %get-tuple-element.56), channel_id=1, source_target_pairs={{0,4},{4,8},{8,12},{12,0},{1,5},{5,9},{9,13},{13,1},{2,6},{6,10},{... | collective-permute-start | bytes 12296 | tf_op jit(solution)/shard_map/ppermute | solution.py:14
  6.8 2.2 %collective-permute-start.1 = (bf16[128,16,1]{0,2,1:T(2,128)(2,1)S(1)}, bf16[128,16,1]{0,2,1:T(2,128)(2,1)S(1)}, u32[]{:S(2)}, u32[]{:S(2)}) collective-permute-start(bf16[128,16,1]{0,2,1:T(2,128)(2,1)S(1)} %get-tuple-element.57), channel_id=1, source_target_pairs={{4,0},{8,4},{12,8},{0,12},{5,1},{9,5},{13,9},{1,13},{6,2},{10,6},{... | collective-permute-start | bytes 12296 | tf_op jit(solution)/shard_map/ppermute | solution.py:15
  9.2 1.5 %collective-permute-done = bf16[128,16,1]{0,2,1:T(2,128)(2,1)S(1)} collective-permute-done((bf16[128,16,1]{0,2,1:T(2,128)(2,1)S(1)}, bf16[128,16,1]{0,2,1:T(2,128)(2,1)S(1)}, u32[]{:S(2)}, u32[]{:S(2)}) %collective-permute-start) | collective-permute-done | bytes 4128 | tf_op jit(solution)/shard_map/ppermute | solution.py:14
  10.8 0.5 collective-permute-start.3
  11.3 0.7 collective-permute-done.2
  12.5 0.9 %fusion.54 = (bf16[128,16,128]{0,2,1:T(8,128)(2,1)S(1)}, bf16[128,16,128]{0,2,1:T(8,128)(2,1)S(1)}, bf16[128,16,128]{0,2,1:T(8,128)(2,1)S(1)}, bf16[128,16,128]{...) fusion(bf16[128,18,130]{0,2,1:T(8,128)(2,1)S(1)} %maximum_selec, ...), kind=kLoop, calls=%fused_computation.202 | loop fusion | bytes 9437184 | tf_op jit(solution)/shard_map/slice | solution.py:37
  13.5 0.5 collective-permute-start.4
  16.7 2.0 %collective-permute-done.4 = bf16[128,292]{0,1:T(8,128)(2,1)S(1)} collective-permute-done((bf16[128,292]{0,1:T(8,128)(2,1)S(1)}, bf16[128,292]{0,1:T(8,128)(2,1)S(1)}, u32[]{:S(2)}, u32[]{:S(2)}) %collective-permute-start.4) | collective-permute-done | bytes 74784 | tf_op jit(solution)/shard_map/ppermute | solution.py:148
  19.0 1.0 %fusion.52 = (bf16[128,16,128]{0,2,1:T(8,128)(2,1)S(1)}, bf16[128,16,128]{0,2,1:T(8,128)(2,1)S(1)}, bf16[128,16,128]{0,2,1:T(8,128)(2,1)S(1)}, bf16[128,16,128]{...) fusion(bf16[128,18,130]{0,2,1:T(8,128)(2,1)S(1)} %pad_maximum_f, ...), kind=kLoop, calls=%fused_computation.200 | loop fusion | bytes 9437184 | tf_op jit(solution)/shard_map/slice | solution.py:37
  19.9 2.5 %fusion.14 = (bf16[256,16,128]{0,2,1:T(8,128)(2,1)S(1)}, bf16[256,16,128]{0,2,1:T(8,128)(2,1)S(1)}, bf16[256,16,128]{0,2,1:T(8,128)(2,1)S(1)}, bf16[256,16,128]{...) fusion(bf16[128,18,130]{0,2,1:T(8,128)(2,1)S(1)} %maximum_selec, ...), kind=kLoop, calls=%fused_computation.81 | loop fusion | flops 18874368 | bytes 10635264 | tf_op jit(solution)/shard_map/concatenate | solution.py:164
  25.3 1.0 %convert_reduce_fusion = (f32[128]{0:T(128)S(1)}, bf16[128,2048]{1,0:T(8,128)(2,1)S(1)}) fusion(f32[128]{0:T(128)S(1)} %copy-done.2, f32[128,2048]{1,0:T(8,128)S(1)} %convolution_add_fusion.24, f32[128,2048]{1,0:T(8,128)S(1)} %convolution_add_fusion.17, bf16[128,2048]{0,1:T(8,128)(2,1)S(1)} %bitcast.351, bf16[3,3,128,256]{3,2,1,0:T(8,128)(2,1)S(1)} %copy-done, ...), kind=kOutput, calls=%fused_computation.90 | convolution fusion | flops 71040896 | bytes 4228104 | tf_op jit(solution)/shard_map/dot_general | solution.py:50
  29.4 0.6 copy.28
  30.5 0.8 %slice_reduce_fusion.1 = (bf16[128,16]{1,0:T(8,128)(2,1)S(1)}, bf16[128,16]{1,0:T(8,128)(2,1)S(1)}) fusion(bf16[128,16,128]{2,1,0:T(8,128)(2,1)S(1)} %bitcast.297), kind=kLoop, calls=%fused_computation.98 | loop fusion | bytes 16384 | tf_op jit(solution)/shard_map/slice | solution.py:179
  31.5 0.9 %collective-permute-done.6 = f32[1216,128]{1,0:T(8,128)} collective-permute-done((f32[1216,128]{1,0:T(8,128)S(1)}, f32[1216,128]{1,0:T(8,128)}, u32[]{:S(2)}, u32[]{:S(2)}) %collective-permute-start.6) | collective-permute-done | bytes 622624 | tf_op jit(solution)/shard_map/ppermute | solution.py:64
  32.4 1.1 %bitcast_add_fusion = f32[1216,128]{1,0:T(8,128)S(1)} fusion(f32[1216,128]{1,0:T(8,128)} %collective-permute-done.6, f32[2,1216,128]{2,1,0:T(8,128)S(1)} %bitcast.300, s32[]{:T(128)S(6)} %select_n.98), kind=kLoop, calls=%fused_computation.94 | loop fusion | flops 155648 | bytes 1867780 | tf_op jit(solution)/shard_map/add | solution.py:64
  33.6 1.9 %collective-permute-start.7 = (bf16[320,128]{1,0:T(8,128)(2,1)S(1)}, bf16[320,128]{1,0:T(8,128)(2,1)S(1)}, u32[]{:S(2)}, u32[]{:S(2)}) collective-permute-start(bf16[320,128]{1,0:T(8,128)(2,1)S(1)} %pad_maximum_fusion.3), channel_id=1, source_target_pairs={{0,4},{4,8},{8,12},{12,0},{1,5},{5,9},{9,13},{13,1},{2,6},{6,10},{... | collective-permute-start | bytes 245768 | tf_op jit(solution)/shard_map/ppermute | solution.py:104
  35.5 2.3 %collective-permute-start.8 = (bf16[320,128]{1,0:T(8,128)(2,1)S(1)}, bf16[320,128]{1,0:T(8,128)(2,1)S(1)}, u32[]{:S(2)}, u32[]{:S(2)}) collective-permute-start(bf16[320,128]{1,0:T(8,128)(2,1)S(1)} %pad_maximum_fusion.4), channel_id=1, source_target_pairs={{0,12},{4,0},{8,4},{12,8},{1,13},{5,1},{9,5},{13,9},{2,14},{6,2},{... | collective-permute-start | bytes 245768 | tf_op jit(solution)/shard_map/ppermute | solution.py:104
  38.4 0.8 %collective-permute-start.12 = (bf16[304,128]{1,0:T(8,128)(2,1)S(1)}, bf16[304,128]{1,0:T(8,128)(2,1)S(1)}, u32[]{:S(2)}, u32[]{:S(2)}) collective-permute-start(bf16[304,128]{1,0:T(8,128)(2,1)S(1)} %get-tuple-element.47), channel_id=1, source_target_pairs={{0,8},{4,12},{8,0},{12,4},{1,9},{5,13},{9,1},{13,5},{2,10},{6,14},... | collective-permute-start | bytes 233480 | tf_op jit(solution)/shard_map/ppermute | solution.py:104
  39.2 1.4 %collective-permute-done.7 = bf16[320,128]{1,0:T(8,128)(2,1)S(1)} collective-permute-done((bf16[320,128]{1,0:T(8,128)(2,1)S(1)}, bf16[320,128]{1,0:T(8,128)(2,1)S(1)}, u32[]{:S(2)}, u32[]{:S(2)}) %collective-permute-start.7) | collective-permute-done | bytes 81952 | tf_op jit(solution)/shard_map/ppermute | solution.py:104
  40.7 0.7 %collective-permute-done.8 = bf16[320,128]{1,0:T(8,128)(2,1)S(1)} collective-permute-done((bf16[320,128]{1,0:T(8,128)(2,1)S(1)}, bf16[320,128]{1,0:T(8,128)(2,1)S(1)}, u32[]{:S(2)}, u32[]{:S(2)}) %collective-permute-start.8) | collective-permute-done | bytes 81952 | tf_op jit(solution)/shard_map/ppermute | solution.py:104
  41.8 0.5 collective-permute-start.9
  42.3 3.1 %collective-permute-done.12 = bf16[304,128]{1,0:T(8,128)(2,1)S(1)} collective-permute-done((bf16[304,128]{1,0:T(8,128)(2,1)S(1)}, bf16[304,128]{1,0:T(8,128)(2,1)S(1)}, u32[]{:S(2)}, u32[]{:S(2)}) %collective-permute-start.12) | collective-permute-done | bytes 77856 | tf_op jit(solution)/shard_map/ppermute | solution.py:104
  45.4 2.1 %collective-permute-start.13 = (bf16[304,128]{1,0:T(8,128)(2,1)S(1)}, bf16[304,128]{1,0:T(8,128)(2,1)S(1)}, u32[]{:S(2)}, u32[]{:S(2)}) collective-permute-start(bf16[304,128]{1,0:T(8,128)(2,1)S(1)} %get-tuple-element.5), channel_id=1, source_target_pairs={{0,12},{4,0},{8,4},{12,8},{1,13},{5,1},{9,5},{13,9},{2,14},{6,2},{... | collective-permute-start | bytes 233480 | tf_op jit(solution)/shard_map/ppermute | solution.py:76
  47.5 0.6 collective-permute-start.15
  48.5 0.9 %fusion.51 = (bf16[128,16,128]{0,2,1:T(8,128)(2,1)S(1)}, bf16[128,16,128]{0,2,1:T(8,128)(2,1)S(1)}, bf16[128,16,128]{0,2,1:T(8,128)(2,1)S(1)}, bf16[128,16,128]{...) fusion(bf16[128,18,130]{0,2,1:T(8,128)(2,1)S(1)} %maximum_selec, ...), kind=kLoop, calls=%fused_computation.199 | loop fusion | bytes 9437184 | tf_op jit(solution)/shard_map/slice | solution.py:37
  54.3 1.6 %collective-permute-start.11 = (bf16[128,2048]{1,0:T(8,128)(2,1)S(1)}, bf16[128,2048]{1,0:T(8,128)(2,1)S(1)}, u32[]{:S(2)}, u32[]{:S(2)}) collective-permute-start(bf16[128,2048]{1,0:T(8,128)(2,1)S(1)} %fusion.2), channel_id=1, source_target_pairs={{0,2},{2,0},{1,3},{3,1},{4,6},{6,4},{5,7},{7,5},{8,10},{10,8},{9,1... | collective-permute-start | bytes 1572872 | tf_op jit(solution)/shard_map/ppermute | solution.py:195
  56.9 10.8 %collective-permute-done.11 = bf16[128,2048]{1,0:T(8,128)(2,1)S(1)} collective-permute-done((bf16[128,2048]{1,0:T(8,128)(2,1)S(1)}, bf16[128,2048]{1,0:T(8,128)(2,1)S(1)}, u32[]{:S(2)}, u32[]{:S(2)}) %collective-permute-start.11) | collective-permute-done | bytes 524320 | tf_op jit(solution)/shard_map/ppermute | solution.py:195
  68.0 0.9 %copy.30 = bf16[16,8,16,128]{3,2,1,0:T(8,128)(2,1)} copy(bf16[16,8,16,128]{3,1,2,0:T(8,128)(2,1)S(1)} %fusion.21) | data formatting | bytes 1048576
  69.3 0.5 slice.466
  70.1 1.2 %fusion.6 = f32[3,3,128,256]{3,2,1,0:T(8,128)} fusion(s32[]{:T(128)S(6)} %select_n.114, f32[3,3,128,256]{3,2,1,0:T(8,128)S(1)} %reshape.214), kind=kLoop, calls=%fused_computation.63 | loop fusion | flops 294912 | bytes 2359300 | tf_op jit(solution)/shard_map/concatenate | solution.py:184
  (113 shorter events, 18.1 us)
Async XLA Ops:
  0.6 8.4 %copy-start.1 = (bf16[128,16,128]{2,1,0:T(8,128)(2,1)S(1)}, bf16[128,16,128]{2,1,0:T(8,128)(2,1)}, u32[]{:S(2)}) copy-start(bf16[128,16,128]{2,1,0:T(8,128)(2,1)} %param.5) | copy-start | bytes 1572868
  2.2 16.6 %collective-permute-start.5 = (bf16[128,16,128]{0,2,1:T(8,128)(2,1)S(1)}, bf16[128,16,128]{0,2,1:T(8,128)(2,1)S(1)}, u32[]{:S(2)}, u32[]{:S(2)}) collective-permute-start(bf16[128,16,128]{0,2,1:T(8,128)(2,1)S(1)} %copy.12), channel_id=1, source_target_pairs={{0,2},{2,0},{1,3},{3,1},{4,6},{6,4},{5,7},{7,5},{8,10},{10,8},{9,1... | collective-permute-start | bytes 1572872 | tf_op jit(solution)/shard_map/ppermute | solution.py:142
  5.2 5.5 %collective-permute-start = (bf16[128,16,1]{0,2,1:T(2,128)(2,1)S(1)}, bf16[128,16,1]{0,2,1:T(2,128)(2,1)S(1)}, u32[]{:S(2)}, u32[]{:S(2)}) collective-permute-start(bf16[128,16,1]{0,2,1:T(2,128)(2,1)S(1)} %get-tuple-element.56), channel_id=1, source_target_pairs={{0,4},{4,8},{8,12},{12,0},{1,5},{5,9},{9,13},{13,1},{2,6},{6,10},{... | collective-permute-start | bytes 12296 | tf_op jit(solution)/shard_map/ppermute | solution.py:14
  6.8 3.9 %collective-permute-start.1 = (bf16[128,16,1]{0,2,1:T(2,128)(2,1)S(1)}, bf16[128,16,1]{0,2,1:T(2,128)(2,1)S(1)}, u32[]{:S(2)}, u32[]{:S(2)}) collective-permute-start(bf16[128,16,1]{0,2,1:T(2,128)(2,1)S(1)} %get-tuple-element.57), channel_id=1, source_target_pairs={{4,0},{8,4},{12,8},{0,12},{5,1},{9,5},{13,9},{1,13},{6,2},{10,6},{... | collective-permute-start | bytes 12296 | tf_op jit(solution)/shard_map/ppermute | solution.py:15
  10.7 1.3 %collective-permute-start.2 = (bf16[128,1,130]{0,2,1:T(8,128)(2,1)S(1)}, bf16[128,1,130]{0,2,1:T(8,128)(2,1)S(1)}, u32[]{:S(2)}, u32[]{:S(2)}) collective-permute-start(bf16[128,1,130]{0,2,1:T(8,128)(2,1)S(1)} %get-tuple-element.54), channel_id=1, source_target_pairs={{0,1},{1,0},{2,3},{3,2},{4,5},{5,4},{6,7},{7,6},{8,9},{9,8},{10,11... | collective-permute-start | bytes 99848 | tf_op jit(solution)/shard_map/ppermute | solution.py:14
  10.8 1.4 %collective-permute-start.3 = (bf16[128,1,130]{0,2,1:T(8,128)(2,1)S(1)}, bf16[128,1,130]{0,2,1:T(8,128)(2,1)S(1)}, u32[]{:S(2)}, u32[]{:S(2)}) collective-permute-start(bf16[128,1,130]{0,2,1:T(8,128)(2,1)S(1)} %get-tuple-element.55), channel_id=1, source_target_pairs={{1,0},{0,1},{3,2},{2,3},{5,4},{4,5},{7,6},{6,7},{9,8},{8,9},{11,10... | collective-permute-start | bytes 99848 | tf_op jit(solution)/shard_map/ppermute | solution.py:15
  12.5 1.5 %copy-start = (bf16[3,3,128,256]{3,2,1,0:T(8,128)(2,1)S(1)}, bf16[3,3,128,256]{3,2,1,0:T(8,128)(2,1)}, u32[]{:S(2)}) copy-start(bf16[3,3,128,256]{3,2,1,0:T(8,128)(2,1)} %param.6) | copy-start | bytes 1769476
  13.5 5.2 %collective-permute-start.4 = (bf16[128,292]{0,1:T(8,128)(2,1)S(1)}, bf16[128,292]{0,1:T(8,128)(2,1)S(1)}, u32[]{:S(2)}, u32[]{:S(2)}) collective-permute-start(bf16[128,292]{0,1:T(8,128)(2,1)S(1)} %pad_maximum_fusion.5), channel_id=1, source_target_pairs={{0,2},{2,0},{1,3},{3,1},{4,6},{6,4},{5,7},{7,5},{8,10},{10,8},{9,1... | collective-permute-start | bytes 224264 | tf_op jit(solution)/shard_map/ppermute | solution.py:148
  24.6 0.7 copy-start.2
  30.2 2.2 %collective-permute-start.6 = (f32[1216,128]{1,0:T(8,128)S(1)}, f32[1216,128]{1,0:T(8,128)}, u32[]{:S(2)}, u32[]{:S(2)}) collective-permute-start(f32[1216,128]{1,0:T(8,128)S(1)} %dynamic-slice_bitcast_fusion), channel_id=1, source_target_pairs={{0,1},{1,0},{2,3},{3,2},{4,5},{5,4},{6,7},{7,6},{8,9},{9,8},{10,11... | collective-permute-start | bytes 1867784 | tf_op jit(solution)/shard_map/ppermute | solution.py:64
  33.6 7.0 %collective-permute-start.7 = (bf16[320,128]{1,0:T(8,128)(2,1)S(1)}, bf16[320,128]{1,0:T(8,128)(2,1)S(1)}, u32[]{:S(2)}, u32[]{:S(2)}) collective-permute-start(bf16[320,128]{1,0:T(8,128)(2,1)S(1)} %pad_maximum_fusion.3), channel_id=1, source_target_pairs={{0,4},{4,8},{8,12},{12,0},{1,5},{5,9},{9,13},{13,1},{2,6},{6,10},{... | collective-permute-start | bytes 245768 | tf_op jit(solution)/shard_map/ppermute | solution.py:104
  35.5 6.0 %collective-permute-start.8 = (bf16[320,128]{1,0:T(8,128)(2,1)S(1)}, bf16[320,128]{1,0:T(8,128)(2,1)S(1)}, u32[]{:S(2)}, u32[]{:S(2)}) collective-permute-start(bf16[320,128]{1,0:T(8,128)(2,1)S(1)} %pad_maximum_fusion.4), channel_id=1, source_target_pairs={{0,12},{4,0},{8,4},{12,8},{1,13},{5,1},{9,5},{13,9},{2,14},{6,2},{... | collective-permute-start | bytes 245768 | tf_op jit(solution)/shard_map/ppermute | solution.py:104
  38.4 7.0 %collective-permute-start.12 = (bf16[304,128]{1,0:T(8,128)(2,1)S(1)}, bf16[304,128]{1,0:T(8,128)(2,1)S(1)}, u32[]{:S(2)}, u32[]{:S(2)}) collective-permute-start(bf16[304,128]{1,0:T(8,128)(2,1)S(1)} %get-tuple-element.47), channel_id=1, source_target_pairs={{0,8},{4,12},{8,0},{12,4},{1,9},{5,13},{9,1},{13,5},{2,10},{6,14},... | collective-permute-start | bytes 233480 | tf_op jit(solution)/shard_map/ppermute | solution.py:104
  41.7 6.5 %collective-permute-start.10 = (bf16[128,1,130]{0,2,1:T(8,128)(2,1)S(1)}, bf16[128,1,130]{0,2,1:T(8,128)(2,1)S(1)}, u32[]{:S(2)}, u32[]{:S(2)}) collective-permute-start(bf16[128,1,130]{0,2,1:T(8,128)(2,1)S(1)} %get-tuple-element.53), channel_id=1, source_target_pairs={{1,0},{0,1},{3,2},{2,3},{5,4},{4,5},{7,6},{6,7},{9,8},{8,9},{11,10... | collective-permute-start | bytes 99848 | tf_op jit(solution)/shard_map/ppermute | solution.py:15
  41.8 6.4 %collective-permute-start.9 = (bf16[128,1,130]{0,2,1:T(8,128)(2,1)S(1)}, bf16[128,1,130]{0,2,1:T(8,128)(2,1)S(1)}, u32[]{:S(2)}, u32[]{:S(2)}) collective-permute-start(bf16[128,1,130]{0,2,1:T(8,128)(2,1)S(1)} %get-tuple-element.52), channel_id=1, source_target_pairs={{0,1},{1,0},{2,3},{3,2},{4,5},{5,4},{6,7},{7,6},{8,9},{9,8},{10,11... | collective-permute-start | bytes 99848 | tf_op jit(solution)/shard_map/ppermute | solution.py:14
  45.4 10.5 %collective-permute-start.13 = (bf16[304,128]{1,0:T(8,128)(2,1)S(1)}, bf16[304,128]{1,0:T(8,128)(2,1)S(1)}, u32[]{:S(2)}, u32[]{:S(2)}) collective-permute-start(bf16[304,128]{1,0:T(8,128)(2,1)S(1)} %get-tuple-element.5), channel_id=1, source_target_pairs={{0,12},{4,0},{8,4},{12,8},{1,13},{5,1},{9,5},{13,9},{2,14},{6,2},{... | collective-permute-start | bytes 233480 | tf_op jit(solution)/shard_map/ppermute | solution.py:76
  47.5 8.4 %collective-permute-start.14 = (bf16[304,128]{1,0:T(8,128)(2,1)S(1)}, bf16[304,128]{1,0:T(8,128)(2,1)S(1)}, u32[]{:S(2)}, u32[]{:S(2)}) collective-permute-start(bf16[304,128]{1,0:T(8,128)(2,1)S(1)} %get-tuple-element.5), channel_id=1, source_target_pairs={{0,8},{4,12},{8,0},{12,4},{1,9},{5,13},{9,1},{13,5},{2,10},{6,14},... | collective-permute-start | bytes 233480 | tf_op jit(solution)/shard_map/ppermute | solution.py:76
  47.5 8.4 %collective-permute-start.15 = (bf16[304,128]{1,0:T(8,128)(2,1)S(1)}, bf16[304,128]{1,0:T(8,128)(2,1)S(1)}, u32[]{:S(2)}, u32[]{:S(2)}) collective-permute-start(bf16[304,128]{1,0:T(8,128)(2,1)S(1)} %get-tuple-element.5), channel_id=1, source_target_pairs={{0,4},{4,8},{8,12},{12,0},{1,5},{5,9},{9,13},{13,1},{2,6},{6,10},{... | collective-permute-start | bytes 233480 | tf_op jit(solution)/shard_map/ppermute | solution.py:76
  54.3 13.3 %collective-permute-start.11 = (bf16[128,2048]{1,0:T(8,128)(2,1)S(1)}, bf16[128,2048]{1,0:T(8,128)(2,1)S(1)}, u32[]{:S(2)}, u32[]{:S(2)}) collective-permute-start(bf16[128,2048]{1,0:T(8,128)(2,1)S(1)} %fusion.2), channel_id=1, source_target_pairs={{0,2},{2,0},{1,3},{3,1},{4,6},{6,4},{5,7},{7,5},{8,10},{10,8},{9,1... | collective-permute-start | bytes 1572872 | tf_op jit(solution)/shard_map/ppermute | solution.py:195
  56.1 12.8 %collective-permute-start.16 = (f32[1216,128]{1,0:T(8,128)S(1)}, f32[1216,128]{1,0:T(8,128)S(1)}, u32[]{:S(2)}, u32[]{:S(2)}) collective-permute-start(f32[1216,128]{1,0:T(8,128)S(1)} %bitcast.332), channel_id=1, source_target_pairs={{0,1},{1,0},{2,3},{3,2},{4,5},{5,4},{6,7},{7,6},{8,9},{9,8},{10,11... | collective-permute-start | bytes 1867784 | tf_op jit(solution)/shard_map/ppermute | solution.py:76

commit v12 on v11

--- a/solution.py
+++ b/solution.py
@@ -153,6 +153,15 @@
         kernel_cols.append(
             lax.dynamic_slice_in_dim(weight, source * own_channels, own_channels, axis=3)
         )
+    kernel_sends = []
+    for shift in range(1, chan_count):
+        target = (chan_index + shift) % chan_count
+        kernel_sends.append(lax.dynamic_slice_in_dim(weight, target * own_channels, own_channels, axis=3))
+    kernel_sends, _ = lax.optimization_barrier((kernel_sends, raw_blocks))
+    kernel_blocks = []
+    for shift in range(1, chan_count):
+        pairs = [(i, (i + shift) % chan_count) for i in range(chan_count)]
+        kernel_blocks.append(lax.ppermute(kernel_sends[shift - 1], "chan", pairs))
     preact = None
     for shift in range(chan_count):
         part = conv_taps(kernel_cols[shift], blocks[shift], row_count, column_count, False)
@@ -160,6 +169,7 @@
     preact = preact + bias_vector[:, None]
     upstream = cotangent.reshape(own_channels, -1).astype(jnp.float32)
     grad_pre = (upstream * gelu_slope(preact)).astype(jnp.bfloat16)
+    grad_pre, kernel_blocks = lax.optimization_barrier((grad_pre, kernel_blocks))
     bias_part = jnp.sum(grad_pre.astype(jnp.float32), axis=1)
     input_local = jnp.concatenate(blocks, axis=0)
     taps = []
@@ -178,6 +188,11 @@
     grad_field = grad_pre.reshape(own_channels, row_count, column_count)
     edges = (grad_field[:, :, column_count - 1 :], grad_field[:, :, :1])
     scattered, (before, after) = sum_start(flat, jnp.bfloat16, edges)
+    grad_blocks = []
+    for shift in range(1, chan_count):
+        pairs = [(i, (i + shift) % chan_count) for i in range(chan_count)]
+        grad_blocks.append(lax.ppermute(grad_field, "chan", pairs))
+    scattered, grad_blocks = lax.optimization_barrier((scattered, grad_blocks))
     flat = sum_finish(scattered, flat.size, jnp.bfloat16)
     weight_local = flat[: weight_part.size].reshape(weight_part.shape)
     bias_grad = flat[weight_part.size :]
@@ -187,16 +202,15 @@
     )
     grad_wide = jnp.concatenate([before, grad_field, after], axis=2)
     grad_pad = mask_rims(padded_2(grad_wide, (("lat", 1),), 1))
-    received = []
-    for shift in range(1, chan_count):
-        kernel_t = jnp.swapaxes(kernel_cols[shift], 2, 3)
-        part = conv_taps(kernel_t, grad_pad, row_count, column_count, True)
+    grad_border = border_of(grad_pad)
+    input_sum = conv_taps(jnp.swapaxes(kernel_cols[0], 2, 3), grad_pad, row_count, column_count, True)
+    for shift in range(1, chan_count):
         pairs = [(i, (i + shift) % chan_count) for i in range(chan_count)]
-        received.append(lax.ppermute(part.astype(jnp.bfloat16), "chan", pairs))
-    own_part = conv_taps(jnp.swapaxes(kernel_cols[0], 2, 3), grad_pad, row_count, column_count, True)
-    for piece in received:
-        own_part = own_part + piece.astype(jnp.float32)
-    input_grad = own_part.astype(jnp.bfloat16).reshape(own_channels, row_count, column_count)
+        border = lax.ppermute(grad_border, "chan", pairs)
+        block = lax.optimization_barrier(with_border(grad_blocks[shift - 1], border))
+        kernel_t = jnp.swapaxes(kernel_blocks[shift - 1], 2, 3)
+        input_sum = input_sum + conv_taps(kernel_t, block, row_count, column_count, True)
+    input_grad = input_sum.astype(jnp.bfloat16).reshape(own_channels, row_count, column_count)
     return (input_grad, weight_grad, bias_grad)
 
 

time: 71.5 us -> 71.6 us (level)
  waiting for transfers between devices: 21.3 us -> 14.6 us
  starting transfers between devices: 17.9 us -> 22.3 us
  other arithmetic: 6.5 us -> 8.08 us
  local copies, waits for them, and re-layouts: 9.36 us -> 10.2 us
    ppermute x1 -> x3, waiting for transfers between devices: 10.8 us -> 3.65 us  [the longest x1 3.36 us: local(): kernel_blocks.append(lax.ppermute(kernel_sends[shift - 1], 'chan', pairs))]
    ppermute x1 -> x3, starting transfers between devices: 1.55 us -> 4.44 us  [the longest x1 1.81 us: local(): kernel_blocks.append(lax.ppermute(kernel_sends[shift - 1], 'chan', pairs))]
    ppermute x4, starting transfers between devices: 2.81 us -> 4.61 us  [direct_all_gather(): pieces.append(lax.ppermute(sent, axis, pairs).astype(jnp.float32))]
    concatenate x1 -> x2, other arithmetic: 0.18 us -> 1.4 us  [with_border(): jnp.concatenate([top[:, None, :], middle, bottom[:, None, :]], axis=1)]
    ppermute x1, waiting for transfers between devices: 0.94 us -> 0.01 us  [direct_reduce_scatter(): lax.ppermute(piece.astype(send_dtype), axis, pairs).astype(jnp.float32)]
    ppermute x4, waiting for transfers between devices: 0.01 us -> 0.85 us  [direct_all_gather(): pieces.append(lax.ppermute(sent, axis, pairs).astype(jnp.float32))]
    slice x3 -> x4, local copies, waits for them, and re-layouts: 2.81 us -> 3.49 us  [window_of(): field[:, first_row:first_row + row_count, first_col:first_col + column_co...]
    unnamed x12 -> x18, local copies, waits for them, and re-layouts: 3.51 us -> 3.57 us
  transfers between devices with their start and end apart: 17 -> 19, of which waited for: 9 -> 10; matrix products, arithmetic and copies ran while one was open for 20% -> 27% of each run, Pallas kernels for 0% -> 0%
where the time goes in v12:
time: 71.6 us; the launch traced here: 71.3 us
  starting transfers between devices  22.3 us (31%)
  waiting for transfers between devices  14.6 us (20%)
  matrix products  14.6 us (20%)
  local copies, waits for them, and re-layouts  10.2 us (14%)
  other arithmetic  8.08 us (11%)
  between operations  1.51 us (2%)
    dot_general x36, matrix products, conv_taps(): jnp.dot(kernel[tap_row, tap_col], window, preferred_element_type=jnp.floa...  11.8 us
    ppermute x3, waiting for transfers between devices, sum_start(): moved = lax.ppermute(piece, 'lon', pairs)  5.89 us
    ppermute x3, starting transfers between devices, sum_start(): moved = lax.ppermute(piece, 'lon', pairs)  4.67 us
    ppermute x4, starting transfers between devices, direct_all_gather(): pieces.append(lax.ppermute(sent, axis, pairs).astype(jnp.float32))  4.61 us
    unnamed x18, local copies, waits for them, and re-layouts  3.57 us
    slice x4, local copies, waits for them, and re-layouts, window_of(): field[:, first_row:first_row + row_count, first_col:first_col + column_co...  3.49 us
    ppermute x1, waiting for transfers between devices, local(): kernel_blocks.append(lax.ppermute(kernel_sends[shift - 1], 'chan', pairs))  3.36 us
    ppermute x3, starting transfers between devices, padded_2(): after = lax.ppermute(initial, axis, down)  3.24 us
  transfers between devices with their start and end apart: 19, of which 10 were waited for; matrix products, arithmetic and copies ran while one was open for 27% of the time, Pallas kernels for 0%

profile of v12, /device:TPU:0, one launch (start us, length us, event | category | flops | bytes accessed | tf_op | source)
XLA Modules:
  0.0 71.3 jit_solution(18382059838019480765)
XLA Ops:
  0.7 1.6 %copy.32 = bf16[128,16,128]{0,2,1:T(8,128)(2,1)S(1)} copy(bf16[128,16,128]{2,1,0:T(8,128)(2,1)} %param.4) | data formatting | bytes 1048576 | tf_op args[0]
  2.2 3.0 %collective-permute-start.5 = (bf16[128,16,128]{0,2,1:T(8,128)(2,1)S(1)}, bf16[128,16,128]{0,2,1:T(8,128)(2,1)}, u32[]{:S(2)}, u32[]{:S(2)}) collective-permute-start(bf16[128,16,128]{0,2,1:T(8,128)(2,1)S(1)} %copy.32), channel_id=1, source_target_pairs={{0,2},{2,0},{1,3},{3,1},{4,6},{6,4},{5,7},{7,5},{8,10},{10,8},{9,1... | collective-permute-start | bytes 1572872 | tf_op jit(solution)/shard_map/ppermute | solution.py:142
  5.2 1.6 %collective-permute-start = (bf16[128,16,1]{0,2,1:T(2,128)(2,1)S(1)}, bf16[128,16,1]{0,2,1:T(2,128)(2,1)S(1)}, u32[]{:S(2)}, u32[]{:S(2)}) collective-permute-start(bf16[128,16,1]{0,2,1:T(2,128)(2,1)S(1)} %get-tuple-element.77), channel_id=1, source_target_pairs={{0,4},{4,8},{8,12},{12,0},{1,5},{5,9},{9,13},{13,1},{2,6},{6,10},{... | collective-permute-start | bytes 12296 | tf_op jit(solution)/shard_map/ppermute | solution.py:14
  6.9 2.2 %collective-permute-start.1 = (bf16[128,16,1]{0,2,1:T(2,128)(2,1)S(1)}, bf16[128,16,1]{0,2,1:T(2,128)(2,1)S(1)}, u32[]{:S(2)}, u32[]{:S(2)}) collective-permute-start(bf16[128,16,1]{0,2,1:T(2,128)(2,1)S(1)} %get-tuple-element.78), channel_id=1, source_target_pairs={{4,0},{8,4},{12,8},{0,12},{5,1},{9,5},{13,9},{1,13},{6,2},{10,6},{... | collective-permute-start | bytes 12296 | tf_op jit(solution)/shard_map/ppermute | solution.py:15
  9.2 1.5 %collective-permute-done = bf16[128,16,1]{0,2,1:T(2,128)(2,1)S(1)} collective-permute-done((bf16[128,16,1]{0,2,1:T(2,128)(2,1)S(1)}, bf16[128,16,1]{0,2,1:T(2,128)(2,1)S(1)}, u32[]{:S(2)}, u32[]{:S(2)}) %collective-permute-start) | collective-permute-done | bytes 4128 | tf_op jit(solution)/shard_map/ppermute | solution.py:14
  11.5 0.6 collective-permute-done.2
  12.6 0.9 %fusion.55 = (bf16[128,16,128]{0,2,1:T(8,128)(2,1)S(1)}, bf16[128,16,128]{0,2,1:T(8,128)(2,1)S(1)}, bf16[128,16,128]{0,2,1:T(8,128)(2,1)S(1)}, bf16[128,16,128]{...) fusion(bf16[128,18,130]{0,2,1:T(8,128)(2,1)S(1)} %maximum_selec, ...), kind=kLoop, calls=%fused_computation.213 | loop fusion | bytes 9437184 | tf_op jit(solution)/shard_map/slice | solution.py:37
  16.8 2.0 %collective-permute-done.4 = bf16[128,292]{0,1:T(8,128)(2,1)S(1)} collective-permute-done((bf16[128,292]{0,1:T(8,128)(2,1)S(1)}, bf16[128,292]{0,1:T(8,128)(2,1)S(1)}, u32[]{:S(2)}, u32[]{:S(2)}) %collective-permute-start.4) | collective-permute-done | bytes 74784 | tf_op jit(solution)/shard_map/ppermute | solution.py:148
  18.8 1.2 %pad_maximum_fusion.2 = bf16[128,18,130]{0,2,1:T(8,128)(2,1)S(1)} fusion(bf16[128,1,130]{0,2,1:T(8,128)(2,1)S(1)} %get-tuple-element.84, bf16[128,16,1]{0,2,1:T(2,128)(2,1)S(1)} %copy.37, bf16[128,16,128]{0,2,1:T(8,128)(2,1)} %collective-permute-done.5, bf16[128,16,1]{0,2,1:T(2,128)(2,1)S(1)} %copy.36, bf16[128,1,130]{0,2,1:T(8,128)(2,1)S(1)} %get-tuple-element.83), kind=kLoop, calls=%fused_computation.93 | loop fusion | flops 2995200 | bytes 1198080 | tf_op jit(solution)/shard_map/concatenate | solution.py:132
  20.0 0.9 %fusion.53 = (bf16[128,16,128]{0,2,1:T(8,128)(2,1)S(1)}, bf16[128,16,128]{0,2,1:T(8,128)(2,1)S(1)}, bf16[128,16,128]{0,2,1:T(8,128)(2,1)S(1)}, bf16[128,16,128]{...) fusion(bf16[128,18,130]{0,2,1:T(8,128)(2,1)S(1)} %pad_maximum_f, ...), kind=kLoop, calls=%fused_computation.211 | loop fusion | bytes 9437184 | tf_op jit(solution)/shard_map/slice | solution.py:37
  21.0 2.7 %fusion.16 = (bf16[256,16,128]{0,2,1:T(8,128)(2,1)S(1)}, bf16[256,16,128]{0,2,1:T(8,128)(2,1)S(1)}, bf16[256,16,128]{0,2,1:T(8,128)(2,1)S(1)}, bf16[256,16,128]{...) fusion(bf16[128,18,130]{0,2,1:T(8,128)(2,1)S(1)} %maximum_selec, ...), kind=kLoop, calls=%fused_computation.83 | loop fusion | flops 18874368 | bytes 10635264 | tf_op jit(solution)/shard_map/concatenate | solution.py:174
  24.0 1.8 %collective-permute-start.6 = (bf16[3,3,128,128]{3,2,1,0:T(8,128)(2,1)S(1)}, bf16[3,3,128,128]{3,2,1,0:T(8,128)(2,1)S(1)}, u32[]{:S(2)}, u32[]{:S(2)}) collective-permute-start(bf16[3,3,128,128]{3,2,1,0:T(8,128)(2,1)S(1)} %get-tuple-element.8), channel_id=1, source_target_pairs={{0,2},{2,0},{1,3},{3,1},{4,6},{6,4},{5,7},{7,5},{8,10},{10,8},{9,1... | collective-permute-start | bytes 884744 | tf_op jit(solution)/shard_map/ppermute | solution.py:164
  28.3 0.9 %fusion.14 = bf16[128,2048]{1,0:T(8,128)(2,1)S(1)} fusion(f32[16,8,16,128]{3,2,1,0:T(8,128)S(1)} %convert.13, f32[128,2048]{1,0:T(8,128)S(1)} %convolution_add_fusion.24, f32[128,2048]{1,0:T(8,128)S(1)} %convolution_add_fusion.17, bf16[128,2048]{0,1:T(8,128)(2,1)S(1)} %bitcast.336, f32[128]{0:T(128)S(1)} %copy-done.4, ...), kind=kOutput, calls=%fused_computation.81 | convolution fusion | flops 70516736 | bytes 4227592 | tf_op jit(solution)/shard_map/dot_general | solution.py:50
  29.2 3.4 %collective-permute-done.6 = bf16[3,3,128,128]{3,2,1,0:T(8,128)(2,1)S(1)} collective-permute-done((bf16[3,3,128,128]{3,2,1,0:T(8,128)(2,1)S(1)}, bf16[3,3,128,128]{3,2,1,0:T(8,128)(2,1)S(1)}, u32[]{:S(2)}, u32[]{:S(2)}) %collective-permute-start.6) | collective-permute-done | bytes 294944 | tf_op jit(solution)/shard_map/ppermute | solution.py:164
  35.9 0.6 copy.53
  37.3 0.8 %slice_reduce_fusion.1 = (bf16[128,16]{1,0:T(8,128)(2,1)S(1)}, bf16[128,16]{1,0:T(8,128)(2,1)S(1)}) fusion(bf16[128,16,128]{2,1,0:T(8,128)(2,1)S(1)} %bitcast.318), kind=kLoop, calls=%fused_computation.99 | loop fusion | bytes 16384 | tf_op jit(solution)/shard_map/slice | solution.py:189
  38.3 1.2 %collective-permute-start.14 = (bf16[128,16,128]{0,2,1:T(8,128)(2,1)S(1)}, bf16[128,16,128]{0,2,1:T(8,128)(2,1)S(1)}, u32[]{:S(2)}, u32[]{:S(2)}) collective-permute-start(bf16[128,16,128]{0,2,1:T(8,128)(2,1)S(1)} %copy.41), channel_id=1, source_target_pairs={{0,2},{2,0},{1,3},{3,1},{4,6},{6,4},{5,7},{7,5},{8,10},{10,8},{9,1... | collective-permute-start | bytes 1572872 | tf_op jit(solution)/shard_map/ppermute | solution.py:194
  39.6 1.1 %bitcast_add_fusion = f32[1216,128]{1,0:T(8,128)S(1)} fusion(f32[1216,128]{1,0:T(8,128)} %collective-permute-done.7, f32[2,1216,128]{2,1,0:T(8,128)S(1)} %bitcast.320, s32[]{:T(128)S(6)} %select_n.101), kind=kLoop, calls=%fused_computation.96 | loop fusion | flops 155648 | bytes 1867780 | tf_op jit(solution)/shard_map/add | solution.py:64
  40.8 1.6 %collective-permute-start.8 = (bf16[320,128]{1,0:T(8,128)(2,1)S(1)}, bf16[320,128]{1,0:T(8,128)(2,1)S(1)}, u32[]{:S(2)}, u32[]{:S(2)}) collective-permute-start(bf16[320,128]{1,0:T(8,128)(2,1)S(1)} %pad_maximum_fusion.4), channel_id=1, source_target_pairs={{0,4},{4,8},{8,12},{12,0},{1,5},{5,9},{9,13},{13,1},{2,6},{6,10},{... | collective-permute-start | bytes 245768 | tf_op jit(solution)/shard_map/ppermute | solution.py:104
  42.4 2.2 %collective-permute-start.9 = (bf16[320,128]{1,0:T(8,128)(2,1)S(1)}, bf16[320,128]{1,0:T(8,128)(2,1)S(1)}, u32[]{:S(2)}, u32[]{:S(2)}) collective-permute-start(bf16[320,128]{1,0:T(8,128)(2,1)S(1)} %pad_maximum_fusion.5), channel_id=1, source_target_pairs={{0,12},{4,0},{8,4},{12,8},{1,13},{5,1},{9,5},{13,9},{2,14},{6,2},{... | collective-permute-start | bytes 245768 | tf_op jit(solution)/shard_map/ppermute | solution.py:104
  44.7 0.8 %collective-permute-start.13 = (bf16[304,128]{1,0:T(8,128)(2,1)S(1)}, bf16[304,128]{1,0:T(8,128)(2,1)S(1)}, u32[]{:S(2)}, u32[]{:S(2)}) collective-permute-start(bf16[304,128]{1,0:T(8,128)(2,1)S(1)} %get-tuple-element.68), channel_id=1, source_target_pairs={{0,8},{4,12},{8,0},{12,4},{1,9},{5,13},{9,1},{13,5},{2,10},{6,14},... | collective-permute-start | bytes 233480 | tf_op jit(solution)/shard_map/ppermute | solution.py:104
  45.5 2.1 %collective-permute-done.8 = bf16[320,128]{1,0:T(8,128)(2,1)S(1)} collective-permute-done((bf16[320,128]{1,0:T(8,128)(2,1)S(1)}, bf16[320,128]{1,0:T(8,128)(2,1)S(1)}, u32[]{:S(2)}, u32[]{:S(2)}) %collective-permute-start.8) | collective-permute-done | bytes 81952 | tf_op jit(solution)/shard_map/ppermute | solution.py:104
  47.7 0.7 collective-permute-done.9
  49.2 3.1 %collective-permute-done.13 = bf16[304,128]{1,0:T(8,128)(2,1)S(1)} collective-permute-done((bf16[304,128]{1,0:T(8,128)(2,1)S(1)}, bf16[304,128]{1,0:T(8,128)(2,1)S(1)}, u32[]{:S(2)}, u32[]{:S(2)}) %collective-permute-start.13) | collective-permute-done | bytes 77856 | tf_op jit(solution)/shard_map/ppermute | solution.py:104
  52.6 3.9 %collective-permute-start.15 = (bf16[304,128]{1,0:T(8,128)(2,1)S(1)}, bf16[304,128]{1,0:T(8,128)(2,1)S(1)}, u32[]{:S(2)}, u32[]{:S(2)}) collective-permute-start(bf16[304,128]{1,0:T(8,128)(2,1)S(1)} %convert_element_type.64), channel_id=1, source_target_pairs={{0,12},{4,0},{8,4},{12,8},{1,13},{5,1},{9,5},{13,9},{2,14},{6,2},{... | collective-permute-start | bytes 233480 | tf_op jit(solution)/shard_map/ppermute | solution.py:76
  56.5 0.7 collective-permute-start.17
  57.6 0.7 fusion.52
  58.3 1.4 %collective-permute-start.12 = (bf16[128,292]{0,1:T(8,128)(2,1)S(1)}, bf16[128,292]{0,1:T(8,128)(2,1)S(1)}, u32[]{:S(2)}, u32[]{:S(2)}) collective-permute-start(bf16[128,292]{0,1:T(8,128)(2,1)S(1)} %pad_maximum_fusion.7), channel_id=1, source_target_pairs={{0,2},{2,0},{1,3},{3,1},{4,6},{6,4},{5,7},{7,5},{8,10},{10,8},{9,1... | collective-permute-start | bytes 224264 | tf_op jit(solution)/shard_map/ppermute | solution.py:209
  62.7 0.8 %collective-permute-done.16 = bf16[304,128]{1,0:T(8,128)(2,1)S(1)} collective-permute-done((bf16[304,128]{1,0:T(8,128)(2,1)S(1)}, bf16[304,128]{1,0:T(8,128)(2,1)S(1)}, u32[]{:S(2)}, u32[]{:S(2)}) %collective-permute-start.16) | collective-permute-done | bytes 77856 | tf_op jit(solution)/shard_map/ppermute | solution.py:76
  64.1 0.9 %fusion.50 = (bf16[128,16,128]{0,2,1:T(8,128)(2,1)S(1)}, bf16[128,16,128]{0,2,1:T(8,128)(2,1)S(1)}, bf16[128,16,128]{0,2,1:T(8,128)(2,1)S(1)}, bf16[128,16,128]{...) fusion(bf16[128,18,130]{0,2,1:T(8,128)(2,1)S(1)} %pad_maximum_f, ...), kind=kLoop, calls=%fused_computation.208 | loop fusion | bytes 9437184 | tf_op jit(solution)/shard_map/slice | solution.py:37
  68.0 0.9 %copy.55 = bf16[16,8,16,128]{3,2,1,0:T(8,128)(2,1)} copy(bf16[16,8,16,128]{3,1,2,0:T(8,128)(2,1)S(1)} %fusion.7) | data formatting | bytes 1048576
  70.1 1.2 %fusion.8 = f32[3,3,128,256]{3,2,1,0:T(8,128)} fusion(s32[]{:T(128)S(6)} %select_n.117, f32[3,3,128,256]{3,2,1,0:T(8,128)S(1)} %reshape.241), kind=kLoop, calls=%fused_computation.65 | loop fusion | flops 294912 | bytes 2359300 | tf_op jit(solution)/shard_map/concatenate | solution.py:199
  (134 shorter events, 20.6 us)
Async XLA Ops:
  0.6 8.5 %copy-start = (bf16[3,3,128,256]{3,2,1,0:T(8,128)(2,1)S(1)}, bf16[3,3,128,256]{3,2,1,0:T(8,128)(2,1)}, u32[]{:S(2)}) copy-start(bf16[3,3,128,256]{3,2,1,0:T(8,128)(2,1)} %param.6) | copy-start | bytes 1769476
  0.6 10.7 %copy-start.1 = (bf16[128,16,128]{2,1,0:T(8,128)(2,1)S(1)}, bf16[128,16,128]{2,1,0:T(8,128)(2,1)}, u32[]{:S(2)}) copy-start(bf16[128,16,128]{2,1,0:T(8,128)(2,1)} %param.5) | copy-start | bytes 1572868
  2.2 16.6 %collective-permute-start.5 = (bf16[128,16,128]{0,2,1:T(8,128)(2,1)S(1)}, bf16[128,16,128]{0,2,1:T(8,128)(2,1)}, u32[]{:S(2)}, u32[]{:S(2)}) collective-permute-start(bf16[128,16,128]{0,2,1:T(8,128)(2,1)S(1)} %copy.32), channel_id=1, source_target_pairs={{0,2},{2,0},{1,3},{3,1},{4,6},{6,4},{5,7},{7,5},{8,10},{10,8},{9,1... | collective-permute-start | bytes 1572872 | tf_op jit(solution)/shard_map/ppermute | solution.py:142
  5.2 5.5 %collective-permute-start = (bf16[128,16,1]{0,2,1:T(2,128)(2,1)S(1)}, bf16[128,16,1]{0,2,1:T(2,128)(2,1)S(1)}, u32[]{:S(2)}, u32[]{:S(2)}) collective-permute-start(bf16[128,16,1]{0,2,1:T(2,128)(2,1)S(1)} %get-tuple-element.77), channel_id=1, source_target_pairs={{0,4},{4,8},{8,12},{12,0},{1,5},{5,9},{9,13},{13,1},{2,6},{6,10},{... | collective-permute-start | bytes 12296 | tf_op jit(solution)/shard_map/ppermute | solution.py:14
  6.9 3.9 %collective-permute-start.1 = (bf16[128,16,1]{0,2,1:T(2,128)(2,1)S(1)}, bf16[128,16,1]{0,2,1:T(2,128)(2,1)S(1)}, u32[]{:S(2)}, u32[]{:S(2)}) collective-permute-start(bf16[128,16,1]{0,2,1:T(2,128)(2,1)S(1)} %get-tuple-element.78), channel_id=1, source_target_pairs={{4,0},{8,4},{12,8},{0,12},{5,1},{9,5},{13,9},{1,13},{6,2},{10,6},{... | collective-permute-start | bytes 12296 | tf_op jit(solution)/shard_map/ppermute | solution.py:15
  10.8 1.3 %collective-permute-start.2 = (bf16[128,1,130]{0,2,1:T(8,128)(2,1)S(1)}, bf16[128,1,130]{0,2,1:T(8,128)(2,1)S(1)}, u32[]{:S(2)}, u32[]{:S(2)}) collective-permute-start(bf16[128,1,130]{0,2,1:T(8,128)(2,1)S(1)} %get-tuple-element.75), channel_id=1, source_target_pairs={{0,1},{1,0},{2,3},{3,2},{4,5},{5,4},{6,7},{7,6},{8,9},{9,8},{10,11... | collective-permute-start | bytes 99848 | tf_op jit(solution)/shard_map/ppermute | solution.py:14
  10.8 1.4 %collective-permute-start.3 = (bf16[128,1,130]{0,2,1:T(8,128)(2,1)S(1)}, bf16[128,1,130]{0,2,1:T(8,128)(2,1)S(1)}, u32[]{:S(2)}, u32[]{:S(2)}) collective-permute-start(bf16[128,1,130]{0,2,1:T(8,128)(2,1)S(1)} %get-tuple-element.76), channel_id=1, source_target_pairs={{1,0},{0,1},{3,2},{2,3},{5,4},{4,5},{7,6},{6,7},{9,8},{8,9},{11,10... | collective-permute-start | bytes 99848 | tf_op jit(solution)/shard_map/ppermute | solution.py:15
  13.5 5.2 %collective-permute-start.4 = (bf16[128,292]{0,1:T(8,128)(2,1)S(1)}, bf16[128,292]{0,1:T(8,128)(2,1)S(1)}, u32[]{:S(2)}, u32[]{:S(2)}) collective-permute-start(bf16[128,292]{0,1:T(8,128)(2,1)S(1)} %pad_maximum_fusion.6), channel_id=1, source_target_pairs={{0,2},{2,0},{1,3},{3,1},{4,6},{6,4},{5,7},{7,5},{8,10},{10,8},{9,1... | collective-permute-start | bytes 224264 | tf_op jit(solution)/shard_map/ppermute | solution.py:148
  24.0 8.6 %collective-permute-start.6 = (bf16[3,3,128,128]{3,2,1,0:T(8,128)(2,1)S(1)}, bf16[3,3,128,128]{3,2,1,0:T(8,128)(2,1)S(1)}, u32[]{:S(2)}, u32[]{:S(2)}) collective-permute-start(bf16[3,3,128,128]{3,2,1,0:T(8,128)(2,1)S(1)} %get-tuple-element.8), channel_id=1, source_target_pairs={{0,2},{2,0},{1,3},{3,1},{4,6},{6,4},{5,7},{7,5},{8,10},{10,8},{9,1... | collective-permute-start | bytes 884744 | tf_op jit(solution)/shard_map/ppermute | solution.py:164
  27.6 0.7 copy-start.4
  32.6 0.8 %copy-start.2 = (bf16[3,3,128,128]{3,2,1,0:T(8,128)(2,1)}, bf16[3,3,128,128]{3,2,1,0:T(8,128)(2,1)S(1)}, u32[]{:S(2)}) copy-start(bf16[3,3,128,128]{3,2,1,0:T(8,128)(2,1)S(1)} %collective-permute-done.6) | copy-start | bytes 884740
  36.6 2.9 %collective-permute-start.7 = (f32[1216,128]{1,0:T(8,128)S(1)}, f32[1216,128]{1,0:T(8,128)}, u32[]{:S(2)}, u32[]{:S(2)}) collective-permute-start(f32[1216,128]{1,0:T(8,128)S(1)} %dynamic-slice_bitcast_fusion), channel_id=1, source_target_pairs={{0,1},{1,0},{2,3},{3,2},{4,5},{5,4},{6,7},{7,6},{8,9},{9,8},{10,11... | collective-permute-start | bytes 1867784 | tf_op jit(solution)/shard_map/ppermute | solution.py:64
  38.3 14.3 %collective-permute-start.14 = (bf16[128,16,128]{0,2,1:T(8,128)(2,1)S(1)}, bf16[128,16,128]{0,2,1:T(8,128)(2,1)S(1)}, u32[]{:S(2)}, u32[]{:S(2)}) collective-permute-start(bf16[128,16,128]{0,2,1:T(8,128)(2,1)S(1)} %copy.41), channel_id=1, source_target_pairs={{0,2},{2,0},{1,3},{3,1},{4,6},{6,4},{5,7},{7,5},{8,10},{10,8},{9,1... | collective-permute-start | bytes 1572872 | tf_op jit(solution)/shard_map/ppermute | solution.py:194
  40.8 6.8 %collective-permute-start.8 = (bf16[320,128]{1,0:T(8,128)(2,1)S(1)}, bf16[320,128]{1,0:T(8,128)(2,1)S(1)}, u32[]{:S(2)}, u32[]{:S(2)}) collective-permute-start(bf16[320,128]{1,0:T(8,128)(2,1)S(1)} %pad_maximum_fusion.4), channel_id=1, source_target_pairs={{0,4},{4,8},{8,12},{12,0},{1,5},{5,9},{9,13},{13,1},{2,6},{6,10},{... | collective-permute-start | bytes 245768 | tf_op jit(solution)/shard_map/ppermute | solution.py:104
  42.4 6.0 %collective-permute-start.9 = (bf16[320,128]{1,0:T(8,128)(2,1)S(1)}, bf16[320,128]{1,0:T(8,128)(2,1)S(1)}, u32[]{:S(2)}, u32[]{:S(2)}) collective-permute-start(bf16[320,128]{1,0:T(8,128)(2,1)S(1)} %pad_maximum_fusion.5), channel_id=1, source_target_pairs={{0,12},{4,0},{8,4},{12,8},{1,13},{5,1},{9,5},{13,9},{2,14},{6,2},{... | collective-permute-start | bytes 245768 | tf_op jit(solution)/shard_map/ppermute | solution.py:104
  44.7 7.6 %collective-permute-start.13 = (bf16[304,128]{1,0:T(8,128)(2,1)S(1)}, bf16[304,128]{1,0:T(8,128)(2,1)S(1)}, u32[]{:S(2)}, u32[]{:S(2)}) collective-permute-start(bf16[304,128]{1,0:T(8,128)(2,1)S(1)} %get-tuple-element.68), channel_id=1, source_target_pairs={{0,8},{4,12},{8,0},{12,4},{1,9},{5,13},{9,1},{13,5},{2,10},{6,14},... | collective-permute-start | bytes 233480 | tf_op jit(solution)/shard_map/ppermute | solution.py:104
  48.6 8.6 %collective-permute-start.10 = (bf16[128,1,130]{0,2,1:T(8,128)(2,1)S(1)}, bf16[128,1,130]{0,2,1:T(8,128)(2,1)S(1)}, u32[]{:S(2)}, u32[]{:S(2)}) collective-permute-start(bf16[128,1,130]{0,2,1:T(8,128)(2,1)S(1)} %get-tuple-element.73), channel_id=1, source_target_pairs={{0,1},{1,0},{2,3},{3,2},{4,5},{5,4},{6,7},{7,6},{8,9},{9,8},{10,11... | collective-permute-start | bytes 99848 | tf_op jit(solution)/shard_map/ppermute | solution.py:14
  48.7 8.5 %collective-permute-start.11 = (bf16[128,1,130]{0,2,1:T(8,128)(2,1)S(1)}, bf16[128,1,130]{0,2,1:T(8,128)(2,1)S(1)}, u32[]{:S(2)}, u32[]{:S(2)}) collective-permute-start(bf16[128,1,130]{0,2,1:T(8,128)(2,1)S(1)} %get-tuple-element.74), channel_id=1, source_target_pairs={{1,0},{0,1},{3,2},{2,3},{5,4},{4,5},{7,6},{6,7},{9,8},{8,9},{11,10... | collective-permute-start | bytes 99848 | tf_op jit(solution)/shard_map/ppermute | solution.py:15
  52.6 10.0 %collective-permute-start.15 = (bf16[304,128]{1,0:T(8,128)(2,1)S(1)}, bf16[304,128]{1,0:T(8,128)(2,1)S(1)}, u32[]{:S(2)}, u32[]{:S(2)}) collective-permute-start(bf16[304,128]{1,0:T(8,128)(2,1)S(1)} %convert_element_type.64), channel_id=1, source_target_pairs={{0,12},{4,0},{8,4},{12,8},{1,13},{5,1},{9,5},{13,9},{2,14},{6,2},{... | collective-permute-start | bytes 233480 | tf_op jit(solution)/shard_map/ppermute | solution.py:76
  56.5 7.0 %collective-permute-start.16 = (bf16[304,128]{1,0:T(8,128)(2,1)S(1)}, bf16[304,128]{1,0:T(8,128)(2,1)S(1)}, u32[]{:S(2)}, u32[]{:S(2)}) collective-permute-start(bf16[304,128]{1,0:T(8,128)(2,1)S(1)} %convert_element_type.64), channel_id=1, source_target_pairs={{0,8},{4,12},{8,0},{12,4},{1,9},{5,13},{9,1},{13,5},{2,10},{6,14},... | collective-permute-start | bytes 233480 | tf_op jit(solution)/shard_map/ppermute | solution.py:76
  56.5 7.1 %collective-permute-start.17 = (bf16[304,128]{1,0:T(8,128)(2,1)S(1)}, bf16[304,128]{1,0:T(8,128)(2,1)S(1)}, u32[]{:S(2)}, u32[]{:S(2)}) collective-permute-start(bf16[304,128]{1,0:T(8,128)(2,1)S(1)} %convert_element_type.64), channel_id=1, source_target_pairs={{0,4},{4,8},{8,12},{12,0},{1,5},{5,9},{9,13},{13,1},{2,6},{6,10},{... | collective-permute-start | bytes 233480 | tf_op jit(solution)/shard_map/ppermute | solution.py:76
  58.3 5.5 %collective-permute-start.12 = (bf16[128,292]{0,1:T(8,128)(2,1)S(1)}, bf16[128,292]{0,1:T(8,128)(2,1)S(1)}, u32[]{:S(2)}, u32[]{:S(2)}) collective-permute-start(bf16[128,292]{0,1:T(8,128)(2,1)S(1)} %pad_maximum_fusion.7), channel_id=1, source_target_pairs={{0,2},{2,0},{1,3},{3,1},{4,6},{6,4},{5,7},{7,5},{8,10},{10,8},{9,1... | collective-permute-start | bytes 224264 | tf_op jit(solution)/shard_map/ppermute | solution.py:209
  63.8 5.2 %collective-permute-start.18 = (f32[1216,128]{1,0:T(8,128)S(1)}, f32[1216,128]{1,0:T(8,128)S(1)}, u32[]{:S(2)}, u32[]{:S(2)}) collective-permute-start(f32[1216,128]{1,0:T(8,128)S(1)} %bitcast.334), channel_id=1, source_target_pairs={{0,1},{1,0},{2,3},{3,2},{4,5},{5,4},{6,7},{7,6},{8,9},{9,8},{10,11... | collective-permute-start | bytes 1867784 | tf_op jit(solution)/shard_map/ppermute | solution.py:76
  64.1 1.0 %copy-start.3 = (bf16[3,3,128,128]{3,2,1,0:T(8,128)(2,1)S(1)}, bf16[3,3,128,128]{3,2,1,0:T(8,128)(2,1)}, u32[]{:S(2)}) copy-start(bf16[3,3,128,128]{3,2,1,0:T(8,128)(2,1)} %copy-done.2) | copy-start | bytes 884740

commit v13 on v12

--- a/solution.py
+++ b/solution.py
@@ -169,14 +169,13 @@
     preact = preact + bias_vector[:, None]
     upstream = cotangent.reshape(own_channels, -1).astype(jnp.float32)
     grad_pre = (upstream * gelu_slope(preact)).astype(jnp.bfloat16)
-    grad_pre, kernel_blocks = lax.optimization_barrier((grad_pre, kernel_blocks))
     bias_part = jnp.sum(grad_pre.astype(jnp.float32), axis=1)
-    input_local = jnp.concatenate(blocks, axis=0)
+    input_global = jnp.roll(jnp.stack(blocks), chan_index, axis=0).reshape(-1, *input_pad.shape[1:])
     taps = []
     for tap_row in range(3):
         row_taps = []
         for tap_col in range(3):
-            window = window_of(input_local, tap_row, tap_col, row_count, column_count)
+            window = window_of(input_global, tap_row, tap_col, row_count, column_count)
             row_taps.append(
                 lax.dot_general(
                     grad_pre, window, (((1,), (1,)), ((), ())), preferred_element_type=jnp.float32
@@ -192,14 +191,10 @@
     for shift in range(1, chan_count):
         pairs = [(i, (i + shift) % chan_count) for i in range(chan_count)]
         grad_blocks.append(lax.ppermute(grad_field, "chan", pairs))
-    scattered, grad_blocks = lax.optimization_barrier((scattered, grad_blocks))
+    scattered, grad_blocks, kernel_blocks = lax.optimization_barrier((scattered, grad_blocks, kernel_blocks))
     flat = sum_finish(scattered, flat.size, jnp.bfloat16)
-    weight_local = flat[: weight_part.size].reshape(weight_part.shape)
+    weight_grad = flat[: weight_part.size].reshape(weight_part.shape)
     bias_grad = flat[weight_part.size :]
-    doubled = jnp.concatenate([weight_local, weight_local], axis=3)
-    weight_grad = lax.dynamic_slice_in_dim(
-        doubled, (chan_count - chan_index) % chan_count * own_channels, chan_count * own_channels, axis=3
-    )
     grad_wide = jnp.concatenate([before, grad_field, after], axis=2)
     grad_pad = mask_rims(padded_2(grad_wide, (("lat", 1),), 1))
     grad_border = border_of(grad_pad)

time: 71.6 us -> 88.2 us (1.23)
  local copies, waits for them, and re-layouts: 10.2 us -> 26.2 us
  waiting for transfers between devices: 14.6 us -> 22.7 us
  starting transfers between devices: 22.3 us -> 16.1 us
  other arithmetic: 8.08 us -> 6.18 us
    unnamed x18 -> x38, local copies, waits for them, and re-layouts: 3.57 us -> 9.38 us
    ppermute x1, waiting for transfers between devices: 3.36 us -> 8.76 us  [local(): kernel_blocks.append(lax.ppermute(kernel_sends[shift - 1], 'chan', pairs))]
    slice x4 -> x5, local copies, waits for them, and re-layouts: 3.49 us -> 7.36 us  [window_of(): field[:, first_row:first_row + row_count, first_col:first_col + column_co...]
    reshape x1 -> x2, local copies, waits for them, and re-layouts: 0.33 us -> 3.6 us  [the longest x1 2.26 us: local(): jnp.roll(jnp.stack(blocks), chan_index, axis=0)]
    concatenate x2, other arithmetic: 3.89 us -> 1.08 us  [the longest x1 0.9 us: local(): jnp.roll(jnp.stack(blocks), chan_index, axis=0)]
    ppermute x3, starting transfers between devices: 4.67 us -> 2.08 us  [sum_start(): moved = lax.ppermute(piece, 'lon', pairs)]
    ppermute x4, starting transfers between devices: 4.61 us -> 2.15 us  [direct_all_gather(): pieces.append(lax.ppermute(sent, axis, pairs).astype(jnp.float32))]
    ppermute x3, waiting for transfers between devices: 2.08 us -> 4.25 us  [padded_2(): before = lax.ppermute(last, axis, up)]
  transfers between devices with their start and end apart: 19 -> 19, of which waited for: 10 -> 10; matrix products, arithmetic and copies ran while one was open for 27% -> 23% of each run, Pallas kernels for 0% -> 0%
where the time goes in v13:
time: 88.2 us; the launch traced here: 87.5 us
  local copies, waits for them, and re-layouts  26.2 us (30%)
  waiting for transfers between devices  22.7 us (26%)
  starting transfers between devices  16.1 us (18%)
  matrix products  14.7 us (17%)
  other arithmetic  6.18 us (7%)
  between operations  1.58 us (2%)
    dot_general x36, matrix products, conv_taps(): jnp.dot(kernel[tap_row, tap_col], window, preferred_element_type=jnp.floa...  11.9 us
    unnamed x38, local copies, waits for them, and re-layouts  9.38 us
    ppermute x1, waiting for transfers between devices, local(): kernel_blocks.append(lax.ppermute(kernel_sends[shift - 1], 'chan', pairs))  8.76 us
    slice x5, local copies, waits for them, and re-layouts, window_of(): field[:, first_row:first_row + row_count, first_col:first_col + column_co...  7.36 us
    ppermute x3, waiting for transfers between devices, sum_start(): moved = lax.ppermute(piece, 'lon', pairs)  6.4 us
    ppermute x3, waiting for transfers between devices, padded_2(): before = lax.ppermute(last, axis, up)  4.25 us
    ppermute x3, starting transfers between devices, padded_2(): after = lax.ppermute(initial, axis, down)  3.8 us
    ppermute x1, starting transfers between devices, local(): raw_blocks.append(lax.ppermute(inputs, 'chan', pairs))  3 us
  transfers between devices with their start and end apart: 19, of which 10 were waited for; matrix products, arithmetic and copies ran while one was open for 23% of the time, Pallas kernels for 0%

profile of v13, /device:TPU:0, one launch (start us, length us, event | category | flops | bytes accessed | tf_op | source)
XLA Modules:
  0.0 87.5 jit_solution(7851278592431067492)
XLA Ops:
  0.6 1.5 %copy.56 = bf16[128,16,128]{0,2,1:T(8,128)(2,1)S(1)} copy(bf16[128,16,128]{2,1,0:T(8,128)(2,1)} %param.4) | data formatting | bytes 1048576 | tf_op args[0]
  2.2 3.0 %collective-permute-start.5 = (bf16[128,16,128]{0,2,1:T(8,128)(2,1)S(1)}, bf16[128,16,128]{0,2,1:T(8,128)(2,1)}, u32[]{:S(2)}, u32[]{:S(2)}) collective-permute-start(bf16[128,16,128]{0,2,1:T(8,128)(2,1)S(1)} %copy.56), channel_id=1, source_target_pairs={{0,2},{2,0},{1,3},{3,1},{4,6},{6,4},{5,7},{7,5},{8,10},{10,8},{9,1... | collective-permute-start | bytes 1572872 | tf_op jit(solution)/shard_map/ppermute | solution.py:142
  5.2 3.7 %collective-permute-start.1 = (bf16[128,16,1]{0,2,1:T(2,128)(2,1)S(1)}, bf16[128,16,1]{0,2,1:T(2,128)(2,1)S(1)}, u32[]{:S(2)}, u32[]{:S(2)}) collective-permute-start(bf16[128,16,1]{0,2,1:T(2,128)(2,1)S(1)} %get-tuple-element.78), channel_id=1, source_target_pairs={{4,0},{8,4},{12,8},{0,12},{5,1},{9,5},{13,9},{1,13},{6,2},{10,6},{... | collective-permute-start | bytes 12296 | tf_op jit(solution)/shard_map/ppermute | solution.py:15
  8.8 1.1 %bitcast_convert_fusion = f32[16,8,16,128]{3,2,1,0:T(8,128)} fusion(bf16[128,16,128]{2,1,0:T(8,128)(2,1)S(1)} %copy-done.13), kind=kLoop, calls=%fused_computation.196 | loop fusion | flops 262144 | bytes 1572864
  10.2 4.1 %collective-permute-done = bf16[128,16,1]{0,2,1:T(2,128)(2,1)S(1)} collective-permute-done((bf16[128,16,1]{0,2,1:T(2,128)(2,1)S(1)}, bf16[128,16,1]{0,2,1:T(2,128)(2,1)S(1)}, u32[]{:S(2)}, u32[]{:S(2)}) %collective-permute-start) | collective-permute-done | bytes 4128 | tf_op jit(solution)/shard_map/ppermute | solution.py:14
  16.3 0.8 fusion.51
  20.7 1.1 %collective-permute-done.4 = bf16[128,292]{0,1:T(8,128)(2,1)S(1)} collective-permute-done((bf16[128,292]{0,1:T(8,128)(2,1)S(1)}, bf16[128,292]{0,1:T(8,128)(2,1)S(1)}, u32[]{:S(2)}, u32[]{:S(2)}) %collective-permute-start.4) | collective-permute-done | bytes 74784 | tf_op jit(solution)/shard_map/ppermute | solution.py:148
  21.9 1.2 %pad_maximum_fusion.1 = bf16[128,18,130]{0,2,1:T(8,128)(2,1)S(1)} fusion(bf16[128,1,130]{0,2,1:T(8,128)(2,1)S(1)} %get-tuple-element.84, bf16[128,16,1]{0,2,1:T(2,128)(2,1)S(1)} %copy.61, bf16[128,16,128]{0,2,1:T(8,128)(2,1)} %collective-permute-done.5, bf16[128,16,1]{0,2,1:T(2,128)(2,1)S(1)} %copy.60, bf16[128,1,130]{0,2,1:T(8,128)(2,1)S(1)} %get-tuple-element.83), kind=kLoop, calls=%fused_computation.72 | loop fusion | flops 2995200 | bytes 1198080 | tf_op jit(solution)/shard_map/concatenate | solution.py:132
  23.1 2.4 %fusion.49 = (bf16[128,16,128]{0,2,1:T(8,128)(2,1)}, bf16[128,16,128]{0,2,1:T(8,128)(2,1)}, bf16[128,16,128]{0,2,1:T(8,128)(2,1)}, bf16[128,16,128]{0,2,1:T(8,12...) fusion(bf16[128,18,130]{0,2,1:T(8,128)(2,1)S(1)} %pad_maximum_f, ...), kind=kLoop, calls=%fused_computation.191 | loop fusion | bytes 9437184 | tf_op jit(solution)/shard_map/slice | solution.py:37
  25.5 0.9 %fusion.6 = bf16[2,128,18,130]{1,3,2,0:T(8,128)(2,1)S(1)} fusion(s32[]{:T(128)S(6)} %select_n.112, bf16[1,128,18,130]{1,3,2,0:T(8,128)(2,1)S(1)} %maximum_select_fusion.1, bf16[1,128,18,130]{1,3,2,0:T(8,128)(2,1)S(1)} %bitcast.327), kind=kLoop, calls=%fused_computation.47 | loop fusion | flops 1797120 | bytes 2396164 | tf_op jit(solution)/shard_map/jit(_roll_dynamic)/concatenate | solution.py:173
  26.4 0.9 %copy.62 = bf16[2,128,18,130]{1,0,3,2:T(2,128)(2,1)S(1)} copy(bf16[2,128,18,130]{1,3,2,0:T(8,128)(2,1)S(1)} %fusion.6) | data formatting | bytes 2396160 | tf_op jit(solution)/shard_map/jit(_roll_dynamic)/dynamic_slice | solution.py:173
  27.3 2.3 %reshape.250 = bf16[256,18,130]{0,2,1:T(8,128)(2,1)S(1)} reshape(bf16[2,128,18,130]{1,0,3,2:T(2,128)(2,1)S(1)} %copy.62) | data formatting | bytes 2396160 | tf_op jit(solution)/shard_map/reshape | solution.py:173
  29.6 2.5 %fusion.45 = (bf16[256,16,128]{0,2,1:T(8,128)(2,1)S(1)}, bf16[256,16,128]{0,2,1:T(8,128)(2,1)S(1)}, bf16[256,16,128]{0,2,1:T(8,128)(2,1)S(1)}, bf16[256,16,128]{...) fusion(bf16[256,18,130]{0,2,1:T(8,128)(2,1)S(1)} %reshape.250), kind=kLoop, calls=%fused_computation.187 | loop fusion | bytes 18874368 | tf_op jit(solution)/shard_map/slice | solution.py:37
  39.7 0.9 %copy-done = f32[16,8,16,128]{3,2,1,0:T(8,128)S(1)} copy-done((f32[16,8,16,128]{3,2,1,0:T(8,128)S(1)}, f32[16,8,16,128]{3,2,1,0:T(8,128)}, u32[]{:S(2)}) %copy-start) | copy-done | bytes 1048600
  40.8 1.0 %convert_reduce_fusion = (f32[128]{0:T(128)S(1)}, bf16[128,2048]{1,0:T(8,128)(2,1)S(1)}) fusion(f32[128]{0:T(128)S(1)} %copy-done.14, f32[128,2048]{1,0:T(8,128)S(1)} %convolution_add_fusion.24, f32[128,2048]{1,0:T(8,128)S(1)} %convolution_add_fusion.17, bf16[128,2048]{0,1:T(8,128)(2,1)S(1)} %bitcast.382, bf16[3,3,128,256]{3,2,1,0:T(8,128)(2,1)S(1)} %copy-done.2, ...), kind=kOutput, calls=%fused_computation.70 | convolution fusion | flops 71040896 | bytes 4228104 | tf_op jit(solution)/shard_map/dot_general | solution.py:50
  46.4 1.4 %slice_reduce_fusion.1 = (bf16[128,16]{1,0:T(8,128)(2,1)}, bf16[128,16]{1,0:T(8,128)(2,1)}) fusion(bf16[128,16,128]{2,1,0:T(8,128)(2,1)S(1)} %bitcast.329), kind=kLoop, calls=%fused_computation.80 | loop fusion | bytes 16384 | tf_op jit(solution)/shard_map/slice | solution.py:188
  47.9 0.9 reshape.265
  48.7 0.9 reshape.263
  50.3 1.8 %collective-permute-start.8 = (bf16[320,128]{1,0:T(8,128)(2,1)S(1)}, bf16[320,128]{1,0:T(8,128)(2,1)S(1)}, u32[]{:S(2)}, u32[]{:S(2)}) collective-permute-start(bf16[320,128]{1,0:T(8,128)(2,1)S(1)} %pad_maximum_fusion.5), channel_id=1, source_target_pairs={{0,12},{4,0},{8,4},{12,8},{1,13},{5,1},{9,5},{13,9},{2,14},{6,2},{... | collective-permute-start | bytes 245768 | tf_op jit(solution)/shard_map/ppermute | solution.py:104
  52.5 1.6 %collective-permute-start.13 = (bf16[3,3,128,128]{3,2,1,0:T(8,128)(2,1)S(1)}, bf16[3,3,128,128]{3,2,1,0:T(8,128)(2,1)S(1)}, u32[]{:S(2)}, u32[]{:S(2)}) collective-permute-start(bf16[3,3,128,128]{3,2,1,0:T(8,128)(2,1)S(1)} %get-tuple-element.7), channel_id=1, source_target_pairs={{0,2},{2,0},{1,3},{3,1},{4,6},{6,4},{5,7},{7,5},{8,10},{10,8},{9,1... | collective-permute-start | bytes 884744 | tf_op jit(solution)/shard_map/ppermute | solution.py:164
  54.1 0.8 collective-permute-done.8
  55.1 4.0 %collective-permute-done.7 = bf16[320,128]{1,0:T(8,128)(2,1)S(1)} collective-permute-done((bf16[320,128]{1,0:T(8,128)(2,1)S(1)}, bf16[320,128]{1,0:T(8,128)(2,1)S(1)}, u32[]{:S(2)}, u32[]{:S(2)}) %collective-permute-start.7) | collective-permute-done | bytes 81952 | tf_op jit(solution)/shard_map/ppermute | solution.py:104
  59.8 1.6 %collective-permute-done.11 = bf16[304,128]{1,0:T(8,128)(2,1)S(1)} collective-permute-done((bf16[304,128]{1,0:T(8,128)(2,1)S(1)}, bf16[304,128]{1,0:T(8,128)(2,1)S(1)}, u32[]{:S(2)}, u32[]{:S(2)}) %collective-permute-start.11) | collective-permute-done | bytes 77856 | tf_op jit(solution)/shard_map/ppermute | solution.py:104
  61.5 8.8 %collective-permute-done.13 = bf16[3,3,128,128]{3,2,1,0:T(8,128)(2,1)S(1)} collective-permute-done((bf16[3,3,128,128]{3,2,1,0:T(8,128)(2,1)S(1)}, bf16[3,3,128,128]{3,2,1,0:T(8,128)(2,1)S(1)}, u32[]{:S(2)}, u32[]{:S(2)}) %collective-permute-start.13) | collective-permute-done | bytes 294944 | tf_op jit(solution)/shard_map/ppermute | solution.py:164
  70.2 0.8 collective-permute-start.15
  71.0 1.3 %collective-permute-start.17 = (bf16[304,128]{1,0:T(8,128)(2,1)S(1)}, bf16[304,128]{1,0:T(8,128)(2,1)S(1)}, u32[]{:S(2)}, u32[]{:S(2)}) collective-permute-start(bf16[304,128]{1,0:T(8,128)(2,1)S(1)} %convert_element_type.64), channel_id=1, source_target_pairs={{0,4},{4,8},{8,12},{12,0},{1,5},{5,9},{9,13},{13,1},{2,6},{6,10},{... | collective-permute-start | bytes 233480 | tf_op jit(solution)/shard_map/ppermute | solution.py:76
  73.5 1.3 %collective-permute-start.14 = (bf16[128,292]{0,1:T(8,128)(2,1)S(1)}, bf16[128,292]{0,1:T(8,128)(2,1)S(1)}, u32[]{:S(2)}, u32[]{:S(2)}) collective-permute-start(bf16[128,292]{0,1:T(8,128)(2,1)S(1)} %pad_maximum_fusion.7), channel_id=1, source_target_pairs={{0,2},{2,0},{1,3},{3,1},{4,6},{6,4},{5,7},{7,5},{8,10},{10,8},{9,1... | collective-permute-start | bytes 224264 | tf_op jit(solution)/shard_map/ppermute | solution.py:204
  77.7 1.2 %collective-permute-done.16 = bf16[304,128]{1,0:T(8,128)(2,1)S(1)} collective-permute-done((bf16[304,128]{1,0:T(8,128)(2,1)S(1)}, bf16[304,128]{1,0:T(8,128)(2,1)S(1)}, u32[]{:S(2)}, u32[]{:S(2)}) %collective-permute-start.16) | collective-permute-done | bytes 77856 | tf_op jit(solution)/shard_map/ppermute | solution.py:76
  79.3 1.2 %pad_maximum_fusion.2 = bf16[128,18,130]{0,2,1:T(8,128)(2,1)S(1)} fusion(bf16[128,1,130]{0,2,1:T(8,128)(2,1)S(1)} %get-tuple-element.80, bf16[128,16,1]{0,2,1:T(2,128)(2,1)S(1)} %copy.70, bf16[128,16,128]{0,2,1:T(8,128)(2,1)} %collective-permute-done.12, bf16[128,16,1]{0,2,1:T(2,128)(2,1)S(1)} %copy.69, bf16[128,1,130]{0,2,1:T(8,128)(2,1)S(1)} %get-tuple-element.79), kind=kLoop, calls=%fused_computation.75 | loop fusion | flops 2995200 | bytes 1198080 | tf_op jit(solution)/shard_map/concatenate | solution.py:132
  80.5 0.9 %fusion.46 = (bf16[128,16,128]{0,2,1:T(8,128)(2,1)S(1)}, bf16[128,16,128]{0,2,1:T(8,128)(2,1)S(1)}, bf16[128,16,128]{0,2,1:T(8,128)(2,1)S(1)}, bf16[128,16,128]{...) fusion(bf16[128,18,130]{0,2,1:T(8,128)(2,1)S(1)} %pad_maximum_f, ...), kind=kLoop, calls=%fused_computation.188 | loop fusion | bytes 9437184 | tf_op jit(solution)/shard_map/slice | solution.py:37
  84.4 0.9 %copy.80 = bf16[16,8,16,128]{3,2,1,0:T(8,128)(2,1)} copy(bf16[16,8,16,128]{3,1,2,0:T(8,128)(2,1)S(1)} %fusion.10) | data formatting | bytes 1048576
  86.1 1.3 %reshape.287 = f32[3,3,128,256]{3,2,1,0:T(8,128)} reshape(f32[294912]{0:T(1024)S(1)} %slice.536) | data formatting | bytes 2359296 | tf_op jit(solution)/shard_map/reshape | solution.py:196
  (157 shorter events, 28.0 us)
Async XLA Ops:
  0.6 8.2 %copy-start.13 = (bf16[128,16,128]{2,1,0:T(8,128)(2,1)S(1)}, bf16[128,16,128]{2,1,0:T(8,128)(2,1)}, u32[]{:S(2)}) copy-start(bf16[128,16,128]{2,1,0:T(8,128)(2,1)} %param.5) | copy-start | bytes 1572868
  2.2 19.7 %collective-permute-start.5 = (bf16[128,16,128]{0,2,1:T(8,128)(2,1)S(1)}, bf16[128,16,128]{0,2,1:T(8,128)(2,1)}, u32[]{:S(2)}, u32[]{:S(2)}) collective-permute-start(bf16[128,16,128]{0,2,1:T(8,128)(2,1)S(1)} %copy.56), channel_id=1, source_target_pairs={{0,2},{2,0},{1,3},{3,1},{4,6},{6,4},{5,7},{7,5},{8,10},{10,8},{9,1... | collective-permute-start | bytes 1572872 | tf_op jit(solution)/shard_map/ppermute | solution.py:142
  5.2 5.0 %collective-permute-start.1 = (bf16[128,16,1]{0,2,1:T(2,128)(2,1)S(1)}, bf16[128,16,1]{0,2,1:T(2,128)(2,1)S(1)}, u32[]{:S(2)}, u32[]{:S(2)}) collective-permute-start(bf16[128,16,1]{0,2,1:T(2,128)(2,1)S(1)} %get-tuple-element.78), channel_id=1, source_target_pairs={{4,0},{8,4},{12,8},{0,12},{5,1},{9,5},{13,9},{1,13},{6,2},{10,6},{... | collective-permute-start | bytes 12296 | tf_op jit(solution)/shard_map/ppermute | solution.py:15
  8.8 5.4 %collective-permute-start = (bf16[128,16,1]{0,2,1:T(2,128)(2,1)S(1)}, bf16[128,16,1]{0,2,1:T(2,128)(2,1)S(1)}, u32[]{:S(2)}, u32[]{:S(2)}) collective-permute-start(bf16[128,16,1]{0,2,1:T(2,128)(2,1)S(1)} %get-tuple-element.77), channel_id=1, source_target_pairs={{0,4},{4,8},{8,12},{12,0},{1,5},{5,9},{9,13},{13,1},{2,6},{6,10},{... | collective-permute-start | bytes 12296 | tf_op jit(solution)/shard_map/ppermute | solution.py:14
  14.5 1.3 %collective-permute-start.3 = (bf16[128,1,130]{0,2,1:T(8,128)(2,1)S(1)}, bf16[128,1,130]{0,2,1:T(8,128)(2,1)S(1)}, u32[]{:S(2)}, u32[]{:S(2)}) collective-permute-start(bf16[128,1,130]{0,2,1:T(8,128)(2,1)S(1)} %get-tuple-element.72), channel_id=1, source_target_pairs={{1,0},{0,1},{3,2},{2,3},{5,4},{4,5},{7,6},{6,7},{9,8},{8,9},{11,10... | collective-permute-start | bytes 99848 | tf_op jit(solution)/shard_map/ppermute | solution.py:15
  14.6 1.4 %collective-permute-start.2 = (bf16[128,1,130]{0,2,1:T(8,128)(2,1)S(1)}, bf16[128,1,130]{0,2,1:T(8,128)(2,1)S(1)}, u32[]{:S(2)}, u32[]{:S(2)}) collective-permute-start(bf16[128,1,130]{0,2,1:T(8,128)(2,1)S(1)} %get-tuple-element.71), channel_id=1, source_target_pairs={{0,1},{1,0},{2,3},{3,2},{4,5},{5,4},{6,7},{7,6},{8,9},{9,8},{10,11... | collective-permute-start | bytes 99848 | tf_op jit(solution)/shard_map/ppermute | solution.py:14
  16.3 1.5 %copy-start.1 = (bf16[3,3,128,256]{3,2,1,0:T(8,128)(2,1)S(1)}, bf16[3,3,128,256]{3,2,1,0:T(8,128)(2,1)}, u32[]{:S(2)}) copy-start(bf16[3,3,128,256]{3,2,1,0:T(8,128)(2,1)} %param.6) | copy-start | bytes 1769476
  17.2 4.6 %collective-permute-start.4 = (bf16[128,292]{0,1:T(8,128)(2,1)S(1)}, bf16[128,292]{0,1:T(8,128)(2,1)S(1)}, u32[]{:S(2)}, u32[]{:S(2)}) collective-permute-start(bf16[128,292]{0,1:T(8,128)(2,1)S(1)} %pad_maximum_fusion.6), channel_id=1, source_target_pairs={{0,2},{2,0},{1,3},{3,1},{4,6},{6,4},{5,7},{7,5},{8,10},{10,8},{9,1... | collective-permute-start | bytes 224264 | tf_op jit(solution)/shard_map/ppermute | solution.py:148
  29.6 2.5 %copy-start.2 = (bf16[3,3,128,256]{3,2,1,0:T(8,128)(2,1)S(1)}, bf16[3,3,128,256]{3,2,1,0:T(8,128)(2,1)}, u32[]{:S(2)}) copy-start(bf16[3,3,128,256]{3,2,1,0:T(8,128)(2,1)} %param.6) | copy-start | bytes 1769476
  29.6 2.5 %copy-start.9 = (bf16[128,16,128]{0,2,1:T(8,128)(2,1)S(1)}, bf16[128,16,128]{0,2,1:T(8,128)(2,1)}, u32[]{:S(2)}) copy-start(bf16[128,16,128]{0,2,1:T(8,128)(2,1)} %get-tuple-element.52) | copy-start | bytes 1572868
  32.1 1.0 %copy-start.8 = (bf16[128,16,128]{0,2,1:T(8,128)(2,1)S(1)}, bf16[128,16,128]{0,2,1:T(8,128)(2,1)}, u32[]{:S(2)}) copy-start(bf16[128,16,128]{0,2,1:T(8,128)(2,1)} %get-tuple-element.51) | copy-start | bytes 1572868
  33.2 1.0 %copy-start.7 = (bf16[128,16,128]{0,2,1:T(8,128)(2,1)S(1)}, bf16[128,16,128]{0,2,1:T(8,128)(2,1)}, u32[]{:S(2)}) copy-start(bf16[128,16,128]{0,2,1:T(8,128)(2,1)} %get-tuple-element.50) | copy-start | bytes 1572868
  34.2 1.0 %copy-start.6 = (bf16[128,16,128]{0,2,1:T(8,128)(2,1)S(1)}, bf16[128,16,128]{0,2,1:T(8,128)(2,1)}, u32[]{:S(2)}) copy-start(bf16[128,16,128]{0,2,1:T(8,128)(2,1)} %get-tuple-element.49) | copy-start | bytes 1572868
  35.3 1.0 %copy-start.5 = (bf16[128,16,128]{0,2,1:T(8,128)(2,1)S(1)}, bf16[128,16,128]{0,2,1:T(8,128)(2,1)}, u32[]{:S(2)}) copy-start(bf16[128,16,128]{0,2,1:T(8,128)(2,1)} %get-tuple-element.48) | copy-start | bytes 1572868
  37.3 1.0 %copy-start.4 = (bf16[128,16,128]{0,2,1:T(8,128)(2,1)S(1)}, bf16[128,16,128]{0,2,1:T(8,128)(2,1)}, u32[]{:S(2)}) copy-start(bf16[128,16,128]{0,2,1:T(8,128)(2,1)} %get-tuple-element.46) | copy-start | bytes 1572868
  39.4 1.2 %copy-start = (f32[16,8,16,128]{3,2,1,0:T(8,128)S(1)}, f32[16,8,16,128]{3,2,1,0:T(8,128)}, u32[]{:S(2)}) copy-start(f32[16,8,16,128]{3,2,1,0:T(8,128)} %bitcast_convert_fusion) | copy-start | bytes 3145732
  39.4 1.4 %copy-start.12 = (bf16[128,16,128]{0,2,1:T(8,128)(2,1)S(1)}, bf16[128,16,128]{0,2,1:T(8,128)(2,1)}, u32[]{:S(2)}) copy-start(bf16[128,16,128]{0,2,1:T(8,128)(2,1)} %get-tuple-element.44) | copy-start | bytes 1572868
  39.4 1.4 %copy-start.14 = (f32[128]{0:T(128)S(1)}, f32[128]{0:T(128)}, u32[]{:S(2)}) copy-start(f32[128]{0:T(128)} %param.7) | copy-start | bytes 1540
  45.7 4.5 %collective-permute-start.6 = (f32[1216,128]{1,0:T(8,128)S(1)}, f32[1216,128]{1,0:T(8,128)S(1)}, u32[]{:S(2)}, u32[]{:S(2)}) collective-permute-start(f32[1216,128]{1,0:T(8,128)S(1)} %dynamic-slice_bitcast_fusion), channel_id=1, source_target_pairs={{0,1},{1,0},{2,3},{3,2},{4,5},{5,4},{6,7},{7,6},{8,9},{9,8},{10,11... | collective-permute-start | bytes 1867784 | tf_op jit(solution)/shard_map/ppermute | solution.py:64
  49.6 2.8 %copy-start.3 = (bf16[3,3,128,256]{3,2,1,0:T(8,128)(2,1)S(1)}, bf16[3,3,128,256]{3,2,1,0:T(8,128)(2,1)}, u32[]{:S(2)}) copy-start(bf16[3,3,128,256]{3,2,1,0:T(8,128)(2,1)} %param.6) | copy-start | bytes 1769476
  49.6 20.6 %collective-permute-start.12 = (bf16[128,16,128]{0,2,1:T(8,128)(2,1)S(1)}, bf16[128,16,128]{0,2,1:T(8,128)(2,1)}, u32[]{:S(2)}, u32[]{:S(2)}) collective-permute-start(bf16[128,16,128]{0,2,1:T(8,128)(2,1)S(1)} %copy.66), channel_id=1, source_target_pairs={{0,2},{2,0},{1,3},{3,1},{4,6},{6,4},{5,7},{7,5},{8,10},{10,8},{9,1... | collective-permute-start | bytes 1572872 | tf_op jit(solution)/shard_map/ppermute | solution.py:193
  50.3 4.6 %collective-permute-start.8 = (bf16[320,128]{1,0:T(8,128)(2,1)S(1)}, bf16[320,128]{1,0:T(8,128)(2,1)S(1)}, u32[]{:S(2)}, u32[]{:S(2)}) collective-permute-start(bf16[320,128]{1,0:T(8,128)(2,1)S(1)} %pad_maximum_fusion.5), channel_id=1, source_target_pairs={{0,12},{4,0},{8,4},{12,8},{1,13},{5,1},{9,5},{13,9},{2,14},{6,2},{... | collective-permute-start | bytes 245768 | tf_op jit(solution)/shard_map/ppermute | solution.py:104
  52.1 6.9 %collective-permute-start.7 = (bf16[320,128]{1,0:T(8,128)(2,1)S(1)}, bf16[320,128]{1,0:T(8,128)(2,1)S(1)}, u32[]{:S(2)}, u32[]{:S(2)}) collective-permute-start(bf16[320,128]{1,0:T(8,128)(2,1)S(1)} %pad_maximum_fusion.4), channel_id=1, source_target_pairs={{0,4},{4,8},{8,12},{12,0},{1,5},{5,9},{9,13},{13,1},{2,6},{6,10},{... | collective-permute-start | bytes 245768 | tf_op jit(solution)/shard_map/ppermute | solution.py:104
  52.5 17.7 %collective-permute-start.13 = (bf16[3,3,128,128]{3,2,1,0:T(8,128)(2,1)S(1)}, bf16[3,3,128,128]{3,2,1,0:T(8,128)(2,1)S(1)}, u32[]{:S(2)}, u32[]{:S(2)}) collective-permute-start(bf16[3,3,128,128]{3,2,1,0:T(8,128)(2,1)S(1)} %get-tuple-element.7), channel_id=1, source_target_pairs={{0,2},{2,0},{1,3},{3,1},{4,6},{6,4},{5,7},{7,5},{8,10},{10,8},{9,1... | collective-permute-start | bytes 884744 | tf_op jit(solution)/shard_map/ppermute | solution.py:164
  54.1 7.4 %collective-permute-start.11 = (bf16[304,128]{1,0:T(8,128)(2,1)S(1)}, bf16[304,128]{1,0:T(8,128)(2,1)S(1)}, u32[]{:S(2)}, u32[]{:S(2)}) collective-permute-start(bf16[304,128]{1,0:T(8,128)(2,1)S(1)} %get-tuple-element.66), channel_id=1, source_target_pairs={{0,8},{4,12},{8,0},{12,4},{1,9},{5,13},{9,1},{13,5},{2,10},{6,14},... | collective-permute-start | bytes 233480 | tf_op jit(solution)/shard_map/ppermute | solution.py:104
  59.2 13.1 %collective-permute-start.10 = (bf16[128,1,130]{0,2,1:T(8,128)(2,1)S(1)}, bf16[128,1,130]{0,2,1:T(8,128)(2,1)S(1)}, u32[]{:S(2)}, u32[]{:S(2)}) collective-permute-start(bf16[128,1,130]{0,2,1:T(8,128)(2,1)S(1)} %get-tuple-element.74), channel_id=1, source_target_pairs={{1,0},{0,1},{3,2},{2,3},{5,4},{4,5},{7,6},{6,7},{9,8},{8,9},{11,10... | collective-permute-start | bytes 99848 | tf_op jit(solution)/shard_map/ppermute | solution.py:15
  59.3 13.0 %collective-permute-start.9 = (bf16[128,1,130]{0,2,1:T(8,128)(2,1)S(1)}, bf16[128,1,130]{0,2,1:T(8,128)(2,1)S(1)}, u32[]{:S(2)}, u32[]{:S(2)}) collective-permute-start(bf16[128,1,130]{0,2,1:T(8,128)(2,1)S(1)} %get-tuple-element.73), channel_id=1, source_target_pairs={{0,1},{1,0},{2,3},{3,2},{4,5},{5,4},{6,7},{7,6},{8,9},{9,8},{10,11... | collective-permute-start | bytes 99848 | tf_op jit(solution)/shard_map/ppermute | solution.py:14
  70.2 7.5 %collective-permute-start.15 = (bf16[304,128]{1,0:T(8,128)(2,1)S(1)}, bf16[304,128]{1,0:T(8,128)(2,1)S(1)}, u32[]{:S(2)}, u32[]{:S(2)}) collective-permute-start(bf16[304,128]{1,0:T(8,128)(2,1)S(1)} %convert_element_type.64), channel_id=1, source_target_pairs={{0,12},{4,0},{8,4},{12,8},{1,13},{5,1},{9,5},{13,9},{2,14},{6,2},{... | collective-permute-start | bytes 233480 | tf_op jit(solution)/shard_map/ppermute | solution.py:76
  71.0 7.9 %collective-permute-start.16 = (bf16[304,128]{1,0:T(8,128)(2,1)S(1)}, bf16[304,128]{1,0:T(8,128)(2,1)S(1)}, u32[]{:S(2)}, u32[]{:S(2)}) collective-permute-start(bf16[304,128]{1,0:T(8,128)(2,1)S(1)} %convert_element_type.64), channel_id=1, source_target_pairs={{0,8},{4,12},{8,0},{12,4},{1,9},{5,13},{9,1},{13,5},{2,10},{6,14},... | collective-permute-start | bytes 233480 | tf_op jit(solution)/shard_map/ppermute | solution.py:76
  71.0 7.9 %collective-permute-start.17 = (bf16[304,128]{1,0:T(8,128)(2,1)S(1)}, bf16[304,128]{1,0:T(8,128)(2,1)S(1)}, u32[]{:S(2)}, u32[]{:S(2)}) collective-permute-start(bf16[304,128]{1,0:T(8,128)(2,1)S(1)} %convert_element_type.64), channel_id=1, source_target_pairs={{0,4},{4,8},{8,12},{12,0},{1,5},{5,9},{9,13},{13,1},{2,6},{6,10},{... | collective-permute-start | bytes 233480 | tf_op jit(solution)/shard_map/ppermute | solution.py:76
  73.5 5.7 %collective-permute-start.14 = (bf16[128,292]{0,1:T(8,128)(2,1)S(1)}, bf16[128,292]{0,1:T(8,128)(2,1)S(1)}, u32[]{:S(2)}, u32[]{:S(2)}) collective-permute-start(bf16[128,292]{0,1:T(8,128)(2,1)S(1)} %pad_maximum_fusion.7), channel_id=1, source_target_pairs={{0,2},{2,0},{1,3},{3,1},{4,6},{6,4},{5,7},{7,5},{8,10},{10,8},{9,1... | collective-permute-start | bytes 224264 | tf_op jit(solution)/shard_map/ppermute | solution.py:204
  79.1 6.2 %collective-permute-start.18 = (f32[1216,128]{1,0:T(8,128)S(1)}, f32[1216,128]{1,0:T(8,128)S(1)}, u32[]{:S(2)}, u32[]{:S(2)}) collective-permute-start(f32[1216,128]{1,0:T(8,128)S(1)} %bitcast.345), channel_id=1, source_target_pairs={{0,1},{1,0},{2,3},{3,2},{4,5},{5,4},{6,7},{7,6},{8,9},{9,8},{10,11... | collective-permute-start | bytes 1867784 | tf_op jit(solution)/shard_map/ppermute | solution.py:76
  (2 other events, 2.1 us)

commit v14 on v8

--- a/solution.py
+++ b/solution.py
@@ -79,12 +79,57 @@
     return stacked.reshape(-1, chunk.shape[-1])
 
 
-def sum_start(flat, send_dtype):
+def piggyback_step(chunks, index, count, step, axis, send_dtype, extra):
+    pairs = [(j, (j + step) % count) for j in range(count)]
+    piece = lax.dynamic_index_in_dim(chunks, (index + step) % count, keepdims=False).astype(send_dtype)
+    size = piece.shape[0]
+    if extra is not None:
+        tail = extra.astype(send_dtype).reshape(-1)
+        tail = jnp.pad(tail, (0, (-tail.size) % chunks.shape[-1])).reshape(-1, chunks.shape[-1])
+        piece = jnp.concatenate([piece, tail], axis=0)
+    moved = lax.ppermute(piece, axis, pairs)
+    got = None if extra is None else moved[size:].reshape(-1)[: extra.size].reshape(extra.shape)
+    return moved[:size].astype(jnp.float32), got
+
+
+def sum_start(flat, send_dtype, field):
+    lanes = 128
     parts = lax.axis_size("lat") * lax.axis_size("lon")
-    quantum = parts * 8 * 128
-    padded = jnp.pad(flat, (0, (-flat.size) % quantum)).reshape(-1, 128)
-    rows = direct_reduce_scatter(padded, "lat", jnp.float32)
-    return direct_reduce_scatter(rows, "lon", send_dtype)
+    quantum = parts * 16 * lanes
+    rows = jnp.pad(flat, (0, (-flat.size) % quantum)).reshape(-1, lanes)
+    channels, height, width = field.shape
+    count, index = lax.axis_size("lat"), lax.axis_index("lat")
+    if count == 2:
+        chunks = rows.reshape(count, -1, lanes)
+        moved, extra = piggyback_step(
+            chunks, index, count, 1, "lat", jnp.float32,
+            jnp.concatenate([field[:, height - 1, :], field[:, 0, :]], axis=1),
+        )
+        rows = lax.dynamic_index_in_dim(chunks, index, keepdims=False) + moved
+        extra = extra.reshape(channels, 2, width).astype(field.dtype)
+        field = jnp.concatenate([extra[:, :1], field, extra[:, 1:]], axis=1)
+    else:
+        rows = direct_reduce_scatter(rows, "lat", jnp.float32)
+        field = padded_2(field, (("lat", 1),), 1)
+    last, first = field[:, :, width - 1], field[:, :, 0]
+    count, index = lax.axis_size("lon"), lax.axis_index("lon")
+    if count < 3:
+        up = [(i, (i + 1) % count) for i in range(count)]
+        down = [(j, i) for i, j in up]
+        before, after = lax.ppermute(last, "lon", up), lax.ppermute(first, "lon", down)
+        rows = direct_reduce_scatter(rows, "lon", send_dtype)
+    else:
+        chunks = rows.reshape(count, -1, lanes)
+        rows = lax.dynamic_index_in_dim(chunks, index, keepdims=False)
+        for step in range(1, count):
+            extra = {1: last, count - 1: first}.get(step)
+            moved, got = piggyback_step(chunks, index, count, step, "lon", send_dtype, extra)
+            rows = rows + moved
+            if step == 1:
+                before = got.astype(field.dtype)
+            if step == count - 1:
+                after = got.astype(field.dtype)
+    return rows, jnp.concatenate([before[:, :, None], field, after[:, :, None]], axis=2)
 
 
 def sum_finish(rows, size, send_dtype):
@@ -154,8 +199,9 @@
         taps.append(jnp.stack(row_taps))
     weight_part = jnp.stack(taps)
     flat = jnp.concatenate([weight_part.reshape(-1), bias_part])
-    scattered = sum_start(flat, jnp.bfloat16)
-    grad_pre, scattered = lax.optimization_barrier((grad_pre, scattered))
+    grad_field = grad_pre.reshape(own_channels, row_count, column_count)
+    scattered, grad_pad = sum_start(flat, jnp.bfloat16, grad_field)
+    grad_pad = mask_rims(grad_pad)
     flat = sum_finish(scattered, flat.size, jnp.bfloat16)
     weight_local = flat[: weight_part.size].reshape(weight_part.shape)
     bias_grad = flat[weight_part.size :]
@@ -163,14 +209,13 @@
     weight_grad = lax.dynamic_slice_in_dim(
         doubled, (chan_count - chan_index) % chan_count * own_channels, chan_count * own_channels, axis=3
     )
-    grad_field = grad_pre.reshape(own_channels, row_count, column_count)
-    grad_pad = mask_rims(padded_2(grad_field, (("lon", 2), ("lat", 1)), 1))
     received = []
     for shift in range(1, chan_count):
         kernel_t = jnp.swapaxes(kernel_cols[shift], 2, 3)
         part = conv_taps(kernel_t, grad_pad, row_count, column_count, True)
         pairs = [(i, (i + shift) % chan_count) for i in range(chan_count)]
         received.append(lax.ppermute(part.astype(jnp.bfloat16), "chan", pairs))
+    grad_pad, received = lax.optimization_barrier((grad_pad, received))
     own_part = conv_taps(jnp.swapaxes(kernel_cols[0], 2, 3), grad_pad, row_count, column_count, True)
     for piece in received:
         own_part = own_part + piece.astype(jnp.float32)

time: 75.8 us -> 79.7 us (1.051)
  waiting for transfers between devices: 30 us -> 24.4 us
  local copies, waits for them, and re-layouts: 7.72 us -> 12.7 us
  other arithmetic: 5.38 us -> 8.79 us
  starting transfers between devices: 16.3 us -> 17.3 us
    ppermute x4 -> x2, waiting for transfers between devices: 7.29 us -> 2.19 us  [padded_2(): before = lax.ppermute(last, axis, up)]
    ppermute x4 -> x2, waiting for transfers between devices: 3.56 us -> 0.17 us  [padded_2(): after = lax.ppermute(initial, axis, down)]
    ppermute x4, starting transfers between devices: 2.15 us -> 4.97 us  [piggyback_step(): moved = lax.ppermute(piece, axis, pairs)]
    ppermute x4 -> x2, starting transfers between devices: 5.1 us -> 2.74 us  [padded_2(): after = lax.ppermute(initial, axis, down)]
    ppermute x1, waiting for transfers between devices: 8.91 us -> 10.9 us  [local(): received.append(lax.ppermute(part.astype(jnp.bfloat16), 'chan', pairs))]
    slice x0 -> x7, local copies, waits for them, and re-layouts: none -> 1.38 us  [the longest x3 0.92 us: piggyback_step(): moved[size:].reshape(-1)[:extra.size].reshape(extra.shape)]
    unnamed x11 -> x18, local copies, waits for them, and re-layouts: 3.4 us -> 4.52 us
    add x2 -> x1, other arithmetic: 0.1 us -> 1.15 us  [sum_start(): rows = lax.dynamic_index_in_dim(chunks, index, keepdims=False) + moved]
  transfers between devices with their start and end apart: 19 -> 15, of which waited for: 11 -> 8; matrix products, arithmetic and copies ran while one was open for 16% -> 19% of each run, Pallas kernels for 0% -> 0%
where the time goes in v14:
time: 79.7 us; the launch traced here: 79.4 us
  waiting for transfers between devices  24.4 us (31%)
  starting transfers between devices  17.3 us (22%)
  matrix products  14.8 us (19%)
  local copies, waits for them, and re-layouts  12.7 us (16%)
  other arithmetic  8.79 us (11%)
  between operations  1.39 us (2%)
    dot_general x36, matrix products, conv_taps(): jnp.dot(kernel[tap_row, tap_col], window, preferred_element_type=jnp.floa...  11.9 us
    ppermute x1, waiting for transfers between devices, local(): received.append(lax.ppermute(part.astype(jnp.bfloat16), 'chan', pairs))  10.9 us
    ppermute x4, waiting for transfers between devices, piggyback_step(): moved = lax.ppermute(piece, axis, pairs)  8.57 us
    ppermute x4, starting transfers between devices, piggyback_step(): moved = lax.ppermute(piece, axis, pairs)  4.97 us
    unnamed x18, local copies, waits for them, and re-layouts  4.52 us
    slice x4, local copies, waits for them, and re-layouts, window_of(): field[:, first_row:first_row + row_count, first_col:first_col + column_co...  3.63 us
    ppermute x1, starting transfers between devices, local(): raw_blocks.append(lax.ppermute(inputs, 'chan', pairs))  3 us
    dot_general x9, matrix products, local(): lax.dot_general(grad_pre, window, (((1,), (1,)), ((), ())), preferred_ele...  2.89 us
  transfers between devices with their start and end apart: 15, of which 8 were waited for; matrix products, arithmetic and copies ran while one was open for 19% of the time, Pallas kernels for 0%

profile of v14, /device:TPU:0, one launch (start us, length us, event | category | flops | bytes accessed | tf_op | source)
XLA Modules:
  0.0 79.4 jit_solution(15188369224641293116)
XLA Ops:
  0.6 1.5 %copy.26 = bf16[128,16,128]{0,2,1:T(8,128)(2,1)S(1)} copy(bf16[128,16,128]{2,1,0:T(8,128)(2,1)} %param.4) | data formatting | bytes 1048576 | tf_op args[0]
  2.2 3.0 %collective-permute-start.5 = (bf16[128,16,128]{0,2,1:T(8,128)(2,1)S(1)}, bf16[128,16,128]{0,2,1:T(8,128)(2,1)}, u32[]{:S(2)}, u32[]{:S(2)}) collective-permute-start(bf16[128,16,128]{0,2,1:T(8,128)(2,1)S(1)} %copy.26), channel_id=1, source_target_pairs={{0,2},{2,0},{1,3},{3,1},{4,6},{6,4},{5,7},{7,5},{8,10},{10,8},{9,1... | collective-permute-start | bytes 1572872 | tf_op jit(solution)/shard_map/ppermute | solution.py:166
  5.2 1.6 %collective-permute-start = (bf16[128,16,1]{0,2,1:T(2,128)(2,1)S(1)}, bf16[128,16,1]{0,2,1:T(2,128)(2,1)S(1)}, u32[]{:S(2)}, u32[]{:S(2)}) collective-permute-start(bf16[128,16,1]{0,2,1:T(2,128)(2,1)S(1)} %get-tuple-element.69), channel_id=1, source_target_pairs={{0,4},{4,8},{8,12},{12,0},{1,5},{5,9},{9,13},{13,1},{2,6},{6,10},{... | collective-permute-start | bytes 12296 | tf_op jit(solution)/shard_map/ppermute | solution.py:14
  6.8 2.2 %collective-permute-start.1 = (bf16[128,16,1]{0,2,1:T(2,128)(2,1)S(1)}, bf16[128,16,1]{0,2,1:T(2,128)(2,1)S(1)}, u32[]{:S(2)}, u32[]{:S(2)}) collective-permute-start(bf16[128,16,1]{0,2,1:T(2,128)(2,1)S(1)} %get-tuple-element.70), channel_id=1, source_target_pairs={{4,0},{8,4},{12,8},{0,12},{5,1},{9,5},{13,9},{1,13},{6,2},{10,6},{... | collective-permute-start | bytes 12296 | tf_op jit(solution)/shard_map/ppermute | solution.py:15
  9.2 1.5 %collective-permute-done = bf16[128,16,1]{0,2,1:T(2,128)(2,1)S(1)} collective-permute-done((bf16[128,16,1]{0,2,1:T(2,128)(2,1)S(1)}, bf16[128,16,1]{0,2,1:T(2,128)(2,1)S(1)}, u32[]{:S(2)}, u32[]{:S(2)}) %collective-permute-start) | collective-permute-done | bytes 4128 | tf_op jit(solution)/shard_map/ppermute | solution.py:14
  11.3 0.7 collective-permute-done.2
  12.5 0.9 %fusion.55 = (bf16[128,16,128]{0,2,1:T(8,128)(2,1)S(1)}, bf16[128,16,128]{0,2,1:T(8,128)(2,1)S(1)}, bf16[128,16,128]{0,2,1:T(8,128)(2,1)S(1)}, bf16[128,16,128]{...) fusion(bf16[128,18,130]{0,2,1:T(8,128)(2,1)S(1)} %maximum_selec, ...), kind=kLoop, calls=%fused_computation.206 | loop fusion | bytes 9437184 | tf_op jit(solution)/shard_map/slice | solution.py:37
  16.7 2.0 %collective-permute-done.4 = bf16[128,292]{0,1:T(8,128)(2,1)S(1)} collective-permute-done((bf16[128,292]{0,1:T(8,128)(2,1)S(1)}, bf16[128,292]{0,1:T(8,128)(2,1)S(1)}, u32[]{:S(2)}, u32[]{:S(2)}) %collective-permute-start.4) | collective-permute-done | bytes 74784 | tf_op jit(solution)/shard_map/ppermute | solution.py:172
  18.8 1.2 %pad_maximum_fusion.3 = bf16[128,18,130]{0,2,1:T(8,128)(2,1)S(1)} fusion(bf16[128,1,130]{0,2,1:T(8,128)(2,1)S(1)} %get-tuple-element.72, bf16[128,16,1]{0,2,1:T(2,128)(2,1)S(1)} %copy.31, bf16[128,16,128]{0,2,1:T(8,128)(2,1)} %collective-permute-done.5, bf16[128,16,1]{0,2,1:T(2,128)(2,1)S(1)} %copy.30, bf16[128,1,130]{0,2,1:T(8,128)(2,1)S(1)} %get-tuple-element.71), kind=kLoop, calls=%fused_computation.93 | loop fusion | flops 2995200 | bytes 1198080 | tf_op jit(solution)/shard_map/concatenate | solution.py:156
  20.0 0.9 %fusion.53 = (bf16[128,16,128]{0,2,1:T(8,128)(2,1)S(1)}, bf16[128,16,128]{0,2,1:T(8,128)(2,1)S(1)}, bf16[128,16,128]{0,2,1:T(8,128)(2,1)S(1)}, bf16[128,16,128]{...) fusion(bf16[128,18,130]{0,2,1:T(8,128)(2,1)S(1)} %pad_maximum_f, ...), kind=kLoop, calls=%fused_computation.204 | loop fusion | bytes 9437184 | tf_op jit(solution)/shard_map/slice | solution.py:37
  20.9 2.7 %fusion.14 = (bf16[256,16,128]{0,2,1:T(8,128)(2,1)S(1)}, bf16[256,16,128]{0,2,1:T(8,128)(2,1)S(1)}, bf16[256,16,128]{0,2,1:T(8,128)(2,1)S(1)}, bf16[256,16,128]{...) fusion(bf16[128,18,130]{0,2,1:T(8,128)(2,1)S(1)} %maximum_selec, ...), kind=kLoop, calls=%fused_computation.81 | loop fusion | flops 18874368 | bytes 10635264 | tf_op jit(solution)/shard_map/concatenate | solution.py:188
  26.4 1.0 %convert_reduce_fusion = (f32[128]{0:T(128)S(1)}, bf16[128,2048]{1,0:T(8,128)(2,1)S(1)}) fusion(f32[128]{0:T(128)S(1)} %copy-done.3, f32[128,2048]{1,0:T(8,128)S(1)} %convolution_add_fusion.24, f32[128,2048]{1,0:T(8,128)S(1)} %convolution_add_fusion.17, bf16[128,2048]{0,1:T(8,128)(2,1)S(1)} %bitcast.369, bf16[3,3,128,256]{3,2,1,0:T(8,128)(2,1)S(1)} %copy-done, ...), kind=kOutput, calls=%fused_computation.90 | convolution fusion | flops 71040896 | bytes 4228104 | tf_op jit(solution)/shard_map/dot_general | solution.py:50
  30.6 0.6 copy.48
  31.5 0.7 reshape.244
  32.3 0.8 copy-done.2
  33.0 0.9 %pad_maximum_fusion.2 = f32[1472,128]{1,0:T(8,128)} fusion(f32[256,128]{1,0:T(8,128)S(1)} %copy-done.2, f32[1216,128]{1,0:T(8,128)S(1)} %dynamic-slice_bitcast_fusion), kind=kLoop, calls=%fused_computation.91 | loop fusion | flops 188416 | bytes 1507328 | tf_op jit(solution)/shard_map/concatenate | solution.py:89
  34.4 2.1 %collective-permute-done.6 = f32[1472,128]{1,0:T(8,128)} collective-permute-done((f32[1472,128]{1,0:T(8,128)}, f32[1472,128]{1,0:T(8,128)}, u32[]{:S(2)}, u32[]{:S(2)}) %collective-permute-start.6) | collective-permute-done | bytes 753696 | tf_op jit(solution)/shard_map/ppermute | solution.py:90
  36.5 0.9 %slice.609 = bf16[256,128]{1,0:T(8,128)(2,1)S(1)} slice(f32[1472,128]{1,0:T(8,128)} %collective-permute-done.6), slice={[1216:1472], [0:128]} | slice | bytes 131072 | tf_op jit(solution)/shard_map/slice | solution.py:91
  38.1 1.1 %slice_add_fusion = f32[1216,128]{1,0:T(8,128)S(1)} fusion(f32[1472,128]{1,0:T(8,128)} %collective-permute-done.6, f32[2,1216,128]{2,1,0:T(8,128)S(1)} %bitcast.316, s32[]{:T(128)S(6)} %select_n.98), kind=kLoop, calls=%fused_computation.95 | loop fusion | flops 155648 | bytes 1867780 | tf_op jit(solution)/shard_map/add | solution.py:108
  39.3 1.9 %collective-permute-start.7 = (bf16[322,128]{1,0:T(8,128)(2,1)S(1)}, bf16[322,128]{1,0:T(8,128)(2,1)S(1)}, u32[]{:S(2)}, u32[]{:S(2)}) collective-permute-start(bf16[322,128]{1,0:T(8,128)(2,1)S(1)} %pad_maximum_fusion.4), channel_id=1, source_target_pairs={{0,4},{4,8},{8,12},{12,0},{1,5},{5,9},{9,13},{13,1},{2,6},{6,10},{... | collective-permute-start | bytes 247304 | tf_op jit(solution)/shard_map/ppermute | solution.py:90
  41.5 2.1 %collective-permute-start.8 = (bf16[322,128]{1,0:T(8,128)(2,1)S(1)}, bf16[322,128]{1,0:T(8,128)(2,1)S(1)}, u32[]{:S(2)}, u32[]{:S(2)}) collective-permute-start(bf16[322,128]{1,0:T(8,128)(2,1)S(1)} %pad_maximum_fusion.5), channel_id=1, source_target_pairs={{0,12},{4,0},{8,4},{12,8},{1,13},{5,1},{9,5},{13,9},{2,14},{6,2},{... | collective-permute-start | bytes 247304 | tf_op jit(solution)/shard_map/ppermute | solution.py:90
  43.6 1.0 %collective-permute-start.10 = (bf16[304,128]{1,0:T(8,128)(2,1)S(1)}, bf16[304,128]{1,0:T(8,128)(2,1)S(1)}, u32[]{:S(2)}, u32[]{:S(2)}) collective-permute-start(bf16[304,128]{1,0:T(8,128)(2,1)S(1)} %get-tuple-element.58), channel_id=1, source_target_pairs={{0,8},{4,12},{8,0},{12,4},{1,9},{5,13},{9,1},{13,5},{2,10},{6,14},... | collective-permute-start | bytes 233480 | tf_op jit(solution)/shard_map/ppermute | solution.py:90
  44.7 6.5 %collective-permute-done.10 = bf16[304,128]{1,0:T(8,128)(2,1)S(1)} collective-permute-done((bf16[304,128]{1,0:T(8,128)(2,1)S(1)}, bf16[304,128]{1,0:T(8,128)(2,1)S(1)}, u32[]{:S(2)}, u32[]{:S(2)}) %collective-permute-start.10) | collective-permute-done | bytes 77856 | tf_op jit(solution)/shard_map/ppermute | solution.py:90
  51.2 2.2 %collective-permute-start.11 = (bf16[304,128]{1,0:T(8,128)(2,1)S(1)}, bf16[304,128]{1,0:T(8,128)(2,1)S(1)}, u32[]{:S(2)}, u32[]{:S(2)}) collective-permute-start(bf16[304,128]{1,0:T(8,128)(2,1)S(1)} %get-tuple-element.7), channel_id=1, source_target_pairs={{0,12},{4,0},{8,4},{12,8},{1,13},{5,1},{9,5},{13,9},{2,14},{6,2},{... | collective-permute-start | bytes 233480 | tf_op jit(solution)/shard_map/ppermute | solution.py:76
  53.4 0.6 collective-permute-start.13
  54.9 0.9 %fusion.52 = (bf16[128,16,128]{0,2,1:T(8,128)(2,1)S(1)}, bf16[128,16,128]{0,2,1:T(8,128)(2,1)S(1)}, bf16[128,16,128]{0,2,1:T(8,128)(2,1)S(1)}, bf16[128,16,128]{...) fusion(bf16[128,18,130]{0,2,1:T(8,128)(2,1)S(1)} %maximum_selec, ...), kind=kLoop, calls=%fused_computation.203 | loop fusion | bytes 9437184 | tf_op jit(solution)/shard_map/slice | solution.py:37
  58.8 1.6 %collective-permute-start.9 = (bf16[128,2048]{1,0:T(8,128)(2,1)S(1)}, bf16[128,2048]{1,0:T(8,128)(2,1)S(1)}, u32[]{:S(2)}, u32[]{:S(2)}) collective-permute-start(bf16[128,2048]{1,0:T(8,128)(2,1)S(1)} %fusion.2), channel_id=1, source_target_pairs={{0,2},{2,0},{1,3},{3,1},{4,6},{6,4},{5,7},{7,5},{8,10},{10,8},{9,1... | collective-permute-start | bytes 1572872 | tf_op jit(solution)/shard_map/ppermute | solution.py:217
  60.4 0.6 collective-permute-done.12
  61.2 10.9 %collective-permute-done.9 = bf16[128,2048]{1,0:T(8,128)(2,1)S(1)} collective-permute-done((bf16[128,2048]{1,0:T(8,128)(2,1)S(1)}, bf16[128,2048]{1,0:T(8,128)(2,1)S(1)}, u32[]{:S(2)}, u32[]{:S(2)}) %collective-permute-start.9) | collective-permute-done | bytes 524320 | tf_op jit(solution)/shard_map/ppermute | solution.py:217
  72.1 0.9 %fusion.51 = (bf16[128,16,128]{0,2,1:T(8,128)(2,1)S(1)}, bf16[128,16,128]{0,2,1:T(8,128)(2,1)S(1)}, bf16[128,16,128]{0,2,1:T(8,128)(2,1)S(1)}, bf16[128,16,128]{...) fusion(bf16[128,18,130]{0,2,1:T(8,128)(2,1)S(1)} %maximum_selec, ...), kind=kLoop, calls=%fused_computation.202 | loop fusion | bytes 9437184 | tf_op jit(solution)/shard_map/slice | solution.py:37
  76.1 0.9 %copy.50 = bf16[16,8,16,128]{3,2,1,0:T(8,128)(2,1)} copy(bf16[16,8,16,128]{3,1,2,0:T(8,128)(2,1)S(1)} %fusion.21) | data formatting | bytes 1048576
  78.2 1.2 %fusion.6 = f32[3,3,128,256]{3,2,1,0:T(8,128)} fusion(s32[]{:T(128)S(6)} %select_n.114, f32[3,3,128,256]{3,2,1,0:T(8,128)S(1)} %reshape.242), kind=kLoop, calls=%fused_computation.63 | loop fusion | flops 294912 | bytes 2359300 | tf_op jit(solution)/shard_map/concatenate | solution.py:208
  (124 shorter events, 20.4 us)
Async XLA Ops:
  0.6 8.4 %copy-start.1 = (bf16[128,16,128]{2,1,0:T(8,128)(2,1)S(1)}, bf16[128,16,128]{2,1,0:T(8,128)(2,1)}, u32[]{:S(2)}) copy-start(bf16[128,16,128]{2,1,0:T(8,128)(2,1)} %param.5) | copy-start | bytes 1572868
  2.2 16.6 %collective-permute-start.5 = (bf16[128,16,128]{0,2,1:T(8,128)(2,1)S(1)}, bf16[128,16,128]{0,2,1:T(8,128)(2,1)}, u32[]{:S(2)}, u32[]{:S(2)}) collective-permute-start(bf16[128,16,128]{0,2,1:T(8,128)(2,1)S(1)} %copy.26), channel_id=1, source_target_pairs={{0,2},{2,0},{1,3},{3,1},{4,6},{6,4},{5,7},{7,5},{8,10},{10,8},{9,1... | collective-permute-start | bytes 1572872 | tf_op jit(solution)/shard_map/ppermute | solution.py:166
  5.2 5.5 %collective-permute-start = (bf16[128,16,1]{0,2,1:T(2,128)(2,1)S(1)}, bf16[128,16,1]{0,2,1:T(2,128)(2,1)S(1)}, u32[]{:S(2)}, u32[]{:S(2)}) collective-permute-start(bf16[128,16,1]{0,2,1:T(2,128)(2,1)S(1)} %get-tuple-element.69), channel_id=1, source_target_pairs={{0,4},{4,8},{8,12},{12,0},{1,5},{5,9},{9,13},{13,1},{2,6},{6,10},{... | collective-permute-start | bytes 12296 | tf_op jit(solution)/shard_map/ppermute | solution.py:14
  6.8 3.9 %collective-permute-start.1 = (bf16[128,16,1]{0,2,1:T(2,128)(2,1)S(1)}, bf16[128,16,1]{0,2,1:T(2,128)(2,1)S(1)}, u32[]{:S(2)}, u32[]{:S(2)}) collective-permute-start(bf16[128,16,1]{0,2,1:T(2,128)(2,1)S(1)} %get-tuple-element.70), channel_id=1, source_target_pairs={{4,0},{8,4},{12,8},{0,12},{5,1},{9,5},{13,9},{1,13},{6,2},{10,6},{... | collective-permute-start | bytes 12296 | tf_op jit(solution)/shard_map/ppermute | solution.py:15
  10.7 1.3 %collective-permute-start.2 = (bf16[128,1,130]{0,2,1:T(8,128)(2,1)S(1)}, bf16[128,1,130]{0,2,1:T(8,128)(2,1)S(1)}, u32[]{:S(2)}, u32[]{:S(2)}) collective-permute-start(bf16[128,1,130]{0,2,1:T(8,128)(2,1)S(1)} %get-tuple-element.65), channel_id=1, source_target_pairs={{0,1},{1,0},{2,3},{3,2},{4,5},{5,4},{6,7},{7,6},{8,9},{9,8},{10,11... | collective-permute-start | bytes 99848 | tf_op jit(solution)/shard_map/ppermute | solution.py:14
  10.8 1.4 %collective-permute-start.3 = (bf16[128,1,130]{0,2,1:T(8,128)(2,1)S(1)}, bf16[128,1,130]{0,2,1:T(8,128)(2,1)S(1)}, u32[]{:S(2)}, u32[]{:S(2)}) collective-permute-start(bf16[128,1,130]{0,2,1:T(8,128)(2,1)S(1)} %get-tuple-element.66), channel_id=1, source_target_pairs={{1,0},{0,1},{3,2},{2,3},{5,4},{4,5},{7,6},{6,7},{9,8},{8,9},{11,10... | collective-permute-start | bytes 99848 | tf_op jit(solution)/shard_map/ppermute | solution.py:15
  12.5 1.5 %copy-start = (bf16[3,3,128,256]{3,2,1,0:T(8,128)(2,1)S(1)}, bf16[3,3,128,256]{3,2,1,0:T(8,128)(2,1)}, u32[]{:S(2)}) copy-start(bf16[3,3,128,256]{3,2,1,0:T(8,128)(2,1)} %param.6) | copy-start | bytes 1769476
  13.5 5.2 %collective-permute-start.4 = (bf16[128,292]{0,1:T(8,128)(2,1)S(1)}, bf16[128,292]{0,1:T(8,128)(2,1)S(1)}, u32[]{:S(2)}, u32[]{:S(2)}) collective-permute-start(bf16[128,292]{0,1:T(8,128)(2,1)S(1)} %pad_maximum_fusion.6), channel_id=1, source_target_pairs={{0,2},{2,0},{1,3},{3,1},{4,6},{6,4},{5,7},{7,5},{8,10},{10,8},{9,1... | collective-permute-start | bytes 224264 | tf_op jit(solution)/shard_map/ppermute | solution.py:172
  25.7 0.7 copy-start.3
  32.1 0.9 %copy-start.2 = (f32[256,128]{1,0:T(8,128)S(1)}, f32[256,128]{1,0:T(8,128)}, u32[]{:S(2)}) copy-start(f32[256,128]{1,0:T(8,128)} %reshape.244) | copy-start | bytes 393220
  34.0 2.6 %collective-permute-start.6 = (f32[1472,128]{1,0:T(8,128)}, f32[1472,128]{1,0:T(8,128)}, u32[]{:S(2)}, u32[]{:S(2)}) collective-permute-start(f32[1472,128]{1,0:T(8,128)} %pad_maximum_fusion.2), channel_id=1, source_target_pairs={{0,1},{1,0},{2,3},{3,2},{4,5},{5,4},{6,7},{7,6},{8,9},{9,8},{10,11... | collective-permute-start | bytes 2261000 | tf_op jit(solution)/shard_map/ppermute | solution.py:90
  39.3 11.8 %collective-permute-start.7 = (bf16[322,128]{1,0:T(8,128)(2,1)S(1)}, bf16[322,128]{1,0:T(8,128)(2,1)S(1)}, u32[]{:S(2)}, u32[]{:S(2)}) collective-permute-start(bf16[322,128]{1,0:T(8,128)(2,1)S(1)} %pad_maximum_fusion.4), channel_id=1, source_target_pairs={{0,4},{4,8},{8,12},{12,0},{1,5},{5,9},{9,13},{13,1},{2,6},{6,10},{... | collective-permute-start | bytes 247304 | tf_op jit(solution)/shard_map/ppermute | solution.py:90
  41.5 9.6 %collective-permute-start.8 = (bf16[322,128]{1,0:T(8,128)(2,1)S(1)}, bf16[322,128]{1,0:T(8,128)(2,1)S(1)}, u32[]{:S(2)}, u32[]{:S(2)}) collective-permute-start(bf16[322,128]{1,0:T(8,128)(2,1)S(1)} %pad_maximum_fusion.5), channel_id=1, source_target_pairs={{0,12},{4,0},{8,4},{12,8},{1,13},{5,1},{9,5},{13,9},{2,14},{6,2},{... | collective-permute-start | bytes 247304 | tf_op jit(solution)/shard_map/ppermute | solution.py:90
  43.6 7.6 %collective-permute-start.10 = (bf16[304,128]{1,0:T(8,128)(2,1)S(1)}, bf16[304,128]{1,0:T(8,128)(2,1)S(1)}, u32[]{:S(2)}, u32[]{:S(2)}) collective-permute-start(bf16[304,128]{1,0:T(8,128)(2,1)S(1)} %get-tuple-element.58), channel_id=1, source_target_pairs={{0,8},{4,12},{8,0},{12,4},{1,9},{5,13},{9,1},{13,5},{2,10},{6,14},... | collective-permute-start | bytes 233480 | tf_op jit(solution)/shard_map/ppermute | solution.py:90
  51.2 9.1 %collective-permute-start.11 = (bf16[304,128]{1,0:T(8,128)(2,1)S(1)}, bf16[304,128]{1,0:T(8,128)(2,1)S(1)}, u32[]{:S(2)}, u32[]{:S(2)}) collective-permute-start(bf16[304,128]{1,0:T(8,128)(2,1)S(1)} %get-tuple-element.7), channel_id=1, source_target_pairs={{0,12},{4,0},{8,4},{12,8},{1,13},{5,1},{9,5},{13,9},{2,14},{6,2},{... | collective-permute-start | bytes 233480 | tf_op jit(solution)/shard_map/ppermute | solution.py:76
  53.4 7.6 %collective-permute-start.12 = (bf16[304,128]{1,0:T(8,128)(2,1)S(1)}, bf16[304,128]{1,0:T(8,128)(2,1)S(1)}, u32[]{:S(2)}, u32[]{:S(2)}) collective-permute-start(bf16[304,128]{1,0:T(8,128)(2,1)S(1)} %get-tuple-element.7), channel_id=1, source_target_pairs={{0,8},{4,12},{8,0},{12,4},{1,9},{5,13},{9,1},{13,5},{2,10},{6,14},... | collective-permute-start | bytes 233480 | tf_op jit(solution)/shard_map/ppermute | solution.py:76
  53.4 7.6 %collective-permute-start.13 = (bf16[304,128]{1,0:T(8,128)(2,1)S(1)}, bf16[304,128]{1,0:T(8,128)(2,1)S(1)}, u32[]{:S(2)}, u32[]{:S(2)}) collective-permute-start(bf16[304,128]{1,0:T(8,128)(2,1)S(1)} %get-tuple-element.7), channel_id=1, source_target_pairs={{0,4},{4,8},{8,12},{12,0},{1,5},{5,9},{9,13},{13,1},{2,6},{6,10},{... | collective-permute-start | bytes 233480 | tf_op jit(solution)/shard_map/ppermute | solution.py:76
  58.8 13.4 %collective-permute-start.9 = (bf16[128,2048]{1,0:T(8,128)(2,1)S(1)}, bf16[128,2048]{1,0:T(8,128)(2,1)S(1)}, u32[]{:S(2)}, u32[]{:S(2)}) collective-permute-start(bf16[128,2048]{1,0:T(8,128)(2,1)S(1)} %fusion.2), channel_id=1, source_target_pairs={{0,2},{2,0},{1,3},{3,1},{4,6},{6,4},{5,7},{7,5},{8,10},{10,8},{9,1... | collective-permute-start | bytes 1572872 | tf_op jit(solution)/shard_map/ppermute | solution.py:217
  61.2 15.9 %collective-permute-start.14 = (f32[1216,128]{1,0:T(8,128)S(1)}, f32[1216,128]{1,0:T(8,128)S(1)}, u32[]{:S(2)}, u32[]{:S(2)}) collective-permute-start(f32[1216,128]{1,0:T(8,128)S(1)} %bitcast.332), channel_id=1, source_target_pairs={{0,1},{1,0},{2,3},{3,2},{4,5},{5,4},{6,7},{7,6},{8,9},{9,8},{10,11... | collective-permute-start | bytes 1867784 | tf_op jit(solution)/shard_map/ppermute | solution.py:76

commit v15 on v14

--- a/solution.py
+++ b/solution.py
@@ -209,13 +209,15 @@
     weight_grad = lax.dynamic_slice_in_dim(
         doubled, (chan_count - chan_index) % chan_count * own_channels, chan_count * own_channels, axis=3
     )
+    outgoing = []
+    for shift in range(1, chan_count):
+        kernel_t = jnp.swapaxes(kernel_cols[shift], 2, 3)
+        outgoing.append(conv_taps(kernel_t, grad_pad, row_count, column_count, True).astype(jnp.bfloat16))
+    grad_pad, outgoing = lax.optimization_barrier((grad_pad, outgoing))
     received = []
     for shift in range(1, chan_count):
-        kernel_t = jnp.swapaxes(kernel_cols[shift], 2, 3)
-        part = conv_taps(kernel_t, grad_pad, row_count, column_count, True)
         pairs = [(i, (i + shift) % chan_count) for i in range(chan_count)]
-        received.append(lax.ppermute(part.astype(jnp.bfloat16), "chan", pairs))
-    grad_pad, received = lax.optimization_barrier((grad_pad, received))
+        received.append(lax.ppermute(outgoing[shift - 1], "chan", pairs))
     own_part = conv_taps(jnp.swapaxes(kernel_cols[0], 2, 3), grad_pad, row_count, column_count, True)
     for piece in received:
         own_part = own_part + piece.astype(jnp.float32)

time: 79.7 us -> 76.9 us (0.965)
  waiting for transfers between devices: 24.4 us -> 21.7 us
    ppermute x1, waiting for transfers between devices: 10.9 us -> 8.82 us  [local(): received.append(lax.ppermute(outgoing[shift - 1], 'chan', pairs))]
  transfers between devices with their start and end apart: 15 -> 15, of which waited for: 8 -> 7; matrix products, arithmetic and copies ran while one was open for 19% -> 19% of each run, Pallas kernels for 0% -> 0%
where the time goes in v15:
time: 76.9 us; the launch traced here: 76.7 us
  waiting for transfers between devices  21.7 us (28%)
  starting transfers between devices  17.3 us (22%)
  matrix products  14.8 us (19%)
  local copies, waits for them, and re-layouts  12.7 us (17%)
  other arithmetic  8.66 us (11%)
  between operations  1.41 us (2%)
    dot_general x36, matrix products, conv_taps(): jnp.dot(kernel[tap_row, tap_col], window, preferred_element_type=jnp.floa...  11.9 us
    ppermute x1, waiting for transfers between devices, local(): received.append(lax.ppermute(outgoing[shift - 1], 'chan', pairs))  8.82 us
    ppermute x4, waiting for transfers between devices, piggyback_step(): moved = lax.ppermute(piece, axis, pairs)  8.57 us
    ppermute x4, starting transfers between devices, piggyback_step(): moved = lax.ppermute(piece, axis, pairs)  4.97 us
    unnamed x18, local copies, waits for them, and re-layouts  4.52 us
    slice x4, local copies, waits for them, and re-layouts, window_of(): field[:, first_row:first_row + row_count, first_col:first_col + column_co...  3.64 us
    ppermute x1, starting transfers between devices, local(): raw_blocks.append(lax.ppermute(inputs, 'chan', pairs))  3 us
    dot_general x9, matrix products, local(): lax.dot_general(grad_pre, window, (((1,), (1,)), ((), ())), preferred_ele...  2.89 us
  transfers between devices with their start and end apart: 15, of which 7 were waited for; matrix products, arithmetic and copies ran while one was open for 19% of the time, Pallas kernels for 0%

profile of v15, /device:TPU:0, one launch (start us, length us, event | category | flops | bytes accessed | tf_op | source)
XLA Modules:
  0.0 76.7 jit_solution(8164614258129101264)
XLA Ops:
  0.6 1.5 %copy.26 = bf16[128,16,128]{0,2,1:T(8,128)(2,1)S(1)} copy(bf16[128,16,128]{2,1,0:T(8,128)(2,1)} %param.4) | data formatting | bytes 1048576 | tf_op args[0]
  2.2 3.0 %collective-permute-start.5 = (bf16[128,16,128]{0,2,1:T(8,128)(2,1)S(1)}, bf16[128,16,128]{0,2,1:T(8,128)(2,1)}, u32[]{:S(2)}, u32[]{:S(2)}) collective-permute-start(bf16[128,16,128]{0,2,1:T(8,128)(2,1)S(1)} %copy.26), channel_id=1, source_target_pairs={{0,2},{2,0},{1,3},{3,1},{4,6},{6,4},{5,7},{7,5},{8,10},{10,8},{9,1... | collective-permute-start | bytes 1572872 | tf_op jit(solution)/shard_map/ppermute | solution.py:166
  5.2 1.6 %collective-permute-start = (bf16[128,16,1]{0,2,1:T(2,128)(2,1)S(1)}, bf16[128,16,1]{0,2,1:T(2,128)(2,1)S(1)}, u32[]{:S(2)}, u32[]{:S(2)}) collective-permute-start(bf16[128,16,1]{0,2,1:T(2,128)(2,1)S(1)} %get-tuple-element.69), channel_id=1, source_target_pairs={{0,4},{4,8},{8,12},{12,0},{1,5},{5,9},{9,13},{13,1},{2,6},{6,10},{... | collective-permute-start | bytes 12296 | tf_op jit(solution)/shard_map/ppermute | solution.py:14
  6.8 2.2 %collective-permute-start.1 = (bf16[128,16,1]{0,2,1:T(2,128)(2,1)S(1)}, bf16[128,16,1]{0,2,1:T(2,128)(2,1)S(1)}, u32[]{:S(2)}, u32[]{:S(2)}) collective-permute-start(bf16[128,16,1]{0,2,1:T(2,128)(2,1)S(1)} %get-tuple-element.70), channel_id=1, source_target_pairs={{4,0},{8,4},{12,8},{0,12},{5,1},{9,5},{13,9},{1,13},{6,2},{10,6},{... | collective-permute-start | bytes 12296 | tf_op jit(solution)/shard_map/ppermute | solution.py:15
  9.2 1.5 %collective-permute-done = bf16[128,16,1]{0,2,1:T(2,128)(2,1)S(1)} collective-permute-done((bf16[128,16,1]{0,2,1:T(2,128)(2,1)S(1)}, bf16[128,16,1]{0,2,1:T(2,128)(2,1)S(1)}, u32[]{:S(2)}, u32[]{:S(2)}) %collective-permute-start) | collective-permute-done | bytes 4128 | tf_op jit(solution)/shard_map/ppermute | solution.py:14
  11.3 0.7 collective-permute-done.2
  12.5 0.9 %fusion.55 = (bf16[128,16,128]{0,2,1:T(8,128)(2,1)S(1)}, bf16[128,16,128]{0,2,1:T(8,128)(2,1)S(1)}, bf16[128,16,128]{0,2,1:T(8,128)(2,1)S(1)}, bf16[128,16,128]{...) fusion(bf16[128,18,130]{0,2,1:T(8,128)(2,1)S(1)} %maximum_selec, ...), kind=kLoop, calls=%fused_computation.206 | loop fusion | bytes 9437184 | tf_op jit(solution)/shard_map/slice | solution.py:37
  16.7 2.0 %collective-permute-done.4 = bf16[128,292]{0,1:T(8,128)(2,1)S(1)} collective-permute-done((bf16[128,292]{0,1:T(8,128)(2,1)S(1)}, bf16[128,292]{0,1:T(8,128)(2,1)S(1)}, u32[]{:S(2)}, u32[]{:S(2)}) %collective-permute-start.4) | collective-permute-done | bytes 74784 | tf_op jit(solution)/shard_map/ppermute | solution.py:172
  18.8 1.2 %pad_maximum_fusion.3 = bf16[128,18,130]{0,2,1:T(8,128)(2,1)S(1)} fusion(bf16[128,1,130]{0,2,1:T(8,128)(2,1)S(1)} %get-tuple-element.72, bf16[128,16,1]{0,2,1:T(2,128)(2,1)S(1)} %copy.31, bf16[128,16,128]{0,2,1:T(8,128)(2,1)} %collective-permute-done.5, bf16[128,16,1]{0,2,1:T(2,128)(2,1)S(1)} %copy.30, bf16[128,1,130]{0,2,1:T(8,128)(2,1)S(1)} %get-tuple-element.71), kind=kLoop, calls=%fused_computation.93 | loop fusion | flops 2995200 | bytes 1198080 | tf_op jit(solution)/shard_map/concatenate | solution.py:156
  20.0 0.9 %fusion.53 = (bf16[128,16,128]{0,2,1:T(8,128)(2,1)S(1)}, bf16[128,16,128]{0,2,1:T(8,128)(2,1)S(1)}, bf16[128,16,128]{0,2,1:T(8,128)(2,1)S(1)}, bf16[128,16,128]{...) fusion(bf16[128,18,130]{0,2,1:T(8,128)(2,1)S(1)} %pad_maximum_f, ...), kind=kLoop, calls=%fused_computation.204 | loop fusion | bytes 9437184 | tf_op jit(solution)/shard_map/slice | solution.py:37
  20.9 2.7 %fusion.14 = (bf16[256,16,128]{0,2,1:T(8,128)(2,1)S(1)}, bf16[256,16,128]{0,2,1:T(8,128)(2,1)S(1)}, bf16[256,16,128]{0,2,1:T(8,128)(2,1)S(1)}, bf16[256,16,128]{...) fusion(bf16[128,18,130]{0,2,1:T(8,128)(2,1)S(1)} %maximum_selec, ...), kind=kLoop, calls=%fused_computation.81 | loop fusion | flops 18874368 | bytes 10635264 | tf_op jit(solution)/shard_map/concatenate | solution.py:188
  26.4 1.0 %convert_reduce_fusion = (f32[128]{0:T(128)S(1)}, bf16[128,2048]{1,0:T(8,128)(2,1)S(1)}) fusion(f32[128]{0:T(128)S(1)} %copy-done.3, f32[128,2048]{1,0:T(8,128)S(1)} %convolution_add_fusion.24, f32[128,2048]{1,0:T(8,128)S(1)} %convolution_add_fusion.17, bf16[128,2048]{0,1:T(8,128)(2,1)S(1)} %bitcast.371, bf16[3,3,128,256]{3,2,1,0:T(8,128)(2,1)S(1)} %copy-done, ...), kind=kOutput, calls=%fused_computation.90 | convolution fusion | flops 71040896 | bytes 4228104 | tf_op jit(solution)/shard_map/dot_general | solution.py:50
  30.6 0.6 copy.48
  31.5 0.7 reshape.244
  32.3 0.8 copy-done.2
  33.0 0.9 %pad_maximum_fusion.2 = f32[1472,128]{1,0:T(8,128)} fusion(f32[256,128]{1,0:T(8,128)S(1)} %copy-done.2, f32[1216,128]{1,0:T(8,128)S(1)} %dynamic-slice_bitcast_fusion), kind=kLoop, calls=%fused_computation.91 | loop fusion | flops 188416 | bytes 1507328 | tf_op jit(solution)/shard_map/concatenate | solution.py:89
  34.4 2.1 %collective-permute-done.6 = f32[1472,128]{1,0:T(8,128)} collective-permute-done((f32[1472,128]{1,0:T(8,128)}, f32[1472,128]{1,0:T(8,128)}, u32[]{:S(2)}, u32[]{:S(2)}) %collective-permute-start.6) | collective-permute-done | bytes 753696 | tf_op jit(solution)/shard_map/ppermute | solution.py:90
  36.5 0.9 %slice.611 = bf16[256,128]{1,0:T(8,128)(2,1)S(1)} slice(f32[1472,128]{1,0:T(8,128)} %collective-permute-done.6), slice={[1216:1472], [0:128]} | slice | bytes 131072 | tf_op jit(solution)/shard_map/slice | solution.py:91
  38.1 1.1 %slice_add_fusion = f32[1216,128]{1,0:T(8,128)S(1)} fusion(f32[1472,128]{1,0:T(8,128)} %collective-permute-done.6, f32[2,1216,128]{2,1,0:T(8,128)S(1)} %bitcast.318, s32[]{:T(128)S(6)} %select_n.98), kind=kLoop, calls=%fused_computation.95 | loop fusion | flops 155648 | bytes 1867780 | tf_op jit(solution)/shard_map/add | solution.py:108
  39.3 1.9 %collective-permute-start.7 = (bf16[322,128]{1,0:T(8,128)(2,1)S(1)}, bf16[322,128]{1,0:T(8,128)(2,1)S(1)}, u32[]{:S(2)}, u32[]{:S(2)}) collective-permute-start(bf16[322,128]{1,0:T(8,128)(2,1)S(1)} %pad_maximum_fusion.4), channel_id=1, source_target_pairs={{0,4},{4,8},{8,12},{12,0},{1,5},{5,9},{9,13},{13,1},{2,6},{6,10},{... | collective-permute-start | bytes 247304 | tf_op jit(solution)/shard_map/ppermute | solution.py:90
  41.5 2.1 %collective-permute-start.8 = (bf16[322,128]{1,0:T(8,128)(2,1)S(1)}, bf16[322,128]{1,0:T(8,128)(2,1)S(1)}, u32[]{:S(2)}, u32[]{:S(2)}) collective-permute-start(bf16[322,128]{1,0:T(8,128)(2,1)S(1)} %pad_maximum_fusion.5), channel_id=1, source_target_pairs={{0,12},{4,0},{8,4},{12,8},{1,13},{5,1},{9,5},{13,9},{2,14},{6,2},{... | collective-permute-start | bytes 247304 | tf_op jit(solution)/shard_map/ppermute | solution.py:90
  43.6 1.0 %collective-permute-start.10 = (bf16[304,128]{1,0:T(8,128)(2,1)S(1)}, bf16[304,128]{1,0:T(8,128)(2,1)S(1)}, u32[]{:S(2)}, u32[]{:S(2)}) collective-permute-start(bf16[304,128]{1,0:T(8,128)(2,1)S(1)} %get-tuple-element.58), channel_id=1, source_target_pairs={{0,8},{4,12},{8,0},{12,4},{1,9},{5,13},{9,1},{13,5},{2,10},{6,14},... | collective-permute-start | bytes 233480 | tf_op jit(solution)/shard_map/ppermute | solution.py:90
  44.7 6.5 %collective-permute-done.10 = bf16[304,128]{1,0:T(8,128)(2,1)S(1)} collective-permute-done((bf16[304,128]{1,0:T(8,128)(2,1)S(1)}, bf16[304,128]{1,0:T(8,128)(2,1)S(1)}, u32[]{:S(2)}, u32[]{:S(2)}) %collective-permute-start.10) | collective-permute-done | bytes 77856 | tf_op jit(solution)/shard_map/ppermute | solution.py:90
  51.2 2.2 %collective-permute-start.11 = (bf16[304,128]{1,0:T(8,128)(2,1)S(1)}, bf16[304,128]{1,0:T(8,128)(2,1)S(1)}, u32[]{:S(2)}, u32[]{:S(2)}) collective-permute-start(bf16[304,128]{1,0:T(8,128)(2,1)S(1)} %get-tuple-element.7), channel_id=1, source_target_pairs={{0,12},{4,0},{8,4},{12,8},{1,13},{5,1},{9,5},{13,9},{2,14},{6,2},{... | collective-permute-start | bytes 233480 | tf_op jit(solution)/shard_map/ppermute | solution.py:76
  53.4 0.6 collective-permute-start.13
  54.9 0.9 %fusion.52 = (bf16[128,16,128]{0,2,1:T(8,128)(2,1)S(1)}, bf16[128,16,128]{0,2,1:T(8,128)(2,1)S(1)}, bf16[128,16,128]{0,2,1:T(8,128)(2,1)S(1)}, bf16[128,16,128]{...) fusion(bf16[128,18,130]{0,2,1:T(8,128)(2,1)S(1)} %maximum_selec, ...), kind=kLoop, calls=%fused_computation.203 | loop fusion | bytes 9437184 | tf_op jit(solution)/shard_map/slice | solution.py:37
  58.8 0.9 %fusion.51 = (bf16[128,16,128]{0,2,1:T(8,128)(2,1)S(1)}, bf16[128,16,128]{0,2,1:T(8,128)(2,1)S(1)}, bf16[128,16,128]{0,2,1:T(8,128)(2,1)S(1)}, bf16[128,16,128]{...) fusion(bf16[128,18,130]{0,2,1:T(8,128)(2,1)S(1)} %maximum_selec, ...), kind=kLoop, calls=%fused_computation.202 | loop fusion | bytes 9437184 | tf_op jit(solution)/shard_map/slice | solution.py:37
  59.7 1.6 %collective-permute-start.9 = (bf16[128,2048]{1,0:T(8,128)(2,1)S(1)}, bf16[128,2048]{1,0:T(8,128)(2,1)S(1)}, u32[]{:S(2)}, u32[]{:S(2)}) collective-permute-start(bf16[128,2048]{1,0:T(8,128)(2,1)S(1)} %fusion.2), channel_id=1, source_target_pairs={{0,2},{2,0},{1,3},{3,1},{4,6},{6,4},{5,7},{7,5},{8,10},{10,8},{9,1... | collective-permute-start | bytes 1572872 | tf_op jit(solution)/shard_map/ppermute | solution.py:220
  64.2 8.8 %collective-permute-done.9 = bf16[128,2048]{1,0:T(8,128)(2,1)S(1)} collective-permute-done((bf16[128,2048]{1,0:T(8,128)(2,1)S(1)}, bf16[128,2048]{1,0:T(8,128)(2,1)S(1)}, u32[]{:S(2)}, u32[]{:S(2)}) %collective-permute-start.9) | collective-permute-done | bytes 524320 | tf_op jit(solution)/shard_map/ppermute | solution.py:220
  73.4 0.9 %copy.50 = bf16[16,8,16,128]{3,2,1,0:T(8,128)(2,1)} copy(bf16[16,8,16,128]{3,1,2,0:T(8,128)(2,1)S(1)} %fusion.21) | data formatting | bytes 1048576
  74.6 0.5 slice.514
  75.5 1.2 %fusion.6 = f32[3,3,128,256]{3,2,1,0:T(8,128)} fusion(s32[]{:T(128)S(6)} %select_n.114, f32[3,3,128,256]{3,2,1,0:T(8,128)S(1)} %reshape.242), kind=kLoop, calls=%fused_computation.63 | loop fusion | flops 294912 | bytes 2359300 | tf_op jit(solution)/shard_map/concatenate | solution.py:208
  (123 shorter events, 19.8 us)
Async XLA Ops:
  0.6 8.4 %copy-start.1 = (bf16[128,16,128]{2,1,0:T(8,128)(2,1)S(1)}, bf16[128,16,128]{2,1,0:T(8,128)(2,1)}, u32[]{:S(2)}) copy-start(bf16[128,16,128]{2,1,0:T(8,128)(2,1)} %param.5) | copy-start | bytes 1572868
  2.2 16.6 %collective-permute-start.5 = (bf16[128,16,128]{0,2,1:T(8,128)(2,1)S(1)}, bf16[128,16,128]{0,2,1:T(8,128)(2,1)}, u32[]{:S(2)}, u32[]{:S(2)}) collective-permute-start(bf16[128,16,128]{0,2,1:T(8,128)(2,1)S(1)} %copy.26), channel_id=1, source_target_pairs={{0,2},{2,0},{1,3},{3,1},{4,6},{6,4},{5,7},{7,5},{8,10},{10,8},{9,1... | collective-permute-start | bytes 1572872 | tf_op jit(solution)/shard_map/ppermute | solution.py:166
  5.2 5.5 %collective-permute-start = (bf16[128,16,1]{0,2,1:T(2,128)(2,1)S(1)}, bf16[128,16,1]{0,2,1:T(2,128)(2,1)S(1)}, u32[]{:S(2)}, u32[]{:S(2)}) collective-permute-start(bf16[128,16,1]{0,2,1:T(2,128)(2,1)S(1)} %get-tuple-element.69), channel_id=1, source_target_pairs={{0,4},{4,8},{8,12},{12,0},{1,5},{5,9},{9,13},{13,1},{2,6},{6,10},{... | collective-permute-start | bytes 12296 | tf_op jit(solution)/shard_map/ppermute | solution.py:14
  6.8 3.9 %collective-permute-start.1 = (bf16[128,16,1]{0,2,1:T(2,128)(2,1)S(1)}, bf16[128,16,1]{0,2,1:T(2,128)(2,1)S(1)}, u32[]{:S(2)}, u32[]{:S(2)}) collective-permute-start(bf16[128,16,1]{0,2,1:T(2,128)(2,1)S(1)} %get-tuple-element.70), channel_id=1, source_target_pairs={{4,0},{8,4},{12,8},{0,12},{5,1},{9,5},{13,9},{1,13},{6,2},{10,6},{... | collective-permute-start | bytes 12296 | tf_op jit(solution)/shard_map/ppermute | solution.py:15
  10.7 1.3 %collective-permute-start.2 = (bf16[128,1,130]{0,2,1:T(8,128)(2,1)S(1)}, bf16[128,1,130]{0,2,1:T(8,128)(2,1)S(1)}, u32[]{:S(2)}, u32[]{:S(2)}) collective-permute-start(bf16[128,1,130]{0,2,1:T(8,128)(2,1)S(1)} %get-tuple-element.65), channel_id=1, source_target_pairs={{0,1},{1,0},{2,3},{3,2},{4,5},{5,4},{6,7},{7,6},{8,9},{9,8},{10,11... | collective-permute-start | bytes 99848 | tf_op jit(solution)/shard_map/ppermute | solution.py:14
  10.8 1.4 %collective-permute-start.3 = (bf16[128,1,130]{0,2,1:T(8,128)(2,1)S(1)}, bf16[128,1,130]{0,2,1:T(8,128)(2,1)S(1)}, u32[]{:S(2)}, u32[]{:S(2)}) collective-permute-start(bf16[128,1,130]{0,2,1:T(8,128)(2,1)S(1)} %get-tuple-element.66), channel_id=1, source_target_pairs={{1,0},{0,1},{3,2},{2,3},{5,4},{4,5},{7,6},{6,7},{9,8},{8,9},{11,10... | collective-permute-start | bytes 99848 | tf_op jit(solution)/shard_map/ppermute | solution.py:15
  12.5 1.5 %copy-start = (bf16[3,3,128,256]{3,2,1,0:T(8,128)(2,1)S(1)}, bf16[3,3,128,256]{3,2,1,0:T(8,128)(2,1)}, u32[]{:S(2)}) copy-start(bf16[3,3,128,256]{3,2,1,0:T(8,128)(2,1)} %param.6) | copy-start | bytes 1769476
  13.5 5.2 %collective-permute-start.4 = (bf16[128,292]{0,1:T(8,128)(2,1)S(1)}, bf16[128,292]{0,1:T(8,128)(2,1)S(1)}, u32[]{:S(2)}, u32[]{:S(2)}) collective-permute-start(bf16[128,292]{0,1:T(8,128)(2,1)S(1)} %pad_maximum_fusion.6), channel_id=1, source_target_pairs={{0,2},{2,0},{1,3},{3,1},{4,6},{6,4},{5,7},{7,5},{8,10},{10,8},{9,1... | collective-permute-start | bytes 224264 | tf_op jit(solution)/shard_map/ppermute | solution.py:172
  25.7 0.7 copy-start.3
  32.1 0.9 %copy-start.2 = (f32[256,128]{1,0:T(8,128)S(1)}, f32[256,128]{1,0:T(8,128)}, u32[]{:S(2)}) copy-start(f32[256,128]{1,0:T(8,128)} %reshape.244) | copy-start | bytes 393220
  34.0 2.6 %collective-permute-start.6 = (f32[1472,128]{1,0:T(8,128)}, f32[1472,128]{1,0:T(8,128)}, u32[]{:S(2)}, u32[]{:S(2)}) collective-permute-start(f32[1472,128]{1,0:T(8,128)} %pad_maximum_fusion.2), channel_id=1, source_target_pairs={{0,1},{1,0},{2,3},{3,2},{4,5},{5,4},{6,7},{7,6},{8,9},{9,8},{10,11... | collective-permute-start | bytes 2261000 | tf_op jit(solution)/shard_map/ppermute | solution.py:90
  39.3 11.8 %collective-permute-start.7 = (bf16[322,128]{1,0:T(8,128)(2,1)S(1)}, bf16[322,128]{1,0:T(8,128)(2,1)S(1)}, u32[]{:S(2)}, u32[]{:S(2)}) collective-permute-start(bf16[322,128]{1,0:T(8,128)(2,1)S(1)} %pad_maximum_fusion.4), channel_id=1, source_target_pairs={{0,4},{4,8},{8,12},{12,0},{1,5},{5,9},{9,13},{13,1},{2,6},{6,10},{... | collective-permute-start | bytes 247304 | tf_op jit(solution)/shard_map/ppermute | solution.py:90
  41.5 9.6 %collective-permute-start.8 = (bf16[322,128]{1,0:T(8,128)(2,1)S(1)}, bf16[322,128]{1,0:T(8,128)(2,1)S(1)}, u32[]{:S(2)}, u32[]{:S(2)}) collective-permute-start(bf16[322,128]{1,0:T(8,128)(2,1)S(1)} %pad_maximum_fusion.5), channel_id=1, source_target_pairs={{0,12},{4,0},{8,4},{12,8},{1,13},{5,1},{9,5},{13,9},{2,14},{6,2},{... | collective-permute-start | bytes 247304 | tf_op jit(solution)/shard_map/ppermute | solution.py:90
  43.6 7.6 %collective-permute-start.10 = (bf16[304,128]{1,0:T(8,128)(2,1)S(1)}, bf16[304,128]{1,0:T(8,128)(2,1)S(1)}, u32[]{:S(2)}, u32[]{:S(2)}) collective-permute-start(bf16[304,128]{1,0:T(8,128)(2,1)S(1)} %get-tuple-element.58), channel_id=1, source_target_pairs={{0,8},{4,12},{8,0},{12,4},{1,9},{5,13},{9,1},{13,5},{2,10},{6,14},... | collective-permute-start | bytes 233480 | tf_op jit(solution)/shard_map/ppermute | solution.py:90
  51.2 12.0 %collective-permute-start.11 = (bf16[304,128]{1,0:T(8,128)(2,1)S(1)}, bf16[304,128]{1,0:T(8,128)(2,1)S(1)}, u32[]{:S(2)}, u32[]{:S(2)}) collective-permute-start(bf16[304,128]{1,0:T(8,128)(2,1)S(1)} %get-tuple-element.7), channel_id=1, source_target_pairs={{0,12},{4,0},{8,4},{12,8},{1,13},{5,1},{9,5},{13,9},{2,14},{6,2},{... | collective-permute-start | bytes 233480 | tf_op jit(solution)/shard_map/ppermute | solution.py:76
  53.4 9.9 %collective-permute-start.12 = (bf16[304,128]{1,0:T(8,128)(2,1)S(1)}, bf16[304,128]{1,0:T(8,128)(2,1)S(1)}, u32[]{:S(2)}, u32[]{:S(2)}) collective-permute-start(bf16[304,128]{1,0:T(8,128)(2,1)S(1)} %get-tuple-element.7), channel_id=1, source_target_pairs={{0,8},{4,12},{8,0},{12,4},{1,9},{5,13},{9,1},{13,5},{2,10},{6,14},... | collective-permute-start | bytes 233480 | tf_op jit(solution)/shard_map/ppermute | solution.py:76
  53.4 9.9 %collective-permute-start.13 = (bf16[304,128]{1,0:T(8,128)(2,1)S(1)}, bf16[304,128]{1,0:T(8,128)(2,1)S(1)}, u32[]{:S(2)}, u32[]{:S(2)}) collective-permute-start(bf16[304,128]{1,0:T(8,128)(2,1)S(1)} %get-tuple-element.7), channel_id=1, source_target_pairs={{0,4},{4,8},{8,12},{12,0},{1,5},{5,9},{9,13},{13,1},{2,6},{6,10},{... | collective-permute-start | bytes 233480 | tf_op jit(solution)/shard_map/ppermute | solution.py:76
  59.7 13.4 %collective-permute-start.9 = (bf16[128,2048]{1,0:T(8,128)(2,1)S(1)}, bf16[128,2048]{1,0:T(8,128)(2,1)S(1)}, u32[]{:S(2)}, u32[]{:S(2)}) collective-permute-start(bf16[128,2048]{1,0:T(8,128)(2,1)S(1)} %fusion.2), channel_id=1, source_target_pairs={{0,2},{2,0},{1,3},{3,1},{4,6},{6,4},{5,7},{7,5},{8,10},{10,8},{9,1... | collective-permute-start | bytes 1572872 | tf_op jit(solution)/shard_map/ppermute | solution.py:220
  63.5 10.8 %collective-permute-start.14 = (f32[1216,128]{1,0:T(8,128)S(1)}, f32[1216,128]{1,0:T(8,128)S(1)}, u32[]{:S(2)}, u32[]{:S(2)}) collective-permute-start(f32[1216,128]{1,0:T(8,128)S(1)} %bitcast.334), channel_id=1, source_target_pairs={{0,1},{1,0},{2,3},{3,2},{4,5},{5,4},{6,7},{7,6},{8,9},{9,8},{10,11... | collective-permute-start | bytes 1867784 | tf_op jit(solution)/shard_map/ppermute | solution.py:76

commit v16 on v11

--- a/solution.py
+++ b/solution.py
@@ -187,12 +187,15 @@
     )
     grad_wide = jnp.concatenate([before, grad_field, after], axis=2)
     grad_pad = mask_rims(padded_2(grad_wide, (("lat", 1),), 1))
+    outgoing = []
+    for shift in range(1, chan_count):
+        kernel_t = jnp.swapaxes(kernel_cols[shift], 2, 3)
+        outgoing.append(conv_taps(kernel_t, grad_pad, row_count, column_count, True).astype(jnp.bfloat16))
+    grad_pad, outgoing = lax.optimization_barrier((grad_pad, outgoing))
     received = []
     for shift in range(1, chan_count):
-        kernel_t = jnp.swapaxes(kernel_cols[shift], 2, 3)
-        part = conv_taps(kernel_t, grad_pad, row_count, column_count, True)
         pairs = [(i, (i + shift) % chan_count) for i in range(chan_count)]
-        received.append(lax.ppermute(part.astype(jnp.bfloat16), "chan", pairs))
+        received.append(lax.ppermute(outgoing[shift - 1], "chan", pairs))
     own_part = conv_taps(jnp.swapaxes(kernel_cols[0], 2, 3), grad_pad, row_count, column_count, True)
     for piece in received:
         own_part = own_part + piece.astype(jnp.float32)

time: 71.5 us -> 70.3 us (0.983)
  waiting for transfers between devices: 21.3 us -> 19 us
  local copies, waits for them, and re-layouts: 9.36 us -> 10.3 us
    ppermute x1, waiting for transfers between devices: 10.8 us -> 8.51 us  [local(): received.append(lax.ppermute(outgoing[shift - 1], 'chan', pairs))]
    slice x3 -> x4, local copies, waits for them, and re-layouts: 2.81 us -> 3.74 us  [window_of(): field[:, first_row:first_row + row_count, first_col:first_col + column_co...]
  transfers between devices with their start and end apart: 17 -> 17, of which waited for: 9 -> 9; matrix products, arithmetic and copies ran while one was open for 20% -> 22% of each run, Pallas kernels for 0% -> 0%
where the time goes in v16:
time: 70.3 us; the launch traced here: 70.1 us
  waiting for transfers between devices  19 us (27%)
  starting transfers between devices  17.9 us (25%)
  matrix products  14.7 us (21%)
  local copies, waits for them, and re-layouts  10.3 us (15%)
  other arithmetic  6.65 us (9%)
  between operations  1.47 us (2%)
    dot_general x36, matrix products, conv_taps(): jnp.dot(kernel[tap_row, tap_col], window, preferred_element_type=jnp.floa...  11.9 us
    ppermute x1, waiting for transfers between devices, local(): received.append(lax.ppermute(outgoing[shift - 1], 'chan', pairs))  8.51 us
    ppermute x3, waiting for transfers between devices, sum_start(): moved = lax.ppermute(piece, 'lon', pairs)  5.21 us
    ppermute x3, starting transfers between devices, sum_start(): moved = lax.ppermute(piece, 'lon', pairs)  4.99 us
    slice x4, local copies, waits for them, and re-layouts, window_of(): field[:, first_row:first_row + row_count, first_col:first_col + column_co...  3.74 us
    unnamed x12, local copies, waits for them, and re-layouts  3.51 us
    ppermute x1, starting transfers between devices, local(): raw_blocks.append(lax.ppermute(inputs, 'chan', pairs))  3 us
    dot_general x9, matrix products, local(): lax.dot_general(grad_pre, window, (((1,), (1,)), ((), ())), preferred_ele...  2.85 us
  transfers between devices with their start and end apart: 17, of which 9 were waited for; matrix products, arithmetic and copies ran while one was open for 22% of the time, Pallas kernels for 0%

profile of v16, /device:TPU:0, one launch (start us, length us, event | category | flops | bytes accessed | tf_op | source)
XLA Modules:
  0.0 70.1 jit_solution(10327972484089570942)
XLA Ops:
  0.6 1.5 %copy.12 = bf16[128,16,128]{0,2,1:T(8,128)(2,1)S(1)} copy(bf16[128,16,128]{2,1,0:T(8,128)(2,1)} %param.4) | data formatting | bytes 1048576 | tf_op args[0]
  2.2 3.0 %collective-permute-start.5 = (bf16[128,16,128]{0,2,1:T(8,128)(2,1)S(1)}, bf16[128,16,128]{0,2,1:T(8,128)(2,1)S(1)}, u32[]{:S(2)}, u32[]{:S(2)}) collective-permute-start(bf16[128,16,128]{0,2,1:T(8,128)(2,1)S(1)} %copy.12), channel_id=1, source_target_pairs={{0,2},{2,0},{1,3},{3,1},{4,6},{6,4},{5,7},{7,5},{8,10},{10,8},{9,1... | collective-permute-start | bytes 1572872 | tf_op jit(solution)/shard_map/ppermute | solution.py:142
  5.2 1.6 %collective-permute-start = (bf16[128,16,1]{0,2,1:T(2,128)(2,1)S(1)}, bf16[128,16,1]{0,2,1:T(2,128)(2,1)S(1)}, u32[]{:S(2)}, u32[]{:S(2)}) collective-permute-start(bf16[128,16,1]{0,2,1:T(2,128)(2,1)S(1)} %get-tuple-element.69), channel_id=1, source_target_pairs={{0,4},{4,8},{8,12},{12,0},{1,5},{5,9},{9,13},{13,1},{2,6},{6,10},{... | collective-permute-start | bytes 12296 | tf_op jit(solution)/shard_map/ppermute | solution.py:14
  6.8 2.2 %collective-permute-start.1 = (bf16[128,16,1]{0,2,1:T(2,128)(2,1)S(1)}, bf16[128,16,1]{0,2,1:T(2,128)(2,1)S(1)}, u32[]{:S(2)}, u32[]{:S(2)}) collective-permute-start(bf16[128,16,1]{0,2,1:T(2,128)(2,1)S(1)} %get-tuple-element.70), channel_id=1, source_target_pairs={{4,0},{8,4},{12,8},{0,12},{5,1},{9,5},{13,9},{1,13},{6,2},{10,6},{... | collective-permute-start | bytes 12296 | tf_op jit(solution)/shard_map/ppermute | solution.py:15
  9.2 1.5 %collective-permute-done = bf16[128,16,1]{0,2,1:T(2,128)(2,1)S(1)} collective-permute-done((bf16[128,16,1]{0,2,1:T(2,128)(2,1)S(1)}, bf16[128,16,1]{0,2,1:T(2,128)(2,1)S(1)}, u32[]{:S(2)}, u32[]{:S(2)}) %collective-permute-start) | collective-permute-done | bytes 4128 | tf_op jit(solution)/shard_map/ppermute | solution.py:14
  10.8 0.5 collective-permute-start.3
  11.3 0.7 collective-permute-done.2
  12.5 0.9 %fusion.55 = (bf16[128,16,128]{0,2,1:T(8,128)(2,1)S(1)}, bf16[128,16,128]{0,2,1:T(8,128)(2,1)S(1)}, bf16[128,16,128]{0,2,1:T(8,128)(2,1)S(1)}, bf16[128,16,128]{...) fusion(bf16[128,18,130]{0,2,1:T(8,128)(2,1)S(1)} %maximum_selec, ...), kind=kLoop, calls=%fused_computation.203 | loop fusion | bytes 9437184 | tf_op jit(solution)/shard_map/slice | solution.py:37
  16.7 2.0 %collective-permute-done.4 = bf16[128,292]{0,1:T(8,128)(2,1)S(1)} collective-permute-done((bf16[128,292]{0,1:T(8,128)(2,1)S(1)}, bf16[128,292]{0,1:T(8,128)(2,1)S(1)}, u32[]{:S(2)}, u32[]{:S(2)}) %collective-permute-start.4) | collective-permute-done | bytes 74784 | tf_op jit(solution)/shard_map/ppermute | solution.py:148
  19.0 1.0 %fusion.53 = (bf16[128,16,128]{0,2,1:T(8,128)(2,1)S(1)}, bf16[128,16,128]{0,2,1:T(8,128)(2,1)S(1)}, bf16[128,16,128]{0,2,1:T(8,128)(2,1)S(1)}, bf16[128,16,128]{...) fusion(bf16[128,18,130]{0,2,1:T(8,128)(2,1)S(1)} %pad_maximum_f, ...), kind=kLoop, calls=%fused_computation.201 | loop fusion | bytes 9437184 | tf_op jit(solution)/shard_map/slice | solution.py:37
  19.9 2.5 %fusion.14 = (bf16[256,16,128]{0,2,1:T(8,128)(2,1)S(1)}, bf16[256,16,128]{0,2,1:T(8,128)(2,1)S(1)}, bf16[256,16,128]{0,2,1:T(8,128)(2,1)S(1)}, bf16[256,16,128]{...) fusion(bf16[128,18,130]{0,2,1:T(8,128)(2,1)S(1)} %maximum_selec, ...), kind=kLoop, calls=%fused_computation.81 | loop fusion | flops 18874368 | bytes 10635264 | tf_op jit(solution)/shard_map/concatenate | solution.py:164
  25.3 1.0 %convert_reduce_fusion = (f32[128]{0:T(128)S(1)}, bf16[128,2048]{1,0:T(8,128)(2,1)S(1)}) fusion(f32[128]{0:T(128)S(1)} %copy-done.2, f32[128,2048]{1,0:T(8,128)S(1)} %convolution_add_fusion.24, f32[128,2048]{1,0:T(8,128)S(1)} %convolution_add_fusion.17, bf16[128,2048]{0,1:T(8,128)(2,1)S(1)} %bitcast.358, bf16[3,3,128,256]{3,2,1,0:T(8,128)(2,1)S(1)} %copy-done, ...), kind=kOutput, calls=%fused_computation.90 | convolution fusion | flops 71040896 | bytes 4228104 | tf_op jit(solution)/shard_map/dot_general | solution.py:50
  29.4 0.6 copy.28
  30.5 0.8 %slice_reduce_fusion.1 = (bf16[128,16]{1,0:T(8,128)(2,1)S(1)}, bf16[128,16]{1,0:T(8,128)(2,1)S(1)}) fusion(bf16[128,16,128]{2,1,0:T(8,128)(2,1)S(1)} %bitcast.304), kind=kLoop, calls=%fused_computation.98 | loop fusion | bytes 16384 | tf_op jit(solution)/shard_map/slice | solution.py:179
  31.5 0.9 %collective-permute-done.6 = f32[1216,128]{1,0:T(8,128)} collective-permute-done((f32[1216,128]{1,0:T(8,128)S(1)}, f32[1216,128]{1,0:T(8,128)}, u32[]{:S(2)}, u32[]{:S(2)}) %collective-permute-start.6) | collective-permute-done | bytes 622624 | tf_op jit(solution)/shard_map/ppermute | solution.py:64
  32.4 1.1 %bitcast_add_fusion = f32[1216,128]{1,0:T(8,128)S(1)} fusion(f32[1216,128]{1,0:T(8,128)} %collective-permute-done.6, f32[2,1216,128]{2,1,0:T(8,128)S(1)} %bitcast.307, s32[]{:T(128)S(6)} %select_n.98), kind=kLoop, calls=%fused_computation.94 | loop fusion | flops 155648 | bytes 1867780 | tf_op jit(solution)/shard_map/add | solution.py:64
  33.6 1.9 %collective-permute-start.7 = (bf16[320,128]{1,0:T(8,128)(2,1)S(1)}, bf16[320,128]{1,0:T(8,128)(2,1)S(1)}, u32[]{:S(2)}, u32[]{:S(2)}) collective-permute-start(bf16[320,128]{1,0:T(8,128)(2,1)S(1)} %pad_maximum_fusion.3), channel_id=1, source_target_pairs={{0,4},{4,8},{8,12},{12,0},{1,5},{5,9},{9,13},{13,1},{2,6},{6,10},{... | collective-permute-start | bytes 245768 | tf_op jit(solution)/shard_map/ppermute | solution.py:104
  35.5 2.3 %collective-permute-start.8 = (bf16[320,128]{1,0:T(8,128)(2,1)S(1)}, bf16[320,128]{1,0:T(8,128)(2,1)S(1)}, u32[]{:S(2)}, u32[]{:S(2)}) collective-permute-start(bf16[320,128]{1,0:T(8,128)(2,1)S(1)} %pad_maximum_fusion.4), channel_id=1, source_target_pairs={{0,12},{4,0},{8,4},{12,8},{1,13},{5,1},{9,5},{13,9},{2,14},{6,2},{... | collective-permute-start | bytes 245768 | tf_op jit(solution)/shard_map/ppermute | solution.py:104
  38.4 0.8 %collective-permute-start.12 = (bf16[304,128]{1,0:T(8,128)(2,1)S(1)}, bf16[304,128]{1,0:T(8,128)(2,1)S(1)}, u32[]{:S(2)}, u32[]{:S(2)}) collective-permute-start(bf16[304,128]{1,0:T(8,128)(2,1)S(1)} %get-tuple-element.60), channel_id=1, source_target_pairs={{0,8},{4,12},{8,0},{12,4},{1,9},{5,13},{9,1},{13,5},{2,10},{6,14},... | collective-permute-start | bytes 233480 | tf_op jit(solution)/shard_map/ppermute | solution.py:104
  39.2 1.4 %collective-permute-done.7 = bf16[320,128]{1,0:T(8,128)(2,1)S(1)} collective-permute-done((bf16[320,128]{1,0:T(8,128)(2,1)S(1)}, bf16[320,128]{1,0:T(8,128)(2,1)S(1)}, u32[]{:S(2)}, u32[]{:S(2)}) %collective-permute-start.7) | collective-permute-done | bytes 81952 | tf_op jit(solution)/shard_map/ppermute | solution.py:104
  40.7 0.7 %collective-permute-done.8 = bf16[320,128]{1,0:T(8,128)(2,1)S(1)} collective-permute-done((bf16[320,128]{1,0:T(8,128)(2,1)S(1)}, bf16[320,128]{1,0:T(8,128)(2,1)S(1)}, u32[]{:S(2)}, u32[]{:S(2)}) %collective-permute-start.8) | collective-permute-done | bytes 81952 | tf_op jit(solution)/shard_map/ppermute | solution.py:104
  41.8 0.5 collective-permute-start.9
  42.3 3.1 %collective-permute-done.12 = bf16[304,128]{1,0:T(8,128)(2,1)S(1)} collective-permute-done((bf16[304,128]{1,0:T(8,128)(2,1)S(1)}, bf16[304,128]{1,0:T(8,128)(2,1)S(1)}, u32[]{:S(2)}, u32[]{:S(2)}) %collective-permute-start.12) | collective-permute-done | bytes 77856 | tf_op jit(solution)/shard_map/ppermute | solution.py:104
  45.4 2.1 %collective-permute-start.13 = (bf16[304,128]{1,0:T(8,128)(2,1)S(1)}, bf16[304,128]{1,0:T(8,128)(2,1)S(1)}, u32[]{:S(2)}, u32[]{:S(2)}) collective-permute-start(bf16[304,128]{1,0:T(8,128)(2,1)S(1)} %get-tuple-element.9), channel_id=1, source_target_pairs={{0,12},{4,0},{8,4},{12,8},{1,13},{5,1},{9,5},{13,9},{2,14},{6,2},{... | collective-permute-start | bytes 233480 | tf_op jit(solution)/shard_map/ppermute | solution.py:76
  47.5 0.6 collective-permute-start.15
  48.5 0.9 %fusion.52 = (bf16[128,16,128]{0,2,1:T(8,128)(2,1)S(1)}, bf16[128,16,128]{0,2,1:T(8,128)(2,1)S(1)}, bf16[128,16,128]{0,2,1:T(8,128)(2,1)S(1)}, bf16[128,16,128]{...) fusion(bf16[128,18,130]{0,2,1:T(8,128)(2,1)S(1)} %maximum_selec, ...), kind=kLoop, calls=%fused_computation.200 | loop fusion | bytes 9437184 | tf_op jit(solution)/shard_map/slice | solution.py:37
  52.4 0.9 %fusion.51 = (bf16[128,16,128]{0,2,1:T(8,128)(2,1)S(1)}, bf16[128,16,128]{0,2,1:T(8,128)(2,1)S(1)}, bf16[128,16,128]{0,2,1:T(8,128)(2,1)S(1)}, bf16[128,16,128]{...) fusion(bf16[128,18,130]{0,2,1:T(8,128)(2,1)S(1)} %maximum_selec, ...), kind=kLoop, calls=%fused_computation.199 | loop fusion | bytes 9437184 | tf_op jit(solution)/shard_map/slice | solution.py:37
  53.3 1.6 %collective-permute-start.11 = (bf16[128,2048]{1,0:T(8,128)(2,1)S(1)}, bf16[128,2048]{1,0:T(8,128)(2,1)S(1)}, u32[]{:S(2)}, u32[]{:S(2)}) collective-permute-start(bf16[128,2048]{1,0:T(8,128)(2,1)S(1)} %fusion.2), channel_id=1, source_target_pairs={{0,2},{2,0},{1,3},{3,1},{4,6},{6,4},{5,7},{7,5},{8,10},{10,8},{9,1... | collective-permute-start | bytes 1572872 | tf_op jit(solution)/shard_map/ppermute | solution.py:198
  58.1 8.5 %collective-permute-done.11 = bf16[128,2048]{1,0:T(8,128)(2,1)S(1)} collective-permute-done((bf16[128,2048]{1,0:T(8,128)(2,1)S(1)}, bf16[128,2048]{1,0:T(8,128)(2,1)S(1)}, u32[]{:S(2)}, u32[]{:S(2)}) %collective-permute-start.11) | collective-permute-done | bytes 524320 | tf_op jit(solution)/shard_map/ppermute | solution.py:198
  66.8 0.9 %copy.30 = bf16[16,8,16,128]{3,2,1,0:T(8,128)(2,1)} copy(bf16[16,8,16,128]{3,1,2,0:T(8,128)(2,1)S(1)} %fusion.21) | data formatting | bytes 1048576
  68.1 0.5 slice.493
  68.9 1.2 %fusion.6 = f32[3,3,128,256]{3,2,1,0:T(8,128)} fusion(s32[]{:T(128)S(6)} %select_n.114, f32[3,3,128,256]{3,2,1,0:T(8,128)S(1)} %reshape.241), kind=kLoop, calls=%fused_computation.63 | loop fusion | flops 294912 | bytes 2359300 | tf_op jit(solution)/shard_map/concatenate | solution.py:184
  (115 shorter events, 18.7 us)
Async XLA Ops:
  0.6 8.4 %copy-start.1 = (bf16[128,16,128]{2,1,0:T(8,128)(2,1)S(1)}, bf16[128,16,128]{2,1,0:T(8,128)(2,1)}, u32[]{:S(2)}) copy-start(bf16[128,16,128]{2,1,0:T(8,128)(2,1)} %param.5) | copy-start | bytes 1572868
  2.2 16.6 %collective-permute-start.5 = (bf16[128,16,128]{0,2,1:T(8,128)(2,1)S(1)}, bf16[128,16,128]{0,2,1:T(8,128)(2,1)S(1)}, u32[]{:S(2)}, u32[]{:S(2)}) collective-permute-start(bf16[128,16,128]{0,2,1:T(8,128)(2,1)S(1)} %copy.12), channel_id=1, source_target_pairs={{0,2},{2,0},{1,3},{3,1},{4,6},{6,4},{5,7},{7,5},{8,10},{10,8},{9,1... | collective-permute-start | bytes 1572872 | tf_op jit(solution)/shard_map/ppermute | solution.py:142
  5.2 5.5 %collective-permute-start = (bf16[128,16,1]{0,2,1:T(2,128)(2,1)S(1)}, bf16[128,16,1]{0,2,1:T(2,128)(2,1)S(1)}, u32[]{:S(2)}, u32[]{:S(2)}) collective-permute-start(bf16[128,16,1]{0,2,1:T(2,128)(2,1)S(1)} %get-tuple-element.69), channel_id=1, source_target_pairs={{0,4},{4,8},{8,12},{12,0},{1,5},{5,9},{9,13},{13,1},{2,6},{6,10},{... | collective-permute-start | bytes 12296 | tf_op jit(solution)/shard_map/ppermute | solution.py:14
  6.8 3.9 %collective-permute-start.1 = (bf16[128,16,1]{0,2,1:T(2,128)(2,1)S(1)}, bf16[128,16,1]{0,2,1:T(2,128)(2,1)S(1)}, u32[]{:S(2)}, u32[]{:S(2)}) collective-permute-start(bf16[128,16,1]{0,2,1:T(2,128)(2,1)S(1)} %get-tuple-element.70), channel_id=1, source_target_pairs={{4,0},{8,4},{12,8},{0,12},{5,1},{9,5},{13,9},{1,13},{6,2},{10,6},{... | collective-permute-start | bytes 12296 | tf_op jit(solution)/shard_map/ppermute | solution.py:15
  10.7 1.3 %collective-permute-start.2 = (bf16[128,1,130]{0,2,1:T(8,128)(2,1)S(1)}, bf16[128,1,130]{0,2,1:T(8,128)(2,1)S(1)}, u32[]{:S(2)}, u32[]{:S(2)}) collective-permute-start(bf16[128,1,130]{0,2,1:T(8,128)(2,1)S(1)} %get-tuple-element.67), channel_id=1, source_target_pairs={{0,1},{1,0},{2,3},{3,2},{4,5},{5,4},{6,7},{7,6},{8,9},{9,8},{10,11... | collective-permute-start | bytes 99848 | tf_op jit(solution)/shard_map/ppermute | solution.py:14
  10.8 1.4 %collective-permute-start.3 = (bf16[128,1,130]{0,2,1:T(8,128)(2,1)S(1)}, bf16[128,1,130]{0,2,1:T(8,128)(2,1)S(1)}, u32[]{:S(2)}, u32[]{:S(2)}) collective-permute-start(bf16[128,1,130]{0,2,1:T(8,128)(2,1)S(1)} %get-tuple-element.68), channel_id=1, source_target_pairs={{1,0},{0,1},{3,2},{2,3},{5,4},{4,5},{7,6},{6,7},{9,8},{8,9},{11,10... | collective-permute-start | bytes 99848 | tf_op jit(solution)/shard_map/ppermute | solution.py:15
  12.5 1.5 %copy-start = (bf16[3,3,128,256]{3,2,1,0:T(8,128)(2,1)S(1)}, bf16[3,3,128,256]{3,2,1,0:T(8,128)(2,1)}, u32[]{:S(2)}) copy-start(bf16[3,3,128,256]{3,2,1,0:T(8,128)(2,1)} %param.6) | copy-start | bytes 1769476
  13.5 5.2 %collective-permute-start.4 = (bf16[128,292]{0,1:T(8,128)(2,1)S(1)}, bf16[128,292]{0,1:T(8,128)(2,1)S(1)}, u32[]{:S(2)}, u32[]{:S(2)}) collective-permute-start(bf16[128,292]{0,1:T(8,128)(2,1)S(1)} %pad_maximum_fusion.5), channel_id=1, source_target_pairs={{0,2},{2,0},{1,3},{3,1},{4,6},{6,4},{5,7},{7,5},{8,10},{10,8},{9,1... | collective-permute-start | bytes 224264 | tf_op jit(solution)/shard_map/ppermute | solution.py:148
  24.6 0.7 copy-start.2
  30.2 2.2 %collective-permute-start.6 = (f32[1216,128]{1,0:T(8,128)S(1)}, f32[1216,128]{1,0:T(8,128)}, u32[]{:S(2)}, u32[]{:S(2)}) collective-permute-start(f32[1216,128]{1,0:T(8,128)S(1)} %dynamic-slice_bitcast_fusion), channel_id=1, source_target_pairs={{0,1},{1,0},{2,3},{3,2},{4,5},{5,4},{6,7},{7,6},{8,9},{9,8},{10,11... | collective-permute-start | bytes 1867784 | tf_op jit(solution)/shard_map/ppermute | solution.py:64
  33.6 7.0 %collective-permute-start.7 = (bf16[320,128]{1,0:T(8,128)(2,1)S(1)}, bf16[320,128]{1,0:T(8,128)(2,1)S(1)}, u32[]{:S(2)}, u32[]{:S(2)}) collective-permute-start(bf16[320,128]{1,0:T(8,128)(2,1)S(1)} %pad_maximum_fusion.3), channel_id=1, source_target_pairs={{0,4},{4,8},{8,12},{12,0},{1,5},{5,9},{9,13},{13,1},{2,6},{6,10},{... | collective-permute-start | bytes 245768 | tf_op jit(solution)/shard_map/ppermute | solution.py:104
  35.5 6.0 %collective-permute-start.8 = (bf16[320,128]{1,0:T(8,128)(2,1)S(1)}, bf16[320,128]{1,0:T(8,128)(2,1)S(1)}, u32[]{:S(2)}, u32[]{:S(2)}) collective-permute-start(bf16[320,128]{1,0:T(8,128)(2,1)S(1)} %pad_maximum_fusion.4), channel_id=1, source_target_pairs={{0,12},{4,0},{8,4},{12,8},{1,13},{5,1},{9,5},{13,9},{2,14},{6,2},{... | collective-permute-start | bytes 245768 | tf_op jit(solution)/shard_map/ppermute | solution.py:104
  38.4 7.0 %collective-permute-start.12 = (bf16[304,128]{1,0:T(8,128)(2,1)S(1)}, bf16[304,128]{1,0:T(8,128)(2,1)S(1)}, u32[]{:S(2)}, u32[]{:S(2)}) collective-permute-start(bf16[304,128]{1,0:T(8,128)(2,1)S(1)} %get-tuple-element.60), channel_id=1, source_target_pairs={{0,8},{4,12},{8,0},{12,4},{1,9},{5,13},{9,1},{13,5},{2,10},{6,14},... | collective-permute-start | bytes 233480 | tf_op jit(solution)/shard_map/ppermute | solution.py:104
  41.7 6.5 %collective-permute-start.10 = (bf16[128,1,130]{0,2,1:T(8,128)(2,1)S(1)}, bf16[128,1,130]{0,2,1:T(8,128)(2,1)S(1)}, u32[]{:S(2)}, u32[]{:S(2)}) collective-permute-start(bf16[128,1,130]{0,2,1:T(8,128)(2,1)S(1)} %get-tuple-element.66), channel_id=1, source_target_pairs={{1,0},{0,1},{3,2},{2,3},{5,4},{4,5},{7,6},{6,7},{9,8},{8,9},{11,10... | collective-permute-start | bytes 99848 | tf_op jit(solution)/shard_map/ppermute | solution.py:15
  41.8 6.4 %collective-permute-start.9 = (bf16[128,1,130]{0,2,1:T(8,128)(2,1)S(1)}, bf16[128,1,130]{0,2,1:T(8,128)(2,1)S(1)}, u32[]{:S(2)}, u32[]{:S(2)}) collective-permute-start(bf16[128,1,130]{0,2,1:T(8,128)(2,1)S(1)} %get-tuple-element.65), channel_id=1, source_target_pairs={{0,1},{1,0},{2,3},{3,2},{4,5},{5,4},{6,7},{7,6},{8,9},{9,8},{10,11... | collective-permute-start | bytes 99848 | tf_op jit(solution)/shard_map/ppermute | solution.py:14
  45.4 11.7 %collective-permute-start.13 = (bf16[304,128]{1,0:T(8,128)(2,1)S(1)}, bf16[304,128]{1,0:T(8,128)(2,1)S(1)}, u32[]{:S(2)}, u32[]{:S(2)}) collective-permute-start(bf16[304,128]{1,0:T(8,128)(2,1)S(1)} %get-tuple-element.9), channel_id=1, source_target_pairs={{0,12},{4,0},{8,4},{12,8},{1,13},{5,1},{9,5},{13,9},{2,14},{6,2},{... | collective-permute-start | bytes 233480 | tf_op jit(solution)/shard_map/ppermute | solution.py:76
  47.5 9.7 %collective-permute-start.14 = (bf16[304,128]{1,0:T(8,128)(2,1)S(1)}, bf16[304,128]{1,0:T(8,128)(2,1)S(1)}, u32[]{:S(2)}, u32[]{:S(2)}) collective-permute-start(bf16[304,128]{1,0:T(8,128)(2,1)S(1)} %get-tuple-element.9), channel_id=1, source_target_pairs={{0,8},{4,12},{8,0},{12,4},{1,9},{5,13},{9,1},{13,5},{2,10},{6,14},... | collective-permute-start | bytes 233480 | tf_op jit(solution)/shard_map/ppermute | solution.py:76
  47.5 9.7 %collective-permute-start.15 = (bf16[304,128]{1,0:T(8,128)(2,1)S(1)}, bf16[304,128]{1,0:T(8,128)(2,1)S(1)}, u32[]{:S(2)}, u32[]{:S(2)}) collective-permute-start(bf16[304,128]{1,0:T(8,128)(2,1)S(1)} %get-tuple-element.9), channel_id=1, source_target_pairs={{0,4},{4,8},{8,12},{12,0},{1,5},{5,9},{9,13},{13,1},{2,6},{6,10},{... | collective-permute-start | bytes 233480 | tf_op jit(solution)/shard_map/ppermute | solution.py:76
  53.3 13.4 %collective-permute-start.11 = (bf16[128,2048]{1,0:T(8,128)(2,1)S(1)}, bf16[128,2048]{1,0:T(8,128)(2,1)S(1)}, u32[]{:S(2)}, u32[]{:S(2)}) collective-permute-start(bf16[128,2048]{1,0:T(8,128)(2,1)S(1)} %fusion.2), channel_id=1, source_target_pairs={{0,2},{2,0},{1,3},{3,1},{4,6},{6,4},{5,7},{7,5},{8,10},{10,8},{9,1... | collective-permute-start | bytes 1572872 | tf_op jit(solution)/shard_map/ppermute | solution.py:198
  57.4 10.3 %collective-permute-start.16 = (f32[1216,128]{1,0:T(8,128)S(1)}, f32[1216,128]{1,0:T(8,128)S(1)}, u32[]{:S(2)}, u32[]{:S(2)}) collective-permute-start(f32[1216,128]{1,0:T(8,128)S(1)} %bitcast.321), channel_id=1, source_target_pairs={{0,1},{1,0},{2,3},{3,2},{4,5},{5,4},{6,7},{7,6},{8,9},{9,8},{10,11... | collective-permute-start | bytes 1867784 | tf_op jit(solution)/shard_map/ppermute | solution.py:76

commit v17 on v16

--- a/solution.py
+++ b/solution.py
@@ -187,15 +187,22 @@
     )
     grad_wide = jnp.concatenate([before, grad_field, after], axis=2)
     grad_pad = mask_rims(padded_2(grad_wide, (("lat", 1),), 1))
+    interiors = []
     outgoing = []
     for shift in range(1, chan_count):
+        pairs = [(i, (i + shift) % chan_count) for i in range(chan_count)]
         kernel_t = jnp.swapaxes(kernel_cols[shift], 2, 3)
-        outgoing.append(conv_taps(kernel_t, grad_pad, row_count, column_count, True).astype(jnp.bfloat16))
+        inner = conv_taps(kernel_t, grad_field, row_count - 2, column_count - 2, True)
+        interiors.append(lax.ppermute(inner.astype(jnp.bfloat16), "chan", pairs))
+        whole = conv_taps(kernel_t, grad_pad, row_count, column_count, True)
+        outgoing.append(border_of(whole.reshape(own_channels, row_count, column_count)).astype(jnp.bfloat16))
     grad_pad, outgoing = lax.optimization_barrier((grad_pad, outgoing))
     received = []
     for shift in range(1, chan_count):
         pairs = [(i, (i + shift) % chan_count) for i in range(chan_count)]
-        received.append(lax.ppermute(outgoing[shift - 1], "chan", pairs))
+        ring = lax.ppermute(outgoing[shift - 1], "chan", pairs)
+        inner = interiors[shift - 1].reshape(own_channels, row_count - 2, column_count - 2)
+        received.append(with_border(inner, ring).reshape(own_channels, -1))
     own_part = conv_taps(jnp.swapaxes(kernel_cols[0], 2, 3), grad_pad, row_count, column_count, True)
     for piece in received:
         own_part = own_part + piece.astype(jnp.float32)

time: 70.3 us -> 110 us (1.56); the launches traced: 70.1 us -> 108 us
  local copies, waits for them, and re-layouts: 10.3 us -> 41 us
  waiting for transfers between devices: 19 us -> 12.8 us
  matrix products: 14.7 us -> 20.4 us
  starting transfers between devices: 17.9 us -> 22.8 us
  other arithmetic: 6.65 us -> 9.57 us
    reshape x0 -> x11, local copies, waits for them, and re-layouts: none -> 16.4 us  [the longest x9 14.1 us: window_of(): return field[:, first_row:first_row + row_count, first_col:first_col + co...]
    dot_general x36 -> x45, matrix products: 11.9 us -> 17.6 us  [conv_taps(): jnp.dot(kernel[tap_row, tap_col], window, preferred_element_type=jnp.floa...]
    unnamed x12 -> x35, local copies, waits for them, and re-layouts: 3.51 us -> 6.85 us
    ppermute x1 -> x2, waiting for transfers between devices: 8.51 us -> 5.9 us  [the longest x1 5.9 us: local(): interiors.append(lax.ppermute(inner.astype(jnp.bfloat16), 'chan', pairs))]
    ppermute x3, waiting for transfers between devices: 5.21 us -> 3.14 us  [sum_start(): moved = lax.ppermute(piece, 'lon', pairs)]
    convert_element_type x0 -> x1, other arithmetic: none -> 1.91 us  [local(): own_part = own_part + piece.astype(jnp.float32)]
    ppermute x3, starting transfers between devices: 4.99 us -> 6.88 us  [sum_start(): moved = lax.ppermute(piece, 'lon', pairs)]
    ppermute x1 -> x2, starting transfers between devices: 1.56 us -> 3.36 us  [the longest x1 1.81 us: local(): interiors.append(lax.ppermute(inner.astype(jnp.bfloat16), 'chan', pairs))]
  transfers between devices with their start and end apart: 17 -> 18, of which waited for: 9 -> 6; matrix products, arithmetic and copies ran while one was open for 22% -> 47% of each run, Pallas kernels for 0% -> 0%
where the time goes in v17:
time: 110 us; the launch traced here: 108 us
  local copies, waits for them, and re-layouts  41 us (37%)
  starting transfers between devices  22.8 us (21%)
  matrix products  20.4 us (19%)
  waiting for transfers between devices  12.8 us (12%)
  other arithmetic  9.57 us (9%)
  between operations  1.56 us (1%)
    dot_general x45, matrix products, conv_taps(): jnp.dot(kernel[tap_row, tap_col], window, preferred_element_type=jnp.floa...  17.6 us
    reshape x9, local copies, waits for them, and re-layouts, window_of(): return field[:, first_row:first_row + row_count, first_col:first_col + co...  14.1 us
    ppermute x3, starting transfers between devices, sum_start(): moved = lax.ppermute(piece, 'lon', pairs)  6.88 us
    unnamed x35, local copies, waits for them, and re-layouts  6.85 us
    ppermute x1, waiting for transfers between devices, local(): interiors.append(lax.ppermute(inner.astype(jnp.bfloat16), 'chan', pairs))  5.9 us
    slice x5, local copies, waits for them, and re-layouts, window_of(): field[:, first_row:first_row + row_count, first_col:first_col + column_co...  5.41 us
    ppermute x4, starting transfers between devices, direct_all_gather(): pieces.append(lax.ppermute(sent, axis, pairs).astype(jnp.float32))  4.1 us
    ppermute x3, waiting for transfers between devices, sum_start(): moved = lax.ppermute(piece, 'lon', pairs)  3.14 us
  transfers between devices with their start and end apart: 18, of which 6 were waited for; matrix products, arithmetic and copies ran while one was open for 47% of the time, Pallas kernels for 0%

profile of v17, /device:TPU:0, one launch (start us, length us, event | category | flops | bytes accessed | tf_op | source)
XLA Modules:
  0.0 108.2 jit_solution(4942728202969074114)
XLA Ops:
  0.7 1.6 %copy.18 = bf16[128,16,128]{0,2,1:T(8,128)(2,1)S(1)} copy(bf16[128,16,128]{2,1,0:T(8,128)(2,1)} %param.4) | data formatting | bytes 1048576 | tf_op args[0]
  2.2 3.0 %collective-permute-start.5 = (bf16[128,16,128]{0,2,1:T(8,128)(2,1)S(1)}, bf16[128,16,128]{0,2,1:T(8,128)(2,1)S(1)}, u32[]{:S(2)}, u32[]{:S(2)}) collective-permute-start(bf16[128,16,128]{0,2,1:T(8,128)(2,1)S(1)} %copy.18), channel_id=1, source_target_pairs={{0,2},{2,0},{1,3},{3,1},{4,6},{6,4},{5,7},{7,5},{8,10},{10,8},{9,1... | collective-permute-start | bytes 1572872 | tf_op jit(solution)/shard_map/ppermute | solution.py:142
  5.2 1.6 %collective-permute-start = (bf16[128,16,1]{0,2,1:T(2,128)(2,1)S(1)}, bf16[128,16,1]{0,2,1:T(2,128)(2,1)S(1)}, u32[]{:S(2)}, u32[]{:S(2)}) collective-permute-start(bf16[128,16,1]{0,2,1:T(2,128)(2,1)S(1)} %get-tuple-element.82), channel_id=1, source_target_pairs={{0,4},{4,8},{8,12},{12,0},{1,5},{5,9},{9,13},{13,1},{2,6},{6,10},{... | collective-permute-start | bytes 12296 | tf_op jit(solution)/shard_map/ppermute | solution.py:14
  6.9 2.2 %collective-permute-start.1 = (bf16[128,16,1]{0,2,1:T(2,128)(2,1)S(1)}, bf16[128,16,1]{0,2,1:T(2,128)(2,1)S(1)}, u32[]{:S(2)}, u32[]{:S(2)}) collective-permute-start(bf16[128,16,1]{0,2,1:T(2,128)(2,1)S(1)} %get-tuple-element.83), channel_id=1, source_target_pairs={{4,0},{8,4},{12,8},{0,12},{5,1},{9,5},{13,9},{1,13},{6,2},{10,6},{... | collective-permute-start | bytes 12296 | tf_op jit(solution)/shard_map/ppermute | solution.py:15
  16.5 2.3 %collective-permute-done.4 = bf16[128,292]{0,1:T(8,128)(2,1)S(1)} collective-permute-done((bf16[128,292]{0,1:T(8,128)(2,1)S(1)}, bf16[128,292]{0,1:T(8,128)(2,1)S(1)}, u32[]{:S(2)}, u32[]{:S(2)}) %collective-permute-start.4) | collective-permute-done | bytes 74784 | tf_op jit(solution)/shard_map/ppermute | solution.py:148
  19.9 2.5 %fusion.19 = (bf16[256,16,128]{0,2,1:T(8,128)(2,1)S(1)}, bf16[256,16,128]{0,2,1:T(8,128)(2,1)S(1)}, bf16[256,16,128]{0,2,1:T(8,128)(2,1)S(1)}, bf16[256,16,128]{...) fusion(bf16[128,18,130]{0,2,1:T(8,128)(2,1)S(1)} %maximum_selec, ...), kind=kLoop, calls=%fused_computation.94 | loop fusion | flops 18874368 | bytes 10635264 | tf_op jit(solution)/shard_map/concatenate | solution.py:164
  25.3 1.0 convert_reduce_fusion
  31.5 2.0 %fusion.61 = (bf16[128,14,126]{0,2,1:T(8,128)(2,1)}, bf16[128,14,126]{0,2,1:T(8,128)(2,1)}, bf16[128,14,126]{0,2,1:T(8,128)(2,1)S(1)}, bf16[128,14,126]{0,2,1:T(...) fusion(bf16[128,16,128]{0,2,1:T(8,128)(2,1)S(1)} %copy.27), kind=kLoop, calls=%fused_computation.224 | loop fusion | bytes 8128512 | tf_op jit(solution)/shard_map/slice | solution.py:37
  33.6 1.9 %reshape.276 = bf16[128,1764]{0,1:T(8,128)(2,1)} reshape(bf16[128,14,126]{0,2,1:T(8,128)(2,1)} %get-tuple-element.77) | data formatting | bytes 903168 | tf_op jit(solution)/shard_map/reshape | solution.py:39
  35.5 1.9 %reshape.277 = bf16[128,1764]{0,1:T(8,128)(2,1)} reshape(bf16[128,14,126]{0,2,1:T(8,128)(2,1)} %get-tuple-element.76) | data formatting | bytes 903168 | tf_op jit(solution)/shard_map/reshape | solution.py:39
  37.4 1.9 %reshape.278 = bf16[128,1764]{0,1:T(8,128)(2,1)} reshape(bf16[128,14,126]{0,2,1:T(8,128)(2,1)} %get-tuple-element.75) | data formatting | bytes 903168 | tf_op jit(solution)/shard_map/reshape | solution.py:39
  39.3 1.9 %reshape.279 = bf16[128,1764]{0,1:T(8,128)(2,1)} reshape(bf16[128,14,126]{0,2,1:T(8,128)(2,1)} %get-tuple-element.74) | data formatting | bytes 903168 | tf_op jit(solution)/shard_map/reshape | solution.py:39
  41.2 1.9 %reshape.280 = bf16[128,1764]{0,1:T(8,128)(2,1)} reshape(bf16[128,14,126]{0,2,1:T(8,128)(2,1)} %get-tuple-element.73) | data formatting | bytes 903168 | tf_op jit(solution)/shard_map/reshape | solution.py:39
  44.9 1.4 %fusion.34 = f32[128,1764]{0,1:T(8,128)S(1)} fusion(bf16[128,1764]{0,1:T(8,128)(2,1)} %reshape.276, bf16[3,3,128,128]{2,3,1,0:T(8,128)(2,1)S(1)} %get-tuple-element.64), kind=kOutput, calls=%fused_computation.192 | convolution fusion | flops 57802752 | bytes 1387520 | tf_op jit(solution)/shard_map/dot_general | solution.py:50
  51.7 1.3 %slice_reduce_fusion.1 = (bf16[128,16]{1,0:T(8,128)(2,1)}, bf16[128,16]{1,0:T(8,128)(2,1)S(1)}) fusion(bf16[128,16,128]{2,1,0:T(8,128)(2,1)S(1)} %bitcast.367), kind=kLoop, calls=%fused_computation.109 | loop fusion | bytes 16384 | tf_op jit(solution)/shard_map/slice | solution.py:179
  54.0 1.9 %reshape.283 = bf16[128,1764]{0,1:T(8,128)(2,1)} reshape(bf16[128,14,126]{0,2,1:T(8,128)(2,1)} %get-tuple-element.70) | data formatting | bytes 903168 | tf_op jit(solution)/shard_map/reshape | solution.py:39
  56.8 1.4 %convolution_add_fusion.1 = f32[128,1764]{0,1:T(8,128)S(1)} fusion(f32[128,1764]{0,1:T(8,128)S(1)} %convolution_add_fusion.2, bf16[128,1764]{0,1:T(8,128)(2,1)} %reshape.283, bf16[3,3,128,128]{2,3,1,0:T(8,128)(2,1)S(1)} %get-tuple-element.64), kind=kOutput, calls=%fused_computation.1 | convolution fusion | flops 58028544 | bytes 2292736 | tf_op jit(solution)/shard_map/dot_general | solution.py:50
  58.7 1.8 %collective-permute-start.12 = (bf16[128,1764]{0,1:T(8,128)(2,1)S(1)}, bf16[128,1764]{0,1:T(8,128)(2,1)}, u32[]{:S(2)}, u32[]{:S(2)}) collective-permute-start(bf16[128,1764]{0,1:T(8,128)(2,1)S(1)} %fusion.5), channel_id=1, source_target_pairs={{0,2},{2,0},{1,3},{3,1},{4,6},{6,4},{5,7},{7,5},{8,10},{10,8},{9,1... | collective-permute-start | bytes 1354760 | tf_op jit(solution)/shard_map/ppermute | solution.py:196
  60.5 1.1 %bitcast_add_fusion = f32[1216,128]{1,0:T(8,128)S(1)} fusion(f32[1216,128]{1,0:T(8,128)} %collective-permute-done.6, f32[2,1216,128]{2,1,0:T(8,128)S(1)} %bitcast.371, s32[]{:T(128)S(6)} %select_n.98), kind=kLoop, calls=%fused_computation.106 | loop fusion | flops 155648 | bytes 1867780 | tf_op jit(solution)/shard_map/add | solution.py:64
  61.7 1.6 %collective-permute-start.7 = (bf16[320,128]{1,0:T(8,128)(2,1)S(1)}, bf16[320,128]{1,0:T(8,128)(2,1)S(1)}, u32[]{:S(2)}, u32[]{:S(2)}) collective-permute-start(bf16[320,128]{1,0:T(8,128)(2,1)S(1)} %pad_maximum_fusion.4), channel_id=1, source_target_pairs={{0,4},{4,8},{8,12},{12,0},{1,5},{5,9},{9,13},{13,1},{2,6},{6,10},{... | collective-permute-start | bytes 245768 | tf_op jit(solution)/shard_map/ppermute | solution.py:104
  63.3 2.4 %collective-permute-start.8 = (bf16[320,128]{1,0:T(8,128)(2,1)S(1)}, bf16[320,128]{1,0:T(8,128)(2,1)S(1)}, u32[]{:S(2)}, u32[]{:S(2)}) collective-permute-start(bf16[320,128]{1,0:T(8,128)(2,1)S(1)} %pad_maximum_fusion.5), channel_id=1, source_target_pairs={{0,12},{4,0},{8,4},{12,8},{1,13},{5,1},{9,5},{13,9},{2,14},{6,2},{... | collective-permute-start | bytes 245768 | tf_op jit(solution)/shard_map/ppermute | solution.py:104
  65.7 5.9 %collective-permute-done.12 = bf16[128,1764]{0,1:T(8,128)(2,1)} collective-permute-done((bf16[128,1764]{0,1:T(8,128)(2,1)S(1)}, bf16[128,1764]{0,1:T(8,128)(2,1)}, u32[]{:S(2)}, u32[]{:S(2)}) %collective-permute-start.12) | collective-permute-done | bytes 451616 | tf_op jit(solution)/shard_map/ppermute | solution.py:196
  71.6 1.1 %reshape.285 = bf16[128,14,126]{0,2,1:T(8,128)(2,1)S(1)} reshape(bf16[128,1764]{0,1:T(8,128)(2,1)} %collective-permute-done.12) | data formatting | bytes 903168 | tf_op jit(solution)/shard_map/reshape | solution.py:204
  72.8 1.2 %copy.45 = bf16[128,14,126]{2,1,0:T(8,128)(2,1)} copy(bf16[128,14,126]{0,2,1:T(8,128)(2,1)S(1)} %reshape.285) | data formatting | bytes 903168 | tf_op jit(solution)/shard_map/reshape | solution.py:204
  74.0 2.8 %collective-permute-start.13 = (bf16[304,128]{1,0:T(8,128)(2,1)S(1)}, bf16[304,128]{1,0:T(8,128)(2,1)S(1)}, u32[]{:S(2)}, u32[]{:S(2)}) collective-permute-start(bf16[304,128]{1,0:T(8,128)(2,1)S(1)} %get-tuple-element.60), channel_id=1, source_target_pairs={{0,8},{4,12},{8,0},{12,4},{1,9},{5,13},{9,1},{13,5},{2,10},{6,14},... | collective-permute-start | bytes 233480 | tf_op jit(solution)/shard_map/ppermute | solution.py:104
  77.8 3.1 %collective-permute-done.13 = bf16[304,128]{1,0:T(8,128)(2,1)S(1)} collective-permute-done((bf16[304,128]{1,0:T(8,128)(2,1)S(1)}, bf16[304,128]{1,0:T(8,128)(2,1)S(1)}, u32[]{:S(2)}, u32[]{:S(2)}) %collective-permute-start.13) | collective-permute-done | bytes 77856 | tf_op jit(solution)/shard_map/ppermute | solution.py:104
  81.0 3.4 %collective-permute-start.14 = (bf16[304,128]{1,0:T(8,128)(2,1)S(1)}, bf16[304,128]{1,0:T(8,128)(2,1)S(1)}, u32[]{:S(2)}, u32[]{:S(2)}) collective-permute-start(bf16[304,128]{1,0:T(8,128)(2,1)S(1)} %get-tuple-element.9), channel_id=1, source_target_pairs={{0,12},{4,0},{8,4},{12,8},{1,13},{5,1},{9,5},{13,9},{2,14},{6,2},{... | collective-permute-start | bytes 233480 | tf_op jit(solution)/shard_map/ppermute | solution.py:76
  91.8 1.6 %collective-permute-start.11 = (bf16[128,284]{1,0:T(8,128)(2,1)S(1)}, bf16[128,284]{1,0:T(8,128)(2,1)S(1)}, u32[]{:S(2)}, u32[]{:S(2)}) collective-permute-start(bf16[128,284]{1,0:T(8,128)(2,1)S(1)} %pad_maximum_fusion.3), channel_id=1, source_target_pairs={{0,2},{2,0},{1,3},{3,1},{4,6},{6,4},{5,7},{7,5},{8,10},{10,8},{9,1... | collective-permute-start | bytes 218120 | tf_op jit(solution)/shard_map/ppermute | solution.py:203
  98.8 1.7 %copy.46 = bf16[128,14,1]{2,1,0:T(8,128)(2,1)S(1)} copy(bf16[128,14,1]{1,0,2:T(8,128)(2,1)} %get-tuple-element.87) | data formatting | bytes 7168 | tf_op jit(solution)/shard_map/broadcast_in_dim | solution.py:131
  101.4 1.9 %maximum_convert_fusion = f32[128,16,128]{2,1,0:T(8,128)S(1)} fusion(bf16[128,1,128]{2,1,0:T(2,128)(2,1)S(1)} %copy.48, bf16[128,14,1]{2,1,0:T(8,128)(2,1)S(1)} %copy.46, bf16[128,14,126]{2,1,0:T(8,128)(2,1)} %copy.45, bf16[128,14,1]{2,1,0:T(8,128)(2,1)S(1)} %copy.44, bf16[128,1,128]{2,1,0:T(2,128)(2,1)S(1)} %copy.47), kind=kLoop, calls=%fused_computation.110 | loop fusion | flops 2621440 | bytes 1572864 | tf_op jit(solution)/shard_map/convert_element_type | solution.py:208
  104.8 1.3 %fusion.8 = f32[2,1216,128]{2,1,0:T(8,128)S(1)} fusion(s32[]{:T(128)S(6)} %select_n.112, f32[1,1216,128]{2,1,0:T(8,128)} %bitcast.122, f32[1,1216,128]{2,1,0:T(8,128)S(1)} %bitcast.387), kind=kLoop, calls=%fused_computation.71 | loop fusion | flops 933888 | bytes 2490372 | tf_op jit(solution)/shard_map/jit(_roll_dynamic)/concatenate | solution.py:78
  107.0 1.2 %fusion.11 = f32[3,3,128,256]{3,2,1,0:T(8,128)} fusion(s32[]{:T(128)S(6)} %select_n.114, f32[3,3,128,256]{3,2,1,0:T(8,128)S(1)} %reshape.288), kind=kLoop, calls=%fused_computation.76 | loop fusion | flops 294912 | bytes 2359300 | tf_op jit(solution)/shard_map/concatenate | solution.py:184
  (172 shorter events, 42.7 us)
Async XLA Ops:
  0.6 8.5 %copy-start.10 = (bf16[128,16,128]{2,1,0:T(8,128)(2,1)S(1)}, bf16[128,16,128]{2,1,0:T(8,128)(2,1)}, u32[]{:S(2)}) copy-start(bf16[128,16,128]{2,1,0:T(8,128)(2,1)} %param.5) | copy-start | bytes 1572868
  0.6 8.6 %copy-start = (bf16[3,3,128,256]{3,2,1,0:T(8,128)(2,1)S(1)}, bf16[3,3,128,256]{3,2,1,0:T(8,128)(2,1)}, u32[]{:S(2)}) copy-start(bf16[3,3,128,256]{3,2,1,0:T(8,128)(2,1)} %param.6) | copy-start | bytes 1769476
  2.2 16.6 %collective-permute-start.5 = (bf16[128,16,128]{0,2,1:T(8,128)(2,1)S(1)}, bf16[128,16,128]{0,2,1:T(8,128)(2,1)S(1)}, u32[]{:S(2)}, u32[]{:S(2)}) collective-permute-start(bf16[128,16,128]{0,2,1:T(8,128)(2,1)S(1)} %copy.18), channel_id=1, source_target_pairs={{0,2},{2,0},{1,3},{3,1},{4,6},{6,4},{5,7},{7,5},{8,10},{10,8},{9,1... | collective-permute-start | bytes 1572872 | tf_op jit(solution)/shard_map/ppermute | solution.py:142
  5.2 5.5 %collective-permute-start = (bf16[128,16,1]{0,2,1:T(2,128)(2,1)S(1)}, bf16[128,16,1]{0,2,1:T(2,128)(2,1)S(1)}, u32[]{:S(2)}, u32[]{:S(2)}) collective-permute-start(bf16[128,16,1]{0,2,1:T(2,128)(2,1)S(1)} %get-tuple-element.82), channel_id=1, source_target_pairs={{0,4},{4,8},{8,12},{12,0},{1,5},{5,9},{9,13},{13,1},{2,6},{6,10},{... | collective-permute-start | bytes 12296 | tf_op jit(solution)/shard_map/ppermute | solution.py:14
  6.9 3.9 %collective-permute-start.1 = (bf16[128,16,1]{0,2,1:T(2,128)(2,1)S(1)}, bf16[128,16,1]{0,2,1:T(2,128)(2,1)S(1)}, u32[]{:S(2)}, u32[]{:S(2)}) collective-permute-start(bf16[128,16,1]{0,2,1:T(2,128)(2,1)S(1)} %get-tuple-element.83), channel_id=1, source_target_pairs={{4,0},{8,4},{12,8},{0,12},{5,1},{9,5},{13,9},{1,13},{6,2},{10,6},{... | collective-permute-start | bytes 12296 | tf_op jit(solution)/shard_map/ppermute | solution.py:15
  10.8 1.3 %collective-permute-start.2 = (bf16[128,1,130]{0,2,1:T(8,128)(2,1)S(1)}, bf16[128,1,130]{0,2,1:T(8,128)(2,1)S(1)}, u32[]{:S(2)}, u32[]{:S(2)}) collective-permute-start(bf16[128,1,130]{0,2,1:T(8,128)(2,1)S(1)} %get-tuple-element.67), channel_id=1, source_target_pairs={{0,1},{1,0},{2,3},{3,2},{4,5},{5,4},{6,7},{7,6},{8,9},{9,8},{10,11... | collective-permute-start | bytes 99848 | tf_op jit(solution)/shard_map/ppermute | solution.py:14
  10.8 1.4 %collective-permute-start.3 = (bf16[128,1,130]{0,2,1:T(8,128)(2,1)S(1)}, bf16[128,1,130]{0,2,1:T(8,128)(2,1)S(1)}, u32[]{:S(2)}, u32[]{:S(2)}) collective-permute-start(bf16[128,1,130]{0,2,1:T(8,128)(2,1)S(1)} %get-tuple-element.68), channel_id=1, source_target_pairs={{1,0},{0,1},{3,2},{2,3},{5,4},{4,5},{7,6},{6,7},{9,8},{8,9},{11,10... | collective-permute-start | bytes 99848 | tf_op jit(solution)/shard_map/ppermute | solution.py:15
  13.3 5.5 %collective-permute-start.4 = (bf16[128,292]{0,1:T(8,128)(2,1)S(1)}, bf16[128,292]{0,1:T(8,128)(2,1)S(1)}, u32[]{:S(2)}, u32[]{:S(2)}) collective-permute-start(bf16[128,292]{0,1:T(8,128)(2,1)S(1)} %pad_maximum_fusion.6), channel_id=1, source_target_pairs={{0,2},{2,0},{1,3},{3,1},{4,6},{6,4},{5,7},{7,5},{8,10},{10,8},{9,1... | collective-permute-start | bytes 224264 | tf_op jit(solution)/shard_map/ppermute | solution.py:148
  24.6 0.7 copy-start.12
  30.9 29.5 %collective-permute-start.6 = (f32[1216,128]{1,0:T(8,128)}, f32[1216,128]{1,0:T(8,128)}, u32[]{:S(2)}, u32[]{:S(2)}) collective-permute-start(f32[1216,128]{1,0:T(8,128)} %dynamic-slice_bitcast_fusion), channel_id=1, source_target_pairs={{0,1},{1,0},{2,3},{3,2},{4,5},{5,4},{6,7},{7,6},{8,9},{9,8},{10,11... | collective-permute-start | bytes 1867784 | tf_op jit(solution)/shard_map/ppermute | solution.py:64
  44.0 2.3 %copy-start.8 = (bf16[128,1764]{0,1:T(8,128)(2,1)S(1)}, bf16[128,1764]{0,1:T(8,128)(2,1)}, u32[]{:S(2)}) copy-start(bf16[128,1764]{0,1:T(8,128)(2,1)} %reshape.277) | copy-start | bytes 1354756
  46.3 1.0 copy-start.7
  47.3 1.0 copy-start.6
  48.3 1.0 copy-start.5
  49.3 1.0 copy-start.4
  50.3 1.0 copy-start.3
  53.0 2.9 %copy-start.1 = (bf16[128,14,126]{0,2,1:T(8,128)(2,1)S(1)}, bf16[128,14,126]{0,2,1:T(8,128)(2,1)}, u32[]{:S(2)}) copy-start(bf16[128,14,126]{0,2,1:T(8,128)(2,1)} %get-tuple-element.69) | copy-start | bytes 1354756
  56.8 1.5 %copy-start.2 = (bf16[128,1764]{0,1:T(8,128)(2,1)S(1)}, bf16[128,1764]{0,1:T(8,128)(2,1)}, u32[]{:S(2)}) copy-start(bf16[128,1764]{0,1:T(8,128)(2,1)} %reshape.284) | copy-start | bytes 1354756
  58.7 13.0 %collective-permute-start.12 = (bf16[128,1764]{0,1:T(8,128)(2,1)S(1)}, bf16[128,1764]{0,1:T(8,128)(2,1)}, u32[]{:S(2)}, u32[]{:S(2)}) collective-permute-start(bf16[128,1764]{0,1:T(8,128)(2,1)S(1)} %fusion.5), channel_id=1, source_target_pairs={{0,2},{2,0},{1,3},{3,1},{4,6},{6,4},{5,7},{7,5},{8,10},{10,8},{9,1... | collective-permute-start | bytes 1354760 | tf_op jit(solution)/shard_map/ppermute | solution.py:196
  61.7 15.2 %collective-permute-start.7 = (bf16[320,128]{1,0:T(8,128)(2,1)S(1)}, bf16[320,128]{1,0:T(8,128)(2,1)S(1)}, u32[]{:S(2)}, u32[]{:S(2)}) collective-permute-start(bf16[320,128]{1,0:T(8,128)(2,1)S(1)} %pad_maximum_fusion.4), channel_id=1, source_target_pairs={{0,4},{4,8},{8,12},{12,0},{1,5},{5,9},{9,13},{13,1},{2,6},{6,10},{... | collective-permute-start | bytes 245768 | tf_op jit(solution)/shard_map/ppermute | solution.py:104
  63.3 13.7 %collective-permute-start.8 = (bf16[320,128]{1,0:T(8,128)(2,1)S(1)}, bf16[320,128]{1,0:T(8,128)(2,1)S(1)}, u32[]{:S(2)}, u32[]{:S(2)}) collective-permute-start(bf16[320,128]{1,0:T(8,128)(2,1)S(1)} %pad_maximum_fusion.5), channel_id=1, source_target_pairs={{0,12},{4,0},{8,4},{12,8},{1,13},{5,1},{9,5},{13,9},{2,14},{6,2},{... | collective-permute-start | bytes 245768 | tf_op jit(solution)/shard_map/ppermute | solution.py:104
  74.0 7.0 %collective-permute-start.13 = (bf16[304,128]{1,0:T(8,128)(2,1)S(1)}, bf16[304,128]{1,0:T(8,128)(2,1)S(1)}, u32[]{:S(2)}, u32[]{:S(2)}) collective-permute-start(bf16[304,128]{1,0:T(8,128)(2,1)S(1)} %get-tuple-element.60), channel_id=1, source_target_pairs={{0,8},{4,12},{8,0},{12,4},{1,9},{5,13},{9,1},{13,5},{2,10},{6,14},... | collective-permute-start | bytes 233480 | tf_op jit(solution)/shard_map/ppermute | solution.py:104
  77.2 7.8 %collective-permute-start.10 = (bf16[128,1,130]{0,2,1:T(8,128)(2,1)S(1)}, bf16[128,1,130]{0,2,1:T(8,128)(2,1)S(1)}, u32[]{:S(2)}, u32[]{:S(2)}) collective-permute-start(bf16[128,1,130]{0,2,1:T(8,128)(2,1)S(1)} %get-tuple-element.66), channel_id=1, source_target_pairs={{1,0},{0,1},{3,2},{2,3},{5,4},{4,5},{7,6},{6,7},{9,8},{8,9},{11,10... | collective-permute-start | bytes 99848 | tf_op jit(solution)/shard_map/ppermute | solution.py:15
  77.3 7.7 %collective-permute-start.9 = (bf16[128,1,130]{0,2,1:T(8,128)(2,1)S(1)}, bf16[128,1,130]{0,2,1:T(8,128)(2,1)S(1)}, u32[]{:S(2)}, u32[]{:S(2)}) collective-permute-start(bf16[128,1,130]{0,2,1:T(8,128)(2,1)S(1)} %get-tuple-element.65), channel_id=1, source_target_pairs={{0,1},{1,0},{2,3},{3,2},{4,5},{5,4},{6,7},{7,6},{8,9},{9,8},{10,11... | collective-permute-start | bytes 99848 | tf_op jit(solution)/shard_map/ppermute | solution.py:14
  81.0 15.9 %collective-permute-start.14 = (bf16[304,128]{1,0:T(8,128)(2,1)S(1)}, bf16[304,128]{1,0:T(8,128)(2,1)S(1)}, u32[]{:S(2)}, u32[]{:S(2)}) collective-permute-start(bf16[304,128]{1,0:T(8,128)(2,1)S(1)} %get-tuple-element.9), channel_id=1, source_target_pairs={{0,12},{4,0},{8,4},{12,8},{1,13},{5,1},{9,5},{13,9},{2,14},{6,2},{... | collective-permute-start | bytes 233480 | tf_op jit(solution)/shard_map/ppermute | solution.py:76
  84.4 12.5 %collective-permute-start.15 = (bf16[304,128]{1,0:T(8,128)(2,1)S(1)}, bf16[304,128]{1,0:T(8,128)(2,1)S(1)}, u32[]{:S(2)}, u32[]{:S(2)}) collective-permute-start(bf16[304,128]{1,0:T(8,128)(2,1)S(1)} %get-tuple-element.9), channel_id=1, source_target_pairs={{0,8},{4,12},{8,0},{12,4},{1,9},{5,13},{9,1},{13,5},{2,10},{6,14},... | collective-permute-start | bytes 233480 | tf_op jit(solution)/shard_map/ppermute | solution.py:76
  84.4 12.5 %collective-permute-start.16 = (bf16[304,128]{1,0:T(8,128)(2,1)S(1)}, bf16[304,128]{1,0:T(8,128)(2,1)S(1)}, u32[]{:S(2)}, u32[]{:S(2)}) collective-permute-start(bf16[304,128]{1,0:T(8,128)(2,1)S(1)} %get-tuple-element.9), channel_id=1, source_target_pairs={{0,4},{4,8},{8,12},{12,0},{1,5},{5,9},{9,13},{13,1},{2,6},{6,10},{... | collective-permute-start | bytes 233480 | tf_op jit(solution)/shard_map/ppermute | solution.py:76
  91.8 2.5 %copy-start.9 = (bf16[3,3,128,128]{2,3,1,0:T(8,128)(2,1)S(1)}, bf16[3,3,128,128]{2,3,1,0:T(8,128)(2,1)}, u32[]{:S(2)}) copy-start(bf16[3,3,128,128]{2,3,1,0:T(8,128)(2,1)} %get-tuple-element.63) | copy-start | bytes 884740
  91.8 5.4 %collective-permute-start.11 = (bf16[128,284]{1,0:T(8,128)(2,1)S(1)}, bf16[128,284]{1,0:T(8,128)(2,1)S(1)}, u32[]{:S(2)}, u32[]{:S(2)}) collective-permute-start(bf16[128,284]{1,0:T(8,128)(2,1)S(1)} %pad_maximum_fusion.3), channel_id=1, source_target_pairs={{0,2},{2,0},{1,3},{3,1},{4,6},{6,4},{5,7},{7,5},{8,10},{10,8},{9,1... | collective-permute-start | bytes 218120 | tf_op jit(solution)/shard_map/ppermute | solution.py:203
  97.1 7.6 %collective-permute-start.17 = (f32[1216,128]{1,0:T(8,128)S(1)}, f32[1216,128]{1,0:T(8,128)}, u32[]{:S(2)}, u32[]{:S(2)}) collective-permute-start(f32[1216,128]{1,0:T(8,128)S(1)} %bitcast.386), channel_id=1, source_target_pairs={{0,1},{1,0},{2,3},{3,2},{4,5},{5,4},{6,7},{7,6},{8,9},{9,8},{10,11... | collective-permute-start | bytes 1867784 | tf_op jit(solution)/shard_map/ppermute | solution.py:76
  97.2 1.6 %copy-start.11 = (bf16[128,284]{1,0:T(8,128)(2,1)}, bf16[128,284]{1,0:T(8,128)(2,1)S(1)}, u32[]{:S(2)}) copy-start(bf16[128,284]{1,0:T(8,128)(2,1)S(1)} %collective-permute-done.11) | copy-start | bytes 218116

commit v18 on v17

--- a/solution.py
+++ b/solution.py
@@ -192,8 +192,9 @@
     for shift in range(1, chan_count):
         pairs = [(i, (i + shift) % chan_count) for i in range(chan_count)]
         kernel_t = jnp.swapaxes(kernel_cols[shift], 2, 3)
-        inner = conv_taps(kernel_t, grad_field, row_count - 2, column_count - 2, True)
-        interiors.append(lax.ppermute(inner.astype(jnp.bfloat16), "chan", pairs))
+        zero_pad = jnp.pad(grad_field, ((0, 0), (1, 1), (1, 1)))
+        early = conv_taps(kernel_t, zero_pad, row_count, column_count, True)
+        interiors.append(lax.ppermute(early.astype(jnp.bfloat16), "chan", pairs))
         whole = conv_taps(kernel_t, grad_pad, row_count, column_count, True)
         outgoing.append(border_of(whole.reshape(own_channels, row_count, column_count)).astype(jnp.bfloat16))
     grad_pad, outgoing = lax.optimization_barrier((grad_pad, outgoing))
@@ -201,7 +202,7 @@
     for shift in range(1, chan_count):
         pairs = [(i, (i + shift) % chan_count) for i in range(chan_count)]
         ring = lax.ppermute(outgoing[shift - 1], "chan", pairs)
-        inner = interiors[shift - 1].reshape(own_channels, row_count - 2, column_count - 2)
+        inner = interiors[shift - 1].reshape(own_channels, row_count, column_count)[:, 1:-1, 1:-1]
         received.append(with_border(inner, ring).reshape(own_channels, -1))
     own_part = conv_taps(jnp.swapaxes(kernel_cols[0], 2, 3), grad_pad, row_count, column_count, True)
     for piece in received:

time: 110 us -> 92 us (0.84)
  local copies, waits for them, and re-layouts: 41 us -> 20.9 us
  other arithmetic: 9.57 us -> 11.4 us
    reshape x11 -> x0, local copies, waits for them, and re-layouts: 16.4 us -> none  [the longest x9 14.1 us: window_of(): return field[:, first_row:first_row + row_count, first_col:first_col + co...]
    unnamed x35 -> x22, local copies, waits for them, and re-layouts: 6.85 us -> 4.83 us
    ppermute x1, waiting for transfers between devices: 5.9 us -> 7.21 us  [local(): interiors.append(lax.ppermute(early.astype(jnp.bfloat16), 'chan', pairs))]
  transfers between devices with their start and end apart: 18 -> 18, of which waited for: 6 -> 6; matrix products, arithmetic and copies ran while one was open for 47% -> 38% of each run, Pallas kernels for 0% -> 0%
where the time goes in v18:
time: 92 us; the launch traced here: 90.9 us
  starting transfers between devices  22.6 us (25%)
  local copies, waits for them, and re-layouts  20.9 us (23%)
  matrix products  20.5 us (22%)
  waiting for transfers between devices  13.8 us (15%)
  other arithmetic  11.4 us (12%)
  between operations  1.55 us (2%)
    dot_general x45, matrix products, conv_taps(): jnp.dot(kernel[tap_row, tap_col], window, preferred_element_type=jnp.floa...  17.7 us
    ppermute x1, waiting for transfers between devices, local(): interiors.append(lax.ppermute(early.astype(jnp.bfloat16), 'chan', pairs))  7.21 us
    ppermute x3, starting transfers between devices, sum_start(): moved = lax.ppermute(piece, 'lon', pairs)  6.85 us
    slice x5, local copies, waits for them, and re-layouts, window_of(): field[:, first_row:first_row + row_count, first_col:first_col + column_co...  5.33 us
    unnamed x22, local copies, waits for them, and re-layouts  4.83 us
    ppermute x4, starting transfers between devices, direct_all_gather(): pieces.append(lax.ppermute(sent, axis, pairs).astype(jnp.float32))  3.95 us
    ppermute x3, waiting for transfers between devices, sum_start(): moved = lax.ppermute(piece, 'lon', pairs)  3.12 us
    ppermute x1, starting transfers between devices, local(): raw_blocks.append(lax.ppermute(inputs, 'chan', pairs))  3 us
  transfers between devices with their start and end apart: 18, of which 6 were waited for; matrix products, arithmetic and copies ran while one was open for 38% of the time, Pallas kernels for 0%

profile of v18, /device:TPU:0, one launch (start us, length us, event | category | flops | bytes accessed | tf_op | source)
XLA Modules:
  0.0 90.9 jit_solution(10516114031098318317)
XLA Ops:
  0.7 1.6 %copy.17 = bf16[128,16,128]{0,2,1:T(8,128)(2,1)S(1)} copy(bf16[128,16,128]{2,1,0:T(8,128)(2,1)} %param.4) | data formatting | bytes 1048576 | tf_op args[0]
  2.2 3.0 %collective-permute-start.5 = (bf16[128,16,128]{0,2,1:T(8,128)(2,1)S(1)}, bf16[128,16,128]{0,2,1:T(8,128)(2,1)}, u32[]{:S(2)}, u32[]{:S(2)}) collective-permute-start(bf16[128,16,128]{0,2,1:T(8,128)(2,1)S(1)} %copy.17), channel_id=1, source_target_pairs={{0,2},{2,0},{1,3},{3,1},{4,6},{6,4},{5,7},{7,5},{8,10},{10,8},{9,1... | collective-permute-start | bytes 1572872 | tf_op jit(solution)/shard_map/ppermute | solution.py:142
  5.2 1.6 %collective-permute-start = (bf16[128,16,1]{0,2,1:T(2,128)(2,1)S(1)}, bf16[128,16,1]{0,2,1:T(2,128)(2,1)S(1)}, u32[]{:S(2)}, u32[]{:S(2)}) collective-permute-start(bf16[128,16,1]{0,2,1:T(2,128)(2,1)S(1)} %get-tuple-element.81), channel_id=1, source_target_pairs={{0,4},{4,8},{8,12},{12,0},{1,5},{5,9},{9,13},{13,1},{2,6},{6,10},{... | collective-permute-start | bytes 12296 | tf_op jit(solution)/shard_map/ppermute | solution.py:14
  6.9 2.2 %collective-permute-start.1 = (bf16[128,16,1]{0,2,1:T(2,128)(2,1)S(1)}, bf16[128,16,1]{0,2,1:T(2,128)(2,1)S(1)}, u32[]{:S(2)}, u32[]{:S(2)}) collective-permute-start(bf16[128,16,1]{0,2,1:T(2,128)(2,1)S(1)} %get-tuple-element.82), channel_id=1, source_target_pairs={{4,0},{8,4},{12,8},{0,12},{5,1},{9,5},{13,9},{1,13},{6,2},{10,6},{... | collective-permute-start | bytes 12296 | tf_op jit(solution)/shard_map/ppermute | solution.py:15
  12.6 0.9 %fusion.76 = (bf16[128,16,128]{0,2,1:T(8,128)(2,1)S(1)}, bf16[128,16,128]{0,2,1:T(8,128)(2,1)S(1)}, bf16[128,16,128]{0,2,1:T(8,128)(2,1)S(1)}, bf16[128,16,128]{...) fusion(bf16[128,18,130]{0,2,1:T(8,128)(2,1)S(1)} %maximum_selec, ...), kind=kLoop, calls=%fused_computation.247 | loop fusion | bytes 9437184 | tf_op jit(solution)/shard_map/slice | solution.py:37
  16.8 2.0 %collective-permute-done.4 = bf16[128,292]{0,1:T(8,128)(2,1)S(1)} collective-permute-done((bf16[128,292]{0,1:T(8,128)(2,1)S(1)}, bf16[128,292]{0,1:T(8,128)(2,1)S(1)}, u32[]{:S(2)}, u32[]{:S(2)}) %collective-permute-start.4) | collective-permute-done | bytes 74784 | tf_op jit(solution)/shard_map/ppermute | solution.py:148
  18.8 1.2 %pad_maximum_fusion.2 = bf16[128,18,130]{0,2,1:T(8,128)(2,1)S(1)} fusion(bf16[128,1,130]{0,2,1:T(8,128)(2,1)S(1)} %get-tuple-element.88, bf16[128,16,1]{0,2,1:T(2,128)(2,1)S(1)} %copy.22, bf16[128,16,128]{0,2,1:T(8,128)(2,1)} %collective-permute-done.5, bf16[128,16,1]{0,2,1:T(2,128)(2,1)S(1)} %copy.21, bf16[128,1,130]{0,2,1:T(8,128)(2,1)S(1)} %get-tuple-element.87), kind=kLoop, calls=%fused_computation.112 | loop fusion | flops 2995200 | bytes 1198080 | tf_op jit(solution)/shard_map/concatenate | solution.py:132
  20.8 2.7 %fusion.19 = (bf16[256,16,128]{0,2,1:T(8,128)(2,1)S(1)}, bf16[256,16,128]{0,2,1:T(8,128)(2,1)S(1)}, bf16[256,16,128]{0,2,1:T(8,128)(2,1)S(1)}, bf16[256,16,128]{...) fusion(bf16[128,18,130]{0,2,1:T(8,128)(2,1)S(1)} %maximum_selec, ...), kind=kLoop, calls=%fused_computation.102 | loop fusion | flops 18874368 | bytes 10635264 | tf_op jit(solution)/shard_map/concatenate | solution.py:164
  26.4 1.0 %convert_reduce_fusion = (f32[128]{0:T(128)S(1)}, bf16[128,2048]{1,0:T(8,128)(2,1)S(1)}) fusion(f32[128]{0:T(128)S(1)} %copy-done.5, f32[128,2048]{1,0:T(8,128)S(1)} %convolution_add_fusion.32, f32[128,2048]{1,0:T(8,128)S(1)} %convolution_add_fusion.25, bf16[128,2048]{0,1:T(8,128)(2,1)S(1)} %bitcast.439, bf16[3,3,128,256]{3,2,1,0:T(8,128)(2,1)S(1)} %copy-done, ...), kind=kOutput, calls=%fused_computation.110 | convolution fusion | flops 71040896 | bytes 4228104 | tf_op jit(solution)/shard_map/dot_general | solution.py:50
  31.1 0.9 dynamic-slice_bitcast_fusion
  32.1 2.2 %pad_slice_fusion = (bf16[128,16,128]{2,1,0:T(8,128)(2,1)}, bf16[128,16,128]{2,1,0:T(8,128)(2,1)S(1)}, bf16[128,16,128]{2,1,0:T(8,128)(2,1)S(1)}, bf16[128,16,12...) fusion(bf16[128,16,128]{2,1,0:T(8,128)(2,1)S(1)} %bitcast.372), kind=kLoop, calls=%fused_computation | loop fusion | bytes 4718592 | tf_op jit(solution)/shard_map/slice | solution.py:37
  37.6 1.4 %convolution_add_fusion.1 = f32[128,2048]{1,0:T(8,128)S(1)} fusion(f32[128,2048]{1,0:T(8,128)S(1)} %convolution_add_fusion.2, bf16[16,8,16,128]{3,2,1,0:T(8,128)(2,1)} %bitcast.417, bf16[3,3,128,128]{2,3,1,0:T(8,128)(2,1)S(1)} %get-tuple-element.64), kind=kOutput, calls=%fused_computation.13 | convolution fusion | flops 67371008 | bytes 2654208 | tf_op jit(solution)/shard_map/dot_general | solution.py:50
  39.1 1.1 %fusion.5 = bf16[128,2048]{1,0:T(8,128)(2,1)} fusion(f32[128,2048]{1,0:T(8,128)S(1)} %convolution_add_fusion.1, bf16[16,8,16,128]{3,2,1,0:T(8,128)(2,1)S(1)} %bitcast.415, bf16[3,3,128,128]{2,3,1,0:T(8,128)(2,1)S(1)} %get-tuple-element.64), kind=kOutput, calls=%fused_computation.57 | convolution fusion | flops 67633152 | bytes 2129920 | tf_op jit(solution)/shard_map/dot_general | solution.py:50
  40.2 1.7 %collective-permute-start.12 = (bf16[128,2048]{1,0:T(8,128)(2,1)}, bf16[128,2048]{1,0:T(8,128)(2,1)}, u32[]{:S(2)}, u32[]{:S(2)}) collective-permute-start(bf16[128,2048]{1,0:T(8,128)(2,1)} %fusion.5), channel_id=1, source_target_pairs={{0,2},{2,0},{1,3},{3,1},{4,6},{6,4},{5,7},{7,5},{8,10},{10,8},{9,1... | collective-permute-start | bytes 1572872 | tf_op jit(solution)/shard_map/ppermute | solution.py:197
  41.9 1.1 %bitcast_add_fusion = f32[1216,128]{1,0:T(8,128)S(1)} fusion(f32[1216,128]{1,0:T(8,128)} %collective-permute-done.6, f32[2,1216,128]{2,1,0:T(8,128)S(1)} %bitcast.378, s32[]{:T(128)S(6)} %select_n.98), kind=kLoop, calls=%fused_computation.114 | loop fusion | flops 155648 | bytes 1867780 | tf_op jit(solution)/shard_map/add | solution.py:64
  43.1 1.6 %collective-permute-start.7 = (bf16[320,128]{1,0:T(8,128)(2,1)S(1)}, bf16[320,128]{1,0:T(8,128)(2,1)S(1)}, u32[]{:S(2)}, u32[]{:S(2)}) collective-permute-start(bf16[320,128]{1,0:T(8,128)(2,1)S(1)} %pad_maximum_fusion.4), channel_id=1, source_target_pairs={{0,4},{4,8},{8,12},{12,0},{1,5},{5,9},{9,13},{13,1},{2,6},{6,10},{... | collective-permute-start | bytes 245768 | tf_op jit(solution)/shard_map/ppermute | solution.py:104
  44.8 2.4 %collective-permute-start.8 = (bf16[320,128]{1,0:T(8,128)(2,1)S(1)}, bf16[320,128]{1,0:T(8,128)(2,1)S(1)}, u32[]{:S(2)}, u32[]{:S(2)}) collective-permute-start(bf16[320,128]{1,0:T(8,128)(2,1)S(1)} %pad_maximum_fusion.5), channel_id=1, source_target_pairs={{0,12},{4,0},{8,4},{12,8},{1,13},{5,1},{9,5},{13,9},{2,14},{6,2},{... | collective-permute-start | bytes 245768 | tf_op jit(solution)/shard_map/ppermute | solution.py:104
  47.6 7.2 %collective-permute-done.12 = bf16[128,2048]{1,0:T(8,128)(2,1)} collective-permute-done((bf16[128,2048]{1,0:T(8,128)(2,1)}, bf16[128,2048]{1,0:T(8,128)(2,1)}, u32[]{:S(2)}, u32[]{:S(2)}) %collective-permute-start.12) | collective-permute-done | bytes 524320 | tf_op jit(solution)/shard_map/ppermute | solution.py:197
  54.8 1.1 %copy.60 = bf16[16,8,16,128]{3,2,1,0:T(8,128)(2,1)S(1)} copy(bf16[16,8,16,128]{3,1,2,0:T(8,128)(2,1)} %bitcast.156) | data formatting | bytes 1048576
  56.0 1.1 %slice.578 = bf16[128,14,126]{2,1,0:T(8,128)(2,1)} slice(bf16[128,16,128]{2,1,0:T(8,128)(2,1)S(1)} %bitcast.438), slice={[0:128], [1:15], [1:127]} | slice | bytes 903168 | tf_op jit(solution)/shard_map/slice | solution.py:205
  57.1 2.8 %collective-permute-start.13 = (bf16[304,128]{1,0:T(8,128)(2,1)S(1)}, bf16[304,128]{1,0:T(8,128)(2,1)S(1)}, u32[]{:S(2)}, u32[]{:S(2)}) collective-permute-start(bf16[304,128]{1,0:T(8,128)(2,1)S(1)} %get-tuple-element.60), channel_id=1, source_target_pairs={{0,8},{4,12},{8,0},{12,4},{1,9},{5,13},{9,1},{13,5},{2,10},{6,14},... | collective-permute-start | bytes 233480 | tf_op jit(solution)/shard_map/ppermute | solution.py:104
  60.9 3.1 %collective-permute-done.13 = bf16[304,128]{1,0:T(8,128)(2,1)S(1)} collective-permute-done((bf16[304,128]{1,0:T(8,128)(2,1)S(1)}, bf16[304,128]{1,0:T(8,128)(2,1)S(1)}, u32[]{:S(2)}, u32[]{:S(2)}) %collective-permute-start.13) | collective-permute-done | bytes 77856 | tf_op jit(solution)/shard_map/ppermute | solution.py:104
  64.7 3.3 %collective-permute-start.14 = (bf16[304,128]{1,0:T(8,128)(2,1)}, bf16[304,128]{1,0:T(8,128)(2,1)S(1)}, u32[]{:S(2)}, u32[]{:S(2)}) collective-permute-start(bf16[304,128]{1,0:T(8,128)(2,1)} %get-tuple-element.9), channel_id=1, source_target_pairs={{0,12},{4,0},{8,4},{12,8},{1,13},{5,1},{9,5},{13,9},{2,14},{6,2},{... | collective-permute-start | bytes 233480 | tf_op jit(solution)/shard_map/ppermute | solution.py:76
  73.2 0.9 copy.46
  75.0 1.6 %collective-permute-start.11 = (bf16[128,284]{1,0:T(8,128)(2,1)S(1)}, bf16[128,284]{1,0:T(8,128)(2,1)S(1)}, u32[]{:S(2)}, u32[]{:S(2)}) collective-permute-start(bf16[128,284]{1,0:T(8,128)(2,1)S(1)} %pad_maximum_fusion.3), channel_id=1, source_target_pairs={{0,2},{2,0},{1,3},{3,1},{4,6},{6,4},{5,7},{7,5},{8,10},{10,8},{9,1... | collective-permute-start | bytes 218120 | tf_op jit(solution)/shard_map/ppermute | solution.py:204
  80.5 0.9 copy.34
  81.4 1.7 %copy.35 = bf16[128,14,1]{2,1,0:T(8,128)(2,1)} copy(bf16[128,14,1]{1,0,2:T(8,128)(2,1)S(1)} %get-tuple-element.86) | data formatting | bytes 7168 | tf_op jit(solution)/shard_map/broadcast_in_dim | solution.py:131
  83.3 1.9 %maximum_convert_fusion = f32[128,16,128]{2,1,0:T(8,128)S(1)} fusion(bf16[128,1,128]{2,1,0:T(2,128)(2,1)S(1)} %copy.37, bf16[128,14,1]{2,1,0:T(8,128)(2,1)} %copy.35, bf16[128,14,126]{2,1,0:T(8,128)(2,1)S(1)} %copy-done.2, bf16[128,14,1]{2,1,0:T(8,128)(2,1)S(1)} %copy.34, bf16[128,1,128]{2,1,0:T(2,128)(2,1)S(1)} %copy.36), kind=kLoop, calls=%fused_computation.135 | loop fusion | flops 2621440 | bytes 1572864 | tf_op jit(solution)/shard_map/convert_element_type | solution.py:209
  85.2 1.3 %fusion.9 = bf16[16,8,16,128]{3,1,2,0:T(8,128)(2,1)S(1)} fusion(f32[128,2048]{1,0:T(8,128)S(1)} %convolution_add_fusion.9, bf16[128,2048]{0,1:T(8,128)(2,1)S(1)} %bitcast.395, f32[16,8,16,128]{3,2,1,0:T(8,128)S(1)} %bitcast.383, bf16[3,3,128,128]{2,3,1,0:T(8,128)(2,1)} %get-tuple-element.63), kind=kOutput, calls=%fused_computation.82 | convolution fusion | flops 67895296 | bytes 3178496 | tf_op jit(solution)/shard_map/dot_general | solution.py:50
  86.5 0.9 copy.62
  87.4 1.3 %fusion.8 = f32[2,1216,128]{2,1,0:T(8,128)S(1)} fusion(s32[]{:T(128)S(6)} %select_n.112, f32[1,1216,128]{2,1,0:T(8,128)} %bitcast.122, f32[1,1216,128]{2,1,0:T(8,128)S(1)} %bitcast.394), kind=kLoop, calls=%fused_computation.79 | loop fusion | flops 933888 | bytes 2490372 | tf_op jit(solution)/shard_map/jit(_roll_dynamic)/concatenate | solution.py:78
  89.7 1.2 %fusion.11 = f32[3,3,128,256]{3,2,1,0:T(8,128)} fusion(s32[]{:T(128)S(6)} %select_n.114, f32[3,3,128,256]{3,2,1,0:T(8,128)S(1)} %reshape.286), kind=kLoop, calls=%fused_computation.84 | loop fusion | flops 294912 | bytes 2359300 | tf_op jit(solution)/shard_map/concatenate | solution.py:184
  (149 shorter events, 30.1 us)
Async XLA Ops:
  0.6 8.5 %copy-start.4 = (bf16[128,16,128]{2,1,0:T(8,128)(2,1)S(1)}, bf16[128,16,128]{2,1,0:T(8,128)(2,1)}, u32[]{:S(2)}) copy-start(bf16[128,16,128]{2,1,0:T(8,128)(2,1)} %param.5) | copy-start | bytes 1572868
  0.6 8.6 %copy-start = (bf16[3,3,128,256]{3,2,1,0:T(8,128)(2,1)S(1)}, bf16[3,3,128,256]{3,2,1,0:T(8,128)(2,1)}, u32[]{:S(2)}) copy-start(bf16[3,3,128,256]{3,2,1,0:T(8,128)(2,1)} %param.6) | copy-start | bytes 1769476
  2.2 16.6 %collective-permute-start.5 = (bf16[128,16,128]{0,2,1:T(8,128)(2,1)S(1)}, bf16[128,16,128]{0,2,1:T(8,128)(2,1)}, u32[]{:S(2)}, u32[]{:S(2)}) collective-permute-start(bf16[128,16,128]{0,2,1:T(8,128)(2,1)S(1)} %copy.17), channel_id=1, source_target_pairs={{0,2},{2,0},{1,3},{3,1},{4,6},{6,4},{5,7},{7,5},{8,10},{10,8},{9,1... | collective-permute-start | bytes 1572872 | tf_op jit(solution)/shard_map/ppermute | solution.py:142
  5.2 5.5 %collective-permute-start = (bf16[128,16,1]{0,2,1:T(2,128)(2,1)S(1)}, bf16[128,16,1]{0,2,1:T(2,128)(2,1)S(1)}, u32[]{:S(2)}, u32[]{:S(2)}) collective-permute-start(bf16[128,16,1]{0,2,1:T(2,128)(2,1)S(1)} %get-tuple-element.81), channel_id=1, source_target_pairs={{0,4},{4,8},{8,12},{12,0},{1,5},{5,9},{9,13},{13,1},{2,6},{6,10},{... | collective-permute-start | bytes 12296 | tf_op jit(solution)/shard_map/ppermute | solution.py:14
  6.9 3.9 %collective-permute-start.1 = (bf16[128,16,1]{0,2,1:T(2,128)(2,1)S(1)}, bf16[128,16,1]{0,2,1:T(2,128)(2,1)S(1)}, u32[]{:S(2)}, u32[]{:S(2)}) collective-permute-start(bf16[128,16,1]{0,2,1:T(2,128)(2,1)S(1)} %get-tuple-element.82), channel_id=1, source_target_pairs={{4,0},{8,4},{12,8},{0,12},{5,1},{9,5},{13,9},{1,13},{6,2},{10,6},{... | collective-permute-start | bytes 12296 | tf_op jit(solution)/shard_map/ppermute | solution.py:15
  10.8 1.3 %collective-permute-start.2 = (bf16[128,1,130]{0,2,1:T(8,128)(2,1)S(1)}, bf16[128,1,130]{0,2,1:T(8,128)(2,1)S(1)}, u32[]{:S(2)}, u32[]{:S(2)}) collective-permute-start(bf16[128,1,130]{0,2,1:T(8,128)(2,1)S(1)} %get-tuple-element.67), channel_id=1, source_target_pairs={{0,1},{1,0},{2,3},{3,2},{4,5},{5,4},{6,7},{7,6},{8,9},{9,8},{10,11... | collective-permute-start | bytes 99848 | tf_op jit(solution)/shard_map/ppermute | solution.py:14
  10.8 1.4 %collective-permute-start.3 = (bf16[128,1,130]{0,2,1:T(8,128)(2,1)S(1)}, bf16[128,1,130]{0,2,1:T(8,128)(2,1)S(1)}, u32[]{:S(2)}, u32[]{:S(2)}) collective-permute-start(bf16[128,1,130]{0,2,1:T(8,128)(2,1)S(1)} %get-tuple-element.68), channel_id=1, source_target_pairs={{1,0},{0,1},{3,2},{2,3},{5,4},{4,5},{7,6},{6,7},{9,8},{8,9},{11,10... | collective-permute-start | bytes 99848 | tf_op jit(solution)/shard_map/ppermute | solution.py:15
  13.5 5.2 %collective-permute-start.4 = (bf16[128,292]{0,1:T(8,128)(2,1)S(1)}, bf16[128,292]{0,1:T(8,128)(2,1)S(1)}, u32[]{:S(2)}, u32[]{:S(2)}) collective-permute-start(bf16[128,292]{0,1:T(8,128)(2,1)S(1)} %pad_maximum_fusion.6), channel_id=1, source_target_pairs={{0,2},{2,0},{1,3},{3,1},{4,6},{6,4},{5,7},{7,5},{8,10},{10,8},{9,1... | collective-permute-start | bytes 224264 | tf_op jit(solution)/shard_map/ppermute | solution.py:148
  25.7 0.7 copy-start.5
  32.0 9.9 %collective-permute-start.6 = (f32[1216,128]{1,0:T(8,128)}, f32[1216,128]{1,0:T(8,128)}, u32[]{:S(2)}, u32[]{:S(2)}) collective-permute-start(f32[1216,128]{1,0:T(8,128)} %dynamic-slice_bitcast_fusion), channel_id=1, source_target_pairs={{0,1},{1,0},{2,3},{3,2},{4,5},{5,4},{6,7},{7,6},{8,9},{9,8},{10,11... | collective-permute-start | bytes 1867784 | tf_op jit(solution)/shard_map/ppermute | solution.py:64
  37.6 1.4 %copy-start.1 = (bf16[128,16,128]{2,1,0:T(8,128)(2,1)S(1)}, bf16[128,16,128]{2,1,0:T(8,128)(2,1)}, u32[]{:S(2)}) copy-start(bf16[128,16,128]{2,1,0:T(8,128)(2,1)} %get-tuple-element.69) | copy-start | bytes 1572868
  40.2 14.6 %collective-permute-start.12 = (bf16[128,2048]{1,0:T(8,128)(2,1)}, bf16[128,2048]{1,0:T(8,128)(2,1)}, u32[]{:S(2)}, u32[]{:S(2)}) collective-permute-start(bf16[128,2048]{1,0:T(8,128)(2,1)} %fusion.5), channel_id=1, source_target_pairs={{0,2},{2,0},{1,3},{3,1},{4,6},{6,4},{5,7},{7,5},{8,10},{10,8},{9,1... | collective-permute-start | bytes 1572872 | tf_op jit(solution)/shard_map/ppermute | solution.py:197
  43.1 16.8 %collective-permute-start.7 = (bf16[320,128]{1,0:T(8,128)(2,1)S(1)}, bf16[320,128]{1,0:T(8,128)(2,1)S(1)}, u32[]{:S(2)}, u32[]{:S(2)}) collective-permute-start(bf16[320,128]{1,0:T(8,128)(2,1)S(1)} %pad_maximum_fusion.4), channel_id=1, source_target_pairs={{0,4},{4,8},{8,12},{12,0},{1,5},{5,9},{9,13},{13,1},{2,6},{6,10},{... | collective-permute-start | bytes 245768 | tf_op jit(solution)/shard_map/ppermute | solution.py:104
  44.8 15.3 %collective-permute-start.8 = (bf16[320,128]{1,0:T(8,128)(2,1)S(1)}, bf16[320,128]{1,0:T(8,128)(2,1)S(1)}, u32[]{:S(2)}, u32[]{:S(2)}) collective-permute-start(bf16[320,128]{1,0:T(8,128)(2,1)S(1)} %pad_maximum_fusion.5), channel_id=1, source_target_pairs={{0,12},{4,0},{8,4},{12,8},{1,13},{5,1},{9,5},{13,9},{2,14},{6,2},{... | collective-permute-start | bytes 245768 | tf_op jit(solution)/shard_map/ppermute | solution.py:104
  57.1 6.9 %collective-permute-start.13 = (bf16[304,128]{1,0:T(8,128)(2,1)S(1)}, bf16[304,128]{1,0:T(8,128)(2,1)S(1)}, u32[]{:S(2)}, u32[]{:S(2)}) collective-permute-start(bf16[304,128]{1,0:T(8,128)(2,1)S(1)} %get-tuple-element.60), channel_id=1, source_target_pairs={{0,8},{4,12},{8,0},{12,4},{1,9},{5,13},{9,1},{13,5},{2,10},{6,14},... | collective-permute-start | bytes 233480 | tf_op jit(solution)/shard_map/ppermute | solution.py:104
  60.3 8.2 %collective-permute-start.10 = (bf16[128,1,130]{0,2,1:T(8,128)(2,1)S(1)}, bf16[128,1,130]{0,2,1:T(8,128)(2,1)S(1)}, u32[]{:S(2)}, u32[]{:S(2)}) collective-permute-start(bf16[128,1,130]{0,2,1:T(8,128)(2,1)S(1)} %get-tuple-element.66), channel_id=1, source_target_pairs={{1,0},{0,1},{3,2},{2,3},{5,4},{4,5},{7,6},{6,7},{9,8},{8,9},{11,10... | collective-permute-start | bytes 99848 | tf_op jit(solution)/shard_map/ppermute | solution.py:15
  60.4 8.2 %collective-permute-start.9 = (bf16[128,1,130]{0,2,1:T(8,128)(2,1)S(1)}, bf16[128,1,130]{0,2,1:T(8,128)(2,1)S(1)}, u32[]{:S(2)}, u32[]{:S(2)}) collective-permute-start(bf16[128,1,130]{0,2,1:T(8,128)(2,1)S(1)} %get-tuple-element.65), channel_id=1, source_target_pairs={{0,1},{1,0},{2,3},{3,2},{4,5},{5,4},{6,7},{7,6},{8,9},{9,8},{10,11... | collective-permute-start | bytes 99848 | tf_op jit(solution)/shard_map/ppermute | solution.py:14
  64.7 15.4 %collective-permute-start.14 = (bf16[304,128]{1,0:T(8,128)(2,1)}, bf16[304,128]{1,0:T(8,128)(2,1)S(1)}, u32[]{:S(2)}, u32[]{:S(2)}) collective-permute-start(bf16[304,128]{1,0:T(8,128)(2,1)} %get-tuple-element.9), channel_id=1, source_target_pairs={{0,12},{4,0},{8,4},{12,8},{1,13},{5,1},{9,5},{13,9},{2,14},{6,2},{... | collective-permute-start | bytes 233480 | tf_op jit(solution)/shard_map/ppermute | solution.py:76
  68.0 12.1 %collective-permute-start.15 = (bf16[304,128]{1,0:T(8,128)(2,1)}, bf16[304,128]{1,0:T(8,128)(2,1)S(1)}, u32[]{:S(2)}, u32[]{:S(2)}) collective-permute-start(bf16[304,128]{1,0:T(8,128)(2,1)} %get-tuple-element.9), channel_id=1, source_target_pairs={{0,8},{4,12},{8,0},{12,4},{1,9},{5,13},{9,1},{13,5},{2,10},{6,14},... | collective-permute-start | bytes 233480 | tf_op jit(solution)/shard_map/ppermute | solution.py:76
  68.0 12.1 %collective-permute-start.16 = (bf16[304,128]{1,0:T(8,128)(2,1)}, bf16[304,128]{1,0:T(8,128)(2,1)S(1)}, u32[]{:S(2)}, u32[]{:S(2)}) collective-permute-start(bf16[304,128]{1,0:T(8,128)(2,1)} %get-tuple-element.9), channel_id=1, source_target_pairs={{0,4},{4,8},{8,12},{12,0},{1,5},{5,9},{9,13},{13,1},{2,6},{6,10},{... | collective-permute-start | bytes 233480 | tf_op jit(solution)/shard_map/ppermute | solution.py:76
  75.0 2.4 %copy-start.3 = (bf16[3,3,128,128]{2,3,1,0:T(8,128)(2,1)S(1)}, bf16[3,3,128,128]{2,3,1,0:T(8,128)(2,1)}, u32[]{:S(2)}) copy-start(bf16[3,3,128,128]{2,3,1,0:T(8,128)(2,1)} %get-tuple-element.63) | copy-start | bytes 884740
  75.0 5.4 %collective-permute-start.11 = (bf16[128,284]{1,0:T(8,128)(2,1)S(1)}, bf16[128,284]{1,0:T(8,128)(2,1)S(1)}, u32[]{:S(2)}, u32[]{:S(2)}) collective-permute-start(bf16[128,284]{1,0:T(8,128)(2,1)S(1)} %pad_maximum_fusion.3), channel_id=1, source_target_pairs={{0,2},{2,0},{1,3},{3,1},{4,6},{6,4},{5,7},{7,5},{8,10},{10,8},{9,1... | collective-permute-start | bytes 218120 | tf_op jit(solution)/shard_map/ppermute | solution.py:204
  80.3 3.0 %copy-start.2 = (bf16[128,14,126]{2,1,0:T(8,128)(2,1)S(1)}, bf16[128,14,126]{2,1,0:T(8,128)(2,1)}, u32[]{:S(2)}) copy-start(bf16[128,14,126]{2,1,0:T(8,128)(2,1)} %slice.578) | copy-start | bytes 1354756
  80.3 7.1 %collective-permute-start.17 = (f32[1216,128]{1,0:T(8,128)S(1)}, f32[1216,128]{1,0:T(8,128)}, u32[]{:S(2)}, u32[]{:S(2)}) collective-permute-start(f32[1216,128]{1,0:T(8,128)S(1)} %bitcast.393), channel_id=1, source_target_pairs={{0,1},{1,0},{2,3},{3,2},{4,5},{5,4},{6,7},{7,6},{8,9},{9,8},{10,11... | collective-permute-start | bytes 1867784 | tf_op jit(solution)/shard_map/ppermute | solution.py:76

commit v19 on v16

--- a/solution.py
+++ b/solution.py
@@ -197,6 +197,7 @@
         pairs = [(i, (i + shift) % chan_count) for i in range(chan_count)]
         received.append(lax.ppermute(outgoing[shift - 1], "chan", pairs))
     own_part = conv_taps(jnp.swapaxes(kernel_cols[0], 2, 3), grad_pad, row_count, column_count, True)
+    own_part, weight_grad, bias_grad = lax.optimization_barrier((own_part, weight_grad, bias_grad))
     for piece in received:
         own_part = own_part + piece.astype(jnp.float32)
     input_grad = own_part.astype(jnp.bfloat16).reshape(own_channels, row_count, column_count)

time: 70.3 us -> 70.1 us (level)
  waiting for transfers between devices: 19 us -> 17 us
  other arithmetic: 6.65 us -> 7.67 us
  matrix products: 14.7 us -> 15.5 us
    ppermute x1, waiting for transfers between devices: 8.51 us -> 5.4 us  [local(): received.append(lax.ppermute(outgoing[shift - 1], 'chan', pairs))]
    ppermute x4, waiting for transfers between devices: 0.01 us -> 1.07 us  [direct_all_gather(): pieces.append(lax.ppermute(sent, axis, pairs).astype(jnp.float32))]
    unnamed x8, other arithmetic: 0.33 us -> 1.35 us
    dot_general x36, matrix products: 11.9 us -> 12.7 us  [conv_taps(): jnp.dot(kernel[tap_row, tap_col], window, preferred_element_type=jnp.floa...]
  transfers between devices with their start and end apart: 17 -> 17, of which waited for: 9 -> 10; matrix products, arithmetic and copies ran while one was open for 22% -> 25% of each run, Pallas kernels for 0% -> 0%
where the time goes in v19:
time: 70.1 us; the launch traced here: 69.8 us
  starting transfers between devices  17.9 us (26%)
  waiting for transfers between devices  17 us (24%)
  matrix products  15.5 us (22%)
  local copies, waits for them, and re-layouts  10.3 us (15%)
  other arithmetic  7.67 us (11%)
  between operations  1.47 us (2%)
    dot_general x36, matrix products, conv_taps(): jnp.dot(kernel[tap_row, tap_col], window, preferred_element_type=jnp.floa...  12.7 us
    ppermute x1, waiting for transfers between devices, local(): received.append(lax.ppermute(outgoing[shift - 1], 'chan', pairs))  5.4 us
    ppermute x3, waiting for transfers between devices, sum_start(): moved = lax.ppermute(piece, 'lon', pairs)  5.21 us
    ppermute x3, starting transfers between devices, sum_start(): moved = lax.ppermute(piece, 'lon', pairs)  4.99 us
    slice x4, local copies, waits for them, and re-layouts, window_of(): field[:, first_row:first_row + row_count, first_col:first_col + column_co...  3.74 us
    unnamed x12, local copies, waits for them, and re-layouts  3.51 us
    ppermute x1, starting transfers between devices, local(): raw_blocks.append(lax.ppermute(inputs, 'chan', pairs))  3 us
    dot_general x9, matrix products, local(): lax.dot_general(grad_pre, window, (((1,), (1,)), ((), ())), preferred_ele...  2.85 us
  transfers between devices with their start and end apart: 17, of which 10 were waited for; matrix products, arithmetic and copies ran while one was open for 25% of the time, Pallas kernels for 0%

profile of v19, /device:TPU:0, one launch (start us, length us, event | category | flops | bytes accessed | tf_op | source)
XLA Modules:
  0.0 69.8 jit_solution(16270307126708301518)
XLA Ops:
  0.6 1.5 %copy.12 = bf16[128,16,128]{0,2,1:T(8,128)(2,1)S(1)} copy(bf16[128,16,128]{2,1,0:T(8,128)(2,1)} %param.4) | data formatting | bytes 1048576 | tf_op args[0]
  2.2 3.0 %collective-permute-start.5 = (bf16[128,16,128]{0,2,1:T(8,128)(2,1)S(1)}, bf16[128,16,128]{0,2,1:T(8,128)(2,1)S(1)}, u32[]{:S(2)}, u32[]{:S(2)}) collective-permute-start(bf16[128,16,128]{0,2,1:T(8,128)(2,1)S(1)} %copy.12), channel_id=1, source_target_pairs={{0,2},{2,0},{1,3},{3,1},{4,6},{6,4},{5,7},{7,5},{8,10},{10,8},{9,1... | collective-permute-start | bytes 1572872 | tf_op jit(solution)/shard_map/ppermute | solution.py:142
  5.2 1.6 %collective-permute-start = (bf16[128,16,1]{0,2,1:T(2,128)(2,1)S(1)}, bf16[128,16,1]{0,2,1:T(2,128)(2,1)S(1)}, u32[]{:S(2)}, u32[]{:S(2)}) collective-permute-start(bf16[128,16,1]{0,2,1:T(2,128)(2,1)S(1)} %get-tuple-element.75), channel_id=1, source_target_pairs={{0,4},{4,8},{8,12},{12,0},{1,5},{5,9},{9,13},{13,1},{2,6},{6,10},{... | collective-permute-start | bytes 12296 | tf_op jit(solution)/shard_map/ppermute | solution.py:14
  6.8 2.2 %collective-permute-start.1 = (bf16[128,16,1]{0,2,1:T(2,128)(2,1)S(1)}, bf16[128,16,1]{0,2,1:T(2,128)(2,1)S(1)}, u32[]{:S(2)}, u32[]{:S(2)}) collective-permute-start(bf16[128,16,1]{0,2,1:T(2,128)(2,1)S(1)} %get-tuple-element.76), channel_id=1, source_target_pairs={{4,0},{8,4},{12,8},{0,12},{5,1},{9,5},{13,9},{1,13},{6,2},{10,6},{... | collective-permute-start | bytes 12296 | tf_op jit(solution)/shard_map/ppermute | solution.py:15
  9.2 1.5 %collective-permute-done = bf16[128,16,1]{0,2,1:T(2,128)(2,1)S(1)} collective-permute-done((bf16[128,16,1]{0,2,1:T(2,128)(2,1)S(1)}, bf16[128,16,1]{0,2,1:T(2,128)(2,1)S(1)}, u32[]{:S(2)}, u32[]{:S(2)}) %collective-permute-start) | collective-permute-done | bytes 4128 | tf_op jit(solution)/shard_map/ppermute | solution.py:14
  11.3 0.7 collective-permute-done.2
  12.5 0.9 %fusion.55 = (bf16[128,16,128]{0,2,1:T(8,128)(2,1)S(1)}, bf16[128,16,128]{0,2,1:T(8,128)(2,1)S(1)}, bf16[128,16,128]{0,2,1:T(8,128)(2,1)S(1)}, bf16[128,16,128]{...) fusion(bf16[128,18,130]{0,2,1:T(8,128)(2,1)S(1)} %maximum_selec, ...), kind=kLoop, calls=%fused_computation.203 | loop fusion | bytes 9437184 | tf_op jit(solution)/shard_map/slice | solution.py:37
  16.7 2.0 %collective-permute-done.4 = bf16[128,292]{0,1:T(8,128)(2,1)S(1)} collective-permute-done((bf16[128,292]{0,1:T(8,128)(2,1)S(1)}, bf16[128,292]{0,1:T(8,128)(2,1)S(1)}, u32[]{:S(2)}, u32[]{:S(2)}) %collective-permute-start.4) | collective-permute-done | bytes 74784 | tf_op jit(solution)/shard_map/ppermute | solution.py:148
  19.0 1.0 %fusion.53 = (bf16[128,16,128]{0,2,1:T(8,128)(2,1)S(1)}, bf16[128,16,128]{0,2,1:T(8,128)(2,1)S(1)}, bf16[128,16,128]{0,2,1:T(8,128)(2,1)S(1)}, bf16[128,16,128]{...) fusion(bf16[128,18,130]{0,2,1:T(8,128)(2,1)S(1)} %pad_maximum_f, ...), kind=kLoop, calls=%fused_computation.201 | loop fusion | bytes 9437184 | tf_op jit(solution)/shard_map/slice | solution.py:37
  19.9 2.5 %fusion.14 = (bf16[256,16,128]{0,2,1:T(8,128)(2,1)S(1)}, bf16[256,16,128]{0,2,1:T(8,128)(2,1)S(1)}, bf16[256,16,128]{0,2,1:T(8,128)(2,1)S(1)}, bf16[256,16,128]{...) fusion(bf16[128,18,130]{0,2,1:T(8,128)(2,1)S(1)} %maximum_selec, ...), kind=kLoop, calls=%fused_computation.81 | loop fusion | flops 18874368 | bytes 10635264 | tf_op jit(solution)/shard_map/concatenate | solution.py:164
  25.3 1.0 %convert_reduce_fusion = (f32[128]{0:T(128)S(1)}, bf16[128,2048]{1,0:T(8,128)(2,1)S(1)}) fusion(f32[128]{0:T(128)S(1)} %copy-done.2, f32[128,2048]{1,0:T(8,128)S(1)} %convolution_add_fusion.24, f32[128,2048]{1,0:T(8,128)S(1)} %convolution_add_fusion.17, bf16[128,2048]{0,1:T(8,128)(2,1)S(1)} %bitcast.358, bf16[3,3,128,256]{3,2,1,0:T(8,128)(2,1)S(1)} %copy-done, ...), kind=kOutput, calls=%fused_computation.90 | convolution fusion | flops 71040896 | bytes 4228104 | tf_op jit(solution)/shard_map/dot_general | solution.py:50
  29.4 0.6 copy.28
  30.5 0.8 %slice_reduce_fusion.1 = (bf16[128,16]{1,0:T(8,128)(2,1)S(1)}, bf16[128,16]{1,0:T(8,128)(2,1)S(1)}) fusion(bf16[128,16,128]{2,1,0:T(8,128)(2,1)S(1)} %bitcast.304), kind=kLoop, calls=%fused_computation.98 | loop fusion | bytes 16384 | tf_op jit(solution)/shard_map/slice | solution.py:179
  31.5 0.9 %collective-permute-done.6 = f32[1216,128]{1,0:T(8,128)} collective-permute-done((f32[1216,128]{1,0:T(8,128)S(1)}, f32[1216,128]{1,0:T(8,128)}, u32[]{:S(2)}, u32[]{:S(2)}) %collective-permute-start.6) | collective-permute-done | bytes 622624 | tf_op jit(solution)/shard_map/ppermute | solution.py:64
  32.4 1.1 %bitcast_add_fusion = f32[1216,128]{1,0:T(8,128)S(1)} fusion(f32[1216,128]{1,0:T(8,128)} %collective-permute-done.6, f32[2,1216,128]{2,1,0:T(8,128)S(1)} %bitcast.307, s32[]{:T(128)S(6)} %select_n.98), kind=kLoop, calls=%fused_computation.94 | loop fusion | flops 155648 | bytes 1867780 | tf_op jit(solution)/shard_map/add | solution.py:64
  33.6 1.9 %collective-permute-start.7 = (bf16[320,128]{1,0:T(8,128)(2,1)S(1)}, bf16[320,128]{1,0:T(8,128)(2,1)S(1)}, u32[]{:S(2)}, u32[]{:S(2)}) collective-permute-start(bf16[320,128]{1,0:T(8,128)(2,1)S(1)} %pad_maximum_fusion.3), channel_id=1, source_target_pairs={{0,4},{4,8},{8,12},{12,0},{1,5},{5,9},{9,13},{13,1},{2,6},{6,10},{... | collective-permute-start | bytes 245768 | tf_op jit(solution)/shard_map/ppermute | solution.py:104
  35.5 2.3 %collective-permute-start.8 = (bf16[320,128]{1,0:T(8,128)(2,1)S(1)}, bf16[320,128]{1,0:T(8,128)(2,1)S(1)}, u32[]{:S(2)}, u32[]{:S(2)}) collective-permute-start(bf16[320,128]{1,0:T(8,128)(2,1)S(1)} %pad_maximum_fusion.4), channel_id=1, source_target_pairs={{0,12},{4,0},{8,4},{12,8},{1,13},{5,1},{9,5},{13,9},{2,14},{6,2},{... | collective-permute-start | bytes 245768 | tf_op jit(solution)/shard_map/ppermute | solution.py:104
  38.4 0.8 %collective-permute-start.11 = (bf16[304,128]{1,0:T(8,128)(2,1)S(1)}, bf16[304,128]{1,0:T(8,128)(2,1)S(1)}, u32[]{:S(2)}, u32[]{:S(2)}) collective-permute-start(bf16[304,128]{1,0:T(8,128)(2,1)S(1)} %get-tuple-element.66), channel_id=1, source_target_pairs={{0,8},{4,12},{8,0},{12,4},{1,9},{5,13},{9,1},{13,5},{2,10},{6,14},... | collective-permute-start | bytes 233480 | tf_op jit(solution)/shard_map/ppermute | solution.py:104
  39.2 1.4 %collective-permute-done.7 = bf16[320,128]{1,0:T(8,128)(2,1)S(1)} collective-permute-done((bf16[320,128]{1,0:T(8,128)(2,1)S(1)}, bf16[320,128]{1,0:T(8,128)(2,1)S(1)}, u32[]{:S(2)}, u32[]{:S(2)}) %collective-permute-start.7) | collective-permute-done | bytes 81952 | tf_op jit(solution)/shard_map/ppermute | solution.py:104
  40.7 0.7 %collective-permute-done.8 = bf16[320,128]{1,0:T(8,128)(2,1)S(1)} collective-permute-done((bf16[320,128]{1,0:T(8,128)(2,1)S(1)}, bf16[320,128]{1,0:T(8,128)(2,1)S(1)}, u32[]{:S(2)}, u32[]{:S(2)}) %collective-permute-start.8) | collective-permute-done | bytes 81952 | tf_op jit(solution)/shard_map/ppermute | solution.py:104
  42.3 3.1 %collective-permute-done.11 = bf16[304,128]{1,0:T(8,128)(2,1)S(1)} collective-permute-done((bf16[304,128]{1,0:T(8,128)(2,1)S(1)}, bf16[304,128]{1,0:T(8,128)(2,1)S(1)}, u32[]{:S(2)}, u32[]{:S(2)}) %collective-permute-start.11) | collective-permute-done | bytes 77856 | tf_op jit(solution)/shard_map/ppermute | solution.py:104
  45.4 2.1 %collective-permute-start.12 = (bf16[304,128]{1,0:T(8,128)(2,1)S(1)}, bf16[304,128]{1,0:T(8,128)(2,1)S(1)}, u32[]{:S(2)}, u32[]{:S(2)}) collective-permute-start(bf16[304,128]{1,0:T(8,128)(2,1)S(1)} %get-tuple-element.15), channel_id=1, source_target_pairs={{0,12},{4,0},{8,4},{12,8},{1,13},{5,1},{9,5},{13,9},{2,14},{6,2},{... | collective-permute-start | bytes 233480 | tf_op jit(solution)/shard_map/ppermute | solution.py:76
  47.5 0.6 collective-permute-start.14
  48.5 0.9 %fusion.52 = (bf16[128,16,128]{0,2,1:T(8,128)(2,1)S(1)}, bf16[128,16,128]{0,2,1:T(8,128)(2,1)S(1)}, bf16[128,16,128]{0,2,1:T(8,128)(2,1)S(1)}, bf16[128,16,128]{...) fusion(bf16[128,18,130]{0,2,1:T(8,128)(2,1)S(1)} %maximum_selec, ...), kind=kLoop, calls=%fused_computation.200 | loop fusion | bytes 9437184 | tf_op jit(solution)/shard_map/slice | solution.py:37
  52.0 1.1 %fusion.2 = bf16[128,2048]{1,0:T(8,128)(2,1)} fusion(f32[128,2048]{1,0:T(8,128)S(1)} %convolution_add_fusion.9, bf16[128,2048]{0,1:T(8,128)(2,1)S(1)} %bitcast.345, bf16[3,3,128,128]{2,3,1,0:T(8,128)(2,1)S(1)} %get-tuple-element.70), kind=kOutput, calls=%fused_computation.38 | convolution fusion | flops 67633152 | bytes 2129920 | tf_op jit(solution)/shard_map/dot_general | solution.py:50
  53.2 0.9 %fusion.51 = (bf16[128,16,128]{0,2,1:T(8,128)(2,1)S(1)}, bf16[128,16,128]{0,2,1:T(8,128)(2,1)S(1)}, bf16[128,16,128]{0,2,1:T(8,128)(2,1)S(1)}, bf16[128,16,128]{...) fusion(bf16[128,18,130]{0,2,1:T(8,128)(2,1)S(1)} %maximum_selec, ...), kind=kLoop, calls=%fused_computation.199 | loop fusion | bytes 9437184 | tf_op jit(solution)/shard_map/slice | solution.py:37
  54.1 1.6 %collective-permute-start.16 = (bf16[128,2048]{1,0:T(8,128)(2,1)}, bf16[128,2048]{1,0:T(8,128)(2,1)}, u32[]{:S(2)}, u32[]{:S(2)}) collective-permute-start(bf16[128,2048]{1,0:T(8,128)(2,1)} %fusion.2), channel_id=1, source_target_pairs={{0,2},{2,0},{1,3},{3,1},{4,6},{6,4},{5,7},{7,5},{8,10},{10,8},{9,1... | collective-permute-start | bytes 1572872 | tf_op jit(solution)/shard_map/ppermute | solution.py:198
  58.9 1.1 %collective-permute-done.15 = f32[1216,128]{1,0:T(8,128)S(1)} collective-permute-done((f32[1216,128]{1,0:T(8,128)S(1)}, f32[1216,128]{1,0:T(8,128)S(1)}, u32[]{:S(2)}, u32[]{:S(2)}) %collective-permute-start.15) | collective-permute-done | bytes 622624 | tf_op jit(solution)/shard_map/ppermute | solution.py:76
  61.2 1.2 %fusion.6 = f32[3,3,128,256]{3,2,1,0:T(8,128)} fusion(s32[]{:T(128)S(6)} %select_n.114, f32[3,3,128,256]{3,2,1,0:T(8,128)S(1)} %reshape.240), kind=kLoop, calls=%fused_computation.63 | loop fusion | flops 294912 | bytes 2359300 | tf_op jit(solution)/shard_map/concatenate | solution.py:184
  62.4 5.4 %collective-permute-done.16 = bf16[128,2048]{1,0:T(8,128)(2,1)} collective-permute-done((bf16[128,2048]{1,0:T(8,128)(2,1)}, bf16[128,2048]{1,0:T(8,128)(2,1)}, u32[]{:S(2)}, u32[]{:S(2)}) %collective-permute-start.16) | collective-permute-done | bytes 524320 | tf_op jit(solution)/shard_map/ppermute | solution.py:198
  67.8 1.2 %fusion.21 = bf16[16,8,16,128]{3,1,2,0:T(8,128)(2,1)S(1)} fusion(f32[128,2048]{1,0:T(8,128)S(1)} %convolution_add_fusion, bf16[128,2048]{1,0:T(8,128)(2,1)} %collective-permute-done.16), kind=kLoop, calls=%fused_computation.96 | loop fusion | flops 786432 | bytes 2097152
  68.9 0.9 %copy.30 = bf16[16,8,16,128]{3,2,1,0:T(8,128)(2,1)} copy(bf16[16,8,16,128]{3,1,2,0:T(8,128)(2,1)S(1)} %fusion.21) | data formatting | bytes 1048576
  (115 shorter events, 19.7 us)
Async XLA Ops:
  0.6 8.4 %copy-start.1 = (bf16[128,16,128]{2,1,0:T(8,128)(2,1)S(1)}, bf16[128,16,128]{2,1,0:T(8,128)(2,1)}, u32[]{:S(2)}) copy-start(bf16[128,16,128]{2,1,0:T(8,128)(2,1)} %param.5) | copy-start | bytes 1572868
  2.2 16.6 %collective-permute-start.5 = (bf16[128,16,128]{0,2,1:T(8,128)(2,1)S(1)}, bf16[128,16,128]{0,2,1:T(8,128)(2,1)S(1)}, u32[]{:S(2)}, u32[]{:S(2)}) collective-permute-start(bf16[128,16,128]{0,2,1:T(8,128)(2,1)S(1)} %copy.12), channel_id=1, source_target_pairs={{0,2},{2,0},{1,3},{3,1},{4,6},{6,4},{5,7},{7,5},{8,10},{10,8},{9,1... | collective-permute-start | bytes 1572872 | tf_op jit(solution)/shard_map/ppermute | solution.py:142
  5.2 5.5 %collective-permute-start = (bf16[128,16,1]{0,2,1:T(2,128)(2,1)S(1)}, bf16[128,16,1]{0,2,1:T(2,128)(2,1)S(1)}, u32[]{:S(2)}, u32[]{:S(2)}) collective-permute-start(bf16[128,16,1]{0,2,1:T(2,128)(2,1)S(1)} %get-tuple-element.75), channel_id=1, source_target_pairs={{0,4},{4,8},{8,12},{12,0},{1,5},{5,9},{9,13},{13,1},{2,6},{6,10},{... | collective-permute-start | bytes 12296 | tf_op jit(solution)/shard_map/ppermute | solution.py:14
  6.8 3.9 %collective-permute-start.1 = (bf16[128,16,1]{0,2,1:T(2,128)(2,1)S(1)}, bf16[128,16,1]{0,2,1:T(2,128)(2,1)S(1)}, u32[]{:S(2)}, u32[]{:S(2)}) collective-permute-start(bf16[128,16,1]{0,2,1:T(2,128)(2,1)S(1)} %get-tuple-element.76), channel_id=1, source_target_pairs={{4,0},{8,4},{12,8},{0,12},{5,1},{9,5},{13,9},{1,13},{6,2},{10,6},{... | collective-permute-start | bytes 12296 | tf_op jit(solution)/shard_map/ppermute | solution.py:15
  10.7 1.3 %collective-permute-start.2 = (bf16[128,1,130]{0,2,1:T(8,128)(2,1)S(1)}, bf16[128,1,130]{0,2,1:T(8,128)(2,1)S(1)}, u32[]{:S(2)}, u32[]{:S(2)}) collective-permute-start(bf16[128,1,130]{0,2,1:T(8,128)(2,1)S(1)} %get-tuple-element.73), channel_id=1, source_target_pairs={{0,1},{1,0},{2,3},{3,2},{4,5},{5,4},{6,7},{7,6},{8,9},{9,8},{10,11... | collective-permute-start | bytes 99848 | tf_op jit(solution)/shard_map/ppermute | solution.py:14
  10.8 1.4 %collective-permute-start.3 = (bf16[128,1,130]{0,2,1:T(8,128)(2,1)S(1)}, bf16[128,1,130]{0,2,1:T(8,128)(2,1)S(1)}, u32[]{:S(2)}, u32[]{:S(2)}) collective-permute-start(bf16[128,1,130]{0,2,1:T(8,128)(2,1)S(1)} %get-tuple-element.74), channel_id=1, source_target_pairs={{1,0},{0,1},{3,2},{2,3},{5,4},{4,5},{7,6},{6,7},{9,8},{8,9},{11,10... | collective-permute-start | bytes 99848 | tf_op jit(solution)/shard_map/ppermute | solution.py:15
  12.5 1.5 %copy-start = (bf16[3,3,128,256]{3,2,1,0:T(8,128)(2,1)S(1)}, bf16[3,3,128,256]{3,2,1,0:T(8,128)(2,1)}, u32[]{:S(2)}) copy-start(bf16[3,3,128,256]{3,2,1,0:T(8,128)(2,1)} %param.6) | copy-start | bytes 1769476
  13.5 5.2 %collective-permute-start.4 = (bf16[128,292]{0,1:T(8,128)(2,1)S(1)}, bf16[128,292]{0,1:T(8,128)(2,1)S(1)}, u32[]{:S(2)}, u32[]{:S(2)}) collective-permute-start(bf16[128,292]{0,1:T(8,128)(2,1)S(1)} %pad_maximum_fusion.5), channel_id=1, source_target_pairs={{0,2},{2,0},{1,3},{3,1},{4,6},{6,4},{5,7},{7,5},{8,10},{10,8},{9,1... | collective-permute-start | bytes 224264 | tf_op jit(solution)/shard_map/ppermute | solution.py:148
  24.6 0.7 copy-start.2
  30.2 2.2 %collective-permute-start.6 = (f32[1216,128]{1,0:T(8,128)S(1)}, f32[1216,128]{1,0:T(8,128)}, u32[]{:S(2)}, u32[]{:S(2)}) collective-permute-start(f32[1216,128]{1,0:T(8,128)S(1)} %dynamic-slice_bitcast_fusion), channel_id=1, source_target_pairs={{0,1},{1,0},{2,3},{3,2},{4,5},{5,4},{6,7},{7,6},{8,9},{9,8},{10,11... | collective-permute-start | bytes 1867784 | tf_op jit(solution)/shard_map/ppermute | solution.py:64
  33.6 7.0 %collective-permute-start.7 = (bf16[320,128]{1,0:T(8,128)(2,1)S(1)}, bf16[320,128]{1,0:T(8,128)(2,1)S(1)}, u32[]{:S(2)}, u32[]{:S(2)}) collective-permute-start(bf16[320,128]{1,0:T(8,128)(2,1)S(1)} %pad_maximum_fusion.3), channel_id=1, source_target_pairs={{0,4},{4,8},{8,12},{12,0},{1,5},{5,9},{9,13},{13,1},{2,6},{6,10},{... | collective-permute-start | bytes 245768 | tf_op jit(solution)/shard_map/ppermute | solution.py:104
  35.5 6.0 %collective-permute-start.8 = (bf16[320,128]{1,0:T(8,128)(2,1)S(1)}, bf16[320,128]{1,0:T(8,128)(2,1)S(1)}, u32[]{:S(2)}, u32[]{:S(2)}) collective-permute-start(bf16[320,128]{1,0:T(8,128)(2,1)S(1)} %pad_maximum_fusion.4), channel_id=1, source_target_pairs={{0,12},{4,0},{8,4},{12,8},{1,13},{5,1},{9,5},{13,9},{2,14},{6,2},{... | collective-permute-start | bytes 245768 | tf_op jit(solution)/shard_map/ppermute | solution.py:104
  38.4 7.0 %collective-permute-start.11 = (bf16[304,128]{1,0:T(8,128)(2,1)S(1)}, bf16[304,128]{1,0:T(8,128)(2,1)S(1)}, u32[]{:S(2)}, u32[]{:S(2)}) collective-permute-start(bf16[304,128]{1,0:T(8,128)(2,1)S(1)} %get-tuple-element.66), channel_id=1, source_target_pairs={{0,8},{4,12},{8,0},{12,4},{1,9},{5,13},{9,1},{13,5},{2,10},{6,14},... | collective-permute-start | bytes 233480 | tf_op jit(solution)/shard_map/ppermute | solution.py:104
  41.7 6.5 %collective-permute-start.10 = (bf16[128,1,130]{0,2,1:T(8,128)(2,1)S(1)}, bf16[128,1,130]{0,2,1:T(8,128)(2,1)S(1)}, u32[]{:S(2)}, u32[]{:S(2)}) collective-permute-start(bf16[128,1,130]{0,2,1:T(8,128)(2,1)S(1)} %get-tuple-element.72), channel_id=1, source_target_pairs={{1,0},{0,1},{3,2},{2,3},{5,4},{4,5},{7,6},{6,7},{9,8},{8,9},{11,10... | collective-permute-start | bytes 99848 | tf_op jit(solution)/shard_map/ppermute | solution.py:15
  41.8 6.4 %collective-permute-start.9 = (bf16[128,1,130]{0,2,1:T(8,128)(2,1)S(1)}, bf16[128,1,130]{0,2,1:T(8,128)(2,1)S(1)}, u32[]{:S(2)}, u32[]{:S(2)}) collective-permute-start(bf16[128,1,130]{0,2,1:T(8,128)(2,1)S(1)} %get-tuple-element.71), channel_id=1, source_target_pairs={{0,1},{1,0},{2,3},{3,2},{4,5},{5,4},{6,7},{7,6},{8,9},{9,8},{10,11... | collective-permute-start | bytes 99848 | tf_op jit(solution)/shard_map/ppermute | solution.py:14
  45.4 12.2 %collective-permute-start.12 = (bf16[304,128]{1,0:T(8,128)(2,1)S(1)}, bf16[304,128]{1,0:T(8,128)(2,1)S(1)}, u32[]{:S(2)}, u32[]{:S(2)}) collective-permute-start(bf16[304,128]{1,0:T(8,128)(2,1)S(1)} %get-tuple-element.15), channel_id=1, source_target_pairs={{0,12},{4,0},{8,4},{12,8},{1,13},{5,1},{9,5},{13,9},{2,14},{6,2},{... | collective-permute-start | bytes 233480 | tf_op jit(solution)/shard_map/ppermute | solution.py:76
  47.5 10.1 %collective-permute-start.13 = (bf16[304,128]{1,0:T(8,128)(2,1)S(1)}, bf16[304,128]{1,0:T(8,128)(2,1)S(1)}, u32[]{:S(2)}, u32[]{:S(2)}) collective-permute-start(bf16[304,128]{1,0:T(8,128)(2,1)S(1)} %get-tuple-element.15), channel_id=1, source_target_pairs={{0,8},{4,12},{8,0},{12,4},{1,9},{5,13},{9,1},{13,5},{2,10},{6,14},... | collective-permute-start | bytes 233480 | tf_op jit(solution)/shard_map/ppermute | solution.py:76
  47.5 10.2 %collective-permute-start.14 = (bf16[304,128]{1,0:T(8,128)(2,1)S(1)}, bf16[304,128]{1,0:T(8,128)(2,1)S(1)}, u32[]{:S(2)}, u32[]{:S(2)}) collective-permute-start(bf16[304,128]{1,0:T(8,128)(2,1)S(1)} %get-tuple-element.15), channel_id=1, source_target_pairs={{0,4},{4,8},{8,12},{12,0},{1,5},{5,9},{9,13},{13,1},{2,6},{6,10},{... | collective-permute-start | bytes 233480 | tf_op jit(solution)/shard_map/ppermute | solution.py:76
  54.1 13.7 %collective-permute-start.16 = (bf16[128,2048]{1,0:T(8,128)(2,1)}, bf16[128,2048]{1,0:T(8,128)(2,1)}, u32[]{:S(2)}, u32[]{:S(2)}) collective-permute-start(bf16[128,2048]{1,0:T(8,128)(2,1)} %fusion.2), channel_id=1, source_target_pairs={{0,2},{2,0},{1,3},{3,1},{4,6},{6,4},{5,7},{7,5},{8,10},{10,8},{9,1... | collective-permute-start | bytes 1572872 | tf_op jit(solution)/shard_map/ppermute | solution.py:198
  57.9 2.1 %collective-permute-start.15 = (f32[1216,128]{1,0:T(8,128)S(1)}, f32[1216,128]{1,0:T(8,128)S(1)}, u32[]{:S(2)}, u32[]{:S(2)}) collective-permute-start(f32[1216,128]{1,0:T(8,128)S(1)} %bitcast.321), channel_id=1, source_target_pairs={{0,1},{1,0},{2,3},{3,2},{4,5},{5,4},{6,7},{7,6},{8,9},{9,8},{10,11... | collective-permute-start | bytes 1867784 | tf_op jit(solution)/shard_map/ppermute | solution.py:76

commit v20 on v19

--- a/solution.py
+++ b/solution.py
@@ -178,6 +178,13 @@
     grad_field = grad_pre.reshape(own_channels, row_count, column_count)
     edges = (grad_field[:, :, column_count - 1 :], grad_field[:, :, :1])
     scattered, (before, after) = sum_start(flat, jnp.bfloat16, edges)
+    grad_wide = jnp.concatenate([before, grad_field, after], axis=2)
+    grad_pad = mask_rims(padded_2(grad_wide, (("lat", 1),), 1))
+    outgoing = []
+    for shift in range(1, chan_count):
+        kernel_t = jnp.swapaxes(kernel_cols[shift], 2, 3)
+        outgoing.append(conv_taps(kernel_t, grad_pad, row_count, column_count, True).astype(jnp.bfloat16))
+    grad_pad, outgoing, scattered = lax.optimization_barrier((grad_pad, outgoing, scattered))
     flat = sum_finish(scattered, flat.size, jnp.bfloat16)
     weight_local = flat[: weight_part.size].reshape(weight_part.shape)
     bias_grad = flat[weight_part.size :]
@@ -185,13 +192,6 @@
     weight_grad = lax.dynamic_slice_in_dim(
         doubled, (chan_count - chan_index) % chan_count * own_channels, chan_count * own_channels, axis=3
     )
-    grad_wide = jnp.concatenate([before, grad_field, after], axis=2)
-    grad_pad = mask_rims(padded_2(grad_wide, (("lat", 1),), 1))
-    outgoing = []
-    for shift in range(1, chan_count):
-        kernel_t = jnp.swapaxes(kernel_cols[shift], 2, 3)
-        outgoing.append(conv_taps(kernel_t, grad_pad, row_count, column_count, True).astype(jnp.bfloat16))
-    grad_pad, outgoing = lax.optimization_barrier((grad_pad, outgoing))
     received = []
     for shift in range(1, chan_count):
         pairs = [(i, (i + shift) % chan_count) for i in range(chan_count)]

time: 70.1 us -> 70.1 us (level)
    ppermute x1, waiting for transfers between devices: 5.4 us -> 2.9 us  [local(): received.append(lax.ppermute(outgoing[shift - 1], 'chan', pairs))]
    ppermute x4, waiting for transfers between devices: 1.07 us -> 3.57 us  [direct_all_gather(): pieces.append(lax.ppermute(sent, axis, pairs).astype(jnp.float32))]
  transfers between devices with their start and end apart: 17 -> 17, of which waited for: 10 -> 11; matrix products, arithmetic and copies ran while one was open for 25% -> 18% of each run, Pallas kernels for 0% -> 0%
where the time goes in v20:
time: 70.1 us; the launch traced here: 69.9 us
  starting transfers between devices  17.9 us (26%)
  waiting for transfers between devices  17 us (24%)
  matrix products  15.6 us (22%)
  local copies, waits for them, and re-layouts  10.3 us (15%)
  other arithmetic  7.67 us (11%)
  between operations  1.47 us (2%)
    dot_general x36, matrix products, conv_taps(): jnp.dot(kernel[tap_row, tap_col], window, preferred_element_type=jnp.floa...  12.7 us
    ppermute x3, waiting for transfers between devices, sum_start(): moved = lax.ppermute(piece, 'lon', pairs)  5.21 us
    ppermute x3, starting transfers between devices, sum_start(): moved = lax.ppermute(piece, 'lon', pairs)  4.99 us
    slice x4, local copies, waits for them, and re-layouts, window_of(): field[:, first_row:first_row + row_count, first_col:first_col + column_co...  3.72 us
    ppermute x4, waiting for transfers between devices, direct_all_gather(): pieces.append(lax.ppermute(sent, axis, pairs).astype(jnp.float32))  3.57 us
    unnamed x12, local copies, waits for them, and re-layouts  3.51 us
    ppermute x1, starting transfers between devices, local(): raw_blocks.append(lax.ppermute(inputs, 'chan', pairs))  3 us
    ppermute x1, waiting for transfers between devices, local(): received.append(lax.ppermute(outgoing[shift - 1], 'chan', pairs))  2.9 us
  transfers between devices with their start and end apart: 17, of which 11 were waited for; matrix products, arithmetic and copies ran while one was open for 18% of the time, Pallas kernels for 0%

profile of v20, /device:TPU:0, one launch (start us, length us, event | category | flops | bytes accessed | tf_op | source)
XLA Modules:
  0.0 69.9 jit_solution(5600553176500504199)
XLA Ops:
  0.6 1.5 %copy.12 = bf16[128,16,128]{0,2,1:T(8,128)(2,1)S(1)} copy(bf16[128,16,128]{2,1,0:T(8,128)(2,1)} %param.4) | data formatting | bytes 1048576 | tf_op args[0]
  2.2 3.0 %collective-permute-start.5 = (bf16[128,16,128]{0,2,1:T(8,128)(2,1)S(1)}, bf16[128,16,128]{0,2,1:T(8,128)(2,1)S(1)}, u32[]{:S(2)}, u32[]{:S(2)}) collective-permute-start(bf16[128,16,128]{0,2,1:T(8,128)(2,1)S(1)} %copy.12), channel_id=1, source_target_pairs={{0,2},{2,0},{1,3},{3,1},{4,6},{6,4},{5,7},{7,5},{8,10},{10,8},{9,1... | collective-permute-start | bytes 1572872 | tf_op jit(solution)/shard_map/ppermute | solution.py:142
  5.2 1.6 %collective-permute-start = (bf16[128,16,1]{0,2,1:T(2,128)(2,1)S(1)}, bf16[128,16,1]{0,2,1:T(2,128)(2,1)S(1)}, u32[]{:S(2)}, u32[]{:S(2)}) collective-permute-start(bf16[128,16,1]{0,2,1:T(2,128)(2,1)S(1)} %get-tuple-element.75), channel_id=1, source_target_pairs={{0,4},{4,8},{8,12},{12,0},{1,5},{5,9},{9,13},{13,1},{2,6},{6,10},{... | collective-permute-start | bytes 12296 | tf_op jit(solution)/shard_map/ppermute | solution.py:14
  6.8 2.2 %collective-permute-start.1 = (bf16[128,16,1]{0,2,1:T(2,128)(2,1)S(1)}, bf16[128,16,1]{0,2,1:T(2,128)(2,1)S(1)}, u32[]{:S(2)}, u32[]{:S(2)}) collective-permute-start(bf16[128,16,1]{0,2,1:T(2,128)(2,1)S(1)} %get-tuple-element.76), channel_id=1, source_target_pairs={{4,0},{8,4},{12,8},{0,12},{5,1},{9,5},{13,9},{1,13},{6,2},{10,6},{... | collective-permute-start | bytes 12296 | tf_op jit(solution)/shard_map/ppermute | solution.py:15
  9.2 1.5 %collective-permute-done = bf16[128,16,1]{0,2,1:T(2,128)(2,1)S(1)} collective-permute-done((bf16[128,16,1]{0,2,1:T(2,128)(2,1)S(1)}, bf16[128,16,1]{0,2,1:T(2,128)(2,1)S(1)}, u32[]{:S(2)}, u32[]{:S(2)}) %collective-permute-start) | collective-permute-done | bytes 4128 | tf_op jit(solution)/shard_map/ppermute | solution.py:14
  11.3 0.7 collective-permute-done.2
  12.5 0.9 %fusion.53 = (bf16[128,16,128]{0,2,1:T(8,128)(2,1)S(1)}, bf16[128,16,128]{0,2,1:T(8,128)(2,1)S(1)}, bf16[128,16,128]{0,2,1:T(8,128)(2,1)S(1)}, bf16[128,16,128]{...) fusion(bf16[128,18,130]{0,2,1:T(8,128)(2,1)S(1)} %maximum_selec, ...), kind=kLoop, calls=%fused_computation.202 | loop fusion | bytes 9437184 | tf_op jit(solution)/shard_map/slice | solution.py:37
  16.7 2.0 %collective-permute-done.4 = bf16[128,292]{0,1:T(8,128)(2,1)S(1)} collective-permute-done((bf16[128,292]{0,1:T(8,128)(2,1)S(1)}, bf16[128,292]{0,1:T(8,128)(2,1)S(1)}, u32[]{:S(2)}, u32[]{:S(2)}) %collective-permute-start.4) | collective-permute-done | bytes 74784 | tf_op jit(solution)/shard_map/ppermute | solution.py:148
  19.0 1.0 %fusion.51 = (bf16[128,16,128]{0,2,1:T(8,128)(2,1)S(1)}, bf16[128,16,128]{0,2,1:T(8,128)(2,1)S(1)}, bf16[128,16,128]{0,2,1:T(8,128)(2,1)S(1)}, bf16[128,16,128]{...) fusion(bf16[128,18,130]{0,2,1:T(8,128)(2,1)S(1)} %pad_maximum_f, ...), kind=kLoop, calls=%fused_computation.200 | loop fusion | bytes 9437184 | tf_op jit(solution)/shard_map/slice | solution.py:37
  19.9 2.5 %fusion.14 = (bf16[256,16,128]{0,2,1:T(8,128)(2,1)S(1)}, bf16[256,16,128]{0,2,1:T(8,128)(2,1)S(1)}, bf16[256,16,128]{0,2,1:T(8,128)(2,1)S(1)}, bf16[256,16,128]{...) fusion(bf16[128,18,130]{0,2,1:T(8,128)(2,1)S(1)} %maximum_selec, ...), kind=kLoop, calls=%fused_computation.81 | loop fusion | flops 18874368 | bytes 10635264 | tf_op jit(solution)/shard_map/concatenate | solution.py:164
  25.3 1.0 %convert_reduce_fusion = (f32[128]{0:T(128)S(1)}, bf16[128,2048]{1,0:T(8,128)(2,1)S(1)}) fusion(f32[128]{0:T(128)S(1)} %copy-done.2, f32[128,2048]{1,0:T(8,128)S(1)} %convolution_add_fusion.24, f32[128,2048]{1,0:T(8,128)S(1)} %convolution_add_fusion.17, bf16[128,2048]{0,1:T(8,128)(2,1)S(1)} %bitcast.357, bf16[3,3,128,256]{3,2,1,0:T(8,128)(2,1)S(1)} %copy-done, ...), kind=kOutput, calls=%fused_computation.90 | convolution fusion | flops 71040896 | bytes 4228104 | tf_op jit(solution)/shard_map/dot_general | solution.py:50
  30.5 0.8 %slice_reduce_fusion.1 = (bf16[128,16]{1,0:T(8,128)(2,1)S(1)}, bf16[128,16]{1,0:T(8,128)(2,1)S(1)}) fusion(bf16[128,16,128]{2,1,0:T(8,128)(2,1)S(1)} %bitcast.303), kind=kLoop, calls=%fused_computation.98 | loop fusion | bytes 16384 | tf_op jit(solution)/shard_map/slice | solution.py:179
  31.5 0.9 %collective-permute-done.6 = f32[1216,128]{1,0:T(8,128)} collective-permute-done((f32[1216,128]{1,0:T(8,128)S(1)}, f32[1216,128]{1,0:T(8,128)}, u32[]{:S(2)}, u32[]{:S(2)}) %collective-permute-start.6) | collective-permute-done | bytes 622624 | tf_op jit(solution)/shard_map/ppermute | solution.py:64
  32.4 1.1 %bitcast_add_fusion = f32[1216,128]{1,0:T(8,128)S(1)} fusion(f32[1216,128]{1,0:T(8,128)} %collective-permute-done.6, f32[2,1216,128]{2,1,0:T(8,128)S(1)} %bitcast.306, s32[]{:T(128)S(6)} %select_n.98), kind=kLoop, calls=%fused_computation.94 | loop fusion | flops 155648 | bytes 1867780 | tf_op jit(solution)/shard_map/add | solution.py:64
  33.6 1.9 %collective-permute-start.7 = (bf16[320,128]{1,0:T(8,128)(2,1)S(1)}, bf16[320,128]{1,0:T(8,128)(2,1)S(1)}, u32[]{:S(2)}, u32[]{:S(2)}) collective-permute-start(bf16[320,128]{1,0:T(8,128)(2,1)S(1)} %pad_maximum_fusion.3), channel_id=1, source_target_pairs={{0,4},{4,8},{8,12},{12,0},{1,5},{5,9},{9,13},{13,1},{2,6},{6,10},{... | collective-permute-start | bytes 245768 | tf_op jit(solution)/shard_map/ppermute | solution.py:104
  35.5 2.3 %collective-permute-start.8 = (bf16[320,128]{1,0:T(8,128)(2,1)S(1)}, bf16[320,128]{1,0:T(8,128)(2,1)S(1)}, u32[]{:S(2)}, u32[]{:S(2)}) collective-permute-start(bf16[320,128]{1,0:T(8,128)(2,1)S(1)} %pad_maximum_fusion.4), channel_id=1, source_target_pairs={{0,12},{4,0},{8,4},{12,8},{1,13},{5,1},{9,5},{13,9},{2,14},{6,2},{... | collective-permute-start | bytes 245768 | tf_op jit(solution)/shard_map/ppermute | solution.py:104
  38.4 0.8 %collective-permute-start.11 = (bf16[304,128]{1,0:T(8,128)(2,1)S(1)}, bf16[304,128]{1,0:T(8,128)(2,1)S(1)}, u32[]{:S(2)}, u32[]{:S(2)}) collective-permute-start(bf16[304,128]{1,0:T(8,128)(2,1)S(1)} %get-tuple-element.66), channel_id=1, source_target_pairs={{0,8},{4,12},{8,0},{12,4},{1,9},{5,13},{9,1},{13,5},{2,10},{6,14},... | collective-permute-start | bytes 233480 | tf_op jit(solution)/shard_map/ppermute | solution.py:104
  39.2 1.4 %collective-permute-done.7 = bf16[320,128]{1,0:T(8,128)(2,1)S(1)} collective-permute-done((bf16[320,128]{1,0:T(8,128)(2,1)S(1)}, bf16[320,128]{1,0:T(8,128)(2,1)S(1)}, u32[]{:S(2)}, u32[]{:S(2)}) %collective-permute-start.7) | collective-permute-done | bytes 81952 | tf_op jit(solution)/shard_map/ppermute | solution.py:104
  40.7 0.7 %collective-permute-done.8 = bf16[320,128]{1,0:T(8,128)(2,1)S(1)} collective-permute-done((bf16[320,128]{1,0:T(8,128)(2,1)S(1)}, bf16[320,128]{1,0:T(8,128)(2,1)S(1)}, u32[]{:S(2)}, u32[]{:S(2)}) %collective-permute-start.8) | collective-permute-done | bytes 81952 | tf_op jit(solution)/shard_map/ppermute | solution.py:104
  42.3 3.1 %collective-permute-done.11 = bf16[304,128]{1,0:T(8,128)(2,1)S(1)} collective-permute-done((bf16[304,128]{1,0:T(8,128)(2,1)S(1)}, bf16[304,128]{1,0:T(8,128)(2,1)S(1)}, u32[]{:S(2)}, u32[]{:S(2)}) %collective-permute-start.11) | collective-permute-done | bytes 77856 | tf_op jit(solution)/shard_map/ppermute | solution.py:104
  45.8 0.9 %fusion.50 = (bf16[128,16,128]{0,2,1:T(8,128)(2,1)S(1)}, bf16[128,16,128]{0,2,1:T(8,128)(2,1)S(1)}, bf16[128,16,128]{0,2,1:T(8,128)(2,1)S(1)}, bf16[128,16,128]{...) fusion(bf16[128,18,130]{0,2,1:T(8,128)(2,1)S(1)} %maximum_selec, ...), kind=kLoop, calls=%fused_computation.199 | loop fusion | bytes 9437184 | tf_op jit(solution)/shard_map/slice | solution.py:37
  49.3 1.1 %fusion.2 = bf16[128,2048]{1,0:T(8,128)(2,1)} fusion(f32[128,2048]{1,0:T(8,128)S(1)} %convolution_add_fusion.9, bf16[128,2048]{0,1:T(8,128)(2,1)S(1)} %bitcast.344, bf16[3,3,128,128]{2,3,1,0:T(8,128)(2,1)S(1)} %get-tuple-element.70), kind=kOutput, calls=%fused_computation.38 | convolution fusion | flops 67633152 | bytes 2129920 | tf_op jit(solution)/shard_map/dot_general | solution.py:50
  50.5 2.1 %collective-permute-start.12 = (bf16[304,128]{1,0:T(8,128)(2,1)S(1)}, bf16[304,128]{1,0:T(8,128)(2,1)S(1)}, u32[]{:S(2)}, u32[]{:S(2)}) collective-permute-start(bf16[304,128]{1,0:T(8,128)(2,1)S(1)} %convert_element_type.70), channel_id=1, source_target_pairs={{0,12},{4,0},{8,4},{12,8},{1,13},{5,1},{9,5},{13,9},{2,14},{6,2},{... | collective-permute-start | bytes 233480 | tf_op jit(solution)/shard_map/ppermute | solution.py:76
  52.6 0.6 collective-permute-start.14
  53.2 0.9 %fusion.49 = (bf16[128,16,128]{0,2,1:T(8,128)(2,1)S(1)}, bf16[128,16,128]{0,2,1:T(8,128)(2,1)S(1)}, bf16[128,16,128]{0,2,1:T(8,128)(2,1)S(1)}, bf16[128,16,128]{...) fusion(bf16[128,18,130]{0,2,1:T(8,128)(2,1)S(1)} %maximum_selec, ...), kind=kLoop, calls=%fused_computation.198 | loop fusion | bytes 9437184 | tf_op jit(solution)/shard_map/slice | solution.py:37
  54.1 1.6 %collective-permute-start.16 = (bf16[128,2048]{1,0:T(8,128)(2,1)}, bf16[128,2048]{1,0:T(8,128)(2,1)}, u32[]{:S(2)}, u32[]{:S(2)}) collective-permute-start(bf16[128,2048]{1,0:T(8,128)(2,1)} %fusion.2), channel_id=1, source_target_pairs={{0,2},{2,0},{1,3},{3,1},{4,6},{6,4},{5,7},{7,5},{8,10},{10,8},{9,1... | collective-permute-start | bytes 1572872 | tf_op jit(solution)/shard_map/ppermute | solution.py:198
  57.7 2.5 %collective-permute-done.13 = bf16[304,128]{1,0:T(8,128)(2,1)S(1)} collective-permute-done((bf16[304,128]{1,0:T(8,128)(2,1)S(1)}, bf16[304,128]{1,0:T(8,128)(2,1)S(1)}, u32[]{:S(2)}, u32[]{:S(2)}) %collective-permute-start.13) | collective-permute-done | bytes 77856 | tf_op jit(solution)/shard_map/ppermute | solution.py:76
  61.5 1.1 %collective-permute-done.15 = f32[1216,128]{1,0:T(8,128)S(1)} collective-permute-done((f32[1216,128]{1,0:T(8,128)S(1)}, f32[1216,128]{1,0:T(8,128)S(1)}, u32[]{:S(2)}, u32[]{:S(2)}) %collective-permute-start.15) | collective-permute-done | bytes 622624 | tf_op jit(solution)/shard_map/ppermute | solution.py:76
  63.7 1.2 %fusion.6 = f32[3,3,128,256]{3,2,1,0:T(8,128)} fusion(s32[]{:T(128)S(6)} %select_n.114, f32[3,3,128,256]{3,2,1,0:T(8,128)S(1)} %reshape.240), kind=kLoop, calls=%fused_computation.63 | loop fusion | flops 294912 | bytes 2359300 | tf_op jit(solution)/shard_map/concatenate | solution.py:191
  64.9 2.9 %collective-permute-done.16 = bf16[128,2048]{1,0:T(8,128)(2,1)} collective-permute-done((bf16[128,2048]{1,0:T(8,128)(2,1)}, bf16[128,2048]{1,0:T(8,128)(2,1)}, u32[]{:S(2)}, u32[]{:S(2)}) %collective-permute-start.16) | collective-permute-done | bytes 524320 | tf_op jit(solution)/shard_map/ppermute | solution.py:198
  67.8 1.2 %fusion.21 = bf16[16,8,16,128]{3,1,2,0:T(8,128)(2,1)S(1)} fusion(f32[128,2048]{1,0:T(8,128)S(1)} %convolution_add_fusion, bf16[128,2048]{1,0:T(8,128)(2,1)} %collective-permute-done.16), kind=kLoop, calls=%fused_computation.96 | loop fusion | flops 786432 | bytes 2097152
  69.0 0.9 %copy.30 = bf16[16,8,16,128]{3,2,1,0:T(8,128)(2,1)} copy(bf16[16,8,16,128]{3,1,2,0:T(8,128)(2,1)S(1)} %fusion.21) | data formatting | bytes 1048576
  (116 shorter events, 20.3 us)
Async XLA Ops:
  0.6 8.4 %copy-start.1 = (bf16[128,16,128]{2,1,0:T(8,128)(2,1)S(1)}, bf16[128,16,128]{2,1,0:T(8,128)(2,1)}, u32[]{:S(2)}) copy-start(bf16[128,16,128]{2,1,0:T(8,128)(2,1)} %param.5) | copy-start | bytes 1572868
  2.2 16.6 %collective-permute-start.5 = (bf16[128,16,128]{0,2,1:T(8,128)(2,1)S(1)}, bf16[128,16,128]{0,2,1:T(8,128)(2,1)S(1)}, u32[]{:S(2)}, u32[]{:S(2)}) collective-permute-start(bf16[128,16,128]{0,2,1:T(8,128)(2,1)S(1)} %copy.12), channel_id=1, source_target_pairs={{0,2},{2,0},{1,3},{3,1},{4,6},{6,4},{5,7},{7,5},{8,10},{10,8},{9,1... | collective-permute-start | bytes 1572872 | tf_op jit(solution)/shard_map/ppermute | solution.py:142
  5.2 5.5 %collective-permute-start = (bf16[128,16,1]{0,2,1:T(2,128)(2,1)S(1)}, bf16[128,16,1]{0,2,1:T(2,128)(2,1)S(1)}, u32[]{:S(2)}, u32[]{:S(2)}) collective-permute-start(bf16[128,16,1]{0,2,1:T(2,128)(2,1)S(1)} %get-tuple-element.75), channel_id=1, source_target_pairs={{0,4},{4,8},{8,12},{12,0},{1,5},{5,9},{9,13},{13,1},{2,6},{6,10},{... | collective-permute-start | bytes 12296 | tf_op jit(solution)/shard_map/ppermute | solution.py:14
  6.8 3.9 %collective-permute-start.1 = (bf16[128,16,1]{0,2,1:T(2,128)(2,1)S(1)}, bf16[128,16,1]{0,2,1:T(2,128)(2,1)S(1)}, u32[]{:S(2)}, u32[]{:S(2)}) collective-permute-start(bf16[128,16,1]{0,2,1:T(2,128)(2,1)S(1)} %get-tuple-element.76), channel_id=1, source_target_pairs={{4,0},{8,4},{12,8},{0,12},{5,1},{9,5},{13,9},{1,13},{6,2},{10,6},{... | collective-permute-start | bytes 12296 | tf_op jit(solution)/shard_map/ppermute | solution.py:15
  10.7 1.3 %collective-permute-start.2 = (bf16[128,1,130]{0,2,1:T(8,128)(2,1)S(1)}, bf16[128,1,130]{0,2,1:T(8,128)(2,1)S(1)}, u32[]{:S(2)}, u32[]{:S(2)}) collective-permute-start(bf16[128,1,130]{0,2,1:T(8,128)(2,1)S(1)} %get-tuple-element.73), channel_id=1, source_target_pairs={{0,1},{1,0},{2,3},{3,2},{4,5},{5,4},{6,7},{7,6},{8,9},{9,8},{10,11... | collective-permute-start | bytes 99848 | tf_op jit(solution)/shard_map/ppermute | solution.py:14
  10.8 1.4 %collective-permute-start.3 = (bf16[128,1,130]{0,2,1:T(8,128)(2,1)S(1)}, bf16[128,1,130]{0,2,1:T(8,128)(2,1)S(1)}, u32[]{:S(2)}, u32[]{:S(2)}) collective-permute-start(bf16[128,1,130]{0,2,1:T(8,128)(2,1)S(1)} %get-tuple-element.74), channel_id=1, source_target_pairs={{1,0},{0,1},{3,2},{2,3},{5,4},{4,5},{7,6},{6,7},{9,8},{8,9},{11,10... | collective-permute-start | bytes 99848 | tf_op jit(solution)/shard_map/ppermute | solution.py:15
  12.5 1.5 %copy-start = (bf16[3,3,128,256]{3,2,1,0:T(8,128)(2,1)S(1)}, bf16[3,3,128,256]{3,2,1,0:T(8,128)(2,1)}, u32[]{:S(2)}) copy-start(bf16[3,3,128,256]{3,2,1,0:T(8,128)(2,1)} %param.6) | copy-start | bytes 1769476
  13.5 5.2 %collective-permute-start.4 = (bf16[128,292]{0,1:T(8,128)(2,1)S(1)}, bf16[128,292]{0,1:T(8,128)(2,1)S(1)}, u32[]{:S(2)}, u32[]{:S(2)}) collective-permute-start(bf16[128,292]{0,1:T(8,128)(2,1)S(1)} %pad_maximum_fusion.5), channel_id=1, source_target_pairs={{0,2},{2,0},{1,3},{3,1},{4,6},{6,4},{5,7},{7,5},{8,10},{10,8},{9,1... | collective-permute-start | bytes 224264 | tf_op jit(solution)/shard_map/ppermute | solution.py:148
  24.6 0.7 copy-start.2
  30.2 2.2 %collective-permute-start.6 = (f32[1216,128]{1,0:T(8,128)S(1)}, f32[1216,128]{1,0:T(8,128)}, u32[]{:S(2)}, u32[]{:S(2)}) collective-permute-start(f32[1216,128]{1,0:T(8,128)S(1)} %dynamic-slice_bitcast_fusion), channel_id=1, source_target_pairs={{0,1},{1,0},{2,3},{3,2},{4,5},{5,4},{6,7},{7,6},{8,9},{9,8},{10,11... | collective-permute-start | bytes 1867784 | tf_op jit(solution)/shard_map/ppermute | solution.py:64
  33.6 7.0 %collective-permute-start.7 = (bf16[320,128]{1,0:T(8,128)(2,1)S(1)}, bf16[320,128]{1,0:T(8,128)(2,1)S(1)}, u32[]{:S(2)}, u32[]{:S(2)}) collective-permute-start(bf16[320,128]{1,0:T(8,128)(2,1)S(1)} %pad_maximum_fusion.3), channel_id=1, source_target_pairs={{0,4},{4,8},{8,12},{12,0},{1,5},{5,9},{9,13},{13,1},{2,6},{6,10},{... | collective-permute-start | bytes 245768 | tf_op jit(solution)/shard_map/ppermute | solution.py:104
  35.5 6.0 %collective-permute-start.8 = (bf16[320,128]{1,0:T(8,128)(2,1)S(1)}, bf16[320,128]{1,0:T(8,128)(2,1)S(1)}, u32[]{:S(2)}, u32[]{:S(2)}) collective-permute-start(bf16[320,128]{1,0:T(8,128)(2,1)S(1)} %pad_maximum_fusion.4), channel_id=1, source_target_pairs={{0,12},{4,0},{8,4},{12,8},{1,13},{5,1},{9,5},{13,9},{2,14},{6,2},{... | collective-permute-start | bytes 245768 | tf_op jit(solution)/shard_map/ppermute | solution.py:104
  38.4 7.0 %collective-permute-start.11 = (bf16[304,128]{1,0:T(8,128)(2,1)S(1)}, bf16[304,128]{1,0:T(8,128)(2,1)S(1)}, u32[]{:S(2)}, u32[]{:S(2)}) collective-permute-start(bf16[304,128]{1,0:T(8,128)(2,1)S(1)} %get-tuple-element.66), channel_id=1, source_target_pairs={{0,8},{4,12},{8,0},{12,4},{1,9},{5,13},{9,1},{13,5},{2,10},{6,14},... | collective-permute-start | bytes 233480 | tf_op jit(solution)/shard_map/ppermute | solution.py:104
  41.7 3.7 %collective-permute-start.10 = (bf16[128,1,130]{0,2,1:T(8,128)(2,1)S(1)}, bf16[128,1,130]{0,2,1:T(8,128)(2,1)S(1)}, u32[]{:S(2)}, u32[]{:S(2)}) collective-permute-start(bf16[128,1,130]{0,2,1:T(8,128)(2,1)S(1)} %get-tuple-element.72), channel_id=1, source_target_pairs={{1,0},{0,1},{3,2},{2,3},{5,4},{4,5},{7,6},{6,7},{9,8},{8,9},{11,10... | collective-permute-start | bytes 99848 | tf_op jit(solution)/shard_map/ppermute | solution.py:15
  41.8 3.6 %collective-permute-start.9 = (bf16[128,1,130]{0,2,1:T(8,128)(2,1)S(1)}, bf16[128,1,130]{0,2,1:T(8,128)(2,1)S(1)}, u32[]{:S(2)}, u32[]{:S(2)}) collective-permute-start(bf16[128,1,130]{0,2,1:T(8,128)(2,1)S(1)} %get-tuple-element.71), channel_id=1, source_target_pairs={{0,1},{1,0},{2,3},{3,2},{4,5},{5,4},{6,7},{7,6},{8,9},{9,8},{10,11... | collective-permute-start | bytes 99848 | tf_op jit(solution)/shard_map/ppermute | solution.py:14
  50.5 7.2 %collective-permute-start.12 = (bf16[304,128]{1,0:T(8,128)(2,1)S(1)}, bf16[304,128]{1,0:T(8,128)(2,1)S(1)}, u32[]{:S(2)}, u32[]{:S(2)}) collective-permute-start(bf16[304,128]{1,0:T(8,128)(2,1)S(1)} %convert_element_type.70), channel_id=1, source_target_pairs={{0,12},{4,0},{8,4},{12,8},{1,13},{5,1},{9,5},{13,9},{2,14},{6,2},{... | collective-permute-start | bytes 233480 | tf_op jit(solution)/shard_map/ppermute | solution.py:76
  52.6 7.6 %collective-permute-start.13 = (bf16[304,128]{1,0:T(8,128)(2,1)S(1)}, bf16[304,128]{1,0:T(8,128)(2,1)S(1)}, u32[]{:S(2)}, u32[]{:S(2)}) collective-permute-start(bf16[304,128]{1,0:T(8,128)(2,1)S(1)} %convert_element_type.70), channel_id=1, source_target_pairs={{0,8},{4,12},{8,0},{12,4},{1,9},{5,13},{9,1},{13,5},{2,10},{6,14},... | collective-permute-start | bytes 233480 | tf_op jit(solution)/shard_map/ppermute | solution.py:76
  52.6 7.7 %collective-permute-start.14 = (bf16[304,128]{1,0:T(8,128)(2,1)S(1)}, bf16[304,128]{1,0:T(8,128)(2,1)S(1)}, u32[]{:S(2)}, u32[]{:S(2)}) collective-permute-start(bf16[304,128]{1,0:T(8,128)(2,1)S(1)} %convert_element_type.70), channel_id=1, source_target_pairs={{0,4},{4,8},{8,12},{12,0},{1,5},{5,9},{9,13},{13,1},{2,6},{6,10},{... | collective-permute-start | bytes 233480 | tf_op jit(solution)/shard_map/ppermute | solution.py:76
  54.1 13.7 %collective-permute-start.16 = (bf16[128,2048]{1,0:T(8,128)(2,1)}, bf16[128,2048]{1,0:T(8,128)(2,1)}, u32[]{:S(2)}, u32[]{:S(2)}) collective-permute-start(bf16[128,2048]{1,0:T(8,128)(2,1)} %fusion.2), channel_id=1, source_target_pairs={{0,2},{2,0},{1,3},{3,1},{4,6},{6,4},{5,7},{7,5},{8,10},{10,8},{9,1... | collective-permute-start | bytes 1572872 | tf_op jit(solution)/shard_map/ppermute | solution.py:198
  60.4 2.1 %collective-permute-start.15 = (f32[1216,128]{1,0:T(8,128)S(1)}, f32[1216,128]{1,0:T(8,128)S(1)}, u32[]{:S(2)}, u32[]{:S(2)}) collective-permute-start(f32[1216,128]{1,0:T(8,128)S(1)} %bitcast.320), channel_id=1, source_target_pairs={{0,1},{1,0},{2,3},{3,2},{4,5},{5,4},{6,7},{7,6},{8,9},{9,8},{10,11... | collective-permute-start | bytes 1867784 | tf_op jit(solution)/shard_map/ppermute | solution.py:76

commit v21 on v19

--- a/solution.py
+++ b/solution.py
@@ -139,7 +139,8 @@
     raw_blocks = []
     for shift in range(1, chan_count):
         pairs = [(i, (i - shift) % chan_count) for i in range(chan_count)]
-        raw_blocks.append(lax.ppermute(inputs, "chan", pairs))
+        stored = inputs.reshape(-1, column_count)
+        raw_blocks.append(lax.ppermute(stored, "chan", pairs).reshape(inputs.shape))
     input_pad = mask_rims(padded_2(inputs, (("lon", 2), ("lat", 1)), 1))
     own_border = border_of(input_pad)
     blocks = [input_pad]

time: 70.1 us -> 78.3 us (1.12)
  waiting for transfers between devices: 17 us -> 20.1 us
  local copies, waits for them, and re-layouts: 10.3 us -> 13.2 us
  other arithmetic: 7.67 us -> 9.81 us
    ppermute x1, waiting for transfers between devices: 1.97 us -> 6.42 us  [local(): border = lax.ppermute(own_border, 'chan', pairs)]
    reshape x0 -> x1, local copies, waits for them, and re-layouts: none -> 2.23 us  [local(): raw_blocks.append(lax.ppermute(stored, 'chan', pairs).reshape(inputs.shape))]
    ppermute x3, waiting for transfers between devices: 2.2 us -> 0.7 us  [padded_2(): before = lax.ppermute(last, axis, up)]
    ppermute x3, starting transfers between devices: 2.2 us -> 3.64 us  [padded_2(): before = lax.ppermute(last, axis, up)]
    ppermute x1, starting transfers between devices: 3 us -> 1.65 us  [local(): raw_blocks.append(lax.ppermute(stored, 'chan', pairs).reshape(inputs.shape))]
    ppermute x1, starting transfers between devices: 0.47 us -> 1.55 us  [local(): border = lax.ppermute(own_border, 'chan', pairs)]
    ppermute x3, starting transfers between devices: 4.99 us -> 3.93 us  [sum_start(): moved = lax.ppermute(piece, 'lon', pairs)]
    concatenate x1, other arithmetic: 0.18 us -> 1.21 us  [with_border(): jnp.concatenate([top[:, None, :], middle, bottom[:, None, :]], axis=1)]
  transfers between devices with their start and end apart: 17 -> 17, of which waited for: 10 -> 8; matrix products, arithmetic and copies ran while one was open for 25% -> 24% of each run, Pallas kernels for 0% -> 0%
where the time goes in v21:
time: 78.3 us; the launch traced here: 77.9 us
  waiting for transfers between devices  20.1 us (26%)
  starting transfers between devices  17.9 us (23%)
  matrix products  15.5 us (20%)
  local copies, waits for them, and re-layouts  13.2 us (17%)
  other arithmetic  9.81 us (13%)
  between operations  1.43 us (2%)
    dot_general x36, matrix products, conv_taps(): jnp.dot(kernel[tap_row, tap_col], window, preferred_element_type=jnp.floa...  12.7 us
    ppermute x1, waiting for transfers between devices, local(): border = lax.ppermute(own_border, 'chan', pairs)  6.42 us
    ppermute x3, waiting for transfers between devices, sum_start(): moved = lax.ppermute(piece, 'lon', pairs)  5.27 us
    ppermute x1, waiting for transfers between devices, local(): received.append(lax.ppermute(outgoing[shift - 1], 'chan', pairs))  5.18 us
    ppermute x3, starting transfers between devices, sum_start(): moved = lax.ppermute(piece, 'lon', pairs)  3.93 us
    ppermute x3, starting transfers between devices, padded_2(): before = lax.ppermute(last, axis, up)  3.64 us
    slice x4, local copies, waits for them, and re-layouts, window_of(): field[:, first_row:first_row + row_count, first_col:first_col + column_co...  3.57 us
    unnamed x13, local copies, waits for them, and re-layouts  3.51 us
  transfers between devices with their start and end apart: 17, of which 8 were waited for; matrix products, arithmetic and copies ran while one was open for 24% of the time, Pallas kernels for 0%

profile of v21, /device:TPU:0, one launch (start us, length us, event | category | flops | bytes accessed | tf_op | source)
XLA Modules:
  0.0 77.9 jit_solution(17605243410561718013)
XLA Ops:
  0.6 1.5 %copy.48 = bf16[128,16,128]{0,2,1:T(8,128)(2,1)S(1)} copy(bf16[128,16,128]{2,1,0:T(8,128)(2,1)} %param.4) | data formatting | bytes 1048576 | tf_op args[0]
  2.2 3.1 %collective-permute-start = (bf16[128,16,1]{0,2,1:T(2,128)(2,1)S(1)}, bf16[128,16,1]{0,2,1:T(2,128)(2,1)S(1)}, u32[]{:S(2)}, u32[]{:S(2)}) collective-permute-start(bf16[128,16,1]{0,2,1:T(2,128)(2,1)S(1)} %get-tuple-element.75), channel_id=1, source_target_pairs={{0,4},{4,8},{8,12},{12,0},{1,5},{5,9},{9,13},{13,1},{2,6},{6,10},{... | collective-permute-start | bytes 12296 | tf_op jit(solution)/shard_map/ppermute | solution.py:14
  5.3 2.1 %collective-permute-start.1 = (bf16[128,16,1]{0,2,1:T(2,128)(2,1)S(1)}, bf16[128,16,1]{0,2,1:T(2,128)(2,1)S(1)}, u32[]{:S(2)}, u32[]{:S(2)}) collective-permute-start(bf16[128,16,1]{0,2,1:T(2,128)(2,1)S(1)} %get-tuple-element.76), channel_id=1, source_target_pairs={{4,0},{8,4},{12,8},{0,12},{5,1},{9,5},{13,9},{1,13},{6,2},{10,6},{... | collective-permute-start | bytes 12296 | tf_op jit(solution)/shard_map/ppermute | solution.py:15
  7.4 1.6 %collective-permute-start.5 = (bf16[2048,128]{1,0:T(8,128)(2,1)}, bf16[2048,128]{1,0:T(8,128)(2,1)}, u32[]{:S(2)}, u32[]{:S(2)}) collective-permute-start(bf16[2048,128]{1,0:T(8,128)(2,1)} %bitcast.364), channel_id=1, source_target_pairs={{0,2},{2,0},{1,3},{3,1},{4,6},{6,4},{5,7},{7,5},{8,10},{10,8},{9,1... | collective-permute-start | bytes 1572872 | tf_op jit(solution)/shard_map/ppermute | solution.py:143
  9.8 0.7 collective-permute-done.2
  11.0 0.8 %fusion.55 = (bf16[128,16,128]{0,2,1:T(8,128)(2,1)S(1)}, bf16[128,16,128]{0,2,1:T(8,128)(2,1)S(1)}, bf16[128,16,128]{0,2,1:T(8,128)(2,1)S(1)}, bf16[128,16,128]{...) fusion(bf16[128,18,130]{0,2,1:T(8,128)(2,1)S(1)} %maximum_selec, ...), kind=kLoop, calls=%fused_computation.203 | loop fusion | bytes 9437184 | tf_op jit(solution)/shard_map/slice | solution.py:37
  11.8 1.5 %collective-permute-start.4 = (bf16[128,292]{0,1:T(8,128)(2,1)S(1)}, bf16[128,292]{0,1:T(8,128)(2,1)S(1)}, u32[]{:S(2)}, u32[]{:S(2)}) collective-permute-start(bf16[128,292]{0,1:T(8,128)(2,1)S(1)} %pad_maximum_fusion.5), channel_id=1, source_target_pairs={{0,2},{2,0},{1,3},{3,1},{4,6},{6,4},{5,7},{7,5},{8,10},{10,8},{9,1... | collective-permute-start | bytes 224264 | tf_op jit(solution)/shard_map/ppermute | solution.py:149
  16.2 6.4 %collective-permute-done.4 = bf16[128,292]{0,1:T(8,128)(2,1)S(1)} collective-permute-done((bf16[128,292]{0,1:T(8,128)(2,1)S(1)}, bf16[128,292]{0,1:T(8,128)(2,1)S(1)}, u32[]{:S(2)}, u32[]{:S(2)}) %collective-permute-start.4) | collective-permute-done | bytes 74784 | tf_op jit(solution)/shard_map/ppermute | solution.py:149
  22.6 2.2 %copy.54 = bf16[128,16,128]{0,2,1:T(8,128)(2,1)} copy(bf16[128,16,128]{2,1,0:T(8,128)(2,1)} %bitcast.28) | data formatting | bytes 1048576 | tf_op jit(solution)/shard_map/reshape | solution.py:143
  24.9 1.2 %pad_maximum_fusion.2 = bf16[128,18,130]{0,2,1:T(8,128)(2,1)S(1)} fusion(bf16[128,1,130]{0,2,1:T(8,128)(2,1)S(1)} %get-tuple-element.78, bf16[128,16,1]{0,2,1:T(2,128)(2,1)S(1)} %copy.55, bf16[128,16,128]{0,2,1:T(8,128)(2,1)} %copy.54, bf16[128,16,1]{0,2,1:T(2,128)(2,1)S(1)} %copy.53, bf16[128,1,130]{0,2,1:T(8,128)(2,1)S(1)} %get-tuple-element.77), kind=kLoop, calls=%fused_computation.92 | loop fusion | flops 2995200 | bytes 1198080 | tf_op jit(solution)/shard_map/concatenate | solution.py:132
  26.1 0.9 %fusion.53 = (bf16[128,16,128]{0,2,1:T(8,128)(2,1)S(1)}, bf16[128,16,128]{0,2,1:T(8,128)(2,1)S(1)}, bf16[128,16,128]{0,2,1:T(8,128)(2,1)S(1)}, bf16[128,16,128]{...) fusion(bf16[128,18,130]{0,2,1:T(8,128)(2,1)S(1)} %pad_maximum_f, ...), kind=kLoop, calls=%fused_computation.201 | loop fusion | bytes 9437184 | tf_op jit(solution)/shard_map/slice | solution.py:37
  27.0 2.7 %fusion.14 = (bf16[256,16,128]{0,2,1:T(8,128)(2,1)S(1)}, bf16[256,16,128]{0,2,1:T(8,128)(2,1)S(1)}, bf16[256,16,128]{0,2,1:T(8,128)(2,1)S(1)}, bf16[256,16,128]{...) fusion(bf16[128,18,130]{0,2,1:T(8,128)(2,1)S(1)} %maximum_selec, ...), kind=kLoop, calls=%fused_computation.81 | loop fusion | flops 18874368 | bytes 10635264 | tf_op jit(solution)/shard_map/concatenate | solution.py:165
  32.6 1.0 %convert_reduce_fusion = (f32[128]{0:T(128)S(1)}, bf16[128,2048]{1,0:T(8,128)(2,1)S(1)}) fusion(f32[128]{0:T(128)S(1)} %copy-done.3, f32[128,2048]{1,0:T(8,128)S(1)} %convolution_add_fusion.24, f32[128,2048]{1,0:T(8,128)S(1)} %convolution_add_fusion.17, bf16[128,2048]{0,1:T(8,128)(2,1)S(1)} %bitcast.360, bf16[3,3,128,256]{3,2,1,0:T(8,128)(2,1)S(1)} %copy-done, ...), kind=kOutput, calls=%fused_computation.90 | convolution fusion | flops 71040896 | bytes 4228104 | tf_op jit(solution)/shard_map/dot_general | solution.py:50
  37.3 0.9 %dynamic-slice_bitcast_fusion = f32[1216,128]{1,0:T(8,128)} fusion(f32[2,1216,128]{2,1,0:T(8,128)S(1)} %bitcast.308, s32[]{:T(128)S(6)} %select_n.100), kind=kLoop, calls=%fused_computation.95 | loop fusion | bytes 1245188 | tf_op jit(solution)/shard_map/jit(dynamic_index_in_dim)/squeeze | solution.py:63
  38.3 0.8 %slice_reduce_fusion.1 = (bf16[128,16]{1,0:T(8,128)(2,1)S(1)}, bf16[128,16]{1,0:T(8,128)(2,1)S(1)}) fusion(bf16[128,16,128]{2,1,0:T(8,128)(2,1)S(1)} %bitcast.306), kind=kLoop, calls=%fused_computation.98 | loop fusion | bytes 16384 | tf_op jit(solution)/shard_map/slice | solution.py:180
  39.3 1.3 %collective-permute-done.6 = f32[1216,128]{1,0:T(8,128)} collective-permute-done((f32[1216,128]{1,0:T(8,128)}, f32[1216,128]{1,0:T(8,128)}, u32[]{:S(2)}, u32[]{:S(2)}) %collective-permute-start.6) | collective-permute-done | bytes 622624 | tf_op jit(solution)/shard_map/ppermute | solution.py:64
  40.6 1.1 %bitcast_add_fusion = f32[1216,128]{1,0:T(8,128)S(1)} fusion(f32[1216,128]{1,0:T(8,128)} %collective-permute-done.6, f32[2,1216,128]{2,1,0:T(8,128)S(1)} %bitcast.309, s32[]{:T(128)S(6)} %select_n.98), kind=kLoop, calls=%fused_computation.94 | loop fusion | flops 155648 | bytes 1867780 | tf_op jit(solution)/shard_map/add | solution.py:64
  41.9 3.8 %collective-permute-start.8 = (bf16[320,128]{1,0:T(8,128)(2,1)S(1)}, bf16[320,128]{1,0:T(8,128)(2,1)S(1)}, u32[]{:S(2)}, u32[]{:S(2)}) collective-permute-start(bf16[320,128]{1,0:T(8,128)(2,1)S(1)} %pad_maximum_fusion.4), channel_id=1, source_target_pairs={{0,12},{4,0},{8,4},{12,8},{1,13},{5,1},{9,5},{13,9},{2,14},{6,2},{... | collective-permute-start | bytes 245768 | tf_op jit(solution)/shard_map/ppermute | solution.py:104
  46.4 2.6 %collective-permute-done.7 = bf16[320,128]{1,0:T(8,128)(2,1)S(1)} collective-permute-done((bf16[320,128]{1,0:T(8,128)(2,1)S(1)}, bf16[320,128]{1,0:T(8,128)(2,1)S(1)}, u32[]{:S(2)}, u32[]{:S(2)}) %collective-permute-start.7) | collective-permute-done | bytes 81952 | tf_op jit(solution)/shard_map/ppermute | solution.py:104
  50.0 2.6 %collective-permute-done.11 = bf16[304,128]{1,0:T(8,128)(2,1)S(1)} collective-permute-done((bf16[304,128]{1,0:T(8,128)(2,1)S(1)}, bf16[304,128]{1,0:T(8,128)(2,1)S(1)}, u32[]{:S(2)}, u32[]{:S(2)}) %collective-permute-start.11) | collective-permute-done | bytes 77856 | tf_op jit(solution)/shard_map/ppermute | solution.py:104
  52.6 1.0 %fusion.49 = (bf16[304,128]{1,0:T(8,128)(2,1)S(1)}, f32[304,128]{1,0:T(8,128)S(1)}) fusion(bf16[320,128]{1,0:T(8,128)(2,1)S(1)} %collective-permute-done.8, bf16[304,128]{1,0:T(8,128)(2,1)S(1)} %collective-permute-done.11, bf16[320,128]{1,0:T(8,128)(2,1)S(1)} %collective-permute-done.7, f32[4,304,128]{2,1,0:T(8,128)} %bitcast.362, s32[]{:T(128)S(6)} %select_n.106), kind=kLoop, calls=%fused_computation.198 | loop fusion | flops 272384 | bytes 622596 | tf_op jit(solution)/shard_map/convert_element_type | solution.py:73
  53.6 2.3 %collective-permute-start.12 = (bf16[304,128]{1,0:T(8,128)(2,1)S(1)}, bf16[304,128]{1,0:T(8,128)(2,1)S(1)}, u32[]{:S(2)}, u32[]{:S(2)}) collective-permute-start(bf16[304,128]{1,0:T(8,128)(2,1)S(1)} %get-tuple-element.15), channel_id=1, source_target_pairs={{0,12},{4,0},{8,4},{12,8},{1,13},{5,1},{9,5},{13,9},{2,14},{6,2},{... | collective-permute-start | bytes 233480 | tf_op jit(solution)/shard_map/ppermute | solution.py:76
  55.8 0.6 collective-permute-start.14
  56.8 0.9 %fusion.52 = (bf16[128,16,128]{0,2,1:T(8,128)(2,1)S(1)}, bf16[128,16,128]{0,2,1:T(8,128)(2,1)S(1)}, bf16[128,16,128]{0,2,1:T(8,128)(2,1)S(1)}, bf16[128,16,128]{...) fusion(bf16[128,18,130]{0,2,1:T(8,128)(2,1)S(1)} %maximum_selec, ...), kind=kLoop, calls=%fused_computation.200 | loop fusion | bytes 9437184 | tf_op jit(solution)/shard_map/slice | solution.py:37
  60.4 1.1 %fusion.2 = bf16[128,2048]{1,0:T(8,128)(2,1)} fusion(f32[128,2048]{1,0:T(8,128)S(1)} %convolution_add_fusion.9, bf16[128,2048]{0,1:T(8,128)(2,1)S(1)} %bitcast.347, bf16[3,3,128,128]{2,3,1,0:T(8,128)(2,1)S(1)} %get-tuple-element.70), kind=kOutput, calls=%fused_computation.38 | convolution fusion | flops 67633152 | bytes 2129920 | tf_op jit(solution)/shard_map/dot_general | solution.py:50
  61.5 0.9 %fusion.51 = (bf16[128,16,128]{0,2,1:T(8,128)(2,1)S(1)}, bf16[128,16,128]{0,2,1:T(8,128)(2,1)S(1)}, bf16[128,16,128]{0,2,1:T(8,128)(2,1)S(1)}, bf16[128,16,128]{...) fusion(bf16[128,18,130]{0,2,1:T(8,128)(2,1)S(1)} %maximum_selec, ...), kind=kLoop, calls=%fused_computation.199 | loop fusion | bytes 9437184 | tf_op jit(solution)/shard_map/slice | solution.py:37
  62.4 1.5 %collective-permute-start.16 = (bf16[128,2048]{1,0:T(8,128)(2,1)}, bf16[128,2048]{1,0:T(8,128)(2,1)}, u32[]{:S(2)}, u32[]{:S(2)}) collective-permute-start(bf16[128,2048]{1,0:T(8,128)(2,1)} %fusion.2), channel_id=1, source_target_pairs={{0,2},{2,0},{1,3},{3,1},{4,6},{6,4},{5,7},{7,5},{8,10},{10,8},{9,1... | collective-permute-start | bytes 1572872 | tf_op jit(solution)/shard_map/ppermute | solution.py:199
  67.2 1.1 %collective-permute-done.15 = f32[1216,128]{1,0:T(8,128)S(1)} collective-permute-done((f32[1216,128]{1,0:T(8,128)S(1)}, f32[1216,128]{1,0:T(8,128)S(1)}, u32[]{:S(2)}, u32[]{:S(2)}) %collective-permute-start.15) | collective-permute-done | bytes 622624 | tf_op jit(solution)/shard_map/ppermute | solution.py:76
  69.5 1.2 %fusion.6 = f32[3,3,128,256]{3,2,1,0:T(8,128)} fusion(s32[]{:T(128)S(6)} %select_n.114, f32[3,3,128,256]{3,2,1,0:T(8,128)S(1)} %reshape.248), kind=kLoop, calls=%fused_computation.63 | loop fusion | flops 294912 | bytes 2359300 | tf_op jit(solution)/shard_map/concatenate | solution.py:185
  70.7 5.2 %collective-permute-done.16 = bf16[128,2048]{1,0:T(8,128)(2,1)} collective-permute-done((bf16[128,2048]{1,0:T(8,128)(2,1)}, bf16[128,2048]{1,0:T(8,128)(2,1)}, u32[]{:S(2)}, u32[]{:S(2)}) %collective-permute-start.16) | collective-permute-done | bytes 524320 | tf_op jit(solution)/shard_map/ppermute | solution.py:199
  75.9 1.2 %fusion.21 = bf16[16,8,16,128]{3,1,2,0:T(8,128)(2,1)S(1)} fusion(f32[128,2048]{1,0:T(8,128)S(1)} %convolution_add_fusion, bf16[128,2048]{1,0:T(8,128)(2,1)} %collective-permute-done.16), kind=kLoop, calls=%fused_computation.96 | loop fusion | flops 786432 | bytes 2097152
  77.0 0.9 %copy.68 = bf16[16,8,16,128]{3,2,1,0:T(8,128)(2,1)} copy(bf16[16,8,16,128]{3,1,2,0:T(8,128)(2,1)S(1)} %fusion.21) | data formatting | bytes 1048576
  (118 shorter events, 19.6 us)
Async XLA Ops:
  0.6 8.4 %copy-start.2 = (bf16[128,16,128]{2,1,0:T(8,128)(2,1)S(1)}, bf16[128,16,128]{2,1,0:T(8,128)(2,1)}, u32[]{:S(2)}) copy-start(bf16[128,16,128]{2,1,0:T(8,128)(2,1)} %param.5) | copy-start | bytes 1572868
  2.2 6.9 %collective-permute-start = (bf16[128,16,1]{0,2,1:T(2,128)(2,1)S(1)}, bf16[128,16,1]{0,2,1:T(2,128)(2,1)S(1)}, u32[]{:S(2)}, u32[]{:S(2)}) collective-permute-start(bf16[128,16,1]{0,2,1:T(2,128)(2,1)S(1)} %get-tuple-element.75), channel_id=1, source_target_pairs={{0,4},{4,8},{8,12},{12,0},{1,5},{5,9},{9,13},{13,1},{2,6},{6,10},{... | collective-permute-start | bytes 12296 | tf_op jit(solution)/shard_map/ppermute | solution.py:14
  5.3 3.9 %collective-permute-start.1 = (bf16[128,16,1]{0,2,1:T(2,128)(2,1)S(1)}, bf16[128,16,1]{0,2,1:T(2,128)(2,1)S(1)}, u32[]{:S(2)}, u32[]{:S(2)}) collective-permute-start(bf16[128,16,1]{0,2,1:T(2,128)(2,1)S(1)} %get-tuple-element.76), channel_id=1, source_target_pairs={{4,0},{8,4},{12,8},{0,12},{5,1},{9,5},{13,9},{1,13},{6,2},{10,6},{... | collective-permute-start | bytes 12296 | tf_op jit(solution)/shard_map/ppermute | solution.py:15
  7.4 15.3 %collective-permute-start.5 = (bf16[2048,128]{1,0:T(8,128)(2,1)}, bf16[2048,128]{1,0:T(8,128)(2,1)}, u32[]{:S(2)}, u32[]{:S(2)}) collective-permute-start(bf16[2048,128]{1,0:T(8,128)(2,1)} %bitcast.364), channel_id=1, source_target_pairs={{0,2},{2,0},{1,3},{3,1},{4,6},{6,4},{5,7},{7,5},{8,10},{10,8},{9,1... | collective-permute-start | bytes 1572872 | tf_op jit(solution)/shard_map/ppermute | solution.py:143
  9.2 1.3 %collective-permute-start.2 = (bf16[128,1,130]{0,2,1:T(8,128)(2,1)S(1)}, bf16[128,1,130]{0,2,1:T(8,128)(2,1)S(1)}, u32[]{:S(2)}, u32[]{:S(2)}) collective-permute-start(bf16[128,1,130]{0,2,1:T(8,128)(2,1)S(1)} %get-tuple-element.73), channel_id=1, source_target_pairs={{0,1},{1,0},{2,3},{3,2},{4,5},{5,4},{6,7},{7,6},{8,9},{9,8},{10,11... | collective-permute-start | bytes 99848 | tf_op jit(solution)/shard_map/ppermute | solution.py:14
  9.3 1.4 %collective-permute-start.3 = (bf16[128,1,130]{0,2,1:T(8,128)(2,1)S(1)}, bf16[128,1,130]{0,2,1:T(8,128)(2,1)S(1)}, u32[]{:S(2)}, u32[]{:S(2)}) collective-permute-start(bf16[128,1,130]{0,2,1:T(8,128)(2,1)S(1)} %get-tuple-element.74), channel_id=1, source_target_pairs={{1,0},{0,1},{3,2},{2,3},{5,4},{4,5},{7,6},{6,7},{9,8},{8,9},{11,10... | collective-permute-start | bytes 99848 | tf_op jit(solution)/shard_map/ppermute | solution.py:15
  11.0 2.4 %copy-start = (bf16[3,3,128,256]{3,2,1,0:T(8,128)(2,1)S(1)}, bf16[3,3,128,256]{3,2,1,0:T(8,128)(2,1)}, u32[]{:S(2)}) copy-start(bf16[3,3,128,256]{3,2,1,0:T(8,128)(2,1)} %param.6) | copy-start | bytes 1769476
  11.8 10.7 %collective-permute-start.4 = (bf16[128,292]{0,1:T(8,128)(2,1)S(1)}, bf16[128,292]{0,1:T(8,128)(2,1)S(1)}, u32[]{:S(2)}, u32[]{:S(2)}) collective-permute-start(bf16[128,292]{0,1:T(8,128)(2,1)S(1)} %pad_maximum_fusion.5), channel_id=1, source_target_pairs={{0,2},{2,0},{1,3},{3,1},{4,6},{6,4},{5,7},{7,5},{8,10},{10,8},{9,1... | collective-permute-start | bytes 224264 | tf_op jit(solution)/shard_map/ppermute | solution.py:149
  31.9 0.7 copy-start.3
  38.2 2.4 %collective-permute-start.6 = (f32[1216,128]{1,0:T(8,128)}, f32[1216,128]{1,0:T(8,128)}, u32[]{:S(2)}, u32[]{:S(2)}) collective-permute-start(f32[1216,128]{1,0:T(8,128)} %dynamic-slice_bitcast_fusion), channel_id=1, source_target_pairs={{0,1},{1,0},{2,3},{3,2},{4,5},{5,4},{6,7},{7,6},{8,9},{9,8},{10,11... | collective-permute-start | bytes 1867784 | tf_op jit(solution)/shard_map/ppermute | solution.py:64
  41.7 4.0 %copy-start.1 = (f32[1216,128]{1,0:T(8,128)}, f32[1216,128]{1,0:T(8,128)S(1)}, u32[]{:S(2)}) copy-start(f32[1216,128]{1,0:T(8,128)S(1)} %bitcast_add_fusion) | copy-start | bytes 1867780
  41.8 7.2 %collective-permute-start.7 = (bf16[320,128]{1,0:T(8,128)(2,1)S(1)}, bf16[320,128]{1,0:T(8,128)(2,1)S(1)}, u32[]{:S(2)}, u32[]{:S(2)}) collective-permute-start(bf16[320,128]{1,0:T(8,128)(2,1)S(1)} %pad_maximum_fusion.3), channel_id=1, source_target_pairs={{0,4},{4,8},{8,12},{12,0},{1,5},{5,9},{9,13},{13,1},{2,6},{6,10},{... | collective-permute-start | bytes 245768 | tf_op jit(solution)/shard_map/ppermute | solution.py:104
  41.9 7.2 %collective-permute-start.8 = (bf16[320,128]{1,0:T(8,128)(2,1)S(1)}, bf16[320,128]{1,0:T(8,128)(2,1)S(1)}, u32[]{:S(2)}, u32[]{:S(2)}) collective-permute-start(bf16[320,128]{1,0:T(8,128)(2,1)S(1)} %pad_maximum_fusion.4), channel_id=1, source_target_pairs={{0,12},{4,0},{8,4},{12,8},{1,13},{5,1},{9,5},{13,9},{2,14},{6,2},{... | collective-permute-start | bytes 245768 | tf_op jit(solution)/shard_map/ppermute | solution.py:104
  46.3 6.3 %collective-permute-start.11 = (bf16[304,128]{1,0:T(8,128)(2,1)S(1)}, bf16[304,128]{1,0:T(8,128)(2,1)S(1)}, u32[]{:S(2)}, u32[]{:S(2)}) collective-permute-start(bf16[304,128]{1,0:T(8,128)(2,1)S(1)} %get-tuple-element.66), channel_id=1, source_target_pairs={{0,8},{4,12},{8,0},{12,4},{1,9},{5,13},{9,1},{13,5},{2,10},{6,14},... | collective-permute-start | bytes 233480 | tf_op jit(solution)/shard_map/ppermute | solution.py:104
  49.4 7.1 %collective-permute-start.10 = (bf16[128,1,130]{0,2,1:T(8,128)(2,1)S(1)}, bf16[128,1,130]{0,2,1:T(8,128)(2,1)S(1)}, u32[]{:S(2)}, u32[]{:S(2)}) collective-permute-start(bf16[128,1,130]{0,2,1:T(8,128)(2,1)S(1)} %get-tuple-element.72), channel_id=1, source_target_pairs={{1,0},{0,1},{3,2},{2,3},{5,4},{4,5},{7,6},{6,7},{9,8},{8,9},{11,10... | collective-permute-start | bytes 99848 | tf_op jit(solution)/shard_map/ppermute | solution.py:15
  49.5 7.0 %collective-permute-start.9 = (bf16[128,1,130]{0,2,1:T(8,128)(2,1)S(1)}, bf16[128,1,130]{0,2,1:T(8,128)(2,1)S(1)}, u32[]{:S(2)}, u32[]{:S(2)}) collective-permute-start(bf16[128,1,130]{0,2,1:T(8,128)(2,1)S(1)} %get-tuple-element.71), channel_id=1, source_target_pairs={{0,1},{1,0},{2,3},{3,2},{4,5},{5,4},{6,7},{7,6},{8,9},{9,8},{10,11... | collective-permute-start | bytes 99848 | tf_op jit(solution)/shard_map/ppermute | solution.py:14
  53.6 12.4 %collective-permute-start.12 = (bf16[304,128]{1,0:T(8,128)(2,1)S(1)}, bf16[304,128]{1,0:T(8,128)(2,1)S(1)}, u32[]{:S(2)}, u32[]{:S(2)}) collective-permute-start(bf16[304,128]{1,0:T(8,128)(2,1)S(1)} %get-tuple-element.15), channel_id=1, source_target_pairs={{0,12},{4,0},{8,4},{12,8},{1,13},{5,1},{9,5},{13,9},{2,14},{6,2},{... | collective-permute-start | bytes 233480 | tf_op jit(solution)/shard_map/ppermute | solution.py:76
  55.8 10.1 %collective-permute-start.13 = (bf16[304,128]{1,0:T(8,128)(2,1)S(1)}, bf16[304,128]{1,0:T(8,128)(2,1)S(1)}, u32[]{:S(2)}, u32[]{:S(2)}) collective-permute-start(bf16[304,128]{1,0:T(8,128)(2,1)S(1)} %get-tuple-element.15), channel_id=1, source_target_pairs={{0,8},{4,12},{8,0},{12,4},{1,9},{5,13},{9,1},{13,5},{2,10},{6,14},... | collective-permute-start | bytes 233480 | tf_op jit(solution)/shard_map/ppermute | solution.py:76
  55.8 10.2 %collective-permute-start.14 = (bf16[304,128]{1,0:T(8,128)(2,1)S(1)}, bf16[304,128]{1,0:T(8,128)(2,1)S(1)}, u32[]{:S(2)}, u32[]{:S(2)}) collective-permute-start(bf16[304,128]{1,0:T(8,128)(2,1)S(1)} %get-tuple-element.15), channel_id=1, source_target_pairs={{0,4},{4,8},{8,12},{12,0},{1,5},{5,9},{9,13},{13,1},{2,6},{6,10},{... | collective-permute-start | bytes 233480 | tf_op jit(solution)/shard_map/ppermute | solution.py:76
  62.4 13.4 %collective-permute-start.16 = (bf16[128,2048]{1,0:T(8,128)(2,1)}, bf16[128,2048]{1,0:T(8,128)(2,1)}, u32[]{:S(2)}, u32[]{:S(2)}) collective-permute-start(bf16[128,2048]{1,0:T(8,128)(2,1)} %fusion.2), channel_id=1, source_target_pairs={{0,2},{2,0},{1,3},{3,1},{4,6},{6,4},{5,7},{7,5},{8,10},{10,8},{9,1... | collective-permute-start | bytes 1572872 | tf_op jit(solution)/shard_map/ppermute | solution.py:199
  66.2 2.1 %collective-permute-start.15 = (f32[1216,128]{1,0:T(8,128)S(1)}, f32[1216,128]{1,0:T(8,128)S(1)}, u32[]{:S(2)}, u32[]{:S(2)}) collective-permute-start(f32[1216,128]{1,0:T(8,128)S(1)} %bitcast.323), channel_id=1, source_target_pairs={{0,1},{1,0},{2,3},{3,2},{4,5},{5,4},{6,7},{7,6},{8,9},{9,8},{10,11... | collective-permute-start | bytes 1867784 | tf_op jit(solution)/shard_map/ppermute | solution.py:76

commit v22 on v12

--- a/solution.py
+++ b/solution.py
@@ -169,7 +169,6 @@
     preact = preact + bias_vector[:, None]
     upstream = cotangent.reshape(own_channels, -1).astype(jnp.float32)
     grad_pre = (upstream * gelu_slope(preact)).astype(jnp.bfloat16)
-    grad_pre, kernel_blocks = lax.optimization_barrier((grad_pre, kernel_blocks))
     bias_part = jnp.sum(grad_pre.astype(jnp.float32), axis=1)
     input_local = jnp.concatenate(blocks, axis=0)
     taps = []
@@ -185,6 +184,7 @@
         taps.append(jnp.stack(row_taps))
     weight_part = jnp.stack(taps)
     flat = jnp.concatenate([weight_part.reshape(-1), bias_part])
+    flat, kernel_blocks = lax.optimization_barrier((flat, kernel_blocks))
     grad_field = grad_pre.reshape(own_channels, row_count, column_count)
     edges = (grad_field[:, :, column_count - 1 :], grad_field[:, :, :1])
     scattered, (before, after) = sum_start(flat, jnp.bfloat16, edges)

time: 71.6 us -> 76.2 us (1.064)
  waiting for transfers between devices: 14.6 us -> 17.9 us
  local copies, waits for them, and re-layouts: 10.2 us -> 11.5 us
    ppermute x1, waiting for transfers between devices: 3.36 us -> 6.68 us  [local(): kernel_blocks.append(lax.ppermute(kernel_sends[shift - 1], 'chan', pairs))]
    unnamed x18 -> x14, local copies, waits for them, and re-layouts: 3.57 us -> 3.55 us
  transfers between devices with their start and end apart: 19 -> 19, of which waited for: 10 -> 10; matrix products, arithmetic and copies ran while one was open for 27% -> 24% of each run, Pallas kernels for 0% -> 0%
where the time goes in v22:
time: 76.2 us; the launch traced here: 75.9 us
  starting transfers between devices  22.3 us (29%)
  waiting for transfers between devices  17.9 us (23%)
  matrix products  14.8 us (19%)
  local copies, waits for them, and re-layouts  11.5 us (15%)
  other arithmetic  7.92 us (10%)
  between operations  1.51 us (2%)
    dot_general x36, matrix products, conv_taps(): jnp.dot(kernel[tap_row, tap_col], window, preferred_element_type=jnp.floa...  11.9 us
    ppermute x1, waiting for transfers between devices, local(): kernel_blocks.append(lax.ppermute(kernel_sends[shift - 1], 'chan', pairs))  6.68 us
    ppermute x3, waiting for transfers between devices, sum_start(): moved = lax.ppermute(piece, 'lon', pairs)  5.89 us
    ppermute x3, starting transfers between devices, sum_start(): moved = lax.ppermute(piece, 'lon', pairs)  4.67 us
    ppermute x4, starting transfers between devices, direct_all_gather(): pieces.append(lax.ppermute(sent, axis, pairs).astype(jnp.float32))  4.62 us
    unnamed x14, local copies, waits for them, and re-layouts  3.55 us
    slice x4, local copies, waits for them, and re-layouts, window_of(): field[:, first_row:first_row + row_count, first_col:first_col + column_co...  3.49 us
    ppermute x3, starting transfers between devices, padded_2(): after = lax.ppermute(initial, axis, down)  3.24 us
  transfers between devices with their start and end apart: 19, of which 10 were waited for; matrix products, arithmetic and copies ran while one was open for 24% of the time, Pallas kernels for 0%

profile of v22, /device:TPU:0, one launch (start us, length us, event | category | flops | bytes accessed | tf_op | source)
XLA Modules:
  0.0 75.9 jit_solution(13152444286211094858)
XLA Ops:
  0.7 1.6 %copy.32 = bf16[128,16,128]{0,2,1:T(8,128)(2,1)S(1)} copy(bf16[128,16,128]{2,1,0:T(8,128)(2,1)} %param.4) | data formatting | bytes 1048576 | tf_op args[0]
  2.2 3.0 %collective-permute-start.5 = (bf16[128,16,128]{0,2,1:T(8,128)(2,1)S(1)}, bf16[128,16,128]{0,2,1:T(8,128)(2,1)}, u32[]{:S(2)}, u32[]{:S(2)}) collective-permute-start(bf16[128,16,128]{0,2,1:T(8,128)(2,1)S(1)} %copy.32), channel_id=1, source_target_pairs={{0,2},{2,0},{1,3},{3,1},{4,6},{6,4},{5,7},{7,5},{8,10},{10,8},{9,1... | collective-permute-start | bytes 1572872 | tf_op jit(solution)/shard_map/ppermute | solution.py:142
  5.2 1.6 %collective-permute-start = (bf16[128,16,1]{0,2,1:T(2,128)(2,1)S(1)}, bf16[128,16,1]{0,2,1:T(2,128)(2,1)S(1)}, u32[]{:S(2)}, u32[]{:S(2)}) collective-permute-start(bf16[128,16,1]{0,2,1:T(2,128)(2,1)S(1)} %get-tuple-element.77), channel_id=1, source_target_pairs={{0,4},{4,8},{8,12},{12,0},{1,5},{5,9},{9,13},{13,1},{2,6},{6,10},{... | collective-permute-start | bytes 12296 | tf_op jit(solution)/shard_map/ppermute | solution.py:14
  6.9 2.2 %collective-permute-start.1 = (bf16[128,16,1]{0,2,1:T(2,128)(2,1)S(1)}, bf16[128,16,1]{0,2,1:T(2,128)(2,1)S(1)}, u32[]{:S(2)}, u32[]{:S(2)}) collective-permute-start(bf16[128,16,1]{0,2,1:T(2,128)(2,1)S(1)} %get-tuple-element.78), channel_id=1, source_target_pairs={{4,0},{8,4},{12,8},{0,12},{5,1},{9,5},{13,9},{1,13},{6,2},{10,6},{... | collective-permute-start | bytes 12296 | tf_op jit(solution)/shard_map/ppermute | solution.py:15
  9.4 1.4 %collective-permute-done = bf16[128,16,1]{0,2,1:T(2,128)(2,1)S(1)} collective-permute-done((bf16[128,16,1]{0,2,1:T(2,128)(2,1)S(1)}, bf16[128,16,1]{0,2,1:T(2,128)(2,1)S(1)}, u32[]{:S(2)}, u32[]{:S(2)}) %collective-permute-start) | collective-permute-done | bytes 4128 | tf_op jit(solution)/shard_map/ppermute | solution.py:14
  11.3 0.7 collective-permute-done.2
  12.6 0.9 %fusion.55 = (bf16[128,16,128]{0,2,1:T(8,128)(2,1)S(1)}, bf16[128,16,128]{0,2,1:T(8,128)(2,1)S(1)}, bf16[128,16,128]{0,2,1:T(8,128)(2,1)S(1)}, bf16[128,16,128]{...) fusion(bf16[128,18,130]{0,2,1:T(8,128)(2,1)S(1)} %maximum_selec, ...), kind=kLoop, calls=%fused_computation.212 | loop fusion | bytes 9437184 | tf_op jit(solution)/shard_map/slice | solution.py:37
  16.8 2.0 %collective-permute-done.4 = bf16[128,292]{0,1:T(8,128)(2,1)S(1)} collective-permute-done((bf16[128,292]{0,1:T(8,128)(2,1)S(1)}, bf16[128,292]{0,1:T(8,128)(2,1)S(1)}, u32[]{:S(2)}, u32[]{:S(2)}) %collective-permute-start.4) | collective-permute-done | bytes 74784 | tf_op jit(solution)/shard_map/ppermute | solution.py:148
  18.8 1.2 %pad_maximum_fusion.3 = bf16[128,18,130]{0,2,1:T(8,128)(2,1)S(1)} fusion(bf16[128,1,130]{0,2,1:T(8,128)(2,1)S(1)} %get-tuple-element.84, bf16[128,16,1]{0,2,1:T(2,128)(2,1)S(1)} %copy.37, bf16[128,16,128]{0,2,1:T(8,128)(2,1)} %collective-permute-done.5, bf16[128,16,1]{0,2,1:T(2,128)(2,1)S(1)} %copy.36, bf16[128,1,130]{0,2,1:T(8,128)(2,1)S(1)} %get-tuple-element.83), kind=kLoop, calls=%fused_computation.92 | loop fusion | flops 2995200 | bytes 1198080 | tf_op jit(solution)/shard_map/concatenate | solution.py:132
  20.0 0.9 %fusion.53 = (bf16[128,16,128]{0,2,1:T(8,128)(2,1)S(1)}, bf16[128,16,128]{0,2,1:T(8,128)(2,1)S(1)}, bf16[128,16,128]{0,2,1:T(8,128)(2,1)S(1)}, bf16[128,16,128]{...) fusion(bf16[128,18,130]{0,2,1:T(8,128)(2,1)S(1)} %pad_maximum_f, ...), kind=kLoop, calls=%fused_computation.210 | loop fusion | bytes 9437184 | tf_op jit(solution)/shard_map/slice | solution.py:37
  21.0 2.7 %fusion.16 = (bf16[256,16,128]{0,2,1:T(8,128)(2,1)S(1)}, bf16[256,16,128]{0,2,1:T(8,128)(2,1)S(1)}, bf16[256,16,128]{0,2,1:T(8,128)(2,1)S(1)}, bf16[256,16,128]{...) fusion(bf16[128,18,130]{0,2,1:T(8,128)(2,1)S(1)} %maximum_selec, ...), kind=kLoop, calls=%fused_computation.82 | loop fusion | flops 18874368 | bytes 10635264 | tf_op jit(solution)/shard_map/concatenate | solution.py:173
  26.5 1.0 %convert_reduce_fusion = (f32[128]{0:T(128)S(1)}, bf16[128,2048]{1,0:T(8,128)(2,1)S(1)}) fusion(f32[128]{0:T(128)S(1)} %copy-done.2, f32[128,2048]{1,0:T(8,128)S(1)} %convolution_add_fusion.24, f32[128,2048]{1,0:T(8,128)S(1)} %convolution_add_fusion.17, bf16[128,2048]{0,1:T(8,128)(2,1)S(1)} %bitcast.374, bf16[3,3,128,256]{3,2,1,0:T(8,128)(2,1)S(1)} %copy-done, ...), kind=kOutput, calls=%fused_computation.90 | convolution fusion | flops 71040896 | bytes 4228104 | tf_op jit(solution)/shard_map/dot_general | solution.py:50
  31.3 1.8 %collective-permute-start.6 = (bf16[3,3,128,128]{3,2,1,0:T(8,128)(2,1)S(1)}, bf16[3,3,128,128]{3,2,1,0:T(8,128)(2,1)S(1)}, u32[]{:S(2)}, u32[]{:S(2)}) collective-permute-start(bf16[3,3,128,128]{3,2,1,0:T(8,128)(2,1)S(1)} %get-tuple-element.8), channel_id=1, source_target_pairs={{0,2},{2,0},{1,3},{3,1},{4,6},{6,4},{5,7},{7,5},{8,10},{10,8},{9,1... | collective-permute-start | bytes 884744 | tf_op jit(solution)/shard_map/ppermute | solution.py:164
  33.1 6.7 %collective-permute-done.6 = bf16[3,3,128,128]{3,2,1,0:T(8,128)(2,1)S(1)} collective-permute-done((bf16[3,3,128,128]{3,2,1,0:T(8,128)(2,1)S(1)}, bf16[3,3,128,128]{3,2,1,0:T(8,128)(2,1)S(1)}, u32[]{:S(2)}, u32[]{:S(2)}) %collective-permute-start.6) | collective-permute-done | bytes 294944 | tf_op jit(solution)/shard_map/ppermute | solution.py:164
  40.7 1.3 %slice_reduce_fusion.1 = (bf16[128,16]{1,0:T(8,128)(2,1)}, bf16[128,16]{1,0:T(8,128)(2,1)S(1)}) fusion(bf16[128,16,128]{2,1,0:T(8,128)(2,1)S(1)} %bitcast.321), kind=kLoop, calls=%fused_computation.98 | loop fusion | bytes 16384 | tf_op jit(solution)/shard_map/slice | solution.py:189
  42.0 0.9 %reshape.217 = bf16[16,128]{1,0:T(8,128)(2,1)S(1)} reshape(bf16[128,16]{1,0:T(8,128)(2,1)} %get-tuple-element.13) | data formatting | bytes 8192 | tf_op jit(solution)/shard_map/reshape | solution.py:103
  42.9 1.2 %collective-permute-start.14 = (bf16[128,16,128]{0,2,1:T(8,128)(2,1)S(1)}, bf16[128,16,128]{0,2,1:T(8,128)(2,1)S(1)}, u32[]{:S(2)}, u32[]{:S(2)}) collective-permute-start(bf16[128,16,128]{0,2,1:T(8,128)(2,1)S(1)} %copy.41), channel_id=1, source_target_pairs={{0,2},{2,0},{1,3},{3,1},{4,6},{6,4},{5,7},{7,5},{8,10},{10,8},{9,1... | collective-permute-start | bytes 1572872 | tf_op jit(solution)/shard_map/ppermute | solution.py:194
  44.2 1.1 %bitcast_add_fusion = f32[1216,128]{1,0:T(8,128)S(1)} fusion(f32[1216,128]{1,0:T(8,128)} %collective-permute-done.7, f32[2,1216,128]{2,1,0:T(8,128)S(1)} %bitcast.323, s32[]{:T(128)S(6)} %select_n.101), kind=kLoop, calls=%fused_computation.95 | loop fusion | flops 155648 | bytes 1867780 | tf_op jit(solution)/shard_map/add | solution.py:64
  45.4 1.6 %collective-permute-start.8 = (bf16[320,128]{1,0:T(8,128)(2,1)S(1)}, bf16[320,128]{1,0:T(8,128)(2,1)S(1)}, u32[]{:S(2)}, u32[]{:S(2)}) collective-permute-start(bf16[320,128]{1,0:T(8,128)(2,1)S(1)} %pad_maximum_fusion.5), channel_id=1, source_target_pairs={{0,4},{4,8},{8,12},{12,0},{1,5},{5,9},{9,13},{13,1},{2,6},{6,10},{... | collective-permute-start | bytes 245768 | tf_op jit(solution)/shard_map/ppermute | solution.py:104
  47.0 2.2 %collective-permute-start.9 = (bf16[320,128]{1,0:T(8,128)(2,1)S(1)}, bf16[320,128]{1,0:T(8,128)(2,1)S(1)}, u32[]{:S(2)}, u32[]{:S(2)}) collective-permute-start(bf16[320,128]{1,0:T(8,128)(2,1)S(1)} %pad_maximum_fusion.6), channel_id=1, source_target_pairs={{0,12},{4,0},{8,4},{12,8},{1,13},{5,1},{9,5},{13,9},{2,14},{6,2},{... | collective-permute-start | bytes 245768 | tf_op jit(solution)/shard_map/ppermute | solution.py:104
  49.3 0.8 %collective-permute-start.13 = (bf16[304,128]{1,0:T(8,128)(2,1)S(1)}, bf16[304,128]{1,0:T(8,128)(2,1)S(1)}, u32[]{:S(2)}, u32[]{:S(2)}) collective-permute-start(bf16[304,128]{1,0:T(8,128)(2,1)S(1)} %get-tuple-element.68), channel_id=1, source_target_pairs={{0,8},{4,12},{8,0},{12,4},{1,9},{5,13},{9,1},{13,5},{2,10},{6,14},... | collective-permute-start | bytes 233480 | tf_op jit(solution)/shard_map/ppermute | solution.py:104
  50.1 2.1 %collective-permute-done.8 = bf16[320,128]{1,0:T(8,128)(2,1)S(1)} collective-permute-done((bf16[320,128]{1,0:T(8,128)(2,1)S(1)}, bf16[320,128]{1,0:T(8,128)(2,1)S(1)}, u32[]{:S(2)}, u32[]{:S(2)}) %collective-permute-start.8) | collective-permute-done | bytes 81952 | tf_op jit(solution)/shard_map/ppermute | solution.py:104
  52.3 0.7 collective-permute-done.9
  53.8 3.1 %collective-permute-done.13 = bf16[304,128]{1,0:T(8,128)(2,1)S(1)} collective-permute-done((bf16[304,128]{1,0:T(8,128)(2,1)S(1)}, bf16[304,128]{1,0:T(8,128)(2,1)S(1)}, u32[]{:S(2)}, u32[]{:S(2)}) %collective-permute-start.13) | collective-permute-done | bytes 77856 | tf_op jit(solution)/shard_map/ppermute | solution.py:104
  57.3 3.9 %collective-permute-start.15 = (bf16[304,128]{1,0:T(8,128)(2,1)S(1)}, bf16[304,128]{1,0:T(8,128)(2,1)S(1)}, u32[]{:S(2)}, u32[]{:S(2)}) collective-permute-start(bf16[304,128]{1,0:T(8,128)(2,1)S(1)} %convert_element_type.64), channel_id=1, source_target_pairs={{0,12},{4,0},{8,4},{12,8},{1,13},{5,1},{9,5},{13,9},{2,14},{6,2},{... | collective-permute-start | bytes 233480 | tf_op jit(solution)/shard_map/ppermute | solution.py:76
  61.1 0.7 collective-permute-start.17
  62.2 0.7 fusion.52
  62.9 1.4 %collective-permute-start.12 = (bf16[128,292]{0,1:T(8,128)(2,1)S(1)}, bf16[128,292]{0,1:T(8,128)(2,1)S(1)}, u32[]{:S(2)}, u32[]{:S(2)}) collective-permute-start(bf16[128,292]{0,1:T(8,128)(2,1)S(1)} %pad_maximum_fusion.8), channel_id=1, source_target_pairs={{0,2},{2,0},{1,3},{3,1},{4,6},{6,4},{5,7},{7,5},{8,10},{10,8},{9,1... | collective-permute-start | bytes 224264 | tf_op jit(solution)/shard_map/ppermute | solution.py:209
  67.3 0.8 %collective-permute-done.16 = bf16[304,128]{1,0:T(8,128)(2,1)S(1)} collective-permute-done((bf16[304,128]{1,0:T(8,128)(2,1)S(1)}, bf16[304,128]{1,0:T(8,128)(2,1)S(1)}, u32[]{:S(2)}, u32[]{:S(2)}) %collective-permute-start.16) | collective-permute-done | bytes 77856 | tf_op jit(solution)/shard_map/ppermute | solution.py:76
  68.7 0.9 %fusion.50 = (bf16[128,16,128]{0,2,1:T(8,128)(2,1)S(1)}, bf16[128,16,128]{0,2,1:T(8,128)(2,1)S(1)}, bf16[128,16,128]{0,2,1:T(8,128)(2,1)S(1)}, bf16[128,16,128]{...) fusion(bf16[128,18,130]{0,2,1:T(8,128)(2,1)S(1)} %pad_maximum_f, ...), kind=kLoop, calls=%fused_computation.207 | loop fusion | bytes 9437184 | tf_op jit(solution)/shard_map/slice | solution.py:37
  72.6 0.9 %copy.55 = bf16[16,8,16,128]{3,2,1,0:T(8,128)(2,1)} copy(bf16[16,8,16,128]{3,1,2,0:T(8,128)(2,1)S(1)} %fusion.7) | data formatting | bytes 1048576
  74.7 1.2 %fusion.8 = f32[3,3,128,256]{3,2,1,0:T(8,128)} fusion(s32[]{:T(128)S(6)} %select_n.117, f32[3,3,128,256]{3,2,1,0:T(8,128)S(1)} %reshape.241), kind=kLoop, calls=%fused_computation.64 | loop fusion | flops 294912 | bytes 2359300 | tf_op jit(solution)/shard_map/concatenate | solution.py:199
  (130 shorter events, 21.0 us)
Async XLA Ops:
  0.6 8.5 %copy-start.1 = (bf16[128,16,128]{2,1,0:T(8,128)(2,1)S(1)}, bf16[128,16,128]{2,1,0:T(8,128)(2,1)}, u32[]{:S(2)}) copy-start(bf16[128,16,128]{2,1,0:T(8,128)(2,1)} %param.5) | copy-start | bytes 1572868
  0.6 8.6 %copy-start = (bf16[3,3,128,256]{3,2,1,0:T(8,128)(2,1)S(1)}, bf16[3,3,128,256]{3,2,1,0:T(8,128)(2,1)}, u32[]{:S(2)}) copy-start(bf16[3,3,128,256]{3,2,1,0:T(8,128)(2,1)} %param.6) | copy-start | bytes 1769476
  2.2 16.6 %collective-permute-start.5 = (bf16[128,16,128]{0,2,1:T(8,128)(2,1)S(1)}, bf16[128,16,128]{0,2,1:T(8,128)(2,1)}, u32[]{:S(2)}, u32[]{:S(2)}) collective-permute-start(bf16[128,16,128]{0,2,1:T(8,128)(2,1)S(1)} %copy.32), channel_id=1, source_target_pairs={{0,2},{2,0},{1,3},{3,1},{4,6},{6,4},{5,7},{7,5},{8,10},{10,8},{9,1... | collective-permute-start | bytes 1572872 | tf_op jit(solution)/shard_map/ppermute | solution.py:142
  5.2 5.5 %collective-permute-start = (bf16[128,16,1]{0,2,1:T(2,128)(2,1)S(1)}, bf16[128,16,1]{0,2,1:T(2,128)(2,1)S(1)}, u32[]{:S(2)}, u32[]{:S(2)}) collective-permute-start(bf16[128,16,1]{0,2,1:T(2,128)(2,1)S(1)} %get-tuple-element.77), channel_id=1, source_target_pairs={{0,4},{4,8},{8,12},{12,0},{1,5},{5,9},{9,13},{13,1},{2,6},{6,10},{... | collective-permute-start | bytes 12296 | tf_op jit(solution)/shard_map/ppermute | solution.py:14
  6.9 3.9 %collective-permute-start.1 = (bf16[128,16,1]{0,2,1:T(2,128)(2,1)S(1)}, bf16[128,16,1]{0,2,1:T(2,128)(2,1)S(1)}, u32[]{:S(2)}, u32[]{:S(2)}) collective-permute-start(bf16[128,16,1]{0,2,1:T(2,128)(2,1)S(1)} %get-tuple-element.78), channel_id=1, source_target_pairs={{4,0},{8,4},{12,8},{0,12},{5,1},{9,5},{13,9},{1,13},{6,2},{10,6},{... | collective-permute-start | bytes 12296 | tf_op jit(solution)/shard_map/ppermute | solution.py:15
  10.8 1.3 %collective-permute-start.2 = (bf16[128,1,130]{0,2,1:T(8,128)(2,1)S(1)}, bf16[128,1,130]{0,2,1:T(8,128)(2,1)S(1)}, u32[]{:S(2)}, u32[]{:S(2)}) collective-permute-start(bf16[128,1,130]{0,2,1:T(8,128)(2,1)S(1)} %get-tuple-element.75), channel_id=1, source_target_pairs={{0,1},{1,0},{2,3},{3,2},{4,5},{5,4},{6,7},{7,6},{8,9},{9,8},{10,11... | collective-permute-start | bytes 99848 | tf_op jit(solution)/shard_map/ppermute | solution.py:14
  10.8 1.4 %collective-permute-start.3 = (bf16[128,1,130]{0,2,1:T(8,128)(2,1)S(1)}, bf16[128,1,130]{0,2,1:T(8,128)(2,1)S(1)}, u32[]{:S(2)}, u32[]{:S(2)}) collective-permute-start(bf16[128,1,130]{0,2,1:T(8,128)(2,1)S(1)} %get-tuple-element.76), channel_id=1, source_target_pairs={{1,0},{0,1},{3,2},{2,3},{5,4},{4,5},{7,6},{6,7},{9,8},{8,9},{11,10... | collective-permute-start | bytes 99848 | tf_op jit(solution)/shard_map/ppermute | solution.py:15
  13.5 5.2 %collective-permute-start.4 = (bf16[128,292]{0,1:T(8,128)(2,1)S(1)}, bf16[128,292]{0,1:T(8,128)(2,1)S(1)}, u32[]{:S(2)}, u32[]{:S(2)}) collective-permute-start(bf16[128,292]{0,1:T(8,128)(2,1)S(1)} %pad_maximum_fusion.7), channel_id=1, source_target_pairs={{0,2},{2,0},{1,3},{3,1},{4,6},{6,4},{5,7},{7,5},{8,10},{10,8},{9,1... | collective-permute-start | bytes 224264 | tf_op jit(solution)/shard_map/ppermute | solution.py:148
  25.8 0.7 copy-start.2
  31.3 8.6 %collective-permute-start.6 = (bf16[3,3,128,128]{3,2,1,0:T(8,128)(2,1)S(1)}, bf16[3,3,128,128]{3,2,1,0:T(8,128)(2,1)S(1)}, u32[]{:S(2)}, u32[]{:S(2)}) collective-permute-start(bf16[3,3,128,128]{3,2,1,0:T(8,128)(2,1)S(1)} %get-tuple-element.8), channel_id=1, source_target_pairs={{0,2},{2,0},{1,3},{3,1},{4,6},{6,4},{5,7},{7,5},{8,10},{10,8},{9,1... | collective-permute-start | bytes 884744 | tf_op jit(solution)/shard_map/ppermute | solution.py:164
  40.0 4.2 %collective-permute-start.7 = (f32[1216,128]{1,0:T(8,128)S(1)}, f32[1216,128]{1,0:T(8,128)}, u32[]{:S(2)}, u32[]{:S(2)}) collective-permute-start(f32[1216,128]{1,0:T(8,128)S(1)} %dynamic-slice_bitcast_fusion), channel_id=1, source_target_pairs={{0,1},{1,0},{2,3},{3,2},{4,5},{5,4},{6,7},{7,6},{8,9},{9,8},{10,11... | collective-permute-start | bytes 1867784 | tf_op jit(solution)/shard_map/ppermute | solution.py:64
  42.9 14.3 %collective-permute-start.14 = (bf16[128,16,128]{0,2,1:T(8,128)(2,1)S(1)}, bf16[128,16,128]{0,2,1:T(8,128)(2,1)S(1)}, u32[]{:S(2)}, u32[]{:S(2)}) collective-permute-start(bf16[128,16,128]{0,2,1:T(8,128)(2,1)S(1)} %copy.41), channel_id=1, source_target_pairs={{0,2},{2,0},{1,3},{3,1},{4,6},{6,4},{5,7},{7,5},{8,10},{10,8},{9,1... | collective-permute-start | bytes 1572872 | tf_op jit(solution)/shard_map/ppermute | solution.py:194
  45.4 6.8 %collective-permute-start.8 = (bf16[320,128]{1,0:T(8,128)(2,1)S(1)}, bf16[320,128]{1,0:T(8,128)(2,1)S(1)}, u32[]{:S(2)}, u32[]{:S(2)}) collective-permute-start(bf16[320,128]{1,0:T(8,128)(2,1)S(1)} %pad_maximum_fusion.5), channel_id=1, source_target_pairs={{0,4},{4,8},{8,12},{12,0},{1,5},{5,9},{9,13},{13,1},{2,6},{6,10},{... | collective-permute-start | bytes 245768 | tf_op jit(solution)/shard_map/ppermute | solution.py:104
  47.0 6.0 %collective-permute-start.9 = (bf16[320,128]{1,0:T(8,128)(2,1)S(1)}, bf16[320,128]{1,0:T(8,128)(2,1)S(1)}, u32[]{:S(2)}, u32[]{:S(2)}) collective-permute-start(bf16[320,128]{1,0:T(8,128)(2,1)S(1)} %pad_maximum_fusion.6), channel_id=1, source_target_pairs={{0,12},{4,0},{8,4},{12,8},{1,13},{5,1},{9,5},{13,9},{2,14},{6,2},{... | collective-permute-start | bytes 245768 | tf_op jit(solution)/shard_map/ppermute | solution.py:104
  49.3 7.6 %collective-permute-start.13 = (bf16[304,128]{1,0:T(8,128)(2,1)S(1)}, bf16[304,128]{1,0:T(8,128)(2,1)S(1)}, u32[]{:S(2)}, u32[]{:S(2)}) collective-permute-start(bf16[304,128]{1,0:T(8,128)(2,1)S(1)} %get-tuple-element.68), channel_id=1, source_target_pairs={{0,8},{4,12},{8,0},{12,4},{1,9},{5,13},{9,1},{13,5},{2,10},{6,14},... | collective-permute-start | bytes 233480 | tf_op jit(solution)/shard_map/ppermute | solution.py:104
  53.2 8.6 %collective-permute-start.10 = (bf16[128,1,130]{0,2,1:T(8,128)(2,1)S(1)}, bf16[128,1,130]{0,2,1:T(8,128)(2,1)S(1)}, u32[]{:S(2)}, u32[]{:S(2)}) collective-permute-start(bf16[128,1,130]{0,2,1:T(8,128)(2,1)S(1)} %get-tuple-element.73), channel_id=1, source_target_pairs={{0,1},{1,0},{2,3},{3,2},{4,5},{5,4},{6,7},{7,6},{8,9},{9,8},{10,11... | collective-permute-start | bytes 99848 | tf_op jit(solution)/shard_map/ppermute | solution.py:14
  53.3 8.5 %collective-permute-start.11 = (bf16[128,1,130]{0,2,1:T(8,128)(2,1)S(1)}, bf16[128,1,130]{0,2,1:T(8,128)(2,1)S(1)}, u32[]{:S(2)}, u32[]{:S(2)}) collective-permute-start(bf16[128,1,130]{0,2,1:T(8,128)(2,1)S(1)} %get-tuple-element.74), channel_id=1, source_target_pairs={{1,0},{0,1},{3,2},{2,3},{5,4},{4,5},{7,6},{6,7},{9,8},{8,9},{11,10... | collective-permute-start | bytes 99848 | tf_op jit(solution)/shard_map/ppermute | solution.py:15
  57.3 10.0 %collective-permute-start.15 = (bf16[304,128]{1,0:T(8,128)(2,1)S(1)}, bf16[304,128]{1,0:T(8,128)(2,1)S(1)}, u32[]{:S(2)}, u32[]{:S(2)}) collective-permute-start(bf16[304,128]{1,0:T(8,128)(2,1)S(1)} %convert_element_type.64), channel_id=1, source_target_pairs={{0,12},{4,0},{8,4},{12,8},{1,13},{5,1},{9,5},{13,9},{2,14},{6,2},{... | collective-permute-start | bytes 233480 | tf_op jit(solution)/shard_map/ppermute | solution.py:76
  61.1 7.0 %collective-permute-start.16 = (bf16[304,128]{1,0:T(8,128)(2,1)S(1)}, bf16[304,128]{1,0:T(8,128)(2,1)S(1)}, u32[]{:S(2)}, u32[]{:S(2)}) collective-permute-start(bf16[304,128]{1,0:T(8,128)(2,1)S(1)} %convert_element_type.64), channel_id=1, source_target_pairs={{0,8},{4,12},{8,0},{12,4},{1,9},{5,13},{9,1},{13,5},{2,10},{6,14},... | collective-permute-start | bytes 233480 | tf_op jit(solution)/shard_map/ppermute | solution.py:76
  61.1 7.1 %collective-permute-start.17 = (bf16[304,128]{1,0:T(8,128)(2,1)S(1)}, bf16[304,128]{1,0:T(8,128)(2,1)S(1)}, u32[]{:S(2)}, u32[]{:S(2)}) collective-permute-start(bf16[304,128]{1,0:T(8,128)(2,1)S(1)} %convert_element_type.64), channel_id=1, source_target_pairs={{0,4},{4,8},{8,12},{12,0},{1,5},{5,9},{9,13},{13,1},{2,6},{6,10},{... | collective-permute-start | bytes 233480 | tf_op jit(solution)/shard_map/ppermute | solution.py:76
  62.9 5.5 %collective-permute-start.12 = (bf16[128,292]{0,1:T(8,128)(2,1)S(1)}, bf16[128,292]{0,1:T(8,128)(2,1)S(1)}, u32[]{:S(2)}, u32[]{:S(2)}) collective-permute-start(bf16[128,292]{0,1:T(8,128)(2,1)S(1)} %pad_maximum_fusion.8), channel_id=1, source_target_pairs={{0,2},{2,0},{1,3},{3,1},{4,6},{6,4},{5,7},{7,5},{8,10},{10,8},{9,1... | collective-permute-start | bytes 224264 | tf_op jit(solution)/shard_map/ppermute | solution.py:209
  68.4 5.1 %collective-permute-start.18 = (f32[1216,128]{1,0:T(8,128)S(1)}, f32[1216,128]{1,0:T(8,128)S(1)}, u32[]{:S(2)}, u32[]{:S(2)}) collective-permute-start(f32[1216,128]{1,0:T(8,128)S(1)} %bitcast.337), channel_id=1, source_target_pairs={{0,1},{1,0},{2,3},{3,2},{4,5},{5,4},{6,7},{7,6},{8,9},{9,8},{10,11... | collective-permute-start | bytes 1867784 | tf_op jit(solution)/shard_map/ppermute | solution.py:76

commit v23 on v19

--- a/solution.py
+++ b/solution.py
@@ -190,12 +190,19 @@
     outgoing = []
     for shift in range(1, chan_count):
         kernel_t = jnp.swapaxes(kernel_cols[shift], 2, 3)
-        outgoing.append(conv_taps(kernel_t, grad_pad, row_count, column_count, True).astype(jnp.bfloat16))
+        half = own_channels // 2 if own_channels % 32 == 0 else own_channels
+        outgoing.append(
+            [
+                conv_taps(kernel_t[:, :, lo : lo + half], grad_pad, row_count, column_count, True).astype(jnp.bfloat16)
+                for lo in range(0, own_channels, half)
+            ]
+        )
     grad_pad, outgoing = lax.optimization_barrier((grad_pad, outgoing))
     received = []
     for shift in range(1, chan_count):
         pairs = [(i, (i + shift) % chan_count) for i in range(chan_count)]
-        received.append(lax.ppermute(outgoing[shift - 1], "chan", pairs))
+        pieces = [lax.ppermute(piece, "chan", pairs) for piece in outgoing[shift - 1]]
+        received.append(jnp.concatenate(pieces, axis=0))
     own_part = conv_taps(jnp.swapaxes(kernel_cols[0], 2, 3), grad_pad, row_count, column_count, True)
     own_part, weight_grad, bias_grad = lax.optimization_barrier((own_part, weight_grad, bias_grad))
     for piece in received:

time: 70.1 us -> 87.5 us (1.25); the launches traced: 69.8 us -> 86.2 us
  matrix products: 15.5 us -> 31.8 us
    dot_general x36 -> x45, matrix products: 12.7 us -> 29 us  [conv_taps(): jnp.dot(kernel[tap_row, tap_col], window, preferred_element_type=jnp.floa...]
    ppermute x1 -> x2, starting transfers between devices: 1.56 us -> 2.09 us  [local(): lax.ppermute(piece, 'chan', pairs)]
    ppermute x1 -> x2, waiting for transfers between devices: 5.4 us -> 4.89 us  [local(): lax.ppermute(piece, 'chan', pairs)]
    unnamed x12 -> x14, local copies, waits for them, and re-layouts: 3.51 us -> 3.52 us
  transfers between devices with their start and end apart: 17 -> 18, of which waited for: 10 -> 11; matrix products, arithmetic and copies ran while one was open for 25% -> 39% of each run, Pallas kernels for 0% -> 0%
where the time goes in v23:
time: 87.5 us; the launch traced here: 86.2 us
  matrix products  31.8 us (36%)
  starting transfers between devices  18.4 us (21%)
  waiting for transfers between devices  16.4 us (19%)
  local copies, waits for them, and re-layouts  10.3 us (12%)
  other arithmetic  7.66 us (9%)
  between operations  1.52 us (2%)
    dot_general x45, matrix products, conv_taps(): jnp.dot(kernel[tap_row, tap_col], window, preferred_element_type=jnp.floa...  29 us
    ppermute x3, waiting for transfers between devices, sum_start(): moved = lax.ppermute(piece, 'lon', pairs)  5.2 us
    ppermute x3, starting transfers between devices, sum_start(): moved = lax.ppermute(piece, 'lon', pairs)  4.99 us
    ppermute x2, waiting for transfers between devices, local(): lax.ppermute(piece, 'chan', pairs)  4.89 us
    slice x4, local copies, waits for them, and re-layouts, window_of(): field[:, first_row:first_row + row_count, first_col:first_col + column_co...  3.74 us
    unnamed x14, local copies, waits for them, and re-layouts  3.52 us
    ppermute x1, starting transfers between devices, local(): raw_blocks.append(lax.ppermute(inputs, 'chan', pairs))  3 us
    dot_general x9, matrix products, local(): lax.dot_general(grad_pre, window, (((1,), (1,)), ((), ())), preferred_ele...  2.85 us
  transfers between devices with their start and end apart: 18, of which 11 were waited for; matrix products, arithmetic and copies ran while one was open for 39% of the time, Pallas kernels for 0%

profile of v23, /device:TPU:0, one launch (start us, length us, event | category | flops | bytes accessed | tf_op | source)
XLA Modules:
  0.0 86.2 jit_solution(3560815992246859617)
XLA Ops:
  0.6 1.5 %copy.12 = bf16[128,16,128]{0,2,1:T(8,128)(2,1)S(1)} copy(bf16[128,16,128]{2,1,0:T(8,128)(2,1)} %param.4) | data formatting | bytes 1048576 | tf_op args[0]
  2.2 3.0 %collective-permute-start.5 = (bf16[128,16,128]{0,2,1:T(8,128)(2,1)S(1)}, bf16[128,16,128]{0,2,1:T(8,128)(2,1)S(1)}, u32[]{:S(2)}, u32[]{:S(2)}) collective-permute-start(bf16[128,16,128]{0,2,1:T(8,128)(2,1)S(1)} %copy.12), channel_id=1, source_target_pairs={{0,2},{2,0},{1,3},{3,1},{4,6},{6,4},{5,7},{7,5},{8,10},{10,8},{9,1... | collective-permute-start | bytes 1572872 | tf_op jit(solution)/shard_map/ppermute | solution.py:142
  5.2 1.6 %collective-permute-start = (bf16[128,16,1]{0,2,1:T(2,128)(2,1)S(1)}, bf16[128,16,1]{0,2,1:T(2,128)(2,1)S(1)}, u32[]{:S(2)}, u32[]{:S(2)}) collective-permute-start(bf16[128,16,1]{0,2,1:T(2,128)(2,1)S(1)} %get-tuple-element.77), channel_id=1, source_target_pairs={{0,4},{4,8},{8,12},{12,0},{1,5},{5,9},{9,13},{13,1},{2,6},{6,10},{... | collective-permute-start | bytes 12296 | tf_op jit(solution)/shard_map/ppermute | solution.py:14
  6.8 2.2 %collective-permute-start.1 = (bf16[128,16,1]{0,2,1:T(2,128)(2,1)S(1)}, bf16[128,16,1]{0,2,1:T(2,128)(2,1)S(1)}, u32[]{:S(2)}, u32[]{:S(2)}) collective-permute-start(bf16[128,16,1]{0,2,1:T(2,128)(2,1)S(1)} %get-tuple-element.78), channel_id=1, source_target_pairs={{4,0},{8,4},{12,8},{0,12},{5,1},{9,5},{13,9},{1,13},{6,2},{10,6},{... | collective-permute-start | bytes 12296 | tf_op jit(solution)/shard_map/ppermute | solution.py:15
  9.2 1.5 %collective-permute-done = bf16[128,16,1]{0,2,1:T(2,128)(2,1)S(1)} collective-permute-done((bf16[128,16,1]{0,2,1:T(2,128)(2,1)S(1)}, bf16[128,16,1]{0,2,1:T(2,128)(2,1)S(1)}, u32[]{:S(2)}, u32[]{:S(2)}) %collective-permute-start) | collective-permute-done | bytes 4128 | tf_op jit(solution)/shard_map/ppermute | solution.py:14
  16.7 2.0 %collective-permute-done.4 = bf16[128,292]{0,1:T(8,128)(2,1)S(1)} collective-permute-done((bf16[128,292]{0,1:T(8,128)(2,1)S(1)}, bf16[128,292]{0,1:T(8,128)(2,1)S(1)}, u32[]{:S(2)}, u32[]{:S(2)}) %collective-permute-start.4) | collective-permute-done | bytes 74784 | tf_op jit(solution)/shard_map/ppermute | solution.py:148
  19.9 2.5 %fusion.15 = (bf16[256,16,128]{0,2,1:T(8,128)(2,1)S(1)}, bf16[256,16,128]{0,2,1:T(8,128)(2,1)S(1)}, bf16[256,16,128]{0,2,1:T(8,128)(2,1)S(1)}, bf16[256,16,128]{...) fusion(bf16[128,18,130]{0,2,1:T(8,128)(2,1)S(1)} %maximum_selec, ...), kind=kLoop, calls=%fused_computation.90 | loop fusion | flops 18874368 | bytes 10635264 | tf_op jit(solution)/shard_map/concatenate | solution.py:164
  32.4 1.1 %bitcast_add_fusion = f32[1216,128]{1,0:T(8,128)S(1)} fusion(f32[1216,128]{1,0:T(8,128)} %collective-permute-done.6, f32[2,1216,128]{2,1,0:T(8,128)S(1)} %bitcast.343, s32[]{:T(128)S(6)} %select_n.98), kind=kLoop, calls=%fused_computation.103 | loop fusion | flops 155648 | bytes 1867780 | tf_op jit(solution)/shard_map/add | solution.py:64
  33.6 1.9 %collective-permute-start.7 = (bf16[320,128]{1,0:T(8,128)(2,1)S(1)}, bf16[320,128]{1,0:T(8,128)(2,1)S(1)}, u32[]{:S(2)}, u32[]{:S(2)}) collective-permute-start(bf16[320,128]{1,0:T(8,128)(2,1)S(1)} %pad_maximum_fusion.3), channel_id=1, source_target_pairs={{0,4},{4,8},{8,12},{12,0},{1,5},{5,9},{9,13},{13,1},{2,6},{6,10},{... | collective-permute-start | bytes 245768 | tf_op jit(solution)/shard_map/ppermute | solution.py:104
  35.5 2.3 %collective-permute-start.8 = (bf16[320,128]{1,0:T(8,128)(2,1)S(1)}, bf16[320,128]{1,0:T(8,128)(2,1)S(1)}, u32[]{:S(2)}, u32[]{:S(2)}) collective-permute-start(bf16[320,128]{1,0:T(8,128)(2,1)S(1)} %pad_maximum_fusion.4), channel_id=1, source_target_pairs={{0,12},{4,0},{8,4},{12,8},{1,13},{5,1},{9,5},{13,9},{2,14},{6,2},{... | collective-permute-start | bytes 245768 | tf_op jit(solution)/shard_map/ppermute | solution.py:104
  39.2 1.4 %collective-permute-done.7 = bf16[320,128]{1,0:T(8,128)(2,1)S(1)} collective-permute-done((bf16[320,128]{1,0:T(8,128)(2,1)S(1)}, bf16[320,128]{1,0:T(8,128)(2,1)S(1)}, u32[]{:S(2)}, u32[]{:S(2)}) %collective-permute-start.7) | collective-permute-done | bytes 81952 | tf_op jit(solution)/shard_map/ppermute | solution.py:104
  42.3 3.1 %collective-permute-done.11 = bf16[304,128]{1,0:T(8,128)(2,1)S(1)} collective-permute-done((bf16[304,128]{1,0:T(8,128)(2,1)S(1)}, bf16[304,128]{1,0:T(8,128)(2,1)S(1)}, u32[]{:S(2)}, u32[]{:S(2)}) %collective-permute-start.11) | collective-permute-done | bytes 77856 | tf_op jit(solution)/shard_map/ppermute | solution.py:104
  45.4 2.1 %collective-permute-start.12 = (bf16[304,128]{1,0:T(8,128)(2,1)S(1)}, bf16[304,128]{1,0:T(8,128)(2,1)S(1)}, u32[]{:S(2)}, u32[]{:S(2)}) collective-permute-start(bf16[304,128]{1,0:T(8,128)(2,1)S(1)} %get-tuple-element.17), channel_id=1, source_target_pairs={{0,12},{4,0},{8,4},{12,8},{1,13},{5,1},{9,5},{13,9},{2,14},{6,2},{... | collective-permute-start | bytes 233480 | tf_op jit(solution)/shard_map/ppermute | solution.py:76
  50.1 1.2 %convolution_add_fusion.31 = f32[64,2048]{1,0:T(8,128)S(1)} fusion(f32[64,2048]{1,0:T(8,128)S(1)} %fusion.28, bf16[128,2048]{0,1:T(8,128)(2,1)S(1)} %bitcast.358, bf16[3,3,128,128]{2,3,1,0:T(8,128)(2,1)} %copy-done), kind=kOutput, calls=%fused_computation.55 | convolution fusion | flops 33685504 | bytes 1605632 | tf_op jit(solution)/shard_map/dot_general | solution.py:50
  52.4 1.2 %convolution_add_fusion.30 = f32[64,2048]{1,0:T(8,128)S(1)} fusion(f32[64,2048]{1,0:T(8,128)S(1)} %convolution_add_fusion.31, bf16[128,2048]{0,1:T(8,128)(2,1)S(1)} %bitcast.356, bf16[3,3,128,128]{2,3,1,0:T(8,128)(2,1)} %copy-done), kind=kOutput, calls=%fused_computation.54 | convolution fusion | flops 33685504 | bytes 1605632 | tf_op jit(solution)/shard_map/dot_general | solution.py:50
  53.5 1.1 %convolution_add_fusion.38 = f32[64,2048]{1,0:T(8,128)S(1)} fusion(f32[64,2048]{1,0:T(8,128)S(1)} %convolution_add_fusion.39, bf16[128,2048]{0,1:T(8,128)(2,1)S(1)} %bitcast.357, bf16[3,3,128,128]{2,3,1,0:T(8,128)(2,1)} %copy-done), kind=kOutput, calls=%fused_computation.62 | convolution fusion | flops 33685504 | bytes 1605632 | tf_op jit(solution)/shard_map/dot_general | solution.py:50
  54.6 1.2 %convolution_add_fusion.29 = f32[64,2048]{1,0:T(8,128)S(1)} fusion(f32[64,2048]{1,0:T(8,128)S(1)} %convolution_add_fusion.30, bf16[128,2048]{0,1:T(8,128)(2,1)S(1)} %bitcast.354, bf16[3,3,128,128]{2,3,1,0:T(8,128)(2,1)} %copy-done), kind=kOutput, calls=%fused_computation.53 | convolution fusion | flops 33685504 | bytes 1605632 | tf_op jit(solution)/shard_map/dot_general | solution.py:50
  55.8 1.1 %convolution_add_fusion.37 = f32[64,2048]{1,0:T(8,128)S(1)} fusion(f32[64,2048]{1,0:T(8,128)S(1)} %convolution_add_fusion.38, bf16[128,2048]{0,1:T(8,128)(2,1)S(1)} %bitcast.355, bf16[3,3,128,128]{2,3,1,0:T(8,128)(2,1)} %copy-done), kind=kOutput, calls=%fused_computation.61 | convolution fusion | flops 33685504 | bytes 1605632 | tf_op jit(solution)/shard_map/dot_general | solution.py:50
  56.9 1.2 %convolution_add_fusion.28 = f32[64,2048]{1,0:T(8,128)S(1)} fusion(f32[64,2048]{1,0:T(8,128)S(1)} %convolution_add_fusion.29, bf16[128,2048]{0,1:T(8,128)(2,1)S(1)} %bitcast.352, bf16[3,3,128,128]{2,3,1,0:T(8,128)(2,1)} %copy-done), kind=kOutput, calls=%fused_computation.52 | convolution fusion | flops 33685504 | bytes 1605632 | tf_op jit(solution)/shard_map/dot_general | solution.py:50
  58.0 1.1 %convolution_add_fusion.36 = f32[64,2048]{1,0:T(8,128)S(1)} fusion(f32[64,2048]{1,0:T(8,128)S(1)} %convolution_add_fusion.37, bf16[128,2048]{0,1:T(8,128)(2,1)S(1)} %bitcast.353, bf16[3,3,128,128]{2,3,1,0:T(8,128)(2,1)} %copy-done), kind=kOutput, calls=%fused_computation.60 | convolution fusion | flops 33685504 | bytes 1605632 | tf_op jit(solution)/shard_map/dot_general | solution.py:50
  59.1 1.2 %convolution_add_fusion.27 = f32[64,2048]{1,0:T(8,128)S(1)} fusion(f32[64,2048]{1,0:T(8,128)S(1)} %convolution_add_fusion.28, bf16[128,2048]{0,1:T(8,128)(2,1)S(1)} %bitcast.350, bf16[3,3,128,128]{2,3,1,0:T(8,128)(2,1)} %copy-done), kind=kOutput, calls=%fused_computation.51 | convolution fusion | flops 33685504 | bytes 1605632 | tf_op jit(solution)/shard_map/dot_general | solution.py:50
  60.3 1.1 %convolution_add_fusion.35 = f32[64,2048]{1,0:T(8,128)S(1)} fusion(f32[64,2048]{1,0:T(8,128)S(1)} %convolution_add_fusion.36, bf16[128,2048]{0,1:T(8,128)(2,1)S(1)} %bitcast.351, bf16[3,3,128,128]{2,3,1,0:T(8,128)(2,1)} %copy-done), kind=kOutput, calls=%fused_computation.59 | convolution fusion | flops 33685504 | bytes 1605632 | tf_op jit(solution)/shard_map/dot_general | solution.py:50
  61.3 1.2 %convolution_add_fusion.26 = f32[64,2048]{1,0:T(8,128)S(1)} fusion(f32[64,2048]{1,0:T(8,128)S(1)} %convolution_add_fusion.27, bf16[128,2048]{0,1:T(8,128)(2,1)S(1)} %bitcast.348, bf16[3,3,128,128]{2,3,1,0:T(8,128)(2,1)} %copy-done), kind=kOutput, calls=%fused_computation.50 | convolution fusion | flops 33685504 | bytes 1605632 | tf_op jit(solution)/shard_map/dot_general | solution.py:50
  62.5 1.1 %convolution_add_fusion.34 = f32[64,2048]{1,0:T(8,128)S(1)} fusion(f32[64,2048]{1,0:T(8,128)S(1)} %convolution_add_fusion.35, bf16[128,2048]{0,1:T(8,128)(2,1)S(1)} %bitcast.349, bf16[3,3,128,128]{2,3,1,0:T(8,128)(2,1)} %copy-done), kind=kOutput, calls=%fused_computation.58 | convolution fusion | flops 33685504 | bytes 1605632 | tf_op jit(solution)/shard_map/dot_general | solution.py:50
  63.6 1.2 %convolution_add_fusion.25 = f32[64,2048]{1,0:T(8,128)S(1)} fusion(f32[64,2048]{1,0:T(8,128)S(1)} %convolution_add_fusion.26, bf16[128,2048]{0,1:T(8,128)(2,1)S(1)} %bitcast.346, bf16[3,3,128,128]{2,3,1,0:T(8,128)(2,1)} %copy-done), kind=kOutput, calls=%fused_computation.49 | convolution fusion | flops 33685504 | bytes 1605632 | tf_op jit(solution)/shard_map/dot_general | solution.py:50
  64.7 1.1 %convolution_add_fusion.33 = f32[64,2048]{1,0:T(8,128)S(1)} fusion(f32[64,2048]{1,0:T(8,128)S(1)} %convolution_add_fusion.34, bf16[128,2048]{0,1:T(8,128)(2,1)S(1)} %bitcast.347, bf16[3,3,128,128]{2,3,1,0:T(8,128)(2,1)} %copy-done), kind=kOutput, calls=%fused_computation.57 | convolution fusion | flops 33685504 | bytes 1605632 | tf_op jit(solution)/shard_map/dot_general | solution.py:50
  65.8 1.9 %fusion.3 = bf16[64,2048]{1,0:T(8,128)(2,1)} fusion(f32[64,2048]{1,0:T(8,128)S(1)} %convolution_add_fusion.25, bf16[128,2048]{0,1:T(8,128)(2,1)S(1)} %bitcast.364, bf16[3,3,128,128]{2,3,1,0:T(8,128)(2,1)} %copy-done), kind=kOutput, calls=%fused_computation.65 | convolution fusion | flops 33816576 | bytes 1343488 | tf_op jit(solution)/shard_map/dot_general | solution.py:50
  67.7 1.8 %fusion.2 = bf16[64,2048]{1,0:T(8,128)(2,1)} fusion(f32[64,2048]{1,0:T(8,128)S(1)} %convolution_add_fusion.33, bf16[128,2048]{0,1:T(8,128)(2,1)S(1)} %bitcast.365, bf16[3,3,128,128]{2,3,1,0:T(8,128)(2,1)} %copy-done), kind=kOutput, calls=%fused_computation.64 | convolution fusion | flops 33816576 | bytes 1343488 | tf_op jit(solution)/shard_map/dot_general | solution.py:50
  70.4 1.6 %collective-permute-start.16 = (bf16[64,2048]{1,0:T(8,128)(2,1)}, bf16[64,2048]{1,0:T(8,128)(2,1)}, u32[]{:S(2)}, u32[]{:S(2)}) collective-permute-start(bf16[64,2048]{1,0:T(8,128)(2,1)} %fusion.2), channel_id=1, source_target_pairs={{0,2},{2,0},{1,3},{3,1},{4,6},{6,4},{5,7},{7,5},{8,10},{10,8},{9,1... | collective-permute-start | bytes 786440 | tf_op jit(solution)/shard_map/ppermute | solution.py:204
  78.0 1.2 %fusion.7 = f32[3,3,128,256]{3,2,1,0:T(8,128)} fusion(s32[]{:T(128)S(6)} %select_n.114, f32[3,3,128,256]{3,2,1,0:T(8,128)S(1)} %reshape.249), kind=kLoop, calls=%fused_computation.72 | loop fusion | flops 294912 | bytes 2359300 | tf_op jit(solution)/shard_map/concatenate | solution.py:184
  80.1 4.1 %collective-permute-done.17 = bf16[64,2048]{1,0:T(8,128)(2,1)} collective-permute-done((bf16[64,2048]{1,0:T(8,128)(2,1)}, bf16[64,2048]{1,0:T(8,128)(2,1)}, u32[]{:S(2)}, u32[]{:S(2)}) %collective-permute-start.17) | collective-permute-done | bytes 262176 | tf_op jit(solution)/shard_map/ppermute | solution.py:204
  84.1 1.2 %fusion.22 = bf16[16,8,16,128]{3,1,2,0:T(8,128)(2,1)S(1)} fusion(f32[128,2048]{1,0:T(8,128)S(1)} %convolution_add_fusion, bf16[64,2048]{1,0:T(8,128)(2,1)} %collective-permute-done.17, bf16[64,2048]{1,0:T(8,128)(2,1)} %collective-permute-done.16), kind=kLoop, calls=%fused_computation.105 | loop fusion | flops 1572864 | bytes 2097152
  (128 shorter events, 32.2 us)
Async XLA Ops:
  0.6 8.4 %copy-start.2 = (bf16[128,16,128]{2,1,0:T(8,128)(2,1)S(1)}, bf16[128,16,128]{2,1,0:T(8,128)(2,1)}, u32[]{:S(2)}) copy-start(bf16[128,16,128]{2,1,0:T(8,128)(2,1)} %param.5) | copy-start | bytes 1572868
  2.2 16.6 %collective-permute-start.5 = (bf16[128,16,128]{0,2,1:T(8,128)(2,1)S(1)}, bf16[128,16,128]{0,2,1:T(8,128)(2,1)S(1)}, u32[]{:S(2)}, u32[]{:S(2)}) collective-permute-start(bf16[128,16,128]{0,2,1:T(8,128)(2,1)S(1)} %copy.12), channel_id=1, source_target_pairs={{0,2},{2,0},{1,3},{3,1},{4,6},{6,4},{5,7},{7,5},{8,10},{10,8},{9,1... | collective-permute-start | bytes 1572872 | tf_op jit(solution)/shard_map/ppermute | solution.py:142
  5.2 5.5 %collective-permute-start = (bf16[128,16,1]{0,2,1:T(2,128)(2,1)S(1)}, bf16[128,16,1]{0,2,1:T(2,128)(2,1)S(1)}, u32[]{:S(2)}, u32[]{:S(2)}) collective-permute-start(bf16[128,16,1]{0,2,1:T(2,128)(2,1)S(1)} %get-tuple-element.77), channel_id=1, source_target_pairs={{0,4},{4,8},{8,12},{12,0},{1,5},{5,9},{9,13},{13,1},{2,6},{6,10},{... | collective-permute-start | bytes 12296 | tf_op jit(solution)/shard_map/ppermute | solution.py:14
  6.8 3.9 %collective-permute-start.1 = (bf16[128,16,1]{0,2,1:T(2,128)(2,1)S(1)}, bf16[128,16,1]{0,2,1:T(2,128)(2,1)S(1)}, u32[]{:S(2)}, u32[]{:S(2)}) collective-permute-start(bf16[128,16,1]{0,2,1:T(2,128)(2,1)S(1)} %get-tuple-element.78), channel_id=1, source_target_pairs={{4,0},{8,4},{12,8},{0,12},{5,1},{9,5},{13,9},{1,13},{6,2},{10,6},{... | collective-permute-start | bytes 12296 | tf_op jit(solution)/shard_map/ppermute | solution.py:15
  10.7 1.3 %collective-permute-start.2 = (bf16[128,1,130]{0,2,1:T(8,128)(2,1)S(1)}, bf16[128,1,130]{0,2,1:T(8,128)(2,1)S(1)}, u32[]{:S(2)}, u32[]{:S(2)}) collective-permute-start(bf16[128,1,130]{0,2,1:T(8,128)(2,1)S(1)} %get-tuple-element.75), channel_id=1, source_target_pairs={{0,1},{1,0},{2,3},{3,2},{4,5},{5,4},{6,7},{7,6},{8,9},{9,8},{10,11... | collective-permute-start | bytes 99848 | tf_op jit(solution)/shard_map/ppermute | solution.py:14
  10.8 1.4 %collective-permute-start.3 = (bf16[128,1,130]{0,2,1:T(8,128)(2,1)S(1)}, bf16[128,1,130]{0,2,1:T(8,128)(2,1)S(1)}, u32[]{:S(2)}, u32[]{:S(2)}) collective-permute-start(bf16[128,1,130]{0,2,1:T(8,128)(2,1)S(1)} %get-tuple-element.76), channel_id=1, source_target_pairs={{1,0},{0,1},{3,2},{2,3},{5,4},{4,5},{7,6},{6,7},{9,8},{8,9},{11,10... | collective-permute-start | bytes 99848 | tf_op jit(solution)/shard_map/ppermute | solution.py:15
  12.5 1.5 %copy-start.1 = (bf16[3,3,128,256]{3,2,1,0:T(8,128)(2,1)S(1)}, bf16[3,3,128,256]{3,2,1,0:T(8,128)(2,1)}, u32[]{:S(2)}) copy-start(bf16[3,3,128,256]{3,2,1,0:T(8,128)(2,1)} %param.6) | copy-start | bytes 1769476
  13.5 5.2 %collective-permute-start.4 = (bf16[128,292]{0,1:T(8,128)(2,1)S(1)}, bf16[128,292]{0,1:T(8,128)(2,1)S(1)}, u32[]{:S(2)}, u32[]{:S(2)}) collective-permute-start(bf16[128,292]{0,1:T(8,128)(2,1)S(1)} %pad_maximum_fusion.5), channel_id=1, source_target_pairs={{0,2},{2,0},{1,3},{3,1},{4,6},{6,4},{5,7},{7,5},{8,10},{10,8},{9,1... | collective-permute-start | bytes 224264 | tf_op jit(solution)/shard_map/ppermute | solution.py:148
  24.6 0.7 copy-start.3
  30.2 2.2 %collective-permute-start.6 = (f32[1216,128]{1,0:T(8,128)S(1)}, f32[1216,128]{1,0:T(8,128)}, u32[]{:S(2)}, u32[]{:S(2)}) collective-permute-start(f32[1216,128]{1,0:T(8,128)S(1)} %dynamic-slice_bitcast_fusion), channel_id=1, source_target_pairs={{0,1},{1,0},{2,3},{3,2},{4,5},{5,4},{6,7},{7,6},{8,9},{9,8},{10,11... | collective-permute-start | bytes 1867784 | tf_op jit(solution)/shard_map/ppermute | solution.py:64
  33.6 7.0 %collective-permute-start.7 = (bf16[320,128]{1,0:T(8,128)(2,1)S(1)}, bf16[320,128]{1,0:T(8,128)(2,1)S(1)}, u32[]{:S(2)}, u32[]{:S(2)}) collective-permute-start(bf16[320,128]{1,0:T(8,128)(2,1)S(1)} %pad_maximum_fusion.3), channel_id=1, source_target_pairs={{0,4},{4,8},{8,12},{12,0},{1,5},{5,9},{9,13},{13,1},{2,6},{6,10},{... | collective-permute-start | bytes 245768 | tf_op jit(solution)/shard_map/ppermute | solution.py:104
  35.5 6.0 %collective-permute-start.8 = (bf16[320,128]{1,0:T(8,128)(2,1)S(1)}, bf16[320,128]{1,0:T(8,128)(2,1)S(1)}, u32[]{:S(2)}, u32[]{:S(2)}) collective-permute-start(bf16[320,128]{1,0:T(8,128)(2,1)S(1)} %pad_maximum_fusion.4), channel_id=1, source_target_pairs={{0,12},{4,0},{8,4},{12,8},{1,13},{5,1},{9,5},{13,9},{2,14},{6,2},{... | collective-permute-start | bytes 245768 | tf_op jit(solution)/shard_map/ppermute | solution.py:104
  37.9 11.9 %copy-start = (bf16[3,3,128,128]{2,3,1,0:T(8,128)(2,1)}, bf16[3,3,128,128]{2,3,1,0:T(8,128)(2,1)S(1)}, u32[]{:S(2)}) copy-start(bf16[3,3,128,128]{2,3,1,0:T(8,128)(2,1)S(1)} %get-tuple-element.72) | copy-start | bytes 884740
  38.4 7.0 %collective-permute-start.11 = (bf16[304,128]{1,0:T(8,128)(2,1)S(1)}, bf16[304,128]{1,0:T(8,128)(2,1)S(1)}, u32[]{:S(2)}, u32[]{:S(2)}) collective-permute-start(bf16[304,128]{1,0:T(8,128)(2,1)S(1)} %get-tuple-element.68), channel_id=1, source_target_pairs={{0,8},{4,12},{8,0},{12,4},{1,9},{5,13},{9,1},{13,5},{2,10},{6,14},... | collective-permute-start | bytes 233480 | tf_op jit(solution)/shard_map/ppermute | solution.py:104
  41.7 6.5 %collective-permute-start.10 = (bf16[128,1,130]{0,2,1:T(8,128)(2,1)S(1)}, bf16[128,1,130]{0,2,1:T(8,128)(2,1)S(1)}, u32[]{:S(2)}, u32[]{:S(2)}) collective-permute-start(bf16[128,1,130]{0,2,1:T(8,128)(2,1)S(1)} %get-tuple-element.74), channel_id=1, source_target_pairs={{1,0},{0,1},{3,2},{2,3},{5,4},{4,5},{7,6},{6,7},{9,8},{8,9},{11,10... | collective-permute-start | bytes 99848 | tf_op jit(solution)/shard_map/ppermute | solution.py:15
  41.8 6.4 %collective-permute-start.9 = (bf16[128,1,130]{0,2,1:T(8,128)(2,1)S(1)}, bf16[128,1,130]{0,2,1:T(8,128)(2,1)S(1)}, u32[]{:S(2)}, u32[]{:S(2)}) collective-permute-start(bf16[128,1,130]{0,2,1:T(8,128)(2,1)S(1)} %get-tuple-element.73), channel_id=1, source_target_pairs={{0,1},{1,0},{2,3},{3,2},{4,5},{5,4},{6,7},{7,6},{8,9},{9,8},{10,11... | collective-permute-start | bytes 99848 | tf_op jit(solution)/shard_map/ppermute | solution.py:14
  45.4 29.1 %collective-permute-start.12 = (bf16[304,128]{1,0:T(8,128)(2,1)S(1)}, bf16[304,128]{1,0:T(8,128)(2,1)S(1)}, u32[]{:S(2)}, u32[]{:S(2)}) collective-permute-start(bf16[304,128]{1,0:T(8,128)(2,1)S(1)} %get-tuple-element.17), channel_id=1, source_target_pairs={{0,12},{4,0},{8,4},{12,8},{1,13},{5,1},{9,5},{13,9},{2,14},{6,2},{... | collective-permute-start | bytes 233480 | tf_op jit(solution)/shard_map/ppermute | solution.py:76
  47.5 27.0 %collective-permute-start.13 = (bf16[304,128]{1,0:T(8,128)(2,1)S(1)}, bf16[304,128]{1,0:T(8,128)(2,1)S(1)}, u32[]{:S(2)}, u32[]{:S(2)}) collective-permute-start(bf16[304,128]{1,0:T(8,128)(2,1)S(1)} %get-tuple-element.17), channel_id=1, source_target_pairs={{0,8},{4,12},{8,0},{12,4},{1,9},{5,13},{9,1},{13,5},{2,10},{6,14},... | collective-permute-start | bytes 233480 | tf_op jit(solution)/shard_map/ppermute | solution.py:76
  47.5 27.0 %collective-permute-start.14 = (bf16[304,128]{1,0:T(8,128)(2,1)S(1)}, bf16[304,128]{1,0:T(8,128)(2,1)S(1)}, u32[]{:S(2)}, u32[]{:S(2)}) collective-permute-start(bf16[304,128]{1,0:T(8,128)(2,1)S(1)} %get-tuple-element.17), channel_id=1, source_target_pairs={{0,4},{4,8},{8,12},{12,0},{1,5},{5,9},{9,13},{13,1},{2,6},{6,10},{... | collective-permute-start | bytes 233480 | tf_op jit(solution)/shard_map/ppermute | solution.py:76
  70.4 9.6 %collective-permute-start.16 = (bf16[64,2048]{1,0:T(8,128)(2,1)}, bf16[64,2048]{1,0:T(8,128)(2,1)}, u32[]{:S(2)}, u32[]{:S(2)}) collective-permute-start(bf16[64,2048]{1,0:T(8,128)(2,1)} %fusion.2), channel_id=1, source_target_pairs={{0,2},{2,0},{1,3},{3,1},{4,6},{6,4},{5,7},{7,5},{8,10},{10,8},{9,1... | collective-permute-start | bytes 786440 | tf_op jit(solution)/shard_map/ppermute | solution.py:204
  72.0 12.1 %collective-permute-start.17 = (bf16[64,2048]{1,0:T(8,128)(2,1)}, bf16[64,2048]{1,0:T(8,128)(2,1)}, u32[]{:S(2)}, u32[]{:S(2)}) collective-permute-start(bf16[64,2048]{1,0:T(8,128)(2,1)} %fusion.3), channel_id=1, source_target_pairs={{0,2},{2,0},{1,3},{3,1},{4,6},{6,4},{5,7},{7,5},{8,10},{10,8},{9,1... | collective-permute-start | bytes 786440 | tf_op jit(solution)/shard_map/ppermute | solution.py:204
  74.7 2.1 %collective-permute-start.15 = (f32[1216,128]{1,0:T(8,128)S(1)}, f32[1216,128]{1,0:T(8,128)S(1)}, u32[]{:S(2)}, u32[]{:S(2)}) collective-permute-start(f32[1216,128]{1,0:T(8,128)S(1)} %bitcast.375), channel_id=1, source_target_pairs={{0,1},{1,0},{2,3},{3,2},{4,5},{5,4},{6,7},{7,6},{8,9},{9,8},{10,11... | collective-permute-start | bytes 1867784 | tf_op jit(solution)/shard_map/ppermute | solution.py:76

commit v24 on v20

--- a/solution.py
+++ b/solution.py
@@ -184,7 +184,13 @@
     for shift in range(1, chan_count):
         kernel_t = jnp.swapaxes(kernel_cols[shift], 2, 3)
         outgoing.append(conv_taps(kernel_t, grad_pad, row_count, column_count, True).astype(jnp.bfloat16))
-    grad_pad, outgoing, scattered = lax.optimization_barrier((grad_pad, outgoing, scattered))
+    grad_pad, outgoing = lax.optimization_barrier((grad_pad, outgoing))
+    received = []
+    for shift in range(1, chan_count):
+        pairs = [(i, (i + shift) % chan_count) for i in range(chan_count)]
+        received.append(lax.ppermute(outgoing[shift - 1], "chan", pairs))
+    own_part = conv_taps(jnp.swapaxes(kernel_cols[0], 2, 3), grad_pad, row_count, column_count, True)
+    own_part, scattered = lax.optimization_barrier((own_part, scattered))
     flat = sum_finish(scattered, flat.size, jnp.bfloat16)
     weight_local = flat[: weight_part.size].reshape(weight_part.shape)
     bias_grad = flat[weight_part.size :]
@@ -192,11 +198,6 @@
     weight_grad = lax.dynamic_slice_in_dim(
         doubled, (chan_count - chan_index) % chan_count * own_channels, chan_count * own_channels, axis=3
     )
-    received = []
-    for shift in range(1, chan_count):
-        pairs = [(i, (i + shift) % chan_count) for i in range(chan_count)]
-        received.append(lax.ppermute(outgoing[shift - 1], "chan", pairs))
-    own_part = conv_taps(jnp.swapaxes(kernel_cols[0], 2, 3), grad_pad, row_count, column_count, True)
     own_part, weight_grad, bias_grad = lax.optimization_barrier((own_part, weight_grad, bias_grad))
     for piece in received:
         own_part = own_part + piece.astype(jnp.float32)

time: 70.1 us -> 81.3 us (1.16)
  waiting for transfers between devices: 17 us -> 28.3 us
    ppermute x1, waiting for transfers between devices: 2.9 us -> 10.3 us  [local(): received.append(lax.ppermute(outgoing[shift - 1], 'chan', pairs))]
    ppermute x4, waiting for transfers between devices: 3.57 us -> 7.51 us  [direct_all_gather(): pieces.append(lax.ppermute(sent, axis, pairs).astype(jnp.float32))]
  transfers between devices with their start and end apart: 17 -> 17, of which waited for: 11 -> 12; matrix products, arithmetic and copies ran while one was open for 18% -> 11% of each run, Pallas kernels for 0% -> 0%
where the time goes in v24:
time: 81.3 us; the launch traced here: 81.1 us
  waiting for transfers between devices  28.3 us (35%)
  starting transfers between devices  17.9 us (22%)
  matrix products  15.5 us (19%)
  local copies, waits for them, and re-layouts  10.3 us (13%)
  other arithmetic  7.67 us (9%)
  between operations  1.41 us (2%)
    dot_general x36, matrix products, conv_taps(): jnp.dot(kernel[tap_row, tap_col], window, preferred_element_type=jnp.floa...  12.7 us
    ppermute x1, waiting for transfers between devices, local(): received.append(lax.ppermute(outgoing[shift - 1], 'chan', pairs))  10.3 us
    ppermute x4, waiting for transfers between devices, direct_all_gather(): pieces.append(lax.ppermute(sent, axis, pairs).astype(jnp.float32))  7.51 us
    ppermute x3, waiting for transfers between devices, sum_start(): moved = lax.ppermute(piece, 'lon', pairs)  5.21 us
    ppermute x3, starting transfers between devices, sum_start(): moved = lax.ppermute(piece, 'lon', pairs)  4.99 us
    slice x4, local copies, waits for them, and re-layouts, window_of(): field[:, first_row:first_row + row_count, first_col:first_col + column_co...  3.71 us
    unnamed x12, local copies, waits for them, and re-layouts  3.51 us
    ppermute x1, starting transfers between devices, local(): raw_blocks.append(lax.ppermute(inputs, 'chan', pairs))  3 us
  transfers between devices with their start and end apart: 17, of which 12 were waited for; matrix products, arithmetic and copies ran while one was open for 11% of the time, Pallas kernels for 0%

profile of v24, /device:TPU:0, one launch (start us, length us, event | category | flops | bytes accessed | tf_op | source)
XLA Modules:
  0.0 81.1 jit_solution(3716201041087419181)
XLA Ops:
  0.6 1.5 %copy.12 = bf16[128,16,128]{0,2,1:T(8,128)(2,1)S(1)} copy(bf16[128,16,128]{2,1,0:T(8,128)(2,1)} %param.4) | data formatting | bytes 1048576 | tf_op args[0]
  2.2 3.0 %collective-permute-start.5 = (bf16[128,16,128]{0,2,1:T(8,128)(2,1)S(1)}, bf16[128,16,128]{0,2,1:T(8,128)(2,1)S(1)}, u32[]{:S(2)}, u32[]{:S(2)}) collective-permute-start(bf16[128,16,128]{0,2,1:T(8,128)(2,1)S(1)} %copy.12), channel_id=1, source_target_pairs={{0,2},{2,0},{1,3},{3,1},{4,6},{6,4},{5,7},{7,5},{8,10},{10,8},{9,1... | collective-permute-start | bytes 1572872 | tf_op jit(solution)/shard_map/ppermute | solution.py:142
  5.2 1.6 %collective-permute-start = (bf16[128,16,1]{0,2,1:T(2,128)(2,1)S(1)}, bf16[128,16,1]{0,2,1:T(2,128)(2,1)S(1)}, u32[]{:S(2)}, u32[]{:S(2)}) collective-permute-start(bf16[128,16,1]{0,2,1:T(2,128)(2,1)S(1)} %get-tuple-element.77), channel_id=1, source_target_pairs={{0,4},{4,8},{8,12},{12,0},{1,5},{5,9},{9,13},{13,1},{2,6},{6,10},{... | collective-permute-start | bytes 12296 | tf_op jit(solution)/shard_map/ppermute | solution.py:14
  6.8 2.2 %collective-permute-start.1 = (bf16[128,16,1]{0,2,1:T(2,128)(2,1)S(1)}, bf16[128,16,1]{0,2,1:T(2,128)(2,1)S(1)}, u32[]{:S(2)}, u32[]{:S(2)}) collective-permute-start(bf16[128,16,1]{0,2,1:T(2,128)(2,1)S(1)} %get-tuple-element.78), channel_id=1, source_target_pairs={{4,0},{8,4},{12,8},{0,12},{5,1},{9,5},{13,9},{1,13},{6,2},{10,6},{... | collective-permute-start | bytes 12296 | tf_op jit(solution)/shard_map/ppermute | solution.py:15
  9.2 1.5 %collective-permute-done = bf16[128,16,1]{0,2,1:T(2,128)(2,1)S(1)} collective-permute-done((bf16[128,16,1]{0,2,1:T(2,128)(2,1)S(1)}, bf16[128,16,1]{0,2,1:T(2,128)(2,1)S(1)}, u32[]{:S(2)}, u32[]{:S(2)}) %collective-permute-start) | collective-permute-done | bytes 4128 | tf_op jit(solution)/shard_map/ppermute | solution.py:14
  11.3 0.7 collective-permute-done.2
  12.5 0.9 %fusion.53 = (bf16[128,16,128]{0,2,1:T(8,128)(2,1)S(1)}, bf16[128,16,128]{0,2,1:T(8,128)(2,1)S(1)}, bf16[128,16,128]{0,2,1:T(8,128)(2,1)S(1)}, bf16[128,16,128]{...) fusion(bf16[128,18,130]{0,2,1:T(8,128)(2,1)S(1)} %maximum_selec, ...), kind=kLoop, calls=%fused_computation.202 | loop fusion | bytes 9437184 | tf_op jit(solution)/shard_map/slice | solution.py:37
  16.7 2.0 %collective-permute-done.4 = bf16[128,292]{0,1:T(8,128)(2,1)S(1)} collective-permute-done((bf16[128,292]{0,1:T(8,128)(2,1)S(1)}, bf16[128,292]{0,1:T(8,128)(2,1)S(1)}, u32[]{:S(2)}, u32[]{:S(2)}) %collective-permute-start.4) | collective-permute-done | bytes 74784 | tf_op jit(solution)/shard_map/ppermute | solution.py:148
  19.0 1.0 %fusion.51 = (bf16[128,16,128]{0,2,1:T(8,128)(2,1)S(1)}, bf16[128,16,128]{0,2,1:T(8,128)(2,1)S(1)}, bf16[128,16,128]{0,2,1:T(8,128)(2,1)S(1)}, bf16[128,16,128]{...) fusion(bf16[128,18,130]{0,2,1:T(8,128)(2,1)S(1)} %pad_maximum_f, ...), kind=kLoop, calls=%fused_computation.200 | loop fusion | bytes 9437184 | tf_op jit(solution)/shard_map/slice | solution.py:37
  19.9 2.5 %fusion.14 = (bf16[256,16,128]{0,2,1:T(8,128)(2,1)S(1)}, bf16[256,16,128]{0,2,1:T(8,128)(2,1)S(1)}, bf16[256,16,128]{0,2,1:T(8,128)(2,1)S(1)}, bf16[256,16,128]{...) fusion(bf16[128,18,130]{0,2,1:T(8,128)(2,1)S(1)} %maximum_selec, ...), kind=kLoop, calls=%fused_computation.81 | loop fusion | flops 18874368 | bytes 10635264 | tf_op jit(solution)/shard_map/concatenate | solution.py:164
  25.3 1.0 %convert_reduce_fusion = (f32[128]{0:T(128)S(1)}, bf16[128,2048]{1,0:T(8,128)(2,1)S(1)}) fusion(f32[128]{0:T(128)S(1)} %copy-done.2, f32[128,2048]{1,0:T(8,128)S(1)} %convolution_add_fusion.24, f32[128,2048]{1,0:T(8,128)S(1)} %convolution_add_fusion.17, bf16[128,2048]{0,1:T(8,128)(2,1)S(1)} %bitcast.357, bf16[3,3,128,256]{3,2,1,0:T(8,128)(2,1)S(1)} %copy-done, ...), kind=kOutput, calls=%fused_computation.90 | convolution fusion | flops 71040896 | bytes 4228104 | tf_op jit(solution)/shard_map/dot_general | solution.py:50
  30.4 0.8 %slice_reduce_fusion.1 = (bf16[128,16]{1,0:T(8,128)(2,1)S(1)}, bf16[128,16]{1,0:T(8,128)(2,1)S(1)}) fusion(bf16[128,16,128]{2,1,0:T(8,128)(2,1)S(1)} %bitcast.303), kind=kLoop, calls=%fused_computation.98 | loop fusion | bytes 16384 | tf_op jit(solution)/shard_map/slice | solution.py:179
  31.4 1.0 %collective-permute-done.6 = f32[1216,128]{1,0:T(8,128)} collective-permute-done((f32[1216,128]{1,0:T(8,128)S(1)}, f32[1216,128]{1,0:T(8,128)}, u32[]{:S(2)}, u32[]{:S(2)}) %collective-permute-start.6) | collective-permute-done | bytes 622624 | tf_op jit(solution)/shard_map/ppermute | solution.py:64
  32.4 1.1 %bitcast_add_fusion = f32[1216,128]{1,0:T(8,128)S(1)} fusion(f32[1216,128]{1,0:T(8,128)} %collective-permute-done.6, f32[2,1216,128]{2,1,0:T(8,128)S(1)} %bitcast.306, s32[]{:T(128)S(6)} %select_n.98), kind=kLoop, calls=%fused_computation.94 | loop fusion | flops 155648 | bytes 1867780 | tf_op jit(solution)/shard_map/add | solution.py:64
  33.6 1.9 %collective-permute-start.7 = (bf16[320,128]{1,0:T(8,128)(2,1)S(1)}, bf16[320,128]{1,0:T(8,128)(2,1)S(1)}, u32[]{:S(2)}, u32[]{:S(2)}) collective-permute-start(bf16[320,128]{1,0:T(8,128)(2,1)S(1)} %pad_maximum_fusion.3), channel_id=1, source_target_pairs={{0,4},{4,8},{8,12},{12,0},{1,5},{5,9},{9,13},{13,1},{2,6},{6,10},{... | collective-permute-start | bytes 245768 | tf_op jit(solution)/shard_map/ppermute | solution.py:104
  35.5 2.3 %collective-permute-start.8 = (bf16[320,128]{1,0:T(8,128)(2,1)S(1)}, bf16[320,128]{1,0:T(8,128)(2,1)S(1)}, u32[]{:S(2)}, u32[]{:S(2)}) collective-permute-start(bf16[320,128]{1,0:T(8,128)(2,1)S(1)} %pad_maximum_fusion.4), channel_id=1, source_target_pairs={{0,12},{4,0},{8,4},{12,8},{1,13},{5,1},{9,5},{13,9},{2,14},{6,2},{... | collective-permute-start | bytes 245768 | tf_op jit(solution)/shard_map/ppermute | solution.py:104
  38.4 0.8 %collective-permute-start.11 = (bf16[304,128]{1,0:T(8,128)(2,1)S(1)}, bf16[304,128]{1,0:T(8,128)(2,1)S(1)}, u32[]{:S(2)}, u32[]{:S(2)}) collective-permute-start(bf16[304,128]{1,0:T(8,128)(2,1)S(1)} %get-tuple-element.68), channel_id=1, source_target_pairs={{0,8},{4,12},{8,0},{12,4},{1,9},{5,13},{9,1},{13,5},{2,10},{6,14},... | collective-permute-start | bytes 233480 | tf_op jit(solution)/shard_map/ppermute | solution.py:104
  39.2 1.4 %collective-permute-done.7 = bf16[320,128]{1,0:T(8,128)(2,1)S(1)} collective-permute-done((bf16[320,128]{1,0:T(8,128)(2,1)S(1)}, bf16[320,128]{1,0:T(8,128)(2,1)S(1)}, u32[]{:S(2)}, u32[]{:S(2)}) %collective-permute-start.7) | collective-permute-done | bytes 81952 | tf_op jit(solution)/shard_map/ppermute | solution.py:104
  40.7 0.7 collective-permute-done.8
  42.3 3.1 %collective-permute-done.11 = bf16[304,128]{1,0:T(8,128)(2,1)S(1)} collective-permute-done((bf16[304,128]{1,0:T(8,128)(2,1)S(1)}, bf16[304,128]{1,0:T(8,128)(2,1)S(1)}, u32[]{:S(2)}, u32[]{:S(2)}) %collective-permute-start.11) | collective-permute-done | bytes 77856 | tf_op jit(solution)/shard_map/ppermute | solution.py:104
  45.8 0.9 %fusion.50 = (bf16[128,16,128]{0,2,1:T(8,128)(2,1)S(1)}, bf16[128,16,128]{0,2,1:T(8,128)(2,1)S(1)}, bf16[128,16,128]{0,2,1:T(8,128)(2,1)S(1)}, bf16[128,16,128]{...) fusion(bf16[128,18,130]{0,2,1:T(8,128)(2,1)S(1)} %maximum_selec, ...), kind=kLoop, calls=%fused_computation.199 | loop fusion | bytes 9437184 | tf_op jit(solution)/shard_map/slice | solution.py:37
  49.3 1.1 %fusion.2 = bf16[128,2048]{1,0:T(8,128)(2,1)} fusion(f32[128,2048]{1,0:T(8,128)S(1)} %convolution_add_fusion.9, bf16[128,2048]{0,1:T(8,128)(2,1)S(1)} %bitcast.342, bf16[3,3,128,128]{2,3,1,0:T(8,128)(2,1)S(1)} %get-tuple-element.72), kind=kOutput, calls=%fused_computation.38 | convolution fusion | flops 67633152 | bytes 2129920 | tf_op jit(solution)/shard_map/dot_general | solution.py:50
  50.4 0.9 %fusion.49 = (bf16[128,16,128]{0,2,1:T(8,128)(2,1)S(1)}, bf16[128,16,128]{0,2,1:T(8,128)(2,1)S(1)}, bf16[128,16,128]{0,2,1:T(8,128)(2,1)S(1)}, bf16[128,16,128]{...) fusion(bf16[128,18,130]{0,2,1:T(8,128)(2,1)S(1)} %maximum_selec, ...), kind=kLoop, calls=%fused_computation.198 | loop fusion | bytes 9437184 | tf_op jit(solution)/shard_map/slice | solution.py:37
  54.3 2.1 %collective-permute-start.12 = (bf16[304,128]{1,0:T(8,128)(2,1)S(1)}, bf16[304,128]{1,0:T(8,128)(2,1)S(1)}, u32[]{:S(2)}, u32[]{:S(2)}) collective-permute-start(bf16[304,128]{1,0:T(8,128)(2,1)S(1)} %convert_element_type.70), channel_id=1, source_target_pairs={{0,12},{4,0},{8,4},{12,8},{1,13},{5,1},{9,5},{13,9},{2,14},{6,2},{... | collective-permute-start | bytes 233480 | tf_op jit(solution)/shard_map/ppermute | solution.py:76
  56.4 0.7 collective-permute-start.14
  57.1 2.1 %collective-permute-done.12 = bf16[304,128]{1,0:T(8,128)(2,1)S(1)} collective-permute-done((bf16[304,128]{1,0:T(8,128)(2,1)S(1)}, bf16[304,128]{1,0:T(8,128)(2,1)S(1)}, u32[]{:S(2)}, u32[]{:S(2)}) %collective-permute-start.12) | collective-permute-done | bytes 77856 | tf_op jit(solution)/shard_map/ppermute | solution.py:76
  59.2 4.9 %collective-permute-done.13 = bf16[304,128]{1,0:T(8,128)(2,1)S(1)} collective-permute-done((bf16[304,128]{1,0:T(8,128)(2,1)S(1)}, bf16[304,128]{1,0:T(8,128)(2,1)S(1)}, u32[]{:S(2)}, u32[]{:S(2)}) %collective-permute-start.13) | collective-permute-done | bytes 77856 | tf_op jit(solution)/shard_map/ppermute | solution.py:76
  64.3 1.5 %collective-permute-start.16 = (bf16[128,2048]{1,0:T(8,128)(2,1)}, bf16[128,2048]{1,0:T(8,128)(2,1)}, u32[]{:S(2)}, u32[]{:S(2)}) collective-permute-start(bf16[128,2048]{1,0:T(8,128)(2,1)} %fusion.2), channel_id=1, source_target_pairs={{0,2},{2,0},{1,3},{3,1},{4,6},{6,4},{5,7},{7,5},{8,10},{10,8},{9,1... | collective-permute-start | bytes 1572872 | tf_op jit(solution)/shard_map/ppermute | solution.py:191
  67.6 1.2 %fusion.6 = f32[3,3,128,256]{3,2,1,0:T(8,128)} fusion(s32[]{:T(128)S(6)} %select_n.114, f32[3,3,128,256]{3,2,1,0:T(8,128)S(1)} %reshape.240), kind=kLoop, calls=%fused_computation.63 | loop fusion | flops 294912 | bytes 2359300 | tf_op jit(solution)/shard_map/concatenate | solution.py:197
  68.7 10.3 %collective-permute-done.16 = bf16[128,2048]{1,0:T(8,128)(2,1)} collective-permute-done((bf16[128,2048]{1,0:T(8,128)(2,1)}, bf16[128,2048]{1,0:T(8,128)(2,1)}, u32[]{:S(2)}, u32[]{:S(2)}) %collective-permute-start.16) | collective-permute-done | bytes 524320 | tf_op jit(solution)/shard_map/ppermute | solution.py:191
  79.0 1.2 %fusion.21 = bf16[16,8,16,128]{3,1,2,0:T(8,128)(2,1)S(1)} fusion(f32[128,2048]{1,0:T(8,128)S(1)} %convolution_add_fusion, bf16[128,2048]{1,0:T(8,128)(2,1)} %collective-permute-done.16), kind=kLoop, calls=%fused_computation.96 | loop fusion | flops 786432 | bytes 2097152
  80.2 0.9 %copy.30 = bf16[16,8,16,128]{3,2,1,0:T(8,128)(2,1)} copy(bf16[16,8,16,128]{3,1,2,0:T(8,128)(2,1)S(1)} %fusion.21) | data formatting | bytes 1048576
  (116 shorter events, 20.8 us)
Async XLA Ops:
  0.6 8.4 %copy-start.1 = (bf16[128,16,128]{2,1,0:T(8,128)(2,1)S(1)}, bf16[128,16,128]{2,1,0:T(8,128)(2,1)}, u32[]{:S(2)}) copy-start(bf16[128,16,128]{2,1,0:T(8,128)(2,1)} %param.5) | copy-start | bytes 1572868
  2.2 16.6 %collective-permute-start.5 = (bf16[128,16,128]{0,2,1:T(8,128)(2,1)S(1)}, bf16[128,16,128]{0,2,1:T(8,128)(2,1)S(1)}, u32[]{:S(2)}, u32[]{:S(2)}) collective-permute-start(bf16[128,16,128]{0,2,1:T(8,128)(2,1)S(1)} %copy.12), channel_id=1, source_target_pairs={{0,2},{2,0},{1,3},{3,1},{4,6},{6,4},{5,7},{7,5},{8,10},{10,8},{9,1... | collective-permute-start | bytes 1572872 | tf_op jit(solution)/shard_map/ppermute | solution.py:142
  5.2 5.5 %collective-permute-start = (bf16[128,16,1]{0,2,1:T(2,128)(2,1)S(1)}, bf16[128,16,1]{0,2,1:T(2,128)(2,1)S(1)}, u32[]{:S(2)}, u32[]{:S(2)}) collective-permute-start(bf16[128,16,1]{0,2,1:T(2,128)(2,1)S(1)} %get-tuple-element.77), channel_id=1, source_target_pairs={{0,4},{4,8},{8,12},{12,0},{1,5},{5,9},{9,13},{13,1},{2,6},{6,10},{... | collective-permute-start | bytes 12296 | tf_op jit(solution)/shard_map/ppermute | solution.py:14
  6.8 3.9 %collective-permute-start.1 = (bf16[128,16,1]{0,2,1:T(2,128)(2,1)S(1)}, bf16[128,16,1]{0,2,1:T(2,128)(2,1)S(1)}, u32[]{:S(2)}, u32[]{:S(2)}) collective-permute-start(bf16[128,16,1]{0,2,1:T(2,128)(2,1)S(1)} %get-tuple-element.78), channel_id=1, source_target_pairs={{4,0},{8,4},{12,8},{0,12},{5,1},{9,5},{13,9},{1,13},{6,2},{10,6},{... | collective-permute-start | bytes 12296 | tf_op jit(solution)/shard_map/ppermute | solution.py:15
  10.7 1.3 %collective-permute-start.2 = (bf16[128,1,130]{0,2,1:T(8,128)(2,1)S(1)}, bf16[128,1,130]{0,2,1:T(8,128)(2,1)S(1)}, u32[]{:S(2)}, u32[]{:S(2)}) collective-permute-start(bf16[128,1,130]{0,2,1:T(8,128)(2,1)S(1)} %get-tuple-element.75), channel_id=1, source_target_pairs={{0,1},{1,0},{2,3},{3,2},{4,5},{5,4},{6,7},{7,6},{8,9},{9,8},{10,11... | collective-permute-start | bytes 99848 | tf_op jit(solution)/shard_map/ppermute | solution.py:14
  10.8 1.4 %collective-permute-start.3 = (bf16[128,1,130]{0,2,1:T(8,128)(2,1)S(1)}, bf16[128,1,130]{0,2,1:T(8,128)(2,1)S(1)}, u32[]{:S(2)}, u32[]{:S(2)}) collective-permute-start(bf16[128,1,130]{0,2,1:T(8,128)(2,1)S(1)} %get-tuple-element.76), channel_id=1, source_target_pairs={{1,0},{0,1},{3,2},{2,3},{5,4},{4,5},{7,6},{6,7},{9,8},{8,9},{11,10... | collective-permute-start | bytes 99848 | tf_op jit(solution)/shard_map/ppermute | solution.py:15
  12.5 1.5 %copy-start = (bf16[3,3,128,256]{3,2,1,0:T(8,128)(2,1)S(1)}, bf16[3,3,128,256]{3,2,1,0:T(8,128)(2,1)}, u32[]{:S(2)}) copy-start(bf16[3,3,128,256]{3,2,1,0:T(8,128)(2,1)} %param.6) | copy-start | bytes 1769476
  13.5 5.2 %collective-permute-start.4 = (bf16[128,292]{0,1:T(8,128)(2,1)S(1)}, bf16[128,292]{0,1:T(8,128)(2,1)S(1)}, u32[]{:S(2)}, u32[]{:S(2)}) collective-permute-start(bf16[128,292]{0,1:T(8,128)(2,1)S(1)} %pad_maximum_fusion.5), channel_id=1, source_target_pairs={{0,2},{2,0},{1,3},{3,1},{4,6},{6,4},{5,7},{7,5},{8,10},{10,8},{9,1... | collective-permute-start | bytes 224264 | tf_op jit(solution)/shard_map/ppermute | solution.py:148
  24.6 0.7 copy-start.2
  30.2 2.2 %collective-permute-start.6 = (f32[1216,128]{1,0:T(8,128)S(1)}, f32[1216,128]{1,0:T(8,128)}, u32[]{:S(2)}, u32[]{:S(2)}) collective-permute-start(f32[1216,128]{1,0:T(8,128)S(1)} %dynamic-slice_bitcast_fusion), channel_id=1, source_target_pairs={{0,1},{1,0},{2,3},{3,2},{4,5},{5,4},{6,7},{7,6},{8,9},{9,8},{10,11... | collective-permute-start | bytes 1867784 | tf_op jit(solution)/shard_map/ppermute | solution.py:64
  33.6 7.0 %collective-permute-start.7 = (bf16[320,128]{1,0:T(8,128)(2,1)S(1)}, bf16[320,128]{1,0:T(8,128)(2,1)S(1)}, u32[]{:S(2)}, u32[]{:S(2)}) collective-permute-start(bf16[320,128]{1,0:T(8,128)(2,1)S(1)} %pad_maximum_fusion.3), channel_id=1, source_target_pairs={{0,4},{4,8},{8,12},{12,0},{1,5},{5,9},{9,13},{13,1},{2,6},{6,10},{... | collective-permute-start | bytes 245768 | tf_op jit(solution)/shard_map/ppermute | solution.py:104
  35.5 6.0 %collective-permute-start.8 = (bf16[320,128]{1,0:T(8,128)(2,1)S(1)}, bf16[320,128]{1,0:T(8,128)(2,1)S(1)}, u32[]{:S(2)}, u32[]{:S(2)}) collective-permute-start(bf16[320,128]{1,0:T(8,128)(2,1)S(1)} %pad_maximum_fusion.4), channel_id=1, source_target_pairs={{0,12},{4,0},{8,4},{12,8},{1,13},{5,1},{9,5},{13,9},{2,14},{6,2},{... | collective-permute-start | bytes 245768 | tf_op jit(solution)/shard_map/ppermute | solution.py:104
  38.4 7.0 %collective-permute-start.11 = (bf16[304,128]{1,0:T(8,128)(2,1)S(1)}, bf16[304,128]{1,0:T(8,128)(2,1)S(1)}, u32[]{:S(2)}, u32[]{:S(2)}) collective-permute-start(bf16[304,128]{1,0:T(8,128)(2,1)S(1)} %get-tuple-element.68), channel_id=1, source_target_pairs={{0,8},{4,12},{8,0},{12,4},{1,9},{5,13},{9,1},{13,5},{2,10},{6,14},... | collective-permute-start | bytes 233480 | tf_op jit(solution)/shard_map/ppermute | solution.py:104
  41.7 3.7 %collective-permute-start.10 = (bf16[128,1,130]{0,2,1:T(8,128)(2,1)S(1)}, bf16[128,1,130]{0,2,1:T(8,128)(2,1)S(1)}, u32[]{:S(2)}, u32[]{:S(2)}) collective-permute-start(bf16[128,1,130]{0,2,1:T(8,128)(2,1)S(1)} %get-tuple-element.74), channel_id=1, source_target_pairs={{1,0},{0,1},{3,2},{2,3},{5,4},{4,5},{7,6},{6,7},{9,8},{8,9},{11,10... | collective-permute-start | bytes 99848 | tf_op jit(solution)/shard_map/ppermute | solution.py:15
  41.8 3.6 %collective-permute-start.9 = (bf16[128,1,130]{0,2,1:T(8,128)(2,1)S(1)}, bf16[128,1,130]{0,2,1:T(8,128)(2,1)S(1)}, u32[]{:S(2)}, u32[]{:S(2)}) collective-permute-start(bf16[128,1,130]{0,2,1:T(8,128)(2,1)S(1)} %get-tuple-element.73), channel_id=1, source_target_pairs={{0,1},{1,0},{2,3},{3,2},{4,5},{5,4},{6,7},{7,6},{8,9},{9,8},{10,11... | collective-permute-start | bytes 99848 | tf_op jit(solution)/shard_map/ppermute | solution.py:14
  54.3 4.9 %collective-permute-start.12 = (bf16[304,128]{1,0:T(8,128)(2,1)S(1)}, bf16[304,128]{1,0:T(8,128)(2,1)S(1)}, u32[]{:S(2)}, u32[]{:S(2)}) collective-permute-start(bf16[304,128]{1,0:T(8,128)(2,1)S(1)} %convert_element_type.70), channel_id=1, source_target_pairs={{0,12},{4,0},{8,4},{12,8},{1,13},{5,1},{9,5},{13,9},{2,14},{6,2},{... | collective-permute-start | bytes 233480 | tf_op jit(solution)/shard_map/ppermute | solution.py:76
  56.4 7.7 %collective-permute-start.13 = (bf16[304,128]{1,0:T(8,128)(2,1)S(1)}, bf16[304,128]{1,0:T(8,128)(2,1)S(1)}, u32[]{:S(2)}, u32[]{:S(2)}) collective-permute-start(bf16[304,128]{1,0:T(8,128)(2,1)S(1)} %convert_element_type.70), channel_id=1, source_target_pairs={{0,8},{4,12},{8,0},{12,4},{1,9},{5,13},{9,1},{13,5},{2,10},{6,14},... | collective-permute-start | bytes 233480 | tf_op jit(solution)/shard_map/ppermute | solution.py:76
  56.4 7.7 %collective-permute-start.14 = (bf16[304,128]{1,0:T(8,128)(2,1)S(1)}, bf16[304,128]{1,0:T(8,128)(2,1)S(1)}, u32[]{:S(2)}, u32[]{:S(2)}) collective-permute-start(bf16[304,128]{1,0:T(8,128)(2,1)S(1)} %convert_element_type.70), channel_id=1, source_target_pairs={{0,4},{4,8},{8,12},{12,0},{1,5},{5,9},{9,13},{13,1},{2,6},{6,10},{... | collective-permute-start | bytes 233480 | tf_op jit(solution)/shard_map/ppermute | solution.py:76
  64.3 2.1 %collective-permute-start.15 = (f32[1216,128]{1,0:T(8,128)S(1)}, f32[1216,128]{1,0:T(8,128)S(1)}, u32[]{:S(2)}, u32[]{:S(2)}) collective-permute-start(f32[1216,128]{1,0:T(8,128)S(1)} %bitcast.320), channel_id=1, source_target_pairs={{0,1},{1,0},{2,3},{3,2},{4,5},{5,4},{6,7},{7,6},{8,9},{9,8},{10,11... | collective-permute-start | bytes 1867784 | tf_op jit(solution)/shard_map/ppermute | solution.py:76
  64.3 14.7 %collective-permute-start.16 = (bf16[128,2048]{1,0:T(8,128)(2,1)}, bf16[128,2048]{1,0:T(8,128)(2,1)}, u32[]{:S(2)}, u32[]{:S(2)}) collective-permute-start(bf16[128,2048]{1,0:T(8,128)(2,1)} %fusion.2), channel_id=1, source_target_pairs={{0,2},{2,0},{1,3},{3,1},{4,6},{6,4},{5,7},{7,5},{8,10},{10,8},{9,1... | collective-permute-start | bytes 1572872 | tf_op jit(solution)/shard_map/ppermute | solution.py:191

commit v25 on v19

--- a/solution.py
+++ b/solution.py
@@ -83,7 +83,7 @@
     parts = lax.axis_size("lat") * lax.axis_size("lon")
     quantum = parts * 16 * 128
     padded = jnp.pad(flat, (0, (-flat.size) % quantum)).reshape(-1, 128)
-    rows = direct_reduce_scatter(padded, "lat", jnp.float32)
+    rows = direct_reduce_scatter(padded, "lat", send_dtype)
     count, index = lax.axis_size("lon"), lax.axis_index("lon")
     last, first = columns
     if count < 3:
@@ -110,7 +110,7 @@
 
 def sum_finish(rows, size, send_dtype):
     rows = direct_all_gather(rows, "lon", send_dtype)
-    rows = direct_all_gather(rows, "lat", jnp.float32)
+    rows = direct_all_gather(rows, "lat", send_dtype)
     return rows.reshape(-1)[:size]
 
 

time: 70.1 us -> 69.5 us (level)
  no operation moved by 1% of the time
where the time goes in v25:
time: 69.5 us; the launch traced here: 69.3 us
  starting transfers between devices  17.9 us (26%)
  waiting for transfers between devices  16.4 us (24%)
  matrix products  15.5 us (22%)
  local copies, waits for them, and re-layouts  10.2 us (15%)
  other arithmetic  7.69 us (11%)
  between operations  1.48 us (2%)
    dot_general x36, matrix products, conv_taps(): jnp.dot(kernel[tap_row, tap_col], window, preferred_element_type=jnp.floa...  12.7 us
    ppermute x1, waiting for transfers between devices, local(): received.append(lax.ppermute(outgoing[shift - 1], 'chan', pairs))  5.42 us
    ppermute x3, waiting for transfers between devices, sum_start(): moved = lax.ppermute(piece, 'lon', pairs)  5.21 us
    ppermute x3, starting transfers between devices, sum_start(): moved = lax.ppermute(piece, 'lon', pairs)  4.99 us
    slice x4, local copies, waits for them, and re-layouts, window_of(): field[:, first_row:first_row + row_count, first_col:first_col + column_co...  3.74 us
    unnamed x12, local copies, waits for them, and re-layouts  3.51 us
    ppermute x1, starting transfers between devices, local(): raw_blocks.append(lax.ppermute(inputs, 'chan', pairs))  3 us
    dot_general x9, matrix products, local(): lax.dot_general(grad_pre, window, (((1,), (1,)), ((), ())), preferred_ele...  2.85 us
  transfers between devices with their start and end apart: 17, of which 10 were waited for; matrix products, arithmetic and copies ran while one was open for 25% of the time, Pallas kernels for 0%

profile of v25, /device:TPU:0, one launch (start us, length us, event | category | flops | bytes accessed | tf_op | source)
XLA Modules:
  0.0 69.3 jit_solution(15631722413542757397)
XLA Ops:
  0.6 1.5 %copy.12 = bf16[128,16,128]{0,2,1:T(8,128)(2,1)S(1)} copy(bf16[128,16,128]{2,1,0:T(8,128)(2,1)} %param.4) | data formatting | bytes 1048576 | tf_op args[0]
  2.2 3.0 %collective-permute-start.5 = (bf16[128,16,128]{0,2,1:T(8,128)(2,1)S(1)}, bf16[128,16,128]{0,2,1:T(8,128)(2,1)S(1)}, u32[]{:S(2)}, u32[]{:S(2)}) collective-permute-start(bf16[128,16,128]{0,2,1:T(8,128)(2,1)S(1)} %copy.12), channel_id=1, source_target_pairs={{0,2},{2,0},{1,3},{3,1},{4,6},{6,4},{5,7},{7,5},{8,10},{10,8},{9,1... | collective-permute-start | bytes 1572872 | tf_op jit(solution)/shard_map/ppermute | solution.py:142
  5.2 1.6 %collective-permute-start = (bf16[128,16,1]{0,2,1:T(2,128)(2,1)S(1)}, bf16[128,16,1]{0,2,1:T(2,128)(2,1)S(1)}, u32[]{:S(2)}, u32[]{:S(2)}) collective-permute-start(bf16[128,16,1]{0,2,1:T(2,128)(2,1)S(1)} %get-tuple-element.77), channel_id=1, source_target_pairs={{0,4},{4,8},{8,12},{12,0},{1,5},{5,9},{9,13},{13,1},{2,6},{6,10},{... | collective-permute-start | bytes 12296 | tf_op jit(solution)/shard_map/ppermute | solution.py:14
  6.8 2.2 %collective-permute-start.1 = (bf16[128,16,1]{0,2,1:T(2,128)(2,1)S(1)}, bf16[128,16,1]{0,2,1:T(2,128)(2,1)S(1)}, u32[]{:S(2)}, u32[]{:S(2)}) collective-permute-start(bf16[128,16,1]{0,2,1:T(2,128)(2,1)S(1)} %get-tuple-element.78), channel_id=1, source_target_pairs={{4,0},{8,4},{12,8},{0,12},{5,1},{9,5},{13,9},{1,13},{6,2},{10,6},{... | collective-permute-start | bytes 12296 | tf_op jit(solution)/shard_map/ppermute | solution.py:15
  9.2 1.5 %collective-permute-done = bf16[128,16,1]{0,2,1:T(2,128)(2,1)S(1)} collective-permute-done((bf16[128,16,1]{0,2,1:T(2,128)(2,1)S(1)}, bf16[128,16,1]{0,2,1:T(2,128)(2,1)S(1)}, u32[]{:S(2)}, u32[]{:S(2)}) %collective-permute-start) | collective-permute-done | bytes 4128 | tf_op jit(solution)/shard_map/ppermute | solution.py:14
  11.3 0.7 collective-permute-done.2
  12.5 0.9 %fusion.57 = (bf16[128,16,128]{0,2,1:T(8,128)(2,1)S(1)}, bf16[128,16,128]{0,2,1:T(8,128)(2,1)S(1)}, bf16[128,16,128]{0,2,1:T(8,128)(2,1)S(1)}, bf16[128,16,128]{...) fusion(bf16[128,18,130]{0,2,1:T(8,128)(2,1)S(1)} %maximum_selec, ...), kind=kLoop, calls=%fused_computation.206 | loop fusion | bytes 9437184 | tf_op jit(solution)/shard_map/slice | solution.py:37
  16.7 2.0 %collective-permute-done.4 = bf16[128,292]{0,1:T(8,128)(2,1)S(1)} collective-permute-done((bf16[128,292]{0,1:T(8,128)(2,1)S(1)}, bf16[128,292]{0,1:T(8,128)(2,1)S(1)}, u32[]{:S(2)}, u32[]{:S(2)}) %collective-permute-start.4) | collective-permute-done | bytes 74784 | tf_op jit(solution)/shard_map/ppermute | solution.py:148
  19.0 1.0 %fusion.55 = (bf16[128,16,128]{0,2,1:T(8,128)(2,1)S(1)}, bf16[128,16,128]{0,2,1:T(8,128)(2,1)S(1)}, bf16[128,16,128]{0,2,1:T(8,128)(2,1)S(1)}, bf16[128,16,128]{...) fusion(bf16[128,18,130]{0,2,1:T(8,128)(2,1)S(1)} %pad_maximum_f, ...), kind=kLoop, calls=%fused_computation.204 | loop fusion | bytes 9437184 | tf_op jit(solution)/shard_map/slice | solution.py:37
  19.9 2.5 %fusion.14 = (bf16[256,16,128]{0,2,1:T(8,128)(2,1)S(1)}, bf16[256,16,128]{0,2,1:T(8,128)(2,1)S(1)}, bf16[256,16,128]{0,2,1:T(8,128)(2,1)S(1)}, bf16[256,16,128]{...) fusion(bf16[128,18,130]{0,2,1:T(8,128)(2,1)S(1)} %maximum_selec, ...), kind=kLoop, calls=%fused_computation.81 | loop fusion | flops 18874368 | bytes 10635264 | tf_op jit(solution)/shard_map/concatenate | solution.py:164
  25.3 1.0 %convert_reduce_fusion = (f32[128]{0:T(128)S(1)}, bf16[128,2048]{1,0:T(8,128)(2,1)S(1)}) fusion(f32[128]{0:T(128)S(1)} %copy-done.2, f32[128,2048]{1,0:T(8,128)S(1)} %convolution_add_fusion.24, f32[128,2048]{1,0:T(8,128)S(1)} %convolution_add_fusion.17, bf16[128,2048]{0,1:T(8,128)(2,1)S(1)} %bitcast.359, bf16[3,3,128,256]{3,2,1,0:T(8,128)(2,1)S(1)} %copy-done, ...), kind=kOutput, calls=%fused_computation.90 | convolution fusion | flops 71040896 | bytes 4228104 | tf_op jit(solution)/shard_map/dot_general | solution.py:50
  29.4 0.6 copy.28
  30.5 0.8 %slice_reduce_fusion.1 = (bf16[128,16]{1,0:T(8,128)(2,1)S(1)}, bf16[128,16]{1,0:T(8,128)(2,1)S(1)}) fusion(bf16[128,16,128]{2,1,0:T(8,128)(2,1)S(1)} %bitcast.306), kind=kLoop, calls=%fused_computation.98 | loop fusion | bytes 16384 | tf_op jit(solution)/shard_map/slice | solution.py:179
  32.0 1.0 %bitcast_add_fusion = f32[1216,128]{1,0:T(8,128)S(1)} fusion(bf16[1216,128]{1,0:T(8,128)(2,1)} %collective-permute-done.6, f32[2,1216,128]{2,1,0:T(8,128)S(1)} %bitcast.322, s32[]{:T(128)S(6)} %select_n.98), kind=kLoop, calls=%fused_computation.94 | loop fusion | flops 311296 | bytes 1556484 | tf_op jit(solution)/shard_map/add | solution.py:64
  33.1 1.9 %collective-permute-start.7 = (bf16[320,128]{1,0:T(8,128)(2,1)S(1)}, bf16[320,128]{1,0:T(8,128)(2,1)S(1)}, u32[]{:S(2)}, u32[]{:S(2)}) collective-permute-start(bf16[320,128]{1,0:T(8,128)(2,1)S(1)} %pad_maximum_fusion.3), channel_id=1, source_target_pairs={{0,4},{4,8},{8,12},{12,0},{1,5},{5,9},{9,13},{13,1},{2,6},{6,10},{... | collective-permute-start | bytes 245768 | tf_op jit(solution)/shard_map/ppermute | solution.py:104
  34.9 2.3 %collective-permute-start.8 = (bf16[320,128]{1,0:T(8,128)(2,1)S(1)}, bf16[320,128]{1,0:T(8,128)(2,1)S(1)}, u32[]{:S(2)}, u32[]{:S(2)}) collective-permute-start(bf16[320,128]{1,0:T(8,128)(2,1)S(1)} %pad_maximum_fusion.4), channel_id=1, source_target_pairs={{0,12},{4,0},{8,4},{12,8},{1,13},{5,1},{9,5},{13,9},{2,14},{6,2},{... | collective-permute-start | bytes 245768 | tf_op jit(solution)/shard_map/ppermute | solution.py:104
  37.8 0.8 %collective-permute-start.11 = (bf16[304,128]{1,0:T(8,128)(2,1)S(1)}, bf16[304,128]{1,0:T(8,128)(2,1)S(1)}, u32[]{:S(2)}, u32[]{:S(2)}) collective-permute-start(bf16[304,128]{1,0:T(8,128)(2,1)S(1)} %get-tuple-element.68), channel_id=1, source_target_pairs={{0,8},{4,12},{8,0},{12,4},{1,9},{5,13},{9,1},{13,5},{2,10},{6,14},... | collective-permute-start | bytes 233480 | tf_op jit(solution)/shard_map/ppermute | solution.py:104
  38.6 1.4 %collective-permute-done.7 = bf16[320,128]{1,0:T(8,128)(2,1)S(1)} collective-permute-done((bf16[320,128]{1,0:T(8,128)(2,1)S(1)}, bf16[320,128]{1,0:T(8,128)(2,1)S(1)}, u32[]{:S(2)}, u32[]{:S(2)}) %collective-permute-start.7) | collective-permute-done | bytes 81952 | tf_op jit(solution)/shard_map/ppermute | solution.py:104
  40.2 0.7 %collective-permute-done.8 = bf16[320,128]{1,0:T(8,128)(2,1)S(1)} collective-permute-done((bf16[320,128]{1,0:T(8,128)(2,1)S(1)}, bf16[320,128]{1,0:T(8,128)(2,1)S(1)}, u32[]{:S(2)}, u32[]{:S(2)}) %collective-permute-start.8) | collective-permute-done | bytes 81952 | tf_op jit(solution)/shard_map/ppermute | solution.py:104
  41.7 3.1 %collective-permute-done.11 = bf16[304,128]{1,0:T(8,128)(2,1)S(1)} collective-permute-done((bf16[304,128]{1,0:T(8,128)(2,1)S(1)}, bf16[304,128]{1,0:T(8,128)(2,1)S(1)}, u32[]{:S(2)}, u32[]{:S(2)}) %collective-permute-start.11) | collective-permute-done | bytes 77856 | tf_op jit(solution)/shard_map/ppermute | solution.py:104
  44.8 2.1 %collective-permute-start.12 = (bf16[304,128]{1,0:T(8,128)(2,1)S(1)}, bf16[304,128]{1,0:T(8,128)(2,1)S(1)}, u32[]{:S(2)}, u32[]{:S(2)}) collective-permute-start(bf16[304,128]{1,0:T(8,128)(2,1)S(1)} %get-tuple-element.17), channel_id=1, source_target_pairs={{0,12},{4,0},{8,4},{12,8},{1,13},{5,1},{9,5},{13,9},{2,14},{6,2},{... | collective-permute-start | bytes 233480 | tf_op jit(solution)/shard_map/ppermute | solution.py:76
  46.9 0.6 collective-permute-start.14
  47.9 0.9 %fusion.54 = (bf16[128,16,128]{0,2,1:T(8,128)(2,1)S(1)}, bf16[128,16,128]{0,2,1:T(8,128)(2,1)S(1)}, bf16[128,16,128]{0,2,1:T(8,128)(2,1)S(1)}, bf16[128,16,128]{...) fusion(bf16[128,18,130]{0,2,1:T(8,128)(2,1)S(1)} %maximum_selec, ...), kind=kLoop, calls=%fused_computation.203 | loop fusion | bytes 9437184 | tf_op jit(solution)/shard_map/slice | solution.py:37
  51.5 1.1 %fusion.2 = bf16[128,2048]{1,0:T(8,128)(2,1)} fusion(f32[128,2048]{1,0:T(8,128)S(1)} %convolution_add_fusion.9, bf16[128,2048]{0,1:T(8,128)(2,1)S(1)} %bitcast.346, bf16[3,3,128,128]{2,3,1,0:T(8,128)(2,1)S(1)} %get-tuple-element.72), kind=kOutput, calls=%fused_computation.38 | convolution fusion | flops 67633152 | bytes 2129920 | tf_op jit(solution)/shard_map/dot_general | solution.py:50
  52.6 0.9 %fusion.53 = (bf16[128,16,128]{0,2,1:T(8,128)(2,1)S(1)}, bf16[128,16,128]{0,2,1:T(8,128)(2,1)S(1)}, bf16[128,16,128]{0,2,1:T(8,128)(2,1)S(1)}, bf16[128,16,128]{...) fusion(bf16[128,18,130]{0,2,1:T(8,128)(2,1)S(1)} %maximum_selec, ...), kind=kLoop, calls=%fused_computation.202 | loop fusion | bytes 9437184 | tf_op jit(solution)/shard_map/slice | solution.py:37
  53.5 1.6 %collective-permute-start.16 = (bf16[128,2048]{1,0:T(8,128)(2,1)}, bf16[128,2048]{1,0:T(8,128)(2,1)}, u32[]{:S(2)}, u32[]{:S(2)}) collective-permute-start(bf16[128,2048]{1,0:T(8,128)(2,1)} %fusion.2), channel_id=1, source_target_pairs={{0,2},{2,0},{1,3},{3,1},{4,6},{6,4},{5,7},{7,5},{8,10},{10,8},{9,1... | collective-permute-start | bytes 1572872 | tf_op jit(solution)/shard_map/ppermute | solution.py:198
  58.4 0.9 %collective-permute-done.15 = bf16[1216,128]{1,0:T(8,128)(2,1)S(1)} collective-permute-done((bf16[1216,128]{1,0:T(8,128)(2,1)S(1)}, bf16[1216,128]{1,0:T(8,128)(2,1)S(1)}, u32[]{:S(2)}, u32[]{:S(2)}) %collective-permute-start.15) | collective-permute-done | bytes 311328 | tf_op jit(solution)/shard_map/ppermute | solution.py:76
  59.8 0.5 slice.493
  60.6 1.2 %fusion.6 = f32[3,3,128,256]{3,2,1,0:T(8,128)} fusion(s32[]{:T(128)S(6)} %select_n.114, f32[3,3,128,256]{3,2,1,0:T(8,128)S(1)} %reshape.239), kind=kLoop, calls=%fused_computation.63 | loop fusion | flops 294912 | bytes 2359300 | tf_op jit(solution)/shard_map/concatenate | solution.py:184
  61.8 5.4 %collective-permute-done.16 = bf16[128,2048]{1,0:T(8,128)(2,1)} collective-permute-done((bf16[128,2048]{1,0:T(8,128)(2,1)}, bf16[128,2048]{1,0:T(8,128)(2,1)}, u32[]{:S(2)}, u32[]{:S(2)}) %collective-permute-start.16) | collective-permute-done | bytes 524320 | tf_op jit(solution)/shard_map/ppermute | solution.py:198
  67.2 1.2 %fusion.21 = bf16[16,8,16,128]{3,1,2,0:T(8,128)(2,1)S(1)} fusion(f32[128,2048]{1,0:T(8,128)S(1)} %convolution_add_fusion, bf16[128,2048]{1,0:T(8,128)(2,1)} %collective-permute-done.16), kind=kLoop, calls=%fused_computation.96 | loop fusion | flops 786432 | bytes 2097152
  68.4 0.9 %copy.30 = bf16[16,8,16,128]{3,2,1,0:T(8,128)(2,1)} copy(bf16[16,8,16,128]{3,1,2,0:T(8,128)(2,1)S(1)} %fusion.21) | data formatting | bytes 1048576
  (116 shorter events, 19.8 us)
Async XLA Ops:
  0.6 8.4 %copy-start.1 = (bf16[128,16,128]{2,1,0:T(8,128)(2,1)S(1)}, bf16[128,16,128]{2,1,0:T(8,128)(2,1)}, u32[]{:S(2)}) copy-start(bf16[128,16,128]{2,1,0:T(8,128)(2,1)} %param.5) | copy-start | bytes 1572868
  2.2 16.6 %collective-permute-start.5 = (bf16[128,16,128]{0,2,1:T(8,128)(2,1)S(1)}, bf16[128,16,128]{0,2,1:T(8,128)(2,1)S(1)}, u32[]{:S(2)}, u32[]{:S(2)}) collective-permute-start(bf16[128,16,128]{0,2,1:T(8,128)(2,1)S(1)} %copy.12), channel_id=1, source_target_pairs={{0,2},{2,0},{1,3},{3,1},{4,6},{6,4},{5,7},{7,5},{8,10},{10,8},{9,1... | collective-permute-start | bytes 1572872 | tf_op jit(solution)/shard_map/ppermute | solution.py:142
  5.2 5.5 %collective-permute-start = (bf16[128,16,1]{0,2,1:T(2,128)(2,1)S(1)}, bf16[128,16,1]{0,2,1:T(2,128)(2,1)S(1)}, u32[]{:S(2)}, u32[]{:S(2)}) collective-permute-start(bf16[128,16,1]{0,2,1:T(2,128)(2,1)S(1)} %get-tuple-element.77), channel_id=1, source_target_pairs={{0,4},{4,8},{8,12},{12,0},{1,5},{5,9},{9,13},{13,1},{2,6},{6,10},{... | collective-permute-start | bytes 12296 | tf_op jit(solution)/shard_map/ppermute | solution.py:14
  6.8 3.9 %collective-permute-start.1 = (bf16[128,16,1]{0,2,1:T(2,128)(2,1)S(1)}, bf16[128,16,1]{0,2,1:T(2,128)(2,1)S(1)}, u32[]{:S(2)}, u32[]{:S(2)}) collective-permute-start(bf16[128,16,1]{0,2,1:T(2,128)(2,1)S(1)} %get-tuple-element.78), channel_id=1, source_target_pairs={{4,0},{8,4},{12,8},{0,12},{5,1},{9,5},{13,9},{1,13},{6,2},{10,6},{... | collective-permute-start | bytes 12296 | tf_op jit(solution)/shard_map/ppermute | solution.py:15
  10.7 1.3 %collective-permute-start.2 = (bf16[128,1,130]{0,2,1:T(8,128)(2,1)S(1)}, bf16[128,1,130]{0,2,1:T(8,128)(2,1)S(1)}, u32[]{:S(2)}, u32[]{:S(2)}) collective-permute-start(bf16[128,1,130]{0,2,1:T(8,128)(2,1)S(1)} %get-tuple-element.75), channel_id=1, source_target_pairs={{0,1},{1,0},{2,3},{3,2},{4,5},{5,4},{6,7},{7,6},{8,9},{9,8},{10,11... | collective-permute-start | bytes 99848 | tf_op jit(solution)/shard_map/ppermute | solution.py:14
  10.8 1.4 %collective-permute-start.3 = (bf16[128,1,130]{0,2,1:T(8,128)(2,1)S(1)}, bf16[128,1,130]{0,2,1:T(8,128)(2,1)S(1)}, u32[]{:S(2)}, u32[]{:S(2)}) collective-permute-start(bf16[128,1,130]{0,2,1:T(8,128)(2,1)S(1)} %get-tuple-element.76), channel_id=1, source_target_pairs={{1,0},{0,1},{3,2},{2,3},{5,4},{4,5},{7,6},{6,7},{9,8},{8,9},{11,10... | collective-permute-start | bytes 99848 | tf_op jit(solution)/shard_map/ppermute | solution.py:15
  12.5 1.5 %copy-start = (bf16[3,3,128,256]{3,2,1,0:T(8,128)(2,1)S(1)}, bf16[3,3,128,256]{3,2,1,0:T(8,128)(2,1)}, u32[]{:S(2)}) copy-start(bf16[3,3,128,256]{3,2,1,0:T(8,128)(2,1)} %param.6) | copy-start | bytes 1769476
  13.5 5.2 %collective-permute-start.4 = (bf16[128,292]{0,1:T(8,128)(2,1)S(1)}, bf16[128,292]{0,1:T(8,128)(2,1)S(1)}, u32[]{:S(2)}, u32[]{:S(2)}) collective-permute-start(bf16[128,292]{0,1:T(8,128)(2,1)S(1)} %pad_maximum_fusion.5), channel_id=1, source_target_pairs={{0,2},{2,0},{1,3},{3,1},{4,6},{6,4},{5,7},{7,5},{8,10},{10,8},{9,1... | collective-permute-start | bytes 224264 | tf_op jit(solution)/shard_map/ppermute | solution.py:148
  24.6 0.7 copy-start.2
  30.2 1.8 %collective-permute-start.6 = (bf16[1216,128]{1,0:T(8,128)(2,1)S(1)}, bf16[1216,128]{1,0:T(8,128)(2,1)}, u32[]{:S(2)}, u32[]{:S(2)}) collective-permute-start(bf16[1216,128]{1,0:T(8,128)(2,1)S(1)} %fusion.22), channel_id=1, source_target_pairs={{0,1},{1,0},{2,3},{3,2},{4,5},{5,4},{6,7},{7,6},{8,9},{9,8},{10,11... | collective-permute-start | bytes 933896 | tf_op jit(solution)/shard_map/ppermute | solution.py:64
  33.1 7.0 %collective-permute-start.7 = (bf16[320,128]{1,0:T(8,128)(2,1)S(1)}, bf16[320,128]{1,0:T(8,128)(2,1)S(1)}, u32[]{:S(2)}, u32[]{:S(2)}) collective-permute-start(bf16[320,128]{1,0:T(8,128)(2,1)S(1)} %pad_maximum_fusion.3), channel_id=1, source_target_pairs={{0,4},{4,8},{8,12},{12,0},{1,5},{5,9},{9,13},{13,1},{2,6},{6,10},{... | collective-permute-start | bytes 245768 | tf_op jit(solution)/shard_map/ppermute | solution.py:104
  34.9 6.0 %collective-permute-start.8 = (bf16[320,128]{1,0:T(8,128)(2,1)S(1)}, bf16[320,128]{1,0:T(8,128)(2,1)S(1)}, u32[]{:S(2)}, u32[]{:S(2)}) collective-permute-start(bf16[320,128]{1,0:T(8,128)(2,1)S(1)} %pad_maximum_fusion.4), channel_id=1, source_target_pairs={{0,12},{4,0},{8,4},{12,8},{1,13},{5,1},{9,5},{13,9},{2,14},{6,2},{... | collective-permute-start | bytes 245768 | tf_op jit(solution)/shard_map/ppermute | solution.py:104
  37.8 7.0 %collective-permute-start.11 = (bf16[304,128]{1,0:T(8,128)(2,1)S(1)}, bf16[304,128]{1,0:T(8,128)(2,1)S(1)}, u32[]{:S(2)}, u32[]{:S(2)}) collective-permute-start(bf16[304,128]{1,0:T(8,128)(2,1)S(1)} %get-tuple-element.68), channel_id=1, source_target_pairs={{0,8},{4,12},{8,0},{12,4},{1,9},{5,13},{9,1},{13,5},{2,10},{6,14},... | collective-permute-start | bytes 233480 | tf_op jit(solution)/shard_map/ppermute | solution.py:104
  41.1 6.5 %collective-permute-start.10 = (bf16[128,1,130]{0,2,1:T(8,128)(2,1)S(1)}, bf16[128,1,130]{0,2,1:T(8,128)(2,1)S(1)}, u32[]{:S(2)}, u32[]{:S(2)}) collective-permute-start(bf16[128,1,130]{0,2,1:T(8,128)(2,1)S(1)} %get-tuple-element.74), channel_id=1, source_target_pairs={{1,0},{0,1},{3,2},{2,3},{5,4},{4,5},{7,6},{6,7},{9,8},{8,9},{11,10... | collective-permute-start | bytes 99848 | tf_op jit(solution)/shard_map/ppermute | solution.py:15
  41.2 6.4 %collective-permute-start.9 = (bf16[128,1,130]{0,2,1:T(8,128)(2,1)S(1)}, bf16[128,1,130]{0,2,1:T(8,128)(2,1)S(1)}, u32[]{:S(2)}, u32[]{:S(2)}) collective-permute-start(bf16[128,1,130]{0,2,1:T(8,128)(2,1)S(1)} %get-tuple-element.73), channel_id=1, source_target_pairs={{0,1},{1,0},{2,3},{3,2},{4,5},{5,4},{6,7},{7,6},{8,9},{9,8},{10,11... | collective-permute-start | bytes 99848 | tf_op jit(solution)/shard_map/ppermute | solution.py:14
  44.8 12.5 %collective-permute-start.12 = (bf16[304,128]{1,0:T(8,128)(2,1)S(1)}, bf16[304,128]{1,0:T(8,128)(2,1)S(1)}, u32[]{:S(2)}, u32[]{:S(2)}) collective-permute-start(bf16[304,128]{1,0:T(8,128)(2,1)S(1)} %get-tuple-element.17), channel_id=1, source_target_pairs={{0,12},{4,0},{8,4},{12,8},{1,13},{5,1},{9,5},{13,9},{2,14},{6,2},{... | collective-permute-start | bytes 233480 | tf_op jit(solution)/shard_map/ppermute | solution.py:76
  46.9 10.5 %collective-permute-start.13 = (bf16[304,128]{1,0:T(8,128)(2,1)S(1)}, bf16[304,128]{1,0:T(8,128)(2,1)S(1)}, u32[]{:S(2)}, u32[]{:S(2)}) collective-permute-start(bf16[304,128]{1,0:T(8,128)(2,1)S(1)} %get-tuple-element.17), channel_id=1, source_target_pairs={{0,8},{4,12},{8,0},{12,4},{1,9},{5,13},{9,1},{13,5},{2,10},{6,14},... | collective-permute-start | bytes 233480 | tf_op jit(solution)/shard_map/ppermute | solution.py:76
  46.9 10.5 %collective-permute-start.14 = (bf16[304,128]{1,0:T(8,128)(2,1)S(1)}, bf16[304,128]{1,0:T(8,128)(2,1)S(1)}, u32[]{:S(2)}, u32[]{:S(2)}) collective-permute-start(bf16[304,128]{1,0:T(8,128)(2,1)S(1)} %get-tuple-element.17), channel_id=1, source_target_pairs={{0,4},{4,8},{8,12},{12,0},{1,5},{5,9},{9,13},{13,1},{2,6},{6,10},{... | collective-permute-start | bytes 233480 | tf_op jit(solution)/shard_map/ppermute | solution.py:76
  53.5 13.7 %collective-permute-start.16 = (bf16[128,2048]{1,0:T(8,128)(2,1)}, bf16[128,2048]{1,0:T(8,128)(2,1)}, u32[]{:S(2)}, u32[]{:S(2)}) collective-permute-start(bf16[128,2048]{1,0:T(8,128)(2,1)} %fusion.2), channel_id=1, source_target_pairs={{0,2},{2,0},{1,3},{3,1},{4,6},{6,4},{5,7},{7,5},{8,10},{10,8},{9,1... | collective-permute-start | bytes 1572872 | tf_op jit(solution)/shard_map/ppermute | solution.py:198
  57.7 1.7 %collective-permute-start.15 = (bf16[1216,128]{1,0:T(8,128)(2,1)S(1)}, bf16[1216,128]{1,0:T(8,128)(2,1)S(1)}, u32[]{:S(2)}, u32[]{:S(2)}) collective-permute-start(bf16[1216,128]{1,0:T(8,128)(2,1)S(1)} %bitcast.363), channel_id=1, source_target_pairs={{0,1},{1,0},{2,3},{3,2},{4,5},{5,4},{6,7},{7,6},{8,9},{9,8},{10,11... | collective-permute-start | bytes 933896 | tf_op jit(solution)/shard_map/ppermute | solution.py:76

commit v26 on v19

--- a/solution.py
+++ b/solution.py
@@ -177,7 +177,7 @@
     flat = jnp.concatenate([weight_part.reshape(-1), bias_part])
     grad_field = grad_pre.reshape(own_channels, row_count, column_count)
     edges = (grad_field[:, :, column_count - 1 :], grad_field[:, :, :1])
-    scattered, (before, after) = sum_start(flat, jnp.bfloat16, edges)
+    scattered, (before, after) = sum_start(flat, jnp.float32, edges)
     flat = sum_finish(scattered, flat.size, jnp.bfloat16)
     weight_local = flat[: weight_part.size].reshape(weight_part.shape)
     bias_grad = flat[weight_part.size :]

time: 70.1 us -> 80.3 us (1.15)
  waiting for transfers between devices: 17 us -> 23.1 us
  local copies, waits for them, and re-layouts: 10.3 us -> 12.8 us
  other arithmetic: 7.67 us -> 9.63 us
    ppermute x3, waiting for transfers between devices: 5.21 us -> 12.3 us  [sum_start(): moved = lax.ppermute(piece, 'lon', pairs)]
    unnamed x12 -> x14, local copies, waits for them, and re-layouts: 3.51 us -> 5.2 us
    concatenate x1, other arithmetic: 0.18 us -> 1.22 us  [with_border(): jnp.concatenate([top[:, None, :], middle, bottom[:, None, :]], axis=1)]
    convert_element_type x1, other arithmetic: 0.04 us -> 0.95 us  [direct_all_gather(): sent = chunk.astype(send_dtype)]
    squeeze x1, local copies, waits for them, and re-layouts: 0.05 us -> 0.87 us  [direct_reduce_scatter(): lax.dynamic_index_in_dim(chunks, (index + step) % count, keepdims=False)]
  transfers between devices with their start and end apart: 17 -> 17, of which waited for: 10 -> 10; matrix products, arithmetic and copies ran while one was open for 25% -> 24% of each run, Pallas kernels for 0% -> 0%
where the time goes in v26:
time: 80.3 us; the launch traced here: 80 us
  waiting for transfers between devices  23.1 us (29%)
  starting transfers between devices  17.6 us (22%)
  matrix products  15.6 us (19%)
  local copies, waits for them, and re-layouts  12.8 us (16%)
  other arithmetic  9.63 us (12%)
  between operations  1.41 us (2%)
    dot_general x36, matrix products, conv_taps(): jnp.dot(kernel[tap_row, tap_col], window, preferred_element_type=jnp.floa...  12.7 us
    ppermute x3, waiting for transfers between devices, sum_start(): moved = lax.ppermute(piece, 'lon', pairs)  12.3 us
    unnamed x14, local copies, waits for them, and re-layouts  5.2 us
    ppermute x1, waiting for transfers between devices, local(): received.append(lax.ppermute(outgoing[shift - 1], 'chan', pairs))  5.17 us
    ppermute x3, starting transfers between devices, sum_start(): moved = lax.ppermute(piece, 'lon', pairs)  5.15 us
    slice x4, local copies, waits for them, and re-layouts, window_of(): field[:, first_row:first_row + row_count, first_col:first_col + column_co...  3.63 us
    ppermute x1, starting transfers between devices, local(): raw_blocks.append(lax.ppermute(inputs, 'chan', pairs))  3 us
    dot_general x9, matrix products, local(): lax.dot_general(grad_pre, window, (((1,), (1,)), ((), ())), preferred_ele...  2.85 us
  transfers between devices with their start and end apart: 17, of which 10 were waited for; matrix products, arithmetic and copies ran while one was open for 24% of the time, Pallas kernels for 0%

profile of v26, /device:TPU:0, one launch (start us, length us, event | category | flops | bytes accessed | tf_op | source)
XLA Modules:
  0.0 80.0 jit_solution(1184640600860939466)
XLA Ops:
  0.6 1.5 %copy.12 = bf16[128,16,128]{0,2,1:T(8,128)(2,1)S(1)} copy(bf16[128,16,128]{2,1,0:T(8,128)(2,1)} %param.4) | data formatting | bytes 1048576 | tf_op args[0]
  2.2 3.0 %collective-permute-start.5 = (bf16[128,16,128]{0,2,1:T(8,128)(2,1)S(1)}, bf16[128,16,128]{0,2,1:T(8,128)(2,1)}, u32[]{:S(2)}, u32[]{:S(2)}) collective-permute-start(bf16[128,16,128]{0,2,1:T(8,128)(2,1)S(1)} %copy.12), channel_id=1, source_target_pairs={{0,2},{2,0},{1,3},{3,1},{4,6},{6,4},{5,7},{7,5},{8,10},{10,8},{9,1... | collective-permute-start | bytes 1572872 | tf_op jit(solution)/shard_map/ppermute | solution.py:142
  5.2 1.6 %collective-permute-start = (bf16[128,16,1]{0,2,1:T(2,128)(2,1)S(1)}, bf16[128,16,1]{0,2,1:T(2,128)(2,1)S(1)}, u32[]{:S(2)}, u32[]{:S(2)}) collective-permute-start(bf16[128,16,1]{0,2,1:T(2,128)(2,1)S(1)} %get-tuple-element.75), channel_id=1, source_target_pairs={{0,4},{4,8},{8,12},{12,0},{1,5},{5,9},{9,13},{13,1},{2,6},{6,10},{... | collective-permute-start | bytes 12296 | tf_op jit(solution)/shard_map/ppermute | solution.py:14
  6.8 2.2 %collective-permute-start.1 = (bf16[128,16,1]{0,2,1:T(2,128)(2,1)S(1)}, bf16[128,16,1]{0,2,1:T(2,128)(2,1)S(1)}, u32[]{:S(2)}, u32[]{:S(2)}) collective-permute-start(bf16[128,16,1]{0,2,1:T(2,128)(2,1)S(1)} %get-tuple-element.76), channel_id=1, source_target_pairs={{4,0},{8,4},{12,8},{0,12},{5,1},{9,5},{13,9},{1,13},{6,2},{10,6},{... | collective-permute-start | bytes 12296 | tf_op jit(solution)/shard_map/ppermute | solution.py:15
  9.2 1.5 %collective-permute-done = bf16[128,16,1]{0,2,1:T(2,128)(2,1)S(1)} collective-permute-done((bf16[128,16,1]{0,2,1:T(2,128)(2,1)S(1)}, bf16[128,16,1]{0,2,1:T(2,128)(2,1)S(1)}, u32[]{:S(2)}, u32[]{:S(2)}) %collective-permute-start) | collective-permute-done | bytes 4128 | tf_op jit(solution)/shard_map/ppermute | solution.py:14
  12.5 0.9 %fusion.50 = (bf16[128,16,128]{0,2,1:T(8,128)(2,1)S(1)}, bf16[128,16,128]{0,2,1:T(8,128)(2,1)S(1)}, bf16[128,16,128]{0,2,1:T(8,128)(2,1)S(1)}, bf16[128,16,128]{...) fusion(bf16[128,18,130]{0,2,1:T(8,128)(2,1)S(1)} %maximum_selec, ...), kind=kLoop, calls=%fused_computation.200 | loop fusion | bytes 9437184 | tf_op jit(solution)/shard_map/slice | solution.py:37
  16.7 2.0 %collective-permute-done.4 = bf16[128,292]{0,1:T(8,128)(2,1)S(1)} collective-permute-done((bf16[128,292]{0,1:T(8,128)(2,1)S(1)}, bf16[128,292]{0,1:T(8,128)(2,1)S(1)}, u32[]{:S(2)}, u32[]{:S(2)}) %collective-permute-start.4) | collective-permute-done | bytes 74784 | tf_op jit(solution)/shard_map/ppermute | solution.py:148
  18.8 1.2 %pad_maximum_fusion.2 = bf16[128,18,130]{0,2,1:T(8,128)(2,1)S(1)} fusion(bf16[128,1,130]{0,2,1:T(8,128)(2,1)S(1)} %get-tuple-element.78, bf16[128,16,1]{0,2,1:T(2,128)(2,1)S(1)} %copy.17, bf16[128,16,128]{0,2,1:T(8,128)(2,1)} %collective-permute-done.5, bf16[128,16,1]{0,2,1:T(2,128)(2,1)S(1)} %copy.16, bf16[128,1,130]{0,2,1:T(8,128)(2,1)S(1)} %get-tuple-element.77), kind=kLoop, calls=%fused_computation.92 | loop fusion | flops 2995200 | bytes 1198080 | tf_op jit(solution)/shard_map/concatenate | solution.py:132
  20.0 0.9 %fusion.48 = (bf16[128,16,128]{0,2,1:T(8,128)(2,1)S(1)}, bf16[128,16,128]{0,2,1:T(8,128)(2,1)S(1)}, bf16[128,16,128]{0,2,1:T(8,128)(2,1)S(1)}, bf16[128,16,128]{...) fusion(bf16[128,18,130]{0,2,1:T(8,128)(2,1)S(1)} %pad_maximum_f, ...), kind=kLoop, calls=%fused_computation.198 | loop fusion | bytes 9437184 | tf_op jit(solution)/shard_map/slice | solution.py:37
  20.9 2.5 %fusion.14 = (bf16[256,16,128]{0,2,1:T(8,128)(2,1)S(1)}, bf16[256,16,128]{0,2,1:T(8,128)(2,1)S(1)}, bf16[256,16,128]{0,2,1:T(8,128)(2,1)S(1)}, bf16[256,16,128]{...) fusion(bf16[128,18,130]{0,2,1:T(8,128)(2,1)S(1)} %maximum_selec, ...), kind=kLoop, calls=%fused_computation.81 | loop fusion | flops 18874368 | bytes 10635264 | tf_op jit(solution)/shard_map/concatenate | solution.py:164
  26.2 1.0 %convert_reduce_fusion = (f32[128]{0:T(128)S(1)}, bf16[128,2048]{1,0:T(8,128)(2,1)S(1)}) fusion(f32[128]{0:T(128)S(1)} %copy-done.2, f32[128,2048]{1,0:T(8,128)S(1)} %convolution_add_fusion.24, f32[128,2048]{1,0:T(8,128)S(1)} %convolution_add_fusion.17, bf16[128,2048]{0,1:T(8,128)(2,1)S(1)} %bitcast.360, bf16[3,3,128,256]{3,2,1,0:T(8,128)(2,1)S(1)} %copy-done, ...), kind=kOutput, calls=%fused_computation.90 | convolution fusion | flops 71040896 | bytes 4228104 | tf_op jit(solution)/shard_map/dot_general | solution.py:50
  31.1 0.9 %dynamic-slice_bitcast_fusion = f32[1216,128]{1,0:T(8,128)} fusion(f32[2,1216,128]{2,1,0:T(8,128)S(1)} %bitcast.306, s32[]{:T(128)S(6)} %select_n.100), kind=kLoop, calls=%fused_computation.95 | loop fusion | bytes 1245188 | tf_op jit(solution)/shard_map/jit(dynamic_index_in_dim)/squeeze | solution.py:63
  32.3 0.8 %copy.25 = bf16[128,16,1]{1,0,2:T(8,128)(2,1)S(1)} copy(bf16[128,16,1]{2,1,0:T(8,128)(2,1)S(1)} %get-tuple-element.73) | data formatting | bytes 8192
  33.2 0.8 %copy.26 = bf16[128,16,1]{1,0,2:T(8,128)(2,1)S(1)} copy(bf16[128,16,1]{2,1,0:T(8,128)(2,1)S(1)} %get-tuple-element.74) | data formatting | bytes 8192
  34.3 1.1 %bitcast_add_fusion = f32[1216,128]{1,0:T(8,128)S(1)} fusion(f32[1216,128]{1,0:T(8,128)} %collective-permute-done.6, f32[2,1216,128]{2,1,0:T(8,128)S(1)} %bitcast.307, s32[]{:T(128)S(6)} %select_n.98), kind=kLoop, calls=%fused_computation.94 | loop fusion | flops 155648 | bytes 1867780 | tf_op jit(solution)/shard_map/add | solution.py:64
  36.2 2.1 %collective-permute-start.7 = (f32[320,128]{1,0:T(8,128)S(1)}, f32[320,128]{1,0:T(8,128)S(1)}, u32[]{:S(2)}, u32[]{:S(2)}) collective-permute-start(f32[320,128]{1,0:T(8,128)S(1)} %pad_maximum_fusion.3), channel_id=1, source_target_pairs={{0,4},{4,8},{8,12},{12,0},{1,5},{5,9},{9,13},{13,1},{2,6},{6,10},{... | collective-permute-start | bytes 491528 | tf_op jit(solution)/shard_map/ppermute | solution.py:104
  38.3 2.1 %collective-permute-start.8 = (f32[320,128]{1,0:T(8,128)S(1)}, f32[320,128]{1,0:T(8,128)S(1)}, u32[]{:S(2)}, u32[]{:S(2)}) collective-permute-start(f32[320,128]{1,0:T(8,128)S(1)} %pad_maximum_fusion.4), channel_id=1, source_target_pairs={{0,12},{4,0},{8,4},{12,8},{1,13},{5,1},{9,5},{13,9},{2,14},{6,2},{... | collective-permute-start | bytes 491528 | tf_op jit(solution)/shard_map/ppermute | solution.py:104
  40.4 1.0 %collective-permute-start.11 = (f32[304,128]{1,0:T(8,128)}, f32[304,128]{1,0:T(8,128)}, u32[]{:S(2)}, u32[]{:S(2)}) collective-permute-start(f32[304,128]{1,0:T(8,128)} %get-tuple-element.64), channel_id=1, source_target_pairs={{0,8},{4,12},{8,0},{12,4},{1,9},{5,13},{9,1},{13,5},{2,10},{6,14},... | collective-permute-start | bytes 466952 | tf_op jit(solution)/shard_map/ppermute | solution.py:104
  42.0 3.4 %collective-permute-done.7 = f32[320,128]{1,0:T(8,128)S(1)} collective-permute-done((f32[320,128]{1,0:T(8,128)S(1)}, f32[320,128]{1,0:T(8,128)S(1)}, u32[]{:S(2)}, u32[]{:S(2)}) %collective-permute-start.7) | collective-permute-done | bytes 163872 | tf_op jit(solution)/shard_map/ppermute | solution.py:104
  45.5 2.5 %collective-permute-done.8 = f32[320,128]{1,0:T(8,128)S(1)} collective-permute-done((f32[320,128]{1,0:T(8,128)S(1)}, f32[320,128]{1,0:T(8,128)S(1)}, u32[]{:S(2)}, u32[]{:S(2)}) %collective-permute-start.8) | collective-permute-done | bytes 163872 | tf_op jit(solution)/shard_map/ppermute | solution.py:104
  48.8 6.5 %collective-permute-done.11 = f32[304,128]{1,0:T(8,128)} collective-permute-done((f32[304,128]{1,0:T(8,128)}, f32[304,128]{1,0:T(8,128)}, u32[]{:S(2)}, u32[]{:S(2)}) %collective-permute-start.11) | collective-permute-done | bytes 155680 | tf_op jit(solution)/shard_map/ppermute | solution.py:104
  55.3 0.9 %fusion.45 = (bf16[304,128]{1,0:T(8,128)(2,1)S(1)}, f32[304,128]{1,0:T(8,128)S(1)}) fusion(f32[320,128]{1,0:T(8,128)S(1)} %collective-permute-done.8, f32[304,128]{1,0:T(8,128)} %collective-permute-done.11, f32[320,128]{1,0:T(8,128)S(1)} %collective-permute-done.7, f32[4,304,128]{2,1,0:T(8,128)S(1)} %bitcast.324, s32[]{:T(128)S(6)} %select_n.106), kind=kLoop, calls=%fused_computation.195 | loop fusion | flops 155648 | bytes 856068 | tf_op jit(solution)/shard_map/convert_element_type | solution.py:73
  56.2 1.7 %collective-permute-start.12 = (bf16[304,128]{1,0:T(8,128)(2,1)S(1)}, bf16[304,128]{1,0:T(8,128)(2,1)S(1)}, u32[]{:S(2)}, u32[]{:S(2)}) collective-permute-start(bf16[304,128]{1,0:T(8,128)(2,1)S(1)} %get-tuple-element.13), channel_id=1, source_target_pairs={{0,12},{4,0},{8,4},{12,8},{1,13},{5,1},{9,5},{13,9},{2,14},{6,2},{... | collective-permute-start | bytes 233480 | tf_op jit(solution)/shard_map/ppermute | solution.py:76
  58.9 0.9 %fusion.47 = (bf16[128,16,128]{0,2,1:T(8,128)(2,1)S(1)}, bf16[128,16,128]{0,2,1:T(8,128)(2,1)S(1)}, bf16[128,16,128]{0,2,1:T(8,128)(2,1)S(1)}, bf16[128,16,128]{...) fusion(bf16[128,18,130]{0,2,1:T(8,128)(2,1)S(1)} %maximum_selec, ...), kind=kLoop, calls=%fused_computation.197 | loop fusion | bytes 9437184 | tf_op jit(solution)/shard_map/slice | solution.py:37
  62.4 1.1 %fusion.2 = bf16[128,2048]{1,0:T(8,128)(2,1)} fusion(f32[128,2048]{1,0:T(8,128)S(1)} %convolution_add_fusion.9, bf16[128,2048]{0,1:T(8,128)(2,1)S(1)} %bitcast.347, bf16[3,3,128,128]{2,3,1,0:T(8,128)(2,1)S(1)} %get-tuple-element.68), kind=kOutput, calls=%fused_computation.38 | convolution fusion | flops 67633152 | bytes 2129920 | tf_op jit(solution)/shard_map/dot_general | solution.py:50
  63.6 0.9 %fusion.46 = (bf16[128,16,128]{0,2,1:T(8,128)(2,1)S(1)}, bf16[128,16,128]{0,2,1:T(8,128)(2,1)S(1)}, bf16[128,16,128]{0,2,1:T(8,128)(2,1)S(1)}, bf16[128,16,128]{...) fusion(bf16[128,18,130]{0,2,1:T(8,128)(2,1)S(1)} %maximum_selec, ...), kind=kLoop, calls=%fused_computation.196 | loop fusion | bytes 9437184 | tf_op jit(solution)/shard_map/slice | solution.py:37
  64.5 1.6 %collective-permute-start.16 = (bf16[128,2048]{1,0:T(8,128)(2,1)}, bf16[128,2048]{1,0:T(8,128)(2,1)}, u32[]{:S(2)}, u32[]{:S(2)}) collective-permute-start(bf16[128,2048]{1,0:T(8,128)(2,1)} %fusion.2), channel_id=1, source_target_pairs={{0,2},{2,0},{1,3},{3,1},{4,6},{6,4},{5,7},{7,5},{8,10},{10,8},{9,1... | collective-permute-start | bytes 1572872 | tf_op jit(solution)/shard_map/ppermute | solution.py:198
  69.3 1.1 %collective-permute-done.15 = f32[1216,128]{1,0:T(8,128)S(1)} collective-permute-done((f32[1216,128]{1,0:T(8,128)S(1)}, f32[1216,128]{1,0:T(8,128)S(1)}, u32[]{:S(2)}, u32[]{:S(2)}) %collective-permute-start.15) | collective-permute-done | bytes 622624 | tf_op jit(solution)/shard_map/ppermute | solution.py:76
  71.6 1.2 %fusion.6 = f32[3,3,128,256]{3,2,1,0:T(8,128)} fusion(s32[]{:T(128)S(6)} %select_n.114, f32[3,3,128,256]{3,2,1,0:T(8,128)S(1)} %reshape.265), kind=kLoop, calls=%fused_computation.63 | loop fusion | flops 294912 | bytes 2359300 | tf_op jit(solution)/shard_map/concatenate | solution.py:184
  72.8 5.2 %collective-permute-done.16 = bf16[128,2048]{1,0:T(8,128)(2,1)} collective-permute-done((bf16[128,2048]{1,0:T(8,128)(2,1)}, bf16[128,2048]{1,0:T(8,128)(2,1)}, u32[]{:S(2)}, u32[]{:S(2)}) %collective-permute-start.16) | collective-permute-done | bytes 524320 | tf_op jit(solution)/shard_map/ppermute | solution.py:198
  77.9 1.2 %fusion.21 = bf16[16,8,16,128]{3,1,2,0:T(8,128)(2,1)S(1)} fusion(f32[128,2048]{1,0:T(8,128)S(1)} %convolution_add_fusion, bf16[128,2048]{1,0:T(8,128)(2,1)} %collective-permute-done.16), kind=kLoop, calls=%fused_computation.96 | loop fusion | flops 786432 | bytes 2097152
  79.1 0.9 %copy.30 = bf16[16,8,16,128]{3,2,1,0:T(8,128)(2,1)} copy(bf16[16,8,16,128]{3,1,2,0:T(8,128)(2,1)S(1)} %fusion.21) | data formatting | bytes 1048576
  (117 shorter events, 22.4 us)
Async XLA Ops:
  0.6 8.4 %copy-start.1 = (bf16[128,16,128]{2,1,0:T(8,128)(2,1)S(1)}, bf16[128,16,128]{2,1,0:T(8,128)(2,1)}, u32[]{:S(2)}) copy-start(bf16[128,16,128]{2,1,0:T(8,128)(2,1)} %param.5) | copy-start | bytes 1572868
  2.2 16.6 %collective-permute-start.5 = (bf16[128,16,128]{0,2,1:T(8,128)(2,1)S(1)}, bf16[128,16,128]{0,2,1:T(8,128)(2,1)}, u32[]{:S(2)}, u32[]{:S(2)}) collective-permute-start(bf16[128,16,128]{0,2,1:T(8,128)(2,1)S(1)} %copy.12), channel_id=1, source_target_pairs={{0,2},{2,0},{1,3},{3,1},{4,6},{6,4},{5,7},{7,5},{8,10},{10,8},{9,1... | collective-permute-start | bytes 1572872 | tf_op jit(solution)/shard_map/ppermute | solution.py:142
  5.2 5.5 %collective-permute-start = (bf16[128,16,1]{0,2,1:T(2,128)(2,1)S(1)}, bf16[128,16,1]{0,2,1:T(2,128)(2,1)S(1)}, u32[]{:S(2)}, u32[]{:S(2)}) collective-permute-start(bf16[128,16,1]{0,2,1:T(2,128)(2,1)S(1)} %get-tuple-element.75), channel_id=1, source_target_pairs={{0,4},{4,8},{8,12},{12,0},{1,5},{5,9},{9,13},{13,1},{2,6},{6,10},{... | collective-permute-start | bytes 12296 | tf_op jit(solution)/shard_map/ppermute | solution.py:14
  6.8 3.9 %collective-permute-start.1 = (bf16[128,16,1]{0,2,1:T(2,128)(2,1)S(1)}, bf16[128,16,1]{0,2,1:T(2,128)(2,1)S(1)}, u32[]{:S(2)}, u32[]{:S(2)}) collective-permute-start(bf16[128,16,1]{0,2,1:T(2,128)(2,1)S(1)} %get-tuple-element.76), channel_id=1, source_target_pairs={{4,0},{8,4},{12,8},{0,12},{5,1},{9,5},{13,9},{1,13},{6,2},{10,6},{... | collective-permute-start | bytes 12296 | tf_op jit(solution)/shard_map/ppermute | solution.py:15
  10.7 1.3 %collective-permute-start.2 = (bf16[128,1,130]{0,2,1:T(8,128)(2,1)S(1)}, bf16[128,1,130]{0,2,1:T(8,128)(2,1)S(1)}, u32[]{:S(2)}, u32[]{:S(2)}) collective-permute-start(bf16[128,1,130]{0,2,1:T(8,128)(2,1)S(1)} %get-tuple-element.71), channel_id=1, source_target_pairs={{0,1},{1,0},{2,3},{3,2},{4,5},{5,4},{6,7},{7,6},{8,9},{9,8},{10,11... | collective-permute-start | bytes 99848 | tf_op jit(solution)/shard_map/ppermute | solution.py:14
  10.8 1.4 %collective-permute-start.3 = (bf16[128,1,130]{0,2,1:T(8,128)(2,1)S(1)}, bf16[128,1,130]{0,2,1:T(8,128)(2,1)S(1)}, u32[]{:S(2)}, u32[]{:S(2)}) collective-permute-start(bf16[128,1,130]{0,2,1:T(8,128)(2,1)S(1)} %get-tuple-element.72), channel_id=1, source_target_pairs={{1,0},{0,1},{3,2},{2,3},{5,4},{4,5},{7,6},{6,7},{9,8},{8,9},{11,10... | collective-permute-start | bytes 99848 | tf_op jit(solution)/shard_map/ppermute | solution.py:15
  12.5 1.5 %copy-start = (bf16[3,3,128,256]{3,2,1,0:T(8,128)(2,1)S(1)}, bf16[3,3,128,256]{3,2,1,0:T(8,128)(2,1)}, u32[]{:S(2)}) copy-start(bf16[3,3,128,256]{3,2,1,0:T(8,128)(2,1)} %param.6) | copy-start | bytes 1769476
  13.5 5.2 %collective-permute-start.4 = (bf16[128,292]{0,1:T(8,128)(2,1)S(1)}, bf16[128,292]{0,1:T(8,128)(2,1)S(1)}, u32[]{:S(2)}, u32[]{:S(2)}) collective-permute-start(bf16[128,292]{0,1:T(8,128)(2,1)S(1)} %pad_maximum_fusion.5), channel_id=1, source_target_pairs={{0,2},{2,0},{1,3},{3,1},{4,6},{6,4},{5,7},{7,5},{8,10},{10,8},{9,1... | collective-permute-start | bytes 224264 | tf_op jit(solution)/shard_map/ppermute | solution.py:148
  25.6 0.7 copy-start.2
  31.9 2.4 %collective-permute-start.6 = (f32[1216,128]{1,0:T(8,128)}, f32[1216,128]{1,0:T(8,128)}, u32[]{:S(2)}, u32[]{:S(2)}) collective-permute-start(f32[1216,128]{1,0:T(8,128)} %dynamic-slice_bitcast_fusion), channel_id=1, source_target_pairs={{0,1},{1,0},{2,3},{3,2},{4,5},{5,4},{6,7},{7,6},{8,9},{9,8},{10,11... | collective-permute-start | bytes 1867784 | tf_op jit(solution)/shard_map/ppermute | solution.py:64
  36.2 9.2 %collective-permute-start.7 = (f32[320,128]{1,0:T(8,128)S(1)}, f32[320,128]{1,0:T(8,128)S(1)}, u32[]{:S(2)}, u32[]{:S(2)}) collective-permute-start(f32[320,128]{1,0:T(8,128)S(1)} %pad_maximum_fusion.3), channel_id=1, source_target_pairs={{0,4},{4,8},{8,12},{12,0},{1,5},{5,9},{9,13},{13,1},{2,6},{6,10},{... | collective-permute-start | bytes 491528 | tf_op jit(solution)/shard_map/ppermute | solution.py:104
  38.3 9.7 %collective-permute-start.8 = (f32[320,128]{1,0:T(8,128)S(1)}, f32[320,128]{1,0:T(8,128)S(1)}, u32[]{:S(2)}, u32[]{:S(2)}) collective-permute-start(f32[320,128]{1,0:T(8,128)S(1)} %pad_maximum_fusion.4), channel_id=1, source_target_pairs={{0,12},{4,0},{8,4},{12,8},{1,13},{5,1},{9,5},{13,9},{2,14},{6,2},{... | collective-permute-start | bytes 491528 | tf_op jit(solution)/shard_map/ppermute | solution.py:104
  40.4 14.9 %collective-permute-start.11 = (f32[304,128]{1,0:T(8,128)}, f32[304,128]{1,0:T(8,128)}, u32[]{:S(2)}, u32[]{:S(2)}) collective-permute-start(f32[304,128]{1,0:T(8,128)} %get-tuple-element.64), channel_id=1, source_target_pairs={{0,8},{4,12},{8,0},{12,4},{1,9},{5,13},{9,1},{13,5},{2,10},{6,14},... | collective-permute-start | bytes 466952 | tf_op jit(solution)/shard_map/ppermute | solution.py:104
  48.2 10.3 %collective-permute-start.10 = (bf16[128,1,130]{0,2,1:T(8,128)(2,1)S(1)}, bf16[128,1,130]{0,2,1:T(8,128)(2,1)S(1)}, u32[]{:S(2)}, u32[]{:S(2)}) collective-permute-start(bf16[128,1,130]{0,2,1:T(8,128)(2,1)S(1)} %get-tuple-element.70), channel_id=1, source_target_pairs={{1,0},{0,1},{3,2},{2,3},{5,4},{4,5},{7,6},{6,7},{9,8},{8,9},{11,10... | collective-permute-start | bytes 99848 | tf_op jit(solution)/shard_map/ppermute | solution.py:15
  48.3 10.3 %collective-permute-start.9 = (bf16[128,1,130]{0,2,1:T(8,128)(2,1)S(1)}, bf16[128,1,130]{0,2,1:T(8,128)(2,1)S(1)}, u32[]{:S(2)}, u32[]{:S(2)}) collective-permute-start(bf16[128,1,130]{0,2,1:T(8,128)(2,1)S(1)} %get-tuple-element.69), channel_id=1, source_target_pairs={{0,1},{1,0},{2,3},{3,2},{4,5},{5,4},{6,7},{7,6},{8,9},{9,8},{10,11... | collective-permute-start | bytes 99848 | tf_op jit(solution)/shard_map/ppermute | solution.py:14
  56.2 11.8 %collective-permute-start.12 = (bf16[304,128]{1,0:T(8,128)(2,1)S(1)}, bf16[304,128]{1,0:T(8,128)(2,1)S(1)}, u32[]{:S(2)}, u32[]{:S(2)}) collective-permute-start(bf16[304,128]{1,0:T(8,128)(2,1)S(1)} %get-tuple-element.13), channel_id=1, source_target_pairs={{0,12},{4,0},{8,4},{12,8},{1,13},{5,1},{9,5},{13,9},{2,14},{6,2},{... | collective-permute-start | bytes 233480 | tf_op jit(solution)/shard_map/ppermute | solution.py:76
  57.9 10.1 %collective-permute-start.13 = (bf16[304,128]{1,0:T(8,128)(2,1)S(1)}, bf16[304,128]{1,0:T(8,128)(2,1)S(1)}, u32[]{:S(2)}, u32[]{:S(2)}) collective-permute-start(bf16[304,128]{1,0:T(8,128)(2,1)S(1)} %get-tuple-element.13), channel_id=1, source_target_pairs={{0,8},{4,12},{8,0},{12,4},{1,9},{5,13},{9,1},{13,5},{2,10},{6,14},... | collective-permute-start | bytes 233480 | tf_op jit(solution)/shard_map/ppermute | solution.py:76
  57.9 10.2 %collective-permute-start.14 = (bf16[304,128]{1,0:T(8,128)(2,1)S(1)}, bf16[304,128]{1,0:T(8,128)(2,1)S(1)}, u32[]{:S(2)}, u32[]{:S(2)}) collective-permute-start(bf16[304,128]{1,0:T(8,128)(2,1)S(1)} %get-tuple-element.13), channel_id=1, source_target_pairs={{0,4},{4,8},{8,12},{12,0},{1,5},{5,9},{9,13},{13,1},{2,6},{6,10},{... | collective-permute-start | bytes 233480 | tf_op jit(solution)/shard_map/ppermute | solution.py:76
  64.5 13.4 %collective-permute-start.16 = (bf16[128,2048]{1,0:T(8,128)(2,1)}, bf16[128,2048]{1,0:T(8,128)(2,1)}, u32[]{:S(2)}, u32[]{:S(2)}) collective-permute-start(bf16[128,2048]{1,0:T(8,128)(2,1)} %fusion.2), channel_id=1, source_target_pairs={{0,2},{2,0},{1,3},{3,1},{4,6},{6,4},{5,7},{7,5},{8,10},{10,8},{9,1... | collective-permute-start | bytes 1572872 | tf_op jit(solution)/shard_map/ppermute | solution.py:198
  68.3 2.1 %collective-permute-start.15 = (f32[1216,128]{1,0:T(8,128)S(1)}, f32[1216,128]{1,0:T(8,128)S(1)}, u32[]{:S(2)}, u32[]{:S(2)}) collective-permute-start(f32[1216,128]{1,0:T(8,128)S(1)} %bitcast.321), channel_id=1, source_target_pairs={{0,1},{1,0},{2,3},{3,2},{4,5},{5,4},{6,7},{7,6},{8,9},{9,8},{10,11... | collective-permute-start | bytes 1867784 | tf_op jit(solution)/shard_map/ppermute | solution.py:76

commit v27 on v19

--- a/solution.py
+++ b/solution.py
@@ -146,7 +146,7 @@
     for shift in range(1, chan_count):
         pairs = [(i, (i - shift) % chan_count) for i in range(chan_count)]
         border = lax.ppermute(own_border, "chan", pairs)
-        blocks.append(lax.optimization_barrier(with_border(raw_blocks[shift - 1], border)))
+        blocks.append(with_border(raw_blocks[shift - 1], border))
     kernel_cols = []
     for shift in range(chan_count):
         source = (chan_index + shift) % chan_count

time: 70.1 us -> 71.7 us (1.023)
  waiting for transfers between devices: 17 us -> 21.5 us
  starting transfers between devices: 17.9 us -> 14.3 us
  local copies, waits for them, and re-layouts: 10.3 us -> 12.5 us
  other arithmetic: 7.67 us -> 5.9 us
    ppermute x3, starting transfers between devices: 4.99 us -> 2.15 us  [sum_start(): moved = lax.ppermute(piece, 'lon', pairs)]
    slice x4 -> x6, local copies, waits for them, and re-layouts: 3.74 us -> 5.99 us  [window_of(): field[:, first_row:first_row + row_count, first_col:first_col + column_co...]
    concatenate x1, other arithmetic: 2.53 us -> 0.37 us  [local(): input_local = jnp.concatenate(blocks, axis=0)]
    ppermute x3, waiting for transfers between devices: 2.2 us -> 4.25 us  [padded_2(): before = lax.ppermute(last, axis, up)]
    ppermute x3, waiting for transfers between devices: 0.17 us -> 1.94 us  [padded_2(): after = lax.ppermute(initial, axis, down)]
    ppermute x3, waiting for transfers between devices: 5.21 us -> 6.65 us  [sum_start(): moved = lax.ppermute(piece, 'lon', pairs)]
    ppermute x3, starting transfers between devices: 2.2 us -> 1 us  [padded_2(): before = lax.ppermute(last, axis, up)]
    ppermute x3, starting transfers between devices: 2.82 us -> 3.8 us  [padded_2(): after = lax.ppermute(initial, axis, down)]
  transfers between devices with their start and end apart: 17 -> 17, of which waited for: 10 -> 11; matrix products, arithmetic and copies ran while one was open for 25% -> 24% of each run, Pallas kernels for 0% -> 0%
where the time goes in v27:
time: 71.7 us; the launch traced here: 71.4 us
  waiting for transfers between devices  21.5 us (30%)
  matrix products  15.7 us (22%)
  starting transfers between devices  14.3 us (20%)
  local copies, waits for them, and re-layouts  12.5 us (17%)
  other arithmetic  5.9 us (8%)
  between operations  1.48 us (2%)
    dot_general x36, matrix products, conv_taps(): jnp.dot(kernel[tap_row, tap_col], window, preferred_element_type=jnp.floa...  12.8 us
    ppermute x3, waiting for transfers between devices, sum_start(): moved = lax.ppermute(piece, 'lon', pairs)  6.65 us
    slice x6, local copies, waits for them, and re-layouts, window_of(): field[:, first_row:first_row + row_count, first_col:first_col + column_co...  5.99 us
    ppermute x1, waiting for transfers between devices, local(): received.append(lax.ppermute(outgoing[shift - 1], 'chan', pairs))  5.4 us
    ppermute x3, waiting for transfers between devices, padded_2(): before = lax.ppermute(last, axis, up)  4.25 us
    ppermute x3, starting transfers between devices, padded_2(): after = lax.ppermute(initial, axis, down)  3.8 us
    unnamed x11, local copies, waits for them, and re-layouts  3.51 us
    ppermute x1, starting transfers between devices, local(): raw_blocks.append(lax.ppermute(inputs, 'chan', pairs))  3 us
  transfers between devices with their start and end apart: 17, of which 11 were waited for; matrix products, arithmetic and copies ran while one was open for 24% of the time, Pallas kernels for 0%

profile of v27, /device:TPU:0, one launch (start us, length us, event | category | flops | bytes accessed | tf_op | source)
XLA Modules:
  0.0 71.4 jit_solution(17106824594696634721)
XLA Ops:
  0.6 1.5 %copy.20 = bf16[128,16,128]{0,2,1:T(8,128)(2,1)S(1)} copy(bf16[128,16,128]{2,1,0:T(8,128)(2,1)} %param.4) | data formatting | bytes 1048576 | tf_op args[0]
  2.2 3.0 %collective-permute-start.5 = (bf16[128,16,128]{0,2,1:T(8,128)(2,1)S(1)}, bf16[128,16,128]{0,2,1:T(8,128)(2,1)S(1)}, u32[]{:S(2)}, u32[]{:S(2)}) collective-permute-start(bf16[128,16,128]{0,2,1:T(8,128)(2,1)S(1)} %copy.20), channel_id=1, source_target_pairs={{0,2},{2,0},{1,3},{3,1},{4,6},{6,4},{5,7},{7,5},{8,10},{10,8},{9,1... | collective-permute-start | bytes 1572872 | tf_op jit(solution)/shard_map/ppermute | solution.py:142
  5.2 3.7 %collective-permute-start.1 = (bf16[128,16,1]{0,2,1:T(2,128)(2,1)S(1)}, bf16[128,16,1]{0,2,1:T(2,128)(2,1)S(1)}, u32[]{:S(2)}, u32[]{:S(2)}) collective-permute-start(bf16[128,16,1]{0,2,1:T(2,128)(2,1)S(1)} %get-tuple-element.77), channel_id=1, source_target_pairs={{4,0},{8,4},{12,8},{0,12},{5,1},{9,5},{13,9},{1,13},{6,2},{10,6},{... | collective-permute-start | bytes 12296 | tf_op jit(solution)/shard_map/ppermute | solution.py:15
  9.0 1.2 %collective-permute-done.1 = bf16[128,16,1]{0,2,1:T(2,128)(2,1)S(1)} collective-permute-done((bf16[128,16,1]{0,2,1:T(2,128)(2,1)S(1)}, bf16[128,16,1]{0,2,1:T(2,128)(2,1)S(1)}, u32[]{:S(2)}, u32[]{:S(2)}) %collective-permute-start.1) | collective-permute-done | bytes 4128 | tf_op jit(solution)/shard_map/ppermute | solution.py:15
  10.2 4.1 %collective-permute-done = bf16[128,16,1]{0,2,1:T(2,128)(2,1)S(1)} collective-permute-done((bf16[128,16,1]{0,2,1:T(2,128)(2,1)S(1)}, bf16[128,16,1]{0,2,1:T(2,128)(2,1)S(1)}, u32[]{:S(2)}, u32[]{:S(2)}) %collective-permute-start) | collective-permute-done | bytes 4128 | tf_op jit(solution)/shard_map/ppermute | solution.py:14
  14.9 0.7 collective-permute-done.3
  16.1 0.8 %fusion.53 = (bf16[128,16,128]{0,2,1:T(8,128)(2,1)S(1)}, bf16[128,16,128]{0,2,1:T(8,128)(2,1)S(1)}, bf16[128,16,128]{0,2,1:T(8,128)(2,1)S(1)}, bf16[128,16,128]{...) fusion(bf16[128,18,130]{0,2,1:T(8,128)(2,1)S(1)} %maximum_selec, ...), kind=kLoop, calls=%fused_computation.185 | loop fusion | bytes 9437184 | tf_op jit(solution)/shard_map/slice | solution.py:37
  17.0 0.6 collective-permute-start.4
  20.4 1.3 %collective-permute-done.4 = bf16[128,292]{0,1:T(8,128)(2,1)S(1)} collective-permute-done((bf16[128,292]{0,1:T(8,128)(2,1)S(1)}, bf16[128,292]{0,1:T(8,128)(2,1)S(1)}, u32[]{:S(2)}, u32[]{:S(2)}) %collective-permute-start.4) | collective-permute-done | bytes 74784 | tf_op jit(solution)/shard_map/ppermute | solution.py:148
  24.6 2.6 %fusion.49 = (bf16[256,16,128]{0,2,1:T(8,128)(2,1)S(1)}, bf16[256,16,128]{0,2,1:T(8,128)(2,1)S(1)}, bf16[256,16,128]{0,2,1:T(8,128)(2,1)S(1)}, bf16[256,16,128]{...) fusion(bf16[256,18,130]{0,2,1:T(8,128)(2,1)S(1)} %maximum_maxim, ...), kind=kLoop, calls=%fused_computation.181 | loop fusion | bytes 18874368 | tf_op jit(solution)/shard_map/slice | solution.py:37
  28.9 1.0 %convert_reduce_fusion = (f32[128]{0:T(128)S(1)}, bf16[128,2048]{1,0:T(8,128)(2,1)S(1)}) fusion(f32[128]{0:T(128)S(1)} %copy-done.2, f32[128,2048]{1,0:T(8,128)S(1)} %convolution_add_fusion.21, f32[128,2048]{1,0:T(8,128)S(1)} %convolution_add_fusion.17, bf16[128,2048]{0,1:T(8,128)(2,1)S(1)} %bitcast.358, bf16[3,3,128,256]{3,2,1,0:T(8,128)(2,1)S(1)} %copy-done, ...), kind=kOutput, calls=%fused_computation.66 | convolution fusion | flops 71040896 | bytes 4228104 | tf_op jit(solution)/shard_map/dot_general | solution.py:50
  33.1 0.6 copy.40
  34.1 0.8 %slice_reduce_fusion.1 = (bf16[128,16]{1,0:T(8,128)(2,1)S(1)}, bf16[128,16]{1,0:T(8,128)(2,1)S(1)}) fusion(bf16[128,16,128]{2,1,0:T(8,128)(2,1)S(1)} %bitcast.305), kind=kLoop, calls=%fused_computation.75 | loop fusion | bytes 16384 | tf_op jit(solution)/shard_map/slice | solution.py:179
  35.1 0.9 %collective-permute-done.6 = f32[1216,128]{1,0:T(8,128)} collective-permute-done((f32[1216,128]{1,0:T(8,128)S(1)}, f32[1216,128]{1,0:T(8,128)}, u32[]{:S(2)}, u32[]{:S(2)}) %collective-permute-start.6) | collective-permute-done | bytes 622624 | tf_op jit(solution)/shard_map/ppermute | solution.py:64
  36.1 1.1 %bitcast_add_fusion = f32[1216,128]{1,0:T(8,128)S(1)} fusion(f32[1216,128]{1,0:T(8,128)} %collective-permute-done.6, f32[2,1216,128]{2,1,0:T(8,128)S(1)} %bitcast.308, s32[]{:T(128)S(6)} %select_n.98), kind=kLoop, calls=%fused_computation.69 | loop fusion | flops 155648 | bytes 1867780 | tf_op jit(solution)/shard_map/add | solution.py:64
  37.3 1.0 %collective-permute-start.8 = (bf16[320,128]{1,0:T(8,128)(2,1)S(1)}, bf16[320,128]{1,0:T(8,128)(2,1)S(1)}, u32[]{:S(2)}, u32[]{:S(2)}) collective-permute-start(bf16[320,128]{1,0:T(8,128)(2,1)S(1)} %pad_maximum_fusion.5), channel_id=1, source_target_pairs={{0,12},{4,0},{8,4},{12,8},{1,13},{5,1},{9,5},{13,9},{2,14},{6,2},{... | collective-permute-start | bytes 245768 | tf_op jit(solution)/shard_map/ppermute | solution.py:104
  38.3 1.1 %collective-permute-start.7 = (bf16[320,128]{1,0:T(8,128)(2,1)S(1)}, bf16[320,128]{1,0:T(8,128)(2,1)S(1)}, u32[]{:S(2)}, u32[]{:S(2)}) collective-permute-start(bf16[320,128]{1,0:T(8,128)(2,1)S(1)} %pad_maximum_fusion.4), channel_id=1, source_target_pairs={{0,4},{4,8},{8,12},{12,0},{1,5},{5,9},{9,13},{13,1},{2,6},{6,10},{... | collective-permute-start | bytes 245768 | tf_op jit(solution)/shard_map/ppermute | solution.py:104
  40.0 1.8 %collective-permute-done.8 = bf16[320,128]{1,0:T(8,128)(2,1)S(1)} collective-permute-done((bf16[320,128]{1,0:T(8,128)(2,1)S(1)}, bf16[320,128]{1,0:T(8,128)(2,1)S(1)}, u32[]{:S(2)}, u32[]{:S(2)}) %collective-permute-start.8) | collective-permute-done | bytes 81952 | tf_op jit(solution)/shard_map/ppermute | solution.py:104
  42.0 3.2 %collective-permute-done.7 = bf16[320,128]{1,0:T(8,128)(2,1)S(1)} collective-permute-done((bf16[320,128]{1,0:T(8,128)(2,1)S(1)}, bf16[320,128]{1,0:T(8,128)(2,1)S(1)}, u32[]{:S(2)}, u32[]{:S(2)}) %collective-permute-start.7) | collective-permute-done | bytes 81952 | tf_op jit(solution)/shard_map/ppermute | solution.py:104
  46.0 1.6 %collective-permute-done.11 = bf16[304,128]{1,0:T(8,128)(2,1)S(1)} collective-permute-done((bf16[304,128]{1,0:T(8,128)(2,1)S(1)}, bf16[304,128]{1,0:T(8,128)(2,1)S(1)}, u32[]{:S(2)}, u32[]{:S(2)}) %collective-permute-start.11) | collective-permute-done | bytes 77856 | tf_op jit(solution)/shard_map/ppermute | solution.py:104
  47.7 1.7 %collective-permute-start.12 = (bf16[304,128]{1,0:T(8,128)(2,1)S(1)}, bf16[304,128]{1,0:T(8,128)(2,1)S(1)}, u32[]{:S(2)}, u32[]{:S(2)}) collective-permute-start(bf16[304,128]{1,0:T(8,128)(2,1)S(1)} %get-tuple-element.15), channel_id=1, source_target_pairs={{0,12},{4,0},{8,4},{12,8},{1,13},{5,1},{9,5},{13,9},{2,14},{6,2},{... | collective-permute-start | bytes 233480 | tf_op jit(solution)/shard_map/ppermute | solution.py:76
  49.4 0.6 collective-permute-start.14
  50.3 0.9 %fusion.51 = (bf16[128,16,128]{0,2,1:T(8,128)(2,1)S(1)}, bf16[128,16,128]{0,2,1:T(8,128)(2,1)S(1)}, bf16[128,16,128]{0,2,1:T(8,128)(2,1)S(1)}, bf16[128,16,128]{...) fusion(bf16[128,18,130]{0,2,1:T(8,128)(2,1)S(1)} %maximum_selec, ...), kind=kLoop, calls=%fused_computation.183 | loop fusion | bytes 9437184 | tf_op jit(solution)/shard_map/slice | solution.py:37
  53.9 1.1 %fusion.5 = bf16[128,2048]{1,0:T(8,128)(2,1)} fusion(f32[128,2048]{1,0:T(8,128)S(1)} %convolution_add_fusion.9, bf16[128,2048]{0,1:T(8,128)(2,1)S(1)} %bitcast.341, bf16[3,3,128,128]{2,3,1,0:T(8,128)(2,1)S(1)} %get-tuple-element.67), kind=kOutput, calls=%fused_computation.38 | convolution fusion | flops 67633152 | bytes 2129920 | tf_op jit(solution)/shard_map/dot_general | solution.py:50
  55.0 0.9 %fusion.50 = (bf16[128,16,128]{0,2,1:T(8,128)(2,1)S(1)}, bf16[128,16,128]{0,2,1:T(8,128)(2,1)S(1)}, bf16[128,16,128]{0,2,1:T(8,128)(2,1)S(1)}, bf16[128,16,128]{...) fusion(bf16[128,18,130]{0,2,1:T(8,128)(2,1)S(1)} %maximum_selec, ...), kind=kLoop, calls=%fused_computation.182 | loop fusion | bytes 9437184 | tf_op jit(solution)/shard_map/slice | solution.py:37
  56.0 1.3 %collective-permute-start.16 = (bf16[128,2048]{1,0:T(8,128)(2,1)}, bf16[128,2048]{1,0:T(8,128)(2,1)}, u32[]{:S(2)}, u32[]{:S(2)}) collective-permute-start(bf16[128,2048]{1,0:T(8,128)(2,1)} %fusion.5), channel_id=1, source_target_pairs={{0,2},{2,0},{1,3},{3,1},{4,6},{6,4},{5,7},{7,5},{8,10},{10,8},{9,1... | collective-permute-start | bytes 1572872 | tf_op jit(solution)/shard_map/ppermute | solution.py:198
  60.5 1.1 %collective-permute-done.15 = f32[1216,128]{1,0:T(8,128)S(1)} collective-permute-done((f32[1216,128]{1,0:T(8,128)S(1)}, f32[1216,128]{1,0:T(8,128)S(1)}, u32[]{:S(2)}, u32[]{:S(2)}) %collective-permute-start.15) | collective-permute-done | bytes 622624 | tf_op jit(solution)/shard_map/ppermute | solution.py:76
  61.9 0.5 slice.487
  62.8 1.2 %fusion.9 = f32[3,3,128,256]{3,2,1,0:T(8,128)} fusion(s32[]{:T(128)S(6)} %select_n.114, f32[3,3,128,256]{3,2,1,0:T(8,128)S(1)} %reshape.240), kind=kLoop, calls=%fused_computation.48 | loop fusion | flops 294912 | bytes 2359300 | tf_op jit(solution)/shard_map/concatenate | solution.py:184
  64.0 5.4 %collective-permute-done.16 = bf16[128,2048]{1,0:T(8,128)(2,1)} collective-permute-done((bf16[128,2048]{1,0:T(8,128)(2,1)}, bf16[128,2048]{1,0:T(8,128)(2,1)}, u32[]{:S(2)}, u32[]{:S(2)}) %collective-permute-start.16) | collective-permute-done | bytes 524320 | tf_op jit(solution)/shard_map/ppermute | solution.py:198
  69.4 1.2 %fusion.16 = bf16[16,8,16,128]{3,1,2,0:T(8,128)(2,1)S(1)} fusion(f32[128,2048]{1,0:T(8,128)S(1)} %convolution_add_fusion, bf16[128,2048]{1,0:T(8,128)(2,1)} %collective-permute-done.16), kind=kLoop, calls=%fused_computation.73 | loop fusion | flops 786432 | bytes 2097152
  70.5 0.9 %copy.42 = bf16[16,8,16,128]{3,2,1,0:T(8,128)(2,1)} copy(bf16[16,8,16,128]{3,1,2,0:T(8,128)(2,1)S(1)} %fusion.16) | data formatting | bytes 1048576
  (118 shorter events, 20.4 us)
Async XLA Ops:
  0.6 8.2 %copy-start.1 = (bf16[128,16,128]{2,1,0:T(8,128)(2,1)S(1)}, bf16[128,16,128]{2,1,0:T(8,128)(2,1)}, u32[]{:S(2)}) copy-start(bf16[128,16,128]{2,1,0:T(8,128)(2,1)} %param.5) | copy-start | bytes 1572868
  2.2 19.5 %collective-permute-start.5 = (bf16[128,16,128]{0,2,1:T(8,128)(2,1)S(1)}, bf16[128,16,128]{0,2,1:T(8,128)(2,1)S(1)}, u32[]{:S(2)}, u32[]{:S(2)}) collective-permute-start(bf16[128,16,128]{0,2,1:T(8,128)(2,1)S(1)} %copy.20), channel_id=1, source_target_pairs={{0,2},{2,0},{1,3},{3,1},{4,6},{6,4},{5,7},{7,5},{8,10},{10,8},{9,1... | collective-permute-start | bytes 1572872 | tf_op jit(solution)/shard_map/ppermute | solution.py:142
  5.2 5.0 %collective-permute-start.1 = (bf16[128,16,1]{0,2,1:T(2,128)(2,1)S(1)}, bf16[128,16,1]{0,2,1:T(2,128)(2,1)S(1)}, u32[]{:S(2)}, u32[]{:S(2)}) collective-permute-start(bf16[128,16,1]{0,2,1:T(2,128)(2,1)S(1)} %get-tuple-element.77), channel_id=1, source_target_pairs={{4,0},{8,4},{12,8},{0,12},{5,1},{9,5},{13,9},{1,13},{6,2},{10,6},{... | collective-permute-start | bytes 12296 | tf_op jit(solution)/shard_map/ppermute | solution.py:15
  8.8 5.4 %collective-permute-start = (bf16[128,16,1]{0,2,1:T(2,128)(2,1)S(1)}, bf16[128,16,1]{0,2,1:T(2,128)(2,1)S(1)}, u32[]{:S(2)}, u32[]{:S(2)}) collective-permute-start(bf16[128,16,1]{0,2,1:T(2,128)(2,1)S(1)} %get-tuple-element.76), channel_id=1, source_target_pairs={{0,4},{4,8},{8,12},{12,0},{1,5},{5,9},{9,13},{13,1},{2,6},{6,10},{... | collective-permute-start | bytes 12296 | tf_op jit(solution)/shard_map/ppermute | solution.py:14
  14.3 1.3 %collective-permute-start.3 = (bf16[128,1,130]{0,2,1:T(8,128)(2,1)S(1)}, bf16[128,1,130]{0,2,1:T(8,128)(2,1)S(1)}, u32[]{:S(2)}, u32[]{:S(2)}) collective-permute-start(bf16[128,1,130]{0,2,1:T(8,128)(2,1)S(1)} %get-tuple-element.73), channel_id=1, source_target_pairs={{1,0},{0,1},{3,2},{2,3},{5,4},{4,5},{7,6},{6,7},{9,8},{8,9},{11,10... | collective-permute-start | bytes 99848 | tf_op jit(solution)/shard_map/ppermute | solution.py:15
  14.4 1.4 %collective-permute-start.2 = (bf16[128,1,130]{0,2,1:T(8,128)(2,1)S(1)}, bf16[128,1,130]{0,2,1:T(8,128)(2,1)S(1)}, u32[]{:S(2)}, u32[]{:S(2)}) collective-permute-start(bf16[128,1,130]{0,2,1:T(8,128)(2,1)S(1)} %get-tuple-element.72), channel_id=1, source_target_pairs={{0,1},{1,0},{2,3},{3,2},{4,5},{5,4},{6,7},{7,6},{8,9},{9,8},{10,11... | collective-permute-start | bytes 99848 | tf_op jit(solution)/shard_map/ppermute | solution.py:14
  16.1 1.5 %copy-start = (bf16[3,3,128,256]{3,2,1,0:T(8,128)(2,1)S(1)}, bf16[3,3,128,256]{3,2,1,0:T(8,128)(2,1)}, u32[]{:S(2)}) copy-start(bf16[3,3,128,256]{3,2,1,0:T(8,128)(2,1)} %param.6) | copy-start | bytes 1769476
  17.0 4.6 %collective-permute-start.4 = (bf16[128,292]{0,1:T(8,128)(2,1)S(1)}, bf16[128,292]{0,1:T(8,128)(2,1)S(1)}, u32[]{:S(2)}, u32[]{:S(2)}) collective-permute-start(bf16[128,292]{0,1:T(8,128)(2,1)S(1)} %pad_maximum_fusion.6), channel_id=1, source_target_pairs={{0,2},{2,0},{1,3},{3,1},{4,6},{6,4},{5,7},{7,5},{8,10},{10,8},{9,1... | collective-permute-start | bytes 224264 | tf_op jit(solution)/shard_map/ppermute | solution.py:148
  28.3 0.7 copy-start.2
  33.8 2.2 %collective-permute-start.6 = (f32[1216,128]{1,0:T(8,128)S(1)}, f32[1216,128]{1,0:T(8,128)}, u32[]{:S(2)}, u32[]{:S(2)}) collective-permute-start(f32[1216,128]{1,0:T(8,128)S(1)} %dynamic-slice_bitcast_fusion), channel_id=1, source_target_pairs={{0,1},{1,0},{2,3},{3,2},{4,5},{5,4},{6,7},{7,6},{8,9},{9,8},{10,11... | collective-permute-start | bytes 1867784 | tf_op jit(solution)/shard_map/ppermute | solution.py:64
  37.3 4.5 %collective-permute-start.8 = (bf16[320,128]{1,0:T(8,128)(2,1)S(1)}, bf16[320,128]{1,0:T(8,128)(2,1)S(1)}, u32[]{:S(2)}, u32[]{:S(2)}) collective-permute-start(bf16[320,128]{1,0:T(8,128)(2,1)S(1)} %pad_maximum_fusion.5), channel_id=1, source_target_pairs={{0,12},{4,0},{8,4},{12,8},{1,13},{5,1},{9,5},{13,9},{2,14},{6,2},{... | collective-permute-start | bytes 245768 | tf_op jit(solution)/shard_map/ppermute | solution.py:104
  38.3 6.9 %collective-permute-start.7 = (bf16[320,128]{1,0:T(8,128)(2,1)S(1)}, bf16[320,128]{1,0:T(8,128)(2,1)S(1)}, u32[]{:S(2)}, u32[]{:S(2)}) collective-permute-start(bf16[320,128]{1,0:T(8,128)(2,1)S(1)} %pad_maximum_fusion.4), channel_id=1, source_target_pairs={{0,4},{4,8},{8,12},{12,0},{1,5},{5,9},{9,13},{13,1},{2,6},{6,10},{... | collective-permute-start | bytes 245768 | tf_op jit(solution)/shard_map/ppermute | solution.py:104
  39.9 7.7 %collective-permute-start.11 = (bf16[304,128]{1,0:T(8,128)(2,1)S(1)}, bf16[304,128]{1,0:T(8,128)(2,1)S(1)}, u32[]{:S(2)}, u32[]{:S(2)}) collective-permute-start(bf16[304,128]{1,0:T(8,128)(2,1)S(1)} %get-tuple-element.57), channel_id=1, source_target_pairs={{0,8},{4,12},{8,0},{12,4},{1,9},{5,13},{9,1},{13,5},{2,10},{6,14},... | collective-permute-start | bytes 233480 | tf_op jit(solution)/shard_map/ppermute | solution.py:104
  45.4 4.6 %collective-permute-start.10 = (bf16[128,1,130]{0,2,1:T(8,128)(2,1)S(1)}, bf16[128,1,130]{0,2,1:T(8,128)(2,1)S(1)}, u32[]{:S(2)}, u32[]{:S(2)}) collective-permute-start(bf16[128,1,130]{0,2,1:T(8,128)(2,1)S(1)} %get-tuple-element.69), channel_id=1, source_target_pairs={{1,0},{0,1},{3,2},{2,3},{5,4},{4,5},{7,6},{6,7},{9,8},{8,9},{11,10... | collective-permute-start | bytes 99848 | tf_op jit(solution)/shard_map/ppermute | solution.py:15
  45.5 4.5 %collective-permute-start.9 = (bf16[128,1,130]{0,2,1:T(8,128)(2,1)S(1)}, bf16[128,1,130]{0,2,1:T(8,128)(2,1)S(1)}, u32[]{:S(2)}, u32[]{:S(2)}) collective-permute-start(bf16[128,1,130]{0,2,1:T(8,128)(2,1)S(1)} %get-tuple-element.68), channel_id=1, source_target_pairs={{0,1},{1,0},{2,3},{3,2},{4,5},{5,4},{6,7},{7,6},{8,9},{9,8},{10,11... | collective-permute-start | bytes 99848 | tf_op jit(solution)/shard_map/ppermute | solution.py:14
  47.7 11.6 %collective-permute-start.12 = (bf16[304,128]{1,0:T(8,128)(2,1)S(1)}, bf16[304,128]{1,0:T(8,128)(2,1)S(1)}, u32[]{:S(2)}, u32[]{:S(2)}) collective-permute-start(bf16[304,128]{1,0:T(8,128)(2,1)S(1)} %get-tuple-element.15), channel_id=1, source_target_pairs={{0,12},{4,0},{8,4},{12,8},{1,13},{5,1},{9,5},{13,9},{2,14},{6,2},{... | collective-permute-start | bytes 233480 | tf_op jit(solution)/shard_map/ppermute | solution.py:76
  49.4 9.9 %collective-permute-start.13 = (bf16[304,128]{1,0:T(8,128)(2,1)S(1)}, bf16[304,128]{1,0:T(8,128)(2,1)S(1)}, u32[]{:S(2)}, u32[]{:S(2)}) collective-permute-start(bf16[304,128]{1,0:T(8,128)(2,1)S(1)} %get-tuple-element.15), channel_id=1, source_target_pairs={{0,8},{4,12},{8,0},{12,4},{1,9},{5,13},{9,1},{13,5},{2,10},{6,14},... | collective-permute-start | bytes 233480 | tf_op jit(solution)/shard_map/ppermute | solution.py:76
  49.4 9.9 %collective-permute-start.14 = (bf16[304,128]{1,0:T(8,128)(2,1)S(1)}, bf16[304,128]{1,0:T(8,128)(2,1)S(1)}, u32[]{:S(2)}, u32[]{:S(2)}) collective-permute-start(bf16[304,128]{1,0:T(8,128)(2,1)S(1)} %get-tuple-element.15), channel_id=1, source_target_pairs={{0,4},{4,8},{8,12},{12,0},{1,5},{5,9},{9,13},{13,1},{2,6},{6,10},{... | collective-permute-start | bytes 233480 | tf_op jit(solution)/shard_map/ppermute | solution.py:76
  56.0 13.4 %collective-permute-start.16 = (bf16[128,2048]{1,0:T(8,128)(2,1)}, bf16[128,2048]{1,0:T(8,128)(2,1)}, u32[]{:S(2)}, u32[]{:S(2)}) collective-permute-start(bf16[128,2048]{1,0:T(8,128)(2,1)} %fusion.5), channel_id=1, source_target_pairs={{0,2},{2,0},{1,3},{3,1},{4,6},{6,4},{5,7},{7,5},{8,10},{10,8},{9,1... | collective-permute-start | bytes 1572872 | tf_op jit(solution)/shard_map/ppermute | solution.py:198
  59.5 2.1 %collective-permute-start.15 = (f32[1216,128]{1,0:T(8,128)S(1)}, f32[1216,128]{1,0:T(8,128)S(1)}, u32[]{:S(2)}, u32[]{:S(2)}) collective-permute-start(f32[1216,128]{1,0:T(8,128)S(1)} %bitcast.322), channel_id=1, source_target_pairs={{0,1},{1,0},{2,3},{3,2},{4,5},{5,4},{6,7},{7,6},{8,9},{9,8},{10,11... | collective-permute-start | bytes 1867784 | tf_op jit(solution)/shard_map/ppermute | solution.py:76

commit v28 on v19

--- a/solution.py
+++ b/solution.py
@@ -161,7 +161,7 @@
     upstream = cotangent.reshape(own_channels, -1).astype(jnp.float32)
     grad_pre = (upstream * gelu_slope(preact)).astype(jnp.bfloat16)
     bias_part = jnp.sum(grad_pre.astype(jnp.float32), axis=1)
-    input_local = jnp.concatenate(blocks, axis=0)
+    input_local = lax.optimization_barrier(jnp.concatenate(blocks, axis=0))
     taps = []
     for tap_row in range(3):
         row_taps = []

time: 70.1 us -> 70.2 us (level)
  local copies, waits for them, and re-layouts: 10.3 us -> 12.7 us
  other arithmetic: 7.67 us -> 5.3 us
    slice x4 -> x5, local copies, waits for them, and re-layouts: 3.74 us -> 6.13 us  [window_of(): field[:, first_row:first_row + row_count, first_col:first_col + column_co...]
    concatenate x1, other arithmetic: 2.53 us -> 0.16 us  [local(): input_local = lax.optimization_barrier(jnp.concatenate(blocks, axis=0))]
where the time goes in v28:
time: 70.2 us; the launch traced here: 69.9 us
  starting transfers between devices  17.8 us (25%)
  waiting for transfers between devices  17.1 us (24%)
  matrix products  15.5 us (22%)
  local copies, waits for them, and re-layouts  12.7 us (18%)
  other arithmetic  5.3 us (8%)
  between operations  1.47 us (2%)
    dot_general x36, matrix products, conv_taps(): jnp.dot(kernel[tap_row, tap_col], window, preferred_element_type=jnp.floa...  12.7 us
    slice x5, local copies, waits for them, and re-layouts, window_of(): field[:, first_row:first_row + row_count, first_col:first_col + column_co...  6.13 us
    ppermute x1, waiting for transfers between devices, local(): received.append(lax.ppermute(outgoing[shift - 1], 'chan', pairs))  5.29 us
    ppermute x3, waiting for transfers between devices, sum_start(): moved = lax.ppermute(piece, 'lon', pairs)  5.21 us
    ppermute x3, starting transfers between devices, sum_start(): moved = lax.ppermute(piece, 'lon', pairs)  4.99 us
    unnamed x12, local copies, waits for them, and re-layouts  3.51 us
    ppermute x1, starting transfers between devices, local(): raw_blocks.append(lax.ppermute(inputs, 'chan', pairs))  3 us
    dot_general x9, matrix products, local(): lax.dot_general(grad_pre, window, (((1,), (1,)), ((), ())), preferred_ele...  2.85 us
  transfers between devices with their start and end apart: 17, of which 10 were waited for; matrix products, arithmetic and copies ran while one was open for 25% of the time, Pallas kernels for 0%

profile of v28, /device:TPU:0, one launch (start us, length us, event | category | flops | bytes accessed | tf_op | source)
XLA Modules:
  0.0 69.9 jit_solution(5721668872081521160)
XLA Ops:
  0.6 1.5 %copy.12 = bf16[128,16,128]{0,2,1:T(8,128)(2,1)S(1)} copy(bf16[128,16,128]{2,1,0:T(8,128)(2,1)} %param.4) | data formatting | bytes 1048576 | tf_op args[0]
  2.2 3.0 %collective-permute-start.5 = (bf16[128,16,128]{0,2,1:T(8,128)(2,1)S(1)}, bf16[128,16,128]{0,2,1:T(8,128)(2,1)S(1)}, u32[]{:S(2)}, u32[]{:S(2)}) collective-permute-start(bf16[128,16,128]{0,2,1:T(8,128)(2,1)S(1)} %copy.12), channel_id=1, source_target_pairs={{0,2},{2,0},{1,3},{3,1},{4,6},{6,4},{5,7},{7,5},{8,10},{10,8},{9,1... | collective-permute-start | bytes 1572872 | tf_op jit(solution)/shard_map/ppermute | solution.py:142
  5.2 1.6 %collective-permute-start = (bf16[128,16,1]{0,2,1:T(2,128)(2,1)S(1)}, bf16[128,16,1]{0,2,1:T(2,128)(2,1)S(1)}, u32[]{:S(2)}, u32[]{:S(2)}) collective-permute-start(bf16[128,16,1]{0,2,1:T(2,128)(2,1)S(1)} %get-tuple-element.75), channel_id=1, source_target_pairs={{0,4},{4,8},{8,12},{12,0},{1,5},{5,9},{9,13},{13,1},{2,6},{6,10},{... | collective-permute-start | bytes 12296 | tf_op jit(solution)/shard_map/ppermute | solution.py:14
  6.8 2.2 %collective-permute-start.1 = (bf16[128,16,1]{0,2,1:T(2,128)(2,1)S(1)}, bf16[128,16,1]{0,2,1:T(2,128)(2,1)S(1)}, u32[]{:S(2)}, u32[]{:S(2)}) collective-permute-start(bf16[128,16,1]{0,2,1:T(2,128)(2,1)S(1)} %get-tuple-element.76), channel_id=1, source_target_pairs={{4,0},{8,4},{12,8},{0,12},{5,1},{9,5},{13,9},{1,13},{6,2},{10,6},{... | collective-permute-start | bytes 12296 | tf_op jit(solution)/shard_map/ppermute | solution.py:15
  9.2 1.5 %collective-permute-done = bf16[128,16,1]{0,2,1:T(2,128)(2,1)S(1)} collective-permute-done((bf16[128,16,1]{0,2,1:T(2,128)(2,1)S(1)}, bf16[128,16,1]{0,2,1:T(2,128)(2,1)S(1)}, u32[]{:S(2)}, u32[]{:S(2)}) %collective-permute-start) | collective-permute-done | bytes 4128 | tf_op jit(solution)/shard_map/ppermute | solution.py:14
  11.3 0.7 collective-permute-done.2
  12.5 0.7 fusion.48
  16.5 2.2 %collective-permute-done.4 = bf16[128,292]{0,1:T(8,128)(2,1)S(1)} collective-permute-done((bf16[128,292]{0,1:T(8,128)(2,1)S(1)}, bf16[128,292]{0,1:T(8,128)(2,1)S(1)}, u32[]{:S(2)}, u32[]{:S(2)}) %collective-permute-start.4) | collective-permute-done | bytes 74784 | tf_op jit(solution)/shard_map/ppermute | solution.py:148
  19.0 1.0 %fusion.46 = (bf16[128,16,128]{0,2,1:T(8,128)(2,1)S(1)}, bf16[128,16,128]{0,2,1:T(8,128)(2,1)S(1)}, bf16[128,16,128]{0,2,1:T(8,128)(2,1)S(1)}, bf16[128,16,128]{...) fusion(bf16[128,18,130]{0,2,1:T(8,128)(2,1)S(1)} %pad_maximum_f, ...), kind=kLoop, calls=%fused_computation.178 | loop fusion | bytes 9437184 | tf_op jit(solution)/shard_map/slice | solution.py:37
  20.1 2.6 %fusion.43 = (bf16[256,16,128]{0,2,1:T(8,128)(2,1)S(1)}, bf16[256,16,128]{0,2,1:T(8,128)(2,1)S(1)}, bf16[256,16,128]{0,2,1:T(8,128)(2,1)S(1)}, bf16[256,16,128]{...) fusion(bf16[256,18,130]{0,2,1:T(8,128)(2,1)S(1)} %pad_maximum_f, ...), kind=kLoop, calls=%fused_computation.175 | loop fusion | bytes 18874368 | tf_op jit(solution)/shard_map/slice | solution.py:37
  25.5 1.0 %convert_reduce_fusion = (f32[128]{0:T(128)S(1)}, bf16[128,2048]{1,0:T(8,128)(2,1)S(1)}) fusion(f32[128]{0:T(128)S(1)} %copy-done.2, f32[128,2048]{1,0:T(8,128)S(1)} %convolution_add_fusion.24, f32[128,2048]{1,0:T(8,128)S(1)} %convolution_add_fusion.17, bf16[128,2048]{0,1:T(8,128)(2,1)S(1)} %bitcast.358, bf16[3,3,128,256]{3,2,1,0:T(8,128)(2,1)S(1)} %copy-done, ...), kind=kOutput, calls=%fused_computation.66 | convolution fusion | flops 71040896 | bytes 4228104 | tf_op jit(solution)/shard_map/dot_general | solution.py:50
  29.7 0.6 copy.28
  30.7 0.8 %slice_reduce_fusion.1 = (bf16[128,16]{1,0:T(8,128)(2,1)S(1)}, bf16[128,16]{1,0:T(8,128)(2,1)S(1)}) fusion(bf16[128,16,128]{2,1,0:T(8,128)(2,1)S(1)} %bitcast.304), kind=kLoop, calls=%fused_computation.74 | loop fusion | bytes 16384 | tf_op jit(solution)/shard_map/slice | solution.py:179
  31.7 0.9 %collective-permute-done.6 = f32[1216,128]{1,0:T(8,128)} collective-permute-done((f32[1216,128]{1,0:T(8,128)S(1)}, f32[1216,128]{1,0:T(8,128)}, u32[]{:S(2)}, u32[]{:S(2)}) %collective-permute-start.6) | collective-permute-done | bytes 622624 | tf_op jit(solution)/shard_map/ppermute | solution.py:64
  32.7 1.1 %bitcast_add_fusion = f32[1216,128]{1,0:T(8,128)S(1)} fusion(f32[1216,128]{1,0:T(8,128)} %collective-permute-done.6, f32[2,1216,128]{2,1,0:T(8,128)S(1)} %bitcast.307, s32[]{:T(128)S(6)} %select_n.98), kind=kLoop, calls=%fused_computation.70 | loop fusion | flops 155648 | bytes 1867780 | tf_op jit(solution)/shard_map/add | solution.py:64
  33.9 1.9 %collective-permute-start.7 = (bf16[320,128]{1,0:T(8,128)(2,1)S(1)}, bf16[320,128]{1,0:T(8,128)(2,1)S(1)}, u32[]{:S(2)}, u32[]{:S(2)}) collective-permute-start(bf16[320,128]{1,0:T(8,128)(2,1)S(1)} %pad_maximum_fusion.3), channel_id=1, source_target_pairs={{0,4},{4,8},{8,12},{12,0},{1,5},{5,9},{9,13},{13,1},{2,6},{6,10},{... | collective-permute-start | bytes 245768 | tf_op jit(solution)/shard_map/ppermute | solution.py:104
  35.8 2.1 %collective-permute-start.8 = (bf16[320,128]{1,0:T(8,128)(2,1)S(1)}, bf16[320,128]{1,0:T(8,128)(2,1)S(1)}, u32[]{:S(2)}, u32[]{:S(2)}) collective-permute-start(bf16[320,128]{1,0:T(8,128)(2,1)S(1)} %pad_maximum_fusion.4), channel_id=1, source_target_pairs={{0,12},{4,0},{8,4},{12,8},{1,13},{5,1},{9,5},{13,9},{2,14},{6,2},{... | collective-permute-start | bytes 245768 | tf_op jit(solution)/shard_map/ppermute | solution.py:104
  38.4 1.0 %collective-permute-start.11 = (bf16[304,128]{1,0:T(8,128)(2,1)S(1)}, bf16[304,128]{1,0:T(8,128)(2,1)S(1)}, u32[]{:S(2)}, u32[]{:S(2)}) collective-permute-start(bf16[304,128]{1,0:T(8,128)(2,1)S(1)} %get-tuple-element.66), channel_id=1, source_target_pairs={{0,8},{4,12},{8,0},{12,4},{1,9},{5,13},{9,1},{13,5},{2,10},{6,14},... | collective-permute-start | bytes 233480 | tf_op jit(solution)/shard_map/ppermute | solution.py:104
  39.5 1.4 %collective-permute-done.7 = bf16[320,128]{1,0:T(8,128)(2,1)S(1)} collective-permute-done((bf16[320,128]{1,0:T(8,128)(2,1)S(1)}, bf16[320,128]{1,0:T(8,128)(2,1)S(1)}, u32[]{:S(2)}, u32[]{:S(2)}) %collective-permute-start.7) | collective-permute-done | bytes 81952 | tf_op jit(solution)/shard_map/ppermute | solution.py:104
  41.0 0.7 %collective-permute-done.8 = bf16[320,128]{1,0:T(8,128)(2,1)S(1)} collective-permute-done((bf16[320,128]{1,0:T(8,128)(2,1)S(1)}, bf16[320,128]{1,0:T(8,128)(2,1)S(1)}, u32[]{:S(2)}, u32[]{:S(2)}) %collective-permute-start.8) | collective-permute-done | bytes 81952 | tf_op jit(solution)/shard_map/ppermute | solution.py:104
  42.5 3.1 %collective-permute-done.11 = bf16[304,128]{1,0:T(8,128)(2,1)S(1)} collective-permute-done((bf16[304,128]{1,0:T(8,128)(2,1)S(1)}, bf16[304,128]{1,0:T(8,128)(2,1)S(1)}, u32[]{:S(2)}, u32[]{:S(2)}) %collective-permute-start.11) | collective-permute-done | bytes 77856 | tf_op jit(solution)/shard_map/ppermute | solution.py:104
  45.7 1.9 %collective-permute-start.12 = (bf16[304,128]{1,0:T(8,128)(2,1)S(1)}, bf16[304,128]{1,0:T(8,128)(2,1)S(1)}, u32[]{:S(2)}, u32[]{:S(2)}) collective-permute-start(bf16[304,128]{1,0:T(8,128)(2,1)S(1)} %get-tuple-element.15), channel_id=1, source_target_pairs={{0,12},{4,0},{8,4},{12,8},{1,13},{5,1},{9,5},{13,9},{2,14},{6,2},{... | collective-permute-start | bytes 233480 | tf_op jit(solution)/shard_map/ppermute | solution.py:76
  47.6 0.6 collective-permute-start.14
  48.6 0.9 %fusion.45 = (bf16[128,16,128]{0,2,1:T(8,128)(2,1)S(1)}, bf16[128,16,128]{0,2,1:T(8,128)(2,1)S(1)}, bf16[128,16,128]{0,2,1:T(8,128)(2,1)S(1)}, bf16[128,16,128]{...) fusion(bf16[128,18,130]{0,2,1:T(8,128)(2,1)S(1)} %maximum_selec, ...), kind=kLoop, calls=%fused_computation.177 | loop fusion | bytes 9437184 | tf_op jit(solution)/shard_map/slice | solution.py:37
  52.1 1.1 %fusion.2 = bf16[128,2048]{1,0:T(8,128)(2,1)} fusion(f32[128,2048]{1,0:T(8,128)S(1)} %convolution_add_fusion.9, bf16[128,2048]{0,1:T(8,128)(2,1)S(1)} %bitcast.345, bf16[3,3,128,128]{2,3,1,0:T(8,128)(2,1)S(1)} %get-tuple-element.70), kind=kOutput, calls=%fused_computation.38 | convolution fusion | flops 67633152 | bytes 2129920 | tf_op jit(solution)/shard_map/dot_general | solution.py:50
  53.3 0.9 %fusion.44 = (bf16[128,16,128]{0,2,1:T(8,128)(2,1)S(1)}, bf16[128,16,128]{0,2,1:T(8,128)(2,1)S(1)}, bf16[128,16,128]{0,2,1:T(8,128)(2,1)S(1)}, bf16[128,16,128]{...) fusion(bf16[128,18,130]{0,2,1:T(8,128)(2,1)S(1)} %maximum_selec, ...), kind=kLoop, calls=%fused_computation.176 | loop fusion | bytes 9437184 | tf_op jit(solution)/shard_map/slice | solution.py:37
  54.2 1.7 %collective-permute-start.16 = (bf16[128,2048]{1,0:T(8,128)(2,1)}, bf16[128,2048]{1,0:T(8,128)(2,1)}, u32[]{:S(2)}, u32[]{:S(2)}) collective-permute-start(bf16[128,2048]{1,0:T(8,128)(2,1)} %fusion.2), channel_id=1, source_target_pairs={{0,2},{2,0},{1,3},{3,1},{4,6},{6,4},{5,7},{7,5},{8,10},{10,8},{9,1... | collective-permute-start | bytes 1572872 | tf_op jit(solution)/shard_map/ppermute | solution.py:198
  59.1 1.1 %collective-permute-done.15 = f32[1216,128]{1,0:T(8,128)S(1)} collective-permute-done((f32[1216,128]{1,0:T(8,128)S(1)}, f32[1216,128]{1,0:T(8,128)S(1)}, u32[]{:S(2)}, u32[]{:S(2)}) %collective-permute-start.15) | collective-permute-done | bytes 622624 | tf_op jit(solution)/shard_map/ppermute | solution.py:76
  61.4 1.2 %fusion.6 = f32[3,3,128,256]{3,2,1,0:T(8,128)} fusion(s32[]{:T(128)S(6)} %select_n.114, f32[3,3,128,256]{3,2,1,0:T(8,128)S(1)} %reshape.240), kind=kLoop, calls=%fused_computation.48 | loop fusion | flops 294912 | bytes 2359300 | tf_op jit(solution)/shard_map/concatenate | solution.py:184
  62.6 5.3 %collective-permute-done.16 = bf16[128,2048]{1,0:T(8,128)(2,1)} collective-permute-done((bf16[128,2048]{1,0:T(8,128)(2,1)}, bf16[128,2048]{1,0:T(8,128)(2,1)}, u32[]{:S(2)}, u32[]{:S(2)}) %collective-permute-start.16) | collective-permute-done | bytes 524320 | tf_op jit(solution)/shard_map/ppermute | solution.py:198
  67.8 1.2 %fusion.13 = bf16[16,8,16,128]{3,1,2,0:T(8,128)(2,1)S(1)} fusion(f32[128,2048]{1,0:T(8,128)S(1)} %convolution_add_fusion, bf16[128,2048]{1,0:T(8,128)(2,1)} %collective-permute-done.16), kind=kLoop, calls=%fused_computation.72 | loop fusion | flops 786432 | bytes 2097152
  69.0 0.9 %copy.30 = bf16[16,8,16,128]{3,2,1,0:T(8,128)(2,1)} copy(bf16[16,8,16,128]{3,1,2,0:T(8,128)(2,1)S(1)} %fusion.13) | data formatting | bytes 1048576
  (116 shorter events, 19.9 us)
Async XLA Ops:
  0.6 8.4 %copy-start.1 = (bf16[128,16,128]{2,1,0:T(8,128)(2,1)S(1)}, bf16[128,16,128]{2,1,0:T(8,128)(2,1)}, u32[]{:S(2)}) copy-start(bf16[128,16,128]{2,1,0:T(8,128)(2,1)} %param.5) | copy-start | bytes 1572868
  2.2 16.6 %collective-permute-start.5 = (bf16[128,16,128]{0,2,1:T(8,128)(2,1)S(1)}, bf16[128,16,128]{0,2,1:T(8,128)(2,1)S(1)}, u32[]{:S(2)}, u32[]{:S(2)}) collective-permute-start(bf16[128,16,128]{0,2,1:T(8,128)(2,1)S(1)} %copy.12), channel_id=1, source_target_pairs={{0,2},{2,0},{1,3},{3,1},{4,6},{6,4},{5,7},{7,5},{8,10},{10,8},{9,1... | collective-permute-start | bytes 1572872 | tf_op jit(solution)/shard_map/ppermute | solution.py:142
  5.2 5.5 %collective-permute-start = (bf16[128,16,1]{0,2,1:T(2,128)(2,1)S(1)}, bf16[128,16,1]{0,2,1:T(2,128)(2,1)S(1)}, u32[]{:S(2)}, u32[]{:S(2)}) collective-permute-start(bf16[128,16,1]{0,2,1:T(2,128)(2,1)S(1)} %get-tuple-element.75), channel_id=1, source_target_pairs={{0,4},{4,8},{8,12},{12,0},{1,5},{5,9},{9,13},{13,1},{2,6},{6,10},{... | collective-permute-start | bytes 12296 | tf_op jit(solution)/shard_map/ppermute | solution.py:14
  6.8 3.9 %collective-permute-start.1 = (bf16[128,16,1]{0,2,1:T(2,128)(2,1)S(1)}, bf16[128,16,1]{0,2,1:T(2,128)(2,1)S(1)}, u32[]{:S(2)}, u32[]{:S(2)}) collective-permute-start(bf16[128,16,1]{0,2,1:T(2,128)(2,1)S(1)} %get-tuple-element.76), channel_id=1, source_target_pairs={{4,0},{8,4},{12,8},{0,12},{5,1},{9,5},{13,9},{1,13},{6,2},{10,6},{... | collective-permute-start | bytes 12296 | tf_op jit(solution)/shard_map/ppermute | solution.py:15
  10.7 1.3 %collective-permute-start.2 = (bf16[128,1,130]{0,2,1:T(8,128)(2,1)S(1)}, bf16[128,1,130]{0,2,1:T(8,128)(2,1)S(1)}, u32[]{:S(2)}, u32[]{:S(2)}) collective-permute-start(bf16[128,1,130]{0,2,1:T(8,128)(2,1)S(1)} %get-tuple-element.73), channel_id=1, source_target_pairs={{0,1},{1,0},{2,3},{3,2},{4,5},{5,4},{6,7},{7,6},{8,9},{9,8},{10,11... | collective-permute-start | bytes 99848 | tf_op jit(solution)/shard_map/ppermute | solution.py:14
  10.8 1.4 %collective-permute-start.3 = (bf16[128,1,130]{0,2,1:T(8,128)(2,1)S(1)}, bf16[128,1,130]{0,2,1:T(8,128)(2,1)S(1)}, u32[]{:S(2)}, u32[]{:S(2)}) collective-permute-start(bf16[128,1,130]{0,2,1:T(8,128)(2,1)S(1)} %get-tuple-element.74), channel_id=1, source_target_pairs={{1,0},{0,1},{3,2},{2,3},{5,4},{4,5},{7,6},{6,7},{9,8},{8,9},{11,10... | collective-permute-start | bytes 99848 | tf_op jit(solution)/shard_map/ppermute | solution.py:15
  12.5 1.2 %copy-start = (bf16[3,3,128,256]{3,2,1,0:T(8,128)(2,1)S(1)}, bf16[3,3,128,256]{3,2,1,0:T(8,128)(2,1)}, u32[]{:S(2)}) copy-start(bf16[3,3,128,256]{3,2,1,0:T(8,128)(2,1)} %param.6) | copy-start | bytes 1769476
  13.3 5.4 %collective-permute-start.4 = (bf16[128,292]{0,1:T(8,128)(2,1)S(1)}, bf16[128,292]{0,1:T(8,128)(2,1)S(1)}, u32[]{:S(2)}, u32[]{:S(2)}) collective-permute-start(bf16[128,292]{0,1:T(8,128)(2,1)S(1)} %pad_maximum_fusion.5), channel_id=1, source_target_pairs={{0,2},{2,0},{1,3},{3,1},{4,6},{6,4},{5,7},{7,5},{8,10},{10,8},{9,1... | collective-permute-start | bytes 224264 | tf_op jit(solution)/shard_map/ppermute | solution.py:148
  24.9 0.7 copy-start.2
  30.4 2.2 %collective-permute-start.6 = (f32[1216,128]{1,0:T(8,128)S(1)}, f32[1216,128]{1,0:T(8,128)}, u32[]{:S(2)}, u32[]{:S(2)}) collective-permute-start(f32[1216,128]{1,0:T(8,128)S(1)} %dynamic-slice_bitcast_fusion), channel_id=1, source_target_pairs={{0,1},{1,0},{2,3},{3,2},{4,5},{5,4},{6,7},{7,6},{8,9},{9,8},{10,11... | collective-permute-start | bytes 1867784 | tf_op jit(solution)/shard_map/ppermute | solution.py:64
  33.9 7.0 %collective-permute-start.7 = (bf16[320,128]{1,0:T(8,128)(2,1)S(1)}, bf16[320,128]{1,0:T(8,128)(2,1)S(1)}, u32[]{:S(2)}, u32[]{:S(2)}) collective-permute-start(bf16[320,128]{1,0:T(8,128)(2,1)S(1)} %pad_maximum_fusion.3), channel_id=1, source_target_pairs={{0,4},{4,8},{8,12},{12,0},{1,5},{5,9},{9,13},{13,1},{2,6},{6,10},{... | collective-permute-start | bytes 245768 | tf_op jit(solution)/shard_map/ppermute | solution.py:104
  35.8 6.0 %collective-permute-start.8 = (bf16[320,128]{1,0:T(8,128)(2,1)S(1)}, bf16[320,128]{1,0:T(8,128)(2,1)S(1)}, u32[]{:S(2)}, u32[]{:S(2)}) collective-permute-start(bf16[320,128]{1,0:T(8,128)(2,1)S(1)} %pad_maximum_fusion.4), channel_id=1, source_target_pairs={{0,12},{4,0},{8,4},{12,8},{1,13},{5,1},{9,5},{13,9},{2,14},{6,2},{... | collective-permute-start | bytes 245768 | tf_op jit(solution)/shard_map/ppermute | solution.py:104
  38.4 7.2 %collective-permute-start.11 = (bf16[304,128]{1,0:T(8,128)(2,1)S(1)}, bf16[304,128]{1,0:T(8,128)(2,1)S(1)}, u32[]{:S(2)}, u32[]{:S(2)}) collective-permute-start(bf16[304,128]{1,0:T(8,128)(2,1)S(1)} %get-tuple-element.66), channel_id=1, source_target_pairs={{0,8},{4,12},{8,0},{12,4},{1,9},{5,13},{9,1},{13,5},{2,10},{6,14},... | collective-permute-start | bytes 233480 | tf_op jit(solution)/shard_map/ppermute | solution.py:104
  42.0 6.3 %collective-permute-start.10 = (bf16[128,1,130]{0,2,1:T(8,128)(2,1)S(1)}, bf16[128,1,130]{0,2,1:T(8,128)(2,1)S(1)}, u32[]{:S(2)}, u32[]{:S(2)}) collective-permute-start(bf16[128,1,130]{0,2,1:T(8,128)(2,1)S(1)} %get-tuple-element.72), channel_id=1, source_target_pairs={{1,0},{0,1},{3,2},{2,3},{5,4},{4,5},{7,6},{6,7},{9,8},{8,9},{11,10... | collective-permute-start | bytes 99848 | tf_op jit(solution)/shard_map/ppermute | solution.py:15
  42.0 6.2 %collective-permute-start.9 = (bf16[128,1,130]{0,2,1:T(8,128)(2,1)S(1)}, bf16[128,1,130]{0,2,1:T(8,128)(2,1)S(1)}, u32[]{:S(2)}, u32[]{:S(2)}) collective-permute-start(bf16[128,1,130]{0,2,1:T(8,128)(2,1)S(1)} %get-tuple-element.71), channel_id=1, source_target_pairs={{0,1},{1,0},{2,3},{3,2},{4,5},{5,4},{6,7},{7,6},{8,9},{9,8},{10,11... | collective-permute-start | bytes 99848 | tf_op jit(solution)/shard_map/ppermute | solution.py:14
  45.7 12.1 %collective-permute-start.12 = (bf16[304,128]{1,0:T(8,128)(2,1)S(1)}, bf16[304,128]{1,0:T(8,128)(2,1)S(1)}, u32[]{:S(2)}, u32[]{:S(2)}) collective-permute-start(bf16[304,128]{1,0:T(8,128)(2,1)S(1)} %get-tuple-element.15), channel_id=1, source_target_pairs={{0,12},{4,0},{8,4},{12,8},{1,13},{5,1},{9,5},{13,9},{2,14},{6,2},{... | collective-permute-start | bytes 233480 | tf_op jit(solution)/shard_map/ppermute | solution.py:76
  47.6 10.3 %collective-permute-start.13 = (bf16[304,128]{1,0:T(8,128)(2,1)S(1)}, bf16[304,128]{1,0:T(8,128)(2,1)S(1)}, u32[]{:S(2)}, u32[]{:S(2)}) collective-permute-start(bf16[304,128]{1,0:T(8,128)(2,1)S(1)} %get-tuple-element.15), channel_id=1, source_target_pairs={{0,8},{4,12},{8,0},{12,4},{1,9},{5,13},{9,1},{13,5},{2,10},{6,14},... | collective-permute-start | bytes 233480 | tf_op jit(solution)/shard_map/ppermute | solution.py:76
  47.6 10.3 %collective-permute-start.14 = (bf16[304,128]{1,0:T(8,128)(2,1)S(1)}, bf16[304,128]{1,0:T(8,128)(2,1)S(1)}, u32[]{:S(2)}, u32[]{:S(2)}) collective-permute-start(bf16[304,128]{1,0:T(8,128)(2,1)S(1)} %get-tuple-element.15), channel_id=1, source_target_pairs={{0,4},{4,8},{8,12},{12,0},{1,5},{5,9},{9,13},{13,1},{2,6},{6,10},{... | collective-permute-start | bytes 233480 | tf_op jit(solution)/shard_map/ppermute | solution.py:76
  54.2 13.7 %collective-permute-start.16 = (bf16[128,2048]{1,0:T(8,128)(2,1)}, bf16[128,2048]{1,0:T(8,128)(2,1)}, u32[]{:S(2)}, u32[]{:S(2)}) collective-permute-start(bf16[128,2048]{1,0:T(8,128)(2,1)} %fusion.2), channel_id=1, source_target_pairs={{0,2},{2,0},{1,3},{3,1},{4,6},{6,4},{5,7},{7,5},{8,10},{10,8},{9,1... | collective-permute-start | bytes 1572872 | tf_op jit(solution)/shard_map/ppermute | solution.py:198
  58.1 2.1 %collective-permute-start.15 = (f32[1216,128]{1,0:T(8,128)S(1)}, f32[1216,128]{1,0:T(8,128)S(1)}, u32[]{:S(2)}, u32[]{:S(2)}) collective-permute-start(f32[1216,128]{1,0:T(8,128)S(1)} %bitcast.321), channel_id=1, source_target_pairs={{0,1},{1,0},{2,3},{3,2},{4,5},{5,4},{6,7},{7,6},{8,9},{9,8},{10,11... | collective-permute-start | bytes 1867784 | tf_op jit(solution)/shard_map/ppermute | solution.py:76

commit v29 on v19

--- a/solution.py
+++ b/solution.py
@@ -96,7 +96,7 @@
     acc = lax.dynamic_index_in_dim(chunks, index, keepdims=False)
     extra = {1: last, count - 1: first}
     got = {}
-    for step in range(1, count):
+    for step in sorted(range(1, count), key=lambda step: step in extra):
         pairs = [(j, (j + step) % count) for j in range(count)]
         piece = lax.dynamic_index_in_dim(chunks, (index + step) % count, keepdims=False).astype(send_dtype)
         if step in extra:

time: 70.1 us -> 70.1 us (level)
  no operation moved by 1% of the time
where the time goes in v29:
time: 70.1 us; the launch traced here: 69.8 us
  starting transfers between devices  17.9 us (26%)
  waiting for transfers between devices  17 us (24%)
  matrix products  15.5 us (22%)
  local copies, waits for them, and re-layouts  10.3 us (15%)
  other arithmetic  7.67 us (11%)
  between operations  1.47 us (2%)
    dot_general x36, matrix products, conv_taps(): jnp.dot(kernel[tap_row, tap_col], window, preferred_element_type=jnp.floa...  12.7 us
    ppermute x1, waiting for transfers between devices, local(): received.append(lax.ppermute(outgoing[shift - 1], 'chan', pairs))  5.4 us
    ppermute x3, waiting for transfers between devices, sum_start(): moved = lax.ppermute(piece, 'lon', pairs)  5.21 us
    ppermute x3, starting transfers between devices, sum_start(): moved = lax.ppermute(piece, 'lon', pairs)  4.99 us
    slice x4, local copies, waits for them, and re-layouts, window_of(): field[:, first_row:first_row + row_count, first_col:first_col + column_co...  3.74 us
    unnamed x12, local copies, waits for them, and re-layouts  3.51 us
    ppermute x1, starting transfers between devices, local(): raw_blocks.append(lax.ppermute(inputs, 'chan', pairs))  3 us
    dot_general x9, matrix products, local(): lax.dot_general(grad_pre, window, (((1,), (1,)), ((), ())), preferred_ele...  2.85 us
  transfers between devices with their start and end apart: 17, of which 10 were waited for; matrix products, arithmetic and copies ran while one was open for 25% of the time, Pallas kernels for 0%

profile of v29, /device:TPU:0, one launch (start us, length us, event | category | flops | bytes accessed | tf_op | source)
XLA Modules:
  0.0 69.8 jit_solution(7373164670560880708)
XLA Ops:
  0.6 1.5 %copy.12 = bf16[128,16,128]{0,2,1:T(8,128)(2,1)S(1)} copy(bf16[128,16,128]{2,1,0:T(8,128)(2,1)} %param.4) | data formatting | bytes 1048576 | tf_op args[0]
  2.2 3.0 %collective-permute-start.5 = (bf16[128,16,128]{0,2,1:T(8,128)(2,1)S(1)}, bf16[128,16,128]{0,2,1:T(8,128)(2,1)S(1)}, u32[]{:S(2)}, u32[]{:S(2)}) collective-permute-start(bf16[128,16,128]{0,2,1:T(8,128)(2,1)S(1)} %copy.12), channel_id=1, source_target_pairs={{0,2},{2,0},{1,3},{3,1},{4,6},{6,4},{5,7},{7,5},{8,10},{10,8},{9,1... | collective-permute-start | bytes 1572872 | tf_op jit(solution)/shard_map/ppermute | solution.py:142
  5.2 1.6 %collective-permute-start = (bf16[128,16,1]{0,2,1:T(2,128)(2,1)S(1)}, bf16[128,16,1]{0,2,1:T(2,128)(2,1)S(1)}, u32[]{:S(2)}, u32[]{:S(2)}) collective-permute-start(bf16[128,16,1]{0,2,1:T(2,128)(2,1)S(1)} %get-tuple-element.75), channel_id=1, source_target_pairs={{0,4},{4,8},{8,12},{12,0},{1,5},{5,9},{9,13},{13,1},{2,6},{6,10},{... | collective-permute-start | bytes 12296 | tf_op jit(solution)/shard_map/ppermute | solution.py:14
  6.8 2.2 %collective-permute-start.1 = (bf16[128,16,1]{0,2,1:T(2,128)(2,1)S(1)}, bf16[128,16,1]{0,2,1:T(2,128)(2,1)S(1)}, u32[]{:S(2)}, u32[]{:S(2)}) collective-permute-start(bf16[128,16,1]{0,2,1:T(2,128)(2,1)S(1)} %get-tuple-element.76), channel_id=1, source_target_pairs={{4,0},{8,4},{12,8},{0,12},{5,1},{9,5},{13,9},{1,13},{6,2},{10,6},{... | collective-permute-start | bytes 12296 | tf_op jit(solution)/shard_map/ppermute | solution.py:15
  9.2 1.5 %collective-permute-done = bf16[128,16,1]{0,2,1:T(2,128)(2,1)S(1)} collective-permute-done((bf16[128,16,1]{0,2,1:T(2,128)(2,1)S(1)}, bf16[128,16,1]{0,2,1:T(2,128)(2,1)S(1)}, u32[]{:S(2)}, u32[]{:S(2)}) %collective-permute-start) | collective-permute-done | bytes 4128 | tf_op jit(solution)/shard_map/ppermute | solution.py:14
  11.3 0.7 collective-permute-done.2
  12.5 0.9 %fusion.55 = (bf16[128,16,128]{0,2,1:T(8,128)(2,1)S(1)}, bf16[128,16,128]{0,2,1:T(8,128)(2,1)S(1)}, bf16[128,16,128]{0,2,1:T(8,128)(2,1)S(1)}, bf16[128,16,128]{...) fusion(bf16[128,18,130]{0,2,1:T(8,128)(2,1)S(1)} %maximum_selec, ...), kind=kLoop, calls=%fused_computation.203 | loop fusion | bytes 9437184 | tf_op jit(solution)/shard_map/slice | solution.py:37
  16.7 2.0 %collective-permute-done.4 = bf16[128,292]{0,1:T(8,128)(2,1)S(1)} collective-permute-done((bf16[128,292]{0,1:T(8,128)(2,1)S(1)}, bf16[128,292]{0,1:T(8,128)(2,1)S(1)}, u32[]{:S(2)}, u32[]{:S(2)}) %collective-permute-start.4) | collective-permute-done | bytes 74784 | tf_op jit(solution)/shard_map/ppermute | solution.py:148
  19.0 1.0 %fusion.53 = (bf16[128,16,128]{0,2,1:T(8,128)(2,1)S(1)}, bf16[128,16,128]{0,2,1:T(8,128)(2,1)S(1)}, bf16[128,16,128]{0,2,1:T(8,128)(2,1)S(1)}, bf16[128,16,128]{...) fusion(bf16[128,18,130]{0,2,1:T(8,128)(2,1)S(1)} %pad_maximum_f, ...), kind=kLoop, calls=%fused_computation.201 | loop fusion | bytes 9437184 | tf_op jit(solution)/shard_map/slice | solution.py:37
  19.9 2.5 %fusion.14 = (bf16[256,16,128]{0,2,1:T(8,128)(2,1)S(1)}, bf16[256,16,128]{0,2,1:T(8,128)(2,1)S(1)}, bf16[256,16,128]{0,2,1:T(8,128)(2,1)S(1)}, bf16[256,16,128]{...) fusion(bf16[128,18,130]{0,2,1:T(8,128)(2,1)S(1)} %maximum_selec, ...), kind=kLoop, calls=%fused_computation.81 | loop fusion | flops 18874368 | bytes 10635264 | tf_op jit(solution)/shard_map/concatenate | solution.py:164
  25.3 1.0 %convert_reduce_fusion = (f32[128]{0:T(128)S(1)}, bf16[128,2048]{1,0:T(8,128)(2,1)S(1)}) fusion(f32[128]{0:T(128)S(1)} %copy-done.2, f32[128,2048]{1,0:T(8,128)S(1)} %convolution_add_fusion.24, f32[128,2048]{1,0:T(8,128)S(1)} %convolution_add_fusion.17, bf16[128,2048]{0,1:T(8,128)(2,1)S(1)} %bitcast.358, bf16[3,3,128,256]{3,2,1,0:T(8,128)(2,1)S(1)} %copy-done, ...), kind=kOutput, calls=%fused_computation.90 | convolution fusion | flops 71040896 | bytes 4228104 | tf_op jit(solution)/shard_map/dot_general | solution.py:50
  29.4 0.6 copy.28
  30.5 0.8 %slice_reduce_fusion.1 = (bf16[128,16]{1,0:T(8,128)(2,1)S(1)}, bf16[128,16]{1,0:T(8,128)(2,1)S(1)}) fusion(bf16[128,16,128]{2,1,0:T(8,128)(2,1)S(1)} %bitcast.304), kind=kLoop, calls=%fused_computation.98 | loop fusion | bytes 16384 | tf_op jit(solution)/shard_map/slice | solution.py:179
  31.5 0.9 %collective-permute-done.6 = f32[1216,128]{1,0:T(8,128)} collective-permute-done((f32[1216,128]{1,0:T(8,128)S(1)}, f32[1216,128]{1,0:T(8,128)}, u32[]{:S(2)}, u32[]{:S(2)}) %collective-permute-start.6) | collective-permute-done | bytes 622624 | tf_op jit(solution)/shard_map/ppermute | solution.py:64
  32.4 1.1 %bitcast_add_fusion = f32[1216,128]{1,0:T(8,128)S(1)} fusion(f32[1216,128]{1,0:T(8,128)} %collective-permute-done.6, f32[2,1216,128]{2,1,0:T(8,128)S(1)} %bitcast.307, s32[]{:T(128)S(6)} %select_n.98), kind=kLoop, calls=%fused_computation.94 | loop fusion | flops 155648 | bytes 1867780 | tf_op jit(solution)/shard_map/add | solution.py:64
  33.6 1.9 %collective-permute-start.7 = (bf16[320,128]{1,0:T(8,128)(2,1)S(1)}, bf16[320,128]{1,0:T(8,128)(2,1)S(1)}, u32[]{:S(2)}, u32[]{:S(2)}) collective-permute-start(bf16[320,128]{1,0:T(8,128)(2,1)S(1)} %pad_maximum_fusion.3), channel_id=1, source_target_pairs={{0,4},{4,8},{8,12},{12,0},{1,5},{5,9},{9,13},{13,1},{2,6},{6,10},{... | collective-permute-start | bytes 245768 | tf_op jit(solution)/shard_map/ppermute | solution.py:104
  35.5 2.3 %collective-permute-start.8 = (bf16[320,128]{1,0:T(8,128)(2,1)S(1)}, bf16[320,128]{1,0:T(8,128)(2,1)S(1)}, u32[]{:S(2)}, u32[]{:S(2)}) collective-permute-start(bf16[320,128]{1,0:T(8,128)(2,1)S(1)} %pad_maximum_fusion.4), channel_id=1, source_target_pairs={{0,12},{4,0},{8,4},{12,8},{1,13},{5,1},{9,5},{13,9},{2,14},{6,2},{... | collective-permute-start | bytes 245768 | tf_op jit(solution)/shard_map/ppermute | solution.py:104
  38.4 0.8 %collective-permute-start.11 = (bf16[304,128]{1,0:T(8,128)(2,1)S(1)}, bf16[304,128]{1,0:T(8,128)(2,1)S(1)}, u32[]{:S(2)}, u32[]{:S(2)}) collective-permute-start(bf16[304,128]{1,0:T(8,128)(2,1)S(1)} %get-tuple-element.66), channel_id=1, source_target_pairs={{0,8},{4,12},{8,0},{12,4},{1,9},{5,13},{9,1},{13,5},{2,10},{6,14},... | collective-permute-start | bytes 233480 | tf_op jit(solution)/shard_map/ppermute | solution.py:104
  39.2 1.4 %collective-permute-done.7 = bf16[320,128]{1,0:T(8,128)(2,1)S(1)} collective-permute-done((bf16[320,128]{1,0:T(8,128)(2,1)S(1)}, bf16[320,128]{1,0:T(8,128)(2,1)S(1)}, u32[]{:S(2)}, u32[]{:S(2)}) %collective-permute-start.7) | collective-permute-done | bytes 81952 | tf_op jit(solution)/shard_map/ppermute | solution.py:104
  40.7 0.7 %collective-permute-done.8 = bf16[320,128]{1,0:T(8,128)(2,1)S(1)} collective-permute-done((bf16[320,128]{1,0:T(8,128)(2,1)S(1)}, bf16[320,128]{1,0:T(8,128)(2,1)S(1)}, u32[]{:S(2)}, u32[]{:S(2)}) %collective-permute-start.8) | collective-permute-done | bytes 81952 | tf_op jit(solution)/shard_map/ppermute | solution.py:104
  42.3 3.1 %collective-permute-done.11 = bf16[304,128]{1,0:T(8,128)(2,1)S(1)} collective-permute-done((bf16[304,128]{1,0:T(8,128)(2,1)S(1)}, bf16[304,128]{1,0:T(8,128)(2,1)S(1)}, u32[]{:S(2)}, u32[]{:S(2)}) %collective-permute-start.11) | collective-permute-done | bytes 77856 | tf_op jit(solution)/shard_map/ppermute | solution.py:104
  45.4 2.1 %collective-permute-start.12 = (bf16[304,128]{1,0:T(8,128)(2,1)S(1)}, bf16[304,128]{1,0:T(8,128)(2,1)S(1)}, u32[]{:S(2)}, u32[]{:S(2)}) collective-permute-start(bf16[304,128]{1,0:T(8,128)(2,1)S(1)} %get-tuple-element.15), channel_id=1, source_target_pairs={{0,12},{4,0},{8,4},{12,8},{1,13},{5,1},{9,5},{13,9},{2,14},{6,2},{... | collective-permute-start | bytes 233480 | tf_op jit(solution)/shard_map/ppermute | solution.py:76
  47.5 0.6 collective-permute-start.14
  48.5 0.9 %fusion.52 = (bf16[128,16,128]{0,2,1:T(8,128)(2,1)S(1)}, bf16[128,16,128]{0,2,1:T(8,128)(2,1)S(1)}, bf16[128,16,128]{0,2,1:T(8,128)(2,1)S(1)}, bf16[128,16,128]{...) fusion(bf16[128,18,130]{0,2,1:T(8,128)(2,1)S(1)} %maximum_selec, ...), kind=kLoop, calls=%fused_computation.200 | loop fusion | bytes 9437184 | tf_op jit(solution)/shard_map/slice | solution.py:37
  52.0 1.1 %fusion.2 = bf16[128,2048]{1,0:T(8,128)(2,1)} fusion(f32[128,2048]{1,0:T(8,128)S(1)} %convolution_add_fusion.9, bf16[128,2048]{0,1:T(8,128)(2,1)S(1)} %bitcast.345, bf16[3,3,128,128]{2,3,1,0:T(8,128)(2,1)S(1)} %get-tuple-element.70), kind=kOutput, calls=%fused_computation.38 | convolution fusion | flops 67633152 | bytes 2129920 | tf_op jit(solution)/shard_map/dot_general | solution.py:50
  53.2 0.9 %fusion.51 = (bf16[128,16,128]{0,2,1:T(8,128)(2,1)S(1)}, bf16[128,16,128]{0,2,1:T(8,128)(2,1)S(1)}, bf16[128,16,128]{0,2,1:T(8,128)(2,1)S(1)}, bf16[128,16,128]{...) fusion(bf16[128,18,130]{0,2,1:T(8,128)(2,1)S(1)} %maximum_selec, ...), kind=kLoop, calls=%fused_computation.199 | loop fusion | bytes 9437184 | tf_op jit(solution)/shard_map/slice | solution.py:37
  54.1 1.6 %collective-permute-start.16 = (bf16[128,2048]{1,0:T(8,128)(2,1)}, bf16[128,2048]{1,0:T(8,128)(2,1)}, u32[]{:S(2)}, u32[]{:S(2)}) collective-permute-start(bf16[128,2048]{1,0:T(8,128)(2,1)} %fusion.2), channel_id=1, source_target_pairs={{0,2},{2,0},{1,3},{3,1},{4,6},{6,4},{5,7},{7,5},{8,10},{10,8},{9,1... | collective-permute-start | bytes 1572872 | tf_op jit(solution)/shard_map/ppermute | solution.py:198
  58.9 1.1 %collective-permute-done.15 = f32[1216,128]{1,0:T(8,128)S(1)} collective-permute-done((f32[1216,128]{1,0:T(8,128)S(1)}, f32[1216,128]{1,0:T(8,128)S(1)}, u32[]{:S(2)}, u32[]{:S(2)}) %collective-permute-start.15) | collective-permute-done | bytes 622624 | tf_op jit(solution)/shard_map/ppermute | solution.py:76
  61.2 1.2 %fusion.6 = f32[3,3,128,256]{3,2,1,0:T(8,128)} fusion(s32[]{:T(128)S(6)} %select_n.114, f32[3,3,128,256]{3,2,1,0:T(8,128)S(1)} %reshape.240), kind=kLoop, calls=%fused_computation.63 | loop fusion | flops 294912 | bytes 2359300 | tf_op jit(solution)/shard_map/concatenate | solution.py:184
  62.4 5.4 %collective-permute-done.16 = bf16[128,2048]{1,0:T(8,128)(2,1)} collective-permute-done((bf16[128,2048]{1,0:T(8,128)(2,1)}, bf16[128,2048]{1,0:T(8,128)(2,1)}, u32[]{:S(2)}, u32[]{:S(2)}) %collective-permute-start.16) | collective-permute-done | bytes 524320 | tf_op jit(solution)/shard_map/ppermute | solution.py:198
  67.8 1.2 %fusion.21 = bf16[16,8,16,128]{3,1,2,0:T(8,128)(2,1)S(1)} fusion(f32[128,2048]{1,0:T(8,128)S(1)} %convolution_add_fusion, bf16[128,2048]{1,0:T(8,128)(2,1)} %collective-permute-done.16), kind=kLoop, calls=%fused_computation.96 | loop fusion | flops 786432 | bytes 2097152
  68.9 0.9 %copy.30 = bf16[16,8,16,128]{3,2,1,0:T(8,128)(2,1)} copy(bf16[16,8,16,128]{3,1,2,0:T(8,128)(2,1)S(1)} %fusion.21) | data formatting | bytes 1048576
  (115 shorter events, 19.7 us)
Async XLA Ops:
  0.6 8.4 %copy-start.1 = (bf16[128,16,128]{2,1,0:T(8,128)(2,1)S(1)}, bf16[128,16,128]{2,1,0:T(8,128)(2,1)}, u32[]{:S(2)}) copy-start(bf16[128,16,128]{2,1,0:T(8,128)(2,1)} %param.5) | copy-start | bytes 1572868
  2.2 16.6 %collective-permute-start.5 = (bf16[128,16,128]{0,2,1:T(8,128)(2,1)S(1)}, bf16[128,16,128]{0,2,1:T(8,128)(2,1)S(1)}, u32[]{:S(2)}, u32[]{:S(2)}) collective-permute-start(bf16[128,16,128]{0,2,1:T(8,128)(2,1)S(1)} %copy.12), channel_id=1, source_target_pairs={{0,2},{2,0},{1,3},{3,1},{4,6},{6,4},{5,7},{7,5},{8,10},{10,8},{9,1... | collective-permute-start | bytes 1572872 | tf_op jit(solution)/shard_map/ppermute | solution.py:142
  5.2 5.5 %collective-permute-start = (bf16[128,16,1]{0,2,1:T(2,128)(2,1)S(1)}, bf16[128,16,1]{0,2,1:T(2,128)(2,1)S(1)}, u32[]{:S(2)}, u32[]{:S(2)}) collective-permute-start(bf16[128,16,1]{0,2,1:T(2,128)(2,1)S(1)} %get-tuple-element.75), channel_id=1, source_target_pairs={{0,4},{4,8},{8,12},{12,0},{1,5},{5,9},{9,13},{13,1},{2,6},{6,10},{... | collective-permute-start | bytes 12296 | tf_op jit(solution)/shard_map/ppermute | solution.py:14
  6.8 3.9 %collective-permute-start.1 = (bf16[128,16,1]{0,2,1:T(2,128)(2,1)S(1)}, bf16[128,16,1]{0,2,1:T(2,128)(2,1)S(1)}, u32[]{:S(2)}, u32[]{:S(2)}) collective-permute-start(bf16[128,16,1]{0,2,1:T(2,128)(2,1)S(1)} %get-tuple-element.76), channel_id=1, source_target_pairs={{4,0},{8,4},{12,8},{0,12},{5,1},{9,5},{13,9},{1,13},{6,2},{10,6},{... | collective-permute-start | bytes 12296 | tf_op jit(solution)/shard_map/ppermute | solution.py:15
  10.7 1.3 %collective-permute-start.2 = (bf16[128,1,130]{0,2,1:T(8,128)(2,1)S(1)}, bf16[128,1,130]{0,2,1:T(8,128)(2,1)S(1)}, u32[]{:S(2)}, u32[]{:S(2)}) collective-permute-start(bf16[128,1,130]{0,2,1:T(8,128)(2,1)S(1)} %get-tuple-element.73), channel_id=1, source_target_pairs={{0,1},{1,0},{2,3},{3,2},{4,5},{5,4},{6,7},{7,6},{8,9},{9,8},{10,11... | collective-permute-start | bytes 99848 | tf_op jit(solution)/shard_map/ppermute | solution.py:14
  10.8 1.4 %collective-permute-start.3 = (bf16[128,1,130]{0,2,1:T(8,128)(2,1)S(1)}, bf16[128,1,130]{0,2,1:T(8,128)(2,1)S(1)}, u32[]{:S(2)}, u32[]{:S(2)}) collective-permute-start(bf16[128,1,130]{0,2,1:T(8,128)(2,1)S(1)} %get-tuple-element.74), channel_id=1, source_target_pairs={{1,0},{0,1},{3,2},{2,3},{5,4},{4,5},{7,6},{6,7},{9,8},{8,9},{11,10... | collective-permute-start | bytes 99848 | tf_op jit(solution)/shard_map/ppermute | solution.py:15
  12.5 1.5 %copy-start = (bf16[3,3,128,256]{3,2,1,0:T(8,128)(2,1)S(1)}, bf16[3,3,128,256]{3,2,1,0:T(8,128)(2,1)}, u32[]{:S(2)}) copy-start(bf16[3,3,128,256]{3,2,1,0:T(8,128)(2,1)} %param.6) | copy-start | bytes 1769476
  13.5 5.2 %collective-permute-start.4 = (bf16[128,292]{0,1:T(8,128)(2,1)S(1)}, bf16[128,292]{0,1:T(8,128)(2,1)S(1)}, u32[]{:S(2)}, u32[]{:S(2)}) collective-permute-start(bf16[128,292]{0,1:T(8,128)(2,1)S(1)} %pad_maximum_fusion.5), channel_id=1, source_target_pairs={{0,2},{2,0},{1,3},{3,1},{4,6},{6,4},{5,7},{7,5},{8,10},{10,8},{9,1... | collective-permute-start | bytes 224264 | tf_op jit(solution)/shard_map/ppermute | solution.py:148
  24.6 0.7 copy-start.2
  30.2 2.2 %collective-permute-start.6 = (f32[1216,128]{1,0:T(8,128)S(1)}, f32[1216,128]{1,0:T(8,128)}, u32[]{:S(2)}, u32[]{:S(2)}) collective-permute-start(f32[1216,128]{1,0:T(8,128)S(1)} %dynamic-slice_bitcast_fusion), channel_id=1, source_target_pairs={{0,1},{1,0},{2,3},{3,2},{4,5},{5,4},{6,7},{7,6},{8,9},{9,8},{10,11... | collective-permute-start | bytes 1867784 | tf_op jit(solution)/shard_map/ppermute | solution.py:64
  33.6 7.0 %collective-permute-start.7 = (bf16[320,128]{1,0:T(8,128)(2,1)S(1)}, bf16[320,128]{1,0:T(8,128)(2,1)S(1)}, u32[]{:S(2)}, u32[]{:S(2)}) collective-permute-start(bf16[320,128]{1,0:T(8,128)(2,1)S(1)} %pad_maximum_fusion.3), channel_id=1, source_target_pairs={{0,4},{4,8},{8,12},{12,0},{1,5},{5,9},{9,13},{13,1},{2,6},{6,10},{... | collective-permute-start | bytes 245768 | tf_op jit(solution)/shard_map/ppermute | solution.py:104
  35.5 6.0 %collective-permute-start.8 = (bf16[320,128]{1,0:T(8,128)(2,1)S(1)}, bf16[320,128]{1,0:T(8,128)(2,1)S(1)}, u32[]{:S(2)}, u32[]{:S(2)}) collective-permute-start(bf16[320,128]{1,0:T(8,128)(2,1)S(1)} %pad_maximum_fusion.4), channel_id=1, source_target_pairs={{0,12},{4,0},{8,4},{12,8},{1,13},{5,1},{9,5},{13,9},{2,14},{6,2},{... | collective-permute-start | bytes 245768 | tf_op jit(solution)/shard_map/ppermute | solution.py:104
  38.4 7.0 %collective-permute-start.11 = (bf16[304,128]{1,0:T(8,128)(2,1)S(1)}, bf16[304,128]{1,0:T(8,128)(2,1)S(1)}, u32[]{:S(2)}, u32[]{:S(2)}) collective-permute-start(bf16[304,128]{1,0:T(8,128)(2,1)S(1)} %get-tuple-element.66), channel_id=1, source_target_pairs={{0,8},{4,12},{8,0},{12,4},{1,9},{5,13},{9,1},{13,5},{2,10},{6,14},... | collective-permute-start | bytes 233480 | tf_op jit(solution)/shard_map/ppermute | solution.py:104
  41.7 6.5 %collective-permute-start.10 = (bf16[128,1,130]{0,2,1:T(8,128)(2,1)S(1)}, bf16[128,1,130]{0,2,1:T(8,128)(2,1)S(1)}, u32[]{:S(2)}, u32[]{:S(2)}) collective-permute-start(bf16[128,1,130]{0,2,1:T(8,128)(2,1)S(1)} %get-tuple-element.72), channel_id=1, source_target_pairs={{1,0},{0,1},{3,2},{2,3},{5,4},{4,5},{7,6},{6,7},{9,8},{8,9},{11,10... | collective-permute-start | bytes 99848 | tf_op jit(solution)/shard_map/ppermute | solution.py:15
  41.8 6.4 %collective-permute-start.9 = (bf16[128,1,130]{0,2,1:T(8,128)(2,1)S(1)}, bf16[128,1,130]{0,2,1:T(8,128)(2,1)S(1)}, u32[]{:S(2)}, u32[]{:S(2)}) collective-permute-start(bf16[128,1,130]{0,2,1:T(8,128)(2,1)S(1)} %get-tuple-element.71), channel_id=1, source_target_pairs={{0,1},{1,0},{2,3},{3,2},{4,5},{5,4},{6,7},{7,6},{8,9},{9,8},{10,11... | collective-permute-start | bytes 99848 | tf_op jit(solution)/shard_map/ppermute | solution.py:14
  45.4 12.2 %collective-permute-start.12 = (bf16[304,128]{1,0:T(8,128)(2,1)S(1)}, bf16[304,128]{1,0:T(8,128)(2,1)S(1)}, u32[]{:S(2)}, u32[]{:S(2)}) collective-permute-start(bf16[304,128]{1,0:T(8,128)(2,1)S(1)} %get-tuple-element.15), channel_id=1, source_target_pairs={{0,12},{4,0},{8,4},{12,8},{1,13},{5,1},{9,5},{13,9},{2,14},{6,2},{... | collective-permute-start | bytes 233480 | tf_op jit(solution)/shard_map/ppermute | solution.py:76
  47.5 10.1 %collective-permute-start.13 = (bf16[304,128]{1,0:T(8,128)(2,1)S(1)}, bf16[304,128]{1,0:T(8,128)(2,1)S(1)}, u32[]{:S(2)}, u32[]{:S(2)}) collective-permute-start(bf16[304,128]{1,0:T(8,128)(2,1)S(1)} %get-tuple-element.15), channel_id=1, source_target_pairs={{0,8},{4,12},{8,0},{12,4},{1,9},{5,13},{9,1},{13,5},{2,10},{6,14},... | collective-permute-start | bytes 233480 | tf_op jit(solution)/shard_map/ppermute | solution.py:76
  47.5 10.2 %collective-permute-start.14 = (bf16[304,128]{1,0:T(8,128)(2,1)S(1)}, bf16[304,128]{1,0:T(8,128)(2,1)S(1)}, u32[]{:S(2)}, u32[]{:S(2)}) collective-permute-start(bf16[304,128]{1,0:T(8,128)(2,1)S(1)} %get-tuple-element.15), channel_id=1, source_target_pairs={{0,4},{4,8},{8,12},{12,0},{1,5},{5,9},{9,13},{13,1},{2,6},{6,10},{... | collective-permute-start | bytes 233480 | tf_op jit(solution)/shard_map/ppermute | solution.py:76
  54.1 13.7 %collective-permute-start.16 = (bf16[128,2048]{1,0:T(8,128)(2,1)}, bf16[128,2048]{1,0:T(8,128)(2,1)}, u32[]{:S(2)}, u32[]{:S(2)}) collective-permute-start(bf16[128,2048]{1,0:T(8,128)(2,1)} %fusion.2), channel_id=1, source_target_pairs={{0,2},{2,0},{1,3},{3,1},{4,6},{6,4},{5,7},{7,5},{8,10},{10,8},{9,1... | collective-permute-start | bytes 1572872 | tf_op jit(solution)/shard_map/ppermute | solution.py:198
  57.9 2.1 %collective-permute-start.15 = (f32[1216,128]{1,0:T(8,128)S(1)}, f32[1216,128]{1,0:T(8,128)S(1)}, u32[]{:S(2)}, u32[]{:S(2)}) collective-permute-start(f32[1216,128]{1,0:T(8,128)S(1)} %bitcast.321), channel_id=1, source_target_pairs={{0,1},{1,0},{2,3},{3,2},{4,5},{5,4},{6,7},{7,6},{8,9},{9,8},{10,11... | collective-permute-start | bytes 1867784 | tf_op jit(solution)/shard_map/ppermute | solution.py:76

commit v30 on v25

--- a/solution.py
+++ b/solution.py
@@ -110,7 +110,7 @@
 
 def sum_finish(rows, size, send_dtype):
     rows = direct_all_gather(rows, "lon", send_dtype)
-    rows = direct_all_gather(rows, "lat", send_dtype)
+    rows = direct_all_gather(rows, "lat", jnp.float32)
     return rows.reshape(-1)[:size]
 
 

time: 69.5 us -> 69.5 us (level)
  no operation moved by 1% of the time
where the time goes in v30:
time: 69.5 us; the launch traced here: 69.3 us
  starting transfers between devices  17.9 us (26%)
  waiting for transfers between devices  16.5 us (24%)
  matrix products  15.5 us (22%)
  local copies, waits for them, and re-layouts  10.3 us (15%)
  other arithmetic  7.55 us (11%)
  between operations  1.47 us (2%)
    dot_general x36, matrix products, conv_taps(): jnp.dot(kernel[tap_row, tap_col], window, preferred_element_type=jnp.floa...  12.7 us
    ppermute x1, waiting for transfers between devices, local(): received.append(lax.ppermute(outgoing[shift - 1], 'chan', pairs))  5.4 us
    ppermute x3, waiting for transfers between devices, sum_start(): moved = lax.ppermute(piece, 'lon', pairs)  5.21 us
    ppermute x3, starting transfers between devices, sum_start(): moved = lax.ppermute(piece, 'lon', pairs)  4.99 us
    slice x4, local copies, waits for them, and re-layouts, window_of(): field[:, first_row:first_row + row_count, first_col:first_col + column_co...  3.74 us
    unnamed x12, local copies, waits for them, and re-layouts  3.51 us
    ppermute x1, starting transfers between devices, local(): raw_blocks.append(lax.ppermute(inputs, 'chan', pairs))  3 us
    dot_general x9, matrix products, local(): lax.dot_general(grad_pre, window, (((1,), (1,)), ((), ())), preferred_ele...  2.85 us
  transfers between devices with their start and end apart: 17, of which 10 were waited for; matrix products, arithmetic and copies ran while one was open for 25% of the time, Pallas kernels for 0%

profile of v30, /device:TPU:0, one launch (start us, length us, event | category | flops | bytes accessed | tf_op | source)
XLA Modules:
  0.0 69.3 jit_solution(1982711397606971210)
XLA Ops:
  0.6 1.5 %copy.12 = bf16[128,16,128]{0,2,1:T(8,128)(2,1)S(1)} copy(bf16[128,16,128]{2,1,0:T(8,128)(2,1)} %param.4) | data formatting | bytes 1048576 | tf_op args[0]
  2.2 3.0 %collective-permute-start.5 = (bf16[128,16,128]{0,2,1:T(8,128)(2,1)S(1)}, bf16[128,16,128]{0,2,1:T(8,128)(2,1)S(1)}, u32[]{:S(2)}, u32[]{:S(2)}) collective-permute-start(bf16[128,16,128]{0,2,1:T(8,128)(2,1)S(1)} %copy.12), channel_id=1, source_target_pairs={{0,2},{2,0},{1,3},{3,1},{4,6},{6,4},{5,7},{7,5},{8,10},{10,8},{9,1... | collective-permute-start | bytes 1572872 | tf_op jit(solution)/shard_map/ppermute | solution.py:142
  5.2 1.6 %collective-permute-start = (bf16[128,16,1]{0,2,1:T(2,128)(2,1)S(1)}, bf16[128,16,1]{0,2,1:T(2,128)(2,1)S(1)}, u32[]{:S(2)}, u32[]{:S(2)}) collective-permute-start(bf16[128,16,1]{0,2,1:T(2,128)(2,1)S(1)} %get-tuple-element.75), channel_id=1, source_target_pairs={{0,4},{4,8},{8,12},{12,0},{1,5},{5,9},{9,13},{13,1},{2,6},{6,10},{... | collective-permute-start | bytes 12296 | tf_op jit(solution)/shard_map/ppermute | solution.py:14
  6.8 2.2 %collective-permute-start.1 = (bf16[128,16,1]{0,2,1:T(2,128)(2,1)S(1)}, bf16[128,16,1]{0,2,1:T(2,128)(2,1)S(1)}, u32[]{:S(2)}, u32[]{:S(2)}) collective-permute-start(bf16[128,16,1]{0,2,1:T(2,128)(2,1)S(1)} %get-tuple-element.76), channel_id=1, source_target_pairs={{4,0},{8,4},{12,8},{0,12},{5,1},{9,5},{13,9},{1,13},{6,2},{10,6},{... | collective-permute-start | bytes 12296 | tf_op jit(solution)/shard_map/ppermute | solution.py:15
  9.2 1.5 %collective-permute-done = bf16[128,16,1]{0,2,1:T(2,128)(2,1)S(1)} collective-permute-done((bf16[128,16,1]{0,2,1:T(2,128)(2,1)S(1)}, bf16[128,16,1]{0,2,1:T(2,128)(2,1)S(1)}, u32[]{:S(2)}, u32[]{:S(2)}) %collective-permute-start) | collective-permute-done | bytes 4128 | tf_op jit(solution)/shard_map/ppermute | solution.py:14
  11.3 0.7 collective-permute-done.2
  12.5 0.9 %fusion.56 = (bf16[128,16,128]{0,2,1:T(8,128)(2,1)S(1)}, bf16[128,16,128]{0,2,1:T(8,128)(2,1)S(1)}, bf16[128,16,128]{0,2,1:T(8,128)(2,1)S(1)}, bf16[128,16,128]{...) fusion(bf16[128,18,130]{0,2,1:T(8,128)(2,1)S(1)} %maximum_selec, ...), kind=kLoop, calls=%fused_computation.204 | loop fusion | bytes 9437184 | tf_op jit(solution)/shard_map/slice | solution.py:37
  16.7 2.0 %collective-permute-done.4 = bf16[128,292]{0,1:T(8,128)(2,1)S(1)} collective-permute-done((bf16[128,292]{0,1:T(8,128)(2,1)S(1)}, bf16[128,292]{0,1:T(8,128)(2,1)S(1)}, u32[]{:S(2)}, u32[]{:S(2)}) %collective-permute-start.4) | collective-permute-done | bytes 74784 | tf_op jit(solution)/shard_map/ppermute | solution.py:148
  19.0 1.0 %fusion.54 = (bf16[128,16,128]{0,2,1:T(8,128)(2,1)S(1)}, bf16[128,16,128]{0,2,1:T(8,128)(2,1)S(1)}, bf16[128,16,128]{0,2,1:T(8,128)(2,1)S(1)}, bf16[128,16,128]{...) fusion(bf16[128,18,130]{0,2,1:T(8,128)(2,1)S(1)} %pad_maximum_f, ...), kind=kLoop, calls=%fused_computation.202 | loop fusion | bytes 9437184 | tf_op jit(solution)/shard_map/slice | solution.py:37
  19.9 2.5 %fusion.14 = (bf16[256,16,128]{0,2,1:T(8,128)(2,1)S(1)}, bf16[256,16,128]{0,2,1:T(8,128)(2,1)S(1)}, bf16[256,16,128]{0,2,1:T(8,128)(2,1)S(1)}, bf16[256,16,128]{...) fusion(bf16[128,18,130]{0,2,1:T(8,128)(2,1)S(1)} %maximum_selec, ...), kind=kLoop, calls=%fused_computation.81 | loop fusion | flops 18874368 | bytes 10635264 | tf_op jit(solution)/shard_map/concatenate | solution.py:164
  25.3 1.0 %convert_reduce_fusion = (f32[128]{0:T(128)S(1)}, bf16[128,2048]{1,0:T(8,128)(2,1)S(1)}) fusion(f32[128]{0:T(128)S(1)} %copy-done.2, f32[128,2048]{1,0:T(8,128)S(1)} %convolution_add_fusion.24, f32[128,2048]{1,0:T(8,128)S(1)} %convolution_add_fusion.17, bf16[128,2048]{0,1:T(8,128)(2,1)S(1)} %bitcast.358, bf16[3,3,128,256]{3,2,1,0:T(8,128)(2,1)S(1)} %copy-done, ...), kind=kOutput, calls=%fused_computation.90 | convolution fusion | flops 71040896 | bytes 4228104 | tf_op jit(solution)/shard_map/dot_general | solution.py:50
  29.4 0.6 copy.28
  30.5 0.8 %slice_reduce_fusion.1 = (bf16[128,16]{1,0:T(8,128)(2,1)S(1)}, bf16[128,16]{1,0:T(8,128)(2,1)S(1)}) fusion(bf16[128,16,128]{2,1,0:T(8,128)(2,1)S(1)} %bitcast.304), kind=kLoop, calls=%fused_computation.98 | loop fusion | bytes 16384 | tf_op jit(solution)/shard_map/slice | solution.py:179
  32.0 1.0 %bitcast_add_fusion = f32[1216,128]{1,0:T(8,128)S(1)} fusion(bf16[1216,128]{1,0:T(8,128)(2,1)} %collective-permute-done.6, f32[2,1216,128]{2,1,0:T(8,128)S(1)} %bitcast.320, s32[]{:T(128)S(6)} %select_n.98), kind=kLoop, calls=%fused_computation.94 | loop fusion | flops 311296 | bytes 1556484 | tf_op jit(solution)/shard_map/add | solution.py:64
  33.1 1.9 %collective-permute-start.7 = (bf16[320,128]{1,0:T(8,128)(2,1)S(1)}, bf16[320,128]{1,0:T(8,128)(2,1)S(1)}, u32[]{:S(2)}, u32[]{:S(2)}) collective-permute-start(bf16[320,128]{1,0:T(8,128)(2,1)S(1)} %pad_maximum_fusion.3), channel_id=1, source_target_pairs={{0,4},{4,8},{8,12},{12,0},{1,5},{5,9},{9,13},{13,1},{2,6},{6,10},{... | collective-permute-start | bytes 245768 | tf_op jit(solution)/shard_map/ppermute | solution.py:104
  34.9 2.3 %collective-permute-start.8 = (bf16[320,128]{1,0:T(8,128)(2,1)S(1)}, bf16[320,128]{1,0:T(8,128)(2,1)S(1)}, u32[]{:S(2)}, u32[]{:S(2)}) collective-permute-start(bf16[320,128]{1,0:T(8,128)(2,1)S(1)} %pad_maximum_fusion.4), channel_id=1, source_target_pairs={{0,12},{4,0},{8,4},{12,8},{1,13},{5,1},{9,5},{13,9},{2,14},{6,2},{... | collective-permute-start | bytes 245768 | tf_op jit(solution)/shard_map/ppermute | solution.py:104
  37.8 0.8 %collective-permute-start.11 = (bf16[304,128]{1,0:T(8,128)(2,1)S(1)}, bf16[304,128]{1,0:T(8,128)(2,1)S(1)}, u32[]{:S(2)}, u32[]{:S(2)}) collective-permute-start(bf16[304,128]{1,0:T(8,128)(2,1)S(1)} %get-tuple-element.66), channel_id=1, source_target_pairs={{0,8},{4,12},{8,0},{12,4},{1,9},{5,13},{9,1},{13,5},{2,10},{6,14},... | collective-permute-start | bytes 233480 | tf_op jit(solution)/shard_map/ppermute | solution.py:104
  38.6 1.4 %collective-permute-done.7 = bf16[320,128]{1,0:T(8,128)(2,1)S(1)} collective-permute-done((bf16[320,128]{1,0:T(8,128)(2,1)S(1)}, bf16[320,128]{1,0:T(8,128)(2,1)S(1)}, u32[]{:S(2)}, u32[]{:S(2)}) %collective-permute-start.7) | collective-permute-done | bytes 81952 | tf_op jit(solution)/shard_map/ppermute | solution.py:104
  40.2 0.7 %collective-permute-done.8 = bf16[320,128]{1,0:T(8,128)(2,1)S(1)} collective-permute-done((bf16[320,128]{1,0:T(8,128)(2,1)S(1)}, bf16[320,128]{1,0:T(8,128)(2,1)S(1)}, u32[]{:S(2)}, u32[]{:S(2)}) %collective-permute-start.8) | collective-permute-done | bytes 81952 | tf_op jit(solution)/shard_map/ppermute | solution.py:104
  41.7 3.1 %collective-permute-done.11 = bf16[304,128]{1,0:T(8,128)(2,1)S(1)} collective-permute-done((bf16[304,128]{1,0:T(8,128)(2,1)S(1)}, bf16[304,128]{1,0:T(8,128)(2,1)S(1)}, u32[]{:S(2)}, u32[]{:S(2)}) %collective-permute-start.11) | collective-permute-done | bytes 77856 | tf_op jit(solution)/shard_map/ppermute | solution.py:104
  44.8 2.1 %collective-permute-start.12 = (bf16[304,128]{1,0:T(8,128)(2,1)S(1)}, bf16[304,128]{1,0:T(8,128)(2,1)S(1)}, u32[]{:S(2)}, u32[]{:S(2)}) collective-permute-start(bf16[304,128]{1,0:T(8,128)(2,1)S(1)} %get-tuple-element.15), channel_id=1, source_target_pairs={{0,12},{4,0},{8,4},{12,8},{1,13},{5,1},{9,5},{13,9},{2,14},{6,2},{... | collective-permute-start | bytes 233480 | tf_op jit(solution)/shard_map/ppermute | solution.py:76
  46.9 0.6 collective-permute-start.14
  47.9 0.9 %fusion.53 = (bf16[128,16,128]{0,2,1:T(8,128)(2,1)S(1)}, bf16[128,16,128]{0,2,1:T(8,128)(2,1)S(1)}, bf16[128,16,128]{0,2,1:T(8,128)(2,1)S(1)}, bf16[128,16,128]{...) fusion(bf16[128,18,130]{0,2,1:T(8,128)(2,1)S(1)} %maximum_selec, ...), kind=kLoop, calls=%fused_computation.201 | loop fusion | bytes 9437184 | tf_op jit(solution)/shard_map/slice | solution.py:37
  51.5 1.1 %fusion.2 = bf16[128,2048]{1,0:T(8,128)(2,1)} fusion(f32[128,2048]{1,0:T(8,128)S(1)} %convolution_add_fusion.9, bf16[128,2048]{0,1:T(8,128)(2,1)S(1)} %bitcast.345, bf16[3,3,128,128]{2,3,1,0:T(8,128)(2,1)S(1)} %get-tuple-element.70), kind=kOutput, calls=%fused_computation.38 | convolution fusion | flops 67633152 | bytes 2129920 | tf_op jit(solution)/shard_map/dot_general | solution.py:50
  52.6 0.9 %fusion.52 = (bf16[128,16,128]{0,2,1:T(8,128)(2,1)S(1)}, bf16[128,16,128]{0,2,1:T(8,128)(2,1)S(1)}, bf16[128,16,128]{0,2,1:T(8,128)(2,1)S(1)}, bf16[128,16,128]{...) fusion(bf16[128,18,130]{0,2,1:T(8,128)(2,1)S(1)} %maximum_selec, ...), kind=kLoop, calls=%fused_computation.200 | loop fusion | bytes 9437184 | tf_op jit(solution)/shard_map/slice | solution.py:37
  53.5 1.6 %collective-permute-start.16 = (bf16[128,2048]{1,0:T(8,128)(2,1)}, bf16[128,2048]{1,0:T(8,128)(2,1)}, u32[]{:S(2)}, u32[]{:S(2)}) collective-permute-start(bf16[128,2048]{1,0:T(8,128)(2,1)} %fusion.2), channel_id=1, source_target_pairs={{0,2},{2,0},{1,3},{3,1},{4,6},{6,4},{5,7},{7,5},{8,10},{10,8},{9,1... | collective-permute-start | bytes 1572872 | tf_op jit(solution)/shard_map/ppermute | solution.py:198
  58.4 1.1 %collective-permute-done.15 = f32[1216,128]{1,0:T(8,128)S(1)} collective-permute-done((f32[1216,128]{1,0:T(8,128)S(1)}, f32[1216,128]{1,0:T(8,128)S(1)}, u32[]{:S(2)}, u32[]{:S(2)}) %collective-permute-start.15) | collective-permute-done | bytes 622624 | tf_op jit(solution)/shard_map/ppermute | solution.py:76
  59.8 0.5 slice.493
  60.6 1.2 %fusion.6 = f32[3,3,128,256]{3,2,1,0:T(8,128)} fusion(s32[]{:T(128)S(6)} %select_n.114, f32[3,3,128,256]{3,2,1,0:T(8,128)S(1)} %reshape.241), kind=kLoop, calls=%fused_computation.63 | loop fusion | flops 294912 | bytes 2359300 | tf_op jit(solution)/shard_map/concatenate | solution.py:184
  61.8 5.4 %collective-permute-done.16 = bf16[128,2048]{1,0:T(8,128)(2,1)} collective-permute-done((bf16[128,2048]{1,0:T(8,128)(2,1)}, bf16[128,2048]{1,0:T(8,128)(2,1)}, u32[]{:S(2)}, u32[]{:S(2)}) %collective-permute-start.16) | collective-permute-done | bytes 524320 | tf_op jit(solution)/shard_map/ppermute | solution.py:198
  67.2 1.2 %fusion.21 = bf16[16,8,16,128]{3,1,2,0:T(8,128)(2,1)S(1)} fusion(f32[128,2048]{1,0:T(8,128)S(1)} %convolution_add_fusion, bf16[128,2048]{1,0:T(8,128)(2,1)} %collective-permute-done.16), kind=kLoop, calls=%fused_computation.96 | loop fusion | flops 786432 | bytes 2097152
  68.4 0.9 %copy.30 = bf16[16,8,16,128]{3,2,1,0:T(8,128)(2,1)} copy(bf16[16,8,16,128]{3,1,2,0:T(8,128)(2,1)S(1)} %fusion.21) | data formatting | bytes 1048576
  (115 shorter events, 19.7 us)
Async XLA Ops:
  0.6 8.4 %copy-start.1 = (bf16[128,16,128]{2,1,0:T(8,128)(2,1)S(1)}, bf16[128,16,128]{2,1,0:T(8,128)(2,1)}, u32[]{:S(2)}) copy-start(bf16[128,16,128]{2,1,0:T(8,128)(2,1)} %param.5) | copy-start | bytes 1572868
  2.2 16.6 %collective-permute-start.5 = (bf16[128,16,128]{0,2,1:T(8,128)(2,1)S(1)}, bf16[128,16,128]{0,2,1:T(8,128)(2,1)S(1)}, u32[]{:S(2)}, u32[]{:S(2)}) collective-permute-start(bf16[128,16,128]{0,2,1:T(8,128)(2,1)S(1)} %copy.12), channel_id=1, source_target_pairs={{0,2},{2,0},{1,3},{3,1},{4,6},{6,4},{5,7},{7,5},{8,10},{10,8},{9,1... | collective-permute-start | bytes 1572872 | tf_op jit(solution)/shard_map/ppermute | solution.py:142
  5.2 5.5 %collective-permute-start = (bf16[128,16,1]{0,2,1:T(2,128)(2,1)S(1)}, bf16[128,16,1]{0,2,1:T(2,128)(2,1)S(1)}, u32[]{:S(2)}, u32[]{:S(2)}) collective-permute-start(bf16[128,16,1]{0,2,1:T(2,128)(2,1)S(1)} %get-tuple-element.75), channel_id=1, source_target_pairs={{0,4},{4,8},{8,12},{12,0},{1,5},{5,9},{9,13},{13,1},{2,6},{6,10},{... | collective-permute-start | bytes 12296 | tf_op jit(solution)/shard_map/ppermute | solution.py:14
  6.8 3.9 %collective-permute-start.1 = (bf16[128,16,1]{0,2,1:T(2,128)(2,1)S(1)}, bf16[128,16,1]{0,2,1:T(2,128)(2,1)S(1)}, u32[]{:S(2)}, u32[]{:S(2)}) collective-permute-start(bf16[128,16,1]{0,2,1:T(2,128)(2,1)S(1)} %get-tuple-element.76), channel_id=1, source_target_pairs={{4,0},{8,4},{12,8},{0,12},{5,1},{9,5},{13,9},{1,13},{6,2},{10,6},{... | collective-permute-start | bytes 12296 | tf_op jit(solution)/shard_map/ppermute | solution.py:15
  10.7 1.3 %collective-permute-start.2 = (bf16[128,1,130]{0,2,1:T(8,128)(2,1)S(1)}, bf16[128,1,130]{0,2,1:T(8,128)(2,1)S(1)}, u32[]{:S(2)}, u32[]{:S(2)}) collective-permute-start(bf16[128,1,130]{0,2,1:T(8,128)(2,1)S(1)} %get-tuple-element.73), channel_id=1, source_target_pairs={{0,1},{1,0},{2,3},{3,2},{4,5},{5,4},{6,7},{7,6},{8,9},{9,8},{10,11... | collective-permute-start | bytes 99848 | tf_op jit(solution)/shard_map/ppermute | solution.py:14
  10.8 1.4 %collective-permute-start.3 = (bf16[128,1,130]{0,2,1:T(8,128)(2,1)S(1)}, bf16[128,1,130]{0,2,1:T(8,128)(2,1)S(1)}, u32[]{:S(2)}, u32[]{:S(2)}) collective-permute-start(bf16[128,1,130]{0,2,1:T(8,128)(2,1)S(1)} %get-tuple-element.74), channel_id=1, source_target_pairs={{1,0},{0,1},{3,2},{2,3},{5,4},{4,5},{7,6},{6,7},{9,8},{8,9},{11,10... | collective-permute-start | bytes 99848 | tf_op jit(solution)/shard_map/ppermute | solution.py:15
  12.5 1.5 %copy-start = (bf16[3,3,128,256]{3,2,1,0:T(8,128)(2,1)S(1)}, bf16[3,3,128,256]{3,2,1,0:T(8,128)(2,1)}, u32[]{:S(2)}) copy-start(bf16[3,3,128,256]{3,2,1,0:T(8,128)(2,1)} %param.6) | copy-start | bytes 1769476
  13.5 5.2 %collective-permute-start.4 = (bf16[128,292]{0,1:T(8,128)(2,1)S(1)}, bf16[128,292]{0,1:T(8,128)(2,1)S(1)}, u32[]{:S(2)}, u32[]{:S(2)}) collective-permute-start(bf16[128,292]{0,1:T(8,128)(2,1)S(1)} %pad_maximum_fusion.5), channel_id=1, source_target_pairs={{0,2},{2,0},{1,3},{3,1},{4,6},{6,4},{5,7},{7,5},{8,10},{10,8},{9,1... | collective-permute-start | bytes 224264 | tf_op jit(solution)/shard_map/ppermute | solution.py:148
  24.6 0.7 copy-start.2
  30.2 1.8 %collective-permute-start.6 = (bf16[1216,128]{1,0:T(8,128)(2,1)S(1)}, bf16[1216,128]{1,0:T(8,128)(2,1)}, u32[]{:S(2)}, u32[]{:S(2)}) collective-permute-start(bf16[1216,128]{1,0:T(8,128)(2,1)S(1)} %fusion.22), channel_id=1, source_target_pairs={{0,1},{1,0},{2,3},{3,2},{4,5},{5,4},{6,7},{7,6},{8,9},{9,8},{10,11... | collective-permute-start | bytes 933896 | tf_op jit(solution)/shard_map/ppermute | solution.py:64
  33.1 7.0 %collective-permute-start.7 = (bf16[320,128]{1,0:T(8,128)(2,1)S(1)}, bf16[320,128]{1,0:T(8,128)(2,1)S(1)}, u32[]{:S(2)}, u32[]{:S(2)}) collective-permute-start(bf16[320,128]{1,0:T(8,128)(2,1)S(1)} %pad_maximum_fusion.3), channel_id=1, source_target_pairs={{0,4},{4,8},{8,12},{12,0},{1,5},{5,9},{9,13},{13,1},{2,6},{6,10},{... | collective-permute-start | bytes 245768 | tf_op jit(solution)/shard_map/ppermute | solution.py:104
  34.9 6.0 %collective-permute-start.8 = (bf16[320,128]{1,0:T(8,128)(2,1)S(1)}, bf16[320,128]{1,0:T(8,128)(2,1)S(1)}, u32[]{:S(2)}, u32[]{:S(2)}) collective-permute-start(bf16[320,128]{1,0:T(8,128)(2,1)S(1)} %pad_maximum_fusion.4), channel_id=1, source_target_pairs={{0,12},{4,0},{8,4},{12,8},{1,13},{5,1},{9,5},{13,9},{2,14},{6,2},{... | collective-permute-start | bytes 245768 | tf_op jit(solution)/shard_map/ppermute | solution.py:104
  37.8 7.0 %collective-permute-start.11 = (bf16[304,128]{1,0:T(8,128)(2,1)S(1)}, bf16[304,128]{1,0:T(8,128)(2,1)S(1)}, u32[]{:S(2)}, u32[]{:S(2)}) collective-permute-start(bf16[304,128]{1,0:T(8,128)(2,1)S(1)} %get-tuple-element.66), channel_id=1, source_target_pairs={{0,8},{4,12},{8,0},{12,4},{1,9},{5,13},{9,1},{13,5},{2,10},{6,14},... | collective-permute-start | bytes 233480 | tf_op jit(solution)/shard_map/ppermute | solution.py:104
  41.1 6.5 %collective-permute-start.10 = (bf16[128,1,130]{0,2,1:T(8,128)(2,1)S(1)}, bf16[128,1,130]{0,2,1:T(8,128)(2,1)S(1)}, u32[]{:S(2)}, u32[]{:S(2)}) collective-permute-start(bf16[128,1,130]{0,2,1:T(8,128)(2,1)S(1)} %get-tuple-element.72), channel_id=1, source_target_pairs={{1,0},{0,1},{3,2},{2,3},{5,4},{4,5},{7,6},{6,7},{9,8},{8,9},{11,10... | collective-permute-start | bytes 99848 | tf_op jit(solution)/shard_map/ppermute | solution.py:15
  41.2 6.4 %collective-permute-start.9 = (bf16[128,1,130]{0,2,1:T(8,128)(2,1)S(1)}, bf16[128,1,130]{0,2,1:T(8,128)(2,1)S(1)}, u32[]{:S(2)}, u32[]{:S(2)}) collective-permute-start(bf16[128,1,130]{0,2,1:T(8,128)(2,1)S(1)} %get-tuple-element.71), channel_id=1, source_target_pairs={{0,1},{1,0},{2,3},{3,2},{4,5},{5,4},{6,7},{7,6},{8,9},{9,8},{10,11... | collective-permute-start | bytes 99848 | tf_op jit(solution)/shard_map/ppermute | solution.py:14
  44.8 12.2 %collective-permute-start.12 = (bf16[304,128]{1,0:T(8,128)(2,1)S(1)}, bf16[304,128]{1,0:T(8,128)(2,1)S(1)}, u32[]{:S(2)}, u32[]{:S(2)}) collective-permute-start(bf16[304,128]{1,0:T(8,128)(2,1)S(1)} %get-tuple-element.15), channel_id=1, source_target_pairs={{0,12},{4,0},{8,4},{12,8},{1,13},{5,1},{9,5},{13,9},{2,14},{6,2},{... | collective-permute-start | bytes 233480 | tf_op jit(solution)/shard_map/ppermute | solution.py:76
  46.9 10.1 %collective-permute-start.13 = (bf16[304,128]{1,0:T(8,128)(2,1)S(1)}, bf16[304,128]{1,0:T(8,128)(2,1)S(1)}, u32[]{:S(2)}, u32[]{:S(2)}) collective-permute-start(bf16[304,128]{1,0:T(8,128)(2,1)S(1)} %get-tuple-element.15), channel_id=1, source_target_pairs={{0,8},{4,12},{8,0},{12,4},{1,9},{5,13},{9,1},{13,5},{2,10},{6,14},... | collective-permute-start | bytes 233480 | tf_op jit(solution)/shard_map/ppermute | solution.py:76
  46.9 10.2 %collective-permute-start.14 = (bf16[304,128]{1,0:T(8,128)(2,1)S(1)}, bf16[304,128]{1,0:T(8,128)(2,1)S(1)}, u32[]{:S(2)}, u32[]{:S(2)}) collective-permute-start(bf16[304,128]{1,0:T(8,128)(2,1)S(1)} %get-tuple-element.15), channel_id=1, source_target_pairs={{0,4},{4,8},{8,12},{12,0},{1,5},{5,9},{9,13},{13,1},{2,6},{6,10},{... | collective-permute-start | bytes 233480 | tf_op jit(solution)/shard_map/ppermute | solution.py:76
  53.5 13.7 %collective-permute-start.16 = (bf16[128,2048]{1,0:T(8,128)(2,1)}, bf16[128,2048]{1,0:T(8,128)(2,1)}, u32[]{:S(2)}, u32[]{:S(2)}) collective-permute-start(bf16[128,2048]{1,0:T(8,128)(2,1)} %fusion.2), channel_id=1, source_target_pairs={{0,2},{2,0},{1,3},{3,1},{4,6},{6,4},{5,7},{7,5},{8,10},{10,8},{9,1... | collective-permute-start | bytes 1572872 | tf_op jit(solution)/shard_map/ppermute | solution.py:198
  57.3 2.1 %collective-permute-start.15 = (f32[1216,128]{1,0:T(8,128)S(1)}, f32[1216,128]{1,0:T(8,128)S(1)}, u32[]{:S(2)}, u32[]{:S(2)}) collective-permute-start(f32[1216,128]{1,0:T(8,128)S(1)} %bitcast.321), channel_id=1, source_target_pairs={{0,1},{1,0},{2,3},{3,2},{4,5},{5,4},{6,7},{7,6},{8,9},{9,8},{10,11... | collective-permute-start | bytes 1867784 | tf_op jit(solution)/shard_map/ppermute | solution.py:76
